TPU v7x, 32 devices: a whole 2x2x4 slice. The times are simulated.
32 devices in a mesh: groups: 2 (over y), ctx: 4 (over z), mp: 4 (over x, core).
Axes of the slice: x: 2, y: 2, z: 4, core: 2. Of those that a mesh axis runs over, the one named last changes fastest.
Arguments:
- features: bfloat16 [4, 512, 1536], P('groups', 'ctx'), parts along dimension 0, may hold values from -6 to 6
- frame_counts: int32 [4], P('groups'), parts along dimension 0, may hold values from 1 to 512, 768 in all
- attn_gain: float32 [1536], replicated, may hold values from 0.25 to 1.75
- w_qkv: bfloat16 [3, 1536, 1024], P(None, None, 'mp'), may hold values from -2 to 2
- w_out: bfloat16 [1024, 1536], P('mp'), may hold values from -0.375 to 0.375
- conv_gain: float32 [1536], replicated, may hold values from 0.25 to 1.75
- w_glu: bfloat16 [2, 1536, 1536], P(None, None, 'mp'), may hold values from -0.15625 to 0.15625
- kernel: float32 [31, 1536], P(None, 'mp'), may hold values from -2 to 2
- bn_scale: float32 [1536], P('mp'), may hold values from 0.5 to 2
- bn_shift: float32 [1536], P('mp'), may hold values from -2.5 to 2.5
- w_pw: bfloat16 [1536, 1536], P('mp'), may hold values from -0.15625 to 0.15625
- clip_level: int32 [1536], replicated, may hold values from 6 to 39
Outputs:
- encoded: bfloat16 [4, 512, 1536], P('groups', ('ctx', 'mp')), parts along dimension 0
There are 2 independent parts, one for each index of `groups`. A program takes and returns all parts, laid end to end along the dimension named above; an argument that names none is the same for every part. Nothing has to cross between parts.
Inputs may be any that keep to these rules, and one draw needn't show every extreme that they name: frame_counts[s] frames of recording s fill slots 0 to frame_counts[s] - 1, later slots are padding; some recording fills all 512 slots.
All inputs are finite; a program needn't handle non-finite values.
Results may differ from a plain program's by a relative error of at most 0.023.
Values may be sent and summed in bfloat16 or wider, within the bound.
No kernel may reach another device: no remote copies, remote signals or barrier semaphores. Data moves between devices by JAX's collectives and lax.ppermute only.
A program may use at most 128 MiB of HBM per device.

v0:
```python
import jax
import jax.numpy as jnp
from jax import lax
from jax.sharding import PartitionSpec as P

HEAD_DIM = 64


epsilon = 1e-05
masked_score = -1e30


def with_halo(x, sides, width):
    for axis, dim in sides:
        devices, length = (lax.axis_size(axis), x.shape[dim])
        up = [(i, (i + 1) % devices) for i in range(devices - 1)]
        down = [(j, i) for i, j in up]
        last = lax.slice_in_dim(x, length - width, length, axis=dim)
        initial = lax.slice_in_dim(x, 0, width, axis=dim)
        before = lax.ppermute(last, axis, up)
        after = lax.ppermute(initial, axis, down)
        x = jnp.concatenate([before, x, after], axis=dim)
    return x


def layer_norm(values, gain):
    centre = jnp.mean(values, axis=-1, keepdims=True)
    centred = values - centre
    variance = jnp.mean(centred * centred, axis=-1, keepdims=True)
    return centred * lax.rsqrt(variance + epsilon) * gain


def gated_units(normed, w_glu):
    halves = jnp.einsum("std,gdc->gstc", normed, w_glu, preferred_element_type=jnp.float32)
    return (halves[0] * jax.nn.sigmoid(halves[1])).astype(jnp.bfloat16)


def shards(
    features,
    frame_counts,
    attn_gain,
    w_qkv,
    w_out,
    conv_gain,
    w_glu,
    kernel,
    bn_scale,
    bn_shift,
    w_pw,
    clip_level,
):
    records, frames_here, model_width = features.shape
    head_count = w_qkv.shape[2] // HEAD_DIM
    ctx_rank = lax.axis_index("ctx")
    score_scale = HEAD_DIM ** (-0.5)
    first_frame = ctx_rank * frames_here
    normed = layer_norm(features.astype(jnp.float32), attn_gain).astype(jnp.bfloat16)
    projected = jnp.einsum(
        "std,idc->istc", normed, w_qkv, preferred_element_type=jnp.float32
    ).astype(jnp.bfloat16)
    queries, key_rows, value_rows = (projected[0], projected[1], projected[2])
    query_heads = queries.reshape(records, frames_here, head_count, HEAD_DIM)
    start_max = jnp.full((records, head_count, frames_here), masked_score, jnp.float32)
    pieces = (
        lax.all_gather(key_rows, "ctx", axis=1, tiled=True),
        lax.all_gather(value_rows, "ctx", axis=1, tiled=True),
    )
    key_count = pieces[0].shape[1]
    key_heads = pieces[0].reshape(records, key_count, head_count, HEAD_DIM)
    value_heads = pieces[1].reshape(records, key_count, head_count, HEAD_DIM)
    scores = (
        jnp.einsum("sqhe,skhe->shqk", query_heads, key_heads, preferred_element_type=jnp.float32)
        * score_scale
    )
    positions = jnp.arange(key_count, dtype=jnp.int32)
    is_live = positions[None, :] < frame_counts[:, None]
    scores = jnp.where(is_live[:, None, None, :], scores, masked_score)
    new_max = jnp.maximum(start_max, jnp.max(scores, axis=-1))
    weights = jnp.exp(scores - new_max[..., None])
    new_sum = jnp.sum(weights, axis=-1)
    contrib = jnp.einsum(
        "shqk,skhe->shqe",
        weights.astype(jnp.bfloat16),
        value_heads,
        preferred_element_type=jnp.float32,
    )
    attended = (contrib / new_sum[..., None]).astype(jnp.bfloat16)
    attended = attended.transpose(0, 2, 1, 3).reshape(records, frames_here, head_count * HEAD_DIM)
    attn_part = jnp.einsum("stc,cd->std", attended, w_out, preferred_element_type=jnp.float32)
    mp_count = lax.axis_size("mp")
    mp_rank = lax.axis_index("mp")
    rows_mine = frames_here // mp_count
    row_start = mp_rank * rows_mine
    attn_sum = lax.psum(attn_part.astype(jnp.bfloat16), "mp").astype(jnp.float32)
    residual = features.astype(jnp.float32) + attn_sum
    gated_rows = gated_units(layer_norm(residual, conv_gain).astype(jnp.bfloat16), w_glu)
    residual_mine = lax.dynamic_slice_in_dim(residual, row_start, rows_mine, 1)
    frame_ids = first_frame + jnp.arange(frames_here, dtype=jnp.int32)
    frame_live = frame_ids[None, :] < frame_counts[:, None]
    gated_rows = jnp.where(frame_live[..., None], gated_rows, jnp.zeros((), jnp.bfloat16))
    rim_width = kernel.shape[0] // 2
    padded = with_halo(gated_rows, (("ctx", 1),), rim_width)
    depthwise = jnp.zeros(gated_rows.shape, jnp.float32)
    for tap_index in range(kernel.shape[0]):
        depthwise = (
            depthwise
            + padded[:, tap_index : tap_index + frames_here, :].astype(jnp.float32)
            * kernel[tap_index]
        )
    activated = jax.nn.silu(depthwise * bn_scale + bn_shift).astype(jnp.bfloat16)
    conv_part = jnp.einsum("stc,cd->std", activated, w_pw, preferred_element_type=jnp.float32)
    conv_rows = lax.psum_scatter(
        conv_part.astype(jnp.bfloat16), "mp", scatter_dimension=1, tiled=True
    ).astype(jnp.float32)
    combined = residual_mine + conv_rows
    clip_bound = clip_level.astype(jnp.float32) / 16.0
    clipped = jnp.clip(combined, -clip_bound, clip_bound)
    mine_ids = first_frame + row_start + jnp.arange(rows_mine, dtype=jnp.int32)
    mine_live = mine_ids[None, :] < frame_counts[:, None]
    return jnp.where(mine_live[..., None], clipped, 0.0).astype(jnp.bfloat16)


def solution(mesh):
    return jax.shard_map(
        shards,
        mesh=mesh,
        in_specs=(
            P("groups", "ctx", None),
            P("groups"),
            P(),
            P(None, None, "mp"),
            P("mp", None),
            P(),
            P(None, None, "mp"),
            P(None, "mp"),
            P("mp"),
            P("mp"),
            P("mp", None),
            P(),
        ),
        out_specs=P("groups", ("ctx", "mp"), None),
        check_vma=False,
    )
```

profile of v0, /device:TPU:0, one launch (start us, length us, event | category | flops | bytes accessed | tf_op | source)
XLA Modules:
  0.0 141.7 jit_solution(3153262464073058169)
XLA Ops:
  6.5 0.0 copy-start
  6.5 0.0 all-reduce.2.cloned.1.call-start
  6.5 1.5 %convert_reduce_fusion = f32[2,128]{1,0:T(2,128)S(1)} fusion(bf16[2,128,1536]{2,1,0:T(8,128)(2,1)} %param.12), kind=kLoop, calls=%fused_computation.4 | loop fusion | flops 786176 | bytes 787456 | tf_op jit(solution)/shard_map/reduce_sum | solution.py:27
  8.0 1.5 %fusion.9 = f32[2,128]{1,0:T(2,128)S(1)} fusion(bf16[2,128,1536]{2,1,0:T(8,128)(2,1)} %param.12, f32[2,128]{1,0:T(2,128)S(1)} %broadcast_multiply_fusion.1), kind=kLoop, calls=%fused_computation.16 | loop fusion | flops 1572608 | bytes 788480 | tf_op jit(solution)/shard_map/reduce_sum | solution.py:29
  9.5 0.0 copy-done
  9.5 0.0 copy-done.1
  9.5 0.0 copy-done.10
  9.5 0.8 fusion.18
  10.4 0.0 copy-start.7
  10.5 18.0 %all-gather = bf16[1,2,512,256]{3,2,0,1:T(8,128)(2,1)} all-gather(bf16[1,2,128,256]{3,2,0,1:T(8,128)(2,1)S(1)} %get-tuple-element.38), channel_id=2, replica_groups=mesh['groups'=2,'ctx'=4,'mp'=4] {'ctx'}, dimensions={2}, use_global_device_ids=true | all-gather | bytes 655360 | tf_op jit(solution)/shard_map/all_gather | solution.py:65
  28.5 2.0 %copy.18 = bf16[1,2,512,256]{2,3,1,0:T(8,128)(2,1)} copy(bf16[1,2,512,256]{3,2,0,1:T(8,128)(2,1)} %all-gather) | data formatting | bytes 1048576 | tf_op jit(solution)/shard_map/all_gather | solution.py:65
  30.5 0.1 copy.17
  30.6 0.0 copy-done.7
  30.6 0.1 iota_compare_fusion
  30.7 2.9 %fusion.6 = (f32[2,4,128]{2,1,0:T(4,128)S(1)}, f32[2,4,128,512]{3,2,1,0:T(8,128)}) fusion(pred[2,512]{1,0:T(4,128)(4,1)S(1)} %iota_compare_fusion, bf16[2,128,4,64]{1,3,2,0:T(8,128)(2,1)S(1)} %bitcast.50, bf16[2,512,4,64]{1,3,2,0:T(8,128)(2,1)} %bitcast.49), kind=kOutput, calls=%fused_computation.13 | convolution fusion | flops 68680704 | bytes 2757632 | tf_op jit(solution)/shard_map/sqhe,skhe->shqk/dot_general | solution.py:72
  33.6 17.0 %all-gather.1 = bf16[1,2,512,256]{3,2,0,1:T(8,128)(2,1)} all-gather(bf16[1,2,128,256]{3,2,0,1:T(8,128)(2,1)S(1)} %get-tuple-element.39), channel_id=3, replica_groups=mesh['groups'=2,'ctx'=4,'mp'=4] {'ctx'}, dimensions={2}, use_global_device_ids=true | all-gather | bytes 655360 | tf_op jit(solution)/shard_map/all_gather | solution.py:66
  50.6 2.1 %copy.19 = bf16[1,2,512,256]{2,3,1,0:T(8,128)(2,1)} copy(bf16[1,2,512,256]{3,2,0,1:T(8,128)(2,1)} %all-gather.1) | data formatting | bytes 1048576 | tf_op jit(solution)/shard_map/all_gather | solution.py:66
  52.6 2.3 %fusion.7 = f32[2,4,128]{2,1,0:T(4,128)S(1)} fusion(f32[2,4,128,512]{3,2,1,0:T(8,128)} %get-tuple-element.46, f32[2,4,128]{2,1,0:T(4,128)S(1)} %broadcast_maximum_fusion, pred[2,512]{1,0:T(4,128)(4,1)S(1)} %iota_compare_fusion), kind=kLoop, calls=%fused_computation.14 | loop fusion | flops 2096128 | bytes 2106368 | tf_op jit(solution)/shard_map/reduce_sum | solution.py:80
  54.9 0.0 copy-done.2
  55.0 0.0 copy-start.4
  55.0 1.8 %fusion.23 = bf16[2,128,4,64]{1,3,2,0:T(8,128)(2,1)S(1)} fusion(bf16[2,512,4,64]{1,3,2,0:T(8,128)(2,1)} %bitcast.51, f32[2,4,128,512]{3,2,1,0:T(8,128)S(1)} %copy-done.2, f32[2,4,128]{2,1,0:T(4,128)S(1)} %broadcast_maximum_fusion, pred[2,512]{1,0:T(4,128)(4,1)S(1)} %iota_compare_fusion, f32[2,128,4]{1,2,0:T(4,128)S(1)} %bitcast.53), kind=kOutput, calls=%fused_computation.55 | convolution fusion | flops 69337088 | bytes 2761728 | tf_op jit(solution)/shard_map/shqk,skhe->shqe/dot_general | solution.py:81
  56.8 0.0 copy-start.5
  56.8 0.0 copy-done.4
  56.8 1.3 convolution_convert_fusion
  58.1 0.0 all-reduce.2.cloned.1.call-update
  58.1 0.0 reduce-scatter.2.cloned.1.call-start
  58.2 0.0 copy-done.5
  58.2 0.1 slice_reduce_fusion.30
  58.3 0.1 broadcast_compare_fusion
  58.3 35.0 %all-reduce.2.cloned.1.call-done = bf16[2,128,1536]{2,1,0:T(8,128)(2,1)} async-done(((bf16[2,128,1536]{2,1,0:T(8,128)(2,1)}), bf16[2,128,1536]{2,1,0:T(8,128)(2,1)}) %all-reduce.2.cloned.1.call-update) | async-done | bytes 786448 | tf_op jit(solution)/shard_map/psum | solution.py:94
  93.3 2.6 %convert_add_fusion = (f32[2,128,1536]{2,1,0:T(8,128)}, f32[2,128]{1,0:T(2,128)S(1)}) fusion(bf16[2,128,1536]{2,1,0:T(8,128)(2,1)S(1)} %copy-done.1, bf16[2,128,1536]{2,1,0:T(8,128)(2,1)} %all-reduce.2.cloned.1.call-done), kind=kLoop, calls=%fused_computation.2 | loop fusion | flops 1572608 | bytes 3146752 | tf_op jit(solution)/shard_map/add | solution.py:95
  96.0 0.0 copy-done.3
  96.0 0.4 multiply_reduce_fusion
  96.4 0.3 copy-done.11
  96.7 1.0 fusion.12
  97.7 0.1 bitcast_select_fusion
  97.8 3.4 %collective-permute-start = (bf16[2,15,384]{2,1,0:T(8,128)(2,1)S(1)}, bf16[2,15,384]{2,1,0:T(8,128)(2,1)S(1)}, u32[]{:S(2)}, u32[]{:S(2)}) collective-permute-start(bf16[2,15,384]{2,1,0:T(8,128)(2,1)S(1)} %get-tuple-element.41), channel_id=1, source_target_pairs={{0,4},{4,8},{8,12},{1,5},{5,9},{9,13},{2,6},{6,10},{10,14},{3,7},{... | collective-permute-start | bytes 69128 | tf_op jit(solution)/shard_map/ppermute | solution.py:20
  101.2 1.3 collective-permute-start.1
  102.5 0.1 slice_reduce_fusion.29
  102.6 0.1 collective-permute-done
  102.7 4.2 %collective-permute-done.1 = bf16[2,15,384]{2,1,0:T(8,128)(2,1)S(1)} collective-permute-done((bf16[2,15,384]{2,1,0:T(8,128)(2,1)S(1)}, bf16[2,15,384]{2,1,0:T(8,128)(2,1)S(1)}, u32[]{:S(2)}, u32[]{:S(2)}) %collective-permute-start.1) | collective-permute-done | bytes 23072 | tf_op jit(solution)/shard_map/ppermute | solution.py:21
  106.9 0.0 copy-done.12
  106.9 0.0 copy-start.6
  107.0 3.5 %convolution_convert_fusion.1 = bf16[2,128,1536]{2,1,0:T(8,128)(2,1)} fusion(bf16[384,1536]{1,0:T(8,128)(2,1)S(1)} %copy-done.9, bf16[2,128,384]{2,1,0:T(8,128)(2,1)S(1)} %bitcast_select_fusion, bf16[2,15,384]{2,1,0:T(8,128)(2,1)S(1)} %collective-permute-done.1, bf16[2,15,384]{2,1,0:T(8,128)(2,1)S(1)} %collective-permute-done, f32[384]{0:T(512)S(1)} %copy-done.12, ...), kind=kOutput, calls=%fused_computation.1 | convolution fusion | flops 320962560 | bytes 2259456 | tf_op jit(solution)/shard_map/stc,cd->std/dot_general | solution.py:111
  110.5 0.0 reduce-scatter.2.cloned.1.call-update
  110.5 0.1 broadcast_compare_fusion.1
  110.6 22.4 %reduce-scatter.2.cloned.1.call-done = bf16[2,32,1536]{2,1,0:T(8,128)(2,1)} async-done(((bf16[2,128,1536]{2,1,0:T(8,128)(2,1)}), bf16[2,32,1536]{2,1,0:T(8,128)(2,1)}) %reduce-scatter.2.cloned.1.call-update) | async-done | bytes 196624 | tf_op jit(solution)/shard_map/reduce_scatter | solution.py:112
  133.0 1.9 %select_convert_fusion = bf16[2,32,1536]{2,1,0:T(8,128)(2,1)} fusion(bf16[2,32,1536]{2,1,0:T(8,128)(2,1)} %reduce-scatter.2.cloned.1.call-done, f32[2,128,1536]{2,1,0:T(8,128)} %get-tuple-element.36, s32[]{:T(128)S(6)} %select_n.16, bf16[1536]{0:T(1024)(128)(2,1)S(1)} %get-tuple-element.44, bf16[1536]{0:T(1024)(128)(2,1)S(1)} %get-tuple-element.43, ...), kind=kLoop, calls=%fused_computation.74 | loop fusion | flops 786432 | bytes 792644 | tf_op jit(solution)/shard_map/convert_element_type | solution.py:120
  (23 shorter events, 0.1 us)
Async XLA Ops:
  6.5 3.0 %copy-start = (bf16[3,1536,256]{2,1,0:T(8,128)(2,1)S(1)}, bf16[3,1536,256]{2,1,0:T(8,128)(2,1)}, u32[]{:S(2)}) copy-start(bf16[3,1536,256]{2,1,0:T(8,128)(2,1)} %param.15) | copy-start | bytes 7077892
  6.5 3.0 %copy-start.1 = (bf16[2,128,1536]{2,1,0:T(8,128)(2,1)S(1)}, bf16[2,128,1536]{2,1,0:T(8,128)(2,1)}, u32[]{:S(2)}) copy-start(bf16[2,128,1536]{2,1,0:T(8,128)(2,1)} %param.12) | copy-start | bytes 2359300
  6.5 3.0 %copy-start.10 = (f32[1536]{0:T(1024)S(1)}, f32[1536]{0:T(1024)}, u32[]{:S(2)}) copy-start(f32[1536]{0:T(1024)} %param.14) | copy-start | bytes 18436
  6.5 86.8 %all-reduce.2.cloned.1.call-start = ((), (), s32[]{:S(2)}) async-start(), calls=%async_computation.1 | async-start | bytes 1572864 | tf_op jit(solution)/shard_map/psum | solution.py:94
  10.4 20.2 %copy-start.7 = (s32[2]{0:T(128)S(1)}, s32[2]{0:T(128)}, u32[]{:S(2)}) copy-start(s32[2]{0:T(128)} %param.13) | copy-start | bytes 28
  52.6 2.3 %copy-start.2 = (f32[2,4,128,512]{3,2,1,0:T(8,128)S(1)}, f32[2,4,128,512]{3,2,1,0:T(8,128)}, u32[]{:S(2)}) copy-start(f32[2,4,128,512]{3,2,1,0:T(8,128)} %get-tuple-element.46) | copy-start | bytes 6291460
  55.0 1.8 %copy-start.4 = (bf16[256,1536]{1,0:T(8,128)(2,1)S(1)}, bf16[256,1536]{1,0:T(8,128)(2,1)}, u32[]{:S(2)}) copy-start(bf16[256,1536]{1,0:T(8,128)(2,1)} %param.16) | copy-start | bytes 2359300
  56.8 1.4 copy-start.5
  58.1 74.9 %reduce-scatter.2.cloned.1.call-start = ((), (), s32[]{:S(2)}) async-start(), calls=%async_computation.2 | async-start | bytes 983040 | tf_op jit(solution)/shard_map/reduce_scatter | solution.py:112
  93.3 2.7 %copy-start.3 = (bf16[2,128,1536]{2,1,0:T(8,128)(2,1)S(1)}, bf16[2,128,1536]{2,1,0:T(8,128)(2,1)}, u32[]{:S(2)}) copy-start(bf16[2,128,1536]{2,1,0:T(8,128)(2,1)} %all-reduce.2.cloned.1.call-done) | copy-start | bytes 2359300
  93.3 3.1 %copy-start.8 = (bf16[2,1536,384]{2,1,0:T(8,128)(2,1)S(1)}, bf16[2,1536,384]{2,1,0:T(8,128)(2,1)}, u32[]{:S(2)}) copy-start(bf16[2,1536,384]{2,1,0:T(8,128)(2,1)} %param.18) | copy-start | bytes 7077892
  96.0 0.7 copy-start.11
  96.7 10.2 %copy-start.9 = (bf16[384,1536]{1,0:T(8,128)(2,1)S(1)}, bf16[384,1536]{1,0:T(8,128)(2,1)}, u32[]{:S(2)}) copy-start(bf16[384,1536]{1,0:T(8,128)(2,1)} %param.22) | copy-start | bytes 3538948
  96.7 10.2 %copy-start.12 = (f32[384]{0:T(512)S(1)}, f32[384]{0:T(512)}, u32[]{:S(2)}) copy-start(f32[384]{0:T(512)} %param.21) | copy-start | bytes 4612
  96.7 10.2 %copy-start.13 = (f32[384]{0:T(512)S(1)}, f32[384]{0:T(512)}, u32[]{:S(2)}) copy-start(f32[384]{0:T(512)} %param.20) | copy-start | bytes 4612
  97.8 4.9 %collective-permute-start = (bf16[2,15,384]{2,1,0:T(8,128)(2,1)S(1)}, bf16[2,15,384]{2,1,0:T(8,128)(2,1)S(1)}, u32[]{:S(2)}, u32[]{:S(2)}) collective-permute-start(bf16[2,15,384]{2,1,0:T(8,128)(2,1)S(1)} %get-tuple-element.41), channel_id=1, source_target_pairs={{0,4},{4,8},{8,12},{1,5},{5,9},{9,13},{2,6},{6,10},{10,14},{3,7},{... | collective-permute-start | bytes 69128 | tf_op jit(solution)/shard_map/ppermute | solution.py:20
  101.2 5.7 %collective-permute-start.1 = (bf16[2,15,384]{2,1,0:T(8,128)(2,1)S(1)}, bf16[2,15,384]{2,1,0:T(8,128)(2,1)S(1)}, u32[]{:S(2)}, u32[]{:S(2)}) collective-permute-start(bf16[2,15,384]{2,1,0:T(8,128)(2,1)S(1)} %get-tuple-element.42), channel_id=1, source_target_pairs={{4,0},{8,4},{12,8},{5,1},{9,5},{13,9},{6,2},{10,6},{14,10},{7,3},{... | collective-permute-start | bytes 69128 | tf_op jit(solution)/shard_map/ppermute | solution.py:21
  106.9 3.7 %copy-start.6 = (s32[1536]{0:T(1024)S(1)}, s32[1536]{0:T(1024)}, u32[]{:S(2)}) copy-start(s32[1536]{0:T(1024)} %param.23) | copy-start | bytes 18436
Sparse Core Ops, SparseCore 0:
  58.2 35.0 all-reduce.1
  110.6 22.3 reduce-scatter.1
where the time goes:
time: 142 us
  waiting for transfers between devices  61.8 us (44%)
  blocking collectives  35 us (25%)
  between operations  13.6 us (10%)
  matrix products  11.3 us (8%)
  other arithmetic  10.6 us (7%)
  local copies, waits for them, and re-layouts  4.75 us (3%)
  starting transfers between devices  4.72 us (3%)
    psum x1, waiting for transfers between devices, shards(): lax.psum(attn_part.astype(jnp.bfloat16), 'mp').astype(jnp.float32)  35 us
    reduce_scatter x1, waiting for transfers between devices, shards(): lax.psum_scatter(conv_part.astype(jnp.bfloat16), 'mp', scatter_dimension=...  22.4 us
    all_gather x1, blocking collectives, shards(): lax.all_gather(key_rows, 'ctx', axis=1, tiled=True)  18 us
    all_gather x1, blocking collectives, shards(): lax.all_gather(value_rows, 'ctx', axis=1, tiled=True)  17 us
    ppermute x1, waiting for transfers between devices, with_halo(): after = lax.ppermute(initial, axis, down)  4.22 us
    dot_general x1, matrix products, shards(): jnp.einsum('stc,cd->std', activated, w_pw, preferred_element_type=jnp.flo...  3.55 us
    ppermute x1, starting transfers between devices, with_halo(): before = lax.ppermute(last, axis, up)  3.39 us
    dot_general x1, matrix products, shards(): jnp.einsum('sqhe,skhe->shqk', query_heads, key_heads, preferred_element_t...  2.88 us
  transfers between devices with their start and end apart: 4, of which 4 were waited for; matrix products, arithmetic and copies ran while one was open for 0% of the time, Pallas kernels for 0%

commit v1 on v0

--- a/solution.py
+++ b/solution.py
@@ -35,6 +35,63 @@
     return (halves[0] * jax.nn.sigmoid(halves[1])).astype(jnp.bfloat16)
 
 
+def xor_pairs(count, mask):
+    return [(i, i ^ mask) for i in range(count)]
+
+
+def bit_count(count):
+    bits = count.bit_length() - 1
+    assert (1 << bits) == count
+    return bits
+
+
+def reduce_scatter_rows(x, axis, dim):
+    count, rank = lax.axis_size(axis), lax.axis_index(axis)
+    bits = bit_count(count)
+    shape = x.shape
+    block = shape[dim] // count
+    acc = x.reshape(shape[:dim] + (2,) * bits + (block,) + shape[dim + 1 :])
+    for b in range(bits):
+        bit_axis = dim + bits - 1 - b
+        mine = (rank >> b) & 1
+        keep = lax.dynamic_index_in_dim(acc, mine, bit_axis, keepdims=False)
+        send = lax.dynamic_index_in_dim(acc, 1 - mine, bit_axis, keepdims=False)
+        got = lax.ppermute(send.astype(jnp.bfloat16), axis, xor_pairs(count, 1 << b))
+        acc = keep.astype(jnp.float32) + got.astype(jnp.float32)
+    return acc
+
+
+def all_gather_rows(x, axis, dim):
+    count, rank = lax.axis_size(axis), lax.axis_index(axis)
+    bits = bit_count(count)
+    shape = x.shape
+    acc = x
+    for k, b in enumerate(reversed(range(bits))):
+        mine = ((rank >> b) & 1) == 0
+        got = lax.ppermute(acc, axis, xor_pairs(count, 1 << b))
+        low = jnp.where(mine, acc, got)
+        high = jnp.where(mine, got, acc)
+        acc = jnp.stack([low, high], axis=dim + k)
+    return acc.reshape(shape[:dim] + (shape[dim] * count,) + shape[dim + 1 :])
+
+
+def ring_gather(x, axis):
+    count = lax.axis_size(axis)
+    right = [(i, (i + 1) % count) for i in range(count)]
+    left = [(i, (i - 1) % count) for i in range(count)]
+    right_steps = count // 2
+    left_steps = count - 1 - right_steps
+    from_left, from_right = [], []
+    going_right, going_left = x, x
+    for step in range(right_steps):
+        going_right = lax.ppermute(going_right, axis, right)
+        from_left.append(going_right)
+        if step < left_steps:
+            going_left = lax.ppermute(going_left, axis, left)
+            from_right.append(going_left)
+    return jnp.stack([x] + from_right + from_left[::-1], axis=0)
+
+
 def shards(
     features,
     frame_counts,
@@ -52,49 +109,48 @@
     records, frames_here, model_width = features.shape
     head_count = w_qkv.shape[2] // HEAD_DIM
     ctx_rank = lax.axis_index("ctx")
+    ctx_count = lax.axis_size("ctx")
     score_scale = HEAD_DIM ** (-0.5)
     first_frame = ctx_rank * frames_here
     normed = layer_norm(features.astype(jnp.float32), attn_gain).astype(jnp.bfloat16)
     projected = jnp.einsum(
         "std,idc->istc", normed, w_qkv, preferred_element_type=jnp.float32
     ).astype(jnp.bfloat16)
-    queries, key_rows, value_rows = (projected[0], projected[1], projected[2])
+    queries = projected[0]
     query_heads = queries.reshape(records, frames_here, head_count, HEAD_DIM)
-    start_max = jnp.full((records, head_count, frames_here), masked_score, jnp.float32)
-    pieces = (
-        lax.all_gather(key_rows, "ctx", axis=1, tiled=True),
-        lax.all_gather(value_rows, "ctx", axis=1, tiled=True),
-    )
-    key_count = pieces[0].shape[1]
-    key_heads = pieces[0].reshape(records, key_count, head_count, HEAD_DIM)
-    value_heads = pieces[1].reshape(records, key_count, head_count, HEAD_DIM)
+    kv_all = ring_gather(projected[1:], "ctx")
+    key_heads = kv_all[:, 0].reshape(ctx_count, records, frames_here, head_count, HEAD_DIM)
+    value_heads = kv_all[:, 1].reshape(ctx_count, records, frames_here, head_count, HEAD_DIM)
     scores = (
-        jnp.einsum("sqhe,skhe->shqk", query_heads, key_heads, preferred_element_type=jnp.float32)
+        jnp.einsum("sqhe,cskhe->shqck", query_heads, key_heads, preferred_element_type=jnp.float32)
         * score_scale
     )
-    positions = jnp.arange(key_count, dtype=jnp.int32)
-    is_live = positions[None, :] < frame_counts[:, None]
-    scores = jnp.where(is_live[:, None, None, :], scores, masked_score)
-    new_max = jnp.maximum(start_max, jnp.max(scores, axis=-1))
-    weights = jnp.exp(scores - new_max[..., None])
-    new_sum = jnp.sum(weights, axis=-1)
+    block_rank = (ctx_rank + jnp.arange(ctx_count, dtype=jnp.int32)) % ctx_count
+    positions = block_rank[:, None] * frames_here + jnp.arange(frames_here, dtype=jnp.int32)
+    is_live = positions[None] < frame_counts[:, None, None]
+    scores = jnp.where(is_live[:, None, None], scores, masked_score)
+    row_max = jnp.max(scores, axis=(-2, -1), keepdims=True)
+    weights = jnp.exp(scores - row_max)
+    row_sum = jnp.sum(weights, axis=(-2, -1))
     contrib = jnp.einsum(
-        "shqk,skhe->shqe",
+        "shqck,cskhe->shqe",
         weights.astype(jnp.bfloat16),
         value_heads,
         preferred_element_type=jnp.float32,
     )
-    attended = (contrib / new_sum[..., None]).astype(jnp.bfloat16)
+    attended = (contrib / row_sum[..., None]).astype(jnp.bfloat16)
     attended = attended.transpose(0, 2, 1, 3).reshape(records, frames_here, head_count * HEAD_DIM)
     attn_part = jnp.einsum("stc,cd->std", attended, w_out, preferred_element_type=jnp.float32)
     mp_count = lax.axis_size("mp")
     mp_rank = lax.axis_index("mp")
     rows_mine = frames_here // mp_count
     row_start = mp_rank * rows_mine
-    attn_sum = lax.psum(attn_part.astype(jnp.bfloat16), "mp").astype(jnp.float32)
-    residual = features.astype(jnp.float32) + attn_sum
-    gated_rows = gated_units(layer_norm(residual, conv_gain).astype(jnp.bfloat16), w_glu)
-    residual_mine = lax.dynamic_slice_in_dim(residual, row_start, rows_mine, 1)
+    attn_mine = reduce_scatter_rows(attn_part.astype(jnp.bfloat16), "mp", 1)
+    features_mine = lax.dynamic_slice_in_dim(features, row_start, rows_mine, 1)
+    residual_mine = features_mine.astype(jnp.float32) + attn_mine
+    normed_mine = layer_norm(residual_mine, conv_gain).astype(jnp.bfloat16)
+    normed_conv = all_gather_rows(normed_mine, "mp", 1)
+    gated_rows = gated_units(normed_conv, w_glu)
     frame_ids = first_frame + jnp.arange(frames_here, dtype=jnp.int32)
     frame_live = frame_ids[None, :] < frame_counts[:, None]
     gated_rows = jnp.where(frame_live[..., None], gated_rows, jnp.zeros((), jnp.bfloat16))
@@ -109,9 +165,7 @@
         )
     activated = jax.nn.silu(depthwise * bn_scale + bn_shift).astype(jnp.bfloat16)
     conv_part = jnp.einsum("stc,cd->std", activated, w_pw, preferred_element_type=jnp.float32)
-    conv_rows = lax.psum_scatter(
-        conv_part.astype(jnp.bfloat16), "mp", scatter_dimension=1, tiled=True
-    ).astype(jnp.float32)
+    conv_rows = reduce_scatter_rows(conv_part.astype(jnp.bfloat16), "mp", 1)
     combined = residual_mine + conv_rows
     clip_bound = clip_level.astype(jnp.float32) / 16.0
     clipped = jnp.clip(combined, -clip_bound, clip_bound)

time: 142 us -> 79.3 us (0.56)
  blocking collectives: 35 us -> 0 us
  waiting for transfers between devices: 61.8 us -> 39.9 us
  between operations: 13.6 us -> 0.4 us
  starting transfers between devices: 4.72 us -> 13 us
  matrix products: 11.3 us -> 7.34 us
  local copies, waits for them, and re-layouts: 4.75 us -> 6.9 us
    ppermute x0 -> x9, waiting for transfers between devices: none -> 36.5 us  [the longest x4 14.1 us: reduce_scatter_rows(): lax.ppermute(send.astype(jnp.bfloat16), axis, xor_pairs(count, 1 << b))]
    psum x1 -> x0, waiting for transfers between devices: 35 us -> none  [shards(): lax.psum(attn_part.astype(jnp.bfloat16), 'mp').astype(jnp.float32)]
    all_gather x2 -> x0, blocking collectives: 35 us -> none  [the longest x1 18 us: shards(): lax.all_gather(key_rows, 'ctx', axis=1, tiled=True)]
    reduce_scatter x1 -> x0, waiting for transfers between devices: 22.4 us -> none  [shards(): lax.psum_scatter(conv_part.astype(jnp.bfloat16), 'mp', scatter_dimension=...]
    ppermute x0 -> x9, starting transfers between devices: none -> 10.1 us  [the longest x4 3.25 us: reduce_scatter_rows(): lax.ppermute(send.astype(jnp.bfloat16), axis, xor_pairs(count, 1 << b))]
    all_gather x2 -> x0, local copies, waits for them, and re-layouts: 4.1 us -> none  [the longest x1 2.05 us: shards(): lax.all_gather(value_rows, 'ctx', axis=1, tiled=True)]
    dot_general x2, matrix products: 4.68 us -> 1.45 us  [the longest x1 0.74 us: shards(): jnp.einsum('shqck,cskhe->shqe', weights.astype(jnp.bfloat16), value_heads...]
    slice x2 -> x5, local copies, waits for them, and re-layouts: 0.15 us -> 3.32 us  [the longest x2 1.88 us: shards(): kv_all[:, 1].reshape(ctx_count, records, frames_here, head_count, HEAD_DIM)]
  transfers between devices with their start and end apart: 4 -> 11, of which waited for: 4 -> 10; matrix products, arithmetic and copies ran while one was open for 0% -> 4% of each run, Pallas kernels for 0% -> 0%
where the time goes in v1:
time: 79.3 us; the launch traced here: 78.7 us
  waiting for transfers between devices  39.9 us (50%)
  starting transfers between devices  13 us (16%)
  other arithmetic  11.2 us (14%)
  matrix products  7.34 us (9%)
  local copies, waits for them, and re-layouts  6.9 us (9%)
    ppermute x4, waiting for transfers between devices, reduce_scatter_rows(): lax.ppermute(send.astype(jnp.bfloat16), axis, xor_pairs(count, 1 << b))  14.1 us
    ppermute x2, waiting for transfers between devices, ring_gather(): going_right = lax.ppermute(going_right, axis, right)  13.2 us
    ppermute x2, waiting for transfers between devices, all_gather_rows(): got = lax.ppermute(acc, axis, xor_pairs(count, 1 << b))  5.08 us
    ppermute x1, waiting for transfers between devices, ring_gather(): going_left = lax.ppermute(going_left, axis, left)  4.09 us
    ppermute x1, waiting for transfers between devices, with_halo(): after = lax.ppermute(initial, axis, down)  3.37 us
    ppermute x4, starting transfers between devices, reduce_scatter_rows(): lax.ppermute(send.astype(jnp.bfloat16), axis, xor_pairs(count, 1 << b))  3.25 us
    ppermute x2, starting transfers between devices, ring_gather(): going_right = lax.ppermute(going_right, axis, right)  3.08 us
    dot_general x1, matrix products, shards(): jnp.einsum('stc,cd->std', activated, w_pw, preferred_element_type=jnp.flo...  2.74 us
  transfers between devices with their start and end apart: 11, of which 10 were waited for; matrix products, arithmetic and copies ran while one was open for 4% of the time, Pallas kernels for 0%

profile of v1, /device:TPU:0, one launch (start us, length us, event | category | flops | bytes accessed | tf_op | source)
XLA Modules:
  0.0 78.7 jit_solution(15436076247640991415)
XLA Ops:
  0.0 1.5 %convert_reduce_fusion = f32[2,128]{1,0:T(2,128)S(1)} fusion(bf16[2,128,1536]{2,1,0:T(8,128)(2,1)} %param.12), kind=kLoop, calls=%fused_computation.9 | loop fusion | flops 786176 | bytes 787456 | tf_op jit(solution)/shard_map/reduce_sum | solution.py:27
  1.5 1.5 %fusion.9 = f32[2,128]{1,0:T(2,128)S(1)} fusion(bf16[2,128,1536]{2,1,0:T(8,128)(2,1)} %param.12, f32[2,128]{1,0:T(2,128)S(1)} %broadcast_multiply_fusion.1), kind=kLoop, calls=%fused_computation.15 | loop fusion | flops 1572608 | bytes 788480 | tf_op jit(solution)/shard_map/reduce_sum | solution.py:29
  3.0 2.0 %fusion.18 = bf16[3,2,128,256]{3,2,0,1:T(8,128)(2,1)S(1)} fusion(bf16[3,1536,256]{2,1,0:T(8,128)(2,1)S(1)} %copy-done, bf16[2,128,1536]{2,1,0:T(8,128)(2,1)} %param.12, f32[1536]{0:T(1024)} %param.14, f32[2,128]{1,0:T(2,128)S(1)} %add_rsqrt_fusion.1, f32[2,128]{1,0:T(2,128)S(1)} %broadcast_multiply_fusion.1), kind=kOutput, calls=%fused_computation.20 | convolution fusion | flops 606142464 | bytes 3547136 | tf_op jit(solution)/shard_map/std,idc->istc/dot_general | solution.py:116
  5.0 3.1 %collective-permute-start.1 = (bf16[2,2,128,256]{3,2,0,1:T(8,128)(2,1)S(1)}, bf16[2,2,128,256]{3,2,0,1:T(8,128)(2,1)}, u32[]{:S(2)}, u32[]{:S(2)}) collective-permute-start(bf16[2,2,128,256]{3,2,0,1:T(8,128)(2,1)S(1)} %get-tuple-element.49), channel_id=1, source_target_pairs={{0,4},{4,8},{8,12},{12,0},{1,5},{5,9},{9,13},{13,1},{2,6},{6,10},{... | collective-permute-start | bytes 786440 | tf_op jit(solution)/shard_map/ppermute | solution.py:87
  8.1 2.1 %collective-permute-start = (bf16[2,2,128,256]{3,2,0,1:T(8,128)(2,1)S(1)}, bf16[2,2,128,256]{3,2,0,1:T(8,128)(2,1)}, u32[]{:S(2)}, u32[]{:S(2)}) collective-permute-start(bf16[2,2,128,256]{3,2,0,1:T(8,128)(2,1)S(1)} %get-tuple-element.49), channel_id=1, source_target_pairs={{0,12},{4,0},{8,4},{12,8},{1,13},{5,1},{9,5},{13,9},{2,14},{6,2},{... | collective-permute-start | bytes 786440 | tf_op jit(solution)/shard_map/ppermute | solution.py:90
  10.2 7.2 %collective-permute-done.1 = bf16[2,2,128,256]{3,2,0,1:T(8,128)(2,1)} collective-permute-done((bf16[2,2,128,256]{3,2,0,1:T(8,128)(2,1)S(1)}, bf16[2,2,128,256]{3,2,0,1:T(8,128)(2,1)}, u32[]{:S(2)}, u32[]{:S(2)}) %collective-permute-start.1) | collective-permute-done | bytes 262176 | tf_op jit(solution)/shard_map/ppermute | solution.py:87
  17.5 0.1 copy.23
  17.7 0.1 broadcast_compare_fusion
  17.7 4.1 %collective-permute-done = bf16[2,2,128,256]{3,2,0,1:T(8,128)(2,1)} collective-permute-done((bf16[2,2,128,256]{3,2,0,1:T(8,128)(2,1)S(1)}, bf16[2,2,128,256]{3,2,0,1:T(8,128)(2,1)}, u32[]{:S(2)}, u32[]{:S(2)}) %collective-permute-start) | collective-permute-done | bytes 262176 | tf_op jit(solution)/shard_map/ppermute | solution.py:90
  21.8 6.0 %collective-permute-done.2 = bf16[2,2,128,256]{3,2,0,1:T(8,128)(2,1)} collective-permute-done((bf16[2,2,128,256]{3,2,0,1:T(8,128)(2,1)}, bf16[2,2,128,256]{3,2,0,1:T(8,128)(2,1)}, u32[]{:S(2)}, u32[]{:S(2)}) %collective-permute-start.2) | collective-permute-done | bytes 262176 | tf_op jit(solution)/shard_map/ppermute | solution.py:87
  27.8 1.2 %pad_maximum_fusion = bf16[4,2,2,128,256]{4,3,1,2,0:T(8,128)(2,1)S(1)} fusion(bf16[1,2,2,128,256]{4,3,1,2,0:T(8,128)(2,1)} %bitcast.10, bf16[1,2,2,128,256]{4,3,1,2,0:T(8,128)(2,1)} %bitcast.9, bf16[1,2,2,128,256]{4,3,1,2,0:T(8,128)(2,1)} %bitcast.8, bf16[1,2,2,128,256]{4,3,1,2,0:T(8,128)(2,1)S(1)} %get-tuple-element.48), kind=kLoop, calls=%fused_computation.53 | loop fusion | flops 1572864 | bytes 2097152 | tf_op jit(solution)/shard_map/stack | solution.py:92
  29.1 0.9 %fusion.88 = (bf16[4,1,2,128,256]{4,3,1,2,0:T(8,128)(2,1)S(1)}, bf16[4,1,2,128,256]{4,3,1,2,0:T(8,128)(2,1)}) fusion(bf16[4,2,2,128,256]{4,3,1,2,0:T(8,128)(2,1)S(1)} %pad_maximum_fusion), kind=kLoop, calls=%fused_computation.208 | loop fusion | bytes 2097152 | tf_op jit(solution)/shard_map/slice | solution.py:123
  29.9 1.3 %copy.24 = bf16[4,1,2,128,256]{3,4,2,0,1:T(8,128)(2,1)S(1)} copy(bf16[4,1,2,128,256]{4,3,1,2,0:T(8,128)(2,1)} %get-tuple-element.39) | data formatting | bytes 1048576 | tf_op jit(solution)/shard_map/slice | solution.py:122
  31.3 1.0 %copy.26 = bf16[4,1,2,128,256]{3,4,2,0,1:T(8,128)(2,1)} copy(bf16[4,1,2,128,256]{4,3,1,2,0:T(8,128)(2,1)S(1)} %get-tuple-element.38) | data formatting | bytes 1048576 | tf_op jit(solution)/shard_map/slice | solution.py:123
  32.3 0.7 fusion.6
  33.0 0.5 fusion.7
  33.5 0.7 fusion.23
  34.3 0.4 copy-done.1
  34.6 0.4 convolution_convert_fusion
  35.2 1.8 %collective-permute-done.3 = bf16[2,2,32,1536]{3,2,0,1:T(8,128)(2,1)} collective-permute-done((bf16[2,2,32,1536]{3,2,0,1:T(8,128)(2,1)S(1)}, bf16[2,2,32,1536]{3,2,0,1:T(8,128)(2,1)}, u32[]{:S(2)}, u32[]{:S(2)}) %collective-permute-start.3) | collective-permute-done | bytes 393248 | tf_op jit(solution)/shard_map/ppermute | solution.py:59
  37.1 1.1 %convert_add_fusion.1 = f32[2,2,32,1536]{3,2,0,1:T(8,128)S(1)} fusion(bf16[2,2,32,1536]{3,2,0,1:T(8,128)(2,1)} %collective-permute-done.3, bf16[2,2,1,32,1536]{4,3,2,1,0:T(8,128)(2,1)S(1)} %get-tuple-element.44), kind=kLoop, calls=%fused_computation.61 | loop fusion | flops 589824 | bytes 1572864 | tf_op jit(solution)/shard_map/add | solution.py:60
  38.2 1.6 %collective-permute-start.4 = (bf16[2,32,1536]{2,1,0:T(8,128)(2,1)S(1)}, bf16[2,32,1536]{2,1,0:T(8,128)(2,1)}, u32[]{:S(2)}, u32[]{:S(2)}) collective-permute-start(bf16[2,32,1536]{2,1,0:T(8,128)(2,1)S(1)} %fusion.49), channel_id=1, source_target_pairs={{0,2},{1,3},{2,0},{3,1},{4,6},{5,7},{6,4},{7,5},{8,10},{9,11},{10,... | collective-permute-start | bytes 589832 | tf_op jit(solution)/shard_map/ppermute | solution.py:59
  39.8 5.6 %collective-permute-done.4 = bf16[2,32,1536]{2,1,0:T(8,128)(2,1)} collective-permute-done((bf16[2,32,1536]{2,1,0:T(8,128)(2,1)S(1)}, bf16[2,32,1536]{2,1,0:T(8,128)(2,1)}, u32[]{:S(2)}, u32[]{:S(2)}) %collective-permute-start.4) | collective-permute-done | bytes 196640 | tf_op jit(solution)/shard_map/ppermute | solution.py:59
  45.3 1.2 %fusion.86 = (f32[2,32]{1,0:T(2,128)S(1)}, f32[2,32,1536]{2,1,0:T(8,128)S(1)}) fusion(bf16[2,32,1536]{2,1,0:T(8,128)(2,1)} %collective-permute-done.4, f32[2,2,32,1536]{3,2,0,1:T(8,128)S(1)} %convert_add_fusion.1, s32[]{:T(128)S(6)} %select_n.73, bf16[2,128,1536]{2,1,0:T(8,128)(2,1)} %param.12, s32[]{:T(128)S(6)} %select_n.68), kind=kLoop, calls=%fused_computation.207 | loop fusion | flops 491456 | bytes 1179912 | tf_op jit(solution)/shard_map/reduce_sum | solution.py:27
  46.5 0.2 multiply_reduce_fusion
  46.7 0.1 multiply_convert_fusion.1
  46.8 1.6 %collective-permute-start.5 = (bf16[2,32,1536]{2,1,0:T(8,128)(2,1)S(1)}, bf16[2,32,1536]{2,1,0:T(8,128)(2,1)S(1)}, u32[]{:S(2)}, u32[]{:S(2)}) collective-permute-start(bf16[2,32,1536]{2,1,0:T(8,128)(2,1)S(1)} %multiply_convert_fusion.1), channel_id=1, source_target_pairs={{0,2},{1,3},{2,0},{3,1},{4,6},{5,7},{6,4},{7,5},{8,10},{9,11},{10,... | collective-permute-start | bytes 589832 | tf_op jit(solution)/shard_map/ppermute | solution.py:71
  48.4 4.6 %collective-permute-done.5 = bf16[2,32,1536]{2,1,0:T(8,128)(2,1)S(1)} collective-permute-done((bf16[2,32,1536]{2,1,0:T(8,128)(2,1)S(1)}, bf16[2,32,1536]{2,1,0:T(8,128)(2,1)S(1)}, u32[]{:S(2)}, u32[]{:S(2)}) %collective-permute-start.5) | collective-permute-done | bytes 196640 | tf_op jit(solution)/shard_map/ppermute | solution.py:71
  53.0 0.2 select_bitcast_fusion.3
  53.4 1.3 %slice_reduce_fusion.30 = (f32[384]{0:T(512)S(1)}, f32[384]{0:T(512)S(1)}, f32[384]{0:T(512)S(1)}, f32[384]{0:T(512)S(1)}, f32[384]{0:T(512)S(1)}, /*index=5*/f3...) fusion(f32[31,384]{1,0:T(8,128)} %param.19), kind=kLoop, calls=%fused_computation.190 | loop fusion | bytes 58368 | tf_op jit(solution)/shard_map/slice | solution.py:164
  54.6 0.1 broadcast_compare_fusion.1
  54.7 0.5 collective-permute-done.6
  55.2 1.3 %select_bitcast_fusion.1 = (bf16[2,2,1,32,1536]{4,3,0,1,2:T(8,128)(2,1)S(1)}, bf16[2,2,1,32,1536]{4,3,0,1,2:T(8,128)(2,1)S(1)}) fusion(bf16[2,2,32,1536]{3,2,0,1:T(8,128)(2,1)} %collective-permute-done.6, pred[]{:T(512)S(6)} %eq.8, bf16[2,1,32,1536]{3,2,0,1:T(8,128)(2,1)S(1)} %get-tuple-element.47, bf16[2,1,32,1536]{3,2,0,1:T(8,128)(2,1)S(1)} %get-tuple-element.46), kind=kLoop, calls=%fused_computation.90 | loop fusion | flops 589824 | bytes 1572865 | tf_op jit(solution)/shard_map/stack | solution.py:74
  56.5 0.1 pad_maximum_fusion.1
  56.6 0.8 fusion.12
  57.4 0.1 bitcast_select_fusion
  57.6 1.6 %collective-permute-start.7 = (bf16[2,15,384]{2,1,0:T(8,128)(2,1)S(1)}, bf16[2,15,384]{2,1,0:T(8,128)(2,1)S(1)}, u32[]{:S(2)}, u32[]{:S(2)}) collective-permute-start(bf16[2,15,384]{2,1,0:T(8,128)(2,1)S(1)} %get-tuple-element.50), channel_id=1, source_target_pairs={{0,4},{4,8},{8,12},{1,5},{5,9},{9,13},{2,6},{6,10},{10,14},{3,7},{... | collective-permute-start | bytes 69128 | tf_op jit(solution)/shard_map/ppermute | solution.py:20
  59.2 1.3 %collective-permute-start.8 = (bf16[2,15,384]{2,1,0:T(8,128)(2,1)S(1)}, bf16[2,15,384]{2,1,0:T(8,128)(2,1)S(1)}, u32[]{:S(2)}, u32[]{:S(2)}) collective-permute-start(bf16[2,15,384]{2,1,0:T(8,128)(2,1)S(1)} %get-tuple-element.51), channel_id=1, source_target_pairs={{4,0},{8,4},{12,8},{5,1},{9,5},{13,9},{6,2},{10,6},{14,10},{7,3},{... | collective-permute-start | bytes 69128 | tf_op jit(solution)/shard_map/ppermute | solution.py:21
  60.5 1.0 %slice_reduce_fusion.29 = (f32[384]{0:T(512)S(1)}, f32[384]{0:T(512)S(1)}, f32[384]{0:T(512)S(1)}, f32[384]{0:T(512)S(1)}, f32[384]{0:T(512)S(1)}, /*index=5*/f3...) fusion(f32[31,384]{1,0:T(8,128)} %param.19), kind=kLoop, calls=%fused_computation.189 | loop fusion | bytes 36864 | tf_op jit(solution)/shard_map/slice | solution.py:164
  61.6 3.4 %collective-permute-done.8 = bf16[2,15,384]{2,1,0:T(8,128)(2,1)S(1)} collective-permute-done((bf16[2,15,384]{2,1,0:T(8,128)(2,1)S(1)}, bf16[2,15,384]{2,1,0:T(8,128)(2,1)S(1)}, u32[]{:S(2)}, u32[]{:S(2)}) %collective-permute-start.8) | collective-permute-done | bytes 23072 | tf_op jit(solution)/shard_map/ppermute | solution.py:21
  64.9 2.7 %convolution_convert_fusion.1 = bf16[2,128,1536]{2,1,0:T(8,128)(2,1)S(1)} fusion(bf16[384,1536]{1,0:T(8,128)(2,1)S(1)} %copy-done.7, bf16[2,128,384]{2,1,0:T(8,128)(2,1)S(1)} %bitcast_select_fusion, bf16[2,15,384]{2,1,0:T(8,128)(2,1)S(1)} %collective-permute-done.8, bf16[2,15,384]{2,1,0:T(8,128)(2,1)S(1)} %collective-permute-done.7, f32[384]{0:T(512)S(1)} %copy-done.8, ...), kind=kOutput, calls=%fused_computation.1 | convolution fusion | flops 320962560 | bytes 2259456 | tf_op jit(solution)/shard_map/stc,cd->std/dot_general | solution.py:167
  67.9 0.5 copy-done.4
  68.4 1.3 %collective-permute-done.9 = bf16[2,2,32,1536]{3,2,0,1:T(8,128)(2,1)} collective-permute-done((bf16[2,2,32,1536]{3,2,0,1:T(8,128)(2,1)S(1)}, bf16[2,2,32,1536]{3,2,0,1:T(8,128)(2,1)}, u32[]{:S(2)}, u32[]{:S(2)}) %collective-permute-start.9) | collective-permute-done | bytes 393248 | tf_op jit(solution)/shard_map/ppermute | solution.py:59
  69.7 1.1 %convert_add_fusion = f32[2,2,32,1536]{3,2,0,1:T(8,128)S(1)} fusion(bf16[2,2,32,1536]{3,2,0,1:T(8,128)(2,1)} %collective-permute-done.9, bf16[2,2,1,32,1536]{4,3,2,1,0:T(8,128)(2,1)S(1)} %get-tuple-element.40), kind=kLoop, calls=%fused_computation.60 | loop fusion | flops 589824 | bytes 1572864 | tf_op jit(solution)/shard_map/add | solution.py:60
  70.9 1.6 %collective-permute-start.10 = (bf16[2,32,1536]{2,1,0:T(8,128)(2,1)S(1)}, bf16[2,32,1536]{2,1,0:T(8,128)(2,1)S(1)}, u32[]{:S(2)}, u32[]{:S(2)}) collective-permute-start(bf16[2,32,1536]{2,1,0:T(8,128)(2,1)S(1)} %fusion.50), channel_id=1, source_target_pairs={{0,2},{1,3},{2,0},{3,1},{4,6},{5,7},{6,4},{7,5},{8,10},{9,11},{10,... | collective-permute-start | bytes 589832 | tf_op jit(solution)/shard_map/ppermute | solution.py:59
  72.4 0.1 broadcast_compare_fusion.2
  72.5 5.4 %collective-permute-done.10 = bf16[2,32,1536]{2,1,0:T(8,128)(2,1)S(1)} collective-permute-done((bf16[2,32,1536]{2,1,0:T(8,128)(2,1)S(1)}, bf16[2,32,1536]{2,1,0:T(8,128)(2,1)S(1)}, u32[]{:S(2)}, u32[]{:S(2)}) %collective-permute-start.10) | collective-permute-done | bytes 196640 | tf_op jit(solution)/shard_map/ppermute | solution.py:59
  77.9 0.8 fusion.46
  (43 shorter events, 0.8 us)
Async XLA Ops:
  0.0 3.0 %copy-start = (bf16[3,1536,256]{2,1,0:T(8,128)(2,1)S(1)}, bf16[3,1536,256]{2,1,0:T(8,128)(2,1)}, u32[]{:S(2)}) copy-start(bf16[3,1536,256]{2,1,0:T(8,128)(2,1)} %param.15) | copy-start | bytes 7077892
  3.0 14.7 %copy-start.5 = (s32[2]{0:T(128)S(1)}, s32[2]{0:T(128)}, u32[]{:S(2)}) copy-start(s32[2]{0:T(128)} %param.13) | copy-start | bytes 28
  5.0 12.4 %collective-permute-start.1 = (bf16[2,2,128,256]{3,2,0,1:T(8,128)(2,1)S(1)}, bf16[2,2,128,256]{3,2,0,1:T(8,128)(2,1)}, u32[]{:S(2)}, u32[]{:S(2)}) collective-permute-start(bf16[2,2,128,256]{3,2,0,1:T(8,128)(2,1)S(1)} %get-tuple-element.49), channel_id=1, source_target_pairs={{0,4},{4,8},{8,12},{12,0},{1,5},{5,9},{9,13},{13,1},{2,6},{6,10},{... | collective-permute-start | bytes 786440 | tf_op jit(solution)/shard_map/ppermute | solution.py:87
  8.1 13.7 %collective-permute-start = (bf16[2,2,128,256]{3,2,0,1:T(8,128)(2,1)S(1)}, bf16[2,2,128,256]{3,2,0,1:T(8,128)(2,1)}, u32[]{:S(2)}, u32[]{:S(2)}) collective-permute-start(bf16[2,2,128,256]{3,2,0,1:T(8,128)(2,1)S(1)} %get-tuple-element.49), channel_id=1, source_target_pairs={{0,12},{4,0},{8,4},{12,8},{1,13},{5,1},{9,5},{13,9},{2,14},{6,2},{... | collective-permute-start | bytes 786440 | tf_op jit(solution)/shard_map/ppermute | solution.py:90
  17.4 10.4 %collective-permute-start.2 = (bf16[2,2,128,256]{3,2,0,1:T(8,128)(2,1)}, bf16[2,2,128,256]{3,2,0,1:T(8,128)(2,1)}, u32[]{:S(2)}, u32[]{:S(2)}) collective-permute-start(bf16[2,2,128,256]{3,2,0,1:T(8,128)(2,1)} %collective-permute-done.1), channel_id=1, source_target_pairs={{0,4},{4,8},{8,12},{12,0},{1,5},{5,9},{9,13},{13,1},{2,6},{6,10},{... | collective-permute-start | bytes 786440 | tf_op jit(solution)/shard_map/ppermute | solution.py:87
  32.3 1.2 %copy-start.2 = (bf16[4,1,2,128,256]{3,4,2,0,1:T(8,128)(2,1)S(1)}, bf16[4,1,2,128,256]{3,4,2,0,1:T(8,128)(2,1)}, u32[]{:S(2)}) copy-start(bf16[4,1,2,128,256]{3,4,2,0,1:T(8,128)(2,1)} %copy.26) | copy-start | bytes 1572868
  33.5 1.1 %copy-start.1 = (bf16[256,1536]{1,0:T(8,128)(2,1)S(1)}, bf16[256,1536]{1,0:T(8,128)(2,1)}, u32[]{:S(2)}) copy-start(bf16[256,1536]{1,0:T(8,128)(2,1)} %param.16) | copy-start | bytes 2359300
  35.1 11.6 %copy-start.3 = (f32[1536]{0:T(1024)S(1)}, f32[1536]{0:T(1024)}, u32[]{:S(2)}) copy-start(f32[1536]{0:T(1024)} %param.17) | copy-start | bytes 18436
  35.2 1.9 %collective-permute-start.3 = (bf16[2,2,32,1536]{3,2,0,1:T(8,128)(2,1)S(1)}, bf16[2,2,32,1536]{3,2,0,1:T(8,128)(2,1)}, u32[]{:S(2)}, u32[]{:S(2)}) collective-permute-start(bf16[2,2,32,1536]{3,2,0,1:T(8,128)(2,1)S(1)} %bitcast.113), channel_id=1, source_target_pairs={{0,1},{1,0},{2,3},{3,2},{4,5},{5,4},{6,7},{7,6},{8,9},{9,8},{10,11... | collective-permute-start | bytes 1179656 | tf_op jit(solution)/shard_map/ppermute | solution.py:59
  38.2 7.1 %collective-permute-start.4 = (bf16[2,32,1536]{2,1,0:T(8,128)(2,1)S(1)}, bf16[2,32,1536]{2,1,0:T(8,128)(2,1)}, u32[]{:S(2)}, u32[]{:S(2)}) collective-permute-start(bf16[2,32,1536]{2,1,0:T(8,128)(2,1)S(1)} %fusion.49), channel_id=1, source_target_pairs={{0,2},{1,3},{2,0},{3,1},{4,6},{5,7},{6,4},{7,5},{8,10},{9,11},{10,... | collective-permute-start | bytes 589832 | tf_op jit(solution)/shard_map/ppermute | solution.py:59
  46.8 6.2 %collective-permute-start.5 = (bf16[2,32,1536]{2,1,0:T(8,128)(2,1)S(1)}, bf16[2,32,1536]{2,1,0:T(8,128)(2,1)S(1)}, u32[]{:S(2)}, u32[]{:S(2)}) collective-permute-start(bf16[2,32,1536]{2,1,0:T(8,128)(2,1)S(1)} %multiply_convert_fusion.1), channel_id=1, source_target_pairs={{0,2},{1,3},{2,0},{3,1},{4,6},{5,7},{6,4},{7,5},{8,10},{9,11},{10,... | collective-permute-start | bytes 589832 | tf_op jit(solution)/shard_map/ppermute | solution.py:71
  53.3 1.9 %collective-permute-start.6 = (bf16[2,2,32,1536]{3,2,0,1:T(8,128)(2,1)S(1)}, bf16[2,2,32,1536]{3,2,0,1:T(8,128)(2,1)}, u32[]{:S(2)}, u32[]{:S(2)}) collective-permute-start(bf16[2,2,32,1536]{3,2,0,1:T(8,128)(2,1)S(1)} %pad_maximum_fusion.2), channel_id=1, source_target_pairs={{0,1},{1,0},{2,3},{3,2},{4,5},{5,4},{6,7},{7,6},{8,9},{9,8},{10,11... | collective-permute-start | bytes 1179656 | tf_op jit(solution)/shard_map/ppermute | solution.py:71
  54.7 1.9 %copy-start.6 = (bf16[2,1536,384]{2,1,0:T(8,128)(2,1)S(1)}, bf16[2,1536,384]{2,1,0:T(8,128)(2,1)}, u32[]{:S(2)}) copy-start(bf16[2,1536,384]{2,1,0:T(8,128)(2,1)} %param.18) | copy-start | bytes 7077892
  56.6 8.3 %copy-start.7 = (bf16[384,1536]{1,0:T(8,128)(2,1)S(1)}, bf16[384,1536]{1,0:T(8,128)(2,1)}, u32[]{:S(2)}) copy-start(bf16[384,1536]{1,0:T(8,128)(2,1)} %param.22) | copy-start | bytes 3538948
  56.6 8.3 %copy-start.8 = (f32[384]{0:T(512)S(1)}, f32[384]{0:T(512)}, u32[]{:S(2)}) copy-start(f32[384]{0:T(512)} %param.21) | copy-start | bytes 4612
  56.6 8.3 %copy-start.9 = (f32[384]{0:T(512)S(1)}, f32[384]{0:T(512)}, u32[]{:S(2)}) copy-start(f32[384]{0:T(512)} %param.20) | copy-start | bytes 4612
  57.6 4.0 %collective-permute-start.7 = (bf16[2,15,384]{2,1,0:T(8,128)(2,1)S(1)}, bf16[2,15,384]{2,1,0:T(8,128)(2,1)S(1)}, u32[]{:S(2)}, u32[]{:S(2)}) collective-permute-start(bf16[2,15,384]{2,1,0:T(8,128)(2,1)S(1)} %get-tuple-element.50), channel_id=1, source_target_pairs={{0,4},{4,8},{8,12},{1,5},{5,9},{9,13},{2,6},{6,10},{10,14},{3,7},{... | collective-permute-start | bytes 69128 | tf_op jit(solution)/shard_map/ppermute | solution.py:20
  59.2 5.7 %collective-permute-start.8 = (bf16[2,15,384]{2,1,0:T(8,128)(2,1)S(1)}, bf16[2,15,384]{2,1,0:T(8,128)(2,1)S(1)}, u32[]{:S(2)}, u32[]{:S(2)}) collective-permute-start(bf16[2,15,384]{2,1,0:T(8,128)(2,1)S(1)} %get-tuple-element.51), channel_id=1, source_target_pairs={{4,0},{8,4},{12,8},{5,1},{9,5},{13,9},{6,2},{10,6},{14,10},{7,3},{... | collective-permute-start | bytes 69128 | tf_op jit(solution)/shard_map/ppermute | solution.py:21
  67.7 0.7 copy-start.4
  67.8 1.9 %collective-permute-start.9 = (bf16[2,2,32,1536]{3,2,0,1:T(8,128)(2,1)S(1)}, bf16[2,2,32,1536]{3,2,0,1:T(8,128)(2,1)}, u32[]{:S(2)}, u32[]{:S(2)}) collective-permute-start(bf16[2,2,32,1536]{3,2,0,1:T(8,128)(2,1)S(1)} %bitcast.114), channel_id=1, source_target_pairs={{0,1},{1,0},{2,3},{3,2},{4,5},{5,4},{6,7},{7,6},{8,9},{9,8},{10,11... | collective-permute-start | bytes 1179656 | tf_op jit(solution)/shard_map/ppermute | solution.py:59
  70.9 7.0 %collective-permute-start.10 = (bf16[2,32,1536]{2,1,0:T(8,128)(2,1)S(1)}, bf16[2,32,1536]{2,1,0:T(8,128)(2,1)S(1)}, u32[]{:S(2)}, u32[]{:S(2)}) collective-permute-start(bf16[2,32,1536]{2,1,0:T(8,128)(2,1)S(1)} %fusion.50), channel_id=1, source_target_pairs={{0,2},{1,3},{2,0},{3,1},{4,6},{5,7},{6,4},{7,5},{8,10},{9,11},{10,... | collective-permute-start | bytes 589832 | tf_op jit(solution)/shard_map/ppermute | solution.py:59

commit v2 on v1

--- a/solution.py
+++ b/solution.py
@@ -92,7 +92,7 @@
     return jnp.stack([x] + from_right + from_left[::-1], axis=0)
 
 
-def shards(
+def chunk(
     features,
     frame_counts,
     attn_gain,
@@ -174,6 +174,21 @@
     return jnp.where(mine_live[..., None], clipped, 0.0).astype(jnp.bfloat16)
 
 
+def shards(features, frame_counts, *weights):
+    records = features.shape[0]
+    pieces = 2 if records % 2 == 0 else 1
+    size = records // pieces
+    outs = [
+        chunk(
+            features[p * size : (p + 1) * size],
+            frame_counts[p * size : (p + 1) * size],
+            *weights,
+        )
+        for p in range(pieces)
+    ]
+    return jnp.concatenate(outs, axis=0)
+
+
 def solution(mesh):
     return jax.shard_map(
         shards,

time: 79.3 us -> 84.3 us (1.063)
  waiting for transfers between devices: 39.9 us -> 19.9 us
  starting transfers between devices: 13 us -> 24.6 us
  local copies, waits for them, and re-layouts: 6.9 us -> 14.3 us
  other arithmetic: 11.2 us -> 15.4 us
  matrix products: 7.34 us -> 8.35 us
    ppermute x2 -> x4, waiting for transfers between devices: 13.2 us -> 5.57 us  [ring_gather(): going_right = lax.ppermute(going_right, axis, right)]
    ppermute x4 -> x8, waiting for transfers between devices: 14.1 us -> 7.5 us  [reduce_scatter_rows(): lax.ppermute(send.astype(jnp.bfloat16), axis, xor_pairs(count, 1 << b))]
    slice x7 -> x14, local copies, waits for them, and re-layouts: 5.64 us -> 12.1 us  [the longest x4 5.31 us: chunk(): kv_all[:, 1].reshape(ctx_count, records, frames_here, head_count, HEAD_DIM)]
    ppermute x1 -> x2, starting transfers between devices: 1.62 us -> 5.84 us  [with_halo(): before = lax.ppermute(last, axis, up)]
    ppermute x1 -> x2, waiting for transfers between devices: 4.09 us -> 0.01 us  [ring_gather(): going_left = lax.ppermute(going_left, axis, left)]
    lt x3, other arithmetic: 0.22 us -> 4.04 us  [the longest x1 1.39 us: chunk(): is_live = positions[None] < frame_counts[:, None, None]]
    ppermute x1 -> x2, starting transfers between devices: 2.09 us -> 5.91 us  [ring_gather(): going_left = lax.ppermute(going_left, axis, left)]
    ppermute x4 -> x8, starting transfers between devices: 3.25 us -> 4.73 us  [reduce_scatter_rows(): lax.ppermute(send.astype(jnp.bfloat16), axis, xor_pairs(count, 1 << b))]
  transfers between devices with their start and end apart: 11 -> 22, of which waited for: 10 -> 9; matrix products, arithmetic and copies ran while one was open for 4% -> 36% of each run, Pallas kernels for 0% -> 0%
where the time goes in v2:
time: 84.3 us; the launch traced here: 83.7 us
  starting transfers between devices  24.6 us (29%)
  waiting for transfers between devices  19.9 us (24%)
  other arithmetic  15.4 us (18%)
  local copies, waits for them, and re-layouts  14.3 us (17%)
  matrix products  8.35 us (10%)
  between operations  1.11 us (1%)
    ppermute x8, waiting for transfers between devices, reduce_scatter_rows(): lax.ppermute(send.astype(jnp.bfloat16), axis, xor_pairs(count, 1 << b))  7.5 us
    ppermute x2, starting transfers between devices, ring_gather(): going_left = lax.ppermute(going_left, axis, left)  5.91 us
    ppermute x2, starting transfers between devices, with_halo(): before = lax.ppermute(last, axis, up)  5.84 us
    ppermute x4, waiting for transfers between devices, ring_gather(): going_right = lax.ppermute(going_right, axis, right)  5.57 us
    slice x4, local copies, waits for them, and re-layouts, chunk(): kv_all[:, 1].reshape(ctx_count, records, frames_here, head_count, HEAD_DIM)  5.31 us
    ppermute x8, starting transfers between devices, reduce_scatter_rows(): lax.ppermute(send.astype(jnp.bfloat16), axis, xor_pairs(count, 1 << b))  4.73 us
    ppermute x4, waiting for transfers between devices, all_gather_rows(): got = lax.ppermute(acc, axis, xor_pairs(count, 1 << b))  4.2 us
    reduce_sum x3, other arithmetic, layer_norm(): centre = jnp.mean(values, axis=-1, keepdims=True)  3.36 us
  transfers between devices with their start and end apart: 22, of which 9 were waited for; matrix products, arithmetic and copies ran while one was open for 36% of the time, Pallas kernels for 0%

profile of v2, /device:TPU:0, one launch (start us, length us, event | category | flops | bytes accessed | tf_op | source)
XLA Modules:
  0.0 83.7 jit_solution(16736951043988314020)
XLA Ops:
  0.0 1.3 %convert_reduce_fusion.1 = f32[128]{0:T(128)S(1)} fusion(bf16[2,128,1536]{2,1,0:T(8,128)(2,1)} %param.12), kind=kLoop, calls=%fused_computation.25 | loop fusion | flops 393088 | bytes 393728 | tf_op jit(solution)/shard_map/reduce_sum | solution.py:27
  1.3 1.4 %fusion.19 = (f32[128]{0:T(128)S(1)}, f32[128]{0:T(128)S(1)}) fusion(f32[128]{0:T(128)S(1)} %broadcast_multiply_fusion.3, bf16[2,128,1536]{2,1,0:T(8,128)(2,1)} %param.12), kind=kLoop, calls=%fused_computation.37 | loop fusion | flops 1179392 | bytes 787968 | tf_op jit(solution)/shard_map/reduce_sum | solution.py:29
  2.8 1.3 %fusion.16 = f32[128]{0:T(128)S(1)} fusion(f32[128]{0:T(128)S(1)} %get-tuple-element.79, bf16[2,128,1536]{2,1,0:T(8,128)(2,1)} %param.12), kind=kLoop, calls=%fused_computation.34 | loop fusion | flops 786304 | bytes 394240 | tf_op jit(solution)/shard_map/reduce_sum | solution.py:29
  4.0 1.5 %fusion.3 = bf16[3,1,128,256]{3,2,0,1:T(8,128)(2,1)S(1)} fusion(bf16[3,1536,256]{2,1,0:T(8,128)(2,1)S(1)} %copy-done, f32[128]{0:T(128)S(1)} %add_rsqrt_fusion.1, f32[128]{0:T(128)S(1)} %get-tuple-element.79, f32[1536]{0:T(1024)} %param.14, bf16[2,128,1536]{2,1,0:T(8,128)(2,1)} %param.12), kind=kOutput, calls=%fused_computation.13 | convolution fusion | flops 303071232 | bytes 2958336 | tf_op jit(solution)/shard_map/std,idc->istc/dot_general | solution.py:116
  5.6 3.1 %collective-permute-start.12 = (bf16[2,1,128,256]{3,2,0,1:T(8,128)(2,1)S(1)}, bf16[2,1,128,256]{3,2,0,1:T(8,128)(2,1)S(1)}, u32[]{:S(2)}, u32[]{:S(2)}) collective-permute-start(bf16[2,1,128,256]{3,2,0,1:T(8,128)(2,1)S(1)} %get-tuple-element.59), channel_id=1, source_target_pairs={{0,4},{4,8},{8,12},{12,0},{1,5},{5,9},{9,13},{13,1},{2,6},{6,10},{... | collective-permute-start | bytes 393224 | tf_op jit(solution)/shard_map/ppermute | solution.py:87
  8.7 2.1 %collective-permute-start.11 = (bf16[2,1,128,256]{3,2,0,1:T(8,128)(2,1)S(1)}, bf16[2,1,128,256]{3,2,0,1:T(8,128)(2,1)S(1)}, u32[]{:S(2)}, u32[]{:S(2)}) collective-permute-start(bf16[2,1,128,256]{3,2,0,1:T(8,128)(2,1)S(1)} %get-tuple-element.59), channel_id=1, source_target_pairs={{0,12},{4,0},{8,4},{12,8},{1,13},{5,1},{9,5},{13,9},{2,14},{6,2},{... | collective-permute-start | bytes 393224 | tf_op jit(solution)/shard_map/ppermute | solution.py:90
  11.3 0.7 slice_bitcast_fusion.1
  12.1 3.8 %collective-permute-start = (bf16[2,1,128,256]{3,2,0,1:T(8,128)(2,1)}, bf16[2,1,128,256]{3,2,0,1:T(8,128)(2,1)}, u32[]{:S(2)}, u32[]{:S(2)}) collective-permute-start(bf16[2,1,128,256]{3,2,0,1:T(8,128)(2,1)} %get-tuple-element.55), channel_id=1, source_target_pairs={{0,12},{4,0},{8,4},{12,8},{1,13},{5,1},{9,5},{13,9},{2,14},{6,2},{... | collective-permute-start | bytes 393224 | tf_op jit(solution)/shard_map/ppermute | solution.py:90
  15.9 0.9 %fusion.143 = (bf16[1,128,1536]{2,1,0:T(8,128)(2,1)}, bf16[1,128,1536]{2,1,0:T(8,128)(2,1)}) fusion(bf16[2,128,1536]{2,1,0:T(8,128)(2,1)S(1)} %copy-done.2), kind=kLoop, calls=%fused_computation.344 | loop fusion | bytes 1572864 | tf_op jit(solution)/shard_map/slice | solution.py:183
  16.8 0.7 fusion.148
  17.5 1.4 %fusion.125 = (pred[4,128]{1,0:T(4,128)(4,1)S(1)}, pred[4,128]{1,0:T(4,128)(4,1)S(1)}) fusion(s32[]{:T(128)} %bitcast.22, s32[4]{0:T(128)S(1)} %fusion.126, s32[]{:T(128)} %bitcast.59), kind=kLoop, calls=%fused_computation.284 | loop fusion | flops 1536 | bytes 1048 | tf_op jit(solution)/shard_map/lt | solution.py:130
  18.9 0.7 slice_reduce_fusion.29
  19.7 0.7 copy.29
  20.5 0.7 slice_reduce_fusion.30
  21.2 5.6 %collective-permute-done.13 = bf16[2,1,128,256]{3,2,0,1:T(8,128)(2,1)} collective-permute-done((bf16[2,1,128,256]{3,2,0,1:T(8,128)(2,1)S(1)}, bf16[2,1,128,256]{3,2,0,1:T(8,128)(2,1)}, u32[]{:S(2)}, u32[]{:S(2)}) %collective-permute-start.13) | collective-permute-done | bytes 131104 | tf_op jit(solution)/shard_map/ppermute | solution.py:87
  26.7 1.0 %pad_maximum_fusion.1 = bf16[4,2,1,128,256]{4,3,1,2,0:T(8,128)(2,1)S(1)} fusion(bf16[1,2,1,128,256]{4,3,1,2,0:T(8,128)(2,1)S(1)} %bitcast.222, bf16[1,2,1,128,256]{4,3,1,2,0:T(8,128)(2,1)} %bitcast.18, bf16[1,2,1,128,256]{4,3,1,2,0:T(8,128)(2,1)S(1)} %bitcast.223, bf16[1,2,1,128,256]{4,3,1,2,0:T(8,128)(2,1)S(1)} %get-tuple-element.58), kind=kLoop, calls=%fused_computation.97 | loop fusion | flops 786432 | bytes 1048576 | tf_op jit(solution)/shard_map/stack | solution.py:92
  27.7 0.8 fusion.145
  28.6 1.2 %copy.41 = bf16[4,1,1,128,256]{3,4,0,2,1:T(8,128)(2,1)S(1)} copy(bf16[4,1,1,128,256]{4,3,1,2,0:T(8,128)(2,1)} %get-tuple-element.47) | data formatting | bytes 524288 | tf_op jit(solution)/shard_map/slice | solution.py:122
  29.8 1.8 %copy.43 = bf16[4,1,1,128,256]{3,4,0,2,1:T(8,128)(2,1)} copy(bf16[4,1,1,128,256]{4,3,1,2,0:T(8,128)(2,1)} %get-tuple-element.46) | data formatting | bytes 524288 | tf_op jit(solution)/shard_map/slice | solution.py:123
  33.1 0.7 dynamic-slice_bitcast_fusion.1
  33.9 1.1 %pad_maximum_fusion = bf16[4,2,1,128,256]{4,3,1,2,0:T(8,128)(2,1)S(1)} fusion(bf16[1,2,1,128,256]{4,3,1,2,0:T(8,128)(2,1)} %bitcast.8, bf16[1,2,1,128,256]{4,3,1,2,0:T(8,128)(2,1)} %bitcast.7, bf16[1,2,1,128,256]{4,3,1,2,0:T(8,128)(2,1)} %bitcast.6, bf16[1,2,1,128,256]{4,3,1,2,0:T(8,128)(2,1)S(1)} %copy-done.4), kind=kLoop, calls=%fused_computation.96 | loop fusion | flops 786432 | bytes 1048576 | tf_op jit(solution)/shard_map/stack | solution.py:92
  35.0 0.9 %fusion.144 = (bf16[4,1,1,128,256]{4,3,1,2,0:T(8,128)(2,1)}, bf16[4,1,1,128,256]{4,3,1,2,0:T(8,128)(2,1)}) fusion(bf16[4,2,1,128,256]{4,3,1,2,0:T(8,128)(2,1)S(1)} %pad_maximum_fusion), kind=kLoop, calls=%fused_computation.345 | loop fusion | bytes 1048576 | tf_op jit(solution)/shard_map/slice | solution.py:123
  35.8 1.8 %copy.30 = bf16[4,1,1,128,256]{3,4,0,2,1:T(8,128)(2,1)} copy(bf16[4,1,1,128,256]{4,3,1,2,0:T(8,128)(2,1)} %get-tuple-element.45) | data formatting | bytes 524288 | tf_op jit(solution)/shard_map/slice | solution.py:122
  37.6 1.8 %copy.32 = bf16[4,1,1,128,256]{3,4,0,2,1:T(8,128)(2,1)} copy(bf16[4,1,1,128,256]{4,3,1,2,0:T(8,128)(2,1)} %get-tuple-element.44) | data formatting | bytes 524288 | tf_op jit(solution)/shard_map/slice | solution.py:123
  39.4 1.4 %fusion.149 = (f32[4,128]{1,0:T(4,128)S(1)}, f32[4,128,4,128]{1,3,2,0:T(8,128)S(1)}) fusion(bf16[128,4,64,1]{0,2,3,1:T(8,128)(2,1)} %bitcast.218, bf16[4,128,4,64]{1,3,2,0:T(8,128)(2,1)} %bitcast.212, pred[4,128]{1,0:T(4,128)(4,1)S(1)} %get-tuple-element.70), kind=kOutput, calls=%fused_computation.350 | convolution fusion | flops 34340352 | bytes 1378816 | tf_op jit(solution)/shard_map/sqhe,cskhe->shqck/dot_general | solution.py:125
  41.7 0.6 collective-permute-start.3
  42.2 1.0 %convert_add_fusion.1 = f32[1,2,32,1536]{3,2,1,0:T(8,128)S(1)} fusion(bf16[1,2,32,1536]{3,2,1,0:T(8,128)(2,1)} %collective-permute-done.14, bf16[1,2,2,32,1536]{4,3,2,1,0:T(8,128)(2,1)S(1)} %bitcast.207, s32[]{:T(128)S(6)} %select_n.133), kind=kLoop, calls=%fused_computation.105 | loop fusion | flops 294912 | bytes 786436 | tf_op jit(solution)/shard_map/add | solution.py:60
  43.2 1.8 %collective-permute-start.15 = (bf16[1,32,1536]{2,1,0:T(8,128)(2,1)S(1)}, bf16[1,32,1536]{2,1,0:T(8,128)(2,1)S(1)}, u32[]{:S(2)}, u32[]{:S(2)}) collective-permute-start(bf16[1,32,1536]{2,1,0:T(8,128)(2,1)S(1)} %fusion.64), channel_id=1, source_target_pairs={{0,2},{1,3},{2,0},{3,1},{4,6},{5,7},{6,4},{7,5},{8,10},{9,11},{10,... | collective-permute-start | bytes 294920 | tf_op jit(solution)/shard_map/ppermute | solution.py:59
  45.5 3.1 %collective-permute-done.15 = bf16[1,32,1536]{2,1,0:T(8,128)(2,1)S(1)} collective-permute-done((bf16[1,32,1536]{2,1,0:T(8,128)(2,1)S(1)}, bf16[1,32,1536]{2,1,0:T(8,128)(2,1)S(1)}, u32[]{:S(2)}, u32[]{:S(2)}) %collective-permute-start.15) | collective-permute-done | bytes 98336 | tf_op jit(solution)/shard_map/ppermute | solution.py:59
  48.6 1.0 %fusion.141 = (f32[32]{0:T(128)S(1)}, f32[1,32,1536]{2,1,0:T(8,128)S(1)}) fusion(bf16[1,32,1536]{2,1,0:T(8,128)(2,1)S(1)} %collective-permute-done.15, f32[1,2,32,1536]{3,2,1,0:T(8,128)S(1)} %convert_add_fusion.1, s32[]{:T(128)S(6)} %select_n.135, bf16[1,128,1536]{2,1,0:T(8,128)(2,1)} %get-tuple-element.43, s32[]{:T(128)S(6)} %select_n.130), kind=kLoop, calls=%fused_computation.343 | loop fusion | flops 245728 | bytes 589960 | tf_op jit(solution)/shard_map/reduce_sum | solution.py:27
  50.2 1.0 %fusion.139 = (f32[32]{0:T(128)S(1)}, f32[1,32,1536]{2,1,0:T(8,128)S(1)}) fusion(bf16[1,32,1536]{2,1,0:T(8,128)(2,1)S(1)} %collective-permute-done.4, f32[1,2,32,1536]{3,2,1,0:T(8,128)S(1)} %convert_add_fusion.3, s32[]{:T(128)S(6)} %select_n.135, bf16[1,128,1536]{2,1,0:T(8,128)(2,1)} %get-tuple-element.42, s32[]{:T(128)S(6)} %select_n.130), kind=kLoop, calls=%fused_computation.342 | loop fusion | flops 245728 | bytes 589960 | tf_op jit(solution)/shard_map/reduce_sum | solution.py:27
  51.6 1.9 %collective-permute-start.16 = (bf16[1,32,1536]{2,1,0:T(8,128)(2,1)S(1)}, bf16[1,32,1536]{2,1,0:T(8,128)(2,1)S(1)}, u32[]{:S(2)}, u32[]{:S(2)}) collective-permute-start(bf16[1,32,1536]{2,1,0:T(8,128)(2,1)S(1)} %get-tuple-element.67), channel_id=1, source_target_pairs={{0,2},{1,3},{2,0},{3,1},{4,6},{5,7},{6,4},{7,5},{8,10},{9,11},{10,... | collective-permute-start | bytes 294920 | tf_op jit(solution)/shard_map/ppermute | solution.py:71
  53.5 1.3 %fusion.128 = (pred[128]{0:T(512)(128)(4,1)S(1)}, pred[128]{0:T(512)(128)(4,1)S(1)}) fusion(s32[]{:T(128)} %bitcast.59, s32[]{:T(128)S(6)} %mul.660, s32[]{:T(128)} %bitcast.22), kind=kLoop, calls=%fused_computation.323 | loop fusion | flops 384 | bytes 268 | tf_op jit(solution)/shard_map/lt | solution.py:155
  55.2 1.3 %collective-permute-done.16 = bf16[1,32,1536]{2,1,0:T(8,128)(2,1)S(1)} collective-permute-done((bf16[1,32,1536]{2,1,0:T(8,128)(2,1)S(1)}, bf16[1,32,1536]{2,1,0:T(8,128)(2,1)S(1)}, u32[]{:S(2)}, u32[]{:S(2)}) %collective-permute-start.16) | collective-permute-done | bytes 98336 | tf_op jit(solution)/shard_map/ppermute | solution.py:71
  56.6 2.9 %collective-permute-done.5 = bf16[1,32,1536]{2,1,0:T(8,128)(2,1)S(1)} collective-permute-done((bf16[1,32,1536]{2,1,0:T(8,128)(2,1)S(1)}, bf16[1,32,1536]{2,1,0:T(8,128)(2,1)S(1)}, u32[]{:S(2)}, u32[]{:S(2)}) %collective-permute-start.5) | collective-permute-done | bytes 98336 | tf_op jit(solution)/shard_map/ppermute | solution.py:71
  60.4 1.3 %collective-permute-start.18 = (bf16[1,15,384]{2,1,0:T(8,128)(2,1)S(1)}, bf16[1,15,384]{2,1,0:T(8,128)(2,1)S(1)}, u32[]{:S(2)}, u32[]{:S(2)}) collective-permute-start(bf16[1,15,384]{2,1,0:T(8,128)(2,1)S(1)} %get-tuple-element.62), channel_id=1, source_target_pairs={{0,4},{4,8},{8,12},{1,5},{5,9},{9,13},{2,6},{6,10},{10,14},{3,7},{... | collective-permute-start | bytes 34568 | tf_op jit(solution)/shard_map/ppermute | solution.py:20
  61.7 1.3 %collective-permute-start.19 = (bf16[1,15,384]{2,1,0:T(8,128)(2,1)S(1)}, bf16[1,15,384]{2,1,0:T(8,128)(2,1)S(1)}, u32[]{:S(2)}, u32[]{:S(2)}) collective-permute-start(bf16[1,15,384]{2,1,0:T(8,128)(2,1)S(1)} %get-tuple-element.63), channel_id=1, source_target_pairs={{4,0},{8,4},{12,8},{5,1},{9,5},{13,9},{6,2},{10,6},{14,10},{7,3},{... | collective-permute-start | bytes 34568 | tf_op jit(solution)/shard_map/ppermute | solution.py:21
  64.0 4.5 %collective-permute-start.7 = (bf16[1,15,384]{2,1,0:T(8,128)(2,1)S(1)}, bf16[1,15,384]{2,1,0:T(8,128)(2,1)S(1)}, u32[]{:S(2)}, u32[]{:S(2)}) collective-permute-start(bf16[1,15,384]{2,1,0:T(8,128)(2,1)S(1)} %get-tuple-element.60), channel_id=1, source_target_pairs={{0,4},{4,8},{8,12},{1,5},{5,9},{9,13},{2,6},{6,10},{10,14},{3,7},{... | collective-permute-start | bytes 34568 | tf_op jit(solution)/shard_map/ppermute | solution.py:20
  68.6 1.3 %collective-permute-start.8 = (bf16[1,15,384]{2,1,0:T(8,128)(2,1)S(1)}, bf16[1,15,384]{2,1,0:T(8,128)(2,1)S(1)}, u32[]{:S(2)}, u32[]{:S(2)}) collective-permute-start(bf16[1,15,384]{2,1,0:T(8,128)(2,1)S(1)} %get-tuple-element.61), channel_id=1, source_target_pairs={{4,0},{8,4},{12,8},{5,1},{9,5},{13,9},{6,2},{10,6},{14,10},{7,3},{... | collective-permute-start | bytes 34568 | tf_op jit(solution)/shard_map/ppermute | solution.py:21
  70.2 1.2 %convolution_convert_fusion = bf16[128,1536]{1,0:T(8,128)(2,1)S(1)} fusion(bf16[384,1536]{1,0:T(8,128)(2,1)S(1)} %copy-done.41, bf16[1,128,384]{2,1,0:T(8,128)(2,1)S(1)} %bitcast_select_fusion, bf16[1,15,384]{2,1,0:T(8,128)(2,1)S(1)} %collective-permute-done.19, bf16[1,15,384]{2,1,0:T(8,128)(2,1)S(1)} %collective-permute-done.18, f32[384]{0:T(512)S(1)} %copy-done.43, ...), kind=kOutput, calls=%fused_computation | convolution fusion | flops 160481280 | bytes 1744896 | tf_op jit(solution)/shard_map/stc,cd->std/dot_general | solution.py:167
  71.5 2.6 %collective-permute-done.8 = bf16[1,15,384]{2,1,0:T(8,128)(2,1)S(1)} collective-permute-done((bf16[1,15,384]{2,1,0:T(8,128)(2,1)S(1)}, bf16[1,15,384]{2,1,0:T(8,128)(2,1)S(1)}, u32[]{:S(2)}, u32[]{:S(2)}) %collective-permute-start.8) | collective-permute-done | bytes 11552 | tf_op jit(solution)/shard_map/ppermute | solution.py:21
  74.2 1.1 %convolution_convert_fusion.2 = bf16[128,1536]{1,0:T(8,128)(2,1)S(1)} fusion(bf16[384,1536]{1,0:T(8,128)(2,1)S(1)} %copy-done.41, bf16[1,128,384]{2,1,0:T(8,128)(2,1)S(1)} %bitcast_select_fusion.1, bf16[1,15,384]{2,1,0:T(8,128)(2,1)S(1)} %collective-permute-done.8, bf16[1,15,384]{2,1,0:T(8,128)(2,1)S(1)} %collective-permute-done.7, f32[384]{0:T(512)S(1)} %copy-done.43, ...), kind=kOutput, calls=%fused_computation.2 | convolution fusion | flops 160481280 | bytes 1744896 | tf_op jit(solution)/shard_map/stc,cd->std/dot_general | solution.py:167
  75.5 0.9 %collective-permute-start.21 = (bf16[1,32,1536]{2,1,0:T(8,128)(2,1)S(1)}, bf16[1,32,1536]{2,1,0:T(8,128)(2,1)S(1)}, u32[]{:S(2)}, u32[]{:S(2)}) collective-permute-start(bf16[1,32,1536]{2,1,0:T(8,128)(2,1)S(1)} %fusion.65), channel_id=1, source_target_pairs={{0,2},{1,3},{2,0},{3,1},{4,6},{5,7},{6,4},{7,5},{8,10},{9,11},{10,... | collective-permute-start | bytes 294920 | tf_op jit(solution)/shard_map/ppermute | solution.py:59
  76.9 0.9 %collective-permute-start.10 = (bf16[1,32,1536]{2,1,0:T(8,128)(2,1)S(1)}, bf16[1,32,1536]{2,1,0:T(8,128)(2,1)S(1)}, u32[]{:S(2)}, u32[]{:S(2)}) collective-permute-start(bf16[1,32,1536]{2,1,0:T(8,128)(2,1)S(1)} %fusion.63), channel_id=1, source_target_pairs={{0,2},{1,3},{2,0},{3,1},{4,6},{5,7},{6,4},{7,5},{8,10},{9,11},{10,... | collective-permute-start | bytes 294920 | tf_op jit(solution)/shard_map/ppermute | solution.py:59
  77.9 1.3 %fusion.130 = (pred[32]{0:T(512)(128)(4,1)S(1)}, pred[32]{0:T(512)(128)(4,1)S(1)}) fusion(s32[]{:T(128)} %bitcast.59, s32[]{:T(128)S(6)} %add.424, s32[]{:T(128)} %bitcast.22), kind=kLoop, calls=%fused_computation.327 | loop fusion | flops 96 | bytes 76 | tf_op jit(solution)/shard_map/lt | solution.py:173
  79.2 2.0 %collective-permute-done.21 = bf16[1,32,1536]{2,1,0:T(8,128)(2,1)S(1)} collective-permute-done((bf16[1,32,1536]{2,1,0:T(8,128)(2,1)S(1)}, bf16[1,32,1536]{2,1,0:T(8,128)(2,1)S(1)}, u32[]{:S(2)}, u32[]{:S(2)}) %collective-permute-start.21) | collective-permute-done | bytes 98336 | tf_op jit(solution)/shard_map/ppermute | solution.py:59
  81.2 1.7 %collective-permute-done.10 = bf16[1,32,1536]{2,1,0:T(8,128)(2,1)S(1)} collective-permute-done((bf16[1,32,1536]{2,1,0:T(8,128)(2,1)S(1)}, bf16[1,32,1536]{2,1,0:T(8,128)(2,1)S(1)}, u32[]{:S(2)}, u32[]{:S(2)}) %collective-permute-start.10) | collective-permute-done | bytes 98336 | tf_op jit(solution)/shard_map/ppermute | solution.py:59
  83.0 0.7 pad_maximum_fusion.6
  (166 shorter events, 7.3 us)
Async XLA Ops:
  1.3 9.5 %copy-start.2 = (bf16[2,128,1536]{2,1,0:T(8,128)(2,1)S(1)}, bf16[2,128,1536]{2,1,0:T(8,128)(2,1)}, u32[]{:S(2)}) copy-start(bf16[2,128,1536]{2,1,0:T(8,128)(2,1)} %param.12) | copy-start | bytes 2359300
  1.3 9.5 %copy-start.42 = (f32[1536]{0:T(1024)S(1)}, f32[1536]{0:T(1024)}, u32[]{:S(2)}) copy-start(f32[1536]{0:T(1024)} %param.14) | copy-start | bytes 18436
  5.6 13.3 %collective-permute-start.12 = (bf16[2,1,128,256]{3,2,0,1:T(8,128)(2,1)S(1)}, bf16[2,1,128,256]{3,2,0,1:T(8,128)(2,1)S(1)}, u32[]{:S(2)}, u32[]{:S(2)}) collective-permute-start(bf16[2,1,128,256]{3,2,0,1:T(8,128)(2,1)S(1)} %get-tuple-element.59), channel_id=1, source_target_pairs={{0,4},{4,8},{8,12},{12,0},{1,5},{5,9},{9,13},{13,1},{2,6},{6,10},{... | collective-permute-start | bytes 393224 | tf_op jit(solution)/shard_map/ppermute | solution.py:87
  8.7 12.5 %collective-permute-start.11 = (bf16[2,1,128,256]{3,2,0,1:T(8,128)(2,1)S(1)}, bf16[2,1,128,256]{3,2,0,1:T(8,128)(2,1)S(1)}, u32[]{:S(2)}, u32[]{:S(2)}) collective-permute-start(bf16[2,1,128,256]{3,2,0,1:T(8,128)(2,1)S(1)} %get-tuple-element.59), channel_id=1, source_target_pairs={{0,12},{4,0},{8,4},{12,8},{1,13},{5,1},{9,5},{13,9},{2,14},{6,2},{... | collective-permute-start | bytes 393224 | tf_op jit(solution)/shard_map/ppermute | solution.py:90
  10.8 8.1 %copy-start.7 = (f32[31,384]{1,0:T(8,128)S(1)}, f32[31,384]{1,0:T(8,128)}, u32[]{:S(2)}) copy-start(f32[31,384]{1,0:T(8,128)} %param.19) | copy-start | bytes 142852
  12.1 9.1 %collective-permute-start.1 = (bf16[2,1,128,256]{3,2,0,1:T(8,128)(2,1)}, bf16[2,1,128,256]{3,2,0,1:T(8,128)(2,1)}, u32[]{:S(2)}, u32[]{:S(2)}) collective-permute-start(bf16[2,1,128,256]{3,2,0,1:T(8,128)(2,1)} %get-tuple-element.55), channel_id=1, source_target_pairs={{0,4},{4,8},{8,12},{12,0},{1,5},{5,9},{9,13},{13,1},{2,6},{6,10},{... | collective-permute-start | bytes 393224 | tf_op jit(solution)/shard_map/ppermute | solution.py:87
  12.1 21.8 %collective-permute-start = (bf16[2,1,128,256]{3,2,0,1:T(8,128)(2,1)}, bf16[2,1,128,256]{3,2,0,1:T(8,128)(2,1)}, u32[]{:S(2)}, u32[]{:S(2)}) collective-permute-start(bf16[2,1,128,256]{3,2,0,1:T(8,128)(2,1)} %get-tuple-element.55), channel_id=1, source_target_pairs={{0,12},{4,0},{8,4},{12,8},{1,13},{5,1},{9,5},{13,9},{2,14},{6,2},{... | collective-permute-start | bytes 393224 | tf_op jit(solution)/shard_map/ppermute | solution.py:90
  18.9 7.8 %collective-permute-start.13 = (bf16[2,1,128,256]{3,2,0,1:T(8,128)(2,1)S(1)}, bf16[2,1,128,256]{3,2,0,1:T(8,128)(2,1)}, u32[]{:S(2)}, u32[]{:S(2)}) collective-permute-start(bf16[2,1,128,256]{3,2,0,1:T(8,128)(2,1)S(1)} %collective-permute-done.12), channel_id=1, source_target_pairs={{0,4},{4,8},{8,12},{12,0},{1,5},{5,9},{9,13},{13,1},{2,6},{6,10},{... | collective-permute-start | bytes 393224 | tf_op jit(solution)/shard_map/ppermute | solution.py:87
  21.2 12.7 %collective-permute-start.2 = (bf16[2,1,128,256]{3,2,0,1:T(8,128)(2,1)}, bf16[2,1,128,256]{3,2,0,1:T(8,128)(2,1)}, u32[]{:S(2)}, u32[]{:S(2)}) collective-permute-start(bf16[2,1,128,256]{3,2,0,1:T(8,128)(2,1)} %collective-permute-done.1), channel_id=1, source_target_pairs={{0,4},{4,8},{8,12},{12,0},{1,5},{5,9},{9,13},{13,1},{2,6},{6,10},{... | collective-permute-start | bytes 393224 | tf_op jit(solution)/shard_map/ppermute | solution.py:87
  33.8 8.4 %collective-permute-start.14 = (bf16[1,2,32,1536]{3,2,1,0:T(8,128)(2,1)}, bf16[1,2,32,1536]{3,2,1,0:T(8,128)(2,1)}, u32[]{:S(2)}, u32[]{:S(2)}) collective-permute-start(bf16[1,2,32,1536]{3,2,1,0:T(8,128)(2,1)} %dynamic-slice_bitcast_fusion.1), channel_id=1, source_target_pairs={{0,1},{1,0},{2,3},{3,2},{4,5},{5,4},{6,7},{7,6},{8,9},{9,8},{10,11... | collective-permute-start | bytes 589832 | tf_op jit(solution)/shard_map/ppermute | solution.py:59
  41.3 10.1 %copy-start.8 = (f32[1536]{0:T(1024)S(1)}, f32[1536]{0:T(1024)}, u32[]{:S(2)}) copy-start(f32[1536]{0:T(1024)} %param.17) | copy-start | bytes 18436
  41.7 3.4 %collective-permute-start.3 = (bf16[1,2,32,1536]{3,2,1,0:T(8,128)(2,1)S(1)}, bf16[1,2,32,1536]{3,2,1,0:T(8,128)(2,1)S(1)}, u32[]{:S(2)}, u32[]{:S(2)}) collective-permute-start(bf16[1,2,32,1536]{3,2,1,0:T(8,128)(2,1)S(1)} %dynamic-slice_bitcast_fusion.3), channel_id=1, source_target_pairs={{0,1},{1,0},{2,3},{3,2},{4,5},{5,4},{6,7},{7,6},{8,9},{9,8},{10,11... | collective-permute-start | bytes 589832 | tf_op jit(solution)/shard_map/ppermute | solution.py:59
  43.2 5.4 %collective-permute-start.15 = (bf16[1,32,1536]{2,1,0:T(8,128)(2,1)S(1)}, bf16[1,32,1536]{2,1,0:T(8,128)(2,1)S(1)}, u32[]{:S(2)}, u32[]{:S(2)}) collective-permute-start(bf16[1,32,1536]{2,1,0:T(8,128)(2,1)S(1)} %fusion.64), channel_id=1, source_target_pairs={{0,2},{1,3},{2,0},{3,1},{4,6},{5,7},{6,4},{7,5},{8,10},{9,11},{10,... | collective-permute-start | bytes 294920 | tf_op jit(solution)/shard_map/ppermute | solution.py:59
  45.2 5.0 %collective-permute-start.4 = (bf16[1,32,1536]{2,1,0:T(8,128)(2,1)S(1)}, bf16[1,32,1536]{2,1,0:T(8,128)(2,1)S(1)}, u32[]{:S(2)}, u32[]{:S(2)}) collective-permute-start(bf16[1,32,1536]{2,1,0:T(8,128)(2,1)S(1)} %fusion.62), channel_id=1, source_target_pairs={{0,2},{1,3},{2,0},{3,1},{4,6},{5,7},{6,4},{7,5},{8,10},{9,11},{10,... | collective-permute-start | bytes 294920 | tf_op jit(solution)/shard_map/ppermute | solution.py:59
  51.2 8.5 %copy-start.1 = (bf16[2,1536,384]{2,1,0:T(8,128)(2,1)S(1)}, bf16[2,1536,384]{2,1,0:T(8,128)(2,1)}, u32[]{:S(2)}) copy-start(bf16[2,1536,384]{2,1,0:T(8,128)(2,1)} %param.18) | copy-start | bytes 7077892
  51.6 4.9 %collective-permute-start.16 = (bf16[1,32,1536]{2,1,0:T(8,128)(2,1)S(1)}, bf16[1,32,1536]{2,1,0:T(8,128)(2,1)S(1)}, u32[]{:S(2)}, u32[]{:S(2)}) collective-permute-start(bf16[1,32,1536]{2,1,0:T(8,128)(2,1)S(1)} %get-tuple-element.67), channel_id=1, source_target_pairs={{0,2},{1,3},{2,0},{3,1},{4,6},{5,7},{6,4},{7,5},{8,10},{9,11},{10,... | collective-permute-start | bytes 294920 | tf_op jit(solution)/shard_map/ppermute | solution.py:71
  54.8 4.7 %collective-permute-start.5 = (bf16[1,32,1536]{2,1,0:T(8,128)(2,1)S(1)}, bf16[1,32,1536]{2,1,0:T(8,128)(2,1)S(1)}, u32[]{:S(2)}, u32[]{:S(2)}) collective-permute-start(bf16[1,32,1536]{2,1,0:T(8,128)(2,1)S(1)} %get-tuple-element.66), channel_id=1, source_target_pairs={{0,2},{1,3},{2,0},{3,1},{4,6},{5,7},{6,4},{7,5},{8,10},{9,11},{10,... | collective-permute-start | bytes 294920 | tf_op jit(solution)/shard_map/ppermute | solution.py:71
  56.5 3.1 %collective-permute-start.17 = (bf16[1,2,32,1536]{3,2,1,0:T(8,128)(2,1)S(1)}, bf16[1,2,32,1536]{3,2,1,0:T(8,128)(2,1)S(1)}, u32[]{:S(2)}, u32[]{:S(2)}) collective-permute-start(bf16[1,2,32,1536]{3,2,1,0:T(8,128)(2,1)S(1)} %pad_maximum_fusion.5), channel_id=1, source_target_pairs={{0,1},{1,0},{2,3},{3,2},{4,5},{5,4},{6,7},{7,6},{8,9},{9,8},{10,11... | collective-permute-start | bytes 589832 | tf_op jit(solution)/shard_map/ppermute | solution.py:71
  59.5 3.4 %collective-permute-start.6 = (bf16[1,2,32,1536]{3,2,1,0:T(8,128)(2,1)S(1)}, bf16[1,2,32,1536]{3,2,1,0:T(8,128)(2,1)S(1)}, u32[]{:S(2)}, u32[]{:S(2)}) collective-permute-start(bf16[1,2,32,1536]{3,2,1,0:T(8,128)(2,1)S(1)} %pad_maximum_fusion.4), channel_id=1, source_target_pairs={{0,1},{1,0},{2,3},{3,2},{4,5},{5,4},{6,7},{7,6},{8,9},{9,8},{10,11... | collective-permute-start | bytes 589832 | tf_op jit(solution)/shard_map/ppermute | solution.py:71
  60.4 9.5 %collective-permute-start.18 = (bf16[1,15,384]{2,1,0:T(8,128)(2,1)S(1)}, bf16[1,15,384]{2,1,0:T(8,128)(2,1)S(1)}, u32[]{:S(2)}, u32[]{:S(2)}) collective-permute-start(bf16[1,15,384]{2,1,0:T(8,128)(2,1)S(1)} %get-tuple-element.62), channel_id=1, source_target_pairs={{0,4},{4,8},{8,12},{1,5},{5,9},{9,13},{2,6},{6,10},{10,14},{3,7},{... | collective-permute-start | bytes 34568 | tf_op jit(solution)/shard_map/ppermute | solution.py:20
  61.7 8.2 %collective-permute-start.19 = (bf16[1,15,384]{2,1,0:T(8,128)(2,1)S(1)}, bf16[1,15,384]{2,1,0:T(8,128)(2,1)S(1)}, u32[]{:S(2)}, u32[]{:S(2)}) collective-permute-start(bf16[1,15,384]{2,1,0:T(8,128)(2,1)S(1)} %get-tuple-element.63), channel_id=1, source_target_pairs={{4,0},{8,4},{12,8},{5,1},{9,5},{13,9},{6,2},{10,6},{14,10},{7,3},{... | collective-permute-start | bytes 34568 | tf_op jit(solution)/shard_map/ppermute | solution.py:21
  63.1 6.8 %copy-start.10 = (f32[384]{0:T(512)S(1)}, f32[384]{0:T(512)}, u32[]{:S(2)}) copy-start(f32[384]{0:T(512)} %get-tuple-element.8) | copy-start | bytes 4612
  63.1 6.8 %copy-start.11 = (f32[384]{0:T(512)S(1)}, f32[384]{0:T(512)}, u32[]{:S(2)}) copy-start(f32[384]{0:T(512)} %get-tuple-element.9) | copy-start | bytes 4612
  63.1 6.8 %copy-start.12 = (f32[384]{0:T(512)S(1)}, f32[384]{0:T(512)}, u32[]{:S(2)}) copy-start(f32[384]{0:T(512)} %get-tuple-element.10) | copy-start | bytes 4612
  63.1 6.8 %copy-start.13 = (f32[384]{0:T(512)S(1)}, f32[384]{0:T(512)}, u32[]{:S(2)}) copy-start(f32[384]{0:T(512)} %get-tuple-element.11) | copy-start | bytes 4612
  63.1 6.8 %copy-start.14 = (f32[384]{0:T(512)S(1)}, f32[384]{0:T(512)}, u32[]{:S(2)}) copy-start(f32[384]{0:T(512)} %get-tuple-element.12) | copy-start | bytes 4612
  63.1 6.8 %copy-start.15 = (f32[384]{0:T(512)S(1)}, f32[384]{0:T(512)}, u32[]{:S(2)}) copy-start(f32[384]{0:T(512)} %get-tuple-element.13) | copy-start | bytes 4612
  63.1 6.8 %copy-start.16 = (f32[384]{0:T(512)S(1)}, f32[384]{0:T(512)}, u32[]{:S(2)}) copy-start(f32[384]{0:T(512)} %get-tuple-element.14) | copy-start | bytes 4612
  63.1 6.8 %copy-start.17 = (f32[384]{0:T(512)S(1)}, f32[384]{0:T(512)}, u32[]{:S(2)}) copy-start(f32[384]{0:T(512)} %get-tuple-element.15) | copy-start | bytes 4612
  63.1 6.8 %copy-start.18 = (f32[384]{0:T(512)S(1)}, f32[384]{0:T(512)}, u32[]{:S(2)}) copy-start(f32[384]{0:T(512)} %get-tuple-element.16) | copy-start | bytes 4612
  63.1 6.8 %copy-start.19 = (f32[384]{0:T(512)S(1)}, f32[384]{0:T(512)}, u32[]{:S(2)}) copy-start(f32[384]{0:T(512)} %get-tuple-element.17) | copy-start | bytes 4612
  63.2 6.8 %copy-start.20 = (f32[384]{0:T(512)S(1)}, f32[384]{0:T(512)}, u32[]{:S(2)}) copy-start(f32[384]{0:T(512)} %get-tuple-element.18) | copy-start | bytes 4612
  63.2 6.8 %copy-start.21 = (f32[384]{0:T(512)S(1)}, f32[384]{0:T(512)}, u32[]{:S(2)}) copy-start(f32[384]{0:T(512)} %get-tuple-element.19) | copy-start | bytes 4612
  63.2 6.8 %copy-start.22 = (f32[384]{0:T(512)S(1)}, f32[384]{0:T(512)}, u32[]{:S(2)}) copy-start(f32[384]{0:T(512)} %get-tuple-element.20) | copy-start | bytes 4612
  63.2 6.8 %copy-start.23 = (f32[384]{0:T(512)S(1)}, f32[384]{0:T(512)}, u32[]{:S(2)}) copy-start(f32[384]{0:T(512)} %get-tuple-element.21) | copy-start | bytes 4612
  63.2 6.8 %copy-start.24 = (f32[384]{0:T(512)S(1)}, f32[384]{0:T(512)}, u32[]{:S(2)}) copy-start(f32[384]{0:T(512)} %get-tuple-element.22) | copy-start | bytes 4612
  63.2 6.8 %copy-start.25 = (f32[384]{0:T(512)S(1)}, f32[384]{0:T(512)}, u32[]{:S(2)}) copy-start(f32[384]{0:T(512)} %get-tuple-element.23) | copy-start | bytes 4612
  63.2 6.8 %copy-start.26 = (f32[384]{0:T(512)S(1)}, f32[384]{0:T(512)}, u32[]{:S(2)}) copy-start(f32[384]{0:T(512)} %get-tuple-element.24) | copy-start | bytes 4612
  63.2 6.8 %copy-start.27 = (f32[384]{0:T(512)S(1)}, f32[384]{0:T(512)}, u32[]{:S(2)}) copy-start(f32[384]{0:T(512)} %get-tuple-element.25) | copy-start | bytes 4612
  63.2 6.8 %copy-start.29 = (f32[384]{0:T(512)S(1)}, f32[384]{0:T(512)}, u32[]{:S(2)}) copy-start(f32[384]{0:T(512)} %get-tuple-element.26) | copy-start | bytes 4612
  63.2 6.8 %copy-start.30 = (f32[384]{0:T(512)S(1)}, f32[384]{0:T(512)}, u32[]{:S(2)}) copy-start(f32[384]{0:T(512)} %get-tuple-element.27) | copy-start | bytes 4612
  63.3 6.8 %copy-start.31 = (f32[384]{0:T(512)S(1)}, f32[384]{0:T(512)}, u32[]{:S(2)}) copy-start(f32[384]{0:T(512)} %get-tuple-element.28) | copy-start | bytes 4612
  64.0 7.5 %collective-permute-start.7 = (bf16[1,15,384]{2,1,0:T(8,128)(2,1)S(1)}, bf16[1,15,384]{2,1,0:T(8,128)(2,1)S(1)}, u32[]{:S(2)}, u32[]{:S(2)}) collective-permute-start(bf16[1,15,384]{2,1,0:T(8,128)(2,1)S(1)} %get-tuple-element.60), channel_id=1, source_target_pairs={{0,4},{4,8},{8,12},{1,5},{5,9},{9,13},{2,6},{6,10},{10,14},{3,7},{... | collective-permute-start | bytes 34568 | tf_op jit(solution)/shard_map/ppermute | solution.py:20
  68.6 5.6 %collective-permute-start.8 = (bf16[1,15,384]{2,1,0:T(8,128)(2,1)S(1)}, bf16[1,15,384]{2,1,0:T(8,128)(2,1)S(1)}, u32[]{:S(2)}, u32[]{:S(2)}) collective-permute-start(bf16[1,15,384]{2,1,0:T(8,128)(2,1)S(1)} %get-tuple-element.61), channel_id=1, source_target_pairs={{4,0},{8,4},{12,8},{5,1},{9,5},{13,9},{6,2},{10,6},{14,10},{7,3},{... | collective-permute-start | bytes 34568 | tf_op jit(solution)/shard_map/ppermute | solution.py:21
  71.4 4.0 %collective-permute-start.20 = (bf16[1,2,32,1536]{3,2,1,0:T(8,128)(2,1)S(1)}, bf16[1,2,32,1536]{3,2,1,0:T(8,128)(2,1)S(1)}, u32[]{:S(2)}, u32[]{:S(2)}) collective-permute-start(bf16[1,2,32,1536]{3,2,1,0:T(8,128)(2,1)S(1)} %dynamic-slice_bitcast_fusion), channel_id=1, source_target_pairs={{0,1},{1,0},{2,3},{3,2},{4,5},{5,4},{6,7},{7,6},{8,9},{9,8},{10,11... | collective-permute-start | bytes 589832 | tf_op jit(solution)/shard_map/ppermute | solution.py:59
  75.3 1.5 %collective-permute-start.9 = (bf16[1,2,32,1536]{3,2,1,0:T(8,128)(2,1)S(1)}, bf16[1,2,32,1536]{3,2,1,0:T(8,128)(2,1)S(1)}, u32[]{:S(2)}, u32[]{:S(2)}) collective-permute-start(bf16[1,2,32,1536]{3,2,1,0:T(8,128)(2,1)S(1)} %dynamic-slice_bitcast_fusion.2), channel_id=1, source_target_pairs={{0,1},{1,0},{2,3},{3,2},{4,5},{5,4},{6,7},{7,6},{8,9},{9,8},{10,11... | collective-permute-start | bytes 589832 | tf_op jit(solution)/shard_map/ppermute | solution.py:59
  75.5 5.7 %collective-permute-start.21 = (bf16[1,32,1536]{2,1,0:T(8,128)(2,1)S(1)}, bf16[1,32,1536]{2,1,0:T(8,128)(2,1)S(1)}, u32[]{:S(2)}, u32[]{:S(2)}) collective-permute-start(bf16[1,32,1536]{2,1,0:T(8,128)(2,1)S(1)} %fusion.65), channel_id=1, source_target_pairs={{0,2},{1,3},{2,0},{3,1},{4,6},{5,7},{6,4},{7,5},{8,10},{9,11},{10,... | collective-permute-start | bytes 294920 | tf_op jit(solution)/shard_map/ppermute | solution.py:59
  76.9 5.9 %collective-permute-start.10 = (bf16[1,32,1536]{2,1,0:T(8,128)(2,1)S(1)}, bf16[1,32,1536]{2,1,0:T(8,128)(2,1)S(1)}, u32[]{:S(2)}, u32[]{:S(2)}) collective-permute-start(bf16[1,32,1536]{2,1,0:T(8,128)(2,1)S(1)} %fusion.63), channel_id=1, source_target_pairs={{0,2},{1,3},{2,0},{3,1},{4,6},{5,7},{6,4},{7,5},{8,10},{9,11},{10,... | collective-permute-start | bytes 294920 | tf_op jit(solution)/shard_map/ppermute | solution.py:59
  (19 other events, 107.6 us)

commit v3 on v1

--- a/solution.py
+++ b/solution.py
@@ -81,15 +81,15 @@
     left = [(i, (i - 1) % count) for i in range(count)]
     right_steps = count // 2
     left_steps = count - 1 - right_steps
-    from_left, from_right = [], []
+    blocks = [(0, x)]
     going_right, going_left = x, x
     for step in range(right_steps):
         going_right = lax.ppermute(going_right, axis, right)
-        from_left.append(going_right)
+        blocks.append((count - 1 - step, going_right))
         if step < left_steps:
             going_left = lax.ppermute(going_left, axis, left)
-            from_right.append(going_left)
-    return jnp.stack([x] + from_right + from_left[::-1], axis=0)
+            blocks.append((step + 1, going_left))
+    return blocks
 
 
 def shards(
@@ -118,26 +118,34 @@
     ).astype(jnp.bfloat16)
     queries = projected[0]
     query_heads = queries.reshape(records, frames_here, head_count, HEAD_DIM)
-    kv_all = ring_gather(projected[1:], "ctx")
-    key_heads = kv_all[:, 0].reshape(ctx_count, records, frames_here, head_count, HEAD_DIM)
-    value_heads = kv_all[:, 1].reshape(ctx_count, records, frames_here, head_count, HEAD_DIM)
-    scores = (
-        jnp.einsum("sqhe,cskhe->shqck", query_heads, key_heads, preferred_element_type=jnp.float32)
-        * score_scale
-    )
-    block_rank = (ctx_rank + jnp.arange(ctx_count, dtype=jnp.int32)) % ctx_count
-    positions = block_rank[:, None] * frames_here + jnp.arange(frames_here, dtype=jnp.int32)
-    is_live = positions[None] < frame_counts[:, None, None]
-    scores = jnp.where(is_live[:, None, None], scores, masked_score)
-    row_max = jnp.max(scores, axis=(-2, -1), keepdims=True)
-    weights = jnp.exp(scores - row_max)
-    row_sum = jnp.sum(weights, axis=(-2, -1))
-    contrib = jnp.einsum(
-        "shqck,cskhe->shqe",
-        weights.astype(jnp.bfloat16),
-        value_heads,
-        preferred_element_type=jnp.float32,
-    )
+    blocks = ring_gather(projected[1:], "ctx")
+    frame_steps = jnp.arange(frames_here, dtype=jnp.int32)
+    block_scores, block_values = [], []
+    for offset, block in blocks:
+        key_heads = block[0].reshape(records, frames_here, head_count, HEAD_DIM)
+        block_values.append(block[1].reshape(records, frames_here, head_count, HEAD_DIM))
+        scores = (
+            jnp.einsum("sqhe,skhe->shqk", query_heads, key_heads, preferred_element_type=jnp.float32)
+            * score_scale
+        )
+        block_rank = (ctx_rank + offset) % ctx_count
+        positions = block_rank * frames_here + frame_steps
+        is_live = positions[None, :] < frame_counts[:, None]
+        block_scores.append(jnp.where(is_live[:, None, None, :], scores, masked_score))
+    row_max = block_scores[0].max(axis=-1)
+    for scores in block_scores[1:]:
+        row_max = jnp.maximum(row_max, scores.max(axis=-1))
+    row_sum = 0.0
+    contrib = 0.0
+    for scores, value_heads in zip(block_scores, block_values):
+        weights = jnp.exp(scores - row_max[..., None])
+        row_sum = row_sum + jnp.sum(weights, axis=-1)
+        contrib = contrib + jnp.einsum(
+            "shqk,skhe->shqe",
+            weights.astype(jnp.bfloat16),
+            value_heads,
+            preferred_element_type=jnp.float32,
+        )
     attended = (contrib / row_sum[..., None]).astype(jnp.bfloat16)
     attended = attended.transpose(0, 2, 1, 3).reshape(records, frames_here, head_count * HEAD_DIM)
     attn_part = jnp.einsum("stc,cd->std", attended, w_out, preferred_element_type=jnp.float32)

time: 79.3 us -> 89.5 us (1.13)
  local copies, waits for them, and re-layouts: 6.9 us -> 20.9 us
  waiting for transfers between devices: 39.9 us -> 29.1 us
  starting transfers between devices: 13 us -> 17 us
  matrix products: 7.34 us -> 11.2 us
  other arithmetic: 11.2 us -> 10 us
    ppermute x2, waiting for transfers between devices: 13.2 us -> 0.01 us  [ring_gather(): going_right = lax.ppermute(going_right, axis, right)]
    slice x3 -> x13, local copies, waits for them, and re-layouts: 3.19 us -> 14.7 us  [the longest x7 9.8 us: shards(): block[1].reshape(records, frames_here, head_count, HEAD_DIM)]
    ppermute x1, waiting for transfers between devices: 4.09 us -> 9.48 us  [ring_gather(): going_left = lax.ppermute(going_left, axis, left)]
    dot_general x2 -> x8, matrix products: 1.45 us -> 6.48 us  [the longest x4 4.73 us: shards(): jnp.einsum('sqhe,skhe->shqk', query_heads, key_heads, preferred_element_t...]
    ppermute x1, waiting for transfers between devices: 3.37 us -> 0.01 us  [with_halo(): after = lax.ppermute(initial, axis, down)]
    ppermute x1, starting transfers between devices: 1.62 us -> 4.55 us  [with_halo(): before = lax.ppermute(last, axis, up)]
    unnamed x20 -> x34, local copies, waits for them, and re-layouts: 0.91 us -> 3.5 us
    another operation x1 -> x0, other arithmetic: 1.24 us -> none  [ring_gather(): return jnp.stack([x] + from_right + from_left[::-1], axis=0)]
  transfers between devices with their start and end apart: 11 -> 11, of which waited for: 10 -> 8; matrix products, arithmetic and copies ran while one was open for 4% -> 18% of each run, Pallas kernels for 0% -> 0%
where the time goes in v3:
time: 89.5 us; the launch traced here: 88.7 us
  waiting for transfers between devices  29.1 us (33%)
  local copies, waits for them, and re-layouts  20.9 us (23%)
  starting transfers between devices  17 us (19%)
  matrix products  11.2 us (13%)
  other arithmetic  10 us (11%)
    ppermute x4, waiting for transfers between devices, reduce_scatter_rows(): lax.ppermute(send.astype(jnp.bfloat16), axis, xor_pairs(count, 1 << b))  14 us
    slice x7, local copies, waits for them, and re-layouts, shards(): block[1].reshape(records, frames_here, head_count, HEAD_DIM)  9.8 us
    ppermute x1, waiting for transfers between devices, ring_gather(): going_left = lax.ppermute(going_left, axis, left)  9.48 us
    ppermute x2, waiting for transfers between devices, all_gather_rows(): got = lax.ppermute(acc, axis, xor_pairs(count, 1 << b))  5.22 us
    dot_general x4, matrix products, shards(): jnp.einsum('sqhe,skhe->shqk', query_heads, key_heads, preferred_element_t...  4.73 us
    ppermute x1, starting transfers between devices, with_halo(): before = lax.ppermute(last, axis, up)  4.55 us
    slice x5, local copies, waits for them, and re-layouts, shards(): key_heads = block[0].reshape(records, frames_here, head_count, HEAD_DIM)  4.21 us
    ppermute x2, starting transfers between devices, ring_gather(): going_right = lax.ppermute(going_right, axis, right)  4.21 us
  transfers between devices with their start and end apart: 11, of which 8 were waited for; matrix products, arithmetic and copies ran while one was open for 18% of the time, Pallas kernels for 0%

profile of v3, /device:TPU:0, one launch (start us, length us, event | category | flops | bytes accessed | tf_op | source)
XLA Modules:
  0.0 88.7 jit_solution(10670347275228308997)
XLA Ops:
  0.0 1.5 %convert_reduce_fusion = f32[2,128]{1,0:T(2,128)S(1)} fusion(bf16[2,128,1536]{2,1,0:T(8,128)(2,1)} %param.12), kind=kLoop, calls=%fused_computation.7 | loop fusion | flops 786176 | bytes 787456 | tf_op jit(solution)/shard_map/reduce_sum | solution.py:27
  1.5 1.5 %fusion.6 = f32[2,128]{1,0:T(2,128)S(1)} fusion(bf16[2,128,1536]{2,1,0:T(8,128)(2,1)} %param.12, f32[2,128]{1,0:T(2,128)S(1)} %broadcast_multiply_fusion.1), kind=kLoop, calls=%fused_computation.10 | loop fusion | flops 1572608 | bytes 788480 | tf_op jit(solution)/shard_map/reduce_sum | solution.py:29
  3.0 0.9 fusion.19
  3.9 0.7 slice.335
  4.6 3.0 %collective-permute-start = (bf16[2,2,128,256]{3,2,0,1:T(8,128)(2,1)}, bf16[2,2,128,256]{3,2,0,1:T(8,128)(2,1)}, u32[]{:S(2)}, u32[]{:S(2)}) collective-permute-start(bf16[2,2,128,256]{3,2,0,1:T(8,128)(2,1)} %slice.335), channel_id=1, source_target_pairs={{0,4},{4,8},{8,12},{12,0},{1,5},{5,9},{9,13},{13,1},{2,6},{6,10},{... | collective-permute-start | bytes 786440 | tf_op jit(solution)/shard_map/ppermute | solution.py:87
  7.6 2.0 %collective-permute-start.1 = (bf16[2,2,128,256]{3,2,0,1:T(8,128)(2,1)}, bf16[2,2,128,256]{3,2,0,1:T(8,128)(2,1)S(1)}, u32[]{:S(2)}, u32[]{:S(2)}) collective-permute-start(bf16[2,2,128,256]{3,2,0,1:T(8,128)(2,1)} %slice.335), channel_id=1, source_target_pairs={{0,12},{4,0},{8,4},{12,8},{1,13},{5,1},{9,5},{13,9},{2,14},{6,2},{... | collective-permute-start | bytes 786440 | tf_op jit(solution)/shard_map/ppermute | solution.py:90
  9.8 0.7 broadcast_compare_fusion
  10.4 0.8 copy.40
  11.7 9.5 %collective-permute-done.1 = bf16[2,2,128,256]{3,2,0,1:T(8,128)(2,1)S(1)} collective-permute-done((bf16[2,2,128,256]{3,2,0,1:T(8,128)(2,1)}, bf16[2,2,128,256]{3,2,0,1:T(8,128)(2,1)S(1)}, u32[]{:S(2)}, u32[]{:S(2)}) %collective-permute-start.1) | collective-permute-done | bytes 262176 | tf_op jit(solution)/shard_map/ppermute | solution.py:90
  21.2 0.7 fusion.97
  21.9 0.8 copy.38
  22.6 1.2 %fusion.101 = (f32[2,4,128]{2,1,0:T(4,128)S(1)}, f32[2,4,128,128]{2,3,1,0:T(8,128)S(1)}) fusion(bf16[2,128,4,64]{1,3,2,0:T(8,128)(2,1)S(1)} %bitcast.119, bf16[2,128,4,64]{1,3,2,0:T(8,128)(2,1)} %bitcast.131, pred[2,128]{1,0:T(4,128)(4,1)S(1)} %get-tuple-element.65), kind=kOutput, calls=%fused_computation.229 | convolution fusion | flops 17169408 | bytes 790784 | tf_op jit(solution)/shard_map/sqhe,skhe->shqk/dot_general | solution.py:128
  23.9 1.2 %collective-permute-start.2 = (bf16[2,2,128,256]{3,2,0,1:T(8,128)(2,1)}, bf16[2,2,128,256]{3,2,0,1:T(8,128)(2,1)}, u32[]{:S(2)}, u32[]{:S(2)}) collective-permute-start(bf16[2,2,128,256]{3,2,0,1:T(8,128)(2,1)} %collective-permute-done), channel_id=1, source_target_pairs={{0,4},{4,8},{8,12},{12,0},{1,5},{5,9},{9,13},{13,1},{2,6},{6,10},{... | collective-permute-start | bytes 786440 | tf_op jit(solution)/shard_map/ppermute | solution.py:87
  25.0 1.7 %fusion.98 = (bf16[1,2,128,256]{3,2,0,1:T(8,128)(2,1)}, bf16[1,2,128,256]{3,2,0,1:T(8,128)(2,1)}) fusion(bf16[2,2,128,256]{3,2,0,1:T(8,128)(2,1)} %collective-permute-done), kind=kLoop, calls=%fused_computation.226 | loop fusion | bytes 524288 | tf_op jit(solution)/shard_map/slice | solution.py:126
  26.7 1.7 %copy.37 = bf16[1,2,128,256]{2,3,1,0:T(8,128)(2,1)} copy(bf16[1,2,128,256]{3,2,0,1:T(8,128)(2,1)} %get-tuple-element.58) | data formatting | bytes 262144 | tf_op jit(solution)/shard_map/slice | solution.py:125
  28.4 1.7 %copy.42 = bf16[1,2,128,256]{2,3,1,0:T(8,128)(2,1)} copy(bf16[1,2,128,256]{3,2,0,1:T(8,128)(2,1)} %get-tuple-element.57) | data formatting | bytes 262144 | tf_op jit(solution)/shard_map/slice | solution.py:126
  30.0 1.7 %copy.44 = bf16[1,2,128,256]{2,3,1,0:T(8,128)(2,1)} copy(bf16[1,2,128,256]{3,2,0,1:T(8,128)(2,1)} %get-tuple-element.55) | data formatting | bytes 262144 | tf_op jit(solution)/shard_map/slice | solution.py:126
  31.7 2.0 %fusion.103 = (f32[2,4,128]{2,1,0:T(4,128)S(1)}, f32[2,4,128,128]{2,3,1,0:T(8,128)}) fusion(bf16[2,128,4,64]{1,3,2,0:T(8,128)(2,1)S(1)} %bitcast.120, bf16[2,128,4,64]{1,3,2,0:T(8,128)(2,1)} %bitcast.129, pred[2,128]{1,0:T(4,128)(4,1)} %get-tuple-element.64), kind=kOutput, calls=%fused_computation.231 | convolution fusion | flops 17169408 | bytes 790784 | tf_op jit(solution)/shard_map/sqhe,skhe->shqk/dot_general | solution.py:128
  33.7 1.7 %fusion.96 = (bf16[1,2,128,256]{3,2,0,1:T(8,128)(2,1)}, bf16[1,2,128,256]{3,2,0,1:T(8,128)(2,1)}) fusion(bf16[2,2,128,256]{3,2,0,1:T(8,128)(2,1)} %collective-permute-done.2), kind=kLoop, calls=%fused_computation.224 | loop fusion | bytes 524288 | tf_op jit(solution)/shard_map/slice | solution.py:126
  35.4 1.7 %copy.39 = bf16[1,2,128,256]{2,3,1,0:T(8,128)(2,1)} copy(bf16[1,2,128,256]{3,2,0,1:T(8,128)(2,1)} %get-tuple-element.54) | data formatting | bytes 262144 | tf_op jit(solution)/shard_map/slice | solution.py:125
  37.0 1.7 %copy.46 = bf16[1,2,128,256]{2,3,1,0:T(8,128)(2,1)} copy(bf16[1,2,128,256]{3,2,0,1:T(8,128)(2,1)} %get-tuple-element.53) | data formatting | bytes 262144 | tf_op jit(solution)/shard_map/slice | solution.py:126
  38.7 1.3 %fusion.100 = (f32[2,4,128]{2,1,0:T(4,128)S(1)}, f32[2,4,128,128]{2,3,1,0:T(8,128)S(1)}) fusion(bf16[2,128,4,64]{1,3,2,0:T(8,128)(2,1)S(1)} %bitcast.121, bf16[2,128,4,64]{1,3,2,0:T(8,128)(2,1)} %bitcast.130, pred[2,128]{1,0:T(4,128)(4,1)} %get-tuple-element.66), kind=kOutput, calls=%fused_computation.228 | convolution fusion | flops 17169408 | bytes 790784 | tf_op jit(solution)/shard_map/sqhe,skhe->shqk/dot_general | solution.py:128
  40.0 1.1 %fusion.54 = f32[2,4,128,64]{2,3,1,0:T(8,128)S(1)} fusion(bf16[2,128,4,64]{1,3,2,0:T(8,128)(2,1)} %bitcast.125, f32[2,4,128,128]{2,3,1,0:T(8,128)S(1)} %get-tuple-element.73, f32[2,4,128]{2,1,0:T(4,128)S(1)} %bitcast.136), kind=kOutput, calls=%fused_computation.105 | convolution fusion | flops 17039360 | bytes 921600 | tf_op jit(solution)/shard_map/shqk,skhe->shqe/dot_general | solution.py:143
  42.5 0.4 copy-done.3
  43.5 1.7 %collective-permute-done.3 = bf16[2,2,32,1536]{3,2,0,1:T(8,128)(2,1)S(1)} collective-permute-done((bf16[2,2,32,1536]{3,2,0,1:T(8,128)(2,1)S(1)}, bf16[2,2,32,1536]{3,2,0,1:T(8,128)(2,1)S(1)}, u32[]{:S(2)}, u32[]{:S(2)}) %collective-permute-start.3) | collective-permute-done | bytes 393248 | tf_op jit(solution)/shard_map/ppermute | solution.py:59
  45.2 0.7 copy-done.6
  45.9 1.1 %convert_add_fusion.1 = f32[2,2,32,1536]{3,2,0,1:T(8,128)S(1)} fusion(bf16[2,2,32,1536]{3,2,0,1:T(8,128)(2,1)} %copy-done.6, bf16[2,2,1,32,1536]{4,3,2,1,0:T(8,128)(2,1)S(1)} %get-tuple-element.46), kind=kLoop, calls=%fused_computation.62 | loop fusion | flops 589824 | bytes 1572864 | tf_op jit(solution)/shard_map/add | solution.py:60
  47.1 1.6 %collective-permute-start.4 = (bf16[2,32,1536]{2,1,0:T(8,128)(2,1)S(1)}, bf16[2,32,1536]{2,1,0:T(8,128)(2,1)}, u32[]{:S(2)}, u32[]{:S(2)}) collective-permute-start(bf16[2,32,1536]{2,1,0:T(8,128)(2,1)S(1)} %fusion.60), channel_id=1, source_target_pairs={{0,2},{1,3},{2,0},{3,1},{4,6},{5,7},{6,4},{7,5},{8,10},{9,11},{10,... | collective-permute-start | bytes 589832 | tf_op jit(solution)/shard_map/ppermute | solution.py:59
  48.6 5.6 %collective-permute-done.4 = bf16[2,32,1536]{2,1,0:T(8,128)(2,1)} collective-permute-done((bf16[2,32,1536]{2,1,0:T(8,128)(2,1)S(1)}, bf16[2,32,1536]{2,1,0:T(8,128)(2,1)}, u32[]{:S(2)}, u32[]{:S(2)}) %collective-permute-start.4) | collective-permute-done | bytes 196640 | tf_op jit(solution)/shard_map/ppermute | solution.py:59
  54.2 1.2 %fusion.93 = (f32[2,32]{1,0:T(2,128)S(1)}, f32[2,32,1536]{2,1,0:T(8,128)S(1)}) fusion(bf16[2,32,1536]{2,1,0:T(8,128)(2,1)} %collective-permute-done.4, f32[2,2,32,1536]{3,2,0,1:T(8,128)S(1)} %convert_add_fusion.1, s32[]{:T(128)S(6)} %select_n.96, bf16[2,128,1536]{2,1,0:T(8,128)(2,1)} %param.12, s32[]{:T(128)S(6)} %select_n.85), kind=kLoop, calls=%fused_computation.222 | loop fusion | flops 491456 | bytes 1179912 | tf_op jit(solution)/shard_map/reduce_sum | solution.py:27
  55.7 1.6 %collective-permute-start.5 = (bf16[2,32,1536]{2,1,0:T(8,128)(2,1)S(1)}, bf16[2,32,1536]{2,1,0:T(8,128)(2,1)S(1)}, u32[]{:S(2)}, u32[]{:S(2)}) collective-permute-start(bf16[2,32,1536]{2,1,0:T(8,128)(2,1)S(1)} %multiply_convert_fusion.1), channel_id=1, source_target_pairs={{0,2},{1,3},{2,0},{3,1},{4,6},{5,7},{6,4},{7,5},{8,10},{9,11},{10,... | collective-permute-start | bytes 589832 | tf_op jit(solution)/shard_map/ppermute | solution.py:71
  57.2 4.6 %collective-permute-done.5 = bf16[2,32,1536]{2,1,0:T(8,128)(2,1)S(1)} collective-permute-done((bf16[2,32,1536]{2,1,0:T(8,128)(2,1)S(1)}, bf16[2,32,1536]{2,1,0:T(8,128)(2,1)S(1)}, u32[]{:S(2)}, u32[]{:S(2)}) %collective-permute-start.5) | collective-permute-done | bytes 196640 | tf_op jit(solution)/shard_map/ppermute | solution.py:71
  62.2 1.2 %slice_reduce_fusion.30 = (f32[384]{0:T(512)S(1)}, f32[384]{0:T(512)S(1)}, f32[384]{0:T(512)S(1)}, f32[384]{0:T(512)S(1)}, f32[384]{0:T(512)S(1)}, /*index=5*/f3...) fusion(f32[31,384]{1,0:T(8,128)} %param.19), kind=kLoop, calls=%fused_computation.202 | loop fusion | bytes 58368 | tf_op jit(solution)/shard_map/slice | solution.py:172
  63.4 0.6 collective-permute-done.6
  64.0 1.1 %select_bitcast_fusion.1 = (bf16[2,2,1,32,1536]{4,3,0,1,2:T(8,128)(2,1)S(1)}, bf16[2,2,1,32,1536]{4,3,0,1,2:T(8,128)(2,1)S(1)}) fusion(bf16[2,2,32,1536]{3,2,0,1:T(8,128)(2,1)} %collective-permute-done.6, pred[]{:T(512)S(6)} %eq.11, bf16[2,1,32,1536]{3,2,0,1:T(8,128)(2,1)S(1)} %get-tuple-element.49, bf16[2,1,32,1536]{3,2,0,1:T(8,128)(2,1)S(1)} %get-tuple-element.48), kind=kLoop, calls=%fused_computation.100 | loop fusion | flops 589824 | bytes 1572865 | tf_op jit(solution)/shard_map/stack | solution.py:74
  65.2 1.5 %copy-done.12 = bf16[2,1536,384]{2,1,0:T(8,128)(2,1)S(1)} copy-done((bf16[2,1536,384]{2,1,0:T(8,128)(2,1)S(1)}, bf16[2,1536,384]{2,1,0:T(8,128)(2,1)}, u32[]{:S(2)}) %copy-start.12) | copy-done | bytes 2359320
  66.7 0.8 fusion.9
  67.7 1.3 %collective-permute-start.8 = (bf16[2,15,384]{2,1,0:T(8,128)(2,1)S(1)}, bf16[2,15,384]{2,1,0:T(8,128)(2,1)S(1)}, u32[]{:S(2)}, u32[]{:S(2)}) collective-permute-start(bf16[2,15,384]{2,1,0:T(8,128)(2,1)S(1)} %get-tuple-element.60), channel_id=1, source_target_pairs={{4,0},{8,4},{12,8},{5,1},{9,5},{13,9},{6,2},{10,6},{14,10},{7,3},{... | collective-permute-start | bytes 69128 | tf_op jit(solution)/shard_map/ppermute | solution.py:21
  69.0 4.5 %collective-permute-start.7 = (bf16[2,15,384]{2,1,0:T(8,128)(2,1)S(1)}, bf16[2,15,384]{2,1,0:T(8,128)(2,1)S(1)}, u32[]{:S(2)}, u32[]{:S(2)}) collective-permute-start(bf16[2,15,384]{2,1,0:T(8,128)(2,1)S(1)} %get-tuple-element.59), channel_id=1, source_target_pairs={{0,4},{4,8},{8,12},{1,5},{5,9},{9,13},{2,6},{6,10},{10,14},{3,7},{... | collective-permute-start | bytes 69128 | tf_op jit(solution)/shard_map/ppermute | solution.py:20
  73.5 1.0 %slice_reduce_fusion.29 = (f32[384]{0:T(512)S(1)}, f32[384]{0:T(512)S(1)}, f32[384]{0:T(512)S(1)}, f32[384]{0:T(512)S(1)}, f32[384]{0:T(512)S(1)}, /*index=5*/f3...) fusion(f32[31,384]{1,0:T(8,128)} %param.19), kind=kLoop, calls=%fused_computation.201 | loop fusion | bytes 36864 | tf_op jit(solution)/shard_map/slice | solution.py:172
  74.6 0.5 collective-permute-done.7
  75.0 2.7 %convolution_convert_fusion.1 = bf16[2,128,1536]{2,1,0:T(8,128)(2,1)S(1)} fusion(bf16[384,1536]{1,0:T(8,128)(2,1)S(1)} %copy-done.13, bf16[2,128,384]{2,1,0:T(8,128)(2,1)S(1)} %bitcast_select_fusion, bf16[2,15,384]{2,1,0:T(8,128)(2,1)S(1)} %collective-permute-done.8, bf16[2,15,384]{2,1,0:T(8,128)(2,1)S(1)} %collective-permute-done.7, f32[384]{0:T(512)S(1)} %copy-done.15, ...), kind=kOutput, calls=%fused_computation.1 | convolution fusion | flops 320962560 | bytes 2259456 | tf_op jit(solution)/shard_map/stc,cd->std/dot_general | solution.py:175
  78.0 0.5 copy-done.9
  78.4 1.3 %collective-permute-done.9 = bf16[2,2,32,1536]{3,2,0,1:T(8,128)(2,1)} collective-permute-done((bf16[2,2,32,1536]{3,2,0,1:T(8,128)(2,1)S(1)}, bf16[2,2,32,1536]{3,2,0,1:T(8,128)(2,1)}, u32[]{:S(2)}, u32[]{:S(2)}) %collective-permute-start.9) | collective-permute-done | bytes 393248 | tf_op jit(solution)/shard_map/ppermute | solution.py:59
  79.8 1.1 %convert_add_fusion = f32[2,2,32,1536]{3,2,0,1:T(8,128)S(1)} fusion(bf16[2,2,32,1536]{3,2,0,1:T(8,128)(2,1)} %collective-permute-done.9, bf16[2,2,1,32,1536]{4,3,2,1,0:T(8,128)(2,1)S(1)} %get-tuple-element.42), kind=kLoop, calls=%fused_computation.61 | loop fusion | flops 589824 | bytes 1572864 | tf_op jit(solution)/shard_map/add | solution.py:60
  80.9 1.6 %collective-permute-start.10 = (bf16[2,32,1536]{2,1,0:T(8,128)(2,1)S(1)}, bf16[2,32,1536]{2,1,0:T(8,128)(2,1)S(1)}, u32[]{:S(2)}, u32[]{:S(2)}) collective-permute-start(bf16[2,32,1536]{2,1,0:T(8,128)(2,1)S(1)} %fusion.61), channel_id=1, source_target_pairs={{0,2},{1,3},{2,0},{3,1},{4,6},{5,7},{6,4},{7,5},{8,10},{9,11},{10,... | collective-permute-start | bytes 589832 | tf_op jit(solution)/shard_map/ppermute | solution.py:59
  82.6 5.4 %collective-permute-done.10 = bf16[2,32,1536]{2,1,0:T(8,128)(2,1)S(1)} collective-permute-done((bf16[2,32,1536]{2,1,0:T(8,128)(2,1)S(1)}, bf16[2,32,1536]{2,1,0:T(8,128)(2,1)S(1)}, u32[]{:S(2)}, u32[]{:S(2)}) %collective-permute-start.10) | collective-permute-done | bytes 196640 | tf_op jit(solution)/shard_map/ppermute | solution.py:59
  87.9 0.8 fusion.48
  (71 shorter events, 3.8 us)
Async XLA Ops:
  0.0 3.0 %copy-start = (bf16[3,1536,256]{2,1,0:T(8,128)(2,1)S(1)}, bf16[3,1536,256]{2,1,0:T(8,128)(2,1)}, u32[]{:S(2)}) copy-start(bf16[3,1536,256]{2,1,0:T(8,128)(2,1)} %param.15) | copy-start | bytes 7077892
  0.0 3.0 %copy-start.2 = (bf16[2,128,1536]{2,1,0:T(8,128)(2,1)S(1)}, bf16[2,128,1536]{2,1,0:T(8,128)(2,1)}, u32[]{:S(2)}) copy-start(bf16[2,128,1536]{2,1,0:T(8,128)(2,1)} %param.12) | copy-start | bytes 2359300
  0.0 3.0 %copy-start.14 = (f32[1536]{0:T(1024)S(1)}, f32[1536]{0:T(1024)}, u32[]{:S(2)}) copy-start(f32[1536]{0:T(1024)} %param.14) | copy-start | bytes 18436
  3.0 6.8 %copy-start.10 = (s32[2]{0:T(128)S(1)}, s32[2]{0:T(128)}, u32[]{:S(2)}) copy-start(s32[2]{0:T(128)} %param.13) | copy-start | bytes 28
  4.6 19.3 %collective-permute-start = (bf16[2,2,128,256]{3,2,0,1:T(8,128)(2,1)}, bf16[2,2,128,256]{3,2,0,1:T(8,128)(2,1)}, u32[]{:S(2)}, u32[]{:S(2)}) collective-permute-start(bf16[2,2,128,256]{3,2,0,1:T(8,128)(2,1)} %slice.335), channel_id=1, source_target_pairs={{0,4},{4,8},{8,12},{12,0},{1,5},{5,9},{9,13},{13,1},{2,6},{6,10},{... | collective-permute-start | bytes 786440 | tf_op jit(solution)/shard_map/ppermute | solution.py:87
  7.6 13.6 %collective-permute-start.1 = (bf16[2,2,128,256]{3,2,0,1:T(8,128)(2,1)}, bf16[2,2,128,256]{3,2,0,1:T(8,128)(2,1)S(1)}, u32[]{:S(2)}, u32[]{:S(2)}) collective-permute-start(bf16[2,2,128,256]{3,2,0,1:T(8,128)(2,1)} %slice.335), channel_id=1, source_target_pairs={{0,12},{4,0},{8,4},{12,8},{1,13},{5,1},{9,5},{13,9},{2,14},{6,2},{... | collective-permute-start | bytes 786440 | tf_op jit(solution)/shard_map/ppermute | solution.py:90
  23.9 9.8 %collective-permute-start.2 = (bf16[2,2,128,256]{3,2,0,1:T(8,128)(2,1)}, bf16[2,2,128,256]{3,2,0,1:T(8,128)(2,1)}, u32[]{:S(2)}, u32[]{:S(2)}) collective-permute-start(bf16[2,2,128,256]{3,2,0,1:T(8,128)(2,1)} %collective-permute-done), channel_id=1, source_target_pairs={{0,4},{4,8},{8,12},{12,0},{1,5},{5,9},{9,13},{13,1},{2,6},{6,10},{... | collective-permute-start | bytes 786440 | tf_op jit(solution)/shard_map/ppermute | solution.py:87
  38.7 2.4 %copy-start.1 = (f32[2,4,128,128]{2,3,1,0:T(8,128)S(1)}, f32[2,4,128,128]{2,3,1,0:T(8,128)}, u32[]{:S(2)}) copy-start(f32[2,4,128,128]{2,3,1,0:T(8,128)} %get-tuple-element.75) | copy-start | bytes 1572868
  38.7 2.4 %copy-start.5 = (bf16[1,2,128,256]{2,3,1,0:T(8,128)(2,1)S(1)}, bf16[1,2,128,256]{2,3,1,0:T(8,128)(2,1)}, u32[]{:S(2)}) copy-start(bf16[1,2,128,256]{2,3,1,0:T(8,128)(2,1)} %copy.42) | copy-start | bytes 393220
  41.1 0.9 %copy-start.4 = (bf16[1,2,128,256]{2,3,1,0:T(8,128)(2,1)S(1)}, bf16[1,2,128,256]{2,3,1,0:T(8,128)(2,1)}, u32[]{:S(2)}) copy-start(bf16[1,2,128,256]{2,3,1,0:T(8,128)(2,1)} %copy.44) | copy-start | bytes 393220
  41.3 0.9 %copy-start.7 = (bf16[1,2,128,256]{2,3,1,0:T(8,128)(2,1)S(1)}, bf16[1,2,128,256]{2,3,1,0:T(8,128)(2,1)}, u32[]{:S(2)}) copy-start(bf16[1,2,128,256]{2,3,1,0:T(8,128)(2,1)} %copy.46) | copy-start | bytes 393220
  41.7 1.2 %copy-start.3 = (bf16[256,1536]{1,0:T(8,128)(2,1)S(1)}, bf16[256,1536]{1,0:T(8,128)(2,1)}, u32[]{:S(2)}) copy-start(bf16[256,1536]{1,0:T(8,128)(2,1)} %param.16) | copy-start | bytes 2359300
  43.4 1.8 %collective-permute-start.3 = (bf16[2,2,32,1536]{3,2,0,1:T(8,128)(2,1)S(1)}, bf16[2,2,32,1536]{3,2,0,1:T(8,128)(2,1)S(1)}, u32[]{:S(2)}, u32[]{:S(2)}) collective-permute-start(bf16[2,2,32,1536]{3,2,0,1:T(8,128)(2,1)S(1)} %bitcast.132), channel_id=1, source_target_pairs={{0,1},{1,0},{2,3},{3,2},{4,5},{5,4},{6,7},{7,6},{8,9},{9,8},{10,11... | collective-permute-start | bytes 1179656 | tf_op jit(solution)/shard_map/ppermute | solution.py:59
  45.2 0.7 copy-start.6
  45.9 9.6 %copy-start.8 = (f32[1536]{0:T(1024)S(1)}, f32[1536]{0:T(1024)}, u32[]{:S(2)}) copy-start(f32[1536]{0:T(1024)} %param.17) | copy-start | bytes 18436
  47.1 7.1 %collective-permute-start.4 = (bf16[2,32,1536]{2,1,0:T(8,128)(2,1)S(1)}, bf16[2,32,1536]{2,1,0:T(8,128)(2,1)}, u32[]{:S(2)}, u32[]{:S(2)}) collective-permute-start(bf16[2,32,1536]{2,1,0:T(8,128)(2,1)S(1)} %fusion.60), channel_id=1, source_target_pairs={{0,2},{1,3},{2,0},{3,1},{4,6},{5,7},{6,4},{7,5},{8,10},{9,11},{10,... | collective-permute-start | bytes 589832 | tf_op jit(solution)/shard_map/ppermute | solution.py:59
  55.7 6.2 %collective-permute-start.5 = (bf16[2,32,1536]{2,1,0:T(8,128)(2,1)S(1)}, bf16[2,32,1536]{2,1,0:T(8,128)(2,1)S(1)}, u32[]{:S(2)}, u32[]{:S(2)}) collective-permute-start(bf16[2,32,1536]{2,1,0:T(8,128)(2,1)S(1)} %multiply_convert_fusion.1), channel_id=1, source_target_pairs={{0,2},{1,3},{2,0},{3,1},{4,6},{5,7},{6,4},{7,5},{8,10},{9,11},{10,... | collective-permute-start | bytes 589832 | tf_op jit(solution)/shard_map/ppermute | solution.py:71
  62.1 1.9 %collective-permute-start.6 = (bf16[2,2,32,1536]{3,2,0,1:T(8,128)(2,1)S(1)}, bf16[2,2,32,1536]{3,2,0,1:T(8,128)(2,1)}, u32[]{:S(2)}, u32[]{:S(2)}) collective-permute-start(bf16[2,2,32,1536]{3,2,0,1:T(8,128)(2,1)S(1)} %pad_maximum_fusion.1), channel_id=1, source_target_pairs={{0,1},{1,0},{2,3},{3,2},{4,5},{5,4},{6,7},{7,6},{8,9},{9,8},{10,11... | collective-permute-start | bytes 1179656 | tf_op jit(solution)/shard_map/ppermute | solution.py:71
  65.1 1.7 %copy-start.12 = (bf16[2,1536,384]{2,1,0:T(8,128)(2,1)S(1)}, bf16[2,1536,384]{2,1,0:T(8,128)(2,1)}, u32[]{:S(2)}) copy-start(bf16[2,1536,384]{2,1,0:T(8,128)(2,1)} %param.18) | copy-start | bytes 7077892
  66.7 8.3 %copy-start.13 = (bf16[384,1536]{1,0:T(8,128)(2,1)S(1)}, bf16[384,1536]{1,0:T(8,128)(2,1)}, u32[]{:S(2)}) copy-start(bf16[384,1536]{1,0:T(8,128)(2,1)} %param.22) | copy-start | bytes 3538948
  66.7 8.3 %copy-start.15 = (f32[384]{0:T(512)S(1)}, f32[384]{0:T(512)}, u32[]{:S(2)}) copy-start(f32[384]{0:T(512)} %param.21) | copy-start | bytes 4612
  66.7 8.3 %copy-start.16 = (f32[384]{0:T(512)S(1)}, f32[384]{0:T(512)}, u32[]{:S(2)}) copy-start(f32[384]{0:T(512)} %param.20) | copy-start | bytes 4612
  67.7 6.9 %collective-permute-start.8 = (bf16[2,15,384]{2,1,0:T(8,128)(2,1)S(1)}, bf16[2,15,384]{2,1,0:T(8,128)(2,1)S(1)}, u32[]{:S(2)}, u32[]{:S(2)}) collective-permute-start(bf16[2,15,384]{2,1,0:T(8,128)(2,1)S(1)} %get-tuple-element.60), channel_id=1, source_target_pairs={{4,0},{8,4},{12,8},{5,1},{9,5},{13,9},{6,2},{10,6},{14,10},{7,3},{... | collective-permute-start | bytes 69128 | tf_op jit(solution)/shard_map/ppermute | solution.py:21
  69.0 6.1 %collective-permute-start.7 = (bf16[2,15,384]{2,1,0:T(8,128)(2,1)S(1)}, bf16[2,15,384]{2,1,0:T(8,128)(2,1)S(1)}, u32[]{:S(2)}, u32[]{:S(2)}) collective-permute-start(bf16[2,15,384]{2,1,0:T(8,128)(2,1)S(1)} %get-tuple-element.59), channel_id=1, source_target_pairs={{0,4},{4,8},{8,12},{1,5},{5,9},{9,13},{2,6},{6,10},{10,14},{3,7},{... | collective-permute-start | bytes 69128 | tf_op jit(solution)/shard_map/ppermute | solution.py:20
  77.7 0.7 copy-start.9
  77.8 4.7 %copy-start.11 = (s32[2]{0:T(128)S(1)}, s32[2]{0:T(128)}, u32[]{:S(2)}) copy-start(s32[2]{0:T(128)} %param.13) | copy-start | bytes 28
  77.9 1.9 %collective-permute-start.9 = (bf16[2,2,32,1536]{3,2,0,1:T(8,128)(2,1)S(1)}, bf16[2,2,32,1536]{3,2,0,1:T(8,128)(2,1)}, u32[]{:S(2)}, u32[]{:S(2)}) collective-permute-start(bf16[2,2,32,1536]{3,2,0,1:T(8,128)(2,1)S(1)} %bitcast.133), channel_id=1, source_target_pairs={{0,1},{1,0},{2,3},{3,2},{4,5},{5,4},{6,7},{7,6},{8,9},{9,8},{10,11... | collective-permute-start | bytes 1179656 | tf_op jit(solution)/shard_map/ppermute | solution.py:59
  80.9 7.0 %collective-permute-start.10 = (bf16[2,32,1536]{2,1,0:T(8,128)(2,1)S(1)}, bf16[2,32,1536]{2,1,0:T(8,128)(2,1)S(1)}, u32[]{:S(2)}, u32[]{:S(2)}) collective-permute-start(bf16[2,32,1536]{2,1,0:T(8,128)(2,1)S(1)} %fusion.61), channel_id=1, source_target_pairs={{0,2},{1,3},{2,0},{3,1},{4,6},{5,7},{6,4},{7,5},{8,10},{9,11},{10,... | collective-permute-start | bytes 589832 | tf_op jit(solution)/shard_map/ppermute | solution.py:59

commit v4 on v1

--- a/solution.py
+++ b/solution.py
@@ -150,19 +150,32 @@
     residual_mine = features_mine.astype(jnp.float32) + attn_mine
     normed_mine = layer_norm(residual_mine, conv_gain).astype(jnp.bfloat16)
     normed_conv = all_gather_rows(normed_mine, "mp", 1)
+    rim_width = kernel.shape[0] // 2
+    frame_ids = first_frame + jnp.arange(frames_here, dtype=jnp.int32)
+    frame_live = (frame_ids[None, :] < frame_counts[:, None])[..., None]
+    edges = jnp.concatenate(
+        [normed_conv[:, :rim_width], normed_conv[:, frames_here - rim_width :]], axis=1
+    )
+    edge_live = jnp.concatenate(
+        [frame_live[:, :rim_width], frame_live[:, frames_here - rim_width :]], axis=1
+    )
+    gated_edges = jnp.where(edge_live, gated_units(edges, w_glu), jnp.zeros((), jnp.bfloat16))
+    ctx_up = [(i, i + 1) for i in range(ctx_count - 1)]
+    ctx_down = [(j, i) for i, j in ctx_up]
+    before = lax.ppermute(gated_edges[:, rim_width:], "ctx", ctx_up)
+    after = lax.ppermute(gated_edges[:, :rim_width], "ctx", ctx_down)
     gated_rows = gated_units(normed_conv, w_glu)
-    frame_ids = first_frame + jnp.arange(frames_here, dtype=jnp.int32)
-    frame_live = frame_ids[None, :] < frame_counts[:, None]
-    gated_rows = jnp.where(frame_live[..., None], gated_rows, jnp.zeros((), jnp.bfloat16))
-    rim_width = kernel.shape[0] // 2
-    padded = with_halo(gated_rows, (("ctx", 1),), rim_width)
-    depthwise = jnp.zeros(gated_rows.shape, jnp.float32)
-    for tap_index in range(kernel.shape[0]):
-        depthwise = (
-            depthwise
-            + padded[:, tap_index : tap_index + frames_here, :].astype(jnp.float32)
-            * kernel[tap_index]
-        )
+    gated_rows = jnp.where(frame_live, gated_rows, jnp.zeros((), jnp.bfloat16))
+    padded = jnp.concatenate([before, gated_rows, after], axis=1)
+    depthwise = lax.conv_general_dilated(
+        padded.astype(jnp.float32),
+        kernel[:, None, :],
+        window_strides=(1,),
+        padding="VALID",
+        dimension_numbers=("NWC", "WIO", "NWC"),
+        feature_group_count=kernel.shape[1],
+        precision=lax.Precision.HIGHEST,
+    )
     activated = jax.nn.silu(depthwise * bn_scale + bn_shift).astype(jnp.bfloat16)
     conv_part = jnp.einsum("stc,cd->std", activated, w_pw, preferred_element_type=jnp.float32)
     conv_rows = reduce_scatter_rows(conv_part.astype(jnp.bfloat16), "mp", 1)

time: 79.3 us -> 79.3 us (level)
  local copies, waits for them, and re-layouts: 6.9 us -> 4.35 us
  waiting for transfers between devices: 39.9 us -> 42.3 us
    slice x3, local copies, waits for them, and re-layouts: 2.33 us -> 0.11 us  [the longest x1 0.07 us: shards(): frame_live[:, :rim_width]]
    dot_general x1, matrix products: 2.74 us -> 0.6 us  [shards(): jnp.einsum('stc,cd->std', activated, w_pw, preferred_element_type=jnp.flo...]
    ppermute x2, waiting for transfers between devices: 5.08 us -> 6.16 us  [all_gather_rows(): got = lax.ppermute(acc, axis, xor_pairs(count, 1 << b))]
    conv_general_dilated x0 -> x1, matrix products: none -> 1.07 us  [shards(): lax.conv_general_dilated(padded.astype(jnp.float32), kernel[:, None, :],...]
    ppermute x2, waiting for transfers between devices: 3.37 us -> 4.28 us  [the longest x1 4.22 us: shards(): after = lax.ppermute(gated_edges[:, :rim_width], 'ctx', ctx_down)]
  transfers between devices with their start and end apart: 11 -> 11, of which waited for: 10 -> 11; matrix products, arithmetic and copies ran while one was open for 4% -> 1% of each run, Pallas kernels for 0% -> 0%
where the time goes in v4:
time: 79.3 us; the launch traced here: 78.9 us
  waiting for transfers between devices  42.3 us (53%)
  starting transfers between devices  13 us (16%)
  other arithmetic  11.3 us (14%)
  matrix products  7.56 us (10%)
  local copies, waits for them, and re-layouts  4.35 us (5%)
    ppermute x4, waiting for transfers between devices, reduce_scatter_rows(): lax.ppermute(send.astype(jnp.bfloat16), axis, xor_pairs(count, 1 << b))  14.6 us
    ppermute x2, waiting for transfers between devices, ring_gather(): going_right = lax.ppermute(going_right, axis, right)  13.2 us
    ppermute x2, waiting for transfers between devices, all_gather_rows(): got = lax.ppermute(acc, axis, xor_pairs(count, 1 << b))  6.16 us
    ppermute x1, waiting for transfers between devices, shards(): after = lax.ppermute(gated_edges[:, :rim_width], 'ctx', ctx_down)  4.22 us
    ppermute x1, waiting for transfers between devices, ring_gather(): going_left = lax.ppermute(going_left, axis, left)  4.09 us
    ppermute x4, starting transfers between devices, reduce_scatter_rows(): lax.ppermute(send.astype(jnp.bfloat16), axis, xor_pairs(count, 1 << b))  3.25 us
    ppermute x2, starting transfers between devices, ring_gather(): going_right = lax.ppermute(going_right, axis, right)  3.08 us
    dot_general x1, matrix products, shards(): jnp.einsum('std,idc->istc', normed, w_qkv, preferred_element_type=jnp.flo...  2.78 us
  transfers between devices with their start and end apart: 11, of which 11 were waited for; matrix products, arithmetic and copies ran while one was open for 1% of the time, Pallas kernels for 0%

profile of v4, /device:TPU:0, one launch (start us, length us, event | category | flops | bytes accessed | tf_op | source)
XLA Modules:
  0.0 78.9 jit_solution(7307359737889422040)
XLA Ops:
  0.0 1.5 %convert_reduce_fusion = f32[2,128]{1,0:T(2,128)S(1)} fusion(bf16[2,128,1536]{2,1,0:T(8,128)(2,1)} %param.12), kind=kLoop, calls=%fused_computation.11 | loop fusion | flops 786176 | bytes 787456 | tf_op jit(solution)/shard_map/reduce_sum | solution.py:27
  1.5 1.5 %fusion.11 = f32[2,128]{1,0:T(2,128)S(1)} fusion(bf16[2,128,1536]{2,1,0:T(8,128)(2,1)} %param.12, f32[2,128]{1,0:T(2,128)S(1)} %broadcast_multiply_fusion.1), kind=kLoop, calls=%fused_computation.17 | loop fusion | flops 1572608 | bytes 788480 | tf_op jit(solution)/shard_map/reduce_sum | solution.py:29
  3.0 2.8 %fusion.20 = bf16[3,2,128,256]{3,2,0,1:T(8,128)(2,1)S(1)} fusion(bf16[3,1536,256]{2,1,0:T(8,128)(2,1)} %param.15, bf16[2,128,1536]{2,1,0:T(8,128)(2,1)} %param.12, f32[1536]{0:T(1024)} %param.14, f32[2,128]{1,0:T(2,128)S(1)} %add_rsqrt_fusion.1, f32[2,128]{1,0:T(2,128)S(1)} %broadcast_multiply_fusion.1), kind=kOutput, calls=%fused_computation.22 | convolution fusion | flops 606142464 | bytes 3547136 | tf_op jit(solution)/shard_map/std,idc->istc/dot_general | solution.py:116
  5.8 3.1 %collective-permute-start.1 = (bf16[2,2,128,256]{3,2,0,1:T(8,128)(2,1)S(1)}, bf16[2,2,128,256]{3,2,0,1:T(8,128)(2,1)}, u32[]{:S(2)}, u32[]{:S(2)}) collective-permute-start(bf16[2,2,128,256]{3,2,0,1:T(8,128)(2,1)S(1)} %get-tuple-element.20), channel_id=1, source_target_pairs={{0,4},{4,8},{8,12},{12,0},{1,5},{5,9},{9,13},{13,1},{2,6},{6,10},{... | collective-permute-start | bytes 786440 | tf_op jit(solution)/shard_map/ppermute | solution.py:87
  8.9 2.1 %collective-permute-start = (bf16[2,2,128,256]{3,2,0,1:T(8,128)(2,1)S(1)}, bf16[2,2,128,256]{3,2,0,1:T(8,128)(2,1)}, u32[]{:S(2)}, u32[]{:S(2)}) collective-permute-start(bf16[2,2,128,256]{3,2,0,1:T(8,128)(2,1)S(1)} %get-tuple-element.20), channel_id=1, source_target_pairs={{0,12},{4,0},{8,4},{12,8},{1,13},{5,1},{9,5},{13,9},{2,14},{6,2},{... | collective-permute-start | bytes 786440 | tf_op jit(solution)/shard_map/ppermute | solution.py:90
  11.0 7.2 %collective-permute-done.1 = bf16[2,2,128,256]{3,2,0,1:T(8,128)(2,1)} collective-permute-done((bf16[2,2,128,256]{3,2,0,1:T(8,128)(2,1)S(1)}, bf16[2,2,128,256]{3,2,0,1:T(8,128)(2,1)}, u32[]{:S(2)}, u32[]{:S(2)}) %collective-permute-start.1) | collective-permute-done | bytes 262176 | tf_op jit(solution)/shard_map/ppermute | solution.py:87
  18.3 0.1 copy.41
  18.5 4.1 %collective-permute-done = bf16[2,2,128,256]{3,2,0,1:T(8,128)(2,1)} collective-permute-done((bf16[2,2,128,256]{3,2,0,1:T(8,128)(2,1)S(1)}, bf16[2,2,128,256]{3,2,0,1:T(8,128)(2,1)}, u32[]{:S(2)}, u32[]{:S(2)}) %collective-permute-start) | collective-permute-done | bytes 262176 | tf_op jit(solution)/shard_map/ppermute | solution.py:90
  22.6 6.0 %collective-permute-done.2 = bf16[2,2,128,256]{3,2,0,1:T(8,128)(2,1)} collective-permute-done((bf16[2,2,128,256]{3,2,0,1:T(8,128)(2,1)}, bf16[2,2,128,256]{3,2,0,1:T(8,128)(2,1)}, u32[]{:S(2)}, u32[]{:S(2)}) %collective-permute-start.2) | collective-permute-done | bytes 262176 | tf_op jit(solution)/shard_map/ppermute | solution.py:87
  28.6 1.2 %pad_maximum_fusion = bf16[4,2,2,128,256]{4,3,1,2,0:T(8,128)(2,1)S(1)} fusion(bf16[1,2,2,128,256]{4,3,1,2,0:T(8,128)(2,1)} %bitcast.10, bf16[1,2,2,128,256]{4,3,1,2,0:T(8,128)(2,1)} %bitcast.9, bf16[1,2,2,128,256]{4,3,1,2,0:T(8,128)(2,1)} %bitcast.8, bf16[1,2,2,128,256]{4,3,1,2,0:T(8,128)(2,1)S(1)} %get-tuple-element.19), kind=kLoop, calls=%fused_computation.28 | loop fusion | flops 1572864 | bytes 2097152 | tf_op jit(solution)/shard_map/stack | solution.py:92
  29.8 0.9 %fusion.79 = (bf16[4,1,2,128,256]{4,3,1,2,0:T(8,128)(2,1)S(1)}, bf16[4,1,2,128,256]{4,3,1,2,0:T(8,128)(2,1)}) fusion(bf16[4,2,2,128,256]{4,3,1,2,0:T(8,128)(2,1)S(1)} %pad_maximum_fusion), kind=kLoop, calls=%fused_computation.123 | loop fusion | bytes 2097152 | tf_op jit(solution)/shard_map/slice | solution.py:123
  30.7 1.3 %copy.42 = bf16[4,1,2,128,256]{3,4,2,0,1:T(8,128)(2,1)S(1)} copy(bf16[4,1,2,128,256]{4,3,1,2,0:T(8,128)(2,1)} %get-tuple-element.8) | data formatting | bytes 1048576 | tf_op jit(solution)/shard_map/slice | solution.py:122
  32.0 1.0 %copy.44 = bf16[4,1,2,128,256]{3,4,2,0,1:T(8,128)(2,1)} copy(bf16[4,1,2,128,256]{4,3,1,2,0:T(8,128)(2,1)S(1)} %get-tuple-element.7) | data formatting | bytes 1048576 | tf_op jit(solution)/shard_map/slice | solution.py:123
  33.0 0.7 fusion.8
  33.8 0.5 fusion.9
  34.3 0.7 fusion.28
  35.1 0.4 copy-done.1
  35.4 0.4 convolution_convert_fusion
  36.0 1.8 %collective-permute-done.3 = bf16[2,2,32,1536]{3,2,0,1:T(8,128)(2,1)} collective-permute-done((bf16[2,2,32,1536]{3,2,0,1:T(8,128)(2,1)S(1)}, bf16[2,2,32,1536]{3,2,0,1:T(8,128)(2,1)}, u32[]{:S(2)}, u32[]{:S(2)}) %collective-permute-start.3) | collective-permute-done | bytes 393248 | tf_op jit(solution)/shard_map/ppermute | solution.py:59
  37.9 1.1 %convert_add_fusion.1 = f32[2,2,32,1536]{3,2,0,1:T(8,128)S(1)} fusion(bf16[2,2,32,1536]{3,2,0,1:T(8,128)(2,1)} %collective-permute-done.3, bf16[2,2,1,32,1536]{4,3,2,1,0:T(8,128)(2,1)S(1)} %get-tuple-element.15), kind=kLoop, calls=%fused_computation.36 | loop fusion | flops 589824 | bytes 1572864 | tf_op jit(solution)/shard_map/add | solution.py:60
  39.0 1.6 %collective-permute-start.4 = (bf16[2,32,1536]{2,1,0:T(8,128)(2,1)S(1)}, bf16[2,32,1536]{2,1,0:T(8,128)(2,1)}, u32[]{:S(2)}, u32[]{:S(2)}) collective-permute-start(bf16[2,32,1536]{2,1,0:T(8,128)(2,1)S(1)} %fusion.57), channel_id=1, source_target_pairs={{0,2},{1,3},{2,0},{3,1},{4,6},{5,7},{6,4},{7,5},{8,10},{9,11},{10,... | collective-permute-start | bytes 589832 | tf_op jit(solution)/shard_map/ppermute | solution.py:59
  40.6 5.6 %collective-permute-done.4 = bf16[2,32,1536]{2,1,0:T(8,128)(2,1)} collective-permute-done((bf16[2,32,1536]{2,1,0:T(8,128)(2,1)S(1)}, bf16[2,32,1536]{2,1,0:T(8,128)(2,1)}, u32[]{:S(2)}, u32[]{:S(2)}) %collective-permute-start.4) | collective-permute-done | bytes 196640 | tf_op jit(solution)/shard_map/ppermute | solution.py:59
  46.1 1.2 %fusion.77 = (f32[2,32]{1,0:T(2,128)S(1)}, f32[2,32,1536]{2,1,0:T(8,128)S(1)}) fusion(bf16[2,32,1536]{2,1,0:T(8,128)(2,1)} %collective-permute-done.4, f32[2,2,32,1536]{3,2,0,1:T(8,128)S(1)} %convert_add_fusion.1, s32[]{:T(128)S(6)} %select_n.77, bf16[2,128,1536]{2,1,0:T(8,128)(2,1)} %param.12, s32[]{:T(128)S(6)} %select_n.72), kind=kLoop, calls=%fused_computation.122 | loop fusion | flops 491456 | bytes 1179912 | tf_op jit(solution)/shard_map/reduce_sum | solution.py:27
  47.3 0.2 multiply_reduce_fusion
  47.5 0.1 multiply_convert_fusion.1
  47.6 1.6 %collective-permute-start.5 = (bf16[2,32,1536]{2,1,0:T(8,128)(2,1)S(1)}, bf16[2,32,1536]{2,1,0:T(8,128)(2,1)S(1)}, u32[]{:S(2)}, u32[]{:S(2)}) collective-permute-start(bf16[2,32,1536]{2,1,0:T(8,128)(2,1)S(1)} %multiply_convert_fusion.1), channel_id=1, source_target_pairs={{0,2},{1,3},{2,0},{3,1},{4,6},{5,7},{6,4},{7,5},{8,10},{9,11},{10,... | collective-permute-start | bytes 589832 | tf_op jit(solution)/shard_map/ppermute | solution.py:71
  49.3 4.6 %collective-permute-done.5 = bf16[2,32,1536]{2,1,0:T(8,128)(2,1)S(1)} collective-permute-done((bf16[2,32,1536]{2,1,0:T(8,128)(2,1)S(1)}, bf16[2,32,1536]{2,1,0:T(8,128)(2,1)S(1)}, u32[]{:S(2)}, u32[]{:S(2)}) %collective-permute-start.5) | collective-permute-done | bytes 196640 | tf_op jit(solution)/shard_map/ppermute | solution.py:71
  53.8 0.2 select_bitcast_fusion.3
  54.1 0.1 fusion.82
  54.2 0.1 add_bitcast_fusion
  54.3 1.6 %collective-permute-done.6 = bf16[2,2,32,1536]{3,2,0,1:T(8,128)(2,1)} collective-permute-done((bf16[2,2,32,1536]{3,2,0,1:T(8,128)(2,1)S(1)}, bf16[2,2,32,1536]{3,2,0,1:T(8,128)(2,1)}, u32[]{:S(2)}, u32[]{:S(2)}) %collective-permute-start.6) | collective-permute-done | bytes 393248 | tf_op jit(solution)/shard_map/ppermute | solution.py:71
  56.0 1.1 %select_bitcast_fusion.1 = (bf16[2,2,1,32,1536]{4,3,0,1,2:T(8,128)(2,1)S(1)}, bf16[2,2,1,32,1536]{4,3,0,1,2:T(8,128)(2,1)S(1)}) fusion(bf16[2,2,32,1536]{3,2,0,1:T(8,128)(2,1)} %collective-permute-done.6, pred[]{:T(512)S(6)} %eq.8, bf16[2,1,32,1536]{3,2,0,1:T(8,128)(2,1)S(1)} %get-tuple-element.18, bf16[2,1,32,1536]{3,2,0,1:T(8,128)(2,1)S(1)} %get-tuple-element.17), kind=kLoop, calls=%fused_computation.67 | loop fusion | flops 589824 | bytes 1572865 | tf_op jit(solution)/shard_map/stack | solution.py:74
  57.0 0.1 pad_maximum_fusion.1
  57.2 0.8 fusion.14
  58.0 0.5 fusion.24
  58.5 0.1 bitcast_select_fusion.1
  58.6 1.6 %collective-permute-start.7 = (bf16[2,15,384]{2,1,0:T(8,128)(2,1)S(1)}, bf16[2,15,384]{2,1,0:T(8,128)(2,1)S(1)}, u32[]{:S(2)}, u32[]{:S(2)}) collective-permute-start(bf16[2,15,384]{2,1,0:T(8,128)(2,1)S(1)} %get-tuple-element.21), channel_id=1, source_target_pairs={{0,4},{4,8},{8,12},{1,5},{5,9},{9,13},{2,6},{6,10},{10,14},{3,7},{... | collective-permute-start | bytes 69128 | tf_op jit(solution)/shard_map/ppermute | solution.py:165
  60.2 1.3 %collective-permute-start.8 = (bf16[2,15,384]{2,1,0:T(8,128)(2,1)S(1)}, bf16[2,15,384]{2,1,0:T(8,128)(2,1)S(1)}, u32[]{:S(2)}, u32[]{:S(2)}) collective-permute-start(bf16[2,15,384]{2,1,0:T(8,128)(2,1)S(1)} %get-tuple-element.22), channel_id=1, source_target_pairs={{4,0},{8,4},{12,8},{5,1},{9,5},{13,9},{6,2},{10,6},{14,10},{7,3},{... | collective-permute-start | bytes 69128 | tf_op jit(solution)/shard_map/ppermute | solution.py:166
  61.5 0.1 bitcast_select_fusion
  61.7 4.2 %collective-permute-done.8 = bf16[2,15,384]{2,1,0:T(8,128)(2,1)S(1)} collective-permute-done((bf16[2,15,384]{2,1,0:T(8,128)(2,1)S(1)}, bf16[2,15,384]{2,1,0:T(8,128)(2,1)S(1)}, u32[]{:S(2)}, u32[]{:S(2)}) %collective-permute-start.8) | collective-permute-done | bytes 23072 | tf_op jit(solution)/shard_map/ppermute | solution.py:166
  66.1 1.1 %fusion.55 = f32[2,128,384]{2,0,1:T(2,128)S(1)} fusion(bf16[2,158,384]{2,1,0:T(8,128)(2,1)S(1)} %pad_maximum_fusion.3, f32[31,1,384]{2,0,1:T(8,128)S(1)} %bitcast.134), kind=kOutput, calls=%fused_computation.73 | convolution fusion | flops 36569088 | bytes 683520 | tf_op jit(solution)/shard_map/conv_general_dilated | solution.py:170
  67.2 0.2 copy-done.6
  67.3 0.6 convolution_convert_fusion.1
  68.2 1.8 %collective-permute-done.9 = bf16[2,2,32,1536]{3,2,0,1:T(8,128)(2,1)} collective-permute-done((bf16[2,2,32,1536]{3,2,0,1:T(8,128)(2,1)S(1)}, bf16[2,2,32,1536]{3,2,0,1:T(8,128)(2,1)}, u32[]{:S(2)}, u32[]{:S(2)}) %collective-permute-start.9) | collective-permute-done | bytes 393248 | tf_op jit(solution)/shard_map/ppermute | solution.py:59
  70.0 1.1 %convert_add_fusion = f32[2,2,32,1536]{3,2,0,1:T(8,128)S(1)} fusion(bf16[2,2,32,1536]{3,2,0,1:T(8,128)(2,1)} %collective-permute-done.9, bf16[2,2,1,32,1536]{4,3,2,1,0:T(8,128)(2,1)S(1)} %get-tuple-element.9), kind=kLoop, calls=%fused_computation.35 | loop fusion | flops 589824 | bytes 1572864 | tf_op jit(solution)/shard_map/add | solution.py:60
  71.1 1.6 %collective-permute-start.10 = (bf16[2,32,1536]{2,1,0:T(8,128)(2,1)S(1)}, bf16[2,32,1536]{2,1,0:T(8,128)(2,1)S(1)}, u32[]{:S(2)}, u32[]{:S(2)}) collective-permute-start(bf16[2,32,1536]{2,1,0:T(8,128)(2,1)S(1)} %fusion.58), channel_id=1, source_target_pairs={{0,2},{1,3},{2,0},{3,1},{4,6},{5,7},{6,4},{7,5},{8,10},{9,11},{10,... | collective-permute-start | bytes 589832 | tf_op jit(solution)/shard_map/ppermute | solution.py:59
  72.7 5.4 %collective-permute-done.10 = bf16[2,32,1536]{2,1,0:T(8,128)(2,1)S(1)} collective-permute-done((bf16[2,32,1536]{2,1,0:T(8,128)(2,1)S(1)}, bf16[2,32,1536]{2,1,0:T(8,128)(2,1)S(1)}, u32[]{:S(2)}, u32[]{:S(2)}) %collective-permute-start.10) | collective-permute-done | bytes 196640 | tf_op jit(solution)/shard_map/ppermute | solution.py:59
  78.1 0.8 fusion.51
  (49 shorter events, 1.2 us)
Async XLA Ops:
  0.0 57.2 %copy-start = (bf16[2,1536,384]{2,1,0:T(8,128)(2,1)S(1)}, bf16[2,1536,384]{2,1,0:T(8,128)(2,1)}, u32[]{:S(2)}) copy-start(bf16[2,1536,384]{2,1,0:T(8,128)(2,1)} %param.18) | copy-start | bytes 7077892
  3.0 15.4 %copy-start.5 = (s32[2]{0:T(128)S(1)}, s32[2]{0:T(128)}, u32[]{:S(2)}) copy-start(s32[2]{0:T(128)} %param.13) | copy-start | bytes 28
  5.8 12.4 %collective-permute-start.1 = (bf16[2,2,128,256]{3,2,0,1:T(8,128)(2,1)S(1)}, bf16[2,2,128,256]{3,2,0,1:T(8,128)(2,1)}, u32[]{:S(2)}, u32[]{:S(2)}) collective-permute-start(bf16[2,2,128,256]{3,2,0,1:T(8,128)(2,1)S(1)} %get-tuple-element.20), channel_id=1, source_target_pairs={{0,4},{4,8},{8,12},{12,0},{1,5},{5,9},{9,13},{13,1},{2,6},{6,10},{... | collective-permute-start | bytes 786440 | tf_op jit(solution)/shard_map/ppermute | solution.py:87
  8.9 13.7 %collective-permute-start = (bf16[2,2,128,256]{3,2,0,1:T(8,128)(2,1)S(1)}, bf16[2,2,128,256]{3,2,0,1:T(8,128)(2,1)}, u32[]{:S(2)}, u32[]{:S(2)}) collective-permute-start(bf16[2,2,128,256]{3,2,0,1:T(8,128)(2,1)S(1)} %get-tuple-element.20), channel_id=1, source_target_pairs={{0,12},{4,0},{8,4},{12,8},{1,13},{5,1},{9,5},{13,9},{2,14},{6,2},{... | collective-permute-start | bytes 786440 | tf_op jit(solution)/shard_map/ppermute | solution.py:90
  18.2 10.4 %collective-permute-start.2 = (bf16[2,2,128,256]{3,2,0,1:T(8,128)(2,1)}, bf16[2,2,128,256]{3,2,0,1:T(8,128)(2,1)}, u32[]{:S(2)}, u32[]{:S(2)}) collective-permute-start(bf16[2,2,128,256]{3,2,0,1:T(8,128)(2,1)} %collective-permute-done.1), channel_id=1, source_target_pairs={{0,4},{4,8},{8,12},{12,0},{1,5},{5,9},{9,13},{13,1},{2,6},{6,10},{... | collective-permute-start | bytes 786440 | tf_op jit(solution)/shard_map/ppermute | solution.py:87
  33.0 1.2 %copy-start.2 = (bf16[4,1,2,128,256]{3,4,2,0,1:T(8,128)(2,1)S(1)}, bf16[4,1,2,128,256]{3,4,2,0,1:T(8,128)(2,1)}, u32[]{:S(2)}) copy-start(bf16[4,1,2,128,256]{3,4,2,0,1:T(8,128)(2,1)} %copy.44) | copy-start | bytes 1572868
  34.3 1.1 %copy-start.1 = (bf16[256,1536]{1,0:T(8,128)(2,1)S(1)}, bf16[256,1536]{1,0:T(8,128)(2,1)}, u32[]{:S(2)}) copy-start(bf16[256,1536]{1,0:T(8,128)(2,1)} %param.16) | copy-start | bytes 2359300
  35.9 11.6 %copy-start.3 = (f32[1536]{0:T(1024)S(1)}, f32[1536]{0:T(1024)}, u32[]{:S(2)}) copy-start(f32[1536]{0:T(1024)} %param.17) | copy-start | bytes 18436
  35.9 1.9 %collective-permute-start.3 = (bf16[2,2,32,1536]{3,2,0,1:T(8,128)(2,1)S(1)}, bf16[2,2,32,1536]{3,2,0,1:T(8,128)(2,1)}, u32[]{:S(2)}, u32[]{:S(2)}) collective-permute-start(bf16[2,2,32,1536]{3,2,0,1:T(8,128)(2,1)S(1)} %bitcast.130), channel_id=1, source_target_pairs={{0,1},{1,0},{2,3},{3,2},{4,5},{5,4},{6,7},{7,6},{8,9},{9,8},{10,11... | collective-permute-start | bytes 1179656 | tf_op jit(solution)/shard_map/ppermute | solution.py:59
  39.0 7.1 %collective-permute-start.4 = (bf16[2,32,1536]{2,1,0:T(8,128)(2,1)S(1)}, bf16[2,32,1536]{2,1,0:T(8,128)(2,1)}, u32[]{:S(2)}, u32[]{:S(2)}) collective-permute-start(bf16[2,32,1536]{2,1,0:T(8,128)(2,1)S(1)} %fusion.57), channel_id=1, source_target_pairs={{0,2},{1,3},{2,0},{3,1},{4,6},{5,7},{6,4},{7,5},{8,10},{9,11},{10,... | collective-permute-start | bytes 589832 | tf_op jit(solution)/shard_map/ppermute | solution.py:59
  47.6 6.2 %collective-permute-start.5 = (bf16[2,32,1536]{2,1,0:T(8,128)(2,1)S(1)}, bf16[2,32,1536]{2,1,0:T(8,128)(2,1)S(1)}, u32[]{:S(2)}, u32[]{:S(2)}) collective-permute-start(bf16[2,32,1536]{2,1,0:T(8,128)(2,1)S(1)} %multiply_convert_fusion.1), channel_id=1, source_target_pairs={{0,2},{1,3},{2,0},{3,1},{4,6},{5,7},{6,4},{7,5},{8,10},{9,11},{10,... | collective-permute-start | bytes 589832 | tf_op jit(solution)/shard_map/ppermute | solution.py:71
  54.0 1.9 %collective-permute-start.6 = (bf16[2,2,32,1536]{3,2,0,1:T(8,128)(2,1)S(1)}, bf16[2,2,32,1536]{3,2,0,1:T(8,128)(2,1)}, u32[]{:S(2)}, u32[]{:S(2)}) collective-permute-start(bf16[2,2,32,1536]{3,2,0,1:T(8,128)(2,1)S(1)} %pad_maximum_fusion.2), channel_id=1, source_target_pairs={{0,1},{1,0},{2,3},{3,2},{4,5},{5,4},{6,7},{7,6},{8,9},{9,8},{10,11... | collective-permute-start | bytes 1179656 | tf_op jit(solution)/shard_map/ppermute | solution.py:71
  58.0 8.1 %copy-start.7 = (f32[31,384]{1,0:T(8,128)S(1)}, f32[31,384]{1,0:T(8,128)}, u32[]{:S(2)}) copy-start(f32[31,384]{1,0:T(8,128)} %param.19) | copy-start | bytes 142852
  58.6 3.1 %collective-permute-start.7 = (bf16[2,15,384]{2,1,0:T(8,128)(2,1)S(1)}, bf16[2,15,384]{2,1,0:T(8,128)(2,1)S(1)}, u32[]{:S(2)}, u32[]{:S(2)}) collective-permute-start(bf16[2,15,384]{2,1,0:T(8,128)(2,1)S(1)} %get-tuple-element.21), channel_id=1, source_target_pairs={{0,4},{4,8},{8,12},{1,5},{5,9},{9,13},{2,6},{6,10},{10,14},{3,7},{... | collective-permute-start | bytes 69128 | tf_op jit(solution)/shard_map/ppermute | solution.py:165
  60.2 5.7 %collective-permute-start.8 = (bf16[2,15,384]{2,1,0:T(8,128)(2,1)S(1)}, bf16[2,15,384]{2,1,0:T(8,128)(2,1)S(1)}, u32[]{:S(2)}, u32[]{:S(2)}) collective-permute-start(bf16[2,15,384]{2,1,0:T(8,128)(2,1)S(1)} %get-tuple-element.22), channel_id=1, source_target_pairs={{4,0},{8,4},{12,8},{5,1},{9,5},{13,9},{6,2},{10,6},{14,10},{7,3},{... | collective-permute-start | bytes 69128 | tf_op jit(solution)/shard_map/ppermute | solution.py:166
  66.0 1.3 %copy-start.6 = (bf16[384,1536]{1,0:T(8,128)(2,1)S(1)}, bf16[384,1536]{1,0:T(8,128)(2,1)}, u32[]{:S(2)}) copy-start(bf16[384,1536]{1,0:T(8,128)(2,1)} %param.22) | copy-start | bytes 3538948
  66.1 1.3 %copy-start.8 = (f32[384]{0:T(512)S(1)}, f32[384]{0:T(512)}, u32[]{:S(2)}) copy-start(f32[384]{0:T(512)} %param.21) | copy-start | bytes 4612
  66.1 1.3 %copy-start.9 = (f32[384]{0:T(512)S(1)}, f32[384]{0:T(512)}, u32[]{:S(2)}) copy-start(f32[384]{0:T(512)} %param.20) | copy-start | bytes 4612
  67.3 0.8 %copy-start.4 = (s32[1536]{0:T(1024)S(1)}, s32[1536]{0:T(1024)}, u32[]{:S(2)}) copy-start(s32[1536]{0:T(1024)} %param.23) | copy-start | bytes 18436
  68.0 1.9 %collective-permute-start.9 = (bf16[2,2,32,1536]{3,2,0,1:T(8,128)(2,1)S(1)}, bf16[2,2,32,1536]{3,2,0,1:T(8,128)(2,1)}, u32[]{:S(2)}, u32[]{:S(2)}) collective-permute-start(bf16[2,2,32,1536]{3,2,0,1:T(8,128)(2,1)S(1)} %bitcast.131), channel_id=1, source_target_pairs={{0,1},{1,0},{2,3},{3,2},{4,5},{5,4},{6,7},{7,6},{8,9},{9,8},{10,11... | collective-permute-start | bytes 1179656 | tf_op jit(solution)/shard_map/ppermute | solution.py:59
  71.1 7.0 %collective-permute-start.10 = (bf16[2,32,1536]{2,1,0:T(8,128)(2,1)S(1)}, bf16[2,32,1536]{2,1,0:T(8,128)(2,1)S(1)}, u32[]{:S(2)}, u32[]{:S(2)}) collective-permute-start(bf16[2,32,1536]{2,1,0:T(8,128)(2,1)S(1)} %fusion.58), channel_id=1, source_target_pairs={{0,2},{1,3},{2,0},{3,1},{4,6},{5,7},{6,4},{7,5},{8,10},{9,11},{10,... | collective-permute-start | bytes 589832 | tf_op jit(solution)/shard_map/ppermute | solution.py:59

commit v5 on v3

--- a/solution.py
+++ b/solution.py
@@ -1,6 +1,10 @@
 import jax
 import jax.numpy as jnp
+import functools
+
 from jax import lax
+from jax.experimental import pallas as pl
+from jax.experimental.pallas import tpu as pltpu
 from jax.sharding import PartitionSpec as P
 
 HEAD_DIM = 64
@@ -81,7 +85,7 @@
     left = [(i, (i - 1) % count) for i in range(count)]
     right_steps = count // 2
     left_steps = count - 1 - right_steps
-    blocks = [(0, x)]
+    blocks = []
     going_right, going_left = x, x
     for step in range(right_steps):
         going_right = lax.ppermute(going_right, axis, right)
@@ -90,6 +94,52 @@
             going_left = lax.ppermute(going_left, axis, left)
             blocks.append((step + 1, going_left))
     return blocks
+
+
+def attention_kernel(counts_ref, starts_ref, proj_ref, *refs, blocks, frames, heads):
+    others, out_ref = refs[:-1], refs[-1]
+    record = pl.program_id(0)
+    limit = counts_ref[record]
+    queries = proj_ref[0, 0]
+    key_rows = jnp.concatenate([proj_ref[1, 0]] + [r[0, 0] for r in others], axis=0)
+    value_rows = jnp.concatenate([proj_ref[2, 0]] + [r[1, 0] for r in others], axis=0)
+    slot = lax.broadcasted_iota(jnp.int32, (1, blocks * frames), 1)
+    block_of = slot // frames
+    start = jnp.zeros_like(slot)
+    for b in range(blocks):
+        start = jnp.where(block_of == b, starts_ref[b], start)
+    live = start + slot % frames < limit
+    for h in range(heads):
+        cols = slice(h * HEAD_DIM, (h + 1) * HEAD_DIM)
+        scores = lax.dot_general(
+            queries[:, cols], key_rows[:, cols], (((1,), (1,)), ((), ())),
+            preferred_element_type=jnp.float32,
+        ) * HEAD_DIM ** (-0.5)
+        scores = jnp.where(live, scores, masked_score)
+        row_max = jnp.max(scores, axis=1, keepdims=True)
+        weights = jnp.exp(scores - row_max)
+        row_sum = jnp.sum(weights, axis=1, keepdims=True)
+        contrib = jnp.dot(weights.astype(jnp.bfloat16), value_rows[:, cols],
+                          preferred_element_type=jnp.float32)
+        out_ref[0, :, cols] = (contrib / row_sum).astype(out_ref.dtype)
+
+
+def attention(projected, others, frame_counts, starts):
+    _, records, frames, width = projected.shape
+    blocks = 1 + len(others)
+    heads = width // HEAD_DIM
+    kernel = functools.partial(attention_kernel, blocks=blocks, frames=frames, heads=heads)
+    return pl.pallas_call(
+        kernel,
+        out_shape=jax.ShapeDtypeStruct((records, frames, width), jnp.bfloat16),
+        grid_spec=pltpu.PrefetchScalarGridSpec(
+            num_scalar_prefetch=2,
+            grid=(records,),
+            in_specs=[pl.BlockSpec((3, 1, frames, width), lambda s, c, o: (0, s, 0, 0))]
+            + [pl.BlockSpec((2, 1, frames, width), lambda s, c, o: (0, s, 0, 0)) for _ in others],
+            out_specs=pl.BlockSpec((1, frames, width), lambda s, c, o: (s, 0, 0)),
+        ),
+    )(frame_counts, starts, projected, *others)
 
 
 def shards(
@@ -116,38 +166,10 @@
     projected = jnp.einsum(
         "std,idc->istc", normed, w_qkv, preferred_element_type=jnp.float32
     ).astype(jnp.bfloat16)
-    queries = projected[0]
-    query_heads = queries.reshape(records, frames_here, head_count, HEAD_DIM)
     blocks = ring_gather(projected[1:], "ctx")
-    frame_steps = jnp.arange(frames_here, dtype=jnp.int32)
-    block_scores, block_values = [], []
-    for offset, block in blocks:
-        key_heads = block[0].reshape(records, frames_here, head_count, HEAD_DIM)
-        block_values.append(block[1].reshape(records, frames_here, head_count, HEAD_DIM))
-        scores = (
-            jnp.einsum("sqhe,skhe->shqk", query_heads, key_heads, preferred_element_type=jnp.float32)
-            * score_scale
-        )
-        block_rank = (ctx_rank + offset) % ctx_count
-        positions = block_rank * frames_here + frame_steps
-        is_live = positions[None, :] < frame_counts[:, None]
-        block_scores.append(jnp.where(is_live[:, None, None, :], scores, masked_score))
-    row_max = block_scores[0].max(axis=-1)
-    for scores in block_scores[1:]:
-        row_max = jnp.maximum(row_max, scores.max(axis=-1))
-    row_sum = 0.0
-    contrib = 0.0
-    for scores, value_heads in zip(block_scores, block_values):
-        weights = jnp.exp(scores - row_max[..., None])
-        row_sum = row_sum + jnp.sum(weights, axis=-1)
-        contrib = contrib + jnp.einsum(
-            "shqk,skhe->shqe",
-            weights.astype(jnp.bfloat16),
-            value_heads,
-            preferred_element_type=jnp.float32,
-        )
-    attended = (contrib / row_sum[..., None]).astype(jnp.bfloat16)
-    attended = attended.transpose(0, 2, 1, 3).reshape(records, frames_here, head_count * HEAD_DIM)
+    offsets = jnp.array([0] + [offset for offset, _ in blocks], jnp.int32)
+    starts = ((ctx_rank + offsets) % ctx_count) * frames_here
+    attended = attention(projected, [block for _, block in blocks], frame_counts, starts)
     attn_part = jnp.einsum("stc,cd->std", attended, w_out, preferred_element_type=jnp.float32)
     mp_count = lax.axis_size("mp")
     mp_rank = lax.axis_index("mp")
@@ -164,13 +186,15 @@
     gated_rows = jnp.where(frame_live[..., None], gated_rows, jnp.zeros((), jnp.bfloat16))
     rim_width = kernel.shape[0] // 2
     padded = with_halo(gated_rows, (("ctx", 1),), rim_width)
-    depthwise = jnp.zeros(gated_rows.shape, jnp.float32)
-    for tap_index in range(kernel.shape[0]):
-        depthwise = (
-            depthwise
-            + padded[:, tap_index : tap_index + frames_here, :].astype(jnp.float32)
-            * kernel[tap_index]
-        )
+    depthwise = lax.conv_general_dilated(
+        padded.astype(jnp.float32),
+        kernel[:, None, :],
+        window_strides=(1,),
+        padding="VALID",
+        dimension_numbers=("NWC", "WIO", "NWC"),
+        feature_group_count=kernel.shape[1],
+        precision=lax.Precision.HIGHEST,
+    )
     activated = jax.nn.silu(depthwise * bn_scale + bn_shift).astype(jnp.bfloat16)
     conv_part = jnp.einsum("stc,cd->std", activated, w_pw, preferred_element_type=jnp.float32)
     conv_rows = reduce_scatter_rows(conv_part.astype(jnp.bfloat16), "mp", 1)

time: 89.5 us -> 80.5 us (0.90)
  local copies, waits for them, and re-layouts: 20.9 us -> 5.2 us
  waiting for transfers between devices: 29.1 us -> 42.4 us
  matrix products: 11.2 us -> 4.87 us
  Pallas kernels: 0 us -> 5.2 us
  starting transfers between devices: 17 us -> 12.7 us
    slice x15 -> x0, local copies, waits for them, and re-layouts: 16.4 us -> none  [the longest x7 9.8 us: shards(): block[1].reshape(records, frames_here, head_count, HEAD_DIM)]
    ppermute x2, waiting for transfers between devices: 0.01 us -> 13.5 us  [ring_gather(): going_right = lax.ppermute(going_right, axis, right)]
    dot_general x8 -> x0, matrix products: 6.48 us -> none  [the longest x4 4.73 us: shards(): jnp.einsum('sqhe,skhe->shqk', query_heads, key_heads, preferred_element_t...]
    ppermute x1, waiting for transfers between devices: 9.48 us -> 3.84 us  [ring_gather(): going_left = lax.ppermute(going_left, axis, left)]
    pallas_call x0 -> x1, Pallas kernels: none -> 5.2 us  [attention(): pl.pallas_call(kernel, out_shape=jax.ShapeDtypeStruct((records, frames, w...]
    ppermute x1, waiting for transfers between devices: 0.01 us -> 4.22 us  [with_halo(): after = lax.ppermute(initial, axis, down)]
    ppermute x1, starting transfers between devices: 4.55 us -> 1.62 us  [with_halo(): before = lax.ppermute(last, axis, up)]
    dot_general x1, matrix products: 2.69 us -> 0.59 us  [shards(): jnp.einsum('stc,cd->std', activated, w_pw, preferred_element_type=jnp.flo...]
  transfers between devices with their start and end apart: 11 -> 11, of which waited for: 8 -> 11; matrix products, arithmetic and copies ran while one was open for 18% -> 2% of each run, Pallas kernels for 0% -> 0%
where the time goes in v5:
time: 80.5 us; the launch traced here: 80.1 us
  waiting for transfers between devices  42.4 us (53%)
  starting transfers between devices  12.7 us (16%)
  other arithmetic  9.42 us (12%)
  local copies, waits for them, and re-layouts  5.2 us (6%)
  Pallas kernels  5.2 us (6%)
  matrix products  4.87 us (6%)
    ppermute x4, waiting for transfers between devices, reduce_scatter_rows(): lax.ppermute(send.astype(jnp.bfloat16), axis, xor_pairs(count, 1 << b))  14.9 us
    ppermute x2, waiting for transfers between devices, ring_gather(): going_right = lax.ppermute(going_right, axis, right)  13.5 us
    ppermute x2, waiting for transfers between devices, all_gather_rows(): got = lax.ppermute(acc, axis, xor_pairs(count, 1 << b))  5.72 us
    pallas_call x1, Pallas kernels, attention(): pl.pallas_call(kernel, out_shape=jax.ShapeDtypeStruct((records, frames, w...  5.2 us
    ppermute x1, waiting for transfers between devices, with_halo(): after = lax.ppermute(initial, axis, down)  4.22 us
    ppermute x1, waiting for transfers between devices, ring_gather(): going_left = lax.ppermute(going_left, axis, left)  3.84 us
    ppermute x4, starting transfers between devices, reduce_scatter_rows(): lax.ppermute(send.astype(jnp.bfloat16), axis, xor_pairs(count, 1 << b))  3.12 us
    ppermute x2, starting transfers between devices, ring_gather(): going_right = lax.ppermute(going_right, axis, right)  3.03 us
  transfers between devices with their start and end apart: 11, of which 11 were waited for; matrix products, arithmetic and copies ran while one was open for 2% of the time, Pallas kernels for 0%

profile of v5, /device:TPU:0, one launch (start us, length us, event | category | flops | bytes accessed | tf_op | source)
XLA Modules:
  0.0 80.1 jit_solution(18275745780738250979)
XLA Ops:
  0.0 1.5 %convert_reduce_fusion = f32[2,128]{1,0:T(2,128)S(1)} fusion(bf16[2,128,1536]{2,1,0:T(8,128)(2,1)} %param.13), kind=kLoop, calls=%fused_computation.7 | loop fusion | flops 786176 | bytes 787456 | tf_op jit(solution)/shard_map/reduce_sum | solution.py:31
  1.5 1.5 %fusion.6 = f32[2,128]{1,0:T(2,128)S(1)} fusion(bf16[2,128,1536]{2,1,0:T(8,128)(2,1)} %param.13, f32[2,128]{1,0:T(2,128)S(1)} %broadcast_multiply_fusion.1), kind=kLoop, calls=%fused_computation.10 | loop fusion | flops 1572608 | bytes 788480 | tf_op jit(solution)/shard_map/reduce_sum | solution.py:33
  3.0 0.9 %fusion.15.proj_ref = bf16[3,2,128,256]{3,2,1,0:T(8,128)(2,1)S(1)} fusion(bf16[3,1536,256]{2,1,0:T(8,128)(2,1)S(1)} %copy-done, bf16[2,128,1536]{2,1,0:T(8,128)(2,1)S(1)} %copy-done.1, f32[1536]{0:T(1024)S(1)} %copy-done.10, f32[2,128]{1,0:T(2,128)S(1)} %add_rsqrt_fusion.1, f32[2,128]{1,0:T(2,128)S(1)} %broadcast_multiply_fusion.1), kind=kOutput, calls=%fused_computation.15 | convolution fusion | flops 606142464 | bytes 3547136 | tf_op jit(solution)/shard_map/std,idc->istc/dot_general | solution.py:166
  3.9 0.8 slice.20
  4.7 3.0 %collective-permute-start = (bf16[2,2,128,256]{3,2,1,0:T(8,128)(2,1)}, bf16[2,2,128,256]{3,2,1,0:T(8,128)(2,1)}, u32[]{:S(2)}, u32[]{:S(2)}) collective-permute-start(bf16[2,2,128,256]{3,2,1,0:T(8,128)(2,1)} %slice.20), channel_id=1, source_target_pairs={{0,4},{4,8},{8,12},{12,0},{1,5},{5,9},{9,13},{13,1},{2,6},{6,10},{... | collective-permute-start | bytes 786440 | tf_op jit(solution)/shard_map/ppermute | solution.py:91
  7.7 2.0 %collective-permute-start.1 = (bf16[2,2,128,256]{3,2,1,0:T(8,128)(2,1)}, bf16[2,2,128,256]{3,2,1,0:T(8,128)(2,1)}, u32[]{:S(2)}, u32[]{:S(2)}) collective-permute-start(bf16[2,2,128,256]{3,2,1,0:T(8,128)(2,1)} %slice.20), channel_id=1, source_target_pairs={{0,12},{4,0},{8,4},{12,8},{1,13},{5,1},{9,5},{13,9},{2,14},{6,2},{... | collective-permute-start | bytes 786440 | tf_op jit(solution)/shard_map/ppermute | solution.py:94
  9.7 7.5 %collective-permute-done.refs_0_ = bf16[2,2,128,256]{3,2,1,0:T(8,128)(2,1)} collective-permute-done((bf16[2,2,128,256]{3,2,1,0:T(8,128)(2,1)}, bf16[2,2,128,256]{3,2,1,0:T(8,128)(2,1)}, u32[]{:S(2)}, u32[]{:S(2)}) %collective-permute-start) | collective-permute-done | bytes 262176 | tf_op jit(solution)/shard_map/ppermute | solution.py:91
  17.2 0.6 fusion.46.starts_ref
  17.8 3.8 %collective-permute-done.1.refs_1_ = bf16[2,2,128,256]{3,2,1,0:T(8,128)(2,1)} collective-permute-done((bf16[2,2,128,256]{3,2,1,0:T(8,128)(2,1)}, bf16[2,2,128,256]{3,2,1,0:T(8,128)(2,1)}, u32[]{:S(2)}, u32[]{:S(2)}) %collective-permute-start.1) | collective-permute-done | bytes 262176 | tf_op jit(solution)/shard_map/ppermute | solution.py:94
  21.6 6.0 %collective-permute-done.2.refs_2_ = bf16[2,2,128,256]{3,2,1,0:T(8,128)(2,1)} collective-permute-done((bf16[2,2,128,256]{3,2,1,0:T(8,128)(2,1)}, bf16[2,2,128,256]{3,2,1,0:T(8,128)(2,1)}, u32[]{:S(2)}, u32[]{:S(2)}) %collective-permute-start.2) | collective-permute-done | bytes 262176 | tf_op jit(solution)/shard_map/ppermute | solution.py:91
  27.6 5.2 %shard_map.127 = bf16[2,128,256]{2,1,0:T(8,128)(2,1)} custom-call(s32[2]{0:T(128)} %counts_ref.1, s32[4]{0:T(128)} %fusion.46.starts_ref, bf16[3,2,128,256]{3,2,1,0:T(8,128)(2,1)} %copy-done.3, bf16[2,2,128,256]{3,2,1,0:T(8,128)(2,1)} %collective-permute-done.refs_0_, bf16[2,2,128,256]{3,2,1,0:T(8,128)(2,1)} %collective-permute-done.1.refs_1_, ...), custom_call_target="tpu_custom_call" | custom-call | tf_op jit(solution)/shard_map/pallas_call | solution.py:132
  32.8 1.6 %convolution_convert_fusion = bf16[2,128,1536]{2,1,0:T(8,128)(2,1)S(1)} fusion(bf16[2,128,256]{2,1,0:T(8,128)(2,1)} %shard_map.127, bf16[256,1536]{1,0:T(8,128)(2,1)} %param.17), kind=kOutput, calls=%fused_computation | convolution fusion | flops 201719808 | bytes 1703936 | tf_op jit(solution)/shard_map/stc,cd->std/dot_general | solution.py:173
  34.5 0.8 copy.56
  35.2 2.1 %collective-permute-done.3 = bf16[2,2,32,1536]{3,2,0,1:T(8,128)(2,1)} collective-permute-done((bf16[2,2,32,1536]{3,2,0,1:T(8,128)(2,1)}, bf16[2,2,32,1536]{3,2,0,1:T(8,128)(2,1)}, u32[]{:S(2)}, u32[]{:S(2)}) %collective-permute-start.3) | collective-permute-done | bytes 393248 | tf_op jit(solution)/shard_map/ppermute | solution.py:63
  37.3 1.1 %convert_add_fusion.1 = f32[2,2,32,1536]{3,2,0,1:T(8,128)S(1)} fusion(bf16[2,2,32,1536]{3,2,0,1:T(8,128)(2,1)} %collective-permute-done.3, bf16[2,2,1,32,1536]{4,3,2,1,0:T(8,128)(2,1)S(1)} %get-tuple-element.11), kind=kLoop, calls=%fused_computation.20 | loop fusion | flops 589824 | bytes 1572864 | tf_op jit(solution)/shard_map/add | solution.py:64
  38.4 0.9 %copy-done.2 = f32[2,2,32,1536]{3,2,0,1:T(8,128)} copy-done((f32[2,2,32,1536]{3,2,0,1:T(8,128)}, f32[2,2,32,1536]{3,2,0,1:T(8,128)S(1)}, u32[]{:S(2)}) %copy-start.2) | copy-done | bytes 786456
  39.3 1.6 %collective-permute-start.4 = (bf16[2,32,1536]{2,1,0:T(8,128)(2,1)S(1)}, bf16[2,32,1536]{2,1,0:T(8,128)(2,1)}, u32[]{:S(2)}, u32[]{:S(2)}) collective-permute-start(bf16[2,32,1536]{2,1,0:T(8,128)(2,1)S(1)} %fusion.39), channel_id=1, source_target_pairs={{0,2},{1,3},{2,0},{3,1},{4,6},{5,7},{6,4},{7,5},{8,10},{9,11},{10,... | collective-permute-start | bytes 589832 | tf_op jit(solution)/shard_map/ppermute | solution.py:63
  40.9 5.6 %collective-permute-done.4 = bf16[2,32,1536]{2,1,0:T(8,128)(2,1)} collective-permute-done((bf16[2,32,1536]{2,1,0:T(8,128)(2,1)S(1)}, bf16[2,32,1536]{2,1,0:T(8,128)(2,1)}, u32[]{:S(2)}, u32[]{:S(2)}) %collective-permute-start.4) | collective-permute-done | bytes 196640 | tf_op jit(solution)/shard_map/ppermute | solution.py:63
  46.4 1.2 %fusion.49 = (f32[2,32]{1,0:T(2,128)S(1)}, f32[2,32,1536]{2,1,0:T(8,128)S(1)}) fusion(bf16[2,32,1536]{2,1,0:T(8,128)(2,1)} %collective-permute-done.4, f32[2,2,32,1536]{3,2,0,1:T(8,128)} %copy-done.2, s32[]{:T(128)S(6)} %select_n.64, bf16[2,128,1536]{2,1,0:T(8,128)(2,1)S(1)} %copy-done.1, s32[]{:T(128)S(6)} %select_n.60), kind=kLoop, calls=%fused_computation.85 | loop fusion | flops 491456 | bytes 1179912 | tf_op jit(solution)/shard_map/reduce_sum | solution.py:31
  47.7 0.2 multiply_reduce_fusion
  47.9 0.1 multiply_convert_fusion.1
  48.0 1.6 %collective-permute-start.5 = (bf16[2,32,1536]{2,1,0:T(8,128)(2,1)S(1)}, bf16[2,32,1536]{2,1,0:T(8,128)(2,1)S(1)}, u32[]{:S(2)}, u32[]{:S(2)}) collective-permute-start(bf16[2,32,1536]{2,1,0:T(8,128)(2,1)S(1)} %multiply_convert_fusion.1), channel_id=1, source_target_pairs={{0,2},{1,3},{2,0},{3,1},{4,6},{5,7},{6,4},{7,5},{8,10},{9,11},{10,... | collective-permute-start | bytes 589832 | tf_op jit(solution)/shard_map/ppermute | solution.py:75
  49.6 4.6 %collective-permute-done.5 = bf16[2,32,1536]{2,1,0:T(8,128)(2,1)S(1)} collective-permute-done((bf16[2,32,1536]{2,1,0:T(8,128)(2,1)S(1)}, bf16[2,32,1536]{2,1,0:T(8,128)(2,1)S(1)}, u32[]{:S(2)}, u32[]{:S(2)}) %collective-permute-start.5) | collective-permute-done | bytes 196640 | tf_op jit(solution)/shard_map/ppermute | solution.py:75
  54.2 0.2 select_bitcast_fusion.3
  54.4 0.1 collective-permute-start.6
  54.5 0.7 broadcast_compare_fusion
  55.3 1.1 %collective-permute-done.6 = bf16[2,2,32,1536]{3,2,0,1:T(8,128)(2,1)} collective-permute-done((bf16[2,2,32,1536]{3,2,0,1:T(8,128)(2,1)S(1)}, bf16[2,2,32,1536]{3,2,0,1:T(8,128)(2,1)}, u32[]{:S(2)}, u32[]{:S(2)}) %collective-permute-start.6) | collective-permute-done | bytes 393248 | tf_op jit(solution)/shard_map/ppermute | solution.py:75
  56.4 1.1 %select_bitcast_fusion.1 = (bf16[2,2,1,32,1536]{4,3,0,1,2:T(8,128)(2,1)S(1)}, bf16[2,2,1,32,1536]{4,3,0,1,2:T(8,128)(2,1)S(1)}) fusion(bf16[2,2,32,1536]{3,2,0,1:T(8,128)(2,1)} %collective-permute-done.6, pred[]{:T(512)S(6)} %eq.8, bf16[2,1,32,1536]{3,2,0,1:T(8,128)(2,1)S(1)} %get-tuple-element.14, bf16[2,1,32,1536]{3,2,0,1:T(8,128)(2,1)S(1)} %get-tuple-element.13), kind=kLoop, calls=%fused_computation.48 | loop fusion | flops 589824 | bytes 1572865 | tf_op jit(solution)/shard_map/stack | solution.py:78
  57.4 0.1 pad_maximum_fusion
  57.6 1.5 %copy-done.7 = bf16[2,1536,384]{2,1,0:T(8,128)(2,1)S(1)} copy-done((bf16[2,1536,384]{2,1,0:T(8,128)(2,1)S(1)}, bf16[2,1536,384]{2,1,0:T(8,128)(2,1)}, u32[]{:S(2)}) %copy-start.7) | copy-done | bytes 2359320
  59.1 0.8 fusion.9
  59.9 0.1 bitcast_select_fusion
  60.1 1.6 %collective-permute-start.7 = (bf16[2,15,384]{2,1,0:T(8,128)(2,1)S(1)}, bf16[2,15,384]{2,1,0:T(8,128)(2,1)S(1)}, u32[]{:S(2)}, u32[]{:S(2)}) collective-permute-start(bf16[2,15,384]{2,1,0:T(8,128)(2,1)S(1)} %get-tuple-element.15), channel_id=1, source_target_pairs={{0,4},{4,8},{8,12},{1,5},{5,9},{9,13},{2,6},{6,10},{10,14},{3,7},{... | collective-permute-start | bytes 69128 | tf_op jit(solution)/shard_map/ppermute | solution.py:24
  61.7 1.3 %collective-permute-start.8 = (bf16[2,15,384]{2,1,0:T(8,128)(2,1)S(1)}, bf16[2,15,384]{2,1,0:T(8,128)(2,1)S(1)}, u32[]{:S(2)}, u32[]{:S(2)}) collective-permute-start(bf16[2,15,384]{2,1,0:T(8,128)(2,1)S(1)} %get-tuple-element.16), channel_id=1, source_target_pairs={{4,0},{8,4},{12,8},{5,1},{9,5},{13,9},{6,2},{10,6},{14,10},{7,3},{... | collective-permute-start | bytes 69128 | tf_op jit(solution)/shard_map/ppermute | solution.py:25
  63.0 0.2 collective-permute-done.7
  63.2 4.2 %collective-permute-done.8 = bf16[2,15,384]{2,1,0:T(8,128)(2,1)S(1)} collective-permute-done((bf16[2,15,384]{2,1,0:T(8,128)(2,1)S(1)}, bf16[2,15,384]{2,1,0:T(8,128)(2,1)S(1)}, u32[]{:S(2)}, u32[]{:S(2)}) %collective-permute-start.8) | collective-permute-done | bytes 23072 | tf_op jit(solution)/shard_map/ppermute | solution.py:25
  67.4 0.1 pad_maximum_fusion.2
  67.5 1.1 %fusion.37 = f32[2,128,384]{2,0,1:T(2,128)S(1)} fusion(bf16[2,158,384]{2,1,0:T(8,128)(2,1)S(1)} %pad_maximum_fusion.2, f32[31,1,384]{2,0,1:T(8,128)S(1)} %bitcast.87), kind=kOutput, calls=%fused_computation.54 | convolution fusion | flops 36569088 | bytes 683520 | tf_op jit(solution)/shard_map/conv_general_dilated | solution.py:189
  68.6 0.2 copy-done.8
  68.8 0.6 convolution_convert_fusion.1
  69.4 0.1 constant_dynamic-slice_fusion.1
  69.5 0.8 copy.55
  70.3 1.9 %collective-permute-done.9 = bf16[2,2,32,1536]{3,2,0,1:T(8,128)(2,1)S(1)} collective-permute-done((bf16[2,2,32,1536]{3,2,0,1:T(8,128)(2,1)}, bf16[2,2,32,1536]{3,2,0,1:T(8,128)(2,1)S(1)}, u32[]{:S(2)}, u32[]{:S(2)}) %collective-permute-start.9) | collective-permute-done | bytes 393248 | tf_op jit(solution)/shard_map/ppermute | solution.py:63
  72.2 0.1 convert_add_fusion
  72.3 1.6 %collective-permute-start.10 = (bf16[2,32,1536]{2,1,0:T(8,128)(2,1)S(1)}, bf16[2,32,1536]{2,1,0:T(8,128)(2,1)S(1)}, u32[]{:S(2)}, u32[]{:S(2)}) collective-permute-start(bf16[2,32,1536]{2,1,0:T(8,128)(2,1)S(1)} %fusion.40), channel_id=1, source_target_pairs={{0,2},{1,3},{2,0},{3,1},{4,6},{5,7},{6,4},{7,5},{8,10},{9,11},{10,... | collective-permute-start | bytes 589832 | tf_op jit(solution)/shard_map/ppermute | solution.py:63
  73.9 0.1 broadcast_compare_fusion.1
  74.0 5.4 %collective-permute-done.10 = bf16[2,32,1536]{2,1,0:T(8,128)(2,1)S(1)} collective-permute-done((bf16[2,32,1536]{2,1,0:T(8,128)(2,1)S(1)}, bf16[2,32,1536]{2,1,0:T(8,128)(2,1)S(1)}, u32[]{:S(2)}, u32[]{:S(2)}) %collective-permute-start.10) | collective-permute-done | bytes 196640 | tf_op jit(solution)/shard_map/ppermute | solution.py:63
  79.3 0.8 fusion.33
  (41 shorter events, 0.3 us)
Async XLA Ops:
  0.0 3.0 %copy-start = (bf16[3,1536,256]{2,1,0:T(8,128)(2,1)S(1)}, bf16[3,1536,256]{2,1,0:T(8,128)(2,1)}, u32[]{:S(2)}) copy-start(bf16[3,1536,256]{2,1,0:T(8,128)(2,1)} %param.16) | copy-start | bytes 7077892
  0.0 3.0 %copy-start.1 = (bf16[2,128,1536]{2,1,0:T(8,128)(2,1)S(1)}, bf16[2,128,1536]{2,1,0:T(8,128)(2,1)}, u32[]{:S(2)}) copy-start(bf16[2,128,1536]{2,1,0:T(8,128)(2,1)} %param.13) | copy-start | bytes 2359300
  0.0 3.0 %copy-start.10 = (f32[1536]{0:T(1024)S(1)}, f32[1536]{0:T(1024)}, u32[]{:S(2)}) copy-start(f32[1536]{0:T(1024)} %param.15) | copy-start | bytes 18436
  3.0 14.2 %copy-start.13 = (s32[4]{0:T(128)S(1)}, s32[4]{0:T(128)}, u32[]{:S(2)}) copy-start(s32[4]{0:T(128)} %constant.78.clone) | copy-start | bytes 52
  3.9 23.7 %copy-start.3 = (bf16[3,2,128,256]{3,2,1,0:T(8,128)(2,1)}, bf16[3,2,128,256]{3,2,1,0:T(8,128)(2,1)S(1)}, u32[]{:S(2)}) copy-start(bf16[3,2,128,256]{3,2,1,0:T(8,128)(2,1)S(1)} %fusion.15.proj_ref) | copy-start | bytes 1179652
  4.7 12.5 %collective-permute-start = (bf16[2,2,128,256]{3,2,1,0:T(8,128)(2,1)}, bf16[2,2,128,256]{3,2,1,0:T(8,128)(2,1)}, u32[]{:S(2)}, u32[]{:S(2)}) collective-permute-start(bf16[2,2,128,256]{3,2,1,0:T(8,128)(2,1)} %slice.20), channel_id=1, source_target_pairs={{0,4},{4,8},{8,12},{12,0},{1,5},{5,9},{9,13},{13,1},{2,6},{6,10},{... | collective-permute-start | bytes 786440 | tf_op jit(solution)/shard_map/ppermute | solution.py:91
  7.7 13.9 %collective-permute-start.1 = (bf16[2,2,128,256]{3,2,1,0:T(8,128)(2,1)}, bf16[2,2,128,256]{3,2,1,0:T(8,128)(2,1)}, u32[]{:S(2)}, u32[]{:S(2)}) collective-permute-start(bf16[2,2,128,256]{3,2,1,0:T(8,128)(2,1)} %slice.20), channel_id=1, source_target_pairs={{0,12},{4,0},{8,4},{12,8},{1,13},{5,1},{9,5},{13,9},{2,14},{6,2},{... | collective-permute-start | bytes 786440 | tf_op jit(solution)/shard_map/ppermute | solution.py:94
  17.2 10.4 %collective-permute-start.2 = (bf16[2,2,128,256]{3,2,1,0:T(8,128)(2,1)}, bf16[2,2,128,256]{3,2,1,0:T(8,128)(2,1)}, u32[]{:S(2)}, u32[]{:S(2)}) collective-permute-start(bf16[2,2,128,256]{3,2,1,0:T(8,128)(2,1)} %collective-permute-done.refs_0_), channel_id=1, source_target_pairs={{0,4},{4,8},{8,12},{12,0},{1,5},{5,9},{9,13},{13,1},{2,6},{6,10},{... | collective-permute-start | bytes 786440 | tf_op jit(solution)/shard_map/ppermute | solution.py:91
  35.2 2.1 %collective-permute-start.3 = (bf16[2,2,32,1536]{3,2,0,1:T(8,128)(2,1)}, bf16[2,2,32,1536]{3,2,0,1:T(8,128)(2,1)}, u32[]{:S(2)}, u32[]{:S(2)}) collective-permute-start(bf16[2,2,32,1536]{3,2,0,1:T(8,128)(2,1)} %bitcast.83), channel_id=1, source_target_pairs={{0,1},{1,0},{2,3},{3,2},{4,5},{5,4},{6,7},{7,6},{8,9},{9,8},{10,11... | collective-permute-start | bytes 1179656 | tf_op jit(solution)/shard_map/ppermute | solution.py:63
  37.3 10.6 %copy-start.4 = (f32[1536]{0:T(1024)S(1)}, f32[1536]{0:T(1024)}, u32[]{:S(2)}) copy-start(f32[1536]{0:T(1024)} %param.18) | copy-start | bytes 18436
  38.4 0.9 %copy-start.2 = (f32[2,2,32,1536]{3,2,0,1:T(8,128)}, f32[2,2,32,1536]{3,2,0,1:T(8,128)S(1)}, u32[]{:S(2)}) copy-start(f32[2,2,32,1536]{3,2,0,1:T(8,128)S(1)} %convert_add_fusion.1) | copy-start | bytes 2359300
  39.3 7.1 %collective-permute-start.4 = (bf16[2,32,1536]{2,1,0:T(8,128)(2,1)S(1)}, bf16[2,32,1536]{2,1,0:T(8,128)(2,1)}, u32[]{:S(2)}, u32[]{:S(2)}) collective-permute-start(bf16[2,32,1536]{2,1,0:T(8,128)(2,1)S(1)} %fusion.39), channel_id=1, source_target_pairs={{0,2},{1,3},{2,0},{3,1},{4,6},{5,7},{6,4},{7,5},{8,10},{9,11},{10,... | collective-permute-start | bytes 589832 | tf_op jit(solution)/shard_map/ppermute | solution.py:63
  48.0 6.2 %collective-permute-start.5 = (bf16[2,32,1536]{2,1,0:T(8,128)(2,1)S(1)}, bf16[2,32,1536]{2,1,0:T(8,128)(2,1)S(1)}, u32[]{:S(2)}, u32[]{:S(2)}) collective-permute-start(bf16[2,32,1536]{2,1,0:T(8,128)(2,1)S(1)} %multiply_convert_fusion.1), channel_id=1, source_target_pairs={{0,2},{1,3},{2,0},{3,1},{4,6},{5,7},{6,4},{7,5},{8,10},{9,11},{10,... | collective-permute-start | bytes 589832 | tf_op jit(solution)/shard_map/ppermute | solution.py:75
  54.4 1.9 %collective-permute-start.6 = (bf16[2,2,32,1536]{3,2,0,1:T(8,128)(2,1)S(1)}, bf16[2,2,32,1536]{3,2,0,1:T(8,128)(2,1)}, u32[]{:S(2)}, u32[]{:S(2)}) collective-permute-start(bf16[2,2,32,1536]{3,2,0,1:T(8,128)(2,1)S(1)} %pad_maximum_fusion.1), channel_id=1, source_target_pairs={{0,1},{1,0},{2,3},{3,2},{4,5},{5,4},{6,7},{7,6},{8,9},{9,8},{10,11... | collective-permute-start | bytes 1179656 | tf_op jit(solution)/shard_map/ppermute | solution.py:75
  57.4 1.7 %copy-start.7 = (bf16[2,1536,384]{2,1,0:T(8,128)(2,1)S(1)}, bf16[2,1536,384]{2,1,0:T(8,128)(2,1)}, u32[]{:S(2)}) copy-start(bf16[2,1536,384]{2,1,0:T(8,128)(2,1)} %param.19) | copy-start | bytes 7077892
  59.9 7.6 %copy-start.9 = (f32[31,384]{1,0:T(8,128)S(1)}, f32[31,384]{1,0:T(8,128)}, u32[]{:S(2)}) copy-start(f32[31,384]{1,0:T(8,128)} %param.20) | copy-start | bytes 142852
  60.1 3.1 %collective-permute-start.7 = (bf16[2,15,384]{2,1,0:T(8,128)(2,1)S(1)}, bf16[2,15,384]{2,1,0:T(8,128)(2,1)S(1)}, u32[]{:S(2)}, u32[]{:S(2)}) collective-permute-start(bf16[2,15,384]{2,1,0:T(8,128)(2,1)S(1)} %get-tuple-element.15), channel_id=1, source_target_pairs={{0,4},{4,8},{8,12},{1,5},{5,9},{9,13},{2,6},{6,10},{10,14},{3,7},{... | collective-permute-start | bytes 69128 | tf_op jit(solution)/shard_map/ppermute | solution.py:24
  61.7 5.7 %collective-permute-start.8 = (bf16[2,15,384]{2,1,0:T(8,128)(2,1)S(1)}, bf16[2,15,384]{2,1,0:T(8,128)(2,1)S(1)}, u32[]{:S(2)}, u32[]{:S(2)}) collective-permute-start(bf16[2,15,384]{2,1,0:T(8,128)(2,1)S(1)} %get-tuple-element.16), channel_id=1, source_target_pairs={{4,0},{8,4},{12,8},{5,1},{9,5},{13,9},{6,2},{10,6},{14,10},{7,3},{... | collective-permute-start | bytes 69128 | tf_op jit(solution)/shard_map/ppermute | solution.py:25
  67.5 1.3 %copy-start.8 = (bf16[384,1536]{1,0:T(8,128)(2,1)S(1)}, bf16[384,1536]{1,0:T(8,128)(2,1)}, u32[]{:S(2)}) copy-start(bf16[384,1536]{1,0:T(8,128)(2,1)} %param.23) | copy-start | bytes 3538948
  67.5 1.3 %copy-start.11 = (f32[384]{0:T(512)S(1)}, f32[384]{0:T(512)}, u32[]{:S(2)}) copy-start(f32[384]{0:T(512)} %param.22) | copy-start | bytes 4612
  67.5 1.3 %copy-start.12 = (f32[384]{0:T(512)S(1)}, f32[384]{0:T(512)}, u32[]{:S(2)}) copy-start(f32[384]{0:T(512)} %param.21) | copy-start | bytes 4612
  69.4 0.9 %copy-start.5 = (s32[1536]{0:T(1024)S(1)}, s32[1536]{0:T(1024)}, u32[]{:S(2)}) copy-start(s32[1536]{0:T(1024)} %param.24) | copy-start | bytes 18436
  69.5 4.4 %copy-start.6 = (s32[2]{0:T(128)S(1)}, s32[2]{0:T(128)}, u32[]{:S(2)}) copy-start(s32[2]{0:T(128)} %counts_ref.1) | copy-start | bytes 28
  70.3 1.9 %collective-permute-start.9 = (bf16[2,2,32,1536]{3,2,0,1:T(8,128)(2,1)}, bf16[2,2,32,1536]{3,2,0,1:T(8,128)(2,1)S(1)}, u32[]{:S(2)}, u32[]{:S(2)}) collective-permute-start(bf16[2,2,32,1536]{3,2,0,1:T(8,128)(2,1)} %bitcast.82), channel_id=1, source_target_pairs={{0,1},{1,0},{2,3},{3,2},{4,5},{5,4},{6,7},{7,6},{8,9},{9,8},{10,11... | collective-permute-start | bytes 1179656 | tf_op jit(solution)/shard_map/ppermute | solution.py:63
  72.3 7.0 %collective-permute-start.10 = (bf16[2,32,1536]{2,1,0:T(8,128)(2,1)S(1)}, bf16[2,32,1536]{2,1,0:T(8,128)(2,1)S(1)}, u32[]{:S(2)}, u32[]{:S(2)}) collective-permute-start(bf16[2,32,1536]{2,1,0:T(8,128)(2,1)S(1)} %fusion.40), channel_id=1, source_target_pairs={{0,2},{1,3},{2,0},{3,1},{4,6},{5,7},{6,4},{7,5},{8,10},{9,11},{10,... | collective-permute-start | bytes 589832 | tf_op jit(solution)/shard_map/ppermute | solution.py:63

commit v6 on v1

--- a/solution.py
+++ b/solution.py
@@ -23,10 +23,20 @@
     return x
 
 
+def row_mean(values):
+    width = values.shape[-1]
+    ones = jnp.full((width, 128), 1.0 / width, jnp.float32)
+    sums = jnp.einsum(
+        "...d,dk->...k", values, ones, precision=lax.Precision.HIGHEST,
+        preferred_element_type=jnp.float32,
+    )
+    return sums[..., :1]
+
+
 def layer_norm(values, gain):
-    centre = jnp.mean(values, axis=-1, keepdims=True)
+    centre = row_mean(values)
     centred = values - centre
-    variance = jnp.mean(centred * centred, axis=-1, keepdims=True)
+    variance = row_mean(centred * centred)
     return centred * lax.rsqrt(variance + epsilon) * gain
 
 
@@ -156,13 +166,15 @@
     gated_rows = jnp.where(frame_live[..., None], gated_rows, jnp.zeros((), jnp.bfloat16))
     rim_width = kernel.shape[0] // 2
     padded = with_halo(gated_rows, (("ctx", 1),), rim_width)
-    depthwise = jnp.zeros(gated_rows.shape, jnp.float32)
-    for tap_index in range(kernel.shape[0]):
-        depthwise = (
-            depthwise
-            + padded[:, tap_index : tap_index + frames_here, :].astype(jnp.float32)
-            * kernel[tap_index]
-        )
+    depthwise = lax.conv_general_dilated(
+        padded.astype(jnp.float32),
+        kernel[:, None, :],
+        window_strides=(1,),
+        padding="VALID",
+        dimension_numbers=("NWC", "WIO", "NWC"),
+        feature_group_count=kernel.shape[1],
+        precision=lax.Precision.HIGHEST,
+    )
     activated = jax.nn.silu(depthwise * bn_scale + bn_shift).astype(jnp.bfloat16)
     conv_part = jnp.einsum("stc,cd->std", activated, w_pw, preferred_element_type=jnp.float32)
     conv_rows = reduce_scatter_rows(conv_part.astype(jnp.bfloat16), "mp", 1)

time: 79.3 us -> 81.5 us (1.028)
  matrix products: 7.34 us -> 12.8 us
  other arithmetic: 11.2 us -> 7.76 us
  waiting for transfers between devices: 39.9 us -> 42.7 us
  local copies, waits for them, and re-layouts: 6.9 us -> 4.31 us
    dot_general x0 -> x4, matrix products: none -> 6.56 us  [row_mean(): jnp.einsum('...d,dk->...k', values, ones, precision=lax.Precision.HIGHEST...]
    reduce_sum x4 -> x0, other arithmetic: 4.31 us -> none  [the longest x2 2.63 us: layer_norm(): centre = jnp.mean(values, axis=-1, keepdims=True)]
    slice x2 -> x1, local copies, waits for them, and re-layouts: 2.32 us -> 0.01 us  [row_mean(): return sums[..., :1]]
    dot_general x1, matrix products: 2.74 us -> 0.59 us  [shards(): jnp.einsum('stc,cd->std', activated, w_pw, preferred_element_type=jnp.flo...]
    ppermute x2, waiting for transfers between devices: 5.08 us -> 6.38 us  [all_gather_rows(): got = lax.ppermute(acc, axis, xor_pairs(count, 1 << b))]
    add x0 -> x1, other arithmetic: none -> 1.08 us  [shards(): residual_mine = features_mine.astype(jnp.float32) + attn_mine]
    conv_general_dilated x0 -> x1, matrix products: none -> 1.07 us  [shards(): lax.conv_general_dilated(padded.astype(jnp.float32), kernel[:, None, :],...]
    ppermute x1, waiting for transfers between devices: 3.37 us -> 4.22 us  [with_halo(): after = lax.ppermute(initial, axis, down)]
  transfers between devices with their start and end apart: 11 -> 11, of which waited for: 10 -> 11; matrix products, arithmetic and copies ran while one was open for 4% -> 1% of each run, Pallas kernels for 0% -> 0%
where the time goes in v6:
time: 81.5 us; the launch traced here: 81 us
  waiting for transfers between devices  42.7 us (52%)
  starting transfers between devices  12.9 us (16%)
  matrix products  12.8 us (16%)
  other arithmetic  7.76 us (10%)
  local copies, waits for them, and re-layouts  4.31 us (5%)
    ppermute x4, waiting for transfers between devices, reduce_scatter_rows(): lax.ppermute(send.astype(jnp.bfloat16), axis, xor_pairs(count, 1 << b))  14.6 us
    ppermute x2, waiting for transfers between devices, ring_gather(): going_right = lax.ppermute(going_right, axis, right)  13.2 us
    dot_general x4, matrix products, row_mean(): jnp.einsum('...d,dk->...k', values, ones, precision=lax.Precision.HIGHEST...  6.56 us
    ppermute x2, waiting for transfers between devices, all_gather_rows(): got = lax.ppermute(acc, axis, xor_pairs(count, 1 << b))  6.38 us
    ppermute x1, waiting for transfers between devices, with_halo(): after = lax.ppermute(initial, axis, down)  4.22 us
    ppermute x1, waiting for transfers between devices, ring_gather(): going_left = lax.ppermute(going_left, axis, left)  4.07 us
    ppermute x4, starting transfers between devices, reduce_scatter_rows(): lax.ppermute(send.astype(jnp.bfloat16), axis, xor_pairs(count, 1 << b))  3.25 us
    ppermute x2, starting transfers between devices, ring_gather(): going_right = lax.ppermute(going_right, axis, right)  3.08 us
  transfers between devices with their start and end apart: 11, of which 11 were waited for; matrix products, arithmetic and copies ran while one was open for 1% of the time, Pallas kernels for 0%

profile of v6, /device:TPU:0, one launch (start us, length us, event | category | flops | bytes accessed | tf_op | source)
XLA Modules:
  0.0 81.0 jit_solution(8484630095637054063)
XLA Ops:
  0.0 2.2 %convolution_bitcast_fusion.1 = f32[2,128,128]{1,2,0:T(8,128)S(1)} fusion(bf16[2,128,1536]{2,1,0:T(8,128)(2,1)} %param.12), kind=kOutput, calls=%fused_computation.20 | convolution fusion | flops 603979776 | bytes 917504 | tf_op jit(solution)/shard_map/...d,dk->...k/dot_general | solution.py:29
  2.2 2.6 %fusion.22 = f32[2,128,1]{1,2,0:T(1,128)S(1)} fusion(bf16[2,128,1536]{2,1,0:T(8,128)(2,1)} %param.12, f32[2,128]{1,0:T(2,128)S(1)} %bitcast.130), kind=kOutput, calls=%fused_computation.22 | convolution fusion | flops 5898496 | bytes 788480 | tf_op jit(solution)/shard_map/...d,dk->...k/dot_general | solution.py:29
  4.8 2.0 %fusion.15 = bf16[3,2,128,256]{3,2,0,1:T(8,128)(2,1)S(1)} fusion(bf16[3,1536,256]{2,1,0:T(8,128)(2,1)S(1)} %copy-done, bf16[2,128,1536]{2,1,0:T(8,128)(2,1)} %param.12, f32[1536]{0:T(1024)} %param.14, f32[2,128]{1,0:T(2,128)S(1)} %bitcast.133, f32[2,128]{1,0:T(2,128)S(1)} %bitcast.131), kind=kOutput, calls=%fused_computation.17 | convolution fusion | flops 606142464 | bytes 3547136 | tf_op jit(solution)/shard_map/std,idc->istc/dot_general | solution.py:126
  6.8 3.1 %collective-permute-start.1 = (bf16[2,2,128,256]{3,2,0,1:T(8,128)(2,1)S(1)}, bf16[2,2,128,256]{3,2,0,1:T(8,128)(2,1)}, u32[]{:S(2)}, u32[]{:S(2)}) collective-permute-start(bf16[2,2,128,256]{3,2,0,1:T(8,128)(2,1)S(1)} %get-tuple-element.16), channel_id=1, source_target_pairs={{0,4},{4,8},{8,12},{12,0},{1,5},{5,9},{9,13},{13,1},{2,6},{6,10},{... | collective-permute-start | bytes 786440 | tf_op jit(solution)/shard_map/ppermute | solution.py:97
  9.9 2.1 %collective-permute-start = (bf16[2,2,128,256]{3,2,0,1:T(8,128)(2,1)S(1)}, bf16[2,2,128,256]{3,2,0,1:T(8,128)(2,1)}, u32[]{:S(2)}, u32[]{:S(2)}) collective-permute-start(bf16[2,2,128,256]{3,2,0,1:T(8,128)(2,1)S(1)} %get-tuple-element.16), channel_id=1, source_target_pairs={{0,12},{4,0},{8,4},{12,8},{1,13},{5,1},{9,5},{13,9},{2,14},{6,2},{... | collective-permute-start | bytes 786440 | tf_op jit(solution)/shard_map/ppermute | solution.py:100
  12.0 7.2 %collective-permute-done.1 = bf16[2,2,128,256]{3,2,0,1:T(8,128)(2,1)} collective-permute-done((bf16[2,2,128,256]{3,2,0,1:T(8,128)(2,1)S(1)}, bf16[2,2,128,256]{3,2,0,1:T(8,128)(2,1)}, u32[]{:S(2)}, u32[]{:S(2)}) %collective-permute-start.1) | collective-permute-done | bytes 262176 | tf_op jit(solution)/shard_map/ppermute | solution.py:97
  19.3 0.1 copy.41
  19.5 0.1 broadcast_compare_fusion
  19.5 4.1 %collective-permute-done = bf16[2,2,128,256]{3,2,0,1:T(8,128)(2,1)} collective-permute-done((bf16[2,2,128,256]{3,2,0,1:T(8,128)(2,1)S(1)}, bf16[2,2,128,256]{3,2,0,1:T(8,128)(2,1)}, u32[]{:S(2)}, u32[]{:S(2)}) %collective-permute-start) | collective-permute-done | bytes 262176 | tf_op jit(solution)/shard_map/ppermute | solution.py:100
  23.6 6.0 %collective-permute-done.2 = bf16[2,2,128,256]{3,2,0,1:T(8,128)(2,1)} collective-permute-done((bf16[2,2,128,256]{3,2,0,1:T(8,128)(2,1)}, bf16[2,2,128,256]{3,2,0,1:T(8,128)(2,1)}, u32[]{:S(2)}, u32[]{:S(2)}) %collective-permute-start.2) | collective-permute-done | bytes 262176 | tf_op jit(solution)/shard_map/ppermute | solution.py:97
  29.6 1.2 %pad_maximum_fusion = bf16[4,2,2,128,256]{4,3,1,2,0:T(8,128)(2,1)S(1)} fusion(bf16[1,2,2,128,256]{4,3,1,2,0:T(8,128)(2,1)} %bitcast.13, bf16[1,2,2,128,256]{4,3,1,2,0:T(8,128)(2,1)} %bitcast.12, bf16[1,2,2,128,256]{4,3,1,2,0:T(8,128)(2,1)} %bitcast.11, bf16[1,2,2,128,256]{4,3,1,2,0:T(8,128)(2,1)S(1)} %get-tuple-element.15), kind=kLoop, calls=%fused_computation.27 | loop fusion | flops 1572864 | bytes 2097152 | tf_op jit(solution)/shard_map/stack | solution.py:102
  30.9 0.9 %fusion.81 = (bf16[4,1,2,128,256]{4,3,1,2,0:T(8,128)(2,1)S(1)}, bf16[4,1,2,128,256]{4,3,1,2,0:T(8,128)(2,1)}) fusion(bf16[4,2,2,128,256]{4,3,1,2,0:T(8,128)(2,1)S(1)} %pad_maximum_fusion), kind=kLoop, calls=%fused_computation.116 | loop fusion | bytes 2097152 | tf_op jit(solution)/shard_map/slice | solution.py:133
  31.8 1.3 %copy.42 = bf16[4,1,2,128,256]{3,4,2,0,1:T(8,128)(2,1)S(1)} copy(bf16[4,1,2,128,256]{4,3,1,2,0:T(8,128)(2,1)} %get-tuple-element.6) | data formatting | bytes 1048576 | tf_op jit(solution)/shard_map/slice | solution.py:132
  33.1 1.0 %copy.44 = bf16[4,1,2,128,256]{3,4,2,0,1:T(8,128)(2,1)} copy(bf16[4,1,2,128,256]{4,3,1,2,0:T(8,128)(2,1)S(1)} %get-tuple-element.5) | data formatting | bytes 1048576 | tf_op jit(solution)/shard_map/slice | solution.py:133
  34.1 0.7 fusion.4
  34.8 0.5 fusion.5
  35.4 0.7 fusion.27
  36.1 0.4 copy-done.1
  36.5 0.4 convolution_convert_fusion
  37.1 1.8 %collective-permute-done.3 = bf16[2,2,32,1536]{3,2,0,1:T(8,128)(2,1)} collective-permute-done((bf16[2,2,32,1536]{3,2,0,1:T(8,128)(2,1)S(1)}, bf16[2,2,32,1536]{3,2,0,1:T(8,128)(2,1)}, u32[]{:S(2)}, u32[]{:S(2)}) %collective-permute-start.3) | collective-permute-done | bytes 393248 | tf_op jit(solution)/shard_map/ppermute | solution.py:69
  38.9 1.1 %convert_add_fusion.1 = f32[2,2,32,1536]{3,2,0,1:T(8,128)S(1)} fusion(bf16[2,2,32,1536]{3,2,0,1:T(8,128)(2,1)} %collective-permute-done.3, bf16[2,2,1,32,1536]{4,3,2,1,0:T(8,128)(2,1)S(1)} %get-tuple-element.11), kind=kLoop, calls=%fused_computation.35 | loop fusion | flops 589824 | bytes 1572864 | tf_op jit(solution)/shard_map/add | solution.py:70
  40.1 1.5 %collective-permute-start.4 = (bf16[2,32,1536]{2,1,0:T(8,128)(2,1)S(1)}, bf16[2,32,1536]{2,1,0:T(8,128)(2,1)}, u32[]{:S(2)}, u32[]{:S(2)}) collective-permute-start(bf16[2,32,1536]{2,1,0:T(8,128)(2,1)S(1)} %fusion.60), channel_id=1, source_target_pairs={{0,2},{1,3},{2,0},{3,1},{4,6},{5,7},{6,4},{7,5},{8,10},{9,11},{10,... | collective-permute-start | bytes 589832 | tf_op jit(solution)/shard_map/ppermute | solution.py:69
  41.6 5.6 %collective-permute-done.4 = bf16[2,32,1536]{2,1,0:T(8,128)(2,1)} collective-permute-done((bf16[2,32,1536]{2,1,0:T(8,128)(2,1)S(1)}, bf16[2,32,1536]{2,1,0:T(8,128)(2,1)}, u32[]{:S(2)}, u32[]{:S(2)}) %collective-permute-start.4) | collective-permute-done | bytes 196640 | tf_op jit(solution)/shard_map/ppermute | solution.py:69
  47.2 1.1 %fusion.52 = f32[2,32,1536]{2,1,0:T(8,128)S(1)} fusion(bf16[2,32,1536]{2,1,0:T(8,128)(2,1)} %collective-permute-done.4, f32[2,2,32,1536]{3,2,0,1:T(8,128)S(1)} %convert_add_fusion.1, s32[]{:T(128)S(6)} %select_n.73, bf16[2,128,1536]{2,1,0:T(8,128)(2,1)} %param.12, s32[]{:T(128)S(6)} %select_n.68), kind=kLoop, calls=%fused_computation.59 | loop fusion | flops 393216 | bytes 1179656 | tf_op jit(solution)/shard_map/add | solution.py:160
  48.2 0.9 %fusion.68 = f32[2,32,1]{1,2,0:T(1,128)S(1)} fusion(f32[2,32,1536]{2,1,0:T(8,128)S(1)} %fusion.52), kind=kOutput, calls=%fused_computation.89 | convolution fusion | flops 1179648 | bytes 393472 | tf_op jit(solution)/shard_map/...d,dk->...k/dot_general | solution.py:29
  49.1 1.0 %fusion.25 = f32[2,32,1]{1,2,0:T(1,128)S(1)} fusion(f32[2,32,1536]{2,1,0:T(8,128)S(1)} %fusion.52, f32[2,32]{1,0:T(2,128)S(1)} %bitcast.124), kind=kOutput, calls=%fused_computation.24 | convolution fusion | flops 1376320 | bytes 393728 | tf_op jit(solution)/shard_map/...d,dk->...k/dot_general | solution.py:29
  50.1 0.1 multiply_convert_fusion.2
  50.2 1.5 %collective-permute-start.5 = (bf16[2,32,1536]{2,1,0:T(8,128)(2,1)S(1)}, bf16[2,32,1536]{2,1,0:T(8,128)(2,1)S(1)}, u32[]{:S(2)}, u32[]{:S(2)}) collective-permute-start(bf16[2,32,1536]{2,1,0:T(8,128)(2,1)S(1)} %multiply_convert_fusion.2), channel_id=1, source_target_pairs={{0,2},{1,3},{2,0},{3,1},{4,6},{5,7},{6,4},{7,5},{8,10},{9,11},{10,... | collective-permute-start | bytes 589832 | tf_op jit(solution)/shard_map/ppermute | solution.py:81
  51.8 4.6 %collective-permute-done.5 = bf16[2,32,1536]{2,1,0:T(8,128)(2,1)S(1)} collective-permute-done((bf16[2,32,1536]{2,1,0:T(8,128)(2,1)S(1)}, bf16[2,32,1536]{2,1,0:T(8,128)(2,1)S(1)}, u32[]{:S(2)}, u32[]{:S(2)}) %collective-permute-start.5) | collective-permute-done | bytes 196640 | tf_op jit(solution)/shard_map/ppermute | solution.py:81
  56.4 0.2 select_bitcast_fusion.3
  56.7 0.1 broadcast_compare_fusion.1
  56.8 1.7 %collective-permute-done.6 = bf16[2,2,32,1536]{3,2,0,1:T(8,128)(2,1)} collective-permute-done((bf16[2,2,32,1536]{3,2,0,1:T(8,128)(2,1)S(1)}, bf16[2,2,32,1536]{3,2,0,1:T(8,128)(2,1)}, u32[]{:S(2)}, u32[]{:S(2)}) %collective-permute-start.6) | collective-permute-done | bytes 393248 | tf_op jit(solution)/shard_map/ppermute | solution.py:81
  58.5 1.1 %select_bitcast_fusion.1 = (bf16[2,2,1,32,1536]{4,3,0,1,2:T(8,128)(2,1)S(1)}, bf16[2,2,1,32,1536]{4,3,0,1,2:T(8,128)(2,1)S(1)}) fusion(bf16[2,2,32,1536]{3,2,0,1:T(8,128)(2,1)} %collective-permute-done.6, pred[]{:T(512)S(6)} %eq.8, bf16[2,1,32,1536]{3,2,0,1:T(8,128)(2,1)S(1)} %get-tuple-element.14, bf16[2,1,32,1536]{3,2,0,1:T(8,128)(2,1)S(1)} %get-tuple-element.13), kind=kLoop, calls=%fused_computation.68 | loop fusion | flops 589824 | bytes 1572865 | tf_op jit(solution)/shard_map/stack | solution.py:84
  59.6 0.1 pad_maximum_fusion.1
  59.8 0.8 fusion.9
  60.6 0.1 bitcast_select_fusion
  60.7 1.6 %collective-permute-start.7 = (bf16[2,15,384]{2,1,0:T(8,128)(2,1)S(1)}, bf16[2,15,384]{2,1,0:T(8,128)(2,1)S(1)}, u32[]{:S(2)}, u32[]{:S(2)}) collective-permute-start(bf16[2,15,384]{2,1,0:T(8,128)(2,1)S(1)} %get-tuple-element.17), channel_id=1, source_target_pairs={{0,4},{4,8},{8,12},{1,5},{5,9},{9,13},{2,6},{6,10},{10,14},{3,7},{... | collective-permute-start | bytes 69128 | tf_op jit(solution)/shard_map/ppermute | solution.py:20
  62.3 1.3 %collective-permute-start.8 = (bf16[2,15,384]{2,1,0:T(8,128)(2,1)S(1)}, bf16[2,15,384]{2,1,0:T(8,128)(2,1)S(1)}, u32[]{:S(2)}, u32[]{:S(2)}) collective-permute-start(bf16[2,15,384]{2,1,0:T(8,128)(2,1)S(1)} %get-tuple-element.18), channel_id=1, source_target_pairs={{4,0},{8,4},{12,8},{5,1},{9,5},{13,9},{6,2},{10,6},{14,10},{7,3},{... | collective-permute-start | bytes 69128 | tf_op jit(solution)/shard_map/ppermute | solution.py:21
  63.6 0.2 collective-permute-done.7
  63.8 4.2 %collective-permute-done.8 = bf16[2,15,384]{2,1,0:T(8,128)(2,1)S(1)} collective-permute-done((bf16[2,15,384]{2,1,0:T(8,128)(2,1)S(1)}, bf16[2,15,384]{2,1,0:T(8,128)(2,1)S(1)}, u32[]{:S(2)}, u32[]{:S(2)}) %collective-permute-start.8) | collective-permute-done | bytes 23072 | tf_op jit(solution)/shard_map/ppermute | solution.py:21
  68.2 1.1 %fusion.58 = f32[2,128,384]{2,0,1:T(2,128)S(1)} fusion(bf16[2,158,384]{2,1,0:T(8,128)(2,1)S(1)} %pad_maximum_fusion.3, f32[31,1,384]{2,0,1:T(8,128)S(1)} %bitcast.132), kind=kOutput, calls=%fused_computation.75 | convolution fusion | flops 36569088 | bytes 683520 | tf_op jit(solution)/shard_map/conv_general_dilated | solution.py:169
  69.3 0.2 copy-done.7
  69.4 0.6 convolution_convert_fusion.1
  70.3 1.8 %collective-permute-done.9 = bf16[2,2,32,1536]{3,2,0,1:T(8,128)(2,1)} collective-permute-done((bf16[2,2,32,1536]{3,2,0,1:T(8,128)(2,1)S(1)}, bf16[2,2,32,1536]{3,2,0,1:T(8,128)(2,1)}, u32[]{:S(2)}, u32[]{:S(2)}) %collective-permute-start.9) | collective-permute-done | bytes 393248 | tf_op jit(solution)/shard_map/ppermute | solution.py:69
  72.1 1.1 %convert_add_fusion = f32[2,2,32,1536]{3,2,0,1:T(8,128)S(1)} fusion(bf16[2,2,32,1536]{3,2,0,1:T(8,128)(2,1)} %collective-permute-done.9, bf16[2,2,1,32,1536]{4,3,2,1,0:T(8,128)(2,1)S(1)} %get-tuple-element.7), kind=kLoop, calls=%fused_computation.34 | loop fusion | flops 589824 | bytes 1572864 | tf_op jit(solution)/shard_map/add | solution.py:70
  73.2 1.6 %collective-permute-start.10 = (bf16[2,32,1536]{2,1,0:T(8,128)(2,1)S(1)}, bf16[2,32,1536]{2,1,0:T(8,128)(2,1)S(1)}, u32[]{:S(2)}, u32[]{:S(2)}) collective-permute-start(bf16[2,32,1536]{2,1,0:T(8,128)(2,1)S(1)} %fusion.61), channel_id=1, source_target_pairs={{0,2},{1,3},{2,0},{3,1},{4,6},{5,7},{6,4},{7,5},{8,10},{9,11},{10,... | collective-permute-start | bytes 589832 | tf_op jit(solution)/shard_map/ppermute | solution.py:69
  74.8 5.4 %collective-permute-done.10 = bf16[2,32,1536]{2,1,0:T(8,128)(2,1)S(1)} collective-permute-done((bf16[2,32,1536]{2,1,0:T(8,128)(2,1)S(1)}, bf16[2,32,1536]{2,1,0:T(8,128)(2,1)S(1)}, u32[]{:S(2)}, u32[]{:S(2)}) %collective-permute-start.10) | collective-permute-done | bytes 196640 | tf_op jit(solution)/shard_map/ppermute | solution.py:69
  80.2 0.8 fusion.51
  (43 shorter events, 0.9 us)
Async XLA Ops:
  0.0 4.8 %copy-start = (bf16[3,1536,256]{2,1,0:T(8,128)(2,1)S(1)}, bf16[3,1536,256]{2,1,0:T(8,128)(2,1)}, u32[]{:S(2)}) copy-start(bf16[3,1536,256]{2,1,0:T(8,128)(2,1)} %param.15) | copy-start | bytes 7077892
  4.8 14.7 %copy-start.5 = (s32[2]{0:T(128)S(1)}, s32[2]{0:T(128)}, u32[]{:S(2)}) copy-start(s32[2]{0:T(128)} %param.13) | copy-start | bytes 28
  6.8 12.4 %collective-permute-start.1 = (bf16[2,2,128,256]{3,2,0,1:T(8,128)(2,1)S(1)}, bf16[2,2,128,256]{3,2,0,1:T(8,128)(2,1)}, u32[]{:S(2)}, u32[]{:S(2)}) collective-permute-start(bf16[2,2,128,256]{3,2,0,1:T(8,128)(2,1)S(1)} %get-tuple-element.16), channel_id=1, source_target_pairs={{0,4},{4,8},{8,12},{12,0},{1,5},{5,9},{9,13},{13,1},{2,6},{6,10},{... | collective-permute-start | bytes 786440 | tf_op jit(solution)/shard_map/ppermute | solution.py:97
  9.9 13.7 %collective-permute-start = (bf16[2,2,128,256]{3,2,0,1:T(8,128)(2,1)S(1)}, bf16[2,2,128,256]{3,2,0,1:T(8,128)(2,1)}, u32[]{:S(2)}, u32[]{:S(2)}) collective-permute-start(bf16[2,2,128,256]{3,2,0,1:T(8,128)(2,1)S(1)} %get-tuple-element.16), channel_id=1, source_target_pairs={{0,12},{4,0},{8,4},{12,8},{1,13},{5,1},{9,5},{13,9},{2,14},{6,2},{... | collective-permute-start | bytes 786440 | tf_op jit(solution)/shard_map/ppermute | solution.py:100
  19.2 10.4 %collective-permute-start.2 = (bf16[2,2,128,256]{3,2,0,1:T(8,128)(2,1)}, bf16[2,2,128,256]{3,2,0,1:T(8,128)(2,1)}, u32[]{:S(2)}, u32[]{:S(2)}) collective-permute-start(bf16[2,2,128,256]{3,2,0,1:T(8,128)(2,1)} %collective-permute-done.1), channel_id=1, source_target_pairs={{0,4},{4,8},{8,12},{12,0},{1,5},{5,9},{9,13},{13,1},{2,6},{6,10},{... | collective-permute-start | bytes 786440 | tf_op jit(solution)/shard_map/ppermute | solution.py:97
  34.1 1.2 %copy-start.2 = (bf16[4,1,2,128,256]{3,4,2,0,1:T(8,128)(2,1)S(1)}, bf16[4,1,2,128,256]{3,4,2,0,1:T(8,128)(2,1)}, u32[]{:S(2)}) copy-start(bf16[4,1,2,128,256]{3,4,2,0,1:T(8,128)(2,1)} %copy.44) | copy-start | bytes 1572868
  35.3 1.1 %copy-start.1 = (bf16[256,1536]{1,0:T(8,128)(2,1)S(1)}, bf16[256,1536]{1,0:T(8,128)(2,1)}, u32[]{:S(2)}) copy-start(bf16[256,1536]{1,0:T(8,128)(2,1)} %param.16) | copy-start | bytes 2359300
  37.0 13.1 %copy-start.3 = (f32[1536]{0:T(1024)S(1)}, f32[1536]{0:T(1024)}, u32[]{:S(2)}) copy-start(f32[1536]{0:T(1024)} %param.17) | copy-start | bytes 18436
  37.0 1.9 %collective-permute-start.3 = (bf16[2,2,32,1536]{3,2,0,1:T(8,128)(2,1)S(1)}, bf16[2,2,32,1536]{3,2,0,1:T(8,128)(2,1)}, u32[]{:S(2)}, u32[]{:S(2)}) collective-permute-start(bf16[2,2,32,1536]{3,2,0,1:T(8,128)(2,1)S(1)} %bitcast.121), channel_id=1, source_target_pairs={{0,1},{1,0},{2,3},{3,2},{4,5},{5,4},{6,7},{7,6},{8,9},{9,8},{10,11... | collective-permute-start | bytes 1179656 | tf_op jit(solution)/shard_map/ppermute | solution.py:69
  40.1 7.1 %collective-permute-start.4 = (bf16[2,32,1536]{2,1,0:T(8,128)(2,1)S(1)}, bf16[2,32,1536]{2,1,0:T(8,128)(2,1)}, u32[]{:S(2)}, u32[]{:S(2)}) collective-permute-start(bf16[2,32,1536]{2,1,0:T(8,128)(2,1)S(1)} %fusion.60), channel_id=1, source_target_pairs={{0,2},{1,3},{2,0},{3,1},{4,6},{5,7},{6,4},{7,5},{8,10},{9,11},{10,... | collective-permute-start | bytes 589832 | tf_op jit(solution)/shard_map/ppermute | solution.py:69
  50.2 6.2 %collective-permute-start.5 = (bf16[2,32,1536]{2,1,0:T(8,128)(2,1)S(1)}, bf16[2,32,1536]{2,1,0:T(8,128)(2,1)S(1)}, u32[]{:S(2)}, u32[]{:S(2)}) collective-permute-start(bf16[2,32,1536]{2,1,0:T(8,128)(2,1)S(1)} %multiply_convert_fusion.2), channel_id=1, source_target_pairs={{0,2},{1,3},{2,0},{3,1},{4,6},{5,7},{6,4},{7,5},{8,10},{9,11},{10,... | collective-permute-start | bytes 589832 | tf_op jit(solution)/shard_map/ppermute | solution.py:81
  56.6 1.9 %collective-permute-start.6 = (bf16[2,2,32,1536]{3,2,0,1:T(8,128)(2,1)S(1)}, bf16[2,2,32,1536]{3,2,0,1:T(8,128)(2,1)}, u32[]{:S(2)}, u32[]{:S(2)}) collective-permute-start(bf16[2,2,32,1536]{3,2,0,1:T(8,128)(2,1)S(1)} %pad_maximum_fusion.2), channel_id=1, source_target_pairs={{0,1},{1,0},{2,3},{3,2},{4,5},{5,4},{6,7},{7,6},{8,9},{9,8},{10,11... | collective-permute-start | bytes 1179656 | tf_op jit(solution)/shard_map/ppermute | solution.py:81
  56.8 2.9 %copy-start.6 = (bf16[2,1536,384]{2,1,0:T(8,128)(2,1)S(1)}, bf16[2,1536,384]{2,1,0:T(8,128)(2,1)}, u32[]{:S(2)}) copy-start(bf16[2,1536,384]{2,1,0:T(8,128)(2,1)} %param.18) | copy-start | bytes 7077892
  59.8 8.4 %copy-start.8 = (f32[31,384]{1,0:T(8,128)S(1)}, f32[31,384]{1,0:T(8,128)}, u32[]{:S(2)}) copy-start(f32[31,384]{1,0:T(8,128)} %param.19) | copy-start | bytes 142852
  60.7 3.1 %collective-permute-start.7 = (bf16[2,15,384]{2,1,0:T(8,128)(2,1)S(1)}, bf16[2,15,384]{2,1,0:T(8,128)(2,1)S(1)}, u32[]{:S(2)}, u32[]{:S(2)}) collective-permute-start(bf16[2,15,384]{2,1,0:T(8,128)(2,1)S(1)} %get-tuple-element.17), channel_id=1, source_target_pairs={{0,4},{4,8},{8,12},{1,5},{5,9},{9,13},{2,6},{6,10},{10,14},{3,7},{... | collective-permute-start | bytes 69128 | tf_op jit(solution)/shard_map/ppermute | solution.py:20
  62.3 5.7 %collective-permute-start.8 = (bf16[2,15,384]{2,1,0:T(8,128)(2,1)S(1)}, bf16[2,15,384]{2,1,0:T(8,128)(2,1)S(1)}, u32[]{:S(2)}, u32[]{:S(2)}) collective-permute-start(bf16[2,15,384]{2,1,0:T(8,128)(2,1)S(1)} %get-tuple-element.18), channel_id=1, source_target_pairs={{4,0},{8,4},{12,8},{5,1},{9,5},{13,9},{6,2},{10,6},{14,10},{7,3},{... | collective-permute-start | bytes 69128 | tf_op jit(solution)/shard_map/ppermute | solution.py:21
  68.1 1.3 %copy-start.7 = (bf16[384,1536]{1,0:T(8,128)(2,1)S(1)}, bf16[384,1536]{1,0:T(8,128)(2,1)}, u32[]{:S(2)}) copy-start(bf16[384,1536]{1,0:T(8,128)(2,1)} %param.22) | copy-start | bytes 3538948
  68.2 1.3 %copy-start.9 = (f32[384]{0:T(512)S(1)}, f32[384]{0:T(512)}, u32[]{:S(2)}) copy-start(f32[384]{0:T(512)} %param.21) | copy-start | bytes 4612
  68.2 1.3 %copy-start.10 = (f32[384]{0:T(512)S(1)}, f32[384]{0:T(512)}, u32[]{:S(2)}) copy-start(f32[384]{0:T(512)} %param.20) | copy-start | bytes 4612
  69.4 0.8 copy-start.4
  70.1 1.9 %collective-permute-start.9 = (bf16[2,2,32,1536]{3,2,0,1:T(8,128)(2,1)S(1)}, bf16[2,2,32,1536]{3,2,0,1:T(8,128)(2,1)}, u32[]{:S(2)}, u32[]{:S(2)}) collective-permute-start(bf16[2,2,32,1536]{3,2,0,1:T(8,128)(2,1)S(1)} %bitcast.122), channel_id=1, source_target_pairs={{0,1},{1,0},{2,3},{3,2},{4,5},{5,4},{6,7},{7,6},{8,9},{9,8},{10,11... | collective-permute-start | bytes 1179656 | tf_op jit(solution)/shard_map/ppermute | solution.py:69
  73.2 7.0 %collective-permute-start.10 = (bf16[2,32,1536]{2,1,0:T(8,128)(2,1)S(1)}, bf16[2,32,1536]{2,1,0:T(8,128)(2,1)S(1)}, u32[]{:S(2)}, u32[]{:S(2)}) collective-permute-start(bf16[2,32,1536]{2,1,0:T(8,128)(2,1)S(1)} %fusion.61), channel_id=1, source_target_pairs={{0,2},{1,3},{2,0},{3,1},{4,6},{5,7},{6,4},{7,5},{8,10},{9,11},{10,... | collective-permute-start | bytes 589832 | tf_op jit(solution)/shard_map/ppermute | solution.py:69

commit v7 on v1

--- a/solution.py
+++ b/solution.py
@@ -90,6 +90,50 @@
             going_left = lax.ppermute(going_left, axis, left)
             from_right.append(going_left)
     return jnp.stack([x] + from_right + from_left[::-1], axis=0)
+
+
+def attend(queries, key_rows, value_rows, positions, frame_counts):
+    scores = jnp.einsum(
+        "sqhe,skhe->shqk", queries, key_rows, preferred_element_type=jnp.float32
+    ) * HEAD_DIM ** (-0.5)
+    is_live = positions[None, :] < frame_counts[:, None]
+    scores = jnp.where(is_live[:, None, None, :], scores, masked_score)
+    row_max = jnp.max(scores, axis=-1, keepdims=True)
+    weights = jnp.exp(scores - row_max)
+    row_sum = jnp.sum(weights, axis=-1)
+    contrib = jnp.einsum(
+        "shqk,skhe->shqe",
+        weights.astype(jnp.bfloat16),
+        value_rows,
+        preferred_element_type=jnp.float32,
+    )
+    return (contrib / row_sum[..., None]).astype(jnp.bfloat16)
+
+
+def attend_by_heads(projected, frame_counts, axis):
+    _, records, frames, width = projected.shape
+    count, rank = lax.axis_size(axis), lax.axis_index(axis)
+    group = width // HEAD_DIM // count
+    split = projected.reshape(3, records, frames, count, group, HEAD_DIM)
+    pieces = [lax.dynamic_index_in_dim(split, rank, 3, keepdims=False)]
+    sources = [rank]
+    for shift in range(1, count):
+        target = (rank + shift) % count
+        send = lax.dynamic_index_in_dim(split, target, 3, keepdims=False)
+        pairs = [(i, (i + shift) % count) for i in range(count)]
+        pieces.append(lax.ppermute(send, axis, pairs))
+        sources.append((rank - shift) % count)
+    every = jnp.concatenate(pieces, axis=2)
+    frame_steps = jnp.arange(frames, dtype=jnp.int32)
+    positions = jnp.concatenate([source * frames + frame_steps for source in sources])
+    attended = attend(every[0], every[1], every[2], positions, frame_counts)
+    back = [attended[:, :, :frames]]
+    for shift in range(1, count):
+        rows = attended[:, :, shift * frames : (shift + 1) * frames]
+        pairs = [(i, (i - shift) % count) for i in range(count)]
+        back.append(lax.ppermute(rows, axis, pairs))
+    ordered = jnp.roll(jnp.stack(back, axis=1), rank, axis=1)
+    return ordered.transpose(0, 3, 1, 2, 4).reshape(records, frames, width)
 
 
 def shards(
@@ -116,30 +160,19 @@
     projected = jnp.einsum(
         "std,idc->istc", normed, w_qkv, preferred_element_type=jnp.float32
     ).astype(jnp.bfloat16)
-    queries = projected[0]
-    query_heads = queries.reshape(records, frames_here, head_count, HEAD_DIM)
-    kv_all = ring_gather(projected[1:], "ctx")
-    key_heads = kv_all[:, 0].reshape(ctx_count, records, frames_here, head_count, HEAD_DIM)
-    value_heads = kv_all[:, 1].reshape(ctx_count, records, frames_here, head_count, HEAD_DIM)
-    scores = (
-        jnp.einsum("sqhe,cskhe->shqck", query_heads, key_heads, preferred_element_type=jnp.float32)
-        * score_scale
-    )
-    block_rank = (ctx_rank + jnp.arange(ctx_count, dtype=jnp.int32)) % ctx_count
-    positions = block_rank[:, None] * frames_here + jnp.arange(frames_here, dtype=jnp.int32)
-    is_live = positions[None] < frame_counts[:, None, None]
-    scores = jnp.where(is_live[:, None, None], scores, masked_score)
-    row_max = jnp.max(scores, axis=(-2, -1), keepdims=True)
-    weights = jnp.exp(scores - row_max)
-    row_sum = jnp.sum(weights, axis=(-2, -1))
-    contrib = jnp.einsum(
-        "shqck,cskhe->shqe",
-        weights.astype(jnp.bfloat16),
-        value_heads,
-        preferred_element_type=jnp.float32,
-    )
-    attended = (contrib / row_sum[..., None]).astype(jnp.bfloat16)
-    attended = attended.transpose(0, 2, 1, 3).reshape(records, frames_here, head_count * HEAD_DIM)
+    if head_count % ctx_count == 0:
+        attended = attend_by_heads(projected, frame_counts, "ctx")
+    else:
+        query_heads = projected[0].reshape(records, frames_here, head_count, HEAD_DIM)
+        kv_all = ring_gather(projected[1:], "ctx")
+        key_heads = kv_all[:, 0].reshape(ctx_count, records, frames_here, head_count, HEAD_DIM)
+        value_heads = kv_all[:, 1].reshape(ctx_count, records, frames_here, head_count, HEAD_DIM)
+        block_rank = (ctx_rank + jnp.arange(ctx_count, dtype=jnp.int32)) % ctx_count
+        positions = block_rank[:, None] * frames_here + jnp.arange(frames_here, dtype=jnp.int32)
+        key_heads = key_heads.transpose(1, 0, 2, 3, 4).reshape(records, -1, head_count, HEAD_DIM)
+        value_heads = value_heads.transpose(1, 0, 2, 3, 4).reshape(records, -1, head_count, HEAD_DIM)
+        attended = attend(query_heads, key_heads, value_heads, positions.reshape(-1), frame_counts)
+        attended = attended.transpose(0, 2, 1, 3).reshape(records, frames_here, head_count * HEAD_DIM)
     attn_part = jnp.einsum("stc,cd->std", attended, w_out, preferred_element_type=jnp.float32)
     mp_count = lax.axis_size("mp")
     mp_rank = lax.axis_index("mp")

time: 79.3 us -> 74.3 us (0.937)
  waiting for transfers between devices: 39.9 us -> 33 us
  starting transfers between devices: 13 us -> 18.8 us
  local copies, waits for them, and re-layouts: 6.9 us -> 4.29 us
  other arithmetic: 11.2 us -> 9.93 us
    ppermute x3 -> x6, waiting for transfers between devices: 17.3 us -> 10.6 us  [the longest x3 5.45 us: attend_by_heads(): back.append(lax.ppermute(rows, axis, pairs))]
    ppermute x3 -> x6, starting transfers between devices: 5.17 us -> 11.3 us  [the longest x3 7.01 us: attend_by_heads(): pieces.append(lax.ppermute(send, axis, pairs))]
    slice x5 -> x1, local copies, waits for them, and re-layouts: 3.32 us -> 0.02 us  [attend_by_heads(): rows = attended[:, :, shift * frames:(shift + 1) * frames]]
    another operation x1 -> x0, other arithmetic: 1.24 us -> none  [ring_gather(): return jnp.stack([x] + from_right + from_left[::-1], axis=0)]
  transfers between devices with their start and end apart: 11 -> 14, of which waited for: 10 -> 12; matrix products, arithmetic and copies ran while one was open for 4% -> 4% of each run, Pallas kernels for 0% -> 0%
where the time goes in v7:
time: 74.3 us; the launch traced here: 73.8 us
  waiting for transfers between devices  33 us (44%)
  starting transfers between devices  18.8 us (25%)
  other arithmetic  9.93 us (13%)
  matrix products  7.31 us (10%)
  local copies, waits for them, and re-layouts  4.29 us (6%)
    ppermute x4, waiting for transfers between devices, reduce_scatter_rows(): lax.ppermute(send.astype(jnp.bfloat16), axis, xor_pairs(count, 1 << b))  14 us
    ppermute x3, starting transfers between devices, attend_by_heads(): pieces.append(lax.ppermute(send, axis, pairs))  7.01 us
    ppermute x3, waiting for transfers between devices, attend_by_heads(): back.append(lax.ppermute(rows, axis, pairs))  5.45 us
    ppermute x3, waiting for transfers between devices, attend_by_heads(): pieces.append(lax.ppermute(send, axis, pairs))  5.16 us
    ppermute x2, waiting for transfers between devices, all_gather_rows(): got = lax.ppermute(acc, axis, xor_pairs(count, 1 << b))  5.09 us
    ppermute x3, starting transfers between devices, attend_by_heads(): back.append(lax.ppermute(rows, axis, pairs))  4.3 us
    ppermute x1, waiting for transfers between devices, with_halo(): after = lax.ppermute(initial, axis, down)  3.37 us
    ppermute x4, starting transfers between devices, reduce_scatter_rows(): lax.ppermute(send.astype(jnp.bfloat16), axis, xor_pairs(count, 1 << b))  3.27 us
  transfers between devices with their start and end apart: 14, of which 12 were waited for; matrix products, arithmetic and copies ran while one was open for 4% of the time, Pallas kernels for 0%

profile of v7, /device:TPU:0, one launch (start us, length us, event | category | flops | bytes accessed | tf_op | source)
XLA Modules:
  0.0 73.8 jit_solution(1678193035370607742)
XLA Ops:
  0.0 1.5 %convert_reduce_fusion = f32[2,128]{1,0:T(2,128)S(1)} fusion(bf16[2,128,1536]{2,1,0:T(8,128)(2,1)} %param.12), kind=kLoop, calls=%fused_computation.9 | loop fusion | flops 786176 | bytes 787456 | tf_op jit(solution)/shard_map/reduce_sum | solution.py:27
  1.5 1.5 %fusion.9 = f32[2,128]{1,0:T(2,128)S(1)} fusion(bf16[2,128,1536]{2,1,0:T(8,128)(2,1)} %param.12, f32[2,128]{1,0:T(2,128)S(1)} %broadcast_multiply_fusion.1), kind=kLoop, calls=%fused_computation.15 | loop fusion | flops 1572608 | bytes 788480 | tf_op jit(solution)/shard_map/reduce_sum | solution.py:29
  3.0 2.0 %fusion.18 = bf16[3,2,128,256]{3,2,0,1:T(8,128)(2,1)S(1)} fusion(bf16[3,1536,256]{2,1,0:T(8,128)(2,1)S(1)} %copy-done, bf16[2,128,1536]{2,1,0:T(8,128)(2,1)} %param.12, f32[1536]{0:T(1024)} %param.14, f32[2,128]{1,0:T(2,128)S(1)} %add_rsqrt_fusion.1, f32[2,128]{1,0:T(2,128)S(1)} %broadcast_multiply_fusion.1), kind=kOutput, calls=%fused_computation.20 | convolution fusion | flops 606142464 | bytes 3547136 | tf_op jit(solution)/shard_map/std,idc->istc/dot_general | solution.py:160
  5.0 0.2 copy.23
  5.3 3.1 %collective-permute-start = (bf16[3,2,128,1,64]{2,4,1,3,0:T(8,128)(2,1)S(1)}, bf16[3,2,128,1,64]{2,4,1,3,0:T(8,128)(2,1)S(1)}, u32[]{:S(2)}, u32[]{:S(2)}) collective-permute-start(bf16[3,2,128,1,64]{2,4,1,3,0:T(8,128)(2,1)S(1)} %get-tuple-element.49), channel_id=1, source_target_pairs={{0,4},{4,8},{8,12},{12,0},{1,5},{5,9},{9,13},{13,1},{2,6},{6,10},{... | collective-permute-start | bytes 294920 | tf_op jit(solution)/shard_map/ppermute | solution.py:124
  8.4 2.6 %collective-permute-start.1 = (bf16[3,2,128,1,64]{2,4,1,3,0:T(8,128)(2,1)S(1)}, bf16[3,2,128,1,64]{2,4,1,3,0:T(8,128)(2,1)S(1)}, u32[]{:S(2)}, u32[]{:S(2)}) collective-permute-start(bf16[3,2,128,1,64]{2,4,1,3,0:T(8,128)(2,1)S(1)} %get-tuple-element.48), channel_id=1, source_target_pairs={{0,8},{4,12},{8,0},{12,4},{1,9},{5,13},{9,1},{13,5},{2,10},{6,14},... | collective-permute-start | bytes 294920 | tf_op jit(solution)/shard_map/ppermute | solution.py:124
  10.9 1.3 %collective-permute-start.2 = (bf16[3,2,128,1,64]{2,4,1,3,0:T(8,128)(2,1)S(1)}, bf16[3,2,128,1,64]{2,4,1,3,0:T(8,128)(2,1)S(1)}, u32[]{:S(2)}, u32[]{:S(2)}) collective-permute-start(bf16[3,2,128,1,64]{2,4,1,3,0:T(8,128)(2,1)S(1)} %get-tuple-element.47), channel_id=1, source_target_pairs={{0,12},{4,0},{8,4},{12,8},{1,13},{5,1},{9,5},{13,9},{2,14},{6,2},{... | collective-permute-start | bytes 294920 | tf_op jit(solution)/shard_map/ppermute | solution.py:124
  12.3 0.1 broadcast_compare_fusion
  12.4 1.6 %collective-permute-done = bf16[3,2,128,1,64]{2,4,1,3,0:T(8,128)(2,1)S(1)} collective-permute-done((bf16[3,2,128,1,64]{2,4,1,3,0:T(8,128)(2,1)S(1)}, bf16[3,2,128,1,64]{2,4,1,3,0:T(8,128)(2,1)S(1)}, u32[]{:S(2)}, u32[]{:S(2)}) %collective-permute-start) | collective-permute-done | bytes 98336 | tf_op jit(solution)/shard_map/ppermute | solution.py:124
  14.0 3.5 %collective-permute-done.1 = bf16[3,2,128,1,64]{2,4,1,3,0:T(8,128)(2,1)S(1)} collective-permute-done((bf16[3,2,128,1,64]{2,4,1,3,0:T(8,128)(2,1)S(1)}, bf16[3,2,128,1,64]{2,4,1,3,0:T(8,128)(2,1)S(1)}, u32[]{:S(2)}, u32[]{:S(2)}) %collective-permute-start.1) | collective-permute-done | bytes 98336 | tf_op jit(solution)/shard_map/ppermute | solution.py:124
  17.6 0.8 %fusion.6 = (f32[2,512]{1,0:T(2,128)S(1)}, f32[2,512,512]{1,2,0:T(8,128)S(1)}) fusion(pred[2,512]{1,0:T(4,128)(4,1)S(1)} %broadcast_compare_fusion, bf16[3,2,512,1,64]{2,4,1,3,0:T(8,128)(2,1)S(1)} %pad_maximum_fusion.1), kind=kOutput, calls=%fused_computation.12 | convolution fusion | flops 68680704 | bytes 2365440 | tf_op jit(solution)/shard_map/sqhe,skhe->shqk/dot_general | solution.py:96
  18.4 0.5 fusion.7
  18.9 0.6 fusion.23
  19.6 3.6 %collective-permute-start.3 = (bf16[2,1,128,64]{2,3,0,1:T(8,128)(2,1)S(1)}, bf16[2,1,128,64]{2,3,0,1:T(8,128)(2,1)S(1)}, u32[]{:S(2)}, u32[]{:S(2)}) collective-permute-start(bf16[2,1,128,64]{2,3,0,1:T(8,128)(2,1)S(1)} %get-tuple-element.54), channel_id=1, source_target_pairs={{0,12},{4,0},{8,4},{12,8},{1,13},{5,1},{9,5},{13,9},{2,14},{6,2},{... | collective-permute-start | bytes 98312 | tf_op jit(solution)/shard_map/ppermute | solution.py:134
  23.3 0.4 collective-permute-start.4
  23.7 0.2 collective-permute-start.5
  23.9 0.9 %collective-permute-done.3 = bf16[2,1,128,64]{2,3,0,1:T(8,128)(2,1)S(1)} collective-permute-done((bf16[2,1,128,64]{2,3,0,1:T(8,128)(2,1)S(1)}, bf16[2,1,128,64]{2,3,0,1:T(8,128)(2,1)S(1)}, u32[]{:S(2)}, u32[]{:S(2)}) %collective-permute-start.3) | collective-permute-done | bytes 32800 | tf_op jit(solution)/shard_map/ppermute | solution.py:134
  24.9 3.4 %collective-permute-done.4 = bf16[2,1,128,64]{2,3,0,1:T(8,128)(2,1)S(1)} collective-permute-done((bf16[2,1,128,64]{2,3,0,1:T(8,128)(2,1)S(1)}, bf16[2,1,128,64]{2,3,0,1:T(8,128)(2,1)S(1)}, u32[]{:S(2)}, u32[]{:S(2)}) %collective-permute-start.4) | collective-permute-done | bytes 32800 | tf_op jit(solution)/shard_map/ppermute | solution.py:134
  28.2 1.2 %collective-permute-done.5 = bf16[2,1,128,64]{2,3,0,1:T(8,128)(2,1)S(1)} collective-permute-done((bf16[2,1,128,64]{2,3,0,1:T(8,128)(2,1)S(1)}, bf16[2,1,128,64]{2,3,0,1:T(8,128)(2,1)S(1)}, u32[]{:S(2)}, u32[]{:S(2)}) %collective-permute-start.5) | collective-permute-done | bytes 32800 | tf_op jit(solution)/shard_map/ppermute | solution.py:134
  29.5 0.4 convolution_convert_fusion
  30.1 1.7 %collective-permute-done.6 = bf16[2,2,32,1536]{3,2,0,1:T(8,128)(2,1)S(1)} collective-permute-done((bf16[2,2,32,1536]{3,2,0,1:T(8,128)(2,1)S(1)}, bf16[2,2,32,1536]{3,2,0,1:T(8,128)(2,1)S(1)}, u32[]{:S(2)}, u32[]{:S(2)}) %collective-permute-start.6) | collective-permute-done | bytes 393248 | tf_op jit(solution)/shard_map/ppermute | solution.py:59
  31.8 0.7 copy-done.2
  32.5 1.1 %convert_add_fusion.1 = f32[2,2,32,1536]{3,2,0,1:T(8,128)S(1)} fusion(bf16[2,2,32,1536]{3,2,0,1:T(8,128)(2,1)} %copy-done.2, bf16[2,2,1,32,1536]{4,3,2,1,0:T(8,128)(2,1)S(1)} %get-tuple-element.42), kind=kLoop, calls=%fused_computation.59 | loop fusion | flops 589824 | bytes 1572864 | tf_op jit(solution)/shard_map/add | solution.py:60
  33.7 1.6 %collective-permute-start.7 = (bf16[2,32,1536]{2,1,0:T(8,128)(2,1)S(1)}, bf16[2,32,1536]{2,1,0:T(8,128)(2,1)}, u32[]{:S(2)}, u32[]{:S(2)}) collective-permute-start(bf16[2,32,1536]{2,1,0:T(8,128)(2,1)S(1)} %fusion.45), channel_id=1, source_target_pairs={{0,2},{1,3},{2,0},{3,1},{4,6},{5,7},{6,4},{7,5},{8,10},{9,11},{10,... | collective-permute-start | bytes 589832 | tf_op jit(solution)/shard_map/ppermute | solution.py:59
  35.2 5.6 %collective-permute-done.7 = bf16[2,32,1536]{2,1,0:T(8,128)(2,1)} collective-permute-done((bf16[2,32,1536]{2,1,0:T(8,128)(2,1)S(1)}, bf16[2,32,1536]{2,1,0:T(8,128)(2,1)}, u32[]{:S(2)}, u32[]{:S(2)}) %collective-permute-start.7) | collective-permute-done | bytes 196640 | tf_op jit(solution)/shard_map/ppermute | solution.py:59
  40.8 1.2 %fusion.83 = (f32[2,32]{1,0:T(2,128)S(1)}, f32[2,32,1536]{2,1,0:T(8,128)S(1)}) fusion(bf16[2,32,1536]{2,1,0:T(8,128)(2,1)} %collective-permute-done.7, f32[2,2,32,1536]{3,2,0,1:T(8,128)S(1)} %convert_add_fusion.1, s32[]{:T(128)S(6)} %select_n.126, bf16[2,128,1536]{2,1,0:T(8,128)(2,1)} %param.12, s32[]{:T(128)S(6)} %select_n.110), kind=kLoop, calls=%fused_computation.218 | loop fusion | flops 491456 | bytes 1179912 | tf_op jit(solution)/shard_map/reduce_sum | solution.py:27
  42.0 0.2 multiply_reduce_fusion
  42.2 0.1 multiply_convert_fusion.1
  42.3 1.6 %collective-permute-start.8 = (bf16[2,32,1536]{2,1,0:T(8,128)(2,1)S(1)}, bf16[2,32,1536]{2,1,0:T(8,128)(2,1)S(1)}, u32[]{:S(2)}, u32[]{:S(2)}) collective-permute-start(bf16[2,32,1536]{2,1,0:T(8,128)(2,1)S(1)} %multiply_convert_fusion.1), channel_id=1, source_target_pairs={{0,2},{1,3},{2,0},{3,1},{4,6},{5,7},{6,4},{7,5},{8,10},{9,11},{10,... | collective-permute-start | bytes 589832 | tf_op jit(solution)/shard_map/ppermute | solution.py:71
  43.9 4.6 %collective-permute-done.8 = bf16[2,32,1536]{2,1,0:T(8,128)(2,1)S(1)} collective-permute-done((bf16[2,32,1536]{2,1,0:T(8,128)(2,1)S(1)}, bf16[2,32,1536]{2,1,0:T(8,128)(2,1)S(1)}, u32[]{:S(2)}, u32[]{:S(2)}) %collective-permute-start.8) | collective-permute-done | bytes 196640 | tf_op jit(solution)/shard_map/ppermute | solution.py:71
  48.5 0.2 select_bitcast_fusion.3
  48.8 1.3 %slice_reduce_fusion.30 = (f32[384]{0:T(512)S(1)}, f32[384]{0:T(512)S(1)}, f32[384]{0:T(512)S(1)}, f32[384]{0:T(512)S(1)}, f32[384]{0:T(512)S(1)}, /*index=5*/f3...) fusion(f32[31,384]{1,0:T(8,128)} %param.19), kind=kLoop, calls=%fused_computation.201 | loop fusion | bytes 58368 | tf_op jit(solution)/shard_map/slice | solution.py:197
  50.2 0.5 collective-permute-done.9
  50.6 1.3 %select_bitcast_fusion.1 = (bf16[2,2,1,32,1536]{4,3,0,1,2:T(8,128)(2,1)S(1)}, bf16[2,2,1,32,1536]{4,3,0,1,2:T(8,128)(2,1)S(1)}) fusion(bf16[2,2,32,1536]{3,2,0,1:T(8,128)(2,1)} %collective-permute-done.9, pred[]{:T(512)S(6)} %eq.16, bf16[2,1,32,1536]{3,2,0,1:T(8,128)(2,1)S(1)} %get-tuple-element.45, bf16[2,1,32,1536]{3,2,0,1:T(8,128)(2,1)S(1)} %get-tuple-element.44), kind=kLoop, calls=%fused_computation.86 | loop fusion | flops 589824 | bytes 1572865 | tf_op jit(solution)/shard_map/stack | solution.py:74
  51.9 0.1 pad_maximum_fusion
  52.1 0.8 %fusion.12 = f32[2,2,128,384]{3,2,0,1:T(8,128)S(1)} fusion(bf16[2,128,1536,1]{2,1,3,0:T(8,128)(2,1)S(1)} %bitcast.127, bf16[2,1536,384]{2,1,0:T(8,128)(2,1)S(1)} %copy-done.6), kind=kOutput, calls=%fused_computation.18 | convolution fusion | flops 603979776 | bytes 3932160 | tf_op jit(solution)/shard_map/std,gdc->gstc/dot_general | solution.py:34
  52.9 0.1 bitcast_select_fusion
  53.1 1.3 %collective-permute-start.10 = (bf16[2,15,384]{2,1,0:T(8,128)(2,1)S(1)}, bf16[2,15,384]{2,1,0:T(8,128)(2,1)S(1)}, u32[]{:S(2)}, u32[]{:S(2)}) collective-permute-start(bf16[2,15,384]{2,1,0:T(8,128)(2,1)S(1)} %get-tuple-element.50), channel_id=1, source_target_pairs={{0,4},{4,8},{8,12},{1,5},{5,9},{9,13},{2,6},{6,10},{10,14},{3,7},{... | collective-permute-start | bytes 69128 | tf_op jit(solution)/shard_map/ppermute | solution.py:20
  54.4 1.3 %collective-permute-start.11 = (bf16[2,15,384]{2,1,0:T(8,128)(2,1)S(1)}, bf16[2,15,384]{2,1,0:T(8,128)(2,1)S(1)}, u32[]{:S(2)}, u32[]{:S(2)}) collective-permute-start(bf16[2,15,384]{2,1,0:T(8,128)(2,1)S(1)} %get-tuple-element.51), channel_id=1, source_target_pairs={{4,0},{8,4},{12,8},{5,1},{9,5},{13,9},{6,2},{10,6},{14,10},{7,3},{... | collective-permute-start | bytes 69128 | tf_op jit(solution)/shard_map/ppermute | solution.py:21
  55.7 1.0 %slice_reduce_fusion.29 = (f32[384]{0:T(512)S(1)}, f32[384]{0:T(512)S(1)}, f32[384]{0:T(512)S(1)}, f32[384]{0:T(512)S(1)}, f32[384]{0:T(512)S(1)}, /*index=5*/f3...) fusion(f32[31,384]{1,0:T(8,128)} %param.19), kind=kLoop, calls=%fused_computation.200 | loop fusion | bytes 36864 | tf_op jit(solution)/shard_map/slice | solution.py:197
  56.7 3.4 %collective-permute-done.11 = bf16[2,15,384]{2,1,0:T(8,128)(2,1)S(1)} collective-permute-done((bf16[2,15,384]{2,1,0:T(8,128)(2,1)S(1)}, bf16[2,15,384]{2,1,0:T(8,128)(2,1)S(1)}, u32[]{:S(2)}, u32[]{:S(2)}) %collective-permute-start.11) | collective-permute-done | bytes 23072 | tf_op jit(solution)/shard_map/ppermute | solution.py:21
  60.1 2.7 %convolution_convert_fusion.1 = bf16[2,128,1536]{2,1,0:T(8,128)(2,1)S(1)} fusion(bf16[384,1536]{1,0:T(8,128)(2,1)S(1)} %copy-done.7, bf16[2,128,384]{2,1,0:T(8,128)(2,1)S(1)} %bitcast_select_fusion, bf16[2,15,384]{2,1,0:T(8,128)(2,1)S(1)} %collective-permute-done.11, bf16[2,15,384]{2,1,0:T(8,128)(2,1)S(1)} %collective-permute-done.10, f32[384]{0:T(512)S(1)} %copy-done.8, ...), kind=kOutput, calls=%fused_computation.1 | convolution fusion | flops 320962560 | bytes 2259456 | tf_op jit(solution)/shard_map/stc,cd->std/dot_general | solution.py:200
  63.1 0.5 copy-done.4
  63.5 1.3 %collective-permute-done.12 = bf16[2,2,32,1536]{3,2,0,1:T(8,128)(2,1)} collective-permute-done((bf16[2,2,32,1536]{3,2,0,1:T(8,128)(2,1)S(1)}, bf16[2,2,32,1536]{3,2,0,1:T(8,128)(2,1)}, u32[]{:S(2)}, u32[]{:S(2)}) %collective-permute-start.12) | collective-permute-done | bytes 393248 | tf_op jit(solution)/shard_map/ppermute | solution.py:59
  64.9 1.1 %convert_add_fusion = f32[2,2,32,1536]{3,2,0,1:T(8,128)S(1)} fusion(bf16[2,2,32,1536]{3,2,0,1:T(8,128)(2,1)} %collective-permute-done.12, bf16[2,2,1,32,1536]{4,3,2,1,0:T(8,128)(2,1)S(1)} %get-tuple-element.38), kind=kLoop, calls=%fused_computation.58 | loop fusion | flops 589824 | bytes 1572864 | tf_op jit(solution)/shard_map/add | solution.py:60
  66.0 1.6 %collective-permute-start.13 = (bf16[2,32,1536]{2,1,0:T(8,128)(2,1)S(1)}, bf16[2,32,1536]{2,1,0:T(8,128)(2,1)S(1)}, u32[]{:S(2)}, u32[]{:S(2)}) collective-permute-start(bf16[2,32,1536]{2,1,0:T(8,128)(2,1)S(1)} %fusion.46), channel_id=1, source_target_pairs={{0,2},{1,3},{2,0},{3,1},{4,6},{5,7},{6,4},{7,5},{8,10},{9,11},{10,... | collective-permute-start | bytes 589832 | tf_op jit(solution)/shard_map/ppermute | solution.py:59
  67.7 5.4 %collective-permute-done.13 = bf16[2,32,1536]{2,1,0:T(8,128)(2,1)S(1)} collective-permute-done((bf16[2,32,1536]{2,1,0:T(8,128)(2,1)S(1)}, bf16[2,32,1536]{2,1,0:T(8,128)(2,1)S(1)}, u32[]{:S(2)}, u32[]{:S(2)}) %collective-permute-start.13) | collective-permute-done | bytes 196640 | tf_op jit(solution)/shard_map/ppermute | solution.py:59
  73.0 0.8 %fusion.42 = bf16[2,32,1536]{2,1,0:T(8,128)(2,1)} fusion(f32[2,32,1536]{2,1,0:T(8,128)S(1)} %get-tuple-element.37, bf16[2,32,1536]{2,1,0:T(8,128)(2,1)S(1)} %collective-permute-done.13, f32[2,2,32,1536]{3,2,0,1:T(8,128)S(1)} %convert_add_fusion, s32[]{:T(128)S(6)} %select_n.126, bf16[1536]{0:T(1024)(128)(2,1)S(1)} %get-tuple-element.56, ...), kind=kLoop, calls=%fused_computation.78 | loop fusion | flops 884736 | bytes 1185860 | tf_op jit(solution)/shard_map/convert_element_type | solution.py:207
  (57 shorter events, 1.1 us)
Async XLA Ops:
  0.0 3.0 %copy-start = (bf16[3,1536,256]{2,1,0:T(8,128)(2,1)S(1)}, bf16[3,1536,256]{2,1,0:T(8,128)(2,1)}, u32[]{:S(2)}) copy-start(bf16[3,1536,256]{2,1,0:T(8,128)(2,1)} %param.15) | copy-start | bytes 7077892
  3.0 9.3 %copy-start.5 = (s32[2]{0:T(128)S(1)}, s32[2]{0:T(128)}, u32[]{:S(2)}) copy-start(s32[2]{0:T(128)} %param.13) | copy-start | bytes 28
  5.3 8.8 %collective-permute-start = (bf16[3,2,128,1,64]{2,4,1,3,0:T(8,128)(2,1)S(1)}, bf16[3,2,128,1,64]{2,4,1,3,0:T(8,128)(2,1)S(1)}, u32[]{:S(2)}, u32[]{:S(2)}) collective-permute-start(bf16[3,2,128,1,64]{2,4,1,3,0:T(8,128)(2,1)S(1)} %get-tuple-element.49), channel_id=1, source_target_pairs={{0,4},{4,8},{8,12},{12,0},{1,5},{5,9},{9,13},{13,1},{2,6},{6,10},{... | collective-permute-start | bytes 294920 | tf_op jit(solution)/shard_map/ppermute | solution.py:124
  8.4 9.2 %collective-permute-start.1 = (bf16[3,2,128,1,64]{2,4,1,3,0:T(8,128)(2,1)S(1)}, bf16[3,2,128,1,64]{2,4,1,3,0:T(8,128)(2,1)S(1)}, u32[]{:S(2)}, u32[]{:S(2)}) collective-permute-start(bf16[3,2,128,1,64]{2,4,1,3,0:T(8,128)(2,1)S(1)} %get-tuple-element.48), channel_id=1, source_target_pairs={{0,8},{4,12},{8,0},{12,4},{1,9},{5,13},{9,1},{13,5},{2,10},{6,14},... | collective-permute-start | bytes 294920 | tf_op jit(solution)/shard_map/ppermute | solution.py:124
  10.9 6.6 %collective-permute-start.2 = (bf16[3,2,128,1,64]{2,4,1,3,0:T(8,128)(2,1)S(1)}, bf16[3,2,128,1,64]{2,4,1,3,0:T(8,128)(2,1)S(1)}, u32[]{:S(2)}, u32[]{:S(2)}) collective-permute-start(bf16[3,2,128,1,64]{2,4,1,3,0:T(8,128)(2,1)S(1)} %get-tuple-element.47), channel_id=1, source_target_pairs={{0,12},{4,0},{8,4},{12,8},{1,13},{5,1},{9,5},{13,9},{2,14},{6,2},{... | collective-permute-start | bytes 294920 | tf_op jit(solution)/shard_map/ppermute | solution.py:124
  18.9 10.6 %copy-start.1 = (bf16[256,1536]{1,0:T(8,128)(2,1)S(1)}, bf16[256,1536]{1,0:T(8,128)(2,1)}, u32[]{:S(2)}) copy-start(bf16[256,1536]{1,0:T(8,128)(2,1)} %param.16) | copy-start | bytes 2359300
  19.6 5.2 %collective-permute-start.3 = (bf16[2,1,128,64]{2,3,0,1:T(8,128)(2,1)S(1)}, bf16[2,1,128,64]{2,3,0,1:T(8,128)(2,1)S(1)}, u32[]{:S(2)}, u32[]{:S(2)}) collective-permute-start(bf16[2,1,128,64]{2,3,0,1:T(8,128)(2,1)S(1)} %get-tuple-element.54), channel_id=1, source_target_pairs={{0,12},{4,0},{8,4},{12,8},{1,13},{5,1},{9,5},{13,9},{2,14},{6,2},{... | collective-permute-start | bytes 98312 | tf_op jit(solution)/shard_map/ppermute | solution.py:134
  23.3 5.0 %collective-permute-start.4 = (bf16[2,1,128,64]{2,3,0,1:T(8,128)(2,1)S(1)}, bf16[2,1,128,64]{2,3,0,1:T(8,128)(2,1)S(1)}, u32[]{:S(2)}, u32[]{:S(2)}) collective-permute-start(bf16[2,1,128,64]{2,3,0,1:T(8,128)(2,1)S(1)} %get-tuple-element.53), channel_id=1, source_target_pairs={{0,8},{4,12},{8,0},{12,4},{1,9},{5,13},{9,1},{13,5},{2,10},{6,14},... | collective-permute-start | bytes 98312 | tf_op jit(solution)/shard_map/ppermute | solution.py:134
  23.7 5.7 %collective-permute-start.5 = (bf16[2,1,128,64]{2,3,0,1:T(8,128)(2,1)S(1)}, bf16[2,1,128,64]{2,3,0,1:T(8,128)(2,1)S(1)}, u32[]{:S(2)}, u32[]{:S(2)}) collective-permute-start(bf16[2,1,128,64]{2,3,0,1:T(8,128)(2,1)S(1)} %get-tuple-element.52), channel_id=1, source_target_pairs={{0,4},{4,8},{8,12},{12,0},{1,5},{5,9},{9,13},{13,1},{2,6},{6,10},{... | collective-permute-start | bytes 98312 | tf_op jit(solution)/shard_map/ppermute | solution.py:134
  30.0 12.2 %copy-start.3 = (f32[1536]{0:T(1024)S(1)}, f32[1536]{0:T(1024)}, u32[]{:S(2)}) copy-start(f32[1536]{0:T(1024)} %param.17) | copy-start | bytes 18436
  30.0 1.8 %collective-permute-start.6 = (bf16[2,2,32,1536]{3,2,0,1:T(8,128)(2,1)S(1)}, bf16[2,2,32,1536]{3,2,0,1:T(8,128)(2,1)S(1)}, u32[]{:S(2)}, u32[]{:S(2)}) collective-permute-start(bf16[2,2,32,1536]{3,2,0,1:T(8,128)(2,1)S(1)} %bitcast.130), channel_id=1, source_target_pairs={{0,1},{1,0},{2,3},{3,2},{4,5},{5,4},{6,7},{7,6},{8,9},{9,8},{10,11... | collective-permute-start | bytes 1179656 | tf_op jit(solution)/shard_map/ppermute | solution.py:59
  31.8 0.7 copy-start.2
  33.7 7.1 %collective-permute-start.7 = (bf16[2,32,1536]{2,1,0:T(8,128)(2,1)S(1)}, bf16[2,32,1536]{2,1,0:T(8,128)(2,1)}, u32[]{:S(2)}, u32[]{:S(2)}) collective-permute-start(bf16[2,32,1536]{2,1,0:T(8,128)(2,1)S(1)} %fusion.45), channel_id=1, source_target_pairs={{0,2},{1,3},{2,0},{3,1},{4,6},{5,7},{6,4},{7,5},{8,10},{9,11},{10,... | collective-permute-start | bytes 589832 | tf_op jit(solution)/shard_map/ppermute | solution.py:59
  42.3 6.2 %collective-permute-start.8 = (bf16[2,32,1536]{2,1,0:T(8,128)(2,1)S(1)}, bf16[2,32,1536]{2,1,0:T(8,128)(2,1)S(1)}, u32[]{:S(2)}, u32[]{:S(2)}) collective-permute-start(bf16[2,32,1536]{2,1,0:T(8,128)(2,1)S(1)} %multiply_convert_fusion.1), channel_id=1, source_target_pairs={{0,2},{1,3},{2,0},{3,1},{4,6},{5,7},{6,4},{7,5},{8,10},{9,11},{10,... | collective-permute-start | bytes 589832 | tf_op jit(solution)/shard_map/ppermute | solution.py:71
  48.7 1.9 %collective-permute-start.9 = (bf16[2,2,32,1536]{3,2,0,1:T(8,128)(2,1)S(1)}, bf16[2,2,32,1536]{3,2,0,1:T(8,128)(2,1)}, u32[]{:S(2)}, u32[]{:S(2)}) collective-permute-start(bf16[2,2,32,1536]{3,2,0,1:T(8,128)(2,1)S(1)} %pad_maximum_fusion.2), channel_id=1, source_target_pairs={{0,1},{1,0},{2,3},{3,2},{4,5},{5,4},{6,7},{7,6},{8,9},{9,8},{10,11... | collective-permute-start | bytes 1179656 | tf_op jit(solution)/shard_map/ppermute | solution.py:71
  50.2 1.9 %copy-start.6 = (bf16[2,1536,384]{2,1,0:T(8,128)(2,1)S(1)}, bf16[2,1536,384]{2,1,0:T(8,128)(2,1)}, u32[]{:S(2)}) copy-start(bf16[2,1536,384]{2,1,0:T(8,128)(2,1)} %param.18) | copy-start | bytes 7077892
  52.1 8.0 %copy-start.7 = (bf16[384,1536]{1,0:T(8,128)(2,1)S(1)}, bf16[384,1536]{1,0:T(8,128)(2,1)}, u32[]{:S(2)}) copy-start(bf16[384,1536]{1,0:T(8,128)(2,1)} %param.22) | copy-start | bytes 3538948
  52.1 8.0 %copy-start.8 = (f32[384]{0:T(512)S(1)}, f32[384]{0:T(512)}, u32[]{:S(2)}) copy-start(f32[384]{0:T(512)} %param.21) | copy-start | bytes 4612
  52.1 8.0 %copy-start.9 = (f32[384]{0:T(512)S(1)}, f32[384]{0:T(512)}, u32[]{:S(2)}) copy-start(f32[384]{0:T(512)} %param.20) | copy-start | bytes 4612
  53.1 3.6 %collective-permute-start.10 = (bf16[2,15,384]{2,1,0:T(8,128)(2,1)S(1)}, bf16[2,15,384]{2,1,0:T(8,128)(2,1)S(1)}, u32[]{:S(2)}, u32[]{:S(2)}) collective-permute-start(bf16[2,15,384]{2,1,0:T(8,128)(2,1)S(1)} %get-tuple-element.50), channel_id=1, source_target_pairs={{0,4},{4,8},{8,12},{1,5},{5,9},{9,13},{2,6},{6,10},{10,14},{3,7},{... | collective-permute-start | bytes 69128 | tf_op jit(solution)/shard_map/ppermute | solution.py:20
  54.4 5.7 %collective-permute-start.11 = (bf16[2,15,384]{2,1,0:T(8,128)(2,1)S(1)}, bf16[2,15,384]{2,1,0:T(8,128)(2,1)S(1)}, u32[]{:S(2)}, u32[]{:S(2)}) collective-permute-start(bf16[2,15,384]{2,1,0:T(8,128)(2,1)S(1)} %get-tuple-element.51), channel_id=1, source_target_pairs={{4,0},{8,4},{12,8},{5,1},{9,5},{13,9},{6,2},{10,6},{14,10},{7,3},{... | collective-permute-start | bytes 69128 | tf_op jit(solution)/shard_map/ppermute | solution.py:21
  62.8 0.7 copy-start.4
  63.0 1.9 %collective-permute-start.12 = (bf16[2,2,32,1536]{3,2,0,1:T(8,128)(2,1)S(1)}, bf16[2,2,32,1536]{3,2,0,1:T(8,128)(2,1)}, u32[]{:S(2)}, u32[]{:S(2)}) collective-permute-start(bf16[2,2,32,1536]{3,2,0,1:T(8,128)(2,1)S(1)} %bitcast.131), channel_id=1, source_target_pairs={{0,1},{1,0},{2,3},{3,2},{4,5},{5,4},{6,7},{7,6},{8,9},{9,8},{10,11... | collective-permute-start | bytes 1179656 | tf_op jit(solution)/shard_map/ppermute | solution.py:59
  66.0 7.0 %collective-permute-start.13 = (bf16[2,32,1536]{2,1,0:T(8,128)(2,1)S(1)}, bf16[2,32,1536]{2,1,0:T(8,128)(2,1)S(1)}, u32[]{:S(2)}, u32[]{:S(2)}) collective-permute-start(bf16[2,32,1536]{2,1,0:T(8,128)(2,1)S(1)} %fusion.46), channel_id=1, source_target_pairs={{0,2},{1,3},{2,0},{3,1},{4,6},{5,7},{6,4},{7,5},{8,10},{9,11},{10,... | collective-permute-start | bytes 589832 | tf_op jit(solution)/shard_map/ppermute | solution.py:59

commit v8 on v7

--- a/solution.py
+++ b/solution.py
@@ -112,28 +112,14 @@
 
 def attend_by_heads(projected, frame_counts, axis):
     _, records, frames, width = projected.shape
-    count, rank = lax.axis_size(axis), lax.axis_index(axis)
-    group = width // HEAD_DIM // count
-    split = projected.reshape(3, records, frames, count, group, HEAD_DIM)
-    pieces = [lax.dynamic_index_in_dim(split, rank, 3, keepdims=False)]
-    sources = [rank]
-    for shift in range(1, count):
-        target = (rank + shift) % count
-        send = lax.dynamic_index_in_dim(split, target, 3, keepdims=False)
-        pairs = [(i, (i + shift) % count) for i in range(count)]
-        pieces.append(lax.ppermute(send, axis, pairs))
-        sources.append((rank - shift) % count)
-    every = jnp.concatenate(pieces, axis=2)
-    frame_steps = jnp.arange(frames, dtype=jnp.int32)
-    positions = jnp.concatenate([source * frames + frame_steps for source in sources])
+    count = lax.axis_size(axis)
+    every = lax.all_to_all(projected, axis, 3, 2, tiled=True)
+    group = every.shape[-1] // HEAD_DIM
+    every = every.reshape(3, records, count * frames, group, HEAD_DIM)
+    positions = jnp.arange(count * frames, dtype=jnp.int32)
     attended = attend(every[0], every[1], every[2], positions, frame_counts)
-    back = [attended[:, :, :frames]]
-    for shift in range(1, count):
-        rows = attended[:, :, shift * frames : (shift + 1) * frames]
-        pairs = [(i, (i - shift) % count) for i in range(count)]
-        back.append(lax.ppermute(rows, axis, pairs))
-    ordered = jnp.roll(jnp.stack(back, axis=1), rank, axis=1)
-    return ordered.transpose(0, 3, 1, 2, 4).reshape(records, frames, width)
+    attended = attended.transpose(0, 2, 1, 3).reshape(records, count * frames, group * HEAD_DIM)
+    return lax.all_to_all(attended, axis, 1, 2, tiled=True)
 
 
 def shards(

time: 74.3 us -> 82.6 us (1.11)
  waiting for transfers between devices: 33 us -> 37 us
  local copies, waits for them, and re-layouts: 4.29 us -> 7.04 us
  starting transfers between devices: 18.8 us -> 20.3 us
    all_to_all x0 -> x2, waiting for transfers between devices: none -> 17.5 us  [the longest x1 11.6 us: attend_by_heads(): every = lax.all_to_all(projected, axis, 3, 2, tiled=True)]
    ppermute x6 -> x0, starting transfers between devices: 11.3 us -> none  [the longest x3 7.01 us: attend_by_heads(): pieces.append(lax.ppermute(send, axis, pairs))]
    ppermute x6 -> x0, waiting for transfers between devices: 10.6 us -> none  [the longest x3 5.45 us: attend_by_heads(): back.append(lax.ppermute(rows, axis, pairs))]
    all_to_all x0 -> x2, starting transfers between devices: none -> 9.64 us  [the longest x1 6.32 us: attend_by_heads(): every = lax.all_to_all(projected, axis, 3, 2, tiled=True)]
    ppermute x1, waiting for transfers between devices: 3.37 us -> 0.01 us  [with_halo(): after = lax.ppermute(initial, axis, down)]
    ppermute x1, starting transfers between devices: 1.29 us -> 4.55 us  [with_halo(): before = lax.ppermute(last, axis, up)]
    unnamed x27 -> x22, local copies, waits for them, and re-layouts: 1.34 us -> 2.39 us
    convert_element_type x1, local copies, waits for them, and re-layouts: 0.22 us -> 1.1 us  [shards(): projected = jnp.einsum('std,idc->istc', normed, w_qkv, preferred_element_...]
  transfers between devices with their start and end apart: 14 -> 10, of which waited for: 12 -> 9; matrix products, arithmetic and copies ran while one was open for 4% -> 3% of each run, Pallas kernels for 0% -> 0%
where the time goes in v8:
time: 82.6 us; the launch traced here: 81.9 us
  waiting for transfers between devices  37 us (45%)
  starting transfers between devices  20.3 us (25%)
  other arithmetic  9.86 us (12%)
  matrix products  7.23 us (9%)
  local copies, waits for them, and re-layouts  7.04 us (9%)
    ppermute x4, waiting for transfers between devices, reduce_scatter_rows(): lax.ppermute(send.astype(jnp.bfloat16), axis, xor_pairs(count, 1 << b))  14 us
    all_to_all x1, waiting for transfers between devices, attend_by_heads(): every = lax.all_to_all(projected, axis, 3, 2, tiled=True)  11.6 us
    all_to_all x1, starting transfers between devices, attend_by_heads(): every = lax.all_to_all(projected, axis, 3, 2, tiled=True)  6.32 us
    all_to_all x1, waiting for transfers between devices, attend_by_heads(): return lax.all_to_all(attended, axis, 1, 2, tiled=True)  5.88 us
    ppermute x2, waiting for transfers between devices, all_gather_rows(): got = lax.ppermute(acc, axis, xor_pairs(count, 1 << b))  5.08 us
    ppermute x1, starting transfers between devices, with_halo(): before = lax.ppermute(last, axis, up)  4.55 us
    all_to_all x1, starting transfers between devices, attend_by_heads(): return lax.all_to_all(attended, axis, 1, 2, tiled=True)  3.33 us
    ppermute x4, starting transfers between devices, reduce_scatter_rows(): lax.ppermute(send.astype(jnp.bfloat16), axis, xor_pairs(count, 1 << b))  3.24 us
  transfers between devices with their start and end apart: 10, of which 9 were waited for; matrix products, arithmetic and copies ran while one was open for 3% of the time, Pallas kernels for 0%

profile of v8, /device:TPU:0, one launch (start us, length us, event | category | flops | bytes accessed | tf_op | source)
XLA Modules:
  0.0 81.9 jit_solution(1544498131136195370)
XLA Ops:
  0.0 1.5 %convert_reduce_fusion = f32[2,128]{1,0:T(2,128)S(1)} fusion(bf16[2,128,1536]{2,1,0:T(8,128)(2,1)} %param.12), kind=kLoop, calls=%fused_computation.9 | loop fusion | flops 786176 | bytes 787456 | tf_op jit(solution)/shard_map/reduce_sum | solution.py:27
  1.5 1.5 %fusion.9 = f32[2,128]{1,0:T(2,128)S(1)} fusion(bf16[2,128,1536]{2,1,0:T(8,128)(2,1)} %param.12, f32[2,128]{1,0:T(2,128)S(1)} %broadcast_multiply_fusion.1), kind=kLoop, calls=%fused_computation.15 | loop fusion | flops 1572608 | bytes 788480 | tf_op jit(solution)/shard_map/reduce_sum | solution.py:29
  3.0 2.0 %fusion.18 = bf16[3,2,128,256]{3,2,0,1:T(8,128)(2,1)S(1)} fusion(bf16[3,1536,256]{2,1,0:T(8,128)(2,1)S(1)} %copy-done, bf16[2,128,1536]{2,1,0:T(8,128)(2,1)} %param.12, f32[1536]{0:T(1024)} %param.14, f32[2,128]{1,0:T(2,128)S(1)} %add_rsqrt_fusion.1, f32[2,128]{1,0:T(2,128)S(1)} %broadcast_multiply_fusion.1), kind=kOutput, calls=%fused_computation.20 | convolution fusion | flops 606142464 | bytes 3547136 | tf_op jit(solution)/shard_map/std,idc->istc/dot_general | solution.py:146
  5.0 1.1 %copy.63 = bf16[3,2,128,256]{2,1,0,3:T(2,128)(2,1)} copy(bf16[3,2,128,256]{3,2,0,1:T(8,128)(2,1)S(1)} %fusion.18) | data formatting | bytes 786432 | tf_op jit(solution)/shard_map/convert_element_type | solution.py:148
  6.1 6.3 %all-to-all-start = ((bf16[3,2,128,256]{2,1,0,3:T(2,128)(2,1)}), bf16[3,2,128,256]{2,1,0,3:T(2,128)(2,1)S(1)}, u32[]{:S(2)}, u32[]{:S(2)}) async-start(bf16[3,2,128,256]{2,1,0,3:T(2,128)(2,1)} %copy.63), calls=%async_computation | async-start | bytes 786432 | tf_op jit(solution)/shard_map/all_to_all | solution.py:116
  12.5 11.6 %all-to-all-done = bf16[3,2,128,256]{2,1,0,3:T(2,128)(2,1)S(1)} async-done(((bf16[3,2,128,256]{2,1,0,3:T(2,128)(2,1)}), bf16[3,2,128,256]{2,1,0,3:T(2,128)(2,1)S(1)}, u32[]{:S(2)}, u32[]{:S(2)}) %all-to-all-start) | async-done | bytes 393248 | tf_op jit(solution)/shard_map/all_to_all | solution.py:116
  24.2 0.1 copy.67
  24.4 0.1 copy.65
  24.5 0.1 copy.66
  24.7 0.8 fusion.6
  25.5 0.5 fusion.7
  26.0 0.7 fusion.22
  26.7 0.2 copy.69
  26.8 0.9 %reshape.250 = bf16[4,2,8192]{2,1,0:T(2,128)(2,1)} reshape(bf16[512,2,64]{2,1,0:T(2,128)(2,1)S(1)} %bitcast.102) | data formatting | bytes 262144
  27.7 3.3 %all-to-all-start.1 = ((bf16[4,2,8192]{2,1,0:T(2,128)(2,1)}), bf16[4,2,8192]{2,1,0:T(2,128)(2,1)S(1)}, u32[]{:S(2)}, u32[]{:S(2)}) async-start(bf16[4,2,8192]{2,1,0:T(2,128)(2,1)} %reshape.250), calls=%async_computation.1 | async-start | bytes 262144 | tf_op jit(solution)/shard_map/all_to_all | solution.py:122
  31.1 5.9 %all-to-all-done.1 = bf16[4,2,8192]{2,1,0:T(2,128)(2,1)S(1)} async-done(((bf16[4,2,8192]{2,1,0:T(2,128)(2,1)}), bf16[4,2,8192]{2,1,0:T(2,128)(2,1)S(1)}, u32[]{:S(2)}, u32[]{:S(2)}) %all-to-all-start.1) | async-done | bytes 131104 | tf_op jit(solution)/shard_map/all_to_all | solution.py:122
  37.0 0.2 reshape.251
  37.2 0.2 copy.82
  37.4 0.4 convolution_convert_fusion
  38.0 1.7 %collective-permute-done = bf16[2,2,32,1536]{3,2,0,1:T(8,128)(2,1)S(1)} collective-permute-done((bf16[2,2,32,1536]{3,2,0,1:T(8,128)(2,1)S(1)}, bf16[2,2,32,1536]{3,2,0,1:T(8,128)(2,1)S(1)}, u32[]{:S(2)}, u32[]{:S(2)}) %collective-permute-start) | collective-permute-done | bytes 393248 | tf_op jit(solution)/shard_map/ppermute | solution.py:59
  39.7 0.7 copy-done.2
  40.4 1.1 %convert_add_fusion.1 = f32[2,2,32,1536]{3,2,0,1:T(8,128)S(1)} fusion(bf16[2,2,32,1536]{3,2,0,1:T(8,128)(2,1)} %copy-done.2, bf16[2,2,1,32,1536]{4,3,2,1,0:T(8,128)(2,1)S(1)} %get-tuple-element.42), kind=kLoop, calls=%fused_computation.58 | loop fusion | flops 589824 | bytes 1572864 | tf_op jit(solution)/shard_map/add | solution.py:60
  41.6 1.6 %collective-permute-start.1 = (bf16[2,32,1536]{2,1,0:T(8,128)(2,1)S(1)}, bf16[2,32,1536]{2,1,0:T(8,128)(2,1)}, u32[]{:S(2)}, u32[]{:S(2)}) collective-permute-start(bf16[2,32,1536]{2,1,0:T(8,128)(2,1)S(1)} %fusion.44), channel_id=1, source_target_pairs={{0,2},{1,3},{2,0},{3,1},{4,6},{5,7},{6,4},{7,5},{8,10},{9,11},{10,... | collective-permute-start | bytes 589832 | tf_op jit(solution)/shard_map/ppermute | solution.py:59
  43.1 5.6 %collective-permute-done.1 = bf16[2,32,1536]{2,1,0:T(8,128)(2,1)} collective-permute-done((bf16[2,32,1536]{2,1,0:T(8,128)(2,1)S(1)}, bf16[2,32,1536]{2,1,0:T(8,128)(2,1)}, u32[]{:S(2)}, u32[]{:S(2)}) %collective-permute-start.1) | collective-permute-done | bytes 196640 | tf_op jit(solution)/shard_map/ppermute | solution.py:59
  48.7 1.2 %fusion.79 = (f32[2,32]{1,0:T(2,128)S(1)}, f32[2,32,1536]{2,1,0:T(8,128)S(1)}) fusion(bf16[2,32,1536]{2,1,0:T(8,128)(2,1)} %collective-permute-done.1, f32[2,2,32,1536]{3,2,0,1:T(8,128)S(1)} %convert_add_fusion.1, s32[]{:T(128)S(6)} %select_n.62, bf16[2,128,1536]{2,1,0:T(8,128)(2,1)} %param.12, s32[]{:T(128)S(6)} %select_n.58), kind=kLoop, calls=%fused_computation.194 | loop fusion | flops 491456 | bytes 1179912 | tf_op jit(solution)/shard_map/reduce_sum | solution.py:27
  49.9 0.2 multiply_reduce_fusion
  50.1 0.1 multiply_convert_fusion.1
  50.2 1.6 %collective-permute-start.2 = (bf16[2,32,1536]{2,1,0:T(8,128)(2,1)S(1)}, bf16[2,32,1536]{2,1,0:T(8,128)(2,1)S(1)}, u32[]{:S(2)}, u32[]{:S(2)}) collective-permute-start(bf16[2,32,1536]{2,1,0:T(8,128)(2,1)S(1)} %multiply_convert_fusion.1), channel_id=1, source_target_pairs={{0,2},{1,3},{2,0},{3,1},{4,6},{5,7},{6,4},{7,5},{8,10},{9,11},{10,... | collective-permute-start | bytes 589832 | tf_op jit(solution)/shard_map/ppermute | solution.py:71
  51.8 4.6 %collective-permute-done.2 = bf16[2,32,1536]{2,1,0:T(8,128)(2,1)S(1)} collective-permute-done((bf16[2,32,1536]{2,1,0:T(8,128)(2,1)S(1)}, bf16[2,32,1536]{2,1,0:T(8,128)(2,1)S(1)}, u32[]{:S(2)}, u32[]{:S(2)}) %collective-permute-start.2) | collective-permute-done | bytes 196640 | tf_op jit(solution)/shard_map/ppermute | solution.py:71
  56.4 0.2 select_bitcast_fusion.3
  56.7 1.3 %slice_reduce_fusion.30 = (f32[384]{0:T(512)S(1)}, f32[384]{0:T(512)S(1)}, f32[384]{0:T(512)S(1)}, f32[384]{0:T(512)S(1)}, f32[384]{0:T(512)S(1)}, /*index=5*/f3...) fusion(f32[31,384]{1,0:T(8,128)} %param.19), kind=kLoop, calls=%fused_computation.180 | loop fusion | bytes 58368 | tf_op jit(solution)/shard_map/slice | solution.py:183
  58.0 0.1 broadcast_compare_fusion
  58.1 0.5 collective-permute-done.3
  58.5 1.3 %select_bitcast_fusion.1 = (bf16[2,2,1,32,1536]{4,3,0,1,2:T(8,128)(2,1)S(1)}, bf16[2,2,1,32,1536]{4,3,0,1,2:T(8,128)(2,1)S(1)}) fusion(bf16[2,2,32,1536]{3,2,0,1:T(8,128)(2,1)} %collective-permute-done.3, pred[]{:T(512)S(6)} %eq.6, bf16[2,1,32,1536]{3,2,0,1:T(8,128)(2,1)S(1)} %get-tuple-element.45, bf16[2,1,32,1536]{3,2,0,1:T(8,128)(2,1)S(1)} %get-tuple-element.44), kind=kLoop, calls=%fused_computation.84 | loop fusion | flops 589824 | bytes 1572865 | tf_op jit(solution)/shard_map/stack | solution.py:74
  59.8 0.1 pad_maximum_fusion
  60.0 0.8 fusion.12
  60.8 0.1 bitcast_select_fusion
  60.9 1.3 %collective-permute-start.5 = (bf16[2,15,384]{2,1,0:T(8,128)(2,1)S(1)}, bf16[2,15,384]{2,1,0:T(8,128)(2,1)S(1)}, u32[]{:S(2)}, u32[]{:S(2)}) collective-permute-start(bf16[2,15,384]{2,1,0:T(8,128)(2,1)S(1)} %get-tuple-element.50), channel_id=1, source_target_pairs={{4,0},{8,4},{12,8},{5,1},{9,5},{13,9},{6,2},{10,6},{14,10},{7,3},{... | collective-permute-start | bytes 69128 | tf_op jit(solution)/shard_map/ppermute | solution.py:21
  62.2 4.5 %collective-permute-start.4 = (bf16[2,15,384]{2,1,0:T(8,128)(2,1)S(1)}, bf16[2,15,384]{2,1,0:T(8,128)(2,1)S(1)}, u32[]{:S(2)}, u32[]{:S(2)}) collective-permute-start(bf16[2,15,384]{2,1,0:T(8,128)(2,1)S(1)} %get-tuple-element.49), channel_id=1, source_target_pairs={{0,4},{4,8},{8,12},{1,5},{5,9},{9,13},{2,6},{6,10},{10,14},{3,7},{... | collective-permute-start | bytes 69128 | tf_op jit(solution)/shard_map/ppermute | solution.py:20
  66.8 1.0 %slice_reduce_fusion.29 = (f32[384]{0:T(512)S(1)}, f32[384]{0:T(512)S(1)}, f32[384]{0:T(512)S(1)}, f32[384]{0:T(512)S(1)}, f32[384]{0:T(512)S(1)}, /*index=5*/f3...) fusion(f32[31,384]{1,0:T(8,128)} %param.19), kind=kLoop, calls=%fused_computation.179 | loop fusion | bytes 36864 | tf_op jit(solution)/shard_map/slice | solution.py:183
  67.8 0.5 collective-permute-done.4
  68.3 2.7 %convolution_convert_fusion.1 = bf16[2,128,1536]{2,1,0:T(8,128)(2,1)S(1)} fusion(bf16[384,1536]{1,0:T(8,128)(2,1)S(1)} %copy-done.7, bf16[2,128,384]{2,1,0:T(8,128)(2,1)S(1)} %bitcast_select_fusion, bf16[2,15,384]{2,1,0:T(8,128)(2,1)S(1)} %collective-permute-done.5, bf16[2,15,384]{2,1,0:T(8,128)(2,1)S(1)} %collective-permute-done.4, f32[384]{0:T(512)S(1)} %copy-done.8, ...), kind=kOutput, calls=%fused_computation.1 | convolution fusion | flops 320962560 | bytes 2259456 | tf_op jit(solution)/shard_map/stc,cd->std/dot_general | solution.py:186
  71.2 0.5 copy-done.4
  71.7 1.3 %collective-permute-done.6 = bf16[2,2,32,1536]{3,2,0,1:T(8,128)(2,1)} collective-permute-done((bf16[2,2,32,1536]{3,2,0,1:T(8,128)(2,1)S(1)}, bf16[2,2,32,1536]{3,2,0,1:T(8,128)(2,1)}, u32[]{:S(2)}, u32[]{:S(2)}) %collective-permute-start.6) | collective-permute-done | bytes 393248 | tf_op jit(solution)/shard_map/ppermute | solution.py:59
  73.0 1.1 %convert_add_fusion = f32[2,2,32,1536]{3,2,0,1:T(8,128)S(1)} fusion(bf16[2,2,32,1536]{3,2,0,1:T(8,128)(2,1)} %collective-permute-done.6, bf16[2,2,1,32,1536]{4,3,2,1,0:T(8,128)(2,1)S(1)} %get-tuple-element.38), kind=kLoop, calls=%fused_computation.57 | loop fusion | flops 589824 | bytes 1572864 | tf_op jit(solution)/shard_map/add | solution.py:60
  74.1 1.5 %collective-permute-start.7 = (bf16[2,32,1536]{2,1,0:T(8,128)(2,1)S(1)}, bf16[2,32,1536]{2,1,0:T(8,128)(2,1)S(1)}, u32[]{:S(2)}, u32[]{:S(2)}) collective-permute-start(bf16[2,32,1536]{2,1,0:T(8,128)(2,1)S(1)} %fusion.45), channel_id=1, source_target_pairs={{0,2},{1,3},{2,0},{3,1},{4,6},{5,7},{6,4},{7,5},{8,10},{9,11},{10,... | collective-permute-start | bytes 589832 | tf_op jit(solution)/shard_map/ppermute | solution.py:59
  75.8 5.4 %collective-permute-done.7 = bf16[2,32,1536]{2,1,0:T(8,128)(2,1)S(1)} collective-permute-done((bf16[2,32,1536]{2,1,0:T(8,128)(2,1)S(1)}, bf16[2,32,1536]{2,1,0:T(8,128)(2,1)S(1)}, u32[]{:S(2)}, u32[]{:S(2)}) %collective-permute-start.7) | collective-permute-done | bytes 196640 | tf_op jit(solution)/shard_map/ppermute | solution.py:59
  81.2 0.8 fusion.41
  (46 shorter events, 1.1 us)
Async XLA Ops:
  0.0 3.0 %copy-start = (bf16[3,1536,256]{2,1,0:T(8,128)(2,1)S(1)}, bf16[3,1536,256]{2,1,0:T(8,128)(2,1)}, u32[]{:S(2)}) copy-start(bf16[3,1536,256]{2,1,0:T(8,128)(2,1)} %param.15) | copy-start | bytes 7077892
  3.0 9.4 %copy-start.5 = (s32[2]{0:T(128)S(1)}, s32[2]{0:T(128)}, u32[]{:S(2)}) copy-start(s32[2]{0:T(128)} %param.13) | copy-start | bytes 28
  6.1 18.0 %all-to-all-start = ((bf16[3,2,128,256]{2,1,0,3:T(2,128)(2,1)}), bf16[3,2,128,256]{2,1,0,3:T(2,128)(2,1)S(1)}, u32[]{:S(2)}, u32[]{:S(2)}) async-start(bf16[3,2,128,256]{2,1,0,3:T(2,128)(2,1)} %copy.63), calls=%async_computation | async-start | bytes 786432 | tf_op jit(solution)/shard_map/all_to_all | solution.py:116
  26.0 11.4 %copy-start.1 = (bf16[256,1536]{1,0:T(8,128)(2,1)S(1)}, bf16[256,1536]{1,0:T(8,128)(2,1)}, u32[]{:S(2)}) copy-start(bf16[256,1536]{1,0:T(8,128)(2,1)} %param.16) | copy-start | bytes 2359300
  27.7 9.2 %all-to-all-start.1 = ((bf16[4,2,8192]{2,1,0:T(2,128)(2,1)}), bf16[4,2,8192]{2,1,0:T(2,128)(2,1)S(1)}, u32[]{:S(2)}, u32[]{:S(2)}) async-start(bf16[4,2,8192]{2,1,0:T(2,128)(2,1)} %reshape.250), calls=%async_computation.1 | async-start | bytes 262144 | tf_op jit(solution)/shard_map/all_to_all | solution.py:122
  37.9 12.2 %copy-start.3 = (f32[1536]{0:T(1024)S(1)}, f32[1536]{0:T(1024)}, u32[]{:S(2)}) copy-start(f32[1536]{0:T(1024)} %param.17) | copy-start | bytes 18436
  37.9 1.8 %collective-permute-start = (bf16[2,2,32,1536]{3,2,0,1:T(8,128)(2,1)S(1)}, bf16[2,2,32,1536]{3,2,0,1:T(8,128)(2,1)S(1)}, u32[]{:S(2)}, u32[]{:S(2)}) collective-permute-start(bf16[2,2,32,1536]{3,2,0,1:T(8,128)(2,1)S(1)} %bitcast.108), channel_id=1, source_target_pairs={{0,1},{1,0},{2,3},{3,2},{4,5},{5,4},{6,7},{7,6},{8,9},{9,8},{10,11... | collective-permute-start | bytes 1179656 | tf_op jit(solution)/shard_map/ppermute | solution.py:59
  39.7 0.7 copy-start.2
  41.6 7.1 %collective-permute-start.1 = (bf16[2,32,1536]{2,1,0:T(8,128)(2,1)S(1)}, bf16[2,32,1536]{2,1,0:T(8,128)(2,1)}, u32[]{:S(2)}, u32[]{:S(2)}) collective-permute-start(bf16[2,32,1536]{2,1,0:T(8,128)(2,1)S(1)} %fusion.44), channel_id=1, source_target_pairs={{0,2},{1,3},{2,0},{3,1},{4,6},{5,7},{6,4},{7,5},{8,10},{9,11},{10,... | collective-permute-start | bytes 589832 | tf_op jit(solution)/shard_map/ppermute | solution.py:59
  50.2 6.2 %collective-permute-start.2 = (bf16[2,32,1536]{2,1,0:T(8,128)(2,1)S(1)}, bf16[2,32,1536]{2,1,0:T(8,128)(2,1)S(1)}, u32[]{:S(2)}, u32[]{:S(2)}) collective-permute-start(bf16[2,32,1536]{2,1,0:T(8,128)(2,1)S(1)} %multiply_convert_fusion.1), channel_id=1, source_target_pairs={{0,2},{1,3},{2,0},{3,1},{4,6},{5,7},{6,4},{7,5},{8,10},{9,11},{10,... | collective-permute-start | bytes 589832 | tf_op jit(solution)/shard_map/ppermute | solution.py:71
  56.6 1.9 %collective-permute-start.3 = (bf16[2,2,32,1536]{3,2,0,1:T(8,128)(2,1)S(1)}, bf16[2,2,32,1536]{3,2,0,1:T(8,128)(2,1)}, u32[]{:S(2)}, u32[]{:S(2)}) collective-permute-start(bf16[2,2,32,1536]{3,2,0,1:T(8,128)(2,1)S(1)} %pad_maximum_fusion.1), channel_id=1, source_target_pairs={{0,1},{1,0},{2,3},{3,2},{4,5},{5,4},{6,7},{7,6},{8,9},{9,8},{10,11... | collective-permute-start | bytes 1179656 | tf_op jit(solution)/shard_map/ppermute | solution.py:71
  58.1 1.9 %copy-start.6 = (bf16[2,1536,384]{2,1,0:T(8,128)(2,1)S(1)}, bf16[2,1536,384]{2,1,0:T(8,128)(2,1)}, u32[]{:S(2)}) copy-start(bf16[2,1536,384]{2,1,0:T(8,128)(2,1)} %param.18) | copy-start | bytes 7077892
  60.0 8.3 %copy-start.7 = (bf16[384,1536]{1,0:T(8,128)(2,1)S(1)}, bf16[384,1536]{1,0:T(8,128)(2,1)}, u32[]{:S(2)}) copy-start(bf16[384,1536]{1,0:T(8,128)(2,1)} %param.22) | copy-start | bytes 3538948
  60.0 8.3 %copy-start.8 = (f32[384]{0:T(512)S(1)}, f32[384]{0:T(512)}, u32[]{:S(2)}) copy-start(f32[384]{0:T(512)} %param.21) | copy-start | bytes 4612
  60.0 8.3 %copy-start.9 = (f32[384]{0:T(512)S(1)}, f32[384]{0:T(512)}, u32[]{:S(2)}) copy-start(f32[384]{0:T(512)} %param.20) | copy-start | bytes 4612
  60.9 6.9 %collective-permute-start.5 = (bf16[2,15,384]{2,1,0:T(8,128)(2,1)S(1)}, bf16[2,15,384]{2,1,0:T(8,128)(2,1)S(1)}, u32[]{:S(2)}, u32[]{:S(2)}) collective-permute-start(bf16[2,15,384]{2,1,0:T(8,128)(2,1)S(1)} %get-tuple-element.50), channel_id=1, source_target_pairs={{4,0},{8,4},{12,8},{5,1},{9,5},{13,9},{6,2},{10,6},{14,10},{7,3},{... | collective-permute-start | bytes 69128 | tf_op jit(solution)/shard_map/ppermute | solution.py:21
  62.2 6.1 %collective-permute-start.4 = (bf16[2,15,384]{2,1,0:T(8,128)(2,1)S(1)}, bf16[2,15,384]{2,1,0:T(8,128)(2,1)S(1)}, u32[]{:S(2)}, u32[]{:S(2)}) collective-permute-start(bf16[2,15,384]{2,1,0:T(8,128)(2,1)S(1)} %get-tuple-element.49), channel_id=1, source_target_pairs={{0,4},{4,8},{8,12},{1,5},{5,9},{9,13},{2,6},{6,10},{10,14},{3,7},{... | collective-permute-start | bytes 69128 | tf_op jit(solution)/shard_map/ppermute | solution.py:20
  71.0 0.7 copy-start.4
  71.1 1.9 %collective-permute-start.6 = (bf16[2,2,32,1536]{3,2,0,1:T(8,128)(2,1)S(1)}, bf16[2,2,32,1536]{3,2,0,1:T(8,128)(2,1)}, u32[]{:S(2)}, u32[]{:S(2)}) collective-permute-start(bf16[2,2,32,1536]{3,2,0,1:T(8,128)(2,1)S(1)} %bitcast.109), channel_id=1, source_target_pairs={{0,1},{1,0},{2,3},{3,2},{4,5},{5,4},{6,7},{7,6},{8,9},{9,8},{10,11... | collective-permute-start | bytes 1179656 | tf_op jit(solution)/shard_map/ppermute | solution.py:59
  74.1 7.0 %collective-permute-start.7 = (bf16[2,32,1536]{2,1,0:T(8,128)(2,1)S(1)}, bf16[2,32,1536]{2,1,0:T(8,128)(2,1)S(1)}, u32[]{:S(2)}, u32[]{:S(2)}) collective-permute-start(bf16[2,32,1536]{2,1,0:T(8,128)(2,1)S(1)} %fusion.45), channel_id=1, source_target_pairs={{0,2},{1,3},{2,0},{3,1},{4,6},{5,7},{6,4},{7,5},{8,10},{9,11},{10,... | collective-permute-start | bytes 589832 | tf_op jit(solution)/shard_map/ppermute | solution.py:59

commit v9 on v7

--- a/solution.py
+++ b/solution.py
@@ -67,11 +67,11 @@
     shape = x.shape
     acc = x
     for k, b in enumerate(reversed(range(bits))):
-        mine = ((rank >> b) & 1) == 0
+        mine = (rank >> b) & 1
         got = lax.ppermute(acc, axis, xor_pairs(count, 1 << b))
-        low = jnp.where(mine, acc, got)
-        high = jnp.where(mine, got, acc)
-        acc = jnp.stack([low, high], axis=dim + k)
+        both = jnp.zeros(acc.shape[: dim + k] + (2,) + acc.shape[dim + k :], acc.dtype)
+        both = lax.dynamic_update_index_in_dim(both, acc, mine, dim + k)
+        acc = lax.dynamic_update_index_in_dim(both, got, 1 - mine, dim + k)
     return acc.reshape(shape[:dim] + (shape[dim] * count,) + shape[dim + 1 :])
 
 
@@ -189,13 +189,15 @@
     gated_rows = jnp.where(frame_live[..., None], gated_rows, jnp.zeros((), jnp.bfloat16))
     rim_width = kernel.shape[0] // 2
     padded = with_halo(gated_rows, (("ctx", 1),), rim_width)
-    depthwise = jnp.zeros(gated_rows.shape, jnp.float32)
-    for tap_index in range(kernel.shape[0]):
-        depthwise = (
-            depthwise
-            + padded[:, tap_index : tap_index + frames_here, :].astype(jnp.float32)
-            * kernel[tap_index]
-        )
+    depthwise = lax.conv_general_dilated(
+        padded.astype(jnp.float32),
+        kernel[:, None, :],
+        window_strides=(1,),
+        padding="VALID",
+        dimension_numbers=("NWC", "WIO", "NWC"),
+        feature_group_count=kernel.shape[1],
+        precision=lax.Precision.HIGHEST,
+    )
     activated = jax.nn.silu(depthwise * bn_scale + bn_shift).astype(jnp.bfloat16)
     conv_part = jnp.einsum("stc,cd->std", activated, w_pw, preferred_element_type=jnp.float32)
     conv_rows = reduce_scatter_rows(conv_part.astype(jnp.bfloat16), "mp", 1)

time: 74.3 us -> 71.6 us (0.964)
  waiting for transfers between devices: 33 us -> 35.6 us
  local copies, waits for them, and re-layouts: 4.29 us -> 1.79 us
  other arithmetic: 9.93 us -> 8.42 us
  matrix products: 7.31 us -> 6.24 us
    slice x2 -> x0, local copies, waits for them, and re-layouts: 2.32 us -> none  [shards(): kernel[tap_index]]
    dot_general x1, matrix products: 2.75 us -> 0.59 us  [shards(): jnp.einsum('stc,cd->std', activated, w_pw, preferred_element_type=jnp.flo...]
    another operation x4 -> x0, other arithmetic: 1.58 us -> none  [all_gather_rows(): acc = jnp.stack([low, high], axis=dim + k)]
    conv_general_dilated x0 -> x1, matrix products: none -> 1.07 us  [shards(): lax.conv_general_dilated(padded.astype(jnp.float32), kernel[:, None, :],...]
    ppermute x2, waiting for transfers between devices: 5.09 us -> 6.15 us  [all_gather_rows(): got = lax.ppermute(acc, axis, xor_pairs(count, 1 << b))]
    ppermute x1, waiting for transfers between devices: 3.37 us -> 4.22 us  [with_halo(): after = lax.ppermute(initial, axis, down)]
  transfers between devices with their start and end apart: 14 -> 14, of which waited for: 12 -> 13; matrix products, arithmetic and copies ran while one was open for 4% -> 1% of each run, Pallas kernels for 0% -> 0%
where the time goes in v9:
time: 71.6 us; the launch traced here: 71.3 us
  waiting for transfers between devices  35.6 us (50%)
  starting transfers between devices  18.8 us (26%)
  other arithmetic  8.42 us (12%)
  matrix products  6.24 us (9%)
  local copies, waits for them, and re-layouts  1.79 us (2%)
    ppermute x4, waiting for transfers between devices, reduce_scatter_rows(): lax.ppermute(send.astype(jnp.bfloat16), axis, xor_pairs(count, 1 << b))  14.4 us
    ppermute x3, starting transfers between devices, attend_by_heads(): pieces.append(lax.ppermute(send, axis, pairs))  7.01 us
    ppermute x2, waiting for transfers between devices, all_gather_rows(): got = lax.ppermute(acc, axis, xor_pairs(count, 1 << b))  6.15 us
    ppermute x3, waiting for transfers between devices, attend_by_heads(): back.append(lax.ppermute(rows, axis, pairs))  5.44 us
    ppermute x3, waiting for transfers between devices, attend_by_heads(): pieces.append(lax.ppermute(send, axis, pairs))  5.16 us
    ppermute x3, starting transfers between devices, attend_by_heads(): back.append(lax.ppermute(rows, axis, pairs))  4.3 us
    ppermute x1, waiting for transfers between devices, with_halo(): after = lax.ppermute(initial, axis, down)  4.22 us
    ppermute x4, starting transfers between devices, reduce_scatter_rows(): lax.ppermute(send.astype(jnp.bfloat16), axis, xor_pairs(count, 1 << b))  3.25 us
  transfers between devices with their start and end apart: 14, of which 13 were waited for; matrix products, arithmetic and copies ran while one was open for 1% of the time, Pallas kernels for 0%

profile of v9, /device:TPU:0, one launch (start us, length us, event | category | flops | bytes accessed | tf_op | source)
XLA Modules:
  0.0 71.3 jit_solution(2638984297024708278)
XLA Ops:
  0.0 1.5 %convert_reduce_fusion = f32[2,128]{1,0:T(2,128)S(1)} fusion(bf16[2,128,1536]{2,1,0:T(8,128)(2,1)} %param.12), kind=kLoop, calls=%fused_computation.9 | loop fusion | flops 786176 | bytes 787456 | tf_op jit(solution)/shard_map/reduce_sum | solution.py:27
  1.5 1.5 %fusion.9 = f32[2,128]{1,0:T(2,128)S(1)} fusion(bf16[2,128,1536]{2,1,0:T(8,128)(2,1)} %param.12, f32[2,128]{1,0:T(2,128)S(1)} %broadcast_multiply_fusion.1), kind=kLoop, calls=%fused_computation.15 | loop fusion | flops 1572608 | bytes 788480 | tf_op jit(solution)/shard_map/reduce_sum | solution.py:29
  3.0 2.0 %fusion.18 = bf16[3,2,128,256]{3,2,0,1:T(8,128)(2,1)S(1)} fusion(bf16[3,1536,256]{2,1,0:T(8,128)(2,1)S(1)} %copy-done, bf16[2,128,1536]{2,1,0:T(8,128)(2,1)} %param.12, f32[1536]{0:T(1024)} %param.14, f32[2,128]{1,0:T(2,128)S(1)} %add_rsqrt_fusion.1, f32[2,128]{1,0:T(2,128)S(1)} %broadcast_multiply_fusion.1), kind=kOutput, calls=%fused_computation.20 | convolution fusion | flops 606142464 | bytes 3547136 | tf_op jit(solution)/shard_map/std,idc->istc/dot_general | solution.py:160
  5.0 0.2 copy.39
  5.3 3.1 %collective-permute-start = (bf16[3,2,128,1,64]{2,4,1,3,0:T(8,128)(2,1)S(1)}, bf16[3,2,128,1,64]{2,4,1,3,0:T(8,128)(2,1)S(1)}, u32[]{:S(2)}, u32[]{:S(2)}) collective-permute-start(bf16[3,2,128,1,64]{2,4,1,3,0:T(8,128)(2,1)S(1)} %get-tuple-element.16), channel_id=1, source_target_pairs={{0,4},{4,8},{8,12},{12,0},{1,5},{5,9},{9,13},{13,1},{2,6},{6,10},{... | collective-permute-start | bytes 294920 | tf_op jit(solution)/shard_map/ppermute | solution.py:124
  8.4 2.6 %collective-permute-start.1 = (bf16[3,2,128,1,64]{2,4,1,3,0:T(8,128)(2,1)S(1)}, bf16[3,2,128,1,64]{2,4,1,3,0:T(8,128)(2,1)S(1)}, u32[]{:S(2)}, u32[]{:S(2)}) collective-permute-start(bf16[3,2,128,1,64]{2,4,1,3,0:T(8,128)(2,1)S(1)} %get-tuple-element.15), channel_id=1, source_target_pairs={{0,8},{4,12},{8,0},{12,4},{1,9},{5,13},{9,1},{13,5},{2,10},{6,14},... | collective-permute-start | bytes 294920 | tf_op jit(solution)/shard_map/ppermute | solution.py:124
  10.9 1.3 %collective-permute-start.2 = (bf16[3,2,128,1,64]{2,4,1,3,0:T(8,128)(2,1)S(1)}, bf16[3,2,128,1,64]{2,4,1,3,0:T(8,128)(2,1)S(1)}, u32[]{:S(2)}, u32[]{:S(2)}) collective-permute-start(bf16[3,2,128,1,64]{2,4,1,3,0:T(8,128)(2,1)S(1)} %get-tuple-element.14), channel_id=1, source_target_pairs={{0,12},{4,0},{8,4},{12,8},{1,13},{5,1},{9,5},{13,9},{2,14},{6,2},{... | collective-permute-start | bytes 294920 | tf_op jit(solution)/shard_map/ppermute | solution.py:124
  12.3 0.1 broadcast_compare_fusion
  12.4 1.6 %collective-permute-done = bf16[3,2,128,1,64]{2,4,1,3,0:T(8,128)(2,1)S(1)} collective-permute-done((bf16[3,2,128,1,64]{2,4,1,3,0:T(8,128)(2,1)S(1)}, bf16[3,2,128,1,64]{2,4,1,3,0:T(8,128)(2,1)S(1)}, u32[]{:S(2)}, u32[]{:S(2)}) %collective-permute-start) | collective-permute-done | bytes 98336 | tf_op jit(solution)/shard_map/ppermute | solution.py:124
  14.0 3.5 %collective-permute-done.1 = bf16[3,2,128,1,64]{2,4,1,3,0:T(8,128)(2,1)S(1)} collective-permute-done((bf16[3,2,128,1,64]{2,4,1,3,0:T(8,128)(2,1)S(1)}, bf16[3,2,128,1,64]{2,4,1,3,0:T(8,128)(2,1)S(1)}, u32[]{:S(2)}, u32[]{:S(2)}) %collective-permute-start.1) | collective-permute-done | bytes 98336 | tf_op jit(solution)/shard_map/ppermute | solution.py:124
  17.6 0.8 %fusion.6 = (f32[2,512]{1,0:T(2,128)S(1)}, f32[2,512,512]{1,2,0:T(8,128)S(1)}) fusion(pred[2,512]{1,0:T(4,128)(4,1)S(1)} %broadcast_compare_fusion, bf16[3,2,512,1,64]{2,4,1,3,0:T(8,128)(2,1)S(1)} %pad_maximum_fusion), kind=kOutput, calls=%fused_computation.12 | convolution fusion | flops 68680704 | bytes 2365440 | tf_op jit(solution)/shard_map/sqhe,skhe->shqk/dot_general | solution.py:96
  18.4 0.5 fusion.7
  18.9 0.6 fusion.23
  19.6 3.6 %collective-permute-start.3 = (bf16[2,1,128,64]{2,3,0,1:T(8,128)(2,1)S(1)}, bf16[2,1,128,64]{2,3,0,1:T(8,128)(2,1)S(1)}, u32[]{:S(2)}, u32[]{:S(2)}) collective-permute-start(bf16[2,1,128,64]{2,3,0,1:T(8,128)(2,1)S(1)} %get-tuple-element.21), channel_id=1, source_target_pairs={{0,12},{4,0},{8,4},{12,8},{1,13},{5,1},{9,5},{13,9},{2,14},{6,2},{... | collective-permute-start | bytes 98312 | tf_op jit(solution)/shard_map/ppermute | solution.py:134
  23.3 0.4 collective-permute-start.4
  23.7 0.2 collective-permute-start.5
  23.9 0.9 %collective-permute-done.3 = bf16[2,1,128,64]{2,3,0,1:T(8,128)(2,1)S(1)} collective-permute-done((bf16[2,1,128,64]{2,3,0,1:T(8,128)(2,1)S(1)}, bf16[2,1,128,64]{2,3,0,1:T(8,128)(2,1)S(1)}, u32[]{:S(2)}, u32[]{:S(2)}) %collective-permute-start.3) | collective-permute-done | bytes 32800 | tf_op jit(solution)/shard_map/ppermute | solution.py:134
  24.9 3.4 %collective-permute-done.4 = bf16[2,1,128,64]{2,3,0,1:T(8,128)(2,1)S(1)} collective-permute-done((bf16[2,1,128,64]{2,3,0,1:T(8,128)(2,1)S(1)}, bf16[2,1,128,64]{2,3,0,1:T(8,128)(2,1)S(1)}, u32[]{:S(2)}, u32[]{:S(2)}) %collective-permute-start.4) | collective-permute-done | bytes 32800 | tf_op jit(solution)/shard_map/ppermute | solution.py:134
  28.2 1.2 %collective-permute-done.5 = bf16[2,1,128,64]{2,3,0,1:T(8,128)(2,1)S(1)} collective-permute-done((bf16[2,1,128,64]{2,3,0,1:T(8,128)(2,1)S(1)}, bf16[2,1,128,64]{2,3,0,1:T(8,128)(2,1)S(1)}, u32[]{:S(2)}, u32[]{:S(2)}) %collective-permute-start.5) | collective-permute-done | bytes 32800 | tf_op jit(solution)/shard_map/ppermute | solution.py:134
  29.5 0.4 convolution_convert_fusion
  30.1 1.7 %collective-permute-done.6 = bf16[2,2,32,1536]{3,2,0,1:T(8,128)(2,1)S(1)} collective-permute-done((bf16[2,2,32,1536]{3,2,0,1:T(8,128)(2,1)S(1)}, bf16[2,2,32,1536]{3,2,0,1:T(8,128)(2,1)S(1)}, u32[]{:S(2)}, u32[]{:S(2)}) %collective-permute-start.6) | collective-permute-done | bytes 393248 | tf_op jit(solution)/shard_map/ppermute | solution.py:59
  31.8 0.8 %copy-done.2 = bf16[2,2,32,1536]{3,2,0,1:T(8,128)(2,1)} copy-done((bf16[2,2,32,1536]{3,2,0,1:T(8,128)(2,1)}, bf16[2,2,32,1536]{3,2,0,1:T(8,128)(2,1)S(1)}, u32[]{:S(2)}) %copy-start.2) | copy-done | bytes 393240
  32.6 1.1 %convert_add_fusion.1 = f32[2,2,32,1536]{3,2,0,1:T(8,128)S(1)} fusion(bf16[2,2,32,1536]{3,2,0,1:T(8,128)(2,1)} %copy-done.2, bf16[2,2,1,32,1536]{4,3,2,1,0:T(8,128)(2,1)S(1)} %get-tuple-element.11), kind=kLoop, calls=%fused_computation.30 | loop fusion | flops 589824 | bytes 1572864 | tf_op jit(solution)/shard_map/add | solution.py:60
  33.7 1.6 %collective-permute-start.7 = (bf16[2,32,1536]{2,1,0:T(8,128)(2,1)S(1)}, bf16[2,32,1536]{2,1,0:T(8,128)(2,1)}, u32[]{:S(2)}, u32[]{:S(2)}) collective-permute-start(bf16[2,32,1536]{2,1,0:T(8,128)(2,1)S(1)} %fusion.48), channel_id=1, source_target_pairs={{0,2},{1,3},{2,0},{3,1},{4,6},{5,7},{6,4},{7,5},{8,10},{9,11},{10,... | collective-permute-start | bytes 589832 | tf_op jit(solution)/shard_map/ppermute | solution.py:59
  35.2 5.6 %collective-permute-done.7 = bf16[2,32,1536]{2,1,0:T(8,128)(2,1)} collective-permute-done((bf16[2,32,1536]{2,1,0:T(8,128)(2,1)S(1)}, bf16[2,32,1536]{2,1,0:T(8,128)(2,1)}, u32[]{:S(2)}, u32[]{:S(2)}) %collective-permute-start.7) | collective-permute-done | bytes 196640 | tf_op jit(solution)/shard_map/ppermute | solution.py:59
  40.8 1.2 %fusion.61 = (f32[2,32]{1,0:T(2,128)S(1)}, f32[2,32,1536]{2,1,0:T(8,128)S(1)}) fusion(bf16[2,32,1536]{2,1,0:T(8,128)(2,1)} %collective-permute-done.7, f32[2,2,32,1536]{3,2,0,1:T(8,128)S(1)} %convert_add_fusion.1, s32[]{:T(128)S(6)} %select_n.108, bf16[2,128,1536]{2,1,0:T(8,128)(2,1)} %param.12, s32[]{:T(128)S(6)} %select_n.92), kind=kLoop, calls=%fused_computation.115 | loop fusion | flops 491456 | bytes 1179912 | tf_op jit(solution)/shard_map/reduce_sum | solution.py:27
  42.0 0.2 multiply_reduce_fusion
  42.2 0.1 bitcast_dynamic-update-slice_fusion.2
  42.4 1.6 %collective-permute-start.8 = (bf16[2,32,1536]{2,1,0:T(8,128)(2,1)S(1)}, bf16[2,32,1536]{2,1,0:T(8,128)(2,1)S(1)}, u32[]{:S(2)}, u32[]{:S(2)}) collective-permute-start(bf16[2,32,1536]{2,1,0:T(8,128)(2,1)S(1)} %get-tuple-element.6), channel_id=1, source_target_pairs={{0,2},{1,3},{2,0},{3,1},{4,6},{5,7},{6,4},{7,5},{8,10},{9,11},{10,... | collective-permute-start | bytes 589832 | tf_op jit(solution)/shard_map/ppermute | solution.py:71
  43.9 0.1 broadcast_compare_fusion.1
  44.0 4.6 %collective-permute-done.8 = bf16[2,32,1536]{2,1,0:T(8,128)(2,1)S(1)} collective-permute-done((bf16[2,32,1536]{2,1,0:T(8,128)(2,1)S(1)}, bf16[2,32,1536]{2,1,0:T(8,128)(2,1)S(1)}, u32[]{:S(2)}, u32[]{:S(2)}) %collective-permute-start.8) | collective-permute-done | bytes 196640 | tf_op jit(solution)/shard_map/ppermute | solution.py:71
  48.8 1.6 %collective-permute-done.9 = bf16[2,2,32,1536]{3,2,1,0:T(8,128)(2,1)S(1)} collective-permute-done((bf16[2,2,32,1536]{3,2,1,0:T(8,128)(2,1)S(1)}, bf16[2,2,32,1536]{3,2,1,0:T(8,128)(2,1)S(1)}, u32[]{:S(2)}, u32[]{:S(2)}) %collective-permute-start.9) | collective-permute-done | bytes 393248 | tf_op jit(solution)/shard_map/ppermute | solution.py:71
  50.4 0.8 %fusion.12 = f32[2,2,128,384]{3,2,0,1:T(8,128)S(1)} fusion(bf16[2,128,1536,1]{2,1,3,0:T(8,128)(2,1)S(1)} %bitcast.134, bf16[2,1536,384]{2,1,0:T(8,128)(2,1)S(1)} %copy-done.6), kind=kOutput, calls=%fused_computation.18 | convolution fusion | flops 603979776 | bytes 3932160 | tf_op jit(solution)/shard_map/std,gdc->gstc/dot_general | solution.py:34
  51.2 0.1 bitcast_select_fusion
  51.4 1.3 %collective-permute-start.10 = (bf16[2,15,384]{2,1,0:T(8,128)(2,1)S(1)}, bf16[2,15,384]{2,1,0:T(8,128)(2,1)S(1)}, u32[]{:S(2)}, u32[]{:S(2)}) collective-permute-start(bf16[2,15,384]{2,1,0:T(8,128)(2,1)S(1)} %get-tuple-element.17), channel_id=1, source_target_pairs={{0,4},{4,8},{8,12},{1,5},{5,9},{9,13},{2,6},{6,10},{10,14},{3,7},{... | collective-permute-start | bytes 69128 | tf_op jit(solution)/shard_map/ppermute | solution.py:20
  52.7 1.3 %collective-permute-start.11 = (bf16[2,15,384]{2,1,0:T(8,128)(2,1)S(1)}, bf16[2,15,384]{2,1,0:T(8,128)(2,1)S(1)}, u32[]{:S(2)}, u32[]{:S(2)}) collective-permute-start(bf16[2,15,384]{2,1,0:T(8,128)(2,1)S(1)} %get-tuple-element.18), channel_id=1, source_target_pairs={{4,0},{8,4},{12,8},{5,1},{9,5},{13,9},{6,2},{10,6},{14,10},{7,3},{... | collective-permute-start | bytes 69128 | tf_op jit(solution)/shard_map/ppermute | solution.py:21
  54.0 0.2 collective-permute-done.10
  54.2 4.2 %collective-permute-done.11 = bf16[2,15,384]{2,1,0:T(8,128)(2,1)S(1)} collective-permute-done((bf16[2,15,384]{2,1,0:T(8,128)(2,1)S(1)}, bf16[2,15,384]{2,1,0:T(8,128)(2,1)S(1)}, u32[]{:S(2)}, u32[]{:S(2)}) %collective-permute-start.11) | collective-permute-done | bytes 23072 | tf_op jit(solution)/shard_map/ppermute | solution.py:21
  58.5 1.1 %fusion.46 = f32[2,128,384]{2,0,1:T(2,128)S(1)} fusion(bf16[2,158,384]{2,1,0:T(8,128)(2,1)S(1)} %pad_maximum_fusion.1, f32[31,1,384]{2,0,1:T(8,128)S(1)} %bitcast.139), kind=kOutput, calls=%fused_computation.64 | convolution fusion | flops 36569088 | bytes 683520 | tf_op jit(solution)/shard_map/conv_general_dilated | solution.py:192
  59.6 0.2 copy-done.7
  59.8 0.6 convolution_convert_fusion.1
  60.5 0.1 collective-permute-start.12
  60.6 1.8 %collective-permute-done.12 = bf16[2,2,32,1536]{3,2,0,1:T(8,128)(2,1)} collective-permute-done((bf16[2,2,32,1536]{3,2,0,1:T(8,128)(2,1)S(1)}, bf16[2,2,32,1536]{3,2,0,1:T(8,128)(2,1)}, u32[]{:S(2)}, u32[]{:S(2)}) %collective-permute-start.12) | collective-permute-done | bytes 393248 | tf_op jit(solution)/shard_map/ppermute | solution.py:59
  62.4 1.1 %convert_add_fusion = f32[2,2,32,1536]{3,2,0,1:T(8,128)S(1)} fusion(bf16[2,2,32,1536]{3,2,0,1:T(8,128)(2,1)} %collective-permute-done.12, bf16[2,2,1,32,1536]{4,3,2,1,0:T(8,128)(2,1)S(1)} %get-tuple-element.9), kind=kLoop, calls=%fused_computation.29 | loop fusion | flops 589824 | bytes 1572864 | tf_op jit(solution)/shard_map/add | solution.py:60
  63.5 1.6 %collective-permute-start.13 = (bf16[2,32,1536]{2,1,0:T(8,128)(2,1)S(1)}, bf16[2,32,1536]{2,1,0:T(8,128)(2,1)S(1)}, u32[]{:S(2)}, u32[]{:S(2)}) collective-permute-start(bf16[2,32,1536]{2,1,0:T(8,128)(2,1)S(1)} %fusion.49), channel_id=1, source_target_pairs={{0,2},{1,3},{2,0},{3,1},{4,6},{5,7},{6,4},{7,5},{8,10},{9,11},{10,... | collective-permute-start | bytes 589832 | tf_op jit(solution)/shard_map/ppermute | solution.py:59
  65.1 0.1 broadcast_compare_fusion.2
  65.1 5.4 %collective-permute-done.13 = bf16[2,32,1536]{2,1,0:T(8,128)(2,1)S(1)} collective-permute-done((bf16[2,32,1536]{2,1,0:T(8,128)(2,1)S(1)}, bf16[2,32,1536]{2,1,0:T(8,128)(2,1)S(1)}, u32[]{:S(2)}, u32[]{:S(2)}) %collective-permute-start.13) | collective-permute-done | bytes 196640 | tf_op jit(solution)/shard_map/ppermute | solution.py:59
  70.5 0.8 %fusion.42 = bf16[2,32,1536]{2,1,0:T(8,128)(2,1)} fusion(f32[2,32,1536]{2,1,0:T(8,128)S(1)} %get-tuple-element.8, bf16[2,32,1536]{2,1,0:T(8,128)(2,1)S(1)} %collective-permute-done.13, f32[2,2,32,1536]{3,2,0,1:T(8,128)S(1)} %convert_add_fusion, s32[]{:T(128)S(6)} %select_n.108, bf16[1536]{0:T(1024)(128)(2,1)S(1)} %get-tuple-element.23, ...), kind=kLoop, calls=%fused_computation.50 | loop fusion | flops 884736 | bytes 1185860 | tf_op jit(solution)/shard_map/convert_element_type | solution.py:209
  (59 shorter events, 1.0 us)
Async XLA Ops:
  0.0 3.0 %copy-start = (bf16[3,1536,256]{2,1,0:T(8,128)(2,1)S(1)}, bf16[3,1536,256]{2,1,0:T(8,128)(2,1)}, u32[]{:S(2)}) copy-start(bf16[3,1536,256]{2,1,0:T(8,128)(2,1)} %param.15) | copy-start | bytes 7077892
  3.0 9.3 %copy-start.5 = (s32[2]{0:T(128)S(1)}, s32[2]{0:T(128)}, u32[]{:S(2)}) copy-start(s32[2]{0:T(128)} %param.13) | copy-start | bytes 28
  5.3 8.8 %collective-permute-start = (bf16[3,2,128,1,64]{2,4,1,3,0:T(8,128)(2,1)S(1)}, bf16[3,2,128,1,64]{2,4,1,3,0:T(8,128)(2,1)S(1)}, u32[]{:S(2)}, u32[]{:S(2)}) collective-permute-start(bf16[3,2,128,1,64]{2,4,1,3,0:T(8,128)(2,1)S(1)} %get-tuple-element.16), channel_id=1, source_target_pairs={{0,4},{4,8},{8,12},{12,0},{1,5},{5,9},{9,13},{13,1},{2,6},{6,10},{... | collective-permute-start | bytes 294920 | tf_op jit(solution)/shard_map/ppermute | solution.py:124
  8.4 9.2 %collective-permute-start.1 = (bf16[3,2,128,1,64]{2,4,1,3,0:T(8,128)(2,1)S(1)}, bf16[3,2,128,1,64]{2,4,1,3,0:T(8,128)(2,1)S(1)}, u32[]{:S(2)}, u32[]{:S(2)}) collective-permute-start(bf16[3,2,128,1,64]{2,4,1,3,0:T(8,128)(2,1)S(1)} %get-tuple-element.15), channel_id=1, source_target_pairs={{0,8},{4,12},{8,0},{12,4},{1,9},{5,13},{9,1},{13,5},{2,10},{6,14},... | collective-permute-start | bytes 294920 | tf_op jit(solution)/shard_map/ppermute | solution.py:124
  10.9 6.6 %collective-permute-start.2 = (bf16[3,2,128,1,64]{2,4,1,3,0:T(8,128)(2,1)S(1)}, bf16[3,2,128,1,64]{2,4,1,3,0:T(8,128)(2,1)S(1)}, u32[]{:S(2)}, u32[]{:S(2)}) collective-permute-start(bf16[3,2,128,1,64]{2,4,1,3,0:T(8,128)(2,1)S(1)} %get-tuple-element.14), channel_id=1, source_target_pairs={{0,12},{4,0},{8,4},{12,8},{1,13},{5,1},{9,5},{13,9},{2,14},{6,2},{... | collective-permute-start | bytes 294920 | tf_op jit(solution)/shard_map/ppermute | solution.py:124
  18.9 10.6 %copy-start.1 = (bf16[256,1536]{1,0:T(8,128)(2,1)S(1)}, bf16[256,1536]{1,0:T(8,128)(2,1)}, u32[]{:S(2)}) copy-start(bf16[256,1536]{1,0:T(8,128)(2,1)} %param.16) | copy-start | bytes 2359300
  19.6 5.2 %collective-permute-start.3 = (bf16[2,1,128,64]{2,3,0,1:T(8,128)(2,1)S(1)}, bf16[2,1,128,64]{2,3,0,1:T(8,128)(2,1)S(1)}, u32[]{:S(2)}, u32[]{:S(2)}) collective-permute-start(bf16[2,1,128,64]{2,3,0,1:T(8,128)(2,1)S(1)} %get-tuple-element.21), channel_id=1, source_target_pairs={{0,12},{4,0},{8,4},{12,8},{1,13},{5,1},{9,5},{13,9},{2,14},{6,2},{... | collective-permute-start | bytes 98312 | tf_op jit(solution)/shard_map/ppermute | solution.py:134
  23.3 5.0 %collective-permute-start.4 = (bf16[2,1,128,64]{2,3,0,1:T(8,128)(2,1)S(1)}, bf16[2,1,128,64]{2,3,0,1:T(8,128)(2,1)S(1)}, u32[]{:S(2)}, u32[]{:S(2)}) collective-permute-start(bf16[2,1,128,64]{2,3,0,1:T(8,128)(2,1)S(1)} %get-tuple-element.20), channel_id=1, source_target_pairs={{0,8},{4,12},{8,0},{12,4},{1,9},{5,13},{9,1},{13,5},{2,10},{6,14},... | collective-permute-start | bytes 98312 | tf_op jit(solution)/shard_map/ppermute | solution.py:134
  23.7 5.7 %collective-permute-start.5 = (bf16[2,1,128,64]{2,3,0,1:T(8,128)(2,1)S(1)}, bf16[2,1,128,64]{2,3,0,1:T(8,128)(2,1)S(1)}, u32[]{:S(2)}, u32[]{:S(2)}) collective-permute-start(bf16[2,1,128,64]{2,3,0,1:T(8,128)(2,1)S(1)} %get-tuple-element.19), channel_id=1, source_target_pairs={{0,4},{4,8},{8,12},{12,0},{1,5},{5,9},{9,13},{13,1},{2,6},{6,10},{... | collective-permute-start | bytes 98312 | tf_op jit(solution)/shard_map/ppermute | solution.py:134
  30.0 12.2 %copy-start.3 = (f32[1536]{0:T(1024)S(1)}, f32[1536]{0:T(1024)}, u32[]{:S(2)}) copy-start(f32[1536]{0:T(1024)} %param.17) | copy-start | bytes 18436
  30.0 1.8 %collective-permute-start.6 = (bf16[2,2,32,1536]{3,2,0,1:T(8,128)(2,1)S(1)}, bf16[2,2,32,1536]{3,2,0,1:T(8,128)(2,1)S(1)}, u32[]{:S(2)}, u32[]{:S(2)}) collective-permute-start(bf16[2,2,32,1536]{3,2,0,1:T(8,128)(2,1)S(1)} %bitcast.137), channel_id=1, source_target_pairs={{0,1},{1,0},{2,3},{3,2},{4,5},{5,4},{6,7},{7,6},{8,9},{9,8},{10,11... | collective-permute-start | bytes 1179656 | tf_op jit(solution)/shard_map/ppermute | solution.py:59
  31.8 0.8 %copy-start.2 = (bf16[2,2,32,1536]{3,2,0,1:T(8,128)(2,1)}, bf16[2,2,32,1536]{3,2,0,1:T(8,128)(2,1)S(1)}, u32[]{:S(2)}) copy-start(bf16[2,2,32,1536]{3,2,0,1:T(8,128)(2,1)S(1)} %collective-permute-done.6) | copy-start | bytes 1179652
  33.7 7.1 %collective-permute-start.7 = (bf16[2,32,1536]{2,1,0:T(8,128)(2,1)S(1)}, bf16[2,32,1536]{2,1,0:T(8,128)(2,1)}, u32[]{:S(2)}, u32[]{:S(2)}) collective-permute-start(bf16[2,32,1536]{2,1,0:T(8,128)(2,1)S(1)} %fusion.48), channel_id=1, source_target_pairs={{0,2},{1,3},{2,0},{3,1},{4,6},{5,7},{6,4},{7,5},{8,10},{9,11},{10,... | collective-permute-start | bytes 589832 | tf_op jit(solution)/shard_map/ppermute | solution.py:59
  42.0 8.4 %copy-start.6 = (bf16[2,1536,384]{2,1,0:T(8,128)(2,1)S(1)}, bf16[2,1536,384]{2,1,0:T(8,128)(2,1)}, u32[]{:S(2)}) copy-start(bf16[2,1536,384]{2,1,0:T(8,128)(2,1)} %param.18) | copy-start | bytes 7077892
  42.4 6.2 %collective-permute-start.8 = (bf16[2,32,1536]{2,1,0:T(8,128)(2,1)S(1)}, bf16[2,32,1536]{2,1,0:T(8,128)(2,1)S(1)}, u32[]{:S(2)}, u32[]{:S(2)}) collective-permute-start(bf16[2,32,1536]{2,1,0:T(8,128)(2,1)S(1)} %get-tuple-element.6), channel_id=1, source_target_pairs={{0,2},{1,3},{2,0},{3,1},{4,6},{5,7},{6,4},{7,5},{8,10},{9,11},{10,... | collective-permute-start | bytes 589832 | tf_op jit(solution)/shard_map/ppermute | solution.py:71
  48.6 1.8 %collective-permute-start.9 = (bf16[2,2,32,1536]{3,2,1,0:T(8,128)(2,1)S(1)}, bf16[2,2,32,1536]{3,2,1,0:T(8,128)(2,1)S(1)}, u32[]{:S(2)}, u32[]{:S(2)}) collective-permute-start(bf16[2,2,32,1536]{3,2,1,0:T(8,128)(2,1)S(1)} %bitcast_dynamic-update-slice_fusion.3), channel_id=1, source_target_pairs={{0,1},{1,0},{2,3},{3,2},{4,5},{5,4},{6,7},{7,6},{8,9},{9,8},{10,11... | collective-permute-start | bytes 1179656 | tf_op jit(solution)/shard_map/ppermute | solution.py:71
  50.4 8.1 %copy-start.8 = (f32[31,384]{1,0:T(8,128)S(1)}, f32[31,384]{1,0:T(8,128)}, u32[]{:S(2)}) copy-start(f32[31,384]{1,0:T(8,128)} %param.19) | copy-start | bytes 142852
  51.4 2.8 %collective-permute-start.10 = (bf16[2,15,384]{2,1,0:T(8,128)(2,1)S(1)}, bf16[2,15,384]{2,1,0:T(8,128)(2,1)S(1)}, u32[]{:S(2)}, u32[]{:S(2)}) collective-permute-start(bf16[2,15,384]{2,1,0:T(8,128)(2,1)S(1)} %get-tuple-element.17), channel_id=1, source_target_pairs={{0,4},{4,8},{8,12},{1,5},{5,9},{9,13},{2,6},{6,10},{10,14},{3,7},{... | collective-permute-start | bytes 69128 | tf_op jit(solution)/shard_map/ppermute | solution.py:20
  52.7 5.7 %collective-permute-start.11 = (bf16[2,15,384]{2,1,0:T(8,128)(2,1)S(1)}, bf16[2,15,384]{2,1,0:T(8,128)(2,1)S(1)}, u32[]{:S(2)}, u32[]{:S(2)}) collective-permute-start(bf16[2,15,384]{2,1,0:T(8,128)(2,1)S(1)} %get-tuple-element.18), channel_id=1, source_target_pairs={{4,0},{8,4},{12,8},{5,1},{9,5},{13,9},{6,2},{10,6},{14,10},{7,3},{... | collective-permute-start | bytes 69128 | tf_op jit(solution)/shard_map/ppermute | solution.py:21
  58.5 1.3 %copy-start.7 = (bf16[384,1536]{1,0:T(8,128)(2,1)S(1)}, bf16[384,1536]{1,0:T(8,128)(2,1)}, u32[]{:S(2)}) copy-start(bf16[384,1536]{1,0:T(8,128)(2,1)} %param.22) | copy-start | bytes 3538948
  58.5 1.3 %copy-start.9 = (f32[384]{0:T(512)S(1)}, f32[384]{0:T(512)}, u32[]{:S(2)}) copy-start(f32[384]{0:T(512)} %param.21) | copy-start | bytes 4612
  58.5 1.3 %copy-start.10 = (f32[384]{0:T(512)S(1)}, f32[384]{0:T(512)}, u32[]{:S(2)}) copy-start(f32[384]{0:T(512)} %param.20) | copy-start | bytes 4612
  59.8 0.8 %copy-start.4 = (s32[1536]{0:T(1024)S(1)}, s32[1536]{0:T(1024)}, u32[]{:S(2)}) copy-start(s32[1536]{0:T(1024)} %param.23) | copy-start | bytes 18436
  60.5 1.9 %collective-permute-start.12 = (bf16[2,2,32,1536]{3,2,0,1:T(8,128)(2,1)S(1)}, bf16[2,2,32,1536]{3,2,0,1:T(8,128)(2,1)}, u32[]{:S(2)}, u32[]{:S(2)}) collective-permute-start(bf16[2,2,32,1536]{3,2,0,1:T(8,128)(2,1)S(1)} %bitcast.138), channel_id=1, source_target_pairs={{0,1},{1,0},{2,3},{3,2},{4,5},{5,4},{6,7},{7,6},{8,9},{9,8},{10,11... | collective-permute-start | bytes 1179656 | tf_op jit(solution)/shard_map/ppermute | solution.py:59
  63.5 7.0 %collective-permute-start.13 = (bf16[2,32,1536]{2,1,0:T(8,128)(2,1)S(1)}, bf16[2,32,1536]{2,1,0:T(8,128)(2,1)S(1)}, u32[]{:S(2)}, u32[]{:S(2)}) collective-permute-start(bf16[2,32,1536]{2,1,0:T(8,128)(2,1)S(1)} %fusion.49), channel_id=1, source_target_pairs={{0,2},{1,3},{2,0},{3,1},{4,6},{5,7},{6,4},{7,5},{8,10},{9,11},{10,... | collective-permute-start | bytes 589832 | tf_op jit(solution)/shard_map/ppermute | solution.py:59

commit v10 on v9

--- a/solution.py
+++ b/solution.py
@@ -127,13 +127,28 @@
     frame_steps = jnp.arange(frames, dtype=jnp.int32)
     positions = jnp.concatenate([source * frames + frame_steps for source in sources])
     attended = attend(every[0], every[1], every[2], positions, frame_counts)
-    back = [attended[:, :, :frames]]
-    for shift in range(1, count):
-        rows = attended[:, :, shift * frames : (shift + 1) * frames]
-        pairs = [(i, (i - shift) % count) for i in range(count)]
-        back.append(lax.ppermute(rows, axis, pairs))
-    ordered = jnp.roll(jnp.stack(back, axis=1), rank, axis=1)
-    return ordered.transpose(0, 3, 1, 2, 4).reshape(records, frames, width)
+    blocks = attended.reshape(records, group, count, frames, HEAD_DIM)
+    natural = (rank - jnp.arange(count, dtype=jnp.int32)) % count
+    return swap_blocks(jnp.take(blocks, natural, axis=2), axis).reshape(records, frames, width)
+
+
+def swap_blocks(chunks, axis):
+    count, rank = lax.axis_size(axis), lax.axis_index(axis)
+    bits = bit_count(count)
+    records, group, _, frames, depth = chunks.shape
+    held = chunks.reshape((records, group) + (2,) * bits + (1, frames, depth))
+    for b in range(bits):
+        mine = (rank >> b) & 1
+        dest_axis = 2 + bits - 1 - b
+        keep = lax.dynamic_index_in_dim(held, mine, dest_axis, keepdims=False)
+        send = lax.dynamic_index_in_dim(held, 1 - mine, dest_axis, keepdims=False)
+        got = lax.ppermute(send, axis, xor_pairs(count, 1 << b))
+        src_axis = 2 + bits - 1 - b
+        both = jnp.zeros(keep.shape[:src_axis] + (2,) + keep.shape[src_axis:], keep.dtype)
+        both = lax.dynamic_update_index_in_dim(both, keep, mine, src_axis)
+        held = lax.dynamic_update_index_in_dim(both, got, 1 - mine, src_axis)
+    held = held.reshape(records, group, count, frames, depth)
+    return held.transpose(0, 3, 2, 1, 4)
 
 
 def shards(

time: 71.6 us -> 72.9 us (1.018)
  starting transfers between devices: 18.8 us -> 22 us
  waiting for transfers between devices: 35.6 us -> 32.9 us
    ppermute x1, waiting for transfers between devices: 4.22 us -> 0.01 us  [with_halo(): after = lax.ppermute(initial, axis, down)]
    ppermute x1, starting transfers between devices: 1.29 us -> 4.55 us  [with_halo(): before = lax.ppermute(last, axis, up)]
    ppermute x1, waiting for transfers between devices: 0.2 us -> 1.49 us  [with_halo(): before = lax.ppermute(last, axis, up)]
    ppermute x3 -> x2, waiting for transfers between devices: 5.44 us -> 5.77 us  [swap_blocks(): got = lax.ppermute(send, axis, xor_pairs(count, 1 << b))]
    ppermute x3 -> x2, starting transfers between devices: 4.3 us -> 4.26 us  [swap_blocks(): got = lax.ppermute(send, axis, xor_pairs(count, 1 << b))]
  transfers between devices with their start and end apart: 14 -> 13, of which waited for: 13 -> 11; matrix products, arithmetic and copies ran while one was open for 1% -> 1% of each run, Pallas kernels for 0% -> 0%
where the time goes in v10:
time: 72.9 us; the launch traced here: 72.6 us
  waiting for transfers between devices  32.9 us (45%)
  starting transfers between devices  22 us (30%)
  other arithmetic  8.54 us (12%)
  matrix products  6.25 us (9%)
  local copies, waits for them, and re-layouts  2.39 us (3%)
    ppermute x4, waiting for transfers between devices, reduce_scatter_rows(): lax.ppermute(send.astype(jnp.bfloat16), axis, xor_pairs(count, 1 << b))  14.4 us
    ppermute x3, starting transfers between devices, attend_by_heads(): pieces.append(lax.ppermute(send, axis, pairs))  7.01 us
    ppermute x2, waiting for transfers between devices, all_gather_rows(): got = lax.ppermute(acc, axis, xor_pairs(count, 1 << b))  6.15 us
    ppermute x2, waiting for transfers between devices, swap_blocks(): got = lax.ppermute(send, axis, xor_pairs(count, 1 << b))  5.77 us
    ppermute x3, waiting for transfers between devices, attend_by_heads(): pieces.append(lax.ppermute(send, axis, pairs))  5.05 us
    ppermute x1, starting transfers between devices, with_halo(): before = lax.ppermute(last, axis, up)  4.55 us
    ppermute x2, starting transfers between devices, swap_blocks(): got = lax.ppermute(send, axis, xor_pairs(count, 1 << b))  4.26 us
    ppermute x4, starting transfers between devices, reduce_scatter_rows(): lax.ppermute(send.astype(jnp.bfloat16), axis, xor_pairs(count, 1 << b))  3.25 us
  transfers between devices with their start and end apart: 13, of which 11 were waited for; matrix products, arithmetic and copies ran while one was open for 1% of the time, Pallas kernels for 0%

profile of v10, /device:TPU:0, one launch (start us, length us, event | category | flops | bytes accessed | tf_op | source)
XLA Modules:
  0.0 72.6 jit_solution(16942187464313231833)
XLA Ops:
  0.0 1.5 %convert_reduce_fusion = f32[2,128]{1,0:T(2,128)S(1)} fusion(bf16[2,128,1536]{2,1,0:T(8,128)(2,1)} %param.12), kind=kLoop, calls=%fused_computation.10 | loop fusion | flops 786176 | bytes 787456 | tf_op jit(solution)/shard_map/reduce_sum | solution.py:27
  1.5 1.5 %fusion.9 = f32[2,128]{1,0:T(2,128)S(1)} fusion(bf16[2,128,1536]{2,1,0:T(8,128)(2,1)} %param.12, f32[2,128]{1,0:T(2,128)S(1)} %broadcast_multiply_fusion.1), kind=kLoop, calls=%fused_computation.16 | loop fusion | flops 1572608 | bytes 788480 | tf_op jit(solution)/shard_map/reduce_sum | solution.py:29
  3.0 2.0 %fusion.18 = bf16[3,2,128,256]{3,2,0,1:T(8,128)(2,1)S(1)} fusion(bf16[3,1536,256]{2,1,0:T(8,128)(2,1)S(1)} %copy-done, bf16[2,128,1536]{2,1,0:T(8,128)(2,1)} %param.12, f32[1536]{0:T(1024)} %param.14, f32[2,128]{1,0:T(2,128)S(1)} %add_rsqrt_fusion.1, f32[2,128]{1,0:T(2,128)S(1)} %broadcast_multiply_fusion.1), kind=kOutput, calls=%fused_computation.21 | convolution fusion | flops 606142464 | bytes 3547136 | tf_op jit(solution)/shard_map/std,idc->istc/dot_general | solution.py:175
  5.0 0.2 copy.45
  5.3 3.1 %collective-permute-start = (bf16[3,2,128,1,64]{2,4,1,3,0:T(8,128)(2,1)S(1)}, bf16[3,2,128,1,64]{2,4,1,3,0:T(8,128)(2,1)S(1)}, u32[]{:S(2)}, u32[]{:S(2)}) collective-permute-start(bf16[3,2,128,1,64]{2,4,1,3,0:T(8,128)(2,1)S(1)} %get-tuple-element.16), channel_id=1, source_target_pairs={{0,4},{4,8},{8,12},{12,0},{1,5},{5,9},{9,13},{13,1},{2,6},{6,10},{... | collective-permute-start | bytes 294920 | tf_op jit(solution)/shard_map/ppermute | solution.py:124
  8.4 2.6 %collective-permute-start.1 = (bf16[3,2,128,1,64]{2,4,1,3,0:T(8,128)(2,1)S(1)}, bf16[3,2,128,1,64]{2,4,1,3,0:T(8,128)(2,1)S(1)}, u32[]{:S(2)}, u32[]{:S(2)}) collective-permute-start(bf16[3,2,128,1,64]{2,4,1,3,0:T(8,128)(2,1)S(1)} %get-tuple-element.15), channel_id=1, source_target_pairs={{0,8},{4,12},{8,0},{12,4},{1,9},{5,13},{9,1},{13,5},{2,10},{6,14},... | collective-permute-start | bytes 294920 | tf_op jit(solution)/shard_map/ppermute | solution.py:124
  10.9 1.3 %collective-permute-start.2 = (bf16[3,2,128,1,64]{2,4,1,3,0:T(8,128)(2,1)S(1)}, bf16[3,2,128,1,64]{2,4,1,3,0:T(8,128)(2,1)S(1)}, u32[]{:S(2)}, u32[]{:S(2)}) collective-permute-start(bf16[3,2,128,1,64]{2,4,1,3,0:T(8,128)(2,1)S(1)} %get-tuple-element.14), channel_id=1, source_target_pairs={{0,12},{4,0},{8,4},{12,8},{1,13},{5,1},{9,5},{13,9},{2,14},{6,2},{... | collective-permute-start | bytes 294920 | tf_op jit(solution)/shard_map/ppermute | solution.py:124
  12.4 0.1 broadcast_compare_fusion
  12.5 1.5 %collective-permute-done = bf16[3,2,128,1,64]{2,4,1,3,0:T(8,128)(2,1)S(1)} collective-permute-done((bf16[3,2,128,1,64]{2,4,1,3,0:T(8,128)(2,1)S(1)}, bf16[3,2,128,1,64]{2,4,1,3,0:T(8,128)(2,1)S(1)}, u32[]{:S(2)}, u32[]{:S(2)}) %collective-permute-start) | collective-permute-done | bytes 98336 | tf_op jit(solution)/shard_map/ppermute | solution.py:124
  14.0 3.5 %collective-permute-done.1 = bf16[3,2,128,1,64]{2,4,1,3,0:T(8,128)(2,1)S(1)} collective-permute-done((bf16[3,2,128,1,64]{2,4,1,3,0:T(8,128)(2,1)S(1)}, bf16[3,2,128,1,64]{2,4,1,3,0:T(8,128)(2,1)S(1)}, u32[]{:S(2)}, u32[]{:S(2)}) %collective-permute-start.1) | collective-permute-done | bytes 98336 | tf_op jit(solution)/shard_map/ppermute | solution.py:124
  17.6 0.8 %fusion.6 = (f32[2,512]{1,0:T(2,128)S(1)}, f32[2,512,512]{1,2,0:T(8,128)S(1)}) fusion(pred[2,512]{1,0:T(4,128)(4,1)S(1)} %broadcast_compare_fusion, bf16[3,2,512,1,64]{2,4,1,3,0:T(8,128)(2,1)S(1)} %pad_maximum_fusion), kind=kOutput, calls=%fused_computation.13 | convolution fusion | flops 68680704 | bytes 2365440 | tf_op jit(solution)/shard_map/sqhe,skhe->shqk/dot_general | solution.py:96
  18.4 0.5 fusion.7
  18.9 0.6 fusion.23
  19.6 0.6 gather_fusion
  20.2 0.1 copy_select_fusion
  20.3 2.6 %collective-permute-start.3 = (bf16[2,1,2,1,128,64]{4,5,3,2,1,0:T(8,128)(2,1)S(1)}, bf16[2,1,2,1,128,64]{4,5,3,2,1,0:T(8,128)(2,1)S(1)}, u32[]{:S(2)}, u32[]{:S(2)}) collective-permute-start(bf16[2,1,2,1,128,64]{4,5,3,2,1,0:T(8,128)(2,1)S(1)} %dynamic-slice_bitcast_fusion.5), channel_id=1, source_target_pairs={{0,4},{4,0},{8,12},{12,8},{1,5},{5,1},{9,13},{13,9},{2,6},{6,2},{1... | collective-permute-start | bytes 196616 | tf_op jit(solution)/shard_map/ppermute | solution.py:145
  22.9 2.2 %collective-permute-done.3 = bf16[2,1,2,1,128,64]{4,5,3,2,1,0:T(8,128)(2,1)S(1)} collective-permute-done((bf16[2,1,2,1,128,64]{4,5,3,2,1,0:T(8,128)(2,1)S(1)}, bf16[2,1,2,1,128,64]{4,5,3,2,1,0:T(8,128)(2,1)S(1)}, u32[]{:S(2)}, u32[]{:S(2)}) %collective-permute-start.3) | collective-permute-done | bytes 65568 | tf_op jit(solution)/shard_map/ppermute | solution.py:145
  25.2 1.7 %collective-permute-start.4 = (bf16[2,1,2,1,128,64]{4,5,2,0,3,1:T(8,128)(2,1)S(1)}, bf16[2,1,2,1,128,64]{4,5,2,0,3,1:T(8,128)(2,1)S(1)}, u32[]{:S(2)}, u32[]{:S(2)}) collective-permute-start(bf16[2,1,2,1,128,64]{4,5,2,0,3,1:T(8,128)(2,1)S(1)} %dynamic-slice_bitcast_fusion.4), channel_id=1, source_target_pairs={{0,8},{4,12},{8,0},{12,4},{1,9},{5,13},{9,1},{13,5},{2,10},{6,14},... | collective-permute-start | bytes 196616 | tf_op jit(solution)/shard_map/ppermute | solution.py:145
  26.9 3.5 %collective-permute-done.4 = bf16[2,1,2,1,128,64]{4,5,2,0,3,1:T(8,128)(2,1)S(1)} collective-permute-done((bf16[2,1,2,1,128,64]{4,5,2,0,3,1:T(8,128)(2,1)S(1)}, bf16[2,1,2,1,128,64]{4,5,2,0,3,1:T(8,128)(2,1)S(1)}, u32[]{:S(2)}, u32[]{:S(2)}) %collective-permute-start.4) | collective-permute-done | bytes 65568 | tf_op jit(solution)/shard_map/ppermute | solution.py:145
  30.5 0.4 convolution_convert_fusion
  31.0 0.1 collective-permute-start.5
  31.1 1.7 %collective-permute-done.5 = bf16[2,2,32,1536]{3,2,0,1:T(8,128)(2,1)S(1)} collective-permute-done((bf16[2,2,32,1536]{3,2,0,1:T(8,128)(2,1)S(1)}, bf16[2,2,32,1536]{3,2,0,1:T(8,128)(2,1)S(1)}, u32[]{:S(2)}, u32[]{:S(2)}) %collective-permute-start.5) | collective-permute-done | bytes 393248 | tf_op jit(solution)/shard_map/ppermute | solution.py:59
  32.8 0.7 %copy-done.2 = bf16[2,2,32,1536]{3,2,0,1:T(8,128)(2,1)} copy-done((bf16[2,2,32,1536]{3,2,0,1:T(8,128)(2,1)}, bf16[2,2,32,1536]{3,2,0,1:T(8,128)(2,1)S(1)}, u32[]{:S(2)}) %copy-start.2) | copy-done | bytes 393240
  33.5 1.1 %convert_add_fusion.1 = f32[2,2,32,1536]{3,2,0,1:T(8,128)S(1)} fusion(bf16[2,2,32,1536]{3,2,0,1:T(8,128)(2,1)} %copy-done.2, bf16[2,2,1,32,1536]{4,3,2,1,0:T(8,128)(2,1)S(1)} %get-tuple-element.11), kind=kLoop, calls=%fused_computation.31 | loop fusion | flops 589824 | bytes 1572864 | tf_op jit(solution)/shard_map/add | solution.py:60
  34.7 1.6 %collective-permute-start.6 = (bf16[2,32,1536]{2,1,0:T(8,128)(2,1)S(1)}, bf16[2,32,1536]{2,1,0:T(8,128)(2,1)}, u32[]{:S(2)}, u32[]{:S(2)}) collective-permute-start(bf16[2,32,1536]{2,1,0:T(8,128)(2,1)S(1)} %fusion.48), channel_id=1, source_target_pairs={{0,2},{1,3},{2,0},{3,1},{4,6},{5,7},{6,4},{7,5},{8,10},{9,11},{10,... | collective-permute-start | bytes 589832 | tf_op jit(solution)/shard_map/ppermute | solution.py:59
  36.2 5.6 %collective-permute-done.6 = bf16[2,32,1536]{2,1,0:T(8,128)(2,1)} collective-permute-done((bf16[2,32,1536]{2,1,0:T(8,128)(2,1)S(1)}, bf16[2,32,1536]{2,1,0:T(8,128)(2,1)}, u32[]{:S(2)}, u32[]{:S(2)}) %collective-permute-start.6) | collective-permute-done | bytes 196640 | tf_op jit(solution)/shard_map/ppermute | solution.py:59
  41.8 1.2 %fusion.62 = (f32[2,32]{1,0:T(2,128)S(1)}, f32[2,32,1536]{2,1,0:T(8,128)S(1)}) fusion(bf16[2,32,1536]{2,1,0:T(8,128)(2,1)} %collective-permute-done.6, f32[2,2,32,1536]{3,2,0,1:T(8,128)S(1)} %convert_add_fusion.1, s32[]{:T(128)S(6)} %select_n.171, bf16[2,128,1536]{2,1,0:T(8,128)(2,1)} %param.12, s32[]{:T(128)S(6)} %select_n.148), kind=kLoop, calls=%fused_computation.127 | loop fusion | flops 491456 | bytes 1179912 | tf_op jit(solution)/shard_map/reduce_sum | solution.py:27
  43.0 0.2 multiply_reduce_fusion
  43.2 0.1 bitcast_dynamic-update-slice_fusion.2
  43.4 1.6 %collective-permute-start.7 = (bf16[2,32,1536]{2,1,0:T(8,128)(2,1)S(1)}, bf16[2,32,1536]{2,1,0:T(8,128)(2,1)S(1)}, u32[]{:S(2)}, u32[]{:S(2)}) collective-permute-start(bf16[2,32,1536]{2,1,0:T(8,128)(2,1)S(1)} %get-tuple-element.6), channel_id=1, source_target_pairs={{0,2},{1,3},{2,0},{3,1},{4,6},{5,7},{6,4},{7,5},{8,10},{9,11},{10,... | collective-permute-start | bytes 589832 | tf_op jit(solution)/shard_map/ppermute | solution.py:71
  44.9 0.1 broadcast_compare_fusion.1
  45.0 4.6 %collective-permute-done.7 = bf16[2,32,1536]{2,1,0:T(8,128)(2,1)S(1)} collective-permute-done((bf16[2,32,1536]{2,1,0:T(8,128)(2,1)S(1)}, bf16[2,32,1536]{2,1,0:T(8,128)(2,1)S(1)}, u32[]{:S(2)}, u32[]{:S(2)}) %collective-permute-start.7) | collective-permute-done | bytes 196640 | tf_op jit(solution)/shard_map/ppermute | solution.py:71
  49.7 1.6 %collective-permute-done.8 = bf16[2,2,32,1536]{3,2,1,0:T(8,128)(2,1)S(1)} collective-permute-done((bf16[2,2,32,1536]{3,2,1,0:T(8,128)(2,1)S(1)}, bf16[2,2,32,1536]{3,2,1,0:T(8,128)(2,1)S(1)}, u32[]{:S(2)}, u32[]{:S(2)}) %collective-permute-start.8) | collective-permute-done | bytes 393248 | tf_op jit(solution)/shard_map/ppermute | solution.py:71
  51.4 0.8 %fusion.12 = f32[2,2,128,384]{3,2,0,1:T(8,128)S(1)} fusion(bf16[2,128,1536,1]{2,1,3,0:T(8,128)(2,1)S(1)} %bitcast.146, bf16[2,1536,384]{2,1,0:T(8,128)(2,1)S(1)} %copy-done.6), kind=kOutput, calls=%fused_computation.19 | convolution fusion | flops 603979776 | bytes 3932160 | tf_op jit(solution)/shard_map/std,gdc->gstc/dot_general | solution.py:34
  52.2 0.1 bitcast_select_fusion
  52.4 1.3 %collective-permute-start.10 = (bf16[2,15,384]{2,1,0:T(8,128)(2,1)S(1)}, bf16[2,15,384]{2,1,0:T(8,128)(2,1)S(1)}, u32[]{:S(2)}, u32[]{:S(2)}) collective-permute-start(bf16[2,15,384]{2,1,0:T(8,128)(2,1)S(1)} %get-tuple-element.18), channel_id=1, source_target_pairs={{4,0},{8,4},{12,8},{5,1},{9,5},{13,9},{6,2},{10,6},{14,10},{7,3},{... | collective-permute-start | bytes 69128 | tf_op jit(solution)/shard_map/ppermute | solution.py:21
  53.7 4.5 %collective-permute-start.9 = (bf16[2,15,384]{2,1,0:T(8,128)(2,1)S(1)}, bf16[2,15,384]{2,1,0:T(8,128)(2,1)S(1)}, u32[]{:S(2)}, u32[]{:S(2)}) collective-permute-start(bf16[2,15,384]{2,1,0:T(8,128)(2,1)S(1)} %get-tuple-element.17), channel_id=1, source_target_pairs={{0,4},{4,8},{8,12},{1,5},{5,9},{9,13},{2,6},{6,10},{10,14},{3,7},{... | collective-permute-start | bytes 69128 | tf_op jit(solution)/shard_map/ppermute | solution.py:20
  58.2 1.5 %collective-permute-done.9 = bf16[2,15,384]{2,1,0:T(8,128)(2,1)S(1)} collective-permute-done((bf16[2,15,384]{2,1,0:T(8,128)(2,1)S(1)}, bf16[2,15,384]{2,1,0:T(8,128)(2,1)S(1)}, u32[]{:S(2)}, u32[]{:S(2)}) %collective-permute-start.9) | collective-permute-done | bytes 23072 | tf_op jit(solution)/shard_map/ppermute | solution.py:20
  59.8 1.1 %fusion.46 = f32[2,128,384]{2,0,1:T(2,128)S(1)} fusion(bf16[2,158,384]{2,1,0:T(8,128)(2,1)S(1)} %pad_maximum_fusion.1, f32[31,1,384]{2,0,1:T(8,128)S(1)} %bitcast.152), kind=kOutput, calls=%fused_computation.65 | convolution fusion | flops 36569088 | bytes 683520 | tf_op jit(solution)/shard_map/conv_general_dilated | solution.py:207
  60.9 0.2 copy-done.7
  61.1 0.6 convolution_convert_fusion.1
  61.8 0.1 collective-permute-start.11
  61.9 1.8 %collective-permute-done.11 = bf16[2,2,32,1536]{3,2,0,1:T(8,128)(2,1)} collective-permute-done((bf16[2,2,32,1536]{3,2,0,1:T(8,128)(2,1)S(1)}, bf16[2,2,32,1536]{3,2,0,1:T(8,128)(2,1)}, u32[]{:S(2)}, u32[]{:S(2)}) %collective-permute-start.11) | collective-permute-done | bytes 393248 | tf_op jit(solution)/shard_map/ppermute | solution.py:59
  63.7 1.1 %convert_add_fusion = f32[2,2,32,1536]{3,2,0,1:T(8,128)S(1)} fusion(bf16[2,2,32,1536]{3,2,0,1:T(8,128)(2,1)} %collective-permute-done.11, bf16[2,2,1,32,1536]{4,3,2,1,0:T(8,128)(2,1)S(1)} %get-tuple-element.9), kind=kLoop, calls=%fused_computation.30 | loop fusion | flops 589824 | bytes 1572864 | tf_op jit(solution)/shard_map/add | solution.py:60
  64.8 1.6 %collective-permute-start.12 = (bf16[2,32,1536]{2,1,0:T(8,128)(2,1)S(1)}, bf16[2,32,1536]{2,1,0:T(8,128)(2,1)S(1)}, u32[]{:S(2)}, u32[]{:S(2)}) collective-permute-start(bf16[2,32,1536]{2,1,0:T(8,128)(2,1)S(1)} %fusion.49), channel_id=1, source_target_pairs={{0,2},{1,3},{2,0},{3,1},{4,6},{5,7},{6,4},{7,5},{8,10},{9,11},{10,... | collective-permute-start | bytes 589832 | tf_op jit(solution)/shard_map/ppermute | solution.py:59
  66.4 0.1 broadcast_compare_fusion.2
  66.5 5.4 %collective-permute-done.12 = bf16[2,32,1536]{2,1,0:T(8,128)(2,1)S(1)} collective-permute-done((bf16[2,32,1536]{2,1,0:T(8,128)(2,1)S(1)}, bf16[2,32,1536]{2,1,0:T(8,128)(2,1)S(1)}, u32[]{:S(2)}, u32[]{:S(2)}) %collective-permute-start.12) | collective-permute-done | bytes 196640 | tf_op jit(solution)/shard_map/ppermute | solution.py:59
  71.9 0.8 %fusion.42 = bf16[2,32,1536]{2,1,0:T(8,128)(2,1)} fusion(f32[2,32,1536]{2,1,0:T(8,128)S(1)} %get-tuple-element.8, bf16[2,32,1536]{2,1,0:T(8,128)(2,1)S(1)} %collective-permute-done.12, f32[2,2,32,1536]{3,2,0,1:T(8,128)S(1)} %convert_add_fusion, s32[]{:T(128)S(6)} %select_n.171, bf16[1536]{0:T(1024)(128)(2,1)S(1)} %get-tuple-element.20, ...), kind=kLoop, calls=%fused_computation.51 | loop fusion | flops 884736 | bytes 1185860 | tf_op jit(solution)/shard_map/convert_element_type | solution.py:224
  (60 shorter events, 1.0 us)
Async XLA Ops:
  0.0 3.0 %copy-start = (bf16[3,1536,256]{2,1,0:T(8,128)(2,1)S(1)}, bf16[3,1536,256]{2,1,0:T(8,128)(2,1)}, u32[]{:S(2)}) copy-start(bf16[3,1536,256]{2,1,0:T(8,128)(2,1)} %param.15) | copy-start | bytes 7077892
  3.0 9.4 %copy-start.5 = (s32[2]{0:T(128)S(1)}, s32[2]{0:T(128)}, u32[]{:S(2)}) copy-start(s32[2]{0:T(128)} %param.13) | copy-start | bytes 28
  5.3 8.8 %collective-permute-start = (bf16[3,2,128,1,64]{2,4,1,3,0:T(8,128)(2,1)S(1)}, bf16[3,2,128,1,64]{2,4,1,3,0:T(8,128)(2,1)S(1)}, u32[]{:S(2)}, u32[]{:S(2)}) collective-permute-start(bf16[3,2,128,1,64]{2,4,1,3,0:T(8,128)(2,1)S(1)} %get-tuple-element.16), channel_id=1, source_target_pairs={{0,4},{4,8},{8,12},{12,0},{1,5},{5,9},{9,13},{13,1},{2,6},{6,10},{... | collective-permute-start | bytes 294920 | tf_op jit(solution)/shard_map/ppermute | solution.py:124
  8.4 9.2 %collective-permute-start.1 = (bf16[3,2,128,1,64]{2,4,1,3,0:T(8,128)(2,1)S(1)}, bf16[3,2,128,1,64]{2,4,1,3,0:T(8,128)(2,1)S(1)}, u32[]{:S(2)}, u32[]{:S(2)}) collective-permute-start(bf16[3,2,128,1,64]{2,4,1,3,0:T(8,128)(2,1)S(1)} %get-tuple-element.15), channel_id=1, source_target_pairs={{0,8},{4,12},{8,0},{12,4},{1,9},{5,13},{9,1},{13,5},{2,10},{6,14},... | collective-permute-start | bytes 294920 | tf_op jit(solution)/shard_map/ppermute | solution.py:124
  10.9 6.6 %collective-permute-start.2 = (bf16[3,2,128,1,64]{2,4,1,3,0:T(8,128)(2,1)S(1)}, bf16[3,2,128,1,64]{2,4,1,3,0:T(8,128)(2,1)S(1)}, u32[]{:S(2)}, u32[]{:S(2)}) collective-permute-start(bf16[3,2,128,1,64]{2,4,1,3,0:T(8,128)(2,1)S(1)} %get-tuple-element.14), channel_id=1, source_target_pairs={{0,12},{4,0},{8,4},{12,8},{1,13},{5,1},{9,5},{13,9},{2,14},{6,2},{... | collective-permute-start | bytes 294920 | tf_op jit(solution)/shard_map/ppermute | solution.py:124
  18.9 11.6 %copy-start.1 = (bf16[256,1536]{1,0:T(8,128)(2,1)S(1)}, bf16[256,1536]{1,0:T(8,128)(2,1)}, u32[]{:S(2)}) copy-start(bf16[256,1536]{1,0:T(8,128)(2,1)} %param.16) | copy-start | bytes 2359300
  20.3 4.9 %collective-permute-start.3 = (bf16[2,1,2,1,128,64]{4,5,3,2,1,0:T(8,128)(2,1)S(1)}, bf16[2,1,2,1,128,64]{4,5,3,2,1,0:T(8,128)(2,1)S(1)}, u32[]{:S(2)}, u32[]{:S(2)}) collective-permute-start(bf16[2,1,2,1,128,64]{4,5,3,2,1,0:T(8,128)(2,1)S(1)} %dynamic-slice_bitcast_fusion.5), channel_id=1, source_target_pairs={{0,4},{4,0},{8,12},{12,8},{1,5},{5,1},{9,13},{13,9},{2,6},{6,2},{1... | collective-permute-start | bytes 196616 | tf_op jit(solution)/shard_map/ppermute | solution.py:145
  25.2 5.3 %collective-permute-start.4 = (bf16[2,1,2,1,128,64]{4,5,2,0,3,1:T(8,128)(2,1)S(1)}, bf16[2,1,2,1,128,64]{4,5,2,0,3,1:T(8,128)(2,1)S(1)}, u32[]{:S(2)}, u32[]{:S(2)}) collective-permute-start(bf16[2,1,2,1,128,64]{4,5,2,0,3,1:T(8,128)(2,1)S(1)} %dynamic-slice_bitcast_fusion.4), channel_id=1, source_target_pairs={{0,8},{4,12},{8,0},{12,4},{1,9},{5,13},{9,1},{13,5},{2,10},{6,14},... | collective-permute-start | bytes 196616 | tf_op jit(solution)/shard_map/ppermute | solution.py:145
  31.0 12.2 %copy-start.3 = (f32[1536]{0:T(1024)S(1)}, f32[1536]{0:T(1024)}, u32[]{:S(2)}) copy-start(f32[1536]{0:T(1024)} %param.17) | copy-start | bytes 18436
  31.0 1.8 %collective-permute-start.5 = (bf16[2,2,32,1536]{3,2,0,1:T(8,128)(2,1)S(1)}, bf16[2,2,32,1536]{3,2,0,1:T(8,128)(2,1)S(1)}, u32[]{:S(2)}, u32[]{:S(2)}) collective-permute-start(bf16[2,2,32,1536]{3,2,0,1:T(8,128)(2,1)S(1)} %bitcast.150), channel_id=1, source_target_pairs={{0,1},{1,0},{2,3},{3,2},{4,5},{5,4},{6,7},{7,6},{8,9},{9,8},{10,11... | collective-permute-start | bytes 1179656 | tf_op jit(solution)/shard_map/ppermute | solution.py:59
  32.8 0.7 %copy-start.2 = (bf16[2,2,32,1536]{3,2,0,1:T(8,128)(2,1)}, bf16[2,2,32,1536]{3,2,0,1:T(8,128)(2,1)S(1)}, u32[]{:S(2)}) copy-start(bf16[2,2,32,1536]{3,2,0,1:T(8,128)(2,1)S(1)} %collective-permute-done.5) | copy-start | bytes 1179652
  34.7 7.1 %collective-permute-start.6 = (bf16[2,32,1536]{2,1,0:T(8,128)(2,1)S(1)}, bf16[2,32,1536]{2,1,0:T(8,128)(2,1)}, u32[]{:S(2)}, u32[]{:S(2)}) collective-permute-start(bf16[2,32,1536]{2,1,0:T(8,128)(2,1)S(1)} %fusion.48), channel_id=1, source_target_pairs={{0,2},{1,3},{2,0},{3,1},{4,6},{5,7},{6,4},{7,5},{8,10},{9,11},{10,... | collective-permute-start | bytes 589832 | tf_op jit(solution)/shard_map/ppermute | solution.py:59
  43.0 8.4 %copy-start.6 = (bf16[2,1536,384]{2,1,0:T(8,128)(2,1)S(1)}, bf16[2,1536,384]{2,1,0:T(8,128)(2,1)}, u32[]{:S(2)}) copy-start(bf16[2,1536,384]{2,1,0:T(8,128)(2,1)} %param.18) | copy-start | bytes 7077892
  43.4 6.2 %collective-permute-start.7 = (bf16[2,32,1536]{2,1,0:T(8,128)(2,1)S(1)}, bf16[2,32,1536]{2,1,0:T(8,128)(2,1)S(1)}, u32[]{:S(2)}, u32[]{:S(2)}) collective-permute-start(bf16[2,32,1536]{2,1,0:T(8,128)(2,1)S(1)} %get-tuple-element.6), channel_id=1, source_target_pairs={{0,2},{1,3},{2,0},{3,1},{4,6},{5,7},{6,4},{7,5},{8,10},{9,11},{10,... | collective-permute-start | bytes 589832 | tf_op jit(solution)/shard_map/ppermute | solution.py:71
  49.6 1.8 %collective-permute-start.8 = (bf16[2,2,32,1536]{3,2,1,0:T(8,128)(2,1)S(1)}, bf16[2,2,32,1536]{3,2,1,0:T(8,128)(2,1)S(1)}, u32[]{:S(2)}, u32[]{:S(2)}) collective-permute-start(bf16[2,2,32,1536]{3,2,1,0:T(8,128)(2,1)S(1)} %bitcast_dynamic-update-slice_fusion.3), channel_id=1, source_target_pairs={{0,1},{1,0},{2,3},{3,2},{4,5},{5,4},{6,7},{7,6},{8,9},{9,8},{10,11... | collective-permute-start | bytes 1179656 | tf_op jit(solution)/shard_map/ppermute | solution.py:71
  51.4 8.4 %copy-start.8 = (f32[31,384]{1,0:T(8,128)S(1)}, f32[31,384]{1,0:T(8,128)}, u32[]{:S(2)}) copy-start(f32[31,384]{1,0:T(8,128)} %param.19) | copy-start | bytes 142852
  52.4 5.9 %collective-permute-start.10 = (bf16[2,15,384]{2,1,0:T(8,128)(2,1)S(1)}, bf16[2,15,384]{2,1,0:T(8,128)(2,1)S(1)}, u32[]{:S(2)}, u32[]{:S(2)}) collective-permute-start(bf16[2,15,384]{2,1,0:T(8,128)(2,1)S(1)} %get-tuple-element.18), channel_id=1, source_target_pairs={{4,0},{8,4},{12,8},{5,1},{9,5},{13,9},{6,2},{10,6},{14,10},{7,3},{... | collective-permute-start | bytes 69128 | tf_op jit(solution)/shard_map/ppermute | solution.py:21
  53.7 6.1 %collective-permute-start.9 = (bf16[2,15,384]{2,1,0:T(8,128)(2,1)S(1)}, bf16[2,15,384]{2,1,0:T(8,128)(2,1)S(1)}, u32[]{:S(2)}, u32[]{:S(2)}) collective-permute-start(bf16[2,15,384]{2,1,0:T(8,128)(2,1)S(1)} %get-tuple-element.17), channel_id=1, source_target_pairs={{0,4},{4,8},{8,12},{1,5},{5,9},{9,13},{2,6},{6,10},{10,14},{3,7},{... | collective-permute-start | bytes 69128 | tf_op jit(solution)/shard_map/ppermute | solution.py:20
  59.8 1.3 %copy-start.7 = (bf16[384,1536]{1,0:T(8,128)(2,1)S(1)}, bf16[384,1536]{1,0:T(8,128)(2,1)}, u32[]{:S(2)}) copy-start(bf16[384,1536]{1,0:T(8,128)(2,1)} %param.22) | copy-start | bytes 3538948
  59.8 1.3 %copy-start.9 = (f32[384]{0:T(512)S(1)}, f32[384]{0:T(512)}, u32[]{:S(2)}) copy-start(f32[384]{0:T(512)} %param.21) | copy-start | bytes 4612
  59.8 1.3 %copy-start.10 = (f32[384]{0:T(512)S(1)}, f32[384]{0:T(512)}, u32[]{:S(2)}) copy-start(f32[384]{0:T(512)} %param.20) | copy-start | bytes 4612
  61.1 0.8 %copy-start.4 = (s32[1536]{0:T(1024)S(1)}, s32[1536]{0:T(1024)}, u32[]{:S(2)}) copy-start(s32[1536]{0:T(1024)} %param.23) | copy-start | bytes 18436
  61.8 1.9 %collective-permute-start.11 = (bf16[2,2,32,1536]{3,2,0,1:T(8,128)(2,1)S(1)}, bf16[2,2,32,1536]{3,2,0,1:T(8,128)(2,1)}, u32[]{:S(2)}, u32[]{:S(2)}) collective-permute-start(bf16[2,2,32,1536]{3,2,0,1:T(8,128)(2,1)S(1)} %bitcast.151), channel_id=1, source_target_pairs={{0,1},{1,0},{2,3},{3,2},{4,5},{5,4},{6,7},{7,6},{8,9},{9,8},{10,11... | collective-permute-start | bytes 1179656 | tf_op jit(solution)/shard_map/ppermute | solution.py:59
  64.8 7.0 %collective-permute-start.12 = (bf16[2,32,1536]{2,1,0:T(8,128)(2,1)S(1)}, bf16[2,32,1536]{2,1,0:T(8,128)(2,1)S(1)}, u32[]{:S(2)}, u32[]{:S(2)}) collective-permute-start(bf16[2,32,1536]{2,1,0:T(8,128)(2,1)S(1)} %fusion.49), channel_id=1, source_target_pairs={{0,2},{1,3},{2,0},{3,1},{4,6},{5,7},{6,4},{7,5},{8,10},{9,11},{10,... | collective-permute-start | bytes 589832 | tf_op jit(solution)/shard_map/ppermute | solution.py:59

commit v11 on v9

--- a/solution.py
+++ b/solution.py
@@ -61,18 +61,21 @@
     return acc
 
 
-def all_gather_rows(x, axis, dim):
+def all_gather_rows(x, axis, dim, rider):
     count, rank = lax.axis_size(axis), lax.axis_index(axis)
     bits = bit_count(count)
     shape = x.shape
     acc = x
     for k, b in enumerate(reversed(range(bits))):
         mine = (rank >> b) & 1
-        got = lax.ppermute(acc, axis, xor_pairs(count, 1 << b))
+        if b == 0:
+            got, rider = lax.ppermute((acc, rider), axis, xor_pairs(count, 1 << b))
+        else:
+            got = lax.ppermute(acc, axis, xor_pairs(count, 1 << b))
         both = jnp.zeros(acc.shape[: dim + k] + (2,) + acc.shape[dim + k :], acc.dtype)
         both = lax.dynamic_update_index_in_dim(both, acc, mine, dim + k)
         acc = lax.dynamic_update_index_in_dim(both, got, 1 - mine, dim + k)
-    return acc.reshape(shape[:dim] + (shape[dim] * count,) + shape[dim + 1 :])
+    return acc.reshape(shape[:dim] + (shape[dim] * count,) + shape[dim + 1 :]), rider
 
 
 def ring_gather(x, axis):
@@ -182,13 +185,29 @@
     features_mine = lax.dynamic_slice_in_dim(features, row_start, rows_mine, 1)
     residual_mine = features_mine.astype(jnp.float32) + attn_mine
     normed_mine = layer_norm(residual_mine, conv_gain).astype(jnp.bfloat16)
-    normed_conv = all_gather_rows(normed_mine, "mp", 1)
-    gated_rows = gated_units(normed_conv, w_glu)
-    frame_ids = first_frame + jnp.arange(frames_here, dtype=jnp.int32)
-    frame_live = frame_ids[None, :] < frame_counts[:, None]
-    gated_rows = jnp.where(frame_live[..., None], gated_rows, jnp.zeros((), jnp.bfloat16))
     rim_width = kernel.shape[0] // 2
-    padded = with_halo(gated_rows, (("ctx", 1),), rim_width)
+    ctx_mp = ctx_count * mp_count
+    halo_moves = []
+    for pair in range(mp_count // 2):
+        pairs = [((c + 1) * mp_count, c * mp_count + 2 * pair) for c in range(ctx_count - 1)]
+        pairs += [
+            ((c - 1) * mp_count + mp_count - 1, c * mp_count + 2 * pair + 1)
+            for c in range(1, ctx_count)
+        ]
+        halo_moves.append(pairs)
+    edge_start = jnp.where(mp_rank == 0, 0, rows_mine - rim_width)
+    edge_rows = lax.dynamic_slice_in_dim(normed_mine, edge_start, rim_width, 1)
+    arrived = [lax.ppermute(edge_rows, ("ctx", "mp"), pairs) for pairs in halo_moves]
+    halo_piece = lax.dynamic_index_in_dim(jnp.stack(arrived), mp_rank // 2, 0, keepdims=False)
+    normed_conv, halo_other = all_gather_rows(normed_mine, "mp", 1, halo_piece)
+    even = (mp_rank & 1) == 0
+    halo_after = jnp.where(even, halo_piece, halo_other)
+    halo_before = jnp.where(even, halo_other, halo_piece)
+    extended = jnp.concatenate([halo_before, normed_conv, halo_after], axis=1)
+    gated_rows = gated_units(extended, w_glu)
+    frame_ids = first_frame - rim_width + jnp.arange(frames_here + 2 * rim_width, dtype=jnp.int32)
+    frame_live = (frame_ids[None, :] >= 0) & (frame_ids[None, :] < frame_counts[:, None])
+    padded = jnp.where(frame_live[..., None], gated_rows, jnp.zeros((), jnp.bfloat16))
     depthwise = lax.conv_general_dilated(
         padded.astype(jnp.float32),
         kernel[:, None, :],

time: 71.6 us -> 74.7 us (1.043)
  starting transfers between devices: 18.8 us -> 20.1 us
  matrix products: 6.24 us -> 7.16 us
    ppermute x2 -> x4, waiting for transfers between devices: 4.42 us -> 6.12 us  [the longest x2 4.52 us: shards(): lax.ppermute(edge_rows, ('ctx', 'mp'), pairs)]
    ppermute x2 -> x1, starting transfers between devices: 1.63 us -> 3.07 us  [all_gather_rows(): got = lax.ppermute(acc, axis, xor_pairs(count, 1 << b))]
    dot_general x1, matrix products: 1.99 us -> 2.78 us  [shards(): jnp.einsum('std,idc->istc', normed, w_qkv, preferred_element_type=jnp.flo...]
    ppermute x2 -> x1, waiting for transfers between devices: 6.15 us -> 5.52 us  [all_gather_rows(): got = lax.ppermute(acc, axis, xor_pairs(count, 1 << b))]
    ppermute x2 -> x4, starting transfers between devices: 2.58 us -> 2.1 us  [the longest x2 1.96 us: shards(): lax.ppermute(edge_rows, ('ctx', 'mp'), pairs)]
  transfers between devices with their start and end apart: 14 -> 15, of which waited for: 13 -> 12; matrix products, arithmetic and copies ran while one was open for 1% -> 1% of each run, Pallas kernels for 0% -> 0%
where the time goes in v11:
time: 74.7 us; the launch traced here: 74.4 us
  waiting for transfers between devices  36.3 us (49%)
  starting transfers between devices  20.1 us (27%)
  other arithmetic  8.52 us (11%)
  matrix products  7.16 us (10%)
  local copies, waits for them, and re-layouts  1.82 us (2%)
    ppermute x4, waiting for transfers between devices, reduce_scatter_rows(): lax.ppermute(send.astype(jnp.bfloat16), axis, xor_pairs(count, 1 << b))  14.1 us
    ppermute x3, starting transfers between devices, attend_by_heads(): pieces.append(lax.ppermute(send, axis, pairs))  7.01 us
    ppermute x1, waiting for transfers between devices, all_gather_rows(): got = lax.ppermute(acc, axis, xor_pairs(count, 1 << b))  5.52 us
    ppermute x3, waiting for transfers between devices, attend_by_heads(): back.append(lax.ppermute(rows, axis, pairs))  5.44 us
    ppermute x3, waiting for transfers between devices, attend_by_heads(): pieces.append(lax.ppermute(send, axis, pairs))  5.16 us
    ppermute x2, waiting for transfers between devices, shards(): lax.ppermute(edge_rows, ('ctx', 'mp'), pairs)  4.52 us
    ppermute x3, starting transfers between devices, attend_by_heads(): back.append(lax.ppermute(rows, axis, pairs))  4.3 us
    ppermute x4, starting transfers between devices, reduce_scatter_rows(): lax.ppermute(send.astype(jnp.bfloat16), axis, xor_pairs(count, 1 << b))  3.64 us
  transfers between devices with their start and end apart: 15, of which 12 were waited for; matrix products, arithmetic and copies ran while one was open for 1% of the time, Pallas kernels for 0%

profile of v11, /device:TPU:0, one launch (start us, length us, event | category | flops | bytes accessed | tf_op | source)
XLA Modules:
  0.0 74.4 jit_solution(3798282256424831370)
XLA Ops:
  0.0 1.5 %convert_reduce_fusion = f32[2,128]{1,0:T(2,128)S(1)} fusion(bf16[2,128,1536]{2,1,0:T(8,128)(2,1)} %param.12), kind=kLoop, calls=%fused_computation.9 | loop fusion | flops 786176 | bytes 787456 | tf_op jit(solution)/shard_map/reduce_sum | solution.py:27
  1.5 1.5 %fusion.9 = f32[2,128]{1,0:T(2,128)S(1)} fusion(bf16[2,128,1536]{2,1,0:T(8,128)(2,1)} %param.12, f32[2,128]{1,0:T(2,128)S(1)} %broadcast_multiply_fusion.1), kind=kLoop, calls=%fused_computation.15 | loop fusion | flops 1572608 | bytes 788480 | tf_op jit(solution)/shard_map/reduce_sum | solution.py:29
  3.0 2.8 %fusion.18 = bf16[3,2,128,256]{3,2,0,1:T(8,128)(2,1)S(1)} fusion(bf16[3,1536,256]{2,1,0:T(8,128)(2,1)} %param.15, bf16[2,128,1536]{2,1,0:T(8,128)(2,1)} %param.12, f32[1536]{0:T(1024)} %param.14, f32[2,128]{1,0:T(2,128)S(1)} %add_rsqrt_fusion.1, f32[2,128]{1,0:T(2,128)S(1)} %broadcast_multiply_fusion.1), kind=kOutput, calls=%fused_computation.20 | convolution fusion | flops 606142464 | bytes 3547136 | tf_op jit(solution)/shard_map/std,idc->istc/dot_general | solution.py:163
  5.8 0.2 copy.42
  6.1 3.1 %collective-permute-start = (bf16[3,2,128,1,64]{2,4,1,3,0:T(8,128)(2,1)S(1)}, bf16[3,2,128,1,64]{2,4,1,3,0:T(8,128)(2,1)S(1)}, u32[]{:S(2)}, u32[]{:S(2)}) collective-permute-start(bf16[3,2,128,1,64]{2,4,1,3,0:T(8,128)(2,1)S(1)} %get-tuple-element.16), channel_id=1, source_target_pairs={{0,4},{4,8},{8,12},{12,0},{1,5},{5,9},{9,13},{13,1},{2,6},{6,10},{... | collective-permute-start | bytes 294920 | tf_op jit(solution)/shard_map/ppermute | solution.py:127
  9.1 2.6 %collective-permute-start.1 = (bf16[3,2,128,1,64]{2,4,1,3,0:T(8,128)(2,1)S(1)}, bf16[3,2,128,1,64]{2,4,1,3,0:T(8,128)(2,1)S(1)}, u32[]{:S(2)}, u32[]{:S(2)}) collective-permute-start(bf16[3,2,128,1,64]{2,4,1,3,0:T(8,128)(2,1)S(1)} %get-tuple-element.15), channel_id=1, source_target_pairs={{0,8},{4,12},{8,0},{12,4},{1,9},{5,13},{9,1},{13,5},{2,10},{6,14},... | collective-permute-start | bytes 294920 | tf_op jit(solution)/shard_map/ppermute | solution.py:127
  11.7 1.3 %collective-permute-start.2 = (bf16[3,2,128,1,64]{2,4,1,3,0:T(8,128)(2,1)S(1)}, bf16[3,2,128,1,64]{2,4,1,3,0:T(8,128)(2,1)S(1)}, u32[]{:S(2)}, u32[]{:S(2)}) collective-permute-start(bf16[3,2,128,1,64]{2,4,1,3,0:T(8,128)(2,1)S(1)} %get-tuple-element.14), channel_id=1, source_target_pairs={{0,12},{4,0},{8,4},{12,8},{1,13},{5,1},{9,5},{13,9},{2,14},{6,2},{... | collective-permute-start | bytes 294920 | tf_op jit(solution)/shard_map/ppermute | solution.py:127
  13.1 0.1 broadcast_compare_fusion
  13.2 1.6 %collective-permute-done = bf16[3,2,128,1,64]{2,4,1,3,0:T(8,128)(2,1)S(1)} collective-permute-done((bf16[3,2,128,1,64]{2,4,1,3,0:T(8,128)(2,1)S(1)}, bf16[3,2,128,1,64]{2,4,1,3,0:T(8,128)(2,1)S(1)}, u32[]{:S(2)}, u32[]{:S(2)}) %collective-permute-start) | collective-permute-done | bytes 98336 | tf_op jit(solution)/shard_map/ppermute | solution.py:127
  14.8 3.5 %collective-permute-done.1 = bf16[3,2,128,1,64]{2,4,1,3,0:T(8,128)(2,1)S(1)} collective-permute-done((bf16[3,2,128,1,64]{2,4,1,3,0:T(8,128)(2,1)S(1)}, bf16[3,2,128,1,64]{2,4,1,3,0:T(8,128)(2,1)S(1)}, u32[]{:S(2)}, u32[]{:S(2)}) %collective-permute-start.1) | collective-permute-done | bytes 98336 | tf_op jit(solution)/shard_map/ppermute | solution.py:127
  18.4 0.8 %fusion.6 = (f32[2,512]{1,0:T(2,128)S(1)}, f32[2,512,512]{1,2,0:T(8,128)S(1)}) fusion(pred[2,512]{1,0:T(4,128)(4,1)S(1)} %broadcast_compare_fusion, bf16[3,2,512,1,64]{2,4,1,3,0:T(8,128)(2,1)S(1)} %pad_maximum_fusion), kind=kOutput, calls=%fused_computation.12 | convolution fusion | flops 68680704 | bytes 2365440 | tf_op jit(solution)/shard_map/sqhe,skhe->shqk/dot_general | solution.py:99
  19.2 0.5 fusion.7
  19.7 0.6 fusion.23
  20.4 3.6 %collective-permute-start.3 = (bf16[2,1,128,64]{2,3,0,1:T(8,128)(2,1)S(1)}, bf16[2,1,128,64]{2,3,0,1:T(8,128)(2,1)S(1)}, u32[]{:S(2)}, u32[]{:S(2)}) collective-permute-start(bf16[2,1,128,64]{2,3,0,1:T(8,128)(2,1)S(1)} %get-tuple-element.21), channel_id=1, source_target_pairs={{0,12},{4,0},{8,4},{12,8},{1,13},{5,1},{9,5},{13,9},{2,14},{6,2},{... | collective-permute-start | bytes 98312 | tf_op jit(solution)/shard_map/ppermute | solution.py:137
  24.0 0.4 collective-permute-start.4
  24.4 0.2 collective-permute-start.5
  24.7 0.9 %collective-permute-done.3 = bf16[2,1,128,64]{2,3,0,1:T(8,128)(2,1)S(1)} collective-permute-done((bf16[2,1,128,64]{2,3,0,1:T(8,128)(2,1)S(1)}, bf16[2,1,128,64]{2,3,0,1:T(8,128)(2,1)S(1)}, u32[]{:S(2)}, u32[]{:S(2)}) %collective-permute-start.3) | collective-permute-done | bytes 32800 | tf_op jit(solution)/shard_map/ppermute | solution.py:137
  25.6 3.4 %collective-permute-done.4 = bf16[2,1,128,64]{2,3,0,1:T(8,128)(2,1)S(1)} collective-permute-done((bf16[2,1,128,64]{2,3,0,1:T(8,128)(2,1)S(1)}, bf16[2,1,128,64]{2,3,0,1:T(8,128)(2,1)S(1)}, u32[]{:S(2)}, u32[]{:S(2)}) %collective-permute-start.4) | collective-permute-done | bytes 32800 | tf_op jit(solution)/shard_map/ppermute | solution.py:137
  29.0 1.1 %collective-permute-done.5 = bf16[2,1,128,64]{2,3,0,1:T(8,128)(2,1)S(1)} collective-permute-done((bf16[2,1,128,64]{2,3,0,1:T(8,128)(2,1)S(1)}, bf16[2,1,128,64]{2,3,0,1:T(8,128)(2,1)S(1)}, u32[]{:S(2)}, u32[]{:S(2)}) %collective-permute-start.5) | collective-permute-done | bytes 32800 | tf_op jit(solution)/shard_map/ppermute | solution.py:137
  30.3 0.4 convolution_convert_fusion
  30.8 0.1 collective-permute-start.6
  30.9 1.7 %collective-permute-done.6 = bf16[2,2,32,1536]{3,2,0,1:T(8,128)(2,1)S(1)} collective-permute-done((bf16[2,2,32,1536]{3,2,0,1:T(8,128)(2,1)S(1)}, bf16[2,2,32,1536]{3,2,0,1:T(8,128)(2,1)S(1)}, u32[]{:S(2)}, u32[]{:S(2)}) %collective-permute-start.6) | collective-permute-done | bytes 393248 | tf_op jit(solution)/shard_map/ppermute | solution.py:59
  32.6 0.8 %copy-done.2 = bf16[2,2,32,1536]{3,2,0,1:T(8,128)(2,1)} copy-done((bf16[2,2,32,1536]{3,2,0,1:T(8,128)(2,1)}, bf16[2,2,32,1536]{3,2,0,1:T(8,128)(2,1)S(1)}, u32[]{:S(2)}) %copy-start.2) | copy-done | bytes 393240
  33.3 1.1 %convert_add_fusion.1 = f32[2,2,32,1536]{3,2,0,1:T(8,128)S(1)} fusion(bf16[2,2,32,1536]{3,2,0,1:T(8,128)(2,1)} %copy-done.2, bf16[2,2,1,32,1536]{4,3,2,1,0:T(8,128)(2,1)S(1)} %get-tuple-element.11), kind=kLoop, calls=%fused_computation.35 | loop fusion | flops 589824 | bytes 1572864 | tf_op jit(solution)/shard_map/add | solution.py:60
  34.5 1.6 %collective-permute-start.7 = (bf16[2,32,1536]{2,1,0:T(8,128)(2,1)S(1)}, bf16[2,32,1536]{2,1,0:T(8,128)(2,1)}, u32[]{:S(2)}, u32[]{:S(2)}) collective-permute-start(bf16[2,32,1536]{2,1,0:T(8,128)(2,1)S(1)} %fusion.52), channel_id=1, source_target_pairs={{0,2},{1,3},{2,0},{3,1},{4,6},{5,7},{6,4},{7,5},{8,10},{9,11},{10,... | collective-permute-start | bytes 589832 | tf_op jit(solution)/shard_map/ppermute | solution.py:59
  36.0 5.6 %collective-permute-done.7 = bf16[2,32,1536]{2,1,0:T(8,128)(2,1)} collective-permute-done((bf16[2,32,1536]{2,1,0:T(8,128)(2,1)S(1)}, bf16[2,32,1536]{2,1,0:T(8,128)(2,1)}, u32[]{:S(2)}, u32[]{:S(2)}) %collective-permute-start.7) | collective-permute-done | bytes 196640 | tf_op jit(solution)/shard_map/ppermute | solution.py:59
  41.6 1.2 %fusion.68 = (f32[2,32]{1,0:T(2,128)S(1)}, f32[2,32,1536]{2,1,0:T(8,128)S(1)}) fusion(bf16[2,32,1536]{2,1,0:T(8,128)(2,1)} %collective-permute-done.7, f32[2,2,32,1536]{3,2,0,1:T(8,128)S(1)} %convert_add_fusion.1, s32[]{:T(128)S(6)} %select_n.133, bf16[2,128,1536]{2,1,0:T(8,128)(2,1)} %param.12, s32[]{:T(128)S(6)} %select_n.117), kind=kLoop, calls=%fused_computation.129 | loop fusion | flops 491456 | bytes 1179912 | tf_op jit(solution)/shard_map/reduce_sum | solution.py:27
  42.8 0.2 multiply_reduce_fusion
  43.0 0.1 bitcast_dynamic-update-slice_fusion.3
  43.2 1.3 %collective-permute-start.8 = (bf16[2,15,1536]{2,1,0:T(8,128)(2,1)S(1)}, bf16[2,15,1536]{2,1,0:T(8,128)(2,1)S(1)}, u32[]{:S(2)}, u32[]{:S(2)}) collective-permute-start(bf16[2,15,1536]{2,1,0:T(8,128)(2,1)S(1)} %constant_dynamic-slice_fusion.2), channel_id=1, source_target_pairs={{4,0},{8,4},{12,8},{3,5},{7,9},{11,13},{20,16},{24,20},{28,24},{19... | collective-permute-start | bytes 276488 | tf_op jit(solution)/shard_map/ppermute | solution.py:200
  44.5 0.7 collective-permute-start.9
  45.2 4.5 %collective-permute-done.8 = bf16[2,15,1536]{2,1,0:T(8,128)(2,1)S(1)} collective-permute-done((bf16[2,15,1536]{2,1,0:T(8,128)(2,1)S(1)}, bf16[2,15,1536]{2,1,0:T(8,128)(2,1)S(1)}, u32[]{:S(2)}, u32[]{:S(2)}) %collective-permute-start.8) | collective-permute-done | bytes 92192 | tf_op jit(solution)/shard_map/ppermute | solution.py:200
  49.9 0.1 compare_and_fusion
  49.9 3.1 %collective-permute-start.11 = (bf16[2,32,1536]{2,1,0:T(8,128)(2,1)S(1)}, bf16[2,32,1536]{2,1,0:T(8,128)(2,1)S(1)}, u32[]{:S(2)}, u32[]{:S(2)}) collective-permute-start(bf16[2,32,1536]{2,1,0:T(8,128)(2,1)S(1)} %get-tuple-element.6), channel_id=1, source_target_pairs={{0,2},{1,3},{2,0},{3,1},{4,6},{5,7},{6,4},{7,5},{8,10},{9,11},{10,... | collective-permute-start | bytes 589832 | tf_op jit(solution)/shard_map/ppermute | solution.py:74
  53.0 5.5 %collective-permute-done.11 = bf16[2,32,1536]{2,1,0:T(8,128)(2,1)S(1)} collective-permute-done((bf16[2,32,1536]{2,1,0:T(8,128)(2,1)S(1)}, bf16[2,32,1536]{2,1,0:T(8,128)(2,1)S(1)}, u32[]{:S(2)}, u32[]{:S(2)}) %collective-permute-start.11) | collective-permute-done | bytes 196640 | tf_op jit(solution)/shard_map/ppermute | solution.py:74
  58.8 1.6 %collective-permute-done.12 = bf16[2,2,32,1536]{3,2,1,0:T(8,128)(2,1)S(1)} collective-permute-done((bf16[2,2,32,1536]{3,2,1,0:T(8,128)(2,1)S(1)}, bf16[2,2,32,1536]{3,2,1,0:T(8,128)(2,1)S(1)}, u32[]{:S(2)}, u32[]{:S(2)}) %collective-permute-start.12) | collective-permute-done | bytes 393248 | tf_op jit(solution)/shard_map/ppermute | solution.py:72
  60.4 0.9 %fusion.12 = f32[2,2,158,384]{3,2,0,1:T(8,128)S(1)} fusion(bf16[2,1536,384]{2,1,0:T(8,128)(2,1)S(1)} %copy-done, bf16[2,15,1536]{2,1,0:T(8,128)(2,1)S(1)} %get-tuple-element.18, bf16[2,128,1536]{2,1,0:T(8,128)(2,1)S(1)} %bitcast.138, bf16[2,15,1536]{2,1,0:T(8,128)(2,1)S(1)} %get-tuple-element.17), kind=kOutput, calls=%fused_computation.18 | convolution fusion | flops 748449792 | bytes 4300800 | tf_op jit(solution)/shard_map/std,gdc->gstc/dot_general | solution.py:34
  61.4 0.2 bitcast_select_fusion
  61.6 1.1 %fusion.50 = f32[2,128,384]{2,0,1:T(2,128)S(1)} fusion(bf16[2,158,384]{2,1,0:T(8,128)(2,1)S(1)} %bitcast_select_fusion, f32[31,1,384]{2,0,1:T(8,128)S(1)} %bitcast.145), kind=kOutput, calls=%fused_computation.69 | convolution fusion | flops 36569088 | bytes 683520 | tf_op jit(solution)/shard_map/conv_general_dilated | solution.py:211
  62.7 0.2 copy-done.6
  62.8 0.6 convolution_convert_fusion.1
  63.5 0.2 collective-permute-start.13
  63.8 1.7 %collective-permute-done.13 = bf16[2,2,32,1536]{3,2,0,1:T(8,128)(2,1)} collective-permute-done((bf16[2,2,32,1536]{3,2,0,1:T(8,128)(2,1)S(1)}, bf16[2,2,32,1536]{3,2,0,1:T(8,128)(2,1)}, u32[]{:S(2)}, u32[]{:S(2)}) %collective-permute-start.13) | collective-permute-done | bytes 393248 | tf_op jit(solution)/shard_map/ppermute | solution.py:59
  65.5 1.1 %convert_add_fusion = f32[2,2,32,1536]{3,2,0,1:T(8,128)S(1)} fusion(bf16[2,2,32,1536]{3,2,0,1:T(8,128)(2,1)} %collective-permute-done.13, bf16[2,2,1,32,1536]{4,3,2,1,0:T(8,128)(2,1)S(1)} %get-tuple-element.9), kind=kLoop, calls=%fused_computation.34 | loop fusion | flops 589824 | bytes 1572864 | tf_op jit(solution)/shard_map/add | solution.py:60
  66.6 1.8 %collective-permute-start.14 = (bf16[2,32,1536]{2,1,0:T(8,128)(2,1)S(1)}, bf16[2,32,1536]{2,1,0:T(8,128)(2,1)S(1)}, u32[]{:S(2)}, u32[]{:S(2)}) collective-permute-start(bf16[2,32,1536]{2,1,0:T(8,128)(2,1)S(1)} %fusion.53), channel_id=1, source_target_pairs={{0,2},{1,3},{2,0},{3,1},{4,6},{5,7},{6,4},{7,5},{8,10},{9,11},{10,... | collective-permute-start | bytes 589832 | tf_op jit(solution)/shard_map/ppermute | solution.py:59
  68.4 0.1 broadcast_compare_fusion.2
  68.5 5.1 %collective-permute-done.14 = bf16[2,32,1536]{2,1,0:T(8,128)(2,1)S(1)} collective-permute-done((bf16[2,32,1536]{2,1,0:T(8,128)(2,1)S(1)}, bf16[2,32,1536]{2,1,0:T(8,128)(2,1)S(1)}, u32[]{:S(2)}, u32[]{:S(2)}) %collective-permute-start.14) | collective-permute-done | bytes 196640 | tf_op jit(solution)/shard_map/ppermute | solution.py:59
  73.6 0.8 %fusion.47 = bf16[2,32,1536]{2,1,0:T(8,128)(2,1)} fusion(f32[2,32,1536]{2,1,0:T(8,128)S(1)} %get-tuple-element.8, bf16[2,32,1536]{2,1,0:T(8,128)(2,1)S(1)} %collective-permute-done.14, f32[2,2,32,1536]{3,2,0,1:T(8,128)S(1)} %convert_add_fusion, s32[]{:T(128)S(6)} %select_n.133, bf16[1536]{0:T(1024)(128)(2,1)S(1)} %get-tuple-element.23, ...), kind=kLoop, calls=%fused_computation.55 | loop fusion | flops 884736 | bytes 1185860 | tf_op jit(solution)/shard_map/convert_element_type | solution.py:228
  (62 shorter events, 1.1 us)
Async XLA Ops:
  0.0 60.4 %copy-start = (bf16[2,1536,384]{2,1,0:T(8,128)(2,1)S(1)}, bf16[2,1536,384]{2,1,0:T(8,128)(2,1)}, u32[]{:S(2)}) copy-start(bf16[2,1536,384]{2,1,0:T(8,128)(2,1)} %param.18) | copy-start | bytes 7077892
  3.0 10.1 %copy-start.5 = (s32[2]{0:T(128)S(1)}, s32[2]{0:T(128)}, u32[]{:S(2)}) copy-start(s32[2]{0:T(128)} %param.13) | copy-start | bytes 28
  6.1 8.8 %collective-permute-start = (bf16[3,2,128,1,64]{2,4,1,3,0:T(8,128)(2,1)S(1)}, bf16[3,2,128,1,64]{2,4,1,3,0:T(8,128)(2,1)S(1)}, u32[]{:S(2)}, u32[]{:S(2)}) collective-permute-start(bf16[3,2,128,1,64]{2,4,1,3,0:T(8,128)(2,1)S(1)} %get-tuple-element.16), channel_id=1, source_target_pairs={{0,4},{4,8},{8,12},{12,0},{1,5},{5,9},{9,13},{13,1},{2,6},{6,10},{... | collective-permute-start | bytes 294920 | tf_op jit(solution)/shard_map/ppermute | solution.py:127
  9.1 9.2 %collective-permute-start.1 = (bf16[3,2,128,1,64]{2,4,1,3,0:T(8,128)(2,1)S(1)}, bf16[3,2,128,1,64]{2,4,1,3,0:T(8,128)(2,1)S(1)}, u32[]{:S(2)}, u32[]{:S(2)}) collective-permute-start(bf16[3,2,128,1,64]{2,4,1,3,0:T(8,128)(2,1)S(1)} %get-tuple-element.15), channel_id=1, source_target_pairs={{0,8},{4,12},{8,0},{12,4},{1,9},{5,13},{9,1},{13,5},{2,10},{6,14},... | collective-permute-start | bytes 294920 | tf_op jit(solution)/shard_map/ppermute | solution.py:127
  11.7 6.6 %collective-permute-start.2 = (bf16[3,2,128,1,64]{2,4,1,3,0:T(8,128)(2,1)S(1)}, bf16[3,2,128,1,64]{2,4,1,3,0:T(8,128)(2,1)S(1)}, u32[]{:S(2)}, u32[]{:S(2)}) collective-permute-start(bf16[3,2,128,1,64]{2,4,1,3,0:T(8,128)(2,1)S(1)} %get-tuple-element.14), channel_id=1, source_target_pairs={{0,12},{4,0},{8,4},{12,8},{1,13},{5,1},{9,5},{13,9},{2,14},{6,2},{... | collective-permute-start | bytes 294920 | tf_op jit(solution)/shard_map/ppermute | solution.py:127
  19.7 10.6 %copy-start.1 = (bf16[256,1536]{1,0:T(8,128)(2,1)S(1)}, bf16[256,1536]{1,0:T(8,128)(2,1)}, u32[]{:S(2)}) copy-start(bf16[256,1536]{1,0:T(8,128)(2,1)} %param.16) | copy-start | bytes 2359300
  20.4 5.2 %collective-permute-start.3 = (bf16[2,1,128,64]{2,3,0,1:T(8,128)(2,1)S(1)}, bf16[2,1,128,64]{2,3,0,1:T(8,128)(2,1)S(1)}, u32[]{:S(2)}, u32[]{:S(2)}) collective-permute-start(bf16[2,1,128,64]{2,3,0,1:T(8,128)(2,1)S(1)} %get-tuple-element.21), channel_id=1, source_target_pairs={{0,12},{4,0},{8,4},{12,8},{1,13},{5,1},{9,5},{13,9},{2,14},{6,2},{... | collective-permute-start | bytes 98312 | tf_op jit(solution)/shard_map/ppermute | solution.py:137
  24.0 5.0 %collective-permute-start.4 = (bf16[2,1,128,64]{2,3,0,1:T(8,128)(2,1)S(1)}, bf16[2,1,128,64]{2,3,0,1:T(8,128)(2,1)S(1)}, u32[]{:S(2)}, u32[]{:S(2)}) collective-permute-start(bf16[2,1,128,64]{2,3,0,1:T(8,128)(2,1)S(1)} %get-tuple-element.20), channel_id=1, source_target_pairs={{0,8},{4,12},{8,0},{12,4},{1,9},{5,13},{9,1},{13,5},{2,10},{6,14},... | collective-permute-start | bytes 98312 | tf_op jit(solution)/shard_map/ppermute | solution.py:137
  24.4 5.7 %collective-permute-start.5 = (bf16[2,1,128,64]{2,3,0,1:T(8,128)(2,1)S(1)}, bf16[2,1,128,64]{2,3,0,1:T(8,128)(2,1)S(1)}, u32[]{:S(2)}, u32[]{:S(2)}) collective-permute-start(bf16[2,1,128,64]{2,3,0,1:T(8,128)(2,1)S(1)} %get-tuple-element.19), channel_id=1, source_target_pairs={{0,4},{4,8},{8,12},{12,0},{1,5},{5,9},{9,13},{13,1},{2,6},{6,10},{... | collective-permute-start | bytes 98312 | tf_op jit(solution)/shard_map/ppermute | solution.py:137
  30.8 12.3 %copy-start.3 = (f32[1536]{0:T(1024)S(1)}, f32[1536]{0:T(1024)}, u32[]{:S(2)}) copy-start(f32[1536]{0:T(1024)} %param.17) | copy-start | bytes 18436
  30.8 1.8 %collective-permute-start.6 = (bf16[2,2,32,1536]{3,2,0,1:T(8,128)(2,1)S(1)}, bf16[2,2,32,1536]{3,2,0,1:T(8,128)(2,1)S(1)}, u32[]{:S(2)}, u32[]{:S(2)}) collective-permute-start(bf16[2,2,32,1536]{3,2,0,1:T(8,128)(2,1)S(1)} %bitcast.141), channel_id=1, source_target_pairs={{0,1},{1,0},{2,3},{3,2},{4,5},{5,4},{6,7},{7,6},{8,9},{9,8},{10,11... | collective-permute-start | bytes 1179656 | tf_op jit(solution)/shard_map/ppermute | solution.py:59
  32.6 0.8 %copy-start.2 = (bf16[2,2,32,1536]{3,2,0,1:T(8,128)(2,1)}, bf16[2,2,32,1536]{3,2,0,1:T(8,128)(2,1)S(1)}, u32[]{:S(2)}) copy-start(bf16[2,2,32,1536]{3,2,0,1:T(8,128)(2,1)S(1)} %collective-permute-done.6) | copy-start | bytes 1179652
  34.5 7.1 %collective-permute-start.7 = (bf16[2,32,1536]{2,1,0:T(8,128)(2,1)S(1)}, bf16[2,32,1536]{2,1,0:T(8,128)(2,1)}, u32[]{:S(2)}, u32[]{:S(2)}) collective-permute-start(bf16[2,32,1536]{2,1,0:T(8,128)(2,1)S(1)} %fusion.52), channel_id=1, source_target_pairs={{0,2},{1,3},{2,0},{3,1},{4,6},{5,7},{6,4},{7,5},{8,10},{9,11},{10,... | collective-permute-start | bytes 589832 | tf_op jit(solution)/shard_map/ppermute | solution.py:59
  43.2 6.5 %collective-permute-start.8 = (bf16[2,15,1536]{2,1,0:T(8,128)(2,1)S(1)}, bf16[2,15,1536]{2,1,0:T(8,128)(2,1)S(1)}, u32[]{:S(2)}, u32[]{:S(2)}) collective-permute-start(bf16[2,15,1536]{2,1,0:T(8,128)(2,1)S(1)} %constant_dynamic-slice_fusion.2), channel_id=1, source_target_pairs={{4,0},{8,4},{12,8},{3,5},{7,9},{11,13},{20,16},{24,20},{28,24},{19... | collective-permute-start | bytes 276488 | tf_op jit(solution)/shard_map/ppermute | solution.py:200
  44.5 5.2 %collective-permute-start.9 = (bf16[2,15,1536]{2,1,0:T(8,128)(2,1)S(1)}, bf16[2,15,1536]{2,1,0:T(8,128)(2,1)S(1)}, u32[]{:S(2)}, u32[]{:S(2)}) collective-permute-start(bf16[2,15,1536]{2,1,0:T(8,128)(2,1)S(1)} %constant_dynamic-slice_fusion.2), channel_id=1, source_target_pairs={{4,2},{8,6},{12,10},{3,7},{7,11},{11,15},{20,18},{24,22},{28,26},{... | collective-permute-start | bytes 276488 | tf_op jit(solution)/shard_map/ppermute | solution.py:200
  49.8 3.2 %collective-permute-start.10 = (bf16[2,15,1536]{2,1,0:T(8,128)(2,1)S(1)}, bf16[2,15,1536]{2,1,0:T(8,128)(2,1)S(1)}, u32[]{:S(2)}, u32[]{:S(2)}) collective-permute-start(bf16[2,15,1536]{2,1,0:T(8,128)(2,1)S(1)} %fusion.59), channel_id=1, source_target_pairs={{0,1},{1,0},{2,3},{3,2},{4,5},{5,4},{6,7},{7,6},{8,9},{9,8},{10,11... | collective-permute-start | bytes 276488 | tf_op jit(solution)/shard_map/ppermute | solution.py:72
  49.9 8.6 %collective-permute-start.11 = (bf16[2,32,1536]{2,1,0:T(8,128)(2,1)S(1)}, bf16[2,32,1536]{2,1,0:T(8,128)(2,1)S(1)}, u32[]{:S(2)}, u32[]{:S(2)}) collective-permute-start(bf16[2,32,1536]{2,1,0:T(8,128)(2,1)S(1)} %get-tuple-element.6), channel_id=1, source_target_pairs={{0,2},{1,3},{2,0},{3,1},{4,6},{5,7},{6,4},{7,5},{8,10},{9,11},{10,... | collective-permute-start | bytes 589832 | tf_op jit(solution)/shard_map/ppermute | solution.py:74
  58.6 1.8 %collective-permute-start.12 = (bf16[2,2,32,1536]{3,2,1,0:T(8,128)(2,1)S(1)}, bf16[2,2,32,1536]{3,2,1,0:T(8,128)(2,1)S(1)}, u32[]{:S(2)}, u32[]{:S(2)}) collective-permute-start(bf16[2,2,32,1536]{3,2,1,0:T(8,128)(2,1)S(1)} %bitcast_dynamic-update-slice_fusion.2), channel_id=1, source_target_pairs={{0,1},{1,0},{2,3},{3,2},{4,5},{5,4},{6,7},{7,6},{8,9},{9,8},{10,11... | collective-permute-start | bytes 1179656 | tf_op jit(solution)/shard_map/ppermute | solution.py:72
  60.4 1.1 %copy-start.7 = (f32[31,384]{1,0:T(8,128)S(1)}, f32[31,384]{1,0:T(8,128)}, u32[]{:S(2)}) copy-start(f32[31,384]{1,0:T(8,128)} %param.19) | copy-start | bytes 142852
  61.5 1.3 %copy-start.6 = (bf16[384,1536]{1,0:T(8,128)(2,1)S(1)}, bf16[384,1536]{1,0:T(8,128)(2,1)}, u32[]{:S(2)}) copy-start(bf16[384,1536]{1,0:T(8,128)(2,1)} %param.22) | copy-start | bytes 3538948
  61.6 1.3 %copy-start.8 = (f32[384]{0:T(512)S(1)}, f32[384]{0:T(512)}, u32[]{:S(2)}) copy-start(f32[384]{0:T(512)} %param.21) | copy-start | bytes 4612
  61.6 1.3 %copy-start.9 = (f32[384]{0:T(512)S(1)}, f32[384]{0:T(512)}, u32[]{:S(2)}) copy-start(f32[384]{0:T(512)} %param.20) | copy-start | bytes 4612
  62.8 0.9 %copy-start.4 = (s32[1536]{0:T(1024)S(1)}, s32[1536]{0:T(1024)}, u32[]{:S(2)}) copy-start(s32[1536]{0:T(1024)} %param.23) | copy-start | bytes 18436
  63.5 1.9 %collective-permute-start.13 = (bf16[2,2,32,1536]{3,2,0,1:T(8,128)(2,1)S(1)}, bf16[2,2,32,1536]{3,2,0,1:T(8,128)(2,1)}, u32[]{:S(2)}, u32[]{:S(2)}) collective-permute-start(bf16[2,2,32,1536]{3,2,0,1:T(8,128)(2,1)S(1)} %bitcast.142), channel_id=1, source_target_pairs={{0,1},{1,0},{2,3},{3,2},{4,5},{5,4},{6,7},{7,6},{8,9},{9,8},{10,11... | collective-permute-start | bytes 1179656 | tf_op jit(solution)/shard_map/ppermute | solution.py:59
  66.6 7.0 %collective-permute-start.14 = (bf16[2,32,1536]{2,1,0:T(8,128)(2,1)S(1)}, bf16[2,32,1536]{2,1,0:T(8,128)(2,1)S(1)}, u32[]{:S(2)}, u32[]{:S(2)}) collective-permute-start(bf16[2,32,1536]{2,1,0:T(8,128)(2,1)S(1)} %fusion.53), channel_id=1, source_target_pairs={{0,2},{1,3},{2,0},{3,1},{4,6},{5,7},{6,4},{7,5},{8,10},{9,11},{10,... | collective-permute-start | bytes 589832 | tf_op jit(solution)/shard_map/ppermute | solution.py:59

commit v12 on v9

--- a/solution.py
+++ b/solution.py
@@ -24,10 +24,11 @@
 
 
 def layer_norm(values, gain):
-    centre = jnp.mean(values, axis=-1, keepdims=True)
-    centred = values - centre
-    variance = jnp.mean(centred * centred, axis=-1, keepdims=True)
-    return centred * lax.rsqrt(variance + epsilon) * gain
+    shift = values[..., :1]
+    offset = values - shift
+    offset_mean = jnp.mean(offset, axis=-1, keepdims=True)
+    variance = jnp.mean(offset * offset, axis=-1, keepdims=True) - offset_mean * offset_mean
+    return (offset - offset_mean) * lax.rsqrt(variance + epsilon) * gain
 
 
 def gated_units(normed, w_glu):

time: 71.6 us -> 75.9 us (1.060)
  local copies, waits for them, and re-layouts: 1.79 us -> 6.18 us
    reduce_sum x4 -> x2, other arithmetic: 4.3 us -> 0.62 us  [layer_norm(): offset_mean = jnp.mean(offset, axis=-1, keepdims=True)]
    convert_element_type x0 -> x1, other arithmetic: none -> 1.46 us  [shards(): features.astype(jnp.float32)]
    add x0 -> x1, other arithmetic: none -> 1.16 us  [shards(): residual_mine = features_mine.astype(jnp.float32) + attn_mine]
    unnamed x29 -> x35, local copies, waits for them, and re-layouts: 1.04 us -> 2.04 us
    convert_element_type x1, local copies, waits for them, and re-layouts: 0.22 us -> 1.21 us  [shards(): projected = jnp.einsum('std,idc->istc', normed, w_qkv, preferred_element_...]
    concatenate x1, other arithmetic: 0.05 us -> 0.94 us  [attend_by_heads(): every = jnp.concatenate(pieces, axis=2)]
  transfers between devices with their start and end apart: 14 -> 14, of which waited for: 13 -> 13; matrix products, arithmetic and copies ran while one was open for 1% -> 0% of each run, Pallas kernels for 0% -> 0%
where the time goes in v12:
time: 75.9 us; the launch traced here: 75.6 us
  waiting for transfers between devices  36.1 us (48%)
  starting transfers between devices  18.6 us (25%)
  other arithmetic  8.37 us (11%)
  local copies, waits for them, and re-layouts  6.18 us (8%)
  matrix products  5.91 us (8%)
    ppermute x4, waiting for transfers between devices, reduce_scatter_rows(): lax.ppermute(send.astype(jnp.bfloat16), axis, xor_pairs(count, 1 << b))  14.7 us
    ppermute x3, starting transfers between devices, attend_by_heads(): pieces.append(lax.ppermute(send, axis, pairs))  6.96 us
    ppermute x2, waiting for transfers between devices, all_gather_rows(): got = lax.ppermute(acc, axis, xor_pairs(count, 1 << b))  6.15 us
    ppermute x3, waiting for transfers between devices, attend_by_heads(): back.append(lax.ppermute(rows, axis, pairs))  5.48 us
    ppermute x3, waiting for transfers between devices, attend_by_heads(): pieces.append(lax.ppermute(send, axis, pairs))  5.37 us
    ppermute x3, starting transfers between devices, attend_by_heads(): back.append(lax.ppermute(rows, axis, pairs))  4.26 us
    ppermute x1, waiting for transfers between devices, with_halo(): after = lax.ppermute(initial, axis, down)  4.22 us
    ppermute x4, starting transfers between devices, reduce_scatter_rows(): lax.ppermute(send.astype(jnp.bfloat16), axis, xor_pairs(count, 1 << b))  3.19 us
  transfers between devices with their start and end apart: 14, of which 13 were waited for; matrix products, arithmetic and copies ran while one was open for 0% of the time, Pallas kernels for 0%

profile of v12, /device:TPU:0, one launch (start us, length us, event | category | flops | bytes accessed | tf_op | source)
XLA Modules:
  0.0 75.6 jit_solution(7452167734639744985)
XLA Ops:
  0.0 1.5 %convert_element_type.85 = f32[2,128,1536]{2,1,0:T(8,128)S(1)} convert(bf16[2,128,1536]{2,1,0:T(8,128)(2,1)} %param.12) | non-fusion elementwise | flops 393216 | bytes 2359296 | tf_op jit(solution)/shard_map/convert_element_type | solution.py:160
  1.6 0.4 subtract_reduce_fusion
  2.1 1.7 %fusion.13 = bf16[3,2,128,256]{3,2,0,1:T(8,128)(2,1)} fusion(bf16[3,1536,256]{2,1,0:T(8,128)(2,1)S(1)} %copy-done, bf16[2,128,1536]{2,1,0:T(8,128)(2,1)S(1)} %copy-done.1, f32[1536]{0:T(1024)S(1)} %copy-done.11, f32[2,128]{1,0:T(2,128)S(1)} %get-tuple-element.29, f32[2,128]{1,0:T(2,128)S(1)} %get-tuple-element.28, f32[2,128]{1,0:T(2,128)S(1)} %slice_reduce_fusion), kind=kOutput, calls=%fused_computation.16 | convolution fusion | flops 606535680 | bytes 3548160 | tf_op jit(solution)/shard_map/std,idc->istc/dot_general | solution.py:161
  3.8 1.2 %copy.39 = bf16[3,2,128,256]{2,3,1,0:T(8,128)(2,1)S(1)} copy(bf16[3,2,128,256]{3,2,0,1:T(8,128)(2,1)} %fusion.13) | data formatting | bytes 786432 | tf_op jit(solution)/shard_map/convert_element_type | solution.py:163
  5.0 0.7 dynamic-slice_bitcast_fusion.4
  5.8 3.0 %collective-permute-start = (bf16[3,2,128,1,64]{2,4,1,3,0:T(8,128)(2,1)}, bf16[3,2,128,1,64]{2,4,1,3,0:T(8,128)(2,1)S(1)}, u32[]{:S(2)}, u32[]{:S(2)}) collective-permute-start(bf16[3,2,128,1,64]{2,4,1,3,0:T(8,128)(2,1)} %get-tuple-element.18), channel_id=1, source_target_pairs={{0,4},{4,8},{8,12},{12,0},{1,5},{5,9},{9,13},{13,1},{2,6},{6,10},{... | collective-permute-start | bytes 294920 | tf_op jit(solution)/shard_map/ppermute | solution.py:125
  8.8 2.6 %collective-permute-start.1 = (bf16[3,2,128,1,64]{2,4,1,3,0:T(8,128)(2,1)}, bf16[3,2,128,1,64]{2,4,1,3,0:T(8,128)(2,1)S(1)}, u32[]{:S(2)}, u32[]{:S(2)}) collective-permute-start(bf16[3,2,128,1,64]{2,4,1,3,0:T(8,128)(2,1)} %get-tuple-element.17), channel_id=1, source_target_pairs={{0,8},{4,12},{8,0},{12,4},{1,9},{5,13},{9,1},{13,5},{2,10},{6,14},... | collective-permute-start | bytes 294920 | tf_op jit(solution)/shard_map/ppermute | solution.py:125
  11.4 1.4 %collective-permute-start.2 = (bf16[3,2,128,1,64]{2,4,1,3,0:T(8,128)(2,1)}, bf16[3,2,128,1,64]{2,4,1,3,0:T(8,128)(2,1)S(1)}, u32[]{:S(2)}, u32[]{:S(2)}) collective-permute-start(bf16[3,2,128,1,64]{2,4,1,3,0:T(8,128)(2,1)} %get-tuple-element.16), channel_id=1, source_target_pairs={{0,12},{4,0},{8,4},{12,8},{1,13},{5,1},{9,5},{13,9},{2,14},{6,2},{... | collective-permute-start | bytes 294920 | tf_op jit(solution)/shard_map/ppermute | solution.py:125
  12.9 1.8 %collective-permute-done = bf16[3,2,128,1,64]{2,4,1,3,0:T(8,128)(2,1)S(1)} collective-permute-done((bf16[3,2,128,1,64]{2,4,1,3,0:T(8,128)(2,1)}, bf16[3,2,128,1,64]{2,4,1,3,0:T(8,128)(2,1)S(1)}, u32[]{:S(2)}, u32[]{:S(2)}) %collective-permute-start) | collective-permute-done | bytes 98336 | tf_op jit(solution)/shard_map/ppermute | solution.py:125
  14.7 3.5 %collective-permute-done.1 = bf16[3,2,128,1,64]{2,4,1,3,0:T(8,128)(2,1)S(1)} collective-permute-done((bf16[3,2,128,1,64]{2,4,1,3,0:T(8,128)(2,1)}, bf16[3,2,128,1,64]{2,4,1,3,0:T(8,128)(2,1)S(1)}, u32[]{:S(2)}, u32[]{:S(2)}) %collective-permute-start.1) | collective-permute-done | bytes 98336 | tf_op jit(solution)/shard_map/ppermute | solution.py:125
  18.2 0.9 %pad_maximum_fusion = bf16[3,2,512,1,64]{2,4,1,3,0:T(8,128)(2,1)S(1)} fusion(bf16[3,2,128,1,64]{2,4,1,3,0:T(8,128)(2,1)S(1)} %collective-permute-done.2, bf16[3,2,128,1,64]{2,4,1,3,0:T(8,128)(2,1)S(1)} %collective-permute-done.1, bf16[3,2,128,1,64]{2,4,1,3,0:T(8,128)(2,1)S(1)} %collective-permute-done, bf16[3,2,128,1,64]{2,4,1,3,0:T(8,128)(2,1)} %get-tuple-element.15), kind=kLoop, calls=%fused_computation.37 | loop fusion | flops 1572864 | bytes 786432 | tf_op jit(solution)/shard_map/concatenate | solution.py:127
  19.2 0.8 %fusion.4 = (f32[2,512]{1,0:T(2,128)S(1)}, f32[2,512,512]{1,2,0:T(8,128)S(1)}) fusion(pred[2,512]{1,0:T(4,128)(4,1)S(1)} %broadcast_compare_fusion, bf16[3,2,512,1,64]{2,4,1,3,0:T(8,128)(2,1)S(1)} %pad_maximum_fusion), kind=kOutput, calls=%fused_computation.8 | convolution fusion | flops 68680704 | bytes 2365440 | tf_op jit(solution)/shard_map/sqhe,skhe->shqk/dot_general | solution.py:97
  20.0 0.5 fusion.5
  20.5 0.6 fusion.18
  21.2 3.6 %collective-permute-start.3 = (bf16[2,1,128,64]{2,3,0,1:T(8,128)(2,1)S(1)}, bf16[2,1,128,64]{2,3,0,1:T(8,128)(2,1)S(1)}, u32[]{:S(2)}, u32[]{:S(2)}) collective-permute-start(bf16[2,1,128,64]{2,3,0,1:T(8,128)(2,1)S(1)} %get-tuple-element.23), channel_id=1, source_target_pairs={{0,12},{4,0},{8,4},{12,8},{1,13},{5,1},{9,5},{13,9},{2,14},{6,2},{... | collective-permute-start | bytes 98312 | tf_op jit(solution)/shard_map/ppermute | solution.py:135
  24.8 0.4 collective-permute-start.4
  25.2 0.2 collective-permute-start.5
  25.4 0.9 %collective-permute-done.3 = bf16[2,1,128,64]{2,3,0,1:T(8,128)(2,1)S(1)} collective-permute-done((bf16[2,1,128,64]{2,3,0,1:T(8,128)(2,1)S(1)}, bf16[2,1,128,64]{2,3,0,1:T(8,128)(2,1)S(1)}, u32[]{:S(2)}, u32[]{:S(2)}) %collective-permute-start.3) | collective-permute-done | bytes 32800 | tf_op jit(solution)/shard_map/ppermute | solution.py:135
  26.4 3.4 %collective-permute-done.4 = bf16[2,1,128,64]{2,3,0,1:T(8,128)(2,1)S(1)} collective-permute-done((bf16[2,1,128,64]{2,3,0,1:T(8,128)(2,1)S(1)}, bf16[2,1,128,64]{2,3,0,1:T(8,128)(2,1)S(1)}, u32[]{:S(2)}, u32[]{:S(2)}) %collective-permute-start.4) | collective-permute-done | bytes 32800 | tf_op jit(solution)/shard_map/ppermute | solution.py:135
  29.8 1.2 %collective-permute-done.5 = bf16[2,1,128,64]{2,3,0,1:T(8,128)(2,1)S(1)} collective-permute-done((bf16[2,1,128,64]{2,3,0,1:T(8,128)(2,1)S(1)}, bf16[2,1,128,64]{2,3,0,1:T(8,128)(2,1)S(1)}, u32[]{:S(2)}, u32[]{:S(2)}) %collective-permute-start.5) | collective-permute-done | bytes 32800 | tf_op jit(solution)/shard_map/ppermute | solution.py:135
  31.0 0.4 convolution_convert_fusion
  31.5 0.8 %copy.78 = bf16[2,2,1,32,1536]{4,3,0,1,2:T(8,128)(2,1)} copy(bf16[2,2,1,32,1536]{4,3,2,1,0:T(8,128)(2,1)S(1)} %get-tuple-element.14) | data formatting | bytes 786432 | tf_op jit(solution)/shard_map/jit(dynamic_index_in_dim)/dynamic_slice | solution.py:59
  32.3 2.1 %collective-permute-done.6 = bf16[2,2,32,1536]{3,2,0,1:T(8,128)(2,1)} collective-permute-done((bf16[2,2,32,1536]{3,2,0,1:T(8,128)(2,1)}, bf16[2,2,32,1536]{3,2,0,1:T(8,128)(2,1)}, u32[]{:S(2)}, u32[]{:S(2)}) %collective-permute-start.6) | collective-permute-done | bytes 393248 | tf_op jit(solution)/shard_map/ppermute | solution.py:60
  34.4 1.1 %convert_add_fusion.1 = f32[2,2,32,1536]{3,2,0,1:T(8,128)S(1)} fusion(bf16[2,2,32,1536]{3,2,0,1:T(8,128)(2,1)} %collective-permute-done.6, bf16[2,2,1,32,1536]{4,3,2,1,0:T(8,128)(2,1)S(1)} %get-tuple-element.13), kind=kLoop, calls=%fused_computation.26 | loop fusion | flops 589824 | bytes 1572864 | tf_op jit(solution)/shard_map/add | solution.py:61
  35.5 0.9 %copy-done.2 = f32[2,2,32,1536]{3,2,0,1:T(8,128)} copy-done((f32[2,2,32,1536]{3,2,0,1:T(8,128)}, f32[2,2,32,1536]{3,2,0,1:T(8,128)S(1)}, u32[]{:S(2)}) %copy-start.2) | copy-done | bytes 786456
  36.4 1.6 %collective-permute-start.7 = (bf16[2,32,1536]{2,1,0:T(8,128)(2,1)S(1)}, bf16[2,32,1536]{2,1,0:T(8,128)(2,1)}, u32[]{:S(2)}, u32[]{:S(2)}) collective-permute-start(bf16[2,32,1536]{2,1,0:T(8,128)(2,1)S(1)} %fusion.44), channel_id=1, source_target_pairs={{0,2},{1,3},{2,0},{3,1},{4,6},{5,7},{6,4},{7,5},{8,10},{9,11},{10,... | collective-permute-start | bytes 589832 | tf_op jit(solution)/shard_map/ppermute | solution.py:60
  37.9 5.6 %collective-permute-done.7 = bf16[2,32,1536]{2,1,0:T(8,128)(2,1)} collective-permute-done((bf16[2,32,1536]{2,1,0:T(8,128)(2,1)S(1)}, bf16[2,32,1536]{2,1,0:T(8,128)(2,1)}, u32[]{:S(2)}, u32[]{:S(2)}) %collective-permute-start.7) | collective-permute-done | bytes 196640 | tf_op jit(solution)/shard_map/ppermute | solution.py:60
  43.5 1.2 %fusion.39 = f32[2,32,1536]{2,1,0:T(8,128)S(1)} fusion(bf16[2,32,1536]{2,1,0:T(8,128)(2,1)} %collective-permute-done.7, f32[2,2,32,1536]{3,2,0,1:T(8,128)} %copy-done.2, s32[]{:T(128)S(6)} %select_n.108, bf16[2,128,1536]{2,1,0:T(8,128)(2,1)S(1)} %copy-done.1, s32[]{:T(128)S(6)} %select_n.92), kind=kLoop, calls=%fused_computation.49 | loop fusion | flops 393216 | bytes 1179656 | tf_op jit(solution)/shard_map/add | solution.py:184
  44.7 0.2 subtract_reduce_fusion.1
  45.0 0.1 bitcast_dynamic-update-slice_fusion.2
  45.2 1.6 %collective-permute-start.8 = (bf16[2,32,1536]{2,1,0:T(8,128)(2,1)S(1)}, bf16[2,32,1536]{2,1,0:T(8,128)(2,1)S(1)}, u32[]{:S(2)}, u32[]{:S(2)}) collective-permute-start(bf16[2,32,1536]{2,1,0:T(8,128)(2,1)S(1)} %get-tuple-element.10), channel_id=1, source_target_pairs={{0,2},{1,3},{2,0},{3,1},{4,6},{5,7},{6,4},{7,5},{8,10},{9,11},{10,... | collective-permute-start | bytes 589832 | tf_op jit(solution)/shard_map/ppermute | solution.py:72
  46.8 4.6 %collective-permute-done.8 = bf16[2,32,1536]{2,1,0:T(8,128)(2,1)S(1)} collective-permute-done((bf16[2,32,1536]{2,1,0:T(8,128)(2,1)S(1)}, bf16[2,32,1536]{2,1,0:T(8,128)(2,1)S(1)}, u32[]{:S(2)}, u32[]{:S(2)}) %collective-permute-start.8) | collective-permute-done | bytes 196640 | tf_op jit(solution)/shard_map/ppermute | solution.py:72
  51.6 1.6 %collective-permute-done.9 = bf16[2,2,32,1536]{3,2,1,0:T(8,128)(2,1)S(1)} collective-permute-done((bf16[2,2,32,1536]{3,2,1,0:T(8,128)(2,1)S(1)}, bf16[2,2,32,1536]{3,2,1,0:T(8,128)(2,1)S(1)}, u32[]{:S(2)}, u32[]{:S(2)}) %collective-permute-start.9) | collective-permute-done | bytes 393248 | tf_op jit(solution)/shard_map/ppermute | solution.py:72
  53.2 0.8 %fusion.7 = f32[2,2,128,384]{3,2,0,1:T(8,128)S(1)} fusion(bf16[2,128,1536,1]{2,1,3,0:T(8,128)(2,1)S(1)} %bitcast.133, bf16[2,1536,384]{2,1,0:T(8,128)(2,1)S(1)} %copy-done.8), kind=kOutput, calls=%fused_computation.14 | convolution fusion | flops 603979776 | bytes 3932160 | tf_op jit(solution)/shard_map/std,gdc->gstc/dot_general | solution.py:35
  54.2 1.3 %collective-permute-start.10 = (bf16[2,15,384]{2,1,0:T(8,128)(2,1)S(1)}, bf16[2,15,384]{2,1,0:T(8,128)(2,1)S(1)}, u32[]{:S(2)}, u32[]{:S(2)}) collective-permute-start(bf16[2,15,384]{2,1,0:T(8,128)(2,1)S(1)} %get-tuple-element.19), channel_id=1, source_target_pairs={{0,4},{4,8},{8,12},{1,5},{5,9},{9,13},{2,6},{6,10},{10,14},{3,7},{... | collective-permute-start | bytes 69128 | tf_op jit(solution)/shard_map/ppermute | solution.py:20
  55.5 1.3 %collective-permute-start.11 = (bf16[2,15,384]{2,1,0:T(8,128)(2,1)S(1)}, bf16[2,15,384]{2,1,0:T(8,128)(2,1)S(1)}, u32[]{:S(2)}, u32[]{:S(2)}) collective-permute-start(bf16[2,15,384]{2,1,0:T(8,128)(2,1)S(1)} %get-tuple-element.20), channel_id=1, source_target_pairs={{4,0},{8,4},{12,8},{5,1},{9,5},{13,9},{6,2},{10,6},{14,10},{7,3},{... | collective-permute-start | bytes 69128 | tf_op jit(solution)/shard_map/ppermute | solution.py:21
  56.8 0.2 collective-permute-done.10
  57.0 4.2 %collective-permute-done.11 = bf16[2,15,384]{2,1,0:T(8,128)(2,1)S(1)} collective-permute-done((bf16[2,15,384]{2,1,0:T(8,128)(2,1)S(1)}, bf16[2,15,384]{2,1,0:T(8,128)(2,1)S(1)}, u32[]{:S(2)}, u32[]{:S(2)}) %collective-permute-start.11) | collective-permute-done | bytes 23072 | tf_op jit(solution)/shard_map/ppermute | solution.py:21
  61.3 1.1 %fusion.42 = f32[2,128,384]{2,0,1:T(2,128)S(1)} fusion(bf16[2,158,384]{2,1,0:T(8,128)(2,1)S(1)} %pad_maximum_fusion.1, f32[31,1,384]{2,0,1:T(8,128)S(1)} %bitcast.137), kind=kOutput, calls=%fused_computation.62 | convolution fusion | flops 36569088 | bytes 683520 | tf_op jit(solution)/shard_map/conv_general_dilated | solution.py:193
  62.4 0.2 copy-done.9
  62.6 0.6 convolution_convert_fusion.1
  63.2 0.8 %constant_dynamic-slice_fusion.1 = (bf16[2,2,1,32,1536]{4,3,2,1,0:T(8,128)(2,1)}, bf16[2,2,1,32,1536]{4,3,2,1,0:T(8,128)(2,1)S(1)}) fusion(bf16[2,2,2,32,1536]{4,3,2,1,0:T(8,128)(2,1)S(1)} %bitcast.134, s32[]{:T(128)S(6)} %select_n.106, s32[]{:T(128)S(6)} %select_n.107), kind=kLoop, calls=%fused_computation.95 | loop fusion | bytes 1572872 | tf_op jit(solution)/shard_map/jit(dynamic_index_in_dim)/dynamic_slice | solution.py:58
  64.1 1.7 %collective-permute-done.12 = bf16[2,2,32,1536]{3,2,0,1:T(8,128)(2,1)S(1)} collective-permute-done((bf16[2,2,32,1536]{3,2,0,1:T(8,128)(2,1)S(1)}, bf16[2,2,32,1536]{3,2,0,1:T(8,128)(2,1)S(1)}, u32[]{:S(2)}, u32[]{:S(2)}) %collective-permute-start.12) | collective-permute-done | bytes 393248 | tf_op jit(solution)/shard_map/ppermute | solution.py:60
  65.8 0.7 copy-done.4
  66.5 1.2 %convert_add_fusion = f32[2,2,32,1536]{3,2,0,1:T(8,128)S(1)} fusion(bf16[2,2,32,1536]{3,2,0,1:T(8,128)(2,1)} %copy-done.4, bf16[2,2,1,32,1536]{4,3,2,1,0:T(8,128)(2,1)} %get-tuple-element.11), kind=kLoop, calls=%fused_computation.25 | loop fusion | flops 589824 | bytes 1572864 | tf_op jit(solution)/shard_map/add | solution.py:61
  67.8 1.6 %collective-permute-start.13 = (bf16[2,32,1536]{2,1,0:T(8,128)(2,1)S(1)}, bf16[2,32,1536]{2,1,0:T(8,128)(2,1)S(1)}, u32[]{:S(2)}, u32[]{:S(2)}) collective-permute-start(bf16[2,32,1536]{2,1,0:T(8,128)(2,1)S(1)} %fusion.45), channel_id=1, source_target_pairs={{0,2},{1,3},{2,0},{3,1},{4,6},{5,7},{6,4},{7,5},{8,10},{9,11},{10,... | collective-permute-start | bytes 589832 | tf_op jit(solution)/shard_map/ppermute | solution.py:60
  69.4 5.4 %collective-permute-done.13 = bf16[2,32,1536]{2,1,0:T(8,128)(2,1)S(1)} collective-permute-done((bf16[2,32,1536]{2,1,0:T(8,128)(2,1)S(1)}, bf16[2,32,1536]{2,1,0:T(8,128)(2,1)S(1)}, u32[]{:S(2)}, u32[]{:S(2)}) %collective-permute-start.13) | collective-permute-done | bytes 196640 | tf_op jit(solution)/shard_map/ppermute | solution.py:60
  74.8 0.8 %fusion.38 = bf16[2,32,1536]{2,1,0:T(8,128)(2,1)} fusion(f32[2,32,1536]{2,1,0:T(8,128)S(1)} %fusion.39, bf16[2,32,1536]{2,1,0:T(8,128)(2,1)S(1)} %collective-permute-done.13, f32[2,2,32,1536]{3,2,0,1:T(8,128)S(1)} %convert_add_fusion, s32[]{:T(128)S(6)} %select_n.108, bf16[1536]{0:T(1024)(128)(2,1)S(1)} %get-tuple-element.25, ...), kind=kLoop, calls=%fused_computation.47 | loop fusion | flops 884736 | bytes 1185860 | tf_op jit(solution)/shard_map/convert_element_type | solution.py:210
  (65 shorter events, 1.5 us)
Async XLA Ops:
  0.0 2.1 %copy-start = (bf16[3,1536,256]{2,1,0:T(8,128)(2,1)S(1)}, bf16[3,1536,256]{2,1,0:T(8,128)(2,1)}, u32[]{:S(2)}) copy-start(bf16[3,1536,256]{2,1,0:T(8,128)(2,1)} %param.15) | copy-start | bytes 7077892
  0.0 1.6 %copy-start.1 = (bf16[2,128,1536]{2,1,0:T(8,128)(2,1)S(1)}, bf16[2,128,1536]{2,1,0:T(8,128)(2,1)}, u32[]{:S(2)}) copy-start(bf16[2,128,1536]{2,1,0:T(8,128)(2,1)} %param.12) | copy-start | bytes 2359300
  0.0 2.1 %copy-start.11 = (f32[1536]{0:T(1024)S(1)}, f32[1536]{0:T(1024)}, u32[]{:S(2)}) copy-start(f32[1536]{0:T(1024)} %param.14) | copy-start | bytes 18436
  2.1 10.6 %copy-start.7 = (s32[2]{0:T(128)S(1)}, s32[2]{0:T(128)}, u32[]{:S(2)}) copy-start(s32[2]{0:T(128)} %param.13) | copy-start | bytes 28
  5.8 8.9 %collective-permute-start = (bf16[3,2,128,1,64]{2,4,1,3,0:T(8,128)(2,1)}, bf16[3,2,128,1,64]{2,4,1,3,0:T(8,128)(2,1)S(1)}, u32[]{:S(2)}, u32[]{:S(2)}) collective-permute-start(bf16[3,2,128,1,64]{2,4,1,3,0:T(8,128)(2,1)} %get-tuple-element.18), channel_id=1, source_target_pairs={{0,4},{4,8},{8,12},{12,0},{1,5},{5,9},{9,13},{13,1},{2,6},{6,10},{... | collective-permute-start | bytes 294920 | tf_op jit(solution)/shard_map/ppermute | solution.py:125
  8.8 9.4 %collective-permute-start.1 = (bf16[3,2,128,1,64]{2,4,1,3,0:T(8,128)(2,1)}, bf16[3,2,128,1,64]{2,4,1,3,0:T(8,128)(2,1)S(1)}, u32[]{:S(2)}, u32[]{:S(2)}) collective-permute-start(bf16[3,2,128,1,64]{2,4,1,3,0:T(8,128)(2,1)} %get-tuple-element.17), channel_id=1, source_target_pairs={{0,8},{4,12},{8,0},{12,4},{1,9},{5,13},{9,1},{13,5},{2,10},{6,14},... | collective-permute-start | bytes 294920 | tf_op jit(solution)/shard_map/ppermute | solution.py:125
  11.4 6.8 %collective-permute-start.2 = (bf16[3,2,128,1,64]{2,4,1,3,0:T(8,128)(2,1)}, bf16[3,2,128,1,64]{2,4,1,3,0:T(8,128)(2,1)S(1)}, u32[]{:S(2)}, u32[]{:S(2)}) collective-permute-start(bf16[3,2,128,1,64]{2,4,1,3,0:T(8,128)(2,1)} %get-tuple-element.16), channel_id=1, source_target_pairs={{0,12},{4,0},{8,4},{12,8},{1,13},{5,1},{9,5},{13,9},{2,14},{6,2},{... | collective-permute-start | bytes 294920 | tf_op jit(solution)/shard_map/ppermute | solution.py:125
  20.5 10.6 %copy-start.3 = (bf16[256,1536]{1,0:T(8,128)(2,1)S(1)}, bf16[256,1536]{1,0:T(8,128)(2,1)}, u32[]{:S(2)}) copy-start(bf16[256,1536]{1,0:T(8,128)(2,1)} %param.16) | copy-start | bytes 2359300
  21.2 5.2 %collective-permute-start.3 = (bf16[2,1,128,64]{2,3,0,1:T(8,128)(2,1)S(1)}, bf16[2,1,128,64]{2,3,0,1:T(8,128)(2,1)S(1)}, u32[]{:S(2)}, u32[]{:S(2)}) collective-permute-start(bf16[2,1,128,64]{2,3,0,1:T(8,128)(2,1)S(1)} %get-tuple-element.23), channel_id=1, source_target_pairs={{0,12},{4,0},{8,4},{12,8},{1,13},{5,1},{9,5},{13,9},{2,14},{6,2},{... | collective-permute-start | bytes 98312 | tf_op jit(solution)/shard_map/ppermute | solution.py:135
  24.8 5.0 %collective-permute-start.4 = (bf16[2,1,128,64]{2,3,0,1:T(8,128)(2,1)S(1)}, bf16[2,1,128,64]{2,3,0,1:T(8,128)(2,1)S(1)}, u32[]{:S(2)}, u32[]{:S(2)}) collective-permute-start(bf16[2,1,128,64]{2,3,0,1:T(8,128)(2,1)S(1)} %get-tuple-element.22), channel_id=1, source_target_pairs={{0,8},{4,12},{8,0},{12,4},{1,9},{5,13},{9,1},{13,5},{2,10},{6,14},... | collective-permute-start | bytes 98312 | tf_op jit(solution)/shard_map/ppermute | solution.py:135
  25.2 5.7 %collective-permute-start.5 = (bf16[2,1,128,64]{2,3,0,1:T(8,128)(2,1)S(1)}, bf16[2,1,128,64]{2,3,0,1:T(8,128)(2,1)S(1)}, u32[]{:S(2)}, u32[]{:S(2)}) collective-permute-start(bf16[2,1,128,64]{2,3,0,1:T(8,128)(2,1)S(1)} %get-tuple-element.21), channel_id=1, source_target_pairs={{0,4},{4,8},{8,12},{12,0},{1,5},{5,9},{9,13},{13,1},{2,6},{6,10},{... | collective-permute-start | bytes 98312 | tf_op jit(solution)/shard_map/ppermute | solution.py:135
  32.3 12.7 %copy-start.5 = (f32[1536]{0:T(1024)S(1)}, f32[1536]{0:T(1024)}, u32[]{:S(2)}) copy-start(f32[1536]{0:T(1024)} %param.17) | copy-start | bytes 18436
  32.3 2.1 %collective-permute-start.6 = (bf16[2,2,32,1536]{3,2,0,1:T(8,128)(2,1)}, bf16[2,2,32,1536]{3,2,0,1:T(8,128)(2,1)}, u32[]{:S(2)}, u32[]{:S(2)}) collective-permute-start(bf16[2,2,32,1536]{3,2,0,1:T(8,128)(2,1)} %bitcast.130), channel_id=1, source_target_pairs={{0,1},{1,0},{2,3},{3,2},{4,5},{5,4},{6,7},{7,6},{8,9},{9,8},{10,11... | collective-permute-start | bytes 1179656 | tf_op jit(solution)/shard_map/ppermute | solution.py:60
  35.5 0.9 %copy-start.2 = (f32[2,2,32,1536]{3,2,0,1:T(8,128)}, f32[2,2,32,1536]{3,2,0,1:T(8,128)S(1)}, u32[]{:S(2)}) copy-start(f32[2,2,32,1536]{3,2,0,1:T(8,128)S(1)} %convert_add_fusion.1) | copy-start | bytes 2359300
  36.4 7.1 %collective-permute-start.7 = (bf16[2,32,1536]{2,1,0:T(8,128)(2,1)S(1)}, bf16[2,32,1536]{2,1,0:T(8,128)(2,1)}, u32[]{:S(2)}, u32[]{:S(2)}) collective-permute-start(bf16[2,32,1536]{2,1,0:T(8,128)(2,1)S(1)} %fusion.44), channel_id=1, source_target_pairs={{0,2},{1,3},{2,0},{3,1},{4,6},{5,7},{6,4},{7,5},{8,10},{9,11},{10,... | collective-permute-start | bytes 589832 | tf_op jit(solution)/shard_map/ppermute | solution.py:60
  44.7 8.5 %copy-start.8 = (bf16[2,1536,384]{2,1,0:T(8,128)(2,1)S(1)}, bf16[2,1536,384]{2,1,0:T(8,128)(2,1)}, u32[]{:S(2)}) copy-start(bf16[2,1536,384]{2,1,0:T(8,128)(2,1)} %param.18) | copy-start | bytes 7077892
  45.2 6.2 %collective-permute-start.8 = (bf16[2,32,1536]{2,1,0:T(8,128)(2,1)S(1)}, bf16[2,32,1536]{2,1,0:T(8,128)(2,1)S(1)}, u32[]{:S(2)}, u32[]{:S(2)}) collective-permute-start(bf16[2,32,1536]{2,1,0:T(8,128)(2,1)S(1)} %get-tuple-element.10), channel_id=1, source_target_pairs={{0,2},{1,3},{2,0},{3,1},{4,6},{5,7},{6,4},{7,5},{8,10},{9,11},{10,... | collective-permute-start | bytes 589832 | tf_op jit(solution)/shard_map/ppermute | solution.py:72
  51.4 1.8 %collective-permute-start.9 = (bf16[2,2,32,1536]{3,2,1,0:T(8,128)(2,1)S(1)}, bf16[2,2,32,1536]{3,2,1,0:T(8,128)(2,1)S(1)}, u32[]{:S(2)}, u32[]{:S(2)}) collective-permute-start(bf16[2,2,32,1536]{3,2,1,0:T(8,128)(2,1)S(1)} %bitcast_dynamic-update-slice_fusion.3), channel_id=1, source_target_pairs={{0,1},{1,0},{2,3},{3,2},{4,5},{5,4},{6,7},{7,6},{8,9},{9,8},{10,11... | collective-permute-start | bytes 1179656 | tf_op jit(solution)/shard_map/ppermute | solution.py:72
  53.2 8.1 %copy-start.10 = (f32[31,384]{1,0:T(8,128)S(1)}, f32[31,384]{1,0:T(8,128)}, u32[]{:S(2)}) copy-start(f32[31,384]{1,0:T(8,128)} %param.19) | copy-start | bytes 142852
  54.2 2.8 %collective-permute-start.10 = (bf16[2,15,384]{2,1,0:T(8,128)(2,1)S(1)}, bf16[2,15,384]{2,1,0:T(8,128)(2,1)S(1)}, u32[]{:S(2)}, u32[]{:S(2)}) collective-permute-start(bf16[2,15,384]{2,1,0:T(8,128)(2,1)S(1)} %get-tuple-element.19), channel_id=1, source_target_pairs={{0,4},{4,8},{8,12},{1,5},{5,9},{9,13},{2,6},{6,10},{10,14},{3,7},{... | collective-permute-start | bytes 69128 | tf_op jit(solution)/shard_map/ppermute | solution.py:20
  55.5 5.7 %collective-permute-start.11 = (bf16[2,15,384]{2,1,0:T(8,128)(2,1)S(1)}, bf16[2,15,384]{2,1,0:T(8,128)(2,1)S(1)}, u32[]{:S(2)}, u32[]{:S(2)}) collective-permute-start(bf16[2,15,384]{2,1,0:T(8,128)(2,1)S(1)} %get-tuple-element.20), channel_id=1, source_target_pairs={{4,0},{8,4},{12,8},{5,1},{9,5},{13,9},{6,2},{10,6},{14,10},{7,3},{... | collective-permute-start | bytes 69128 | tf_op jit(solution)/shard_map/ppermute | solution.py:21
  61.3 1.3 %copy-start.9 = (bf16[384,1536]{1,0:T(8,128)(2,1)S(1)}, bf16[384,1536]{1,0:T(8,128)(2,1)}, u32[]{:S(2)}) copy-start(bf16[384,1536]{1,0:T(8,128)(2,1)} %param.22) | copy-start | bytes 3538948
  61.3 1.3 %copy-start.12 = (f32[384]{0:T(512)S(1)}, f32[384]{0:T(512)}, u32[]{:S(2)}) copy-start(f32[384]{0:T(512)} %param.21) | copy-start | bytes 4612
  61.3 1.3 %copy-start.13 = (f32[384]{0:T(512)S(1)}, f32[384]{0:T(512)}, u32[]{:S(2)}) copy-start(f32[384]{0:T(512)} %param.20) | copy-start | bytes 4612
  62.6 1.5 %copy-start.6 = (s32[1536]{0:T(1024)S(1)}, s32[1536]{0:T(1024)}, u32[]{:S(2)}) copy-start(s32[1536]{0:T(1024)} %param.23) | copy-start | bytes 18436
  64.0 1.8 %collective-permute-start.12 = (bf16[2,2,32,1536]{3,2,0,1:T(8,128)(2,1)S(1)}, bf16[2,2,32,1536]{3,2,0,1:T(8,128)(2,1)S(1)}, u32[]{:S(2)}, u32[]{:S(2)}) collective-permute-start(bf16[2,2,32,1536]{3,2,0,1:T(8,128)(2,1)S(1)} %bitcast.136), channel_id=1, source_target_pairs={{0,1},{1,0},{2,3},{3,2},{4,5},{5,4},{6,7},{7,6},{8,9},{9,8},{10,11... | collective-permute-start | bytes 1179656 | tf_op jit(solution)/shard_map/ppermute | solution.py:60
  65.8 0.7 copy-start.4
  67.8 7.0 %collective-permute-start.13 = (bf16[2,32,1536]{2,1,0:T(8,128)(2,1)S(1)}, bf16[2,32,1536]{2,1,0:T(8,128)(2,1)S(1)}, u32[]{:S(2)}, u32[]{:S(2)}) collective-permute-start(bf16[2,32,1536]{2,1,0:T(8,128)(2,1)S(1)} %fusion.45), channel_id=1, source_target_pairs={{0,2},{1,3},{2,0},{3,1},{4,6},{5,7},{6,4},{7,5},{8,10},{9,11},{10,... | collective-permute-start | bytes 589832 | tf_op jit(solution)/shard_map/ppermute | solution.py:60

commit v13 on v9

--- a/solution.py
+++ b/solution.py
@@ -45,13 +45,13 @@
     return bits
 
 
-def reduce_scatter_rows(x, axis, dim):
+def reduce_scatter_rows(x, axis, dim, first_bit=0):
     count, rank = lax.axis_size(axis), lax.axis_index(axis)
     bits = bit_count(count)
     shape = x.shape
-    block = shape[dim] // count
-    acc = x.reshape(shape[:dim] + (2,) * bits + (block,) + shape[dim + 1 :])
-    for b in range(bits):
+    block = shape[dim] // (count >> first_bit)
+    acc = x.reshape(shape[:dim] + (2,) * (bits - first_bit) + (block,) + shape[dim + 1 :])
+    for b in range(first_bit, bits):
         bit_axis = dim + bits - 1 - b
         mine = (rank >> b) & 1
         keep = lax.dynamic_index_in_dim(acc, mine, bit_axis, keepdims=False)
@@ -59,6 +59,25 @@
         got = lax.ppermute(send.astype(jnp.bfloat16), axis, xor_pairs(count, 1 << b))
         acc = keep.astype(jnp.float32) + got.astype(jnp.float32)
     return acc
+
+
+def project_and_reduce(inputs, weights, pair_weights, axis):
+    count, rank = lax.axis_size(axis), lax.axis_index(axis)
+    records, frames, channels = inputs.shape
+    pair_inputs = lax.ppermute(inputs, axis, xor_pairs(count, 1))
+    mine = rank & 1
+
+    def kept_rows(rows):
+        rows = rows.reshape(records, count // 2, 2, frames // count, channels)
+        return lax.dynamic_index_in_dim(rows, mine, 2, keepdims=False)
+
+    part = jnp.einsum(
+        "sbrc,cd->sbrd", kept_rows(inputs), weights, preferred_element_type=jnp.float32
+    ) + jnp.einsum(
+        "sbrc,cd->sbrd", kept_rows(pair_inputs), pair_weights, preferred_element_type=jnp.float32
+    )
+    part = part.astype(jnp.bfloat16).reshape(records, frames // 2, part.shape[-1])
+    return reduce_scatter_rows(part, axis, 1, first_bit=1)
 
 
 def all_gather_rows(x, axis, dim):
@@ -173,12 +192,13 @@
         value_heads = value_heads.transpose(1, 0, 2, 3, 4).reshape(records, -1, head_count, HEAD_DIM)
         attended = attend(query_heads, key_heads, value_heads, positions.reshape(-1), frame_counts)
         attended = attended.transpose(0, 2, 1, 3).reshape(records, frames_here, head_count * HEAD_DIM)
-    attn_part = jnp.einsum("stc,cd->std", attended, w_out, preferred_element_type=jnp.float32)
+    w_out_pair = lax.ppermute(w_out, "mp", xor_pairs(lax.axis_size("mp"), 1))
+    w_pw_pair = lax.ppermute(w_pw, "mp", xor_pairs(lax.axis_size("mp"), 1))
     mp_count = lax.axis_size("mp")
     mp_rank = lax.axis_index("mp")
     rows_mine = frames_here // mp_count
     row_start = mp_rank * rows_mine
-    attn_mine = reduce_scatter_rows(attn_part.astype(jnp.bfloat16), "mp", 1)
+    attn_mine = project_and_reduce(attended, w_out, w_out_pair, "mp")
     features_mine = lax.dynamic_slice_in_dim(features, row_start, rows_mine, 1)
     residual_mine = features_mine.astype(jnp.float32) + attn_mine
     normed_mine = layer_norm(residual_mine, conv_gain).astype(jnp.bfloat16)
@@ -199,8 +219,7 @@
         precision=lax.Precision.HIGHEST,
     )
     activated = jax.nn.silu(depthwise * bn_scale + bn_shift).astype(jnp.bfloat16)
-    conv_part = jnp.einsum("stc,cd->std", activated, w_pw, preferred_element_type=jnp.float32)
-    conv_rows = reduce_scatter_rows(conv_part.astype(jnp.bfloat16), "mp", 1)
+    conv_rows = project_and_reduce(activated, w_pw, w_pw_pair, "mp")
     combined = residual_mine + conv_rows
     clip_bound = clip_level.astype(jnp.float32) / 16.0
     clipped = jnp.clip(combined, -clip_bound, clip_bound)

time: 71.6 us -> 71.5 us (level)
  matrix products: 6.24 us -> 11.7 us
  other arithmetic: 8.42 us -> 5.31 us
  waiting for transfers between devices: 35.6 us -> 33 us
    dot_general x2 -> x4, matrix products: 0.97 us -> 6.03 us  [the longest x2 3.31 us: project_and_reduce(): jnp.einsum('sbrc,cd->sbrd', kept_rows(pair_inputs), pair_weights, preferr...]
    ppermute x4 -> x2, waiting for transfers between devices: 14.4 us -> 11.1 us  [reduce_scatter_rows(): lax.ppermute(send.astype(jnp.bfloat16), axis, xor_pairs(count, 1 << b))]
    add x2 -> x0, other arithmetic: 2.18 us -> none  [reduce_scatter_rows(): acc = keep.astype(jnp.float32) + got.astype(jnp.float32)]
    reduce_sum x2, other arithmetic: 2.63 us -> 1.61 us  [layer_norm(): centre = jnp.mean(values, axis=-1, keepdims=True)]
    ppermute x0 -> x4, waiting for transfers between devices: none -> 0.97 us  [the longest x2 0.96 us: project_and_reduce(): pair_inputs = lax.ppermute(inputs, axis, xor_pairs(count, 1))]
    unnamed x29 -> x33, local copies, waits for them, and re-layouts: 1.04 us -> 0.14 us
    ppermute x4 -> x2, starting transfers between devices: 3.25 us -> 3.12 us  [reduce_scatter_rows(): lax.ppermute(send.astype(jnp.bfloat16), axis, xor_pairs(count, 1 << b))]
  transfers between devices with their start and end apart: 14 -> 16, of which waited for: 13 -> 12; matrix products, arithmetic and copies ran while one was open for 1% -> 15% of each run, Pallas kernels for 0% -> 0%
where the time goes in v13:
time: 71.5 us; the launch traced here: 71.2 us
  waiting for transfers between devices  33 us (46%)
  starting transfers between devices  19.3 us (27%)
  matrix products  11.7 us (16%)
  other arithmetic  5.31 us (7%)
  local copies, waits for them, and re-layouts  1.36 us (2%)
    ppermute x2, waiting for transfers between devices, reduce_scatter_rows(): lax.ppermute(send.astype(jnp.bfloat16), axis, xor_pairs(count, 1 << b))  11.1 us
    ppermute x3, starting transfers between devices, attend_by_heads(): pieces.append(lax.ppermute(send, axis, pairs))  7.01 us
    ppermute x2, waiting for transfers between devices, all_gather_rows(): got = lax.ppermute(acc, axis, xor_pairs(count, 1 << b))  6.47 us
    ppermute x3, waiting for transfers between devices, attend_by_heads(): back.append(lax.ppermute(rows, axis, pairs))  5.45 us
    ppermute x3, waiting for transfers between devices, attend_by_heads(): pieces.append(lax.ppermute(send, axis, pairs))  4.64 us
    ppermute x3, starting transfers between devices, attend_by_heads(): back.append(lax.ppermute(rows, axis, pairs))  4.3 us
    ppermute x1, waiting for transfers between devices, with_halo(): after = lax.ppermute(initial, axis, down)  4.22 us
    dot_general x2, matrix products, project_and_reduce(): jnp.einsum('sbrc,cd->sbrd', kept_rows(pair_inputs), pair_weights, preferr...  3.31 us
  transfers between devices with their start and end apart: 16, of which 12 were waited for; matrix products, arithmetic and copies ran while one was open for 15% of the time, Pallas kernels for 0%

profile of v13, /device:TPU:0, one launch (start us, length us, event | category | flops | bytes accessed | tf_op | source)
XLA Modules:
  0.0 71.2 jit_solution(12038279257183502887)
XLA Ops:
  0.0 1.5 %convert_reduce_fusion = f32[2,128]{1,0:T(2,128)S(1)} fusion(bf16[2,128,1536]{2,1,0:T(8,128)(2,1)} %param.12), kind=kLoop, calls=%fused_computation.11 | loop fusion | flops 786176 | bytes 787456 | tf_op jit(solution)/shard_map/reduce_sum | solution.py:27
  1.5 1.5 %fusion.11 = f32[2,128]{1,0:T(2,128)S(1)} fusion(bf16[2,128,1536]{2,1,0:T(8,128)(2,1)} %param.12, f32[2,128]{1,0:T(2,128)S(1)} %broadcast_multiply_fusion.1), kind=kLoop, calls=%fused_computation.17 | loop fusion | flops 1572608 | bytes 788480 | tf_op jit(solution)/shard_map/reduce_sum | solution.py:29
  3.0 2.0 %fusion.20 = bf16[3,2,128,256]{3,2,0,1:T(8,128)(2,1)S(1)} fusion(bf16[3,1536,256]{2,1,0:T(8,128)(2,1)S(1)} %copy-done, bf16[2,128,1536]{2,1,0:T(8,128)(2,1)} %param.12, f32[1536]{0:T(1024)} %param.14, f32[2,128]{1,0:T(2,128)S(1)} %add_rsqrt_fusion.1, f32[2,128]{1,0:T(2,128)S(1)} %broadcast_multiply_fusion.1), kind=kOutput, calls=%fused_computation.22 | convolution fusion | flops 606142464 | bytes 3547136 | tf_op jit(solution)/shard_map/std,idc->istc/dot_general | solution.py:179
  5.0 0.2 copy.24
  5.3 3.1 %collective-permute-start = (bf16[3,2,128,1,64]{2,4,1,3,0:T(8,128)(2,1)S(1)}, bf16[3,2,128,1,64]{2,4,1,3,0:T(8,128)(2,1)S(1)}, u32[]{:S(2)}, u32[]{:S(2)}) collective-permute-start(bf16[3,2,128,1,64]{2,4,1,3,0:T(8,128)(2,1)S(1)} %get-tuple-element.10), channel_id=1, source_target_pairs={{0,4},{4,8},{8,12},{12,0},{1,5},{5,9},{9,13},{13,1},{2,6},{6,10},{... | collective-permute-start | bytes 294920 | tf_op jit(solution)/shard_map/ppermute | solution.py:143
  8.4 2.6 %collective-permute-start.1 = (bf16[3,2,128,1,64]{2,4,1,3,0:T(8,128)(2,1)S(1)}, bf16[3,2,128,1,64]{2,4,1,3,0:T(8,128)(2,1)S(1)}, u32[]{:S(2)}, u32[]{:S(2)}) collective-permute-start(bf16[3,2,128,1,64]{2,4,1,3,0:T(8,128)(2,1)S(1)} %get-tuple-element.9), channel_id=1, source_target_pairs={{0,8},{4,12},{8,0},{12,4},{1,9},{5,13},{9,1},{13,5},{2,10},{6,14},... | collective-permute-start | bytes 294920 | tf_op jit(solution)/shard_map/ppermute | solution.py:143
  10.9 1.3 %collective-permute-start.2 = (bf16[3,2,128,1,64]{2,4,1,3,0:T(8,128)(2,1)S(1)}, bf16[3,2,128,1,64]{2,4,1,3,0:T(8,128)(2,1)S(1)}, u32[]{:S(2)}, u32[]{:S(2)}) collective-permute-start(bf16[3,2,128,1,64]{2,4,1,3,0:T(8,128)(2,1)S(1)} %get-tuple-element.8), channel_id=1, source_target_pairs={{0,12},{4,0},{8,4},{12,8},{1,13},{5,1},{9,5},{13,9},{2,14},{6,2},{... | collective-permute-start | bytes 294920 | tf_op jit(solution)/shard_map/ppermute | solution.py:143
  12.3 0.5 collective-permute-start.14
  12.9 0.1 broadcast_compare_fusion
  12.9 1.1 %collective-permute-done = bf16[3,2,128,1,64]{2,4,1,3,0:T(8,128)(2,1)S(1)} collective-permute-done((bf16[3,2,128,1,64]{2,4,1,3,0:T(8,128)(2,1)S(1)}, bf16[3,2,128,1,64]{2,4,1,3,0:T(8,128)(2,1)S(1)}, u32[]{:S(2)}, u32[]{:S(2)}) %collective-permute-start) | collective-permute-done | bytes 98336 | tf_op jit(solution)/shard_map/ppermute | solution.py:143
  14.0 3.5 %collective-permute-done.1 = bf16[3,2,128,1,64]{2,4,1,3,0:T(8,128)(2,1)S(1)} collective-permute-done((bf16[3,2,128,1,64]{2,4,1,3,0:T(8,128)(2,1)S(1)}, bf16[3,2,128,1,64]{2,4,1,3,0:T(8,128)(2,1)S(1)}, u32[]{:S(2)}, u32[]{:S(2)}) %collective-permute-start.1) | collective-permute-done | bytes 98336 | tf_op jit(solution)/shard_map/ppermute | solution.py:143
  17.6 0.8 %fusion.8 = (f32[2,512]{1,0:T(2,128)S(1)}, f32[2,512,512]{1,2,0:T(8,128)S(1)}) fusion(pred[2,512]{1,0:T(4,128)(4,1)S(1)} %broadcast_compare_fusion, bf16[3,2,512,1,64]{2,4,1,3,0:T(8,128)(2,1)S(1)} %pad_maximum_fusion), kind=kOutput, calls=%fused_computation.14 | convolution fusion | flops 68680704 | bytes 2365440 | tf_op jit(solution)/shard_map/sqhe,skhe->shqk/dot_general | solution.py:115
  18.4 0.5 fusion.9
  18.9 0.6 fusion.27
  19.6 3.6 %collective-permute-start.3 = (bf16[2,1,128,64]{2,3,0,1:T(8,128)(2,1)S(1)}, bf16[2,1,128,64]{2,3,0,1:T(8,128)(2,1)S(1)}, u32[]{:S(2)}, u32[]{:S(2)}) collective-permute-start(bf16[2,1,128,64]{2,3,0,1:T(8,128)(2,1)S(1)} %get-tuple-element.15), channel_id=1, source_target_pairs={{0,12},{4,0},{8,4},{12,8},{1,13},{5,1},{9,5},{13,9},{2,14},{6,2},{... | collective-permute-start | bytes 98312 | tf_op jit(solution)/shard_map/ppermute | solution.py:153
  23.2 0.4 collective-permute-start.4
  23.7 0.2 collective-permute-start.5
  23.9 0.9 %collective-permute-done.3 = bf16[2,1,128,64]{2,3,0,1:T(8,128)(2,1)S(1)} collective-permute-done((bf16[2,1,128,64]{2,3,0,1:T(8,128)(2,1)S(1)}, bf16[2,1,128,64]{2,3,0,1:T(8,128)(2,1)S(1)}, u32[]{:S(2)}, u32[]{:S(2)}) %collective-permute-start.3) | collective-permute-done | bytes 32800 | tf_op jit(solution)/shard_map/ppermute | solution.py:153
  24.9 3.4 %collective-permute-done.4 = bf16[2,1,128,64]{2,3,0,1:T(8,128)(2,1)S(1)} collective-permute-done((bf16[2,1,128,64]{2,3,0,1:T(8,128)(2,1)S(1)}, bf16[2,1,128,64]{2,3,0,1:T(8,128)(2,1)S(1)}, u32[]{:S(2)}, u32[]{:S(2)}) %collective-permute-start.4) | collective-permute-done | bytes 32800 | tf_op jit(solution)/shard_map/ppermute | solution.py:153
  28.2 1.2 %collective-permute-done.5 = bf16[2,1,128,64]{2,3,0,1:T(8,128)(2,1)S(1)} collective-permute-done((bf16[2,1,128,64]{2,3,0,1:T(8,128)(2,1)S(1)}, bf16[2,1,128,64]{2,3,0,1:T(8,128)(2,1)S(1)}, u32[]{:S(2)}, u32[]{:S(2)}) %collective-permute-start.5) | collective-permute-done | bytes 32800 | tf_op jit(solution)/shard_map/ppermute | solution.py:153
  29.5 0.2 copy.26
  29.7 0.2 reshape_reshape.3
  30.0 2.4 %fusion.36 = f32[2,2,32,1536]{3,2,1,0:T(8,128)} fusion(bf16[256,1536]{1,0:T(8,128)(2,1)} %param.16, bf16[2,2,2,32,256]{4,3,2,1,0:T(8,128)(2,1)S(1)} %reshape_reshape.3, s32[]{:T(128)S(6)} %select_n.109), kind=kOutput, calls=%fused_computation.36 | convolution fusion | flops 100663296 | bytes 1638404 | tf_op jit(solution)/shard_map/sbrc,cd->sbrd/dot_general | solution.py:74
  32.4 0.1 copy.28
  32.5 1.7 %fusion = bf16[2,2,32,1536]{3,2,1,0:T(8,128)(2,1)S(1)} fusion(f32[2,2,32,1536]{3,2,1,0:T(8,128)} %fusion.36, bf16[256,1536]{1,0:T(8,128)(2,1)} %collective-permute-done.7, bf16[2,2,2,32,256]{4,3,2,1,0:T(8,128)(2,1)S(1)} %bitcast.140, s32[]{:T(128)S(6)} %select_n.109), kind=kOutput, calls=%fused_computation.2 | convolution fusion | flops 101056512 | bytes 2031620 | tf_op jit(solution)/shard_map/sbrc,cd->sbrd/dot_general | solution.py:76
  34.2 1.6 %collective-permute-start.8 = (bf16[2,32,1536]{2,1,0:T(8,128)(2,1)S(1)}, bf16[2,32,1536]{2,1,0:T(8,128)(2,1)S(1)}, u32[]{:S(2)}, u32[]{:S(2)}) collective-permute-start(bf16[2,32,1536]{2,1,0:T(8,128)(2,1)S(1)} %dynamic-slice_bitcast_fusion.1), channel_id=1, source_target_pairs={{0,2},{1,3},{2,0},{3,1},{4,6},{5,7},{6,4},{7,5},{8,10},{9,11},{10,... | collective-permute-start | bytes 589832 | tf_op jit(solution)/shard_map/ppermute | solution.py:59
  35.8 5.7 %collective-permute-done.8 = bf16[2,32,1536]{2,1,0:T(8,128)(2,1)S(1)} collective-permute-done((bf16[2,32,1536]{2,1,0:T(8,128)(2,1)S(1)}, bf16[2,32,1536]{2,1,0:T(8,128)(2,1)S(1)}, u32[]{:S(2)}, u32[]{:S(2)}) %collective-permute-start.8) | collective-permute-done | bytes 196640 | tf_op jit(solution)/shard_map/ppermute | solution.py:59
  41.5 0.1 fusion.69
  41.7 0.2 multiply_reduce_fusion
  42.0 0.1 bitcast_dynamic-update-slice_fusion.3
  42.1 1.6 %collective-permute-start.9 = (bf16[2,32,1536]{2,1,0:T(8,128)(2,1)S(1)}, bf16[2,32,1536]{2,1,0:T(8,128)(2,1)S(1)}, u32[]{:S(2)}, u32[]{:S(2)}) collective-permute-start(bf16[2,32,1536]{2,1,0:T(8,128)(2,1)S(1)} %get-tuple-element.6), channel_id=1, source_target_pairs={{0,2},{1,3},{2,0},{3,1},{4,6},{5,7},{6,4},{7,5},{8,10},{9,11},{10,... | collective-permute-start | bytes 589832 | tf_op jit(solution)/shard_map/ppermute | solution.py:90
  43.7 0.1 broadcast_compare_fusion.1
  43.7 4.9 %collective-permute-done.9 = bf16[2,32,1536]{2,1,0:T(8,128)(2,1)S(1)} collective-permute-done((bf16[2,32,1536]{2,1,0:T(8,128)(2,1)S(1)}, bf16[2,32,1536]{2,1,0:T(8,128)(2,1)S(1)}, u32[]{:S(2)}, u32[]{:S(2)}) %collective-permute-start.9) | collective-permute-done | bytes 196640 | tf_op jit(solution)/shard_map/ppermute | solution.py:90
  48.8 1.6 %collective-permute-done.10 = bf16[2,2,32,1536]{3,2,1,0:T(8,128)(2,1)S(1)} collective-permute-done((bf16[2,2,32,1536]{3,2,1,0:T(8,128)(2,1)S(1)}, bf16[2,2,32,1536]{3,2,1,0:T(8,128)(2,1)S(1)}, u32[]{:S(2)}, u32[]{:S(2)}) %collective-permute-start.10) | collective-permute-done | bytes 393248 | tf_op jit(solution)/shard_map/ppermute | solution.py:90
  50.5 0.8 %fusion.14 = f32[2,2,128,384]{3,2,0,1:T(8,128)S(1)} fusion(bf16[2,128,1536,1]{2,1,3,0:T(8,128)(2,1)S(1)} %bitcast.139, bf16[2,1536,384]{2,1,0:T(8,128)(2,1)S(1)} %copy-done.9), kind=kOutput, calls=%fused_computation.20 | convolution fusion | flops 603979776 | bytes 3932160 | tf_op jit(solution)/shard_map/std,gdc->gstc/dot_general | solution.py:34
  51.3 0.1 bitcast_select_fusion
  51.5 1.3 %collective-permute-start.11 = (bf16[2,15,384]{2,1,0:T(8,128)(2,1)S(1)}, bf16[2,15,384]{2,1,0:T(8,128)(2,1)S(1)}, u32[]{:S(2)}, u32[]{:S(2)}) collective-permute-start(bf16[2,15,384]{2,1,0:T(8,128)(2,1)S(1)} %get-tuple-element.11), channel_id=1, source_target_pairs={{0,4},{4,8},{8,12},{1,5},{5,9},{9,13},{2,6},{6,10},{10,14},{3,7},{... | collective-permute-start | bytes 69128 | tf_op jit(solution)/shard_map/ppermute | solution.py:20
  52.8 1.3 %collective-permute-start.12 = (bf16[2,15,384]{2,1,0:T(8,128)(2,1)S(1)}, bf16[2,15,384]{2,1,0:T(8,128)(2,1)S(1)}, u32[]{:S(2)}, u32[]{:S(2)}) collective-permute-start(bf16[2,15,384]{2,1,0:T(8,128)(2,1)S(1)} %get-tuple-element.12), channel_id=1, source_target_pairs={{4,0},{8,4},{12,8},{5,1},{9,5},{13,9},{6,2},{10,6},{14,10},{7,3},{... | collective-permute-start | bytes 69128 | tf_op jit(solution)/shard_map/ppermute | solution.py:21
  54.1 0.2 collective-permute-done.11
  54.3 4.2 %collective-permute-done.12 = bf16[2,15,384]{2,1,0:T(8,128)(2,1)S(1)} collective-permute-done((bf16[2,15,384]{2,1,0:T(8,128)(2,1)S(1)}, bf16[2,15,384]{2,1,0:T(8,128)(2,1)S(1)}, u32[]{:S(2)}, u32[]{:S(2)}) %collective-permute-start.12) | collective-permute-done | bytes 23072 | tf_op jit(solution)/shard_map/ppermute | solution.py:21
  58.6 1.5 %fusion.51 = bf16[2,128,384]{2,0,1:T(2,128)(2,1)S(1)} fusion(bf16[2,158,384]{2,1,0:T(8,128)(2,1)S(1)} %pad_maximum_fusion.1, f32[384]{0:T(512)S(1)} %copy-done.11, f32[384]{0:T(512)S(1)} %copy-done.12, f32[31,1,384]{2,0,1:T(8,128)S(1)} %bitcast.144), kind=kOutput, calls=%fused_computation.58 | convolution fusion | flops 37257216 | bytes 489984 | tf_op jit(solution)/shard_map/conv_general_dilated | solution.py:212
  60.1 0.1 dynamic-slice_bitcast_fusion.4
  60.2 0.4 fusion.24
  60.6 1.0 %collective-permute-done.13 = bf16[2,128,384]{2,0,1:T(2,128)(2,1)S(1)} collective-permute-done((bf16[2,128,384]{2,0,1:T(2,128)(2,1)S(1)}, bf16[2,128,384]{2,0,1:T(2,128)(2,1)S(1)}, u32[]{:S(2)}, u32[]{:S(2)}) %collective-permute-start.13) | collective-permute-done | bytes 196640 | tf_op jit(solution)/shard_map/ppermute | solution.py:67
  61.6 1.7 %fusion.1 = bf16[2,2,32,1536]{3,2,0,1:T(8,128)(2,1)S(1)} fusion(f32[2,2,32,1536]{3,2,0,1:T(8,128)S(1)} %fusion.24, bf16[384,1536]{1,0:T(8,128)(2,1)} %collective-permute-done.14, bf16[2,2,32,384]{3,0,2,1:T(2,128)(2,1)S(1)} %dynamic-slice_bitcast_fusion.3), kind=kOutput, calls=%fused_computation.3 | convolution fusion | flops 151388160 | bytes 2457600 | tf_op jit(solution)/shard_map/sbrc,cd->sbrd/dot_general | solution.py:76
  63.3 1.6 %collective-permute-start.15 = (bf16[2,32,1536]{2,1,0:T(8,128)(2,1)S(1)}, bf16[2,32,1536]{2,1,0:T(8,128)(2,1)S(1)}, u32[]{:S(2)}, u32[]{:S(2)}) collective-permute-start(bf16[2,32,1536]{2,1,0:T(8,128)(2,1)S(1)} %dynamic-slice_bitcast_fusion), channel_id=1, source_target_pairs={{0,2},{1,3},{2,0},{3,1},{4,6},{5,7},{6,4},{7,5},{8,10},{9,11},{10,... | collective-permute-start | bytes 589832 | tf_op jit(solution)/shard_map/ppermute | solution.py:59
  65.0 5.4 %collective-permute-done.15 = bf16[2,32,1536]{2,1,0:T(8,128)(2,1)S(1)} collective-permute-done((bf16[2,32,1536]{2,1,0:T(8,128)(2,1)S(1)}, bf16[2,32,1536]{2,1,0:T(8,128)(2,1)S(1)}, u32[]{:S(2)}, u32[]{:S(2)}) %collective-permute-start.15) | collective-permute-done | bytes 196640 | tf_op jit(solution)/shard_map/ppermute | solution.py:59
  70.3 0.8 %fusion.49 = bf16[2,32,1536]{2,1,0:T(8,128)(2,1)} fusion(bf16[2,32,1536]{2,1,0:T(8,128)(2,1)S(1)} %collective-permute-done.15, bf16[2,2,32,1536]{3,2,0,1:T(8,128)(2,1)S(1)} %fusion.1, s32[]{:T(128)S(6)} %select_n.110, bf16[1536]{0:T(1024)(128)(2,1)S(1)} %get-tuple-element.17, bf16[1536]{0:T(1024)(128)(2,1)S(1)} %get-tuple-element.16, ...), kind=kLoop, calls=%fused_computation.53 | loop fusion | flops 1474560 | bytes 1185864 | tf_op jit(solution)/shard_map/convert_element_type | solution.py:228
  (68 shorter events, 1.0 us)
Async XLA Ops:
  0.0 3.0 %copy-start = (bf16[3,1536,256]{2,1,0:T(8,128)(2,1)S(1)}, bf16[3,1536,256]{2,1,0:T(8,128)(2,1)}, u32[]{:S(2)}) copy-start(bf16[3,1536,256]{2,1,0:T(8,128)(2,1)} %param.15) | copy-start | bytes 7077892
  3.0 9.9 %copy-start.5 = (s32[2]{0:T(128)S(1)}, s32[2]{0:T(128)}, u32[]{:S(2)}) copy-start(s32[2]{0:T(128)} %param.13) | copy-start | bytes 28
  5.3 8.8 %collective-permute-start = (bf16[3,2,128,1,64]{2,4,1,3,0:T(8,128)(2,1)S(1)}, bf16[3,2,128,1,64]{2,4,1,3,0:T(8,128)(2,1)S(1)}, u32[]{:S(2)}, u32[]{:S(2)}) collective-permute-start(bf16[3,2,128,1,64]{2,4,1,3,0:T(8,128)(2,1)S(1)} %get-tuple-element.10), channel_id=1, source_target_pairs={{0,4},{4,8},{8,12},{12,0},{1,5},{5,9},{9,13},{13,1},{2,6},{6,10},{... | collective-permute-start | bytes 294920 | tf_op jit(solution)/shard_map/ppermute | solution.py:143
  8.4 9.2 %collective-permute-start.1 = (bf16[3,2,128,1,64]{2,4,1,3,0:T(8,128)(2,1)S(1)}, bf16[3,2,128,1,64]{2,4,1,3,0:T(8,128)(2,1)S(1)}, u32[]{:S(2)}, u32[]{:S(2)}) collective-permute-start(bf16[3,2,128,1,64]{2,4,1,3,0:T(8,128)(2,1)S(1)} %get-tuple-element.9), channel_id=1, source_target_pairs={{0,8},{4,12},{8,0},{12,4},{1,9},{5,13},{9,1},{13,5},{2,10},{6,14},... | collective-permute-start | bytes 294920 | tf_op jit(solution)/shard_map/ppermute | solution.py:143
  10.9 6.6 %collective-permute-start.2 = (bf16[3,2,128,1,64]{2,4,1,3,0:T(8,128)(2,1)S(1)}, bf16[3,2,128,1,64]{2,4,1,3,0:T(8,128)(2,1)S(1)}, u32[]{:S(2)}, u32[]{:S(2)}) collective-permute-start(bf16[3,2,128,1,64]{2,4,1,3,0:T(8,128)(2,1)S(1)} %get-tuple-element.8), channel_id=1, source_target_pairs={{0,12},{4,0},{8,4},{12,8},{1,13},{5,1},{9,5},{13,9},{2,14},{6,2},{... | collective-permute-start | bytes 294920 | tf_op jit(solution)/shard_map/ppermute | solution.py:143
  12.3 20.2 %collective-permute-start.7 = (bf16[256,1536]{1,0:T(8,128)(2,1)}, bf16[256,1536]{1,0:T(8,128)(2,1)}, u32[]{:S(2)}, u32[]{:S(2)}) collective-permute-start(bf16[256,1536]{1,0:T(8,128)(2,1)} %param.16), channel_id=1, source_target_pairs={{0,1},{1,0},{2,3},{3,2},{4,5},{5,4},{6,7},{7,6},{8,9},{9,8},{10,11... | collective-permute-start | bytes 2359304 | tf_op jit(solution)/shard_map/ppermute | solution.py:195
  12.3 49.3 %collective-permute-start.14 = (bf16[384,1536]{1,0:T(8,128)(2,1)}, bf16[384,1536]{1,0:T(8,128)(2,1)}, u32[]{:S(2)}, u32[]{:S(2)}) collective-permute-start(bf16[384,1536]{1,0:T(8,128)(2,1)} %param.22), channel_id=1, source_target_pairs={{0,1},{1,0},{2,3},{3,2},{4,5},{5,4},{6,7},{7,6},{8,9},{9,8},{10,11... | collective-permute-start | bytes 3538952 | tf_op jit(solution)/shard_map/ppermute | solution.py:196
  12.8 6.1 %copy-start.7 = (s32[128]{0:T(128)}, s32[128]{0:T(128)S(1)}, u32[]{:S(2)}) copy-start(s32[128]{0:T(128)S(1)} %iota_add_fusion.3) | copy-start | bytes 1540
  19.6 5.2 %collective-permute-start.3 = (bf16[2,1,128,64]{2,3,0,1:T(8,128)(2,1)S(1)}, bf16[2,1,128,64]{2,3,0,1:T(8,128)(2,1)S(1)}, u32[]{:S(2)}, u32[]{:S(2)}) collective-permute-start(bf16[2,1,128,64]{2,3,0,1:T(8,128)(2,1)S(1)} %get-tuple-element.15), channel_id=1, source_target_pairs={{0,12},{4,0},{8,4},{12,8},{1,13},{5,1},{9,5},{13,9},{2,14},{6,2},{... | collective-permute-start | bytes 98312 | tf_op jit(solution)/shard_map/ppermute | solution.py:153
  23.2 5.0 %collective-permute-start.4 = (bf16[2,1,128,64]{2,3,0,1:T(8,128)(2,1)S(1)}, bf16[2,1,128,64]{2,3,0,1:T(8,128)(2,1)S(1)}, u32[]{:S(2)}, u32[]{:S(2)}) collective-permute-start(bf16[2,1,128,64]{2,3,0,1:T(8,128)(2,1)S(1)} %get-tuple-element.14), channel_id=1, source_target_pairs={{0,8},{4,12},{8,0},{12,4},{1,9},{5,13},{9,1},{13,5},{2,10},{6,14},... | collective-permute-start | bytes 98312 | tf_op jit(solution)/shard_map/ppermute | solution.py:153
  23.7 5.7 %collective-permute-start.5 = (bf16[2,1,128,64]{2,3,0,1:T(8,128)(2,1)S(1)}, bf16[2,1,128,64]{2,3,0,1:T(8,128)(2,1)S(1)}, u32[]{:S(2)}, u32[]{:S(2)}) collective-permute-start(bf16[2,1,128,64]{2,3,0,1:T(8,128)(2,1)S(1)} %get-tuple-element.13), channel_id=1, source_target_pairs={{0,4},{4,8},{8,12},{12,0},{1,5},{5,9},{9,13},{13,1},{2,6},{6,10},{... | collective-permute-start | bytes 98312 | tf_op jit(solution)/shard_map/ppermute | solution.py:153
  29.9 5.9 %copy-start.4 = (s32[1536]{0:T(1024)S(1)}, s32[1536]{0:T(1024)}, u32[]{:S(2)}) copy-start(s32[1536]{0:T(1024)} %param.23) | copy-start | bytes 18436
  29.9 11.6 %copy-start.1 = (bf16[2,128,1536]{2,1,0:T(8,128)(2,1)S(1)}, bf16[2,128,1536]{2,1,0:T(8,128)(2,1)}, u32[]{:S(2)}) copy-start(bf16[2,128,1536]{2,1,0:T(8,128)(2,1)} %param.12) | copy-start | bytes 2359300
  29.9 2.4 %collective-permute-start.6 = (bf16[2,128,256]{1,2,0:T(8,128)(2,1)S(1)}, bf16[2,128,256]{1,2,0:T(8,128)(2,1)S(1)}, u32[]{:S(2)}, u32[]{:S(2)}) collective-permute-start(bf16[2,128,256]{1,2,0:T(8,128)(2,1)S(1)} %bitcast.141), channel_id=1, source_target_pairs={{0,1},{1,0},{2,3},{3,2},{4,5},{5,4},{6,7},{7,6},{8,9},{9,8},{10,11... | collective-permute-start | bytes 393224 | tf_op jit(solution)/shard_map/ppermute | solution.py:67
  32.4 9.6 %copy-start.3 = (f32[1536]{0:T(1024)S(1)}, f32[1536]{0:T(1024)}, u32[]{:S(2)}) copy-start(f32[1536]{0:T(1024)} %param.17) | copy-start | bytes 18436
  32.5 11.2 %copy-start.6 = (s32[2]{0:T(128)S(1)}, s32[2]{0:T(128)}, u32[]{:S(2)}) copy-start(s32[2]{0:T(128)} %param.13) | copy-start | bytes 28
  32.5 11.2 %copy-start.8 = (s32[128]{0:T(128)S(1)}, s32[128]{0:T(128)}, u32[]{:S(2)}) copy-start(s32[128]{0:T(128)} %copy-done.7) | copy-start | bytes 1540
  34.2 7.3 %collective-permute-start.8 = (bf16[2,32,1536]{2,1,0:T(8,128)(2,1)S(1)}, bf16[2,32,1536]{2,1,0:T(8,128)(2,1)S(1)}, u32[]{:S(2)}, u32[]{:S(2)}) collective-permute-start(bf16[2,32,1536]{2,1,0:T(8,128)(2,1)S(1)} %dynamic-slice_bitcast_fusion.1), channel_id=1, source_target_pairs={{0,2},{1,3},{2,0},{3,1},{4,6},{5,7},{6,4},{7,5},{8,10},{9,11},{10,... | collective-permute-start | bytes 589832 | tf_op jit(solution)/shard_map/ppermute | solution.py:59
  41.9 8.6 %copy-start.9 = (bf16[2,1536,384]{2,1,0:T(8,128)(2,1)S(1)}, bf16[2,1536,384]{2,1,0:T(8,128)(2,1)}, u32[]{:S(2)}) copy-start(bf16[2,1536,384]{2,1,0:T(8,128)(2,1)} %param.18) | copy-start | bytes 7077892
  42.1 6.5 %collective-permute-start.9 = (bf16[2,32,1536]{2,1,0:T(8,128)(2,1)S(1)}, bf16[2,32,1536]{2,1,0:T(8,128)(2,1)S(1)}, u32[]{:S(2)}, u32[]{:S(2)}) collective-permute-start(bf16[2,32,1536]{2,1,0:T(8,128)(2,1)S(1)} %get-tuple-element.6), channel_id=1, source_target_pairs={{0,2},{1,3},{2,0},{3,1},{4,6},{5,7},{6,4},{7,5},{8,10},{9,11},{10,... | collective-permute-start | bytes 589832 | tf_op jit(solution)/shard_map/ppermute | solution.py:90
  48.6 1.8 %collective-permute-start.10 = (bf16[2,2,32,1536]{3,2,1,0:T(8,128)(2,1)S(1)}, bf16[2,2,32,1536]{3,2,1,0:T(8,128)(2,1)S(1)}, u32[]{:S(2)}, u32[]{:S(2)}) collective-permute-start(bf16[2,2,32,1536]{3,2,1,0:T(8,128)(2,1)S(1)} %bitcast_dynamic-update-slice_fusion.2), channel_id=1, source_target_pairs={{0,1},{1,0},{2,3},{3,2},{4,5},{5,4},{6,7},{7,6},{8,9},{9,8},{10,11... | collective-permute-start | bytes 1179656 | tf_op jit(solution)/shard_map/ppermute | solution.py:90
  50.5 8.1 %copy-start.10 = (f32[31,384]{1,0:T(8,128)S(1)}, f32[31,384]{1,0:T(8,128)}, u32[]{:S(2)}) copy-start(f32[31,384]{1,0:T(8,128)} %param.19) | copy-start | bytes 142852
  50.5 8.1 %copy-start.11 = (f32[384]{0:T(512)S(1)}, f32[384]{0:T(512)}, u32[]{:S(2)}) copy-start(f32[384]{0:T(512)} %param.21) | copy-start | bytes 4612
  50.5 8.1 %copy-start.12 = (f32[384]{0:T(512)S(1)}, f32[384]{0:T(512)}, u32[]{:S(2)}) copy-start(f32[384]{0:T(512)} %param.20) | copy-start | bytes 4612
  51.5 2.8 %collective-permute-start.11 = (bf16[2,15,384]{2,1,0:T(8,128)(2,1)S(1)}, bf16[2,15,384]{2,1,0:T(8,128)(2,1)S(1)}, u32[]{:S(2)}, u32[]{:S(2)}) collective-permute-start(bf16[2,15,384]{2,1,0:T(8,128)(2,1)S(1)} %get-tuple-element.11), channel_id=1, source_target_pairs={{0,4},{4,8},{8,12},{1,5},{5,9},{9,13},{2,6},{6,10},{10,14},{3,7},{... | collective-permute-start | bytes 69128 | tf_op jit(solution)/shard_map/ppermute | solution.py:20
  52.8 5.7 %collective-permute-start.12 = (bf16[2,15,384]{2,1,0:T(8,128)(2,1)S(1)}, bf16[2,15,384]{2,1,0:T(8,128)(2,1)S(1)}, u32[]{:S(2)}, u32[]{:S(2)}) collective-permute-start(bf16[2,15,384]{2,1,0:T(8,128)(2,1)S(1)} %get-tuple-element.12), channel_id=1, source_target_pairs={{4,0},{8,4},{12,8},{5,1},{9,5},{13,9},{6,2},{10,6},{14,10},{7,3},{... | collective-permute-start | bytes 69128 | tf_op jit(solution)/shard_map/ppermute | solution.py:21
  58.6 1.6 %copy-start.2 = (bf16[384,1536]{1,0:T(8,128)(2,1)S(1)}, bf16[384,1536]{1,0:T(8,128)(2,1)}, u32[]{:S(2)}) copy-start(bf16[384,1536]{1,0:T(8,128)(2,1)} %param.22) | copy-start | bytes 3538948
  60.1 1.5 %collective-permute-start.13 = (bf16[2,128,384]{2,0,1:T(2,128)(2,1)S(1)}, bf16[2,128,384]{2,0,1:T(2,128)(2,1)S(1)}, u32[]{:S(2)}, u32[]{:S(2)}) collective-permute-start(bf16[2,128,384]{2,0,1:T(2,128)(2,1)S(1)} %fusion.51), channel_id=1, source_target_pairs={{0,1},{1,0},{2,3},{3,2},{4,5},{5,4},{6,7},{7,6},{8,9},{9,8},{10,11... | collective-permute-start | bytes 589832 | tf_op jit(solution)/shard_map/ppermute | solution.py:67
  63.3 7.0 %collective-permute-start.15 = (bf16[2,32,1536]{2,1,0:T(8,128)(2,1)S(1)}, bf16[2,32,1536]{2,1,0:T(8,128)(2,1)S(1)}, u32[]{:S(2)}, u32[]{:S(2)}) collective-permute-start(bf16[2,32,1536]{2,1,0:T(8,128)(2,1)S(1)} %dynamic-slice_bitcast_fusion), channel_id=1, source_target_pairs={{0,2},{1,3},{2,0},{3,1},{4,6},{5,7},{6,4},{7,5},{8,10},{9,11},{10,... | collective-permute-start | bytes 589832 | tf_op jit(solution)/shard_map/ppermute | solution.py:59

commit v14 on v13

--- a/solution.py
+++ b/solution.py
@@ -67,16 +67,14 @@
     pair_inputs = lax.ppermute(inputs, axis, xor_pairs(count, 1))
     mine = rank & 1
 
-    def kept_rows(rows):
-        rows = rows.reshape(records, count // 2, 2, frames // count, channels)
-        return lax.dynamic_index_in_dim(rows, mine, 2, keepdims=False)
-
     part = jnp.einsum(
-        "sbrc,cd->sbrd", kept_rows(inputs), weights, preferred_element_type=jnp.float32
+        "src,cd->srd", inputs, weights, preferred_element_type=jnp.float32
     ) + jnp.einsum(
-        "sbrc,cd->sbrd", kept_rows(pair_inputs), pair_weights, preferred_element_type=jnp.float32
-    )
-    part = part.astype(jnp.bfloat16).reshape(records, frames // 2, part.shape[-1])
+        "src,cd->srd", pair_inputs, pair_weights, preferred_element_type=jnp.float32
+    )
+    part = part.astype(jnp.bfloat16).reshape(records, count // 2, 2, frames // count, -1)
+    part = lax.dynamic_index_in_dim(part, mine, 2, keepdims=False)
+    part = part.reshape(records, frames // 2, part.shape[-1])
     return reduce_scatter_rows(part, axis, 1, first_bit=1)
 
 

time: 71.5 us -> 73 us (1.021)
  local copies, waits for them, and re-layouts: 1.36 us -> 3.7 us
  matrix products: 11.7 us -> 9.54 us
  other arithmetic: 5.31 us -> 6.46 us
    dot_general x4, matrix products: 6.03 us -> 4.29 us  [the longest x2 2.16 us: project_and_reduce(): jnp.einsum('src,cd->srd', inputs, weights, preferred_element_type=jnp.flo...]
    reshape x0 -> x1, local copies, waits for them, and re-layouts: none -> 1.65 us  [attend_by_heads(): return ordered.transpose(0, 3, 1, 2, 4).reshape(records, frames, width)]
    concatenate x1, other arithmetic: 0.05 us -> 1.08 us  [attend_by_heads(): every = jnp.concatenate(pieces, axis=2)]
  transfers between devices with their start and end apart: 16 -> 16, of which waited for: 12 -> 12; matrix products, arithmetic and copies ran while one was open for 15% -> 17% of each run, Pallas kernels for 0% -> 0%
where the time goes in v14:
time: 73 us; the launch traced here: 72.7 us
  waiting for transfers between devices  33.5 us (46%)
  starting transfers between devices  19.1 us (26%)
  matrix products  9.54 us (13%)
  other arithmetic  6.46 us (9%)
  local copies, waits for them, and re-layouts  3.7 us (5%)
    ppermute x2, waiting for transfers between devices, reduce_scatter_rows(): lax.ppermute(send.astype(jnp.bfloat16), axis, xor_pairs(count, 1 << b))  11.2 us
    ppermute x3, starting transfers between devices, attend_by_heads(): pieces.append(lax.ppermute(send, axis, pairs))  6.96 us
    ppermute x2, waiting for transfers between devices, all_gather_rows(): got = lax.ppermute(acc, axis, xor_pairs(count, 1 << b))  6.57 us
    ppermute x3, waiting for transfers between devices, attend_by_heads(): back.append(lax.ppermute(rows, axis, pairs))  5.48 us
    ppermute x3, waiting for transfers between devices, attend_by_heads(): pieces.append(lax.ppermute(send, axis, pairs))  4.97 us
    ppermute x3, starting transfers between devices, attend_by_heads(): back.append(lax.ppermute(rows, axis, pairs))  4.26 us
    ppermute x1, waiting for transfers between devices, with_halo(): after = lax.ppermute(initial, axis, down)  4.22 us
    ppermute x2, starting transfers between devices, reduce_scatter_rows(): lax.ppermute(send.astype(jnp.bfloat16), axis, xor_pairs(count, 1 << b))  3.11 us
  transfers between devices with their start and end apart: 16, of which 12 were waited for; matrix products, arithmetic and copies ran while one was open for 17% of the time, Pallas kernels for 0%

profile of v14, /device:TPU:0, one launch (start us, length us, event | category | flops | bytes accessed | tf_op | source)
XLA Modules:
  0.0 72.7 jit_solution(4435260862370243601)
XLA Ops:
  0.0 1.5 %convert_reduce_fusion = f32[2,128]{1,0:T(2,128)S(1)} fusion(bf16[2,128,1536]{2,1,0:T(8,128)(2,1)} %param.12), kind=kLoop, calls=%fused_computation.11 | loop fusion | flops 786176 | bytes 787456 | tf_op jit(solution)/shard_map/reduce_sum | solution.py:27
  1.5 1.5 %fusion.11 = f32[2,128]{1,0:T(2,128)S(1)} fusion(bf16[2,128,1536]{2,1,0:T(8,128)(2,1)} %param.12, f32[2,128]{1,0:T(2,128)S(1)} %broadcast_multiply_fusion.1), kind=kLoop, calls=%fused_computation.17 | loop fusion | flops 1572608 | bytes 788480 | tf_op jit(solution)/shard_map/reduce_sum | solution.py:29
  3.0 2.0 %fusion.20 = bf16[3,2,128,256]{3,2,0,1:T(8,128)(2,1)S(1)} fusion(bf16[3,1536,256]{2,1,0:T(8,128)(2,1)S(1)} %copy-done, bf16[2,128,1536]{2,1,0:T(8,128)(2,1)} %param.12, f32[1536]{0:T(1024)} %param.14, f32[2,128]{1,0:T(2,128)S(1)} %add_rsqrt_fusion.1, f32[2,128]{1,0:T(2,128)S(1)} %broadcast_multiply_fusion.1), kind=kOutput, calls=%fused_computation.22 | convolution fusion | flops 606142464 | bytes 3547136 | tf_op jit(solution)/shard_map/std,idc->istc/dot_general | solution.py:177
  5.0 0.2 copy.38
  5.2 0.8 %dynamic-slice_bitcast_fusion.6 = (bf16[3,2,128,1,64]{2,4,1,3,0:T(8,128)(2,1)}, bf16[3,2,128,1,64]{2,4,1,3,0:T(8,128)(2,1)}, bf16[3,2,128,1,64]{2,4,1,3,0:T(8,128)(2,1)}, bf16[3,2,128,1,64]{2,4,1,3,0:T(8,128)(2,1)}) fusion(bf16[3,2,128,4,1,64]{2,5,3,1,0,4:T(8,128)(2,1)S(1)} %bitcast.134, s32[]{:T(128)S(6)} %select_n.102, s32[]{:T(128)S(6)} %select_n.108, ...), kind=kLoop, calls=%fused_computation.77 | loop fusion | bytes 786448 | tf_op jit(solution)/shard_map/jit(dynamic_index_in_dim)/squeeze | solution.py:135
  6.0 3.0 %collective-permute-start = (bf16[3,2,128,1,64]{2,4,1,3,0:T(8,128)(2,1)}, bf16[3,2,128,1,64]{2,4,1,3,0:T(8,128)(2,1)}, u32[]{:S(2)}, u32[]{:S(2)}) collective-permute-start(bf16[3,2,128,1,64]{2,4,1,3,0:T(8,128)(2,1)} %get-tuple-element.10), channel_id=1, source_target_pairs={{0,4},{4,8},{8,12},{12,0},{1,5},{5,9},{9,13},{13,1},{2,6},{6,10},{... | collective-permute-start | bytes 294920 | tf_op jit(solution)/shard_map/ppermute | solution.py:141
  9.0 2.6 %collective-permute-start.1 = (bf16[3,2,128,1,64]{2,4,1,3,0:T(8,128)(2,1)}, bf16[3,2,128,1,64]{2,4,1,3,0:T(8,128)(2,1)}, u32[]{:S(2)}, u32[]{:S(2)}) collective-permute-start(bf16[3,2,128,1,64]{2,4,1,3,0:T(8,128)(2,1)} %get-tuple-element.9), channel_id=1, source_target_pairs={{0,8},{4,12},{8,0},{12,4},{1,9},{5,13},{9,1},{13,5},{2,10},{6,14},... | collective-permute-start | bytes 294920 | tf_op jit(solution)/shard_map/ppermute | solution.py:141
  11.6 1.3 %collective-permute-start.2 = (bf16[3,2,128,1,64]{2,4,1,3,0:T(8,128)(2,1)}, bf16[3,2,128,1,64]{2,4,1,3,0:T(8,128)(2,1)}, u32[]{:S(2)}, u32[]{:S(2)}) collective-permute-start(bf16[3,2,128,1,64]{2,4,1,3,0:T(8,128)(2,1)} %get-tuple-element.8), channel_id=1, source_target_pairs={{0,12},{4,0},{8,4},{12,8},{1,13},{5,1},{9,5},{13,9},{2,14},{6,2},{... | collective-permute-start | bytes 294920 | tf_op jit(solution)/shard_map/ppermute | solution.py:141
  13.0 0.5 collective-permute-start.14
  13.5 0.1 broadcast_compare_fusion
  13.6 1.4 %collective-permute-done = bf16[3,2,128,1,64]{2,4,1,3,0:T(8,128)(2,1)} collective-permute-done((bf16[3,2,128,1,64]{2,4,1,3,0:T(8,128)(2,1)}, bf16[3,2,128,1,64]{2,4,1,3,0:T(8,128)(2,1)}, u32[]{:S(2)}, u32[]{:S(2)}) %collective-permute-start) | collective-permute-done | bytes 98336 | tf_op jit(solution)/shard_map/ppermute | solution.py:141
  15.0 3.5 %collective-permute-done.1 = bf16[3,2,128,1,64]{2,4,1,3,0:T(8,128)(2,1)} collective-permute-done((bf16[3,2,128,1,64]{2,4,1,3,0:T(8,128)(2,1)}, bf16[3,2,128,1,64]{2,4,1,3,0:T(8,128)(2,1)}, u32[]{:S(2)}, u32[]{:S(2)}) %collective-permute-start.1) | collective-permute-done | bytes 98336 | tf_op jit(solution)/shard_map/ppermute | solution.py:141
  18.5 1.1 %pad_maximum_fusion = bf16[3,2,512,1,64]{2,4,1,3,0:T(8,128)(2,1)S(1)} fusion(bf16[3,2,128,1,64]{2,4,1,3,0:T(8,128)(2,1)} %collective-permute-done.2, bf16[3,2,128,1,64]{2,4,1,3,0:T(8,128)(2,1)} %collective-permute-done.1, bf16[3,2,128,1,64]{2,4,1,3,0:T(8,128)(2,1)} %collective-permute-done, bf16[3,2,128,1,64]{2,4,1,3,0:T(8,128)(2,1)} %get-tuple-element.7), kind=kLoop, calls=%fused_computation.44 | loop fusion | flops 1572864 | bytes 786432 | tf_op jit(solution)/shard_map/concatenate | solution.py:143
  19.6 0.8 %fusion.8 = (f32[2,512]{1,0:T(2,128)S(1)}, f32[2,512,512]{1,2,0:T(8,128)S(1)}) fusion(pred[2,512]{1,0:T(4,128)(4,1)S(1)} %broadcast_compare_fusion, bf16[3,2,512,1,64]{2,4,1,3,0:T(8,128)(2,1)S(1)} %pad_maximum_fusion), kind=kOutput, calls=%fused_computation.14 | convolution fusion | flops 68680704 | bytes 2365440 | tf_op jit(solution)/shard_map/sqhe,skhe->shqk/dot_general | solution.py:113
  20.4 0.5 fusion.9
  20.9 0.6 fusion.27
  21.6 3.6 %collective-permute-start.3 = (bf16[2,1,128,64]{2,3,0,1:T(8,128)(2,1)S(1)}, bf16[2,1,128,64]{2,3,0,1:T(8,128)(2,1)S(1)}, u32[]{:S(2)}, u32[]{:S(2)}) collective-permute-start(bf16[2,1,128,64]{2,3,0,1:T(8,128)(2,1)S(1)} %get-tuple-element.15), channel_id=1, source_target_pairs={{0,12},{4,0},{8,4},{12,8},{1,13},{5,1},{9,5},{13,9},{2,14},{6,2},{... | collective-permute-start | bytes 98312 | tf_op jit(solution)/shard_map/ppermute | solution.py:151
  25.2 0.4 collective-permute-start.4
  25.6 0.2 collective-permute-start.5
  25.9 0.9 %collective-permute-done.3 = bf16[2,1,128,64]{2,3,0,1:T(8,128)(2,1)S(1)} collective-permute-done((bf16[2,1,128,64]{2,3,0,1:T(8,128)(2,1)S(1)}, bf16[2,1,128,64]{2,3,0,1:T(8,128)(2,1)S(1)}, u32[]{:S(2)}, u32[]{:S(2)}) %collective-permute-start.3) | collective-permute-done | bytes 32800 | tf_op jit(solution)/shard_map/ppermute | solution.py:151
  26.8 3.4 %collective-permute-done.4 = bf16[2,1,128,64]{2,3,0,1:T(8,128)(2,1)S(1)} collective-permute-done((bf16[2,1,128,64]{2,3,0,1:T(8,128)(2,1)S(1)}, bf16[2,1,128,64]{2,3,0,1:T(8,128)(2,1)S(1)}, u32[]{:S(2)}, u32[]{:S(2)}) %collective-permute-start.4) | collective-permute-done | bytes 32800 | tf_op jit(solution)/shard_map/ppermute | solution.py:151
  30.2 1.2 %collective-permute-done.5 = bf16[2,1,128,64]{2,3,0,1:T(8,128)(2,1)S(1)} collective-permute-done((bf16[2,1,128,64]{2,3,0,1:T(8,128)(2,1)S(1)}, bf16[2,1,128,64]{2,3,0,1:T(8,128)(2,1)S(1)}, u32[]{:S(2)}, u32[]{:S(2)}) %collective-permute-start.5) | collective-permute-done | bytes 32800 | tf_op jit(solution)/shard_map/ppermute | solution.py:151
  31.5 0.7 copy.40
  32.1 1.7 %copy.42 = bf16[2,128,256]{2,1,0:T(8,128)(2,1)} copy(bf16[2,128,256]{1,2,0:T(8,128)(2,1)} %bitcast.135) | data formatting | bytes 262144 | tf_op jit(solution)/shard_map/reshape | solution.py:153
  33.8 1.6 %fusion.35 = f32[2,128,1536]{2,1,0:T(8,128)S(1)} fusion(bf16[2,128,256]{1,2,0:T(8,128)(2,1)} %bitcast.136, bf16[256,1536]{1,0:T(8,128)(2,1)} %param.16), kind=kOutput, calls=%fused_computation.34 | convolution fusion | flops 201326592 | bytes 2490368 | tf_op jit(solution)/shard_map/src,cd->srd/dot_general | solution.py:70
  35.4 1.6 %fusion = bf16[2,128,1536]{2,1,0:T(8,128)(2,1)S(1)} fusion(f32[2,128,1536]{2,1,0:T(8,128)S(1)} %fusion.35, bf16[2,128,256]{2,1,0:T(8,128)(2,1)S(1)} %collective-permute-done.6, bf16[256,1536]{1,0:T(8,128)(2,1)} %collective-permute-done.7), kind=kOutput, calls=%fused_computation.2 | convolution fusion | flops 202113024 | bytes 3276800 | tf_op jit(solution)/shard_map/src,cd->srd/dot_general | solution.py:72
  37.0 1.6 %collective-permute-start.8 = (bf16[2,32,1536]{2,1,0:T(8,128)(2,1)S(1)}, bf16[2,32,1536]{2,1,0:T(8,128)(2,1)S(1)}, u32[]{:S(2)}, u32[]{:S(2)}) collective-permute-start(bf16[2,32,1536]{2,1,0:T(8,128)(2,1)S(1)} %dynamic-slice_bitcast_fusion.1), channel_id=1, source_target_pairs={{0,2},{1,3},{2,0},{3,1},{4,6},{5,7},{6,4},{7,5},{8,10},{9,11},{10,... | collective-permute-start | bytes 589832 | tf_op jit(solution)/shard_map/ppermute | solution.py:59
  38.6 5.8 %collective-permute-done.8 = bf16[2,32,1536]{2,1,0:T(8,128)(2,1)S(1)} collective-permute-done((bf16[2,32,1536]{2,1,0:T(8,128)(2,1)S(1)}, bf16[2,32,1536]{2,1,0:T(8,128)(2,1)S(1)}, u32[]{:S(2)}, u32[]{:S(2)}) %collective-permute-start.8) | collective-permute-done | bytes 196640 | tf_op jit(solution)/shard_map/ppermute | solution.py:59
  44.4 0.2 fusion.61
  44.6 0.2 multiply_reduce_fusion
  44.9 0.1 bitcast_dynamic-update-slice_fusion.2
  45.0 1.6 %collective-permute-start.9 = (bf16[2,32,1536]{2,1,0:T(8,128)(2,1)S(1)}, bf16[2,32,1536]{2,1,0:T(8,128)(2,1)S(1)}, u32[]{:S(2)}, u32[]{:S(2)}) collective-permute-start(bf16[2,32,1536]{2,1,0:T(8,128)(2,1)S(1)} %get-tuple-element.6), channel_id=1, source_target_pairs={{0,2},{1,3},{2,0},{3,1},{4,6},{5,7},{6,4},{7,5},{8,10},{9,11},{10,... | collective-permute-start | bytes 589832 | tf_op jit(solution)/shard_map/ppermute | solution.py:88
  46.6 5.0 %collective-permute-done.9 = bf16[2,32,1536]{2,1,0:T(8,128)(2,1)S(1)} collective-permute-done((bf16[2,32,1536]{2,1,0:T(8,128)(2,1)S(1)}, bf16[2,32,1536]{2,1,0:T(8,128)(2,1)S(1)}, u32[]{:S(2)}, u32[]{:S(2)}) %collective-permute-start.9) | collective-permute-done | bytes 196640 | tf_op jit(solution)/shard_map/ppermute | solution.py:88
  51.8 1.6 %collective-permute-done.10 = bf16[2,2,32,1536]{3,2,1,0:T(8,128)(2,1)S(1)} collective-permute-done((bf16[2,2,32,1536]{3,2,1,0:T(8,128)(2,1)S(1)}, bf16[2,2,32,1536]{3,2,1,0:T(8,128)(2,1)S(1)}, u32[]{:S(2)}, u32[]{:S(2)}) %collective-permute-start.10) | collective-permute-done | bytes 393248 | tf_op jit(solution)/shard_map/ppermute | solution.py:88
  53.5 0.8 %fusion.14 = f32[2,2,128,384]{3,2,0,1:T(8,128)S(1)} fusion(bf16[2,128,1536,1]{2,1,3,0:T(8,128)(2,1)S(1)} %bitcast.137, bf16[2,1536,384]{2,1,0:T(8,128)(2,1)S(1)} %copy-done.8), kind=kOutput, calls=%fused_computation.20 | convolution fusion | flops 603979776 | bytes 3932160 | tf_op jit(solution)/shard_map/std,gdc->gstc/dot_general | solution.py:34
  54.2 0.1 bitcast_select_fusion
  54.4 1.3 %collective-permute-start.11 = (bf16[2,15,384]{2,1,0:T(8,128)(2,1)S(1)}, bf16[2,15,384]{2,1,0:T(8,128)(2,1)S(1)}, u32[]{:S(2)}, u32[]{:S(2)}) collective-permute-start(bf16[2,15,384]{2,1,0:T(8,128)(2,1)S(1)} %get-tuple-element.11), channel_id=1, source_target_pairs={{0,4},{4,8},{8,12},{1,5},{5,9},{9,13},{2,6},{6,10},{10,14},{3,7},{... | collective-permute-start | bytes 69128 | tf_op jit(solution)/shard_map/ppermute | solution.py:20
  55.7 1.3 %collective-permute-start.12 = (bf16[2,15,384]{2,1,0:T(8,128)(2,1)S(1)}, bf16[2,15,384]{2,1,0:T(8,128)(2,1)S(1)}, u32[]{:S(2)}, u32[]{:S(2)}) collective-permute-start(bf16[2,15,384]{2,1,0:T(8,128)(2,1)S(1)} %get-tuple-element.12), channel_id=1, source_target_pairs={{4,0},{8,4},{12,8},{5,1},{9,5},{13,9},{6,2},{10,6},{14,10},{7,3},{... | collective-permute-start | bytes 69128 | tf_op jit(solution)/shard_map/ppermute | solution.py:21
  57.0 0.2 collective-permute-done.11
  57.2 4.2 %collective-permute-done.12 = bf16[2,15,384]{2,1,0:T(8,128)(2,1)S(1)} collective-permute-done((bf16[2,15,384]{2,1,0:T(8,128)(2,1)S(1)}, bf16[2,15,384]{2,1,0:T(8,128)(2,1)S(1)}, u32[]{:S(2)}, u32[]{:S(2)}) %collective-permute-start.12) | collective-permute-done | bytes 23072 | tf_op jit(solution)/shard_map/ppermute | solution.py:21
  61.5 1.1 %fusion.52 = f32[2,128,384]{2,0,1:T(2,128)S(1)} fusion(bf16[2,158,384]{2,1,0:T(8,128)(2,1)S(1)} %pad_maximum_fusion.1, f32[31,1,384]{2,0,1:T(8,128)S(1)} %bitcast.138), kind=kOutput, calls=%fused_computation.62 | convolution fusion | flops 36569088 | bytes 683520 | tf_op jit(solution)/shard_map/conv_general_dilated | solution.py:210
  62.6 0.1 multiply_convert_fusion
  62.8 0.6 fusion.24
  63.4 0.8 %collective-permute-done.13 = bf16[2,128,384]{2,1,0:T(8,128)(2,1)S(1)} collective-permute-done((bf16[2,128,384]{2,1,0:T(8,128)(2,1)S(1)}, bf16[2,128,384]{2,1,0:T(8,128)(2,1)S(1)}, u32[]{:S(2)}, u32[]{:S(2)}) %collective-permute-start.13) | collective-permute-done | bytes 196640 | tf_op jit(solution)/shard_map/ppermute | solution.py:67
  64.3 0.6 fusion.1
  64.9 1.6 %collective-permute-start.15 = (bf16[2,32,1536]{2,1,0:T(8,128)(2,1)S(1)}, bf16[2,32,1536]{2,1,0:T(8,128)(2,1)S(1)}, u32[]{:S(2)}, u32[]{:S(2)}) collective-permute-start(bf16[2,32,1536]{2,1,0:T(8,128)(2,1)S(1)} %dynamic-slice_bitcast_fusion), channel_id=1, source_target_pairs={{0,2},{1,3},{2,0},{3,1},{4,6},{5,7},{6,4},{7,5},{8,10},{9,11},{10,... | collective-permute-start | bytes 589832 | tf_op jit(solution)/shard_map/ppermute | solution.py:59
  66.5 5.4 %collective-permute-done.15 = bf16[2,32,1536]{2,1,0:T(8,128)(2,1)S(1)} collective-permute-done((bf16[2,32,1536]{2,1,0:T(8,128)(2,1)S(1)}, bf16[2,32,1536]{2,1,0:T(8,128)(2,1)S(1)}, u32[]{:S(2)}, u32[]{:S(2)}) %collective-permute-start.15) | collective-permute-done | bytes 196640 | tf_op jit(solution)/shard_map/ppermute | solution.py:59
  71.9 0.8 %fusion.48 = bf16[2,32,1536]{2,1,0:T(8,128)(2,1)} fusion(bf16[2,32,1536]{2,1,0:T(8,128)(2,1)S(1)} %collective-permute-done.15, bf16[2,2,2,32,1536]{4,3,2,1,0:T(8,128)(2,1)S(1)} %bitcast.133, s32[]{:T(128)S(6)} %select_n.113, s32[]{:T(128)S(6)} %select_n.115, bf16[1536]{0:T(1024)(128)(2,1)S(1)} %get-tuple-element.17, ...), kind=kLoop, calls=%fused_computation.50 | loop fusion | flops 1474560 | bytes 1185868 | tf_op jit(solution)/shard_map/convert_element_type | solution.py:226
  (59 shorter events, 0.9 us)
Async XLA Ops:
  0.0 3.0 %copy-start = (bf16[3,1536,256]{2,1,0:T(8,128)(2,1)S(1)}, bf16[3,1536,256]{2,1,0:T(8,128)(2,1)}, u32[]{:S(2)}) copy-start(bf16[3,1536,256]{2,1,0:T(8,128)(2,1)} %param.15) | copy-start | bytes 7077892
  3.0 10.5 %copy-start.7 = (s32[2]{0:T(128)S(1)}, s32[2]{0:T(128)}, u32[]{:S(2)}) copy-start(s32[2]{0:T(128)} %param.13) | copy-start | bytes 28
  6.0 9.0 %collective-permute-start = (bf16[3,2,128,1,64]{2,4,1,3,0:T(8,128)(2,1)}, bf16[3,2,128,1,64]{2,4,1,3,0:T(8,128)(2,1)}, u32[]{:S(2)}, u32[]{:S(2)}) collective-permute-start(bf16[3,2,128,1,64]{2,4,1,3,0:T(8,128)(2,1)} %get-tuple-element.10), channel_id=1, source_target_pairs={{0,4},{4,8},{8,12},{12,0},{1,5},{5,9},{9,13},{13,1},{2,6},{6,10},{... | collective-permute-start | bytes 294920 | tf_op jit(solution)/shard_map/ppermute | solution.py:141
  9.0 9.5 %collective-permute-start.1 = (bf16[3,2,128,1,64]{2,4,1,3,0:T(8,128)(2,1)}, bf16[3,2,128,1,64]{2,4,1,3,0:T(8,128)(2,1)}, u32[]{:S(2)}, u32[]{:S(2)}) collective-permute-start(bf16[3,2,128,1,64]{2,4,1,3,0:T(8,128)(2,1)} %get-tuple-element.9), channel_id=1, source_target_pairs={{0,8},{4,12},{8,0},{12,4},{1,9},{5,13},{9,1},{13,5},{2,10},{6,14},... | collective-permute-start | bytes 294920 | tf_op jit(solution)/shard_map/ppermute | solution.py:141
  11.6 6.9 %collective-permute-start.2 = (bf16[3,2,128,1,64]{2,4,1,3,0:T(8,128)(2,1)}, bf16[3,2,128,1,64]{2,4,1,3,0:T(8,128)(2,1)}, u32[]{:S(2)}, u32[]{:S(2)}) collective-permute-start(bf16[3,2,128,1,64]{2,4,1,3,0:T(8,128)(2,1)} %get-tuple-element.8), channel_id=1, source_target_pairs={{0,12},{4,0},{8,4},{12,8},{1,13},{5,1},{9,5},{13,9},{2,14},{6,2},{... | collective-permute-start | bytes 294920 | tf_op jit(solution)/shard_map/ppermute | solution.py:141
  12.9 22.5 %collective-permute-start.7 = (bf16[256,1536]{1,0:T(8,128)(2,1)}, bf16[256,1536]{1,0:T(8,128)(2,1)}, u32[]{:S(2)}, u32[]{:S(2)}) collective-permute-start(bf16[256,1536]{1,0:T(8,128)(2,1)} %param.16), channel_id=1, source_target_pairs={{0,1},{1,0},{2,3},{3,2},{4,5},{5,4},{6,7},{7,6},{8,9},{9,8},{10,11... | collective-permute-start | bytes 2359304 | tf_op jit(solution)/shard_map/ppermute | solution.py:193
  13.0 50.5 %collective-permute-start.14 = (bf16[384,1536]{1,0:T(8,128)(2,1)}, bf16[384,1536]{1,0:T(8,128)(2,1)S(1)}, u32[]{:S(2)}, u32[]{:S(2)}) collective-permute-start(bf16[384,1536]{1,0:T(8,128)(2,1)} %param.22), channel_id=1, source_target_pairs={{0,1},{1,0},{2,3},{3,2},{4,5},{5,4},{6,7},{7,6},{8,9},{9,8},{10,11... | collective-permute-start | bytes 3538952 | tf_op jit(solution)/shard_map/ppermute | solution.py:194
  21.6 5.2 %collective-permute-start.3 = (bf16[2,1,128,64]{2,3,0,1:T(8,128)(2,1)S(1)}, bf16[2,1,128,64]{2,3,0,1:T(8,128)(2,1)S(1)}, u32[]{:S(2)}, u32[]{:S(2)}) collective-permute-start(bf16[2,1,128,64]{2,3,0,1:T(8,128)(2,1)S(1)} %get-tuple-element.15), channel_id=1, source_target_pairs={{0,12},{4,0},{8,4},{12,8},{1,13},{5,1},{9,5},{13,9},{2,14},{6,2},{... | collective-permute-start | bytes 98312 | tf_op jit(solution)/shard_map/ppermute | solution.py:151
  25.2 5.0 %collective-permute-start.4 = (bf16[2,1,128,64]{2,3,0,1:T(8,128)(2,1)S(1)}, bf16[2,1,128,64]{2,3,0,1:T(8,128)(2,1)S(1)}, u32[]{:S(2)}, u32[]{:S(2)}) collective-permute-start(bf16[2,1,128,64]{2,3,0,1:T(8,128)(2,1)S(1)} %get-tuple-element.14), channel_id=1, source_target_pairs={{0,8},{4,12},{8,0},{12,4},{1,9},{5,13},{9,1},{13,5},{2,10},{6,14},... | collective-permute-start | bytes 98312 | tf_op jit(solution)/shard_map/ppermute | solution.py:151
  25.6 5.7 %collective-permute-start.5 = (bf16[2,1,128,64]{2,3,0,1:T(8,128)(2,1)S(1)}, bf16[2,1,128,64]{2,3,0,1:T(8,128)(2,1)S(1)}, u32[]{:S(2)}, u32[]{:S(2)}) collective-permute-start(bf16[2,1,128,64]{2,3,0,1:T(8,128)(2,1)S(1)} %get-tuple-element.13), channel_id=1, source_target_pairs={{0,4},{4,8},{8,12},{12,0},{1,5},{5,9},{9,13},{13,1},{2,6},{6,10},{... | collective-permute-start | bytes 98312 | tf_op jit(solution)/shard_map/ppermute | solution.py:151
  33.8 1.6 %collective-permute-start.6 = (bf16[2,128,256]{2,1,0:T(8,128)(2,1)}, bf16[2,128,256]{2,1,0:T(8,128)(2,1)S(1)}, u32[]{:S(2)}, u32[]{:S(2)}) collective-permute-start(bf16[2,128,256]{2,1,0:T(8,128)(2,1)} %copy.42), channel_id=1, source_target_pairs={{0,1},{1,0},{2,3},{3,2},{4,5},{5,4},{6,7},{7,6},{8,9},{9,8},{10,11... | collective-permute-start | bytes 393224 | tf_op jit(solution)/shard_map/ppermute | solution.py:67
  35.4 3.2 %copy-start.4 = (s32[1536]{0:T(1024)S(1)}, s32[1536]{0:T(1024)}, u32[]{:S(2)}) copy-start(s32[1536]{0:T(1024)} %param.23) | copy-start | bytes 18436
  35.4 9.0 %copy-start.1 = (bf16[2,128,1536]{2,1,0:T(8,128)(2,1)S(1)}, bf16[2,128,1536]{2,1,0:T(8,128)(2,1)}, u32[]{:S(2)}) copy-start(bf16[2,128,1536]{2,1,0:T(8,128)(2,1)} %param.12) | copy-start | bytes 2359300
  35.4 9.4 %copy-start.3 = (f32[1536]{0:T(1024)S(1)}, f32[1536]{0:T(1024)}, u32[]{:S(2)}) copy-start(f32[1536]{0:T(1024)} %param.17) | copy-start | bytes 18436
  37.0 7.4 %collective-permute-start.8 = (bf16[2,32,1536]{2,1,0:T(8,128)(2,1)S(1)}, bf16[2,32,1536]{2,1,0:T(8,128)(2,1)S(1)}, u32[]{:S(2)}, u32[]{:S(2)}) collective-permute-start(bf16[2,32,1536]{2,1,0:T(8,128)(2,1)S(1)} %dynamic-slice_bitcast_fusion.1), channel_id=1, source_target_pairs={{0,2},{1,3},{2,0},{3,1},{4,6},{5,7},{6,4},{7,5},{8,10},{9,11},{10,... | collective-permute-start | bytes 589832 | tf_op jit(solution)/shard_map/ppermute | solution.py:59
  44.8 8.6 %copy-start.8 = (bf16[2,1536,384]{2,1,0:T(8,128)(2,1)S(1)}, bf16[2,1536,384]{2,1,0:T(8,128)(2,1)}, u32[]{:S(2)}) copy-start(bf16[2,1536,384]{2,1,0:T(8,128)(2,1)} %param.18) | copy-start | bytes 7077892
  45.0 6.6 %collective-permute-start.9 = (bf16[2,32,1536]{2,1,0:T(8,128)(2,1)S(1)}, bf16[2,32,1536]{2,1,0:T(8,128)(2,1)S(1)}, u32[]{:S(2)}, u32[]{:S(2)}) collective-permute-start(bf16[2,32,1536]{2,1,0:T(8,128)(2,1)S(1)} %get-tuple-element.6), channel_id=1, source_target_pairs={{0,2},{1,3},{2,0},{3,1},{4,6},{5,7},{6,4},{7,5},{8,10},{9,11},{10,... | collective-permute-start | bytes 589832 | tf_op jit(solution)/shard_map/ppermute | solution.py:88
  51.6 1.8 %collective-permute-start.10 = (bf16[2,2,32,1536]{3,2,1,0:T(8,128)(2,1)S(1)}, bf16[2,2,32,1536]{3,2,1,0:T(8,128)(2,1)S(1)}, u32[]{:S(2)}, u32[]{:S(2)}) collective-permute-start(bf16[2,2,32,1536]{3,2,1,0:T(8,128)(2,1)S(1)} %bitcast_dynamic-update-slice_fusion.3), channel_id=1, source_target_pairs={{0,1},{1,0},{2,3},{3,2},{4,5},{5,4},{6,7},{7,6},{8,9},{9,8},{10,11... | collective-permute-start | bytes 1179656 | tf_op jit(solution)/shard_map/ppermute | solution.py:88
  53.4 8.0 %copy-start.9 = (f32[31,384]{1,0:T(8,128)S(1)}, f32[31,384]{1,0:T(8,128)}, u32[]{:S(2)}) copy-start(f32[31,384]{1,0:T(8,128)} %param.19) | copy-start | bytes 142852
  54.4 2.8 %collective-permute-start.11 = (bf16[2,15,384]{2,1,0:T(8,128)(2,1)S(1)}, bf16[2,15,384]{2,1,0:T(8,128)(2,1)S(1)}, u32[]{:S(2)}, u32[]{:S(2)}) collective-permute-start(bf16[2,15,384]{2,1,0:T(8,128)(2,1)S(1)} %get-tuple-element.11), channel_id=1, source_target_pairs={{0,4},{4,8},{8,12},{1,5},{5,9},{9,13},{2,6},{6,10},{10,14},{3,7},{... | collective-permute-start | bytes 69128 | tf_op jit(solution)/shard_map/ppermute | solution.py:20
  55.7 5.7 %collective-permute-start.12 = (bf16[2,15,384]{2,1,0:T(8,128)(2,1)S(1)}, bf16[2,15,384]{2,1,0:T(8,128)(2,1)S(1)}, u32[]{:S(2)}, u32[]{:S(2)}) collective-permute-start(bf16[2,15,384]{2,1,0:T(8,128)(2,1)S(1)} %get-tuple-element.12), channel_id=1, source_target_pairs={{4,0},{8,4},{12,8},{5,1},{9,5},{13,9},{6,2},{10,6},{14,10},{7,3},{... | collective-permute-start | bytes 69128 | tf_op jit(solution)/shard_map/ppermute | solution.py:21
  61.5 1.1 %copy-start.5 = (f32[384]{0:T(512)S(1)}, f32[384]{0:T(512)}, u32[]{:S(2)}) copy-start(f32[384]{0:T(512)} %param.21) | copy-start | bytes 4612
  61.5 1.1 %copy-start.6 = (f32[384]{0:T(512)S(1)}, f32[384]{0:T(512)}, u32[]{:S(2)}) copy-start(f32[384]{0:T(512)} %param.20) | copy-start | bytes 4612
  61.5 1.3 %copy-start.2 = (bf16[384,1536]{1,0:T(8,128)(2,1)S(1)}, bf16[384,1536]{1,0:T(8,128)(2,1)}, u32[]{:S(2)}) copy-start(bf16[384,1536]{1,0:T(8,128)(2,1)} %param.22) | copy-start | bytes 3538948
  62.7 1.5 %collective-permute-start.13 = (bf16[2,128,384]{2,1,0:T(8,128)(2,1)S(1)}, bf16[2,128,384]{2,1,0:T(8,128)(2,1)S(1)}, u32[]{:S(2)}, u32[]{:S(2)}) collective-permute-start(bf16[2,128,384]{2,1,0:T(8,128)(2,1)S(1)} %multiply_convert_fusion), channel_id=1, source_target_pairs={{0,1},{1,0},{2,3},{3,2},{4,5},{5,4},{6,7},{7,6},{8,9},{9,8},{10,11... | collective-permute-start | bytes 589832 | tf_op jit(solution)/shard_map/ppermute | solution.py:67
  64.9 7.0 %collective-permute-start.15 = (bf16[2,32,1536]{2,1,0:T(8,128)(2,1)S(1)}, bf16[2,32,1536]{2,1,0:T(8,128)(2,1)S(1)}, u32[]{:S(2)}, u32[]{:S(2)}) collective-permute-start(bf16[2,32,1536]{2,1,0:T(8,128)(2,1)S(1)} %dynamic-slice_bitcast_fusion), channel_id=1, source_target_pairs={{0,2},{1,3},{2,0},{3,1},{4,6},{5,7},{6,4},{7,5},{8,10},{9,11},{10,... | collective-permute-start | bytes 589832 | tf_op jit(solution)/shard_map/ppermute | solution.py:59

commit v15 on v9

--- a/solution.py
+++ b/solution.py
@@ -50,15 +50,16 @@
     bits = bit_count(count)
     shape = x.shape
     block = shape[dim] // count
-    acc = x.reshape(shape[:dim] + (2,) * bits + (block,) + shape[dim + 1 :])
+    parts = [x.reshape(shape[:dim] + (2,) * bits + (block,) + shape[dim + 1 :])]
     for b in range(bits):
         bit_axis = dim + bits - 1 - b
         mine = (rank >> b) & 1
-        keep = lax.dynamic_index_in_dim(acc, mine, bit_axis, keepdims=False)
-        send = lax.dynamic_index_in_dim(acc, 1 - mine, bit_axis, keepdims=False)
+        keep = [lax.dynamic_index_in_dim(p, mine, bit_axis, keepdims=False) for p in parts]
+        send = [lax.dynamic_index_in_dim(p, 1 - mine, bit_axis, keepdims=False) for p in parts]
+        send = sum(p.astype(jnp.float32) for p in send) if len(send) > 1 else send[0]
         got = lax.ppermute(send.astype(jnp.bfloat16), axis, xor_pairs(count, 1 << b))
-        acc = keep.astype(jnp.float32) + got.astype(jnp.float32)
-    return acc
+        parts = keep + [got]
+    return sum(p.astype(jnp.float32) for p in parts)
 
 
 def all_gather_rows(x, axis, dim):

time: 71.6 us -> 72.5 us (1.013)
  other arithmetic: 8.42 us -> 9.29 us
    add x2 -> x0, other arithmetic: 2.18 us -> none  [reduce_scatter_rows(): acc = keep.astype(jnp.float32) + got.astype(jnp.float32)]
    convert_element_type x0 -> x2, other arithmetic: none -> 1.95 us  [reduce_scatter_rows(): send.astype(jnp.bfloat16)]
    convert_element_type x1, other arithmetic: 0.78 us -> 1.74 us  [shards(): return jnp.where(mine_live[..., None], clipped, 0.0).astype(jnp.bfloat16)]
    squeeze x0 -> x2, local copies, waits for them, and re-layouts: none -> 0.81 us  [reduce_scatter_rows(): lax.dynamic_index_in_dim(p, 1 - mine, bit_axis, keepdims=False)]
    unnamed x29 -> x27, local copies, waits for them, and re-layouts: 1.04 us -> 0.29 us
where the time goes in v15:
time: 72.5 us; the launch traced here: 72.2 us
  waiting for transfers between devices  36 us (50%)
  starting transfers between devices  18.7 us (26%)
  other arithmetic  9.29 us (13%)
  matrix products  6.25 us (9%)
  local copies, waits for them, and re-layouts  1.6 us (2%)
    ppermute x4, waiting for transfers between devices, reduce_scatter_rows(): lax.ppermute(send.astype(jnp.bfloat16), axis, xor_pairs(count, 1 << b))  14.8 us
    ppermute x3, starting transfers between devices, attend_by_heads(): pieces.append(lax.ppermute(send, axis, pairs))  7.01 us
    ppermute x2, waiting for transfers between devices, all_gather_rows(): got = lax.ppermute(acc, axis, xor_pairs(count, 1 << b))  6.15 us
    ppermute x3, waiting for transfers between devices, attend_by_heads(): back.append(lax.ppermute(rows, axis, pairs))  5.45 us
    ppermute x3, waiting for transfers between devices, attend_by_heads(): pieces.append(lax.ppermute(send, axis, pairs))  5.16 us
    ppermute x3, starting transfers between devices, attend_by_heads(): back.append(lax.ppermute(rows, axis, pairs))  4.3 us
    ppermute x1, waiting for transfers between devices, with_halo(): after = lax.ppermute(initial, axis, down)  4.22 us
    ppermute x4, starting transfers between devices, reduce_scatter_rows(): lax.ppermute(send.astype(jnp.bfloat16), axis, xor_pairs(count, 1 << b))  3.19 us
  transfers between devices with their start and end apart: 14, of which 13 were waited for; matrix products, arithmetic and copies ran while one was open for 1% of the time, Pallas kernels for 0%

profile of v15, /device:TPU:0, one launch (start us, length us, event | category | flops | bytes accessed | tf_op | source)
XLA Modules:
  0.0 72.2 jit_solution(11671807747736341397)
XLA Ops:
  0.0 1.5 %convert_reduce_fusion = f32[2,128]{1,0:T(2,128)S(1)} fusion(bf16[2,128,1536]{2,1,0:T(8,128)(2,1)} %param.12), kind=kLoop, calls=%fused_computation.9 | loop fusion | flops 786176 | bytes 787456 | tf_op jit(solution)/shard_map/reduce_sum | solution.py:27
  1.5 1.5 %fusion.9 = f32[2,128]{1,0:T(2,128)S(1)} fusion(bf16[2,128,1536]{2,1,0:T(8,128)(2,1)} %param.12, f32[2,128]{1,0:T(2,128)S(1)} %broadcast_multiply_fusion.1), kind=kLoop, calls=%fused_computation.15 | loop fusion | flops 1572608 | bytes 788480 | tf_op jit(solution)/shard_map/reduce_sum | solution.py:29
  3.0 2.0 %fusion.18 = bf16[3,2,128,256]{3,2,0,1:T(8,128)(2,1)S(1)} fusion(bf16[3,1536,256]{2,1,0:T(8,128)(2,1)S(1)} %copy-done, bf16[2,128,1536]{2,1,0:T(8,128)(2,1)} %param.12, f32[1536]{0:T(1024)} %param.14, f32[2,128]{1,0:T(2,128)S(1)} %add_rsqrt_fusion.1, f32[2,128]{1,0:T(2,128)S(1)} %broadcast_multiply_fusion.1), kind=kOutput, calls=%fused_computation.20 | convolution fusion | flops 606142464 | bytes 3547136 | tf_op jit(solution)/shard_map/std,idc->istc/dot_general | solution.py:161
  5.0 0.2 copy.43
  5.3 3.1 %collective-permute-start = (bf16[3,2,128,1,64]{2,4,1,3,0:T(8,128)(2,1)S(1)}, bf16[3,2,128,1,64]{2,4,1,3,0:T(8,128)(2,1)S(1)}, u32[]{:S(2)}, u32[]{:S(2)}) collective-permute-start(bf16[3,2,128,1,64]{2,4,1,3,0:T(8,128)(2,1)S(1)} %get-tuple-element.12), channel_id=1, source_target_pairs={{0,4},{4,8},{8,12},{12,0},{1,5},{5,9},{9,13},{13,1},{2,6},{6,10},{... | collective-permute-start | bytes 294920 | tf_op jit(solution)/shard_map/ppermute | solution.py:125
  8.4 2.6 %collective-permute-start.1 = (bf16[3,2,128,1,64]{2,4,1,3,0:T(8,128)(2,1)S(1)}, bf16[3,2,128,1,64]{2,4,1,3,0:T(8,128)(2,1)S(1)}, u32[]{:S(2)}, u32[]{:S(2)}) collective-permute-start(bf16[3,2,128,1,64]{2,4,1,3,0:T(8,128)(2,1)S(1)} %get-tuple-element.11), channel_id=1, source_target_pairs={{0,8},{4,12},{8,0},{12,4},{1,9},{5,13},{9,1},{13,5},{2,10},{6,14},... | collective-permute-start | bytes 294920 | tf_op jit(solution)/shard_map/ppermute | solution.py:125
  10.9 1.3 %collective-permute-start.2 = (bf16[3,2,128,1,64]{2,4,1,3,0:T(8,128)(2,1)S(1)}, bf16[3,2,128,1,64]{2,4,1,3,0:T(8,128)(2,1)S(1)}, u32[]{:S(2)}, u32[]{:S(2)}) collective-permute-start(bf16[3,2,128,1,64]{2,4,1,3,0:T(8,128)(2,1)S(1)} %get-tuple-element.10), channel_id=1, source_target_pairs={{0,12},{4,0},{8,4},{12,8},{1,13},{5,1},{9,5},{13,9},{2,14},{6,2},{... | collective-permute-start | bytes 294920 | tf_op jit(solution)/shard_map/ppermute | solution.py:125
  12.3 0.1 broadcast_compare_fusion
  12.4 1.6 %collective-permute-done = bf16[3,2,128,1,64]{2,4,1,3,0:T(8,128)(2,1)S(1)} collective-permute-done((bf16[3,2,128,1,64]{2,4,1,3,0:T(8,128)(2,1)S(1)}, bf16[3,2,128,1,64]{2,4,1,3,0:T(8,128)(2,1)S(1)}, u32[]{:S(2)}, u32[]{:S(2)}) %collective-permute-start) | collective-permute-done | bytes 98336 | tf_op jit(solution)/shard_map/ppermute | solution.py:125
  14.0 3.5 %collective-permute-done.1 = bf16[3,2,128,1,64]{2,4,1,3,0:T(8,128)(2,1)S(1)} collective-permute-done((bf16[3,2,128,1,64]{2,4,1,3,0:T(8,128)(2,1)S(1)}, bf16[3,2,128,1,64]{2,4,1,3,0:T(8,128)(2,1)S(1)}, u32[]{:S(2)}, u32[]{:S(2)}) %collective-permute-start.1) | collective-permute-done | bytes 98336 | tf_op jit(solution)/shard_map/ppermute | solution.py:125
  17.6 0.8 %fusion.6 = (f32[2,512]{1,0:T(2,128)S(1)}, f32[2,512,512]{1,2,0:T(8,128)S(1)}) fusion(pred[2,512]{1,0:T(4,128)(4,1)S(1)} %broadcast_compare_fusion, bf16[3,2,512,1,64]{2,4,1,3,0:T(8,128)(2,1)S(1)} %pad_maximum_fusion), kind=kOutput, calls=%fused_computation.12 | convolution fusion | flops 68680704 | bytes 2365440 | tf_op jit(solution)/shard_map/sqhe,skhe->shqk/dot_general | solution.py:97
  18.4 0.5 fusion.7
  18.9 0.6 fusion.23
  19.6 3.6 %collective-permute-start.3 = (bf16[2,1,128,64]{2,3,0,1:T(8,128)(2,1)S(1)}, bf16[2,1,128,64]{2,3,0,1:T(8,128)(2,1)S(1)}, u32[]{:S(2)}, u32[]{:S(2)}) collective-permute-start(bf16[2,1,128,64]{2,3,0,1:T(8,128)(2,1)S(1)} %get-tuple-element.17), channel_id=1, source_target_pairs={{0,12},{4,0},{8,4},{12,8},{1,13},{5,1},{9,5},{13,9},{2,14},{6,2},{... | collective-permute-start | bytes 98312 | tf_op jit(solution)/shard_map/ppermute | solution.py:135
  23.3 0.4 collective-permute-start.4
  23.7 0.2 collective-permute-start.5
  23.9 0.9 %collective-permute-done.3 = bf16[2,1,128,64]{2,3,0,1:T(8,128)(2,1)S(1)} collective-permute-done((bf16[2,1,128,64]{2,3,0,1:T(8,128)(2,1)S(1)}, bf16[2,1,128,64]{2,3,0,1:T(8,128)(2,1)S(1)}, u32[]{:S(2)}, u32[]{:S(2)}) %collective-permute-start.3) | collective-permute-done | bytes 32800 | tf_op jit(solution)/shard_map/ppermute | solution.py:135
  24.9 3.4 %collective-permute-done.4 = bf16[2,1,128,64]{2,3,0,1:T(8,128)(2,1)S(1)} collective-permute-done((bf16[2,1,128,64]{2,3,0,1:T(8,128)(2,1)S(1)}, bf16[2,1,128,64]{2,3,0,1:T(8,128)(2,1)S(1)}, u32[]{:S(2)}, u32[]{:S(2)}) %collective-permute-start.4) | collective-permute-done | bytes 32800 | tf_op jit(solution)/shard_map/ppermute | solution.py:135
  28.2 1.2 %collective-permute-done.5 = bf16[2,1,128,64]{2,3,0,1:T(8,128)(2,1)S(1)} collective-permute-done((bf16[2,1,128,64]{2,3,0,1:T(8,128)(2,1)S(1)}, bf16[2,1,128,64]{2,3,0,1:T(8,128)(2,1)S(1)}, u32[]{:S(2)}, u32[]{:S(2)}) %collective-permute-start.5) | collective-permute-done | bytes 32800 | tf_op jit(solution)/shard_map/ppermute | solution.py:135
  29.5 0.4 convolution_convert_fusion
  30.0 0.1 collective-permute-start.6
  30.0 1.8 %collective-permute-done.6 = bf16[2,2,32,1536]{3,2,0,1:T(8,128)(2,1)} collective-permute-done((bf16[2,2,32,1536]{3,2,0,1:T(8,128)(2,1)S(1)}, bf16[2,2,32,1536]{3,2,0,1:T(8,128)(2,1)}, u32[]{:S(2)}, u32[]{:S(2)}) %collective-permute-start.6) | collective-permute-done | bytes 393248 | tf_op jit(solution)/shard_map/ppermute | solution.py:60
  31.9 1.0 %fusion.45 = bf16[2,32,1536]{2,1,0:T(8,128)(2,1)S(1)} fusion(bf16[2,2,32,1536]{3,2,0,1:T(8,128)(2,1)} %collective-permute-done.6, s32[]{:T(128)S(6)} %select_n.121, bf16[2,2,2,32,1536]{4,3,2,1,0:T(8,128)(2,1)S(1)} %bitcast.134, s32[]{:T(128)S(6)} %select_n.122, s32[]{:T(128)S(6)} %select_n.119), kind=kLoop, calls=%fused_computation.51 | loop fusion | flops 393216 | bytes 589836 | tf_op jit(solution)/shard_map/convert_element_type | solution.py:60
  32.9 1.6 %collective-permute-start.7 = (bf16[2,32,1536]{2,1,0:T(8,128)(2,1)S(1)}, bf16[2,32,1536]{2,1,0:T(8,128)(2,1)}, u32[]{:S(2)}, u32[]{:S(2)}) collective-permute-start(bf16[2,32,1536]{2,1,0:T(8,128)(2,1)S(1)} %fusion.45), channel_id=1, source_target_pairs={{0,2},{1,3},{2,0},{3,1},{4,6},{5,7},{6,4},{7,5},{8,10},{9,11},{10,... | collective-permute-start | bytes 589832 | tf_op jit(solution)/shard_map/ppermute | solution.py:60
  34.4 5.6 %collective-permute-done.7 = bf16[2,32,1536]{2,1,0:T(8,128)(2,1)} collective-permute-done((bf16[2,32,1536]{2,1,0:T(8,128)(2,1)S(1)}, bf16[2,32,1536]{2,1,0:T(8,128)(2,1)}, u32[]{:S(2)}, u32[]{:S(2)}) %collective-permute-start.7) | collective-permute-done | bytes 196640 | tf_op jit(solution)/shard_map/ppermute | solution.py:60
  40.0 1.3 %fusion.63 = (f32[2,32]{1,0:T(2,128)S(1)}, f32[2,32,1536]{2,1,0:T(8,128)S(1)}) fusion(bf16[2,32,1536]{2,1,0:T(8,128)(2,1)} %collective-permute-done.7, bf16[2,2,32,1536]{3,2,0,1:T(8,128)(2,1)} %collective-permute-done.6, s32[]{:T(128)S(6)} %select_n.116, bf16[2,2,2,32,1536]{4,3,2,1,0:T(8,128)(2,1)S(1)} %bitcast.135, s32[]{:T(128)S(6)} %select_n.117, ...), kind=kLoop, calls=%fused_computation.111 | loop fusion | flops 786368 | bytes 1179920 | tf_op jit(solution)/shard_map/reduce_sum | solution.py:27
  41.3 0.2 multiply_reduce_fusion
  41.5 0.1 bitcast_dynamic-update-slice_fusion.2
  41.7 1.6 %collective-permute-start.8 = (bf16[2,32,1536]{2,1,0:T(8,128)(2,1)S(1)}, bf16[2,32,1536]{2,1,0:T(8,128)(2,1)S(1)}, u32[]{:S(2)}, u32[]{:S(2)}) collective-permute-start(bf16[2,32,1536]{2,1,0:T(8,128)(2,1)S(1)} %get-tuple-element.6), channel_id=1, source_target_pairs={{0,2},{1,3},{2,0},{3,1},{4,6},{5,7},{6,4},{7,5},{8,10},{9,11},{10,... | collective-permute-start | bytes 589832 | tf_op jit(solution)/shard_map/ppermute | solution.py:72
  43.2 0.1 broadcast_compare_fusion.1
  43.3 4.6 %collective-permute-done.8 = bf16[2,32,1536]{2,1,0:T(8,128)(2,1)S(1)} collective-permute-done((bf16[2,32,1536]{2,1,0:T(8,128)(2,1)S(1)}, bf16[2,32,1536]{2,1,0:T(8,128)(2,1)S(1)}, u32[]{:S(2)}, u32[]{:S(2)}) %collective-permute-start.8) | collective-permute-done | bytes 196640 | tf_op jit(solution)/shard_map/ppermute | solution.py:72
  48.1 1.6 %collective-permute-done.9 = bf16[2,2,32,1536]{3,2,1,0:T(8,128)(2,1)S(1)} collective-permute-done((bf16[2,2,32,1536]{3,2,1,0:T(8,128)(2,1)S(1)}, bf16[2,2,32,1536]{3,2,1,0:T(8,128)(2,1)S(1)}, u32[]{:S(2)}, u32[]{:S(2)}) %collective-permute-start.9) | collective-permute-done | bytes 393248 | tf_op jit(solution)/shard_map/ppermute | solution.py:72
  49.7 0.8 %fusion.12 = f32[2,2,128,384]{3,2,0,1:T(8,128)S(1)} fusion(bf16[2,128,1536,1]{2,1,3,0:T(8,128)(2,1)S(1)} %bitcast.140, bf16[2,1536,384]{2,1,0:T(8,128)(2,1)S(1)} %copy-done.5), kind=kOutput, calls=%fused_computation.18 | convolution fusion | flops 603979776 | bytes 3932160 | tf_op jit(solution)/shard_map/std,gdc->gstc/dot_general | solution.py:34
  50.5 0.1 bitcast_select_fusion
  50.7 1.3 %collective-permute-start.10 = (bf16[2,15,384]{2,1,0:T(8,128)(2,1)S(1)}, bf16[2,15,384]{2,1,0:T(8,128)(2,1)S(1)}, u32[]{:S(2)}, u32[]{:S(2)}) collective-permute-start(bf16[2,15,384]{2,1,0:T(8,128)(2,1)S(1)} %get-tuple-element.13), channel_id=1, source_target_pairs={{0,4},{4,8},{8,12},{1,5},{5,9},{9,13},{2,6},{6,10},{10,14},{3,7},{... | collective-permute-start | bytes 69128 | tf_op jit(solution)/shard_map/ppermute | solution.py:20
  52.0 1.3 %collective-permute-start.11 = (bf16[2,15,384]{2,1,0:T(8,128)(2,1)S(1)}, bf16[2,15,384]{2,1,0:T(8,128)(2,1)S(1)}, u32[]{:S(2)}, u32[]{:S(2)}) collective-permute-start(bf16[2,15,384]{2,1,0:T(8,128)(2,1)S(1)} %get-tuple-element.14), channel_id=1, source_target_pairs={{4,0},{8,4},{12,8},{5,1},{9,5},{13,9},{6,2},{10,6},{14,10},{7,3},{... | collective-permute-start | bytes 69128 | tf_op jit(solution)/shard_map/ppermute | solution.py:21
  53.3 0.2 collective-permute-done.10
  53.5 4.2 %collective-permute-done.11 = bf16[2,15,384]{2,1,0:T(8,128)(2,1)S(1)} collective-permute-done((bf16[2,15,384]{2,1,0:T(8,128)(2,1)S(1)}, bf16[2,15,384]{2,1,0:T(8,128)(2,1)S(1)}, u32[]{:S(2)}, u32[]{:S(2)}) %collective-permute-start.11) | collective-permute-done | bytes 23072 | tf_op jit(solution)/shard_map/ppermute | solution.py:21
  57.8 1.1 %fusion.50 = f32[2,128,384]{2,0,1:T(2,128)S(1)} fusion(bf16[2,158,384]{2,1,0:T(8,128)(2,1)S(1)} %pad_maximum_fusion.1, f32[31,1,384]{2,0,1:T(8,128)S(1)} %bitcast.142), kind=kOutput, calls=%fused_computation.64 | convolution fusion | flops 36569088 | bytes 683520 | tf_op jit(solution)/shard_map/conv_general_dilated | solution.py:193
  58.9 0.2 copy-done.6
  59.0 0.6 convolution_convert_fusion.1
  59.7 0.8 %copy_bitcast_fusion = bf16[2,2,32,1536]{3,2,0,1:T(8,128)(2,1)} fusion(bf16[2,2,2,32,1536]{4,3,2,1,0:T(8,128)(2,1)S(1)} %bitcast.137, s32[]{:T(128)S(6)} %select_n.120), kind=kLoop, calls=%fused_computation.55 | loop fusion | bytes 786436 | tf_op jit(solution)/shard_map/jit(dynamic_index_in_dim)/squeeze | solution.py:58
  60.5 2.0 %collective-permute-done.12 = bf16[2,2,32,1536]{3,2,0,1:T(8,128)(2,1)} collective-permute-done((bf16[2,2,32,1536]{3,2,0,1:T(8,128)(2,1)}, bf16[2,2,32,1536]{3,2,0,1:T(8,128)(2,1)}, u32[]{:S(2)}, u32[]{:S(2)}) %collective-permute-start.12) | collective-permute-done | bytes 393248 | tf_op jit(solution)/shard_map/ppermute | solution.py:60
  62.5 1.0 %fusion.38 = bf16[2,32,1536]{2,1,0:T(8,128)(2,1)S(1)} fusion(bf16[2,2,32,1536]{3,2,0,1:T(8,128)(2,1)} %collective-permute-done.12, s32[]{:T(128)S(6)} %select_n.121, bf16[2,2,2,32,1536]{4,3,2,1,0:T(8,128)(2,1)S(1)} %bitcast.138, s32[]{:T(128)S(6)} %select_n.122, s32[]{:T(128)S(6)} %select_n.119), kind=kLoop, calls=%fused_computation.40 | loop fusion | flops 393216 | bytes 589836 | tf_op jit(solution)/shard_map/convert_element_type | solution.py:60
  63.5 1.6 %collective-permute-start.13 = (bf16[2,32,1536]{2,1,0:T(8,128)(2,1)S(1)}, bf16[2,32,1536]{2,1,0:T(8,128)(2,1)S(1)}, u32[]{:S(2)}, u32[]{:S(2)}) collective-permute-start(bf16[2,32,1536]{2,1,0:T(8,128)(2,1)S(1)} %fusion.38), channel_id=1, source_target_pairs={{0,2},{1,3},{2,0},{3,1},{4,6},{5,7},{6,4},{7,5},{8,10},{9,11},{10,... | collective-permute-start | bytes 589832 | tf_op jit(solution)/shard_map/ppermute | solution.py:60
  65.0 0.1 broadcast_compare_fusion.2
  65.1 5.4 %collective-permute-done.13 = bf16[2,32,1536]{2,1,0:T(8,128)(2,1)S(1)} collective-permute-done((bf16[2,32,1536]{2,1,0:T(8,128)(2,1)S(1)}, bf16[2,32,1536]{2,1,0:T(8,128)(2,1)S(1)}, u32[]{:S(2)}, u32[]{:S(2)}) %collective-permute-start.13) | collective-permute-done | bytes 196640 | tf_op jit(solution)/shard_map/ppermute | solution.py:60
  70.5 1.7 %fusion.44 = bf16[2,32,1536]{2,1,0:T(8,128)(2,1)} fusion(f32[2,32,1536]{2,1,0:T(8,128)S(1)} %get-tuple-element.8, bf16[2,32,1536]{2,1,0:T(8,128)(2,1)S(1)} %collective-permute-done.13, bf16[2,2,32,1536]{3,2,0,1:T(8,128)(2,1)} %collective-permute-done.12, s32[]{:T(128)S(6)} %select_n.116, bf16[2,2,2,32,1536]{4,3,2,1,0:T(8,128)(2,1)S(1)} %bitcast.139, ...), kind=kLoop, calls=%fused_computation.47 | loop fusion | flops 1179648 | bytes 1185868 | tf_op jit(solution)/shard_map/convert_element_type | solution.py:210
  (53 shorter events, 0.7 us)
Async XLA Ops:
  0.0 3.0 %copy-start = (bf16[3,1536,256]{2,1,0:T(8,128)(2,1)S(1)}, bf16[3,1536,256]{2,1,0:T(8,128)(2,1)}, u32[]{:S(2)}) copy-start(bf16[3,1536,256]{2,1,0:T(8,128)(2,1)} %param.15) | copy-start | bytes 7077892
  3.0 9.3 %copy-start.4 = (s32[2]{0:T(128)S(1)}, s32[2]{0:T(128)}, u32[]{:S(2)}) copy-start(s32[2]{0:T(128)} %param.13) | copy-start | bytes 28
  5.3 8.8 %collective-permute-start = (bf16[3,2,128,1,64]{2,4,1,3,0:T(8,128)(2,1)S(1)}, bf16[3,2,128,1,64]{2,4,1,3,0:T(8,128)(2,1)S(1)}, u32[]{:S(2)}, u32[]{:S(2)}) collective-permute-start(bf16[3,2,128,1,64]{2,4,1,3,0:T(8,128)(2,1)S(1)} %get-tuple-element.12), channel_id=1, source_target_pairs={{0,4},{4,8},{8,12},{12,0},{1,5},{5,9},{9,13},{13,1},{2,6},{6,10},{... | collective-permute-start | bytes 294920 | tf_op jit(solution)/shard_map/ppermute | solution.py:125
  8.4 9.2 %collective-permute-start.1 = (bf16[3,2,128,1,64]{2,4,1,3,0:T(8,128)(2,1)S(1)}, bf16[3,2,128,1,64]{2,4,1,3,0:T(8,128)(2,1)S(1)}, u32[]{:S(2)}, u32[]{:S(2)}) collective-permute-start(bf16[3,2,128,1,64]{2,4,1,3,0:T(8,128)(2,1)S(1)} %get-tuple-element.11), channel_id=1, source_target_pairs={{0,8},{4,12},{8,0},{12,4},{1,9},{5,13},{9,1},{13,5},{2,10},{6,14},... | collective-permute-start | bytes 294920 | tf_op jit(solution)/shard_map/ppermute | solution.py:125
  10.9 6.6 %collective-permute-start.2 = (bf16[3,2,128,1,64]{2,4,1,3,0:T(8,128)(2,1)S(1)}, bf16[3,2,128,1,64]{2,4,1,3,0:T(8,128)(2,1)S(1)}, u32[]{:S(2)}, u32[]{:S(2)}) collective-permute-start(bf16[3,2,128,1,64]{2,4,1,3,0:T(8,128)(2,1)S(1)} %get-tuple-element.10), channel_id=1, source_target_pairs={{0,12},{4,0},{8,4},{12,8},{1,13},{5,1},{9,5},{13,9},{2,14},{6,2},{... | collective-permute-start | bytes 294920 | tf_op jit(solution)/shard_map/ppermute | solution.py:125
  18.9 10.6 %copy-start.1 = (bf16[256,1536]{1,0:T(8,128)(2,1)S(1)}, bf16[256,1536]{1,0:T(8,128)(2,1)}, u32[]{:S(2)}) copy-start(bf16[256,1536]{1,0:T(8,128)(2,1)} %param.16) | copy-start | bytes 2359300
  19.6 5.2 %collective-permute-start.3 = (bf16[2,1,128,64]{2,3,0,1:T(8,128)(2,1)S(1)}, bf16[2,1,128,64]{2,3,0,1:T(8,128)(2,1)S(1)}, u32[]{:S(2)}, u32[]{:S(2)}) collective-permute-start(bf16[2,1,128,64]{2,3,0,1:T(8,128)(2,1)S(1)} %get-tuple-element.17), channel_id=1, source_target_pairs={{0,12},{4,0},{8,4},{12,8},{1,13},{5,1},{9,5},{13,9},{2,14},{6,2},{... | collective-permute-start | bytes 98312 | tf_op jit(solution)/shard_map/ppermute | solution.py:135
  23.3 5.0 %collective-permute-start.4 = (bf16[2,1,128,64]{2,3,0,1:T(8,128)(2,1)S(1)}, bf16[2,1,128,64]{2,3,0,1:T(8,128)(2,1)S(1)}, u32[]{:S(2)}, u32[]{:S(2)}) collective-permute-start(bf16[2,1,128,64]{2,3,0,1:T(8,128)(2,1)S(1)} %get-tuple-element.16), channel_id=1, source_target_pairs={{0,8},{4,12},{8,0},{12,4},{1,9},{5,13},{9,1},{13,5},{2,10},{6,14},... | collective-permute-start | bytes 98312 | tf_op jit(solution)/shard_map/ppermute | solution.py:135
  23.7 5.7 %collective-permute-start.5 = (bf16[2,1,128,64]{2,3,0,1:T(8,128)(2,1)S(1)}, bf16[2,1,128,64]{2,3,0,1:T(8,128)(2,1)S(1)}, u32[]{:S(2)}, u32[]{:S(2)}) collective-permute-start(bf16[2,1,128,64]{2,3,0,1:T(8,128)(2,1)S(1)} %get-tuple-element.15), channel_id=1, source_target_pairs={{0,4},{4,8},{8,12},{12,0},{1,5},{5,9},{9,13},{13,1},{2,6},{6,10},{... | collective-permute-start | bytes 98312 | tf_op jit(solution)/shard_map/ppermute | solution.py:135
  29.9 11.6 %copy-start.2 = (f32[1536]{0:T(1024)S(1)}, f32[1536]{0:T(1024)}, u32[]{:S(2)}) copy-start(f32[1536]{0:T(1024)} %param.17) | copy-start | bytes 18436
  30.0 1.9 %collective-permute-start.6 = (bf16[2,2,32,1536]{3,2,0,1:T(8,128)(2,1)S(1)}, bf16[2,2,32,1536]{3,2,0,1:T(8,128)(2,1)}, u32[]{:S(2)}, u32[]{:S(2)}) collective-permute-start(bf16[2,2,32,1536]{3,2,0,1:T(8,128)(2,1)S(1)} %copy_bitcast_fusion.1), channel_id=1, source_target_pairs={{0,1},{1,0},{2,3},{3,2},{4,5},{5,4},{6,7},{7,6},{8,9},{9,8},{10,11... | collective-permute-start | bytes 1179656 | tf_op jit(solution)/shard_map/ppermute | solution.py:60
  32.9 7.1 %collective-permute-start.7 = (bf16[2,32,1536]{2,1,0:T(8,128)(2,1)S(1)}, bf16[2,32,1536]{2,1,0:T(8,128)(2,1)}, u32[]{:S(2)}, u32[]{:S(2)}) collective-permute-start(bf16[2,32,1536]{2,1,0:T(8,128)(2,1)S(1)} %fusion.45), channel_id=1, source_target_pairs={{0,2},{1,3},{2,0},{3,1},{4,6},{5,7},{6,4},{7,5},{8,10},{9,11},{10,... | collective-permute-start | bytes 589832 | tf_op jit(solution)/shard_map/ppermute | solution.py:60
  41.3 8.4 %copy-start.5 = (bf16[2,1536,384]{2,1,0:T(8,128)(2,1)S(1)}, bf16[2,1536,384]{2,1,0:T(8,128)(2,1)}, u32[]{:S(2)}) copy-start(bf16[2,1536,384]{2,1,0:T(8,128)(2,1)} %param.18) | copy-start | bytes 7077892
  41.7 6.2 %collective-permute-start.8 = (bf16[2,32,1536]{2,1,0:T(8,128)(2,1)S(1)}, bf16[2,32,1536]{2,1,0:T(8,128)(2,1)S(1)}, u32[]{:S(2)}, u32[]{:S(2)}) collective-permute-start(bf16[2,32,1536]{2,1,0:T(8,128)(2,1)S(1)} %get-tuple-element.6), channel_id=1, source_target_pairs={{0,2},{1,3},{2,0},{3,1},{4,6},{5,7},{6,4},{7,5},{8,10},{9,11},{10,... | collective-permute-start | bytes 589832 | tf_op jit(solution)/shard_map/ppermute | solution.py:72
  47.9 1.8 %collective-permute-start.9 = (bf16[2,2,32,1536]{3,2,1,0:T(8,128)(2,1)S(1)}, bf16[2,2,32,1536]{3,2,1,0:T(8,128)(2,1)S(1)}, u32[]{:S(2)}, u32[]{:S(2)}) collective-permute-start(bf16[2,2,32,1536]{3,2,1,0:T(8,128)(2,1)S(1)} %bitcast_dynamic-update-slice_fusion.3), channel_id=1, source_target_pairs={{0,1},{1,0},{2,3},{3,2},{4,5},{5,4},{6,7},{7,6},{8,9},{9,8},{10,11... | collective-permute-start | bytes 1179656 | tf_op jit(solution)/shard_map/ppermute | solution.py:72
  49.7 8.1 %copy-start.7 = (f32[31,384]{1,0:T(8,128)S(1)}, f32[31,384]{1,0:T(8,128)}, u32[]{:S(2)}) copy-start(f32[31,384]{1,0:T(8,128)} %param.19) | copy-start | bytes 142852
  50.7 2.8 %collective-permute-start.10 = (bf16[2,15,384]{2,1,0:T(8,128)(2,1)S(1)}, bf16[2,15,384]{2,1,0:T(8,128)(2,1)S(1)}, u32[]{:S(2)}, u32[]{:S(2)}) collective-permute-start(bf16[2,15,384]{2,1,0:T(8,128)(2,1)S(1)} %get-tuple-element.13), channel_id=1, source_target_pairs={{0,4},{4,8},{8,12},{1,5},{5,9},{9,13},{2,6},{6,10},{10,14},{3,7},{... | collective-permute-start | bytes 69128 | tf_op jit(solution)/shard_map/ppermute | solution.py:20
  52.0 5.7 %collective-permute-start.11 = (bf16[2,15,384]{2,1,0:T(8,128)(2,1)S(1)}, bf16[2,15,384]{2,1,0:T(8,128)(2,1)S(1)}, u32[]{:S(2)}, u32[]{:S(2)}) collective-permute-start(bf16[2,15,384]{2,1,0:T(8,128)(2,1)S(1)} %get-tuple-element.14), channel_id=1, source_target_pairs={{4,0},{8,4},{12,8},{5,1},{9,5},{13,9},{6,2},{10,6},{14,10},{7,3},{... | collective-permute-start | bytes 69128 | tf_op jit(solution)/shard_map/ppermute | solution.py:21
  57.8 1.3 %copy-start.6 = (bf16[384,1536]{1,0:T(8,128)(2,1)S(1)}, bf16[384,1536]{1,0:T(8,128)(2,1)}, u32[]{:S(2)}) copy-start(bf16[384,1536]{1,0:T(8,128)(2,1)} %param.22) | copy-start | bytes 3538948
  57.8 1.3 %copy-start.8 = (f32[384]{0:T(512)S(1)}, f32[384]{0:T(512)}, u32[]{:S(2)}) copy-start(f32[384]{0:T(512)} %param.21) | copy-start | bytes 4612
  57.8 1.3 %copy-start.9 = (f32[384]{0:T(512)S(1)}, f32[384]{0:T(512)}, u32[]{:S(2)}) copy-start(f32[384]{0:T(512)} %param.20) | copy-start | bytes 4612
  59.0 1.4 %copy-start.3 = (s32[1536]{0:T(1024)S(1)}, s32[1536]{0:T(1024)}, u32[]{:S(2)}) copy-start(s32[1536]{0:T(1024)} %param.23) | copy-start | bytes 18436
  60.4 2.1 %collective-permute-start.12 = (bf16[2,2,32,1536]{3,2,0,1:T(8,128)(2,1)}, bf16[2,2,32,1536]{3,2,0,1:T(8,128)(2,1)}, u32[]{:S(2)}, u32[]{:S(2)}) collective-permute-start(bf16[2,2,32,1536]{3,2,0,1:T(8,128)(2,1)} %copy_bitcast_fusion), channel_id=1, source_target_pairs={{0,1},{1,0},{2,3},{3,2},{4,5},{5,4},{6,7},{7,6},{8,9},{9,8},{10,11... | collective-permute-start | bytes 1179656 | tf_op jit(solution)/shard_map/ppermute | solution.py:60
  63.5 7.0 %collective-permute-start.13 = (bf16[2,32,1536]{2,1,0:T(8,128)(2,1)S(1)}, bf16[2,32,1536]{2,1,0:T(8,128)(2,1)S(1)}, u32[]{:S(2)}, u32[]{:S(2)}) collective-permute-start(bf16[2,32,1536]{2,1,0:T(8,128)(2,1)S(1)} %fusion.38), channel_id=1, source_target_pairs={{0,2},{1,3},{2,0},{3,1},{4,6},{5,7},{6,4},{7,5},{8,10},{9,11},{10,... | collective-permute-start | bytes 589832 | tf_op jit(solution)/shard_map/ppermute | solution.py:60

commit v16 on v9

--- a/solution.py
+++ b/solution.py
@@ -160,7 +160,7 @@
     projected = jnp.einsum(
         "std,idc->istc", normed, w_qkv, preferred_element_type=jnp.float32
     ).astype(jnp.bfloat16)
-    if head_count % ctx_count == 0:
+    if head_count % ctx_count == 0 and ctx_count > 4:
         attended = attend_by_heads(projected, frame_counts, "ctx")
     else:
         query_heads = projected[0].reshape(records, frames_here, head_count, HEAD_DIM)

time: 71.6 us -> 76.6 us (1.070)
  waiting for transfers between devices: 35.6 us -> 42.5 us
  starting transfers between devices: 18.8 us -> 13 us
  local copies, waits for them, and re-layouts: 1.79 us -> 4.47 us
  other arithmetic: 8.42 us -> 9.78 us
    ppermute x6 -> x3, waiting for transfers between devices: 10.6 us -> 17.3 us  [the longest x2 13.2 us: ring_gather(): going_right = lax.ppermute(going_right, axis, right)]
    ppermute x6 -> x3, starting transfers between devices: 11.3 us -> 5.17 us  [the longest x2 3.08 us: ring_gather(): going_right = lax.ppermute(going_right, axis, right)]
    slice x1 -> x5, local copies, waits for them, and re-layouts: 0.02 us -> 3.33 us  [the longest x2 1.89 us: shards(): kv_all[:, 1].reshape(ctx_count, records, frames_here, head_count, HEAD_DIM)]
    another operation x0 -> x1, other arithmetic: none -> 1.24 us  [ring_gather(): return jnp.stack([x] + from_right + from_left[::-1], axis=0)]
  transfers between devices with their start and end apart: 14 -> 11, of which waited for: 13 -> 11; matrix products, arithmetic and copies ran while one was open for 1% -> 1% of each run, Pallas kernels for 0% -> 0%
where the time goes in v16:
time: 76.6 us; the launch traced here: 76.1 us
  waiting for transfers between devices  42.5 us (55%)
  starting transfers between devices  13 us (17%)
  other arithmetic  9.78 us (13%)
  matrix products  6.08 us (8%)
  local copies, waits for them, and re-layouts  4.47 us (6%)
    ppermute x4, waiting for transfers between devices, reduce_scatter_rows(): lax.ppermute(send.astype(jnp.bfloat16), axis, xor_pairs(count, 1 << b))  14.6 us
    ppermute x2, waiting for transfers between devices, ring_gather(): going_right = lax.ppermute(going_right, axis, right)  13.2 us
    ppermute x2, waiting for transfers between devices, all_gather_rows(): got = lax.ppermute(acc, axis, xor_pairs(count, 1 << b))  6.15 us
    ppermute x1, waiting for transfers between devices, with_halo(): after = lax.ppermute(initial, axis, down)  4.22 us
    ppermute x1, waiting for transfers between devices, ring_gather(): going_left = lax.ppermute(going_left, axis, left)  4.08 us
    ppermute x4, starting transfers between devices, reduce_scatter_rows(): lax.ppermute(send.astype(jnp.bfloat16), axis, xor_pairs(count, 1 << b))  3.25 us
    ppermute x2, starting transfers between devices, ring_gather(): going_right = lax.ppermute(going_right, axis, right)  3.08 us
    reduce_sum x2, other arithmetic, layer_norm(): centre = jnp.mean(values, axis=-1, keepdims=True)  2.63 us
  transfers between devices with their start and end apart: 11, of which 11 were waited for; matrix products, arithmetic and copies ran while one was open for 1% of the time, Pallas kernels for 0%

profile of v16, /device:TPU:0, one launch (start us, length us, event | category | flops | bytes accessed | tf_op | source)
XLA Modules:
  0.0 76.1 jit_solution(519695623989134651)
XLA Ops:
  0.0 1.5 %convert_reduce_fusion = f32[2,128]{1,0:T(2,128)S(1)} fusion(bf16[2,128,1536]{2,1,0:T(8,128)(2,1)} %param.12), kind=kLoop, calls=%fused_computation.9 | loop fusion | flops 786176 | bytes 787456 | tf_op jit(solution)/shard_map/reduce_sum | solution.py:27
  1.5 1.5 %fusion.9 = f32[2,128]{1,0:T(2,128)S(1)} fusion(bf16[2,128,1536]{2,1,0:T(8,128)(2,1)} %param.12, f32[2,128]{1,0:T(2,128)S(1)} %broadcast_multiply_fusion.1), kind=kLoop, calls=%fused_computation.15 | loop fusion | flops 1572608 | bytes 788480 | tf_op jit(solution)/shard_map/reduce_sum | solution.py:29
  3.0 2.0 %fusion.18 = bf16[3,2,128,256]{3,2,0,1:T(8,128)(2,1)S(1)} fusion(bf16[3,1536,256]{2,1,0:T(8,128)(2,1)S(1)} %copy-done, bf16[2,128,1536]{2,1,0:T(8,128)(2,1)} %param.12, f32[1536]{0:T(1024)} %param.14, f32[2,128]{1,0:T(2,128)S(1)} %add_rsqrt_fusion.1, f32[2,128]{1,0:T(2,128)S(1)} %broadcast_multiply_fusion.1), kind=kOutput, calls=%fused_computation.20 | convolution fusion | flops 606142464 | bytes 3547136 | tf_op jit(solution)/shard_map/std,idc->istc/dot_general | solution.py:160
  5.0 3.1 %collective-permute-start.1 = (bf16[2,2,128,256]{3,2,0,1:T(8,128)(2,1)S(1)}, bf16[2,2,128,256]{3,2,0,1:T(8,128)(2,1)}, u32[]{:S(2)}, u32[]{:S(2)}) collective-permute-start(bf16[2,2,128,256]{3,2,0,1:T(8,128)(2,1)S(1)} %get-tuple-element.16), channel_id=1, source_target_pairs={{0,4},{4,8},{8,12},{12,0},{1,5},{5,9},{9,13},{13,1},{2,6},{6,10},{... | collective-permute-start | bytes 786440 | tf_op jit(solution)/shard_map/ppermute | solution.py:87
  8.1 2.1 %collective-permute-start = (bf16[2,2,128,256]{3,2,0,1:T(8,128)(2,1)S(1)}, bf16[2,2,128,256]{3,2,0,1:T(8,128)(2,1)}, u32[]{:S(2)}, u32[]{:S(2)}) collective-permute-start(bf16[2,2,128,256]{3,2,0,1:T(8,128)(2,1)S(1)} %get-tuple-element.16), channel_id=1, source_target_pairs={{0,12},{4,0},{8,4},{12,8},{1,13},{5,1},{9,5},{13,9},{2,14},{6,2},{... | collective-permute-start | bytes 786440 | tf_op jit(solution)/shard_map/ppermute | solution.py:90
  10.2 7.2 %collective-permute-done.1 = bf16[2,2,128,256]{3,2,0,1:T(8,128)(2,1)} collective-permute-done((bf16[2,2,128,256]{3,2,0,1:T(8,128)(2,1)S(1)}, bf16[2,2,128,256]{3,2,0,1:T(8,128)(2,1)}, u32[]{:S(2)}, u32[]{:S(2)}) %collective-permute-start.1) | collective-permute-done | bytes 262176 | tf_op jit(solution)/shard_map/ppermute | solution.py:87
  17.5 0.1 copy.40
  17.7 0.1 broadcast_compare_fusion
  17.7 4.1 %collective-permute-done = bf16[2,2,128,256]{3,2,0,1:T(8,128)(2,1)} collective-permute-done((bf16[2,2,128,256]{3,2,0,1:T(8,128)(2,1)S(1)}, bf16[2,2,128,256]{3,2,0,1:T(8,128)(2,1)}, u32[]{:S(2)}, u32[]{:S(2)}) %collective-permute-start) | collective-permute-done | bytes 262176 | tf_op jit(solution)/shard_map/ppermute | solution.py:90
  21.8 6.0 %collective-permute-done.2 = bf16[2,2,128,256]{3,2,0,1:T(8,128)(2,1)} collective-permute-done((bf16[2,2,128,256]{3,2,0,1:T(8,128)(2,1)}, bf16[2,2,128,256]{3,2,0,1:T(8,128)(2,1)}, u32[]{:S(2)}, u32[]{:S(2)}) %collective-permute-start.2) | collective-permute-done | bytes 262176 | tf_op jit(solution)/shard_map/ppermute | solution.py:87
  27.8 1.2 %pad_maximum_fusion = bf16[4,2,2,128,256]{4,3,1,2,0:T(8,128)(2,1)S(1)} fusion(bf16[1,2,2,128,256]{4,3,1,2,0:T(8,128)(2,1)} %bitcast.9, bf16[1,2,2,128,256]{4,3,1,2,0:T(8,128)(2,1)} %bitcast.8, bf16[1,2,2,128,256]{4,3,1,2,0:T(8,128)(2,1)} %bitcast.7, bf16[1,2,2,128,256]{4,3,1,2,0:T(8,128)(2,1)S(1)} %get-tuple-element.15), kind=kLoop, calls=%fused_computation.25 | loop fusion | flops 1572864 | bytes 2097152 | tf_op jit(solution)/shard_map/stack | solution.py:92
  29.1 0.9 %fusion.68 = (bf16[4,1,2,128,256]{4,3,1,2,0:T(8,128)(2,1)S(1)}, bf16[4,1,2,128,256]{4,3,1,2,0:T(8,128)(2,1)}) fusion(bf16[4,2,2,128,256]{4,3,1,2,0:T(8,128)(2,1)S(1)} %pad_maximum_fusion), kind=kLoop, calls=%fused_computation.107 | loop fusion | bytes 2097152 | tf_op jit(solution)/shard_map/slice | solution.py:169
  30.0 1.3 %copy.41 = bf16[4,1,2,128,256]{3,4,2,0,1:T(8,128)(2,1)S(1)} copy(bf16[4,1,2,128,256]{4,3,1,2,0:T(8,128)(2,1)} %get-tuple-element.10) | data formatting | bytes 1048576 | tf_op jit(solution)/shard_map/slice | solution.py:168
  31.3 1.0 %copy.43 = bf16[4,1,2,128,256]{3,4,2,0,1:T(8,128)(2,1)} copy(bf16[4,1,2,128,256]{4,3,1,2,0:T(8,128)(2,1)S(1)} %get-tuple-element.9) | data formatting | bytes 1048576 | tf_op jit(solution)/shard_map/slice | solution.py:169
  32.3 0.6 fusion.6
  32.9 0.6 fusion.7
  33.5 0.7 fusion.23
  34.2 0.4 copy-done.1
  34.6 0.4 convolution_convert_fusion
  35.1 0.1 collective-permute-start.3
  35.2 1.8 %collective-permute-done.3 = bf16[2,2,32,1536]{3,2,0,1:T(8,128)(2,1)} collective-permute-done((bf16[2,2,32,1536]{3,2,0,1:T(8,128)(2,1)S(1)}, bf16[2,2,32,1536]{3,2,0,1:T(8,128)(2,1)}, u32[]{:S(2)}, u32[]{:S(2)}) %collective-permute-start.3) | collective-permute-done | bytes 393248 | tf_op jit(solution)/shard_map/ppermute | solution.py:59
  37.1 1.1 %convert_add_fusion.1 = f32[2,2,32,1536]{3,2,0,1:T(8,128)S(1)} fusion(bf16[2,2,32,1536]{3,2,0,1:T(8,128)(2,1)} %collective-permute-done.3, bf16[2,2,1,32,1536]{4,3,2,1,0:T(8,128)(2,1)S(1)} %get-tuple-element.13), kind=kLoop, calls=%fused_computation.32 | loop fusion | flops 589824 | bytes 1572864 | tf_op jit(solution)/shard_map/add | solution.py:60
  38.2 1.6 %collective-permute-start.4 = (bf16[2,32,1536]{2,1,0:T(8,128)(2,1)S(1)}, bf16[2,32,1536]{2,1,0:T(8,128)(2,1)}, u32[]{:S(2)}, u32[]{:S(2)}) collective-permute-start(bf16[2,32,1536]{2,1,0:T(8,128)(2,1)S(1)} %fusion.54), channel_id=1, source_target_pairs={{0,2},{1,3},{2,0},{3,1},{4,6},{5,7},{6,4},{7,5},{8,10},{9,11},{10,... | collective-permute-start | bytes 589832 | tf_op jit(solution)/shard_map/ppermute | solution.py:59
  39.7 5.6 %collective-permute-done.4 = bf16[2,32,1536]{2,1,0:T(8,128)(2,1)} collective-permute-done((bf16[2,32,1536]{2,1,0:T(8,128)(2,1)S(1)}, bf16[2,32,1536]{2,1,0:T(8,128)(2,1)}, u32[]{:S(2)}, u32[]{:S(2)}) %collective-permute-start.4) | collective-permute-done | bytes 196640 | tf_op jit(solution)/shard_map/ppermute | solution.py:59
  45.3 1.2 %fusion.66 = (f32[2,32]{1,0:T(2,128)S(1)}, f32[2,32,1536]{2,1,0:T(8,128)S(1)}) fusion(bf16[2,32,1536]{2,1,0:T(8,128)(2,1)} %collective-permute-done.4, f32[2,2,32,1536]{3,2,0,1:T(8,128)S(1)} %convert_add_fusion.1, s32[]{:T(128)S(6)} %select_n.55, bf16[2,128,1536]{2,1,0:T(8,128)(2,1)} %param.12, s32[]{:T(128)S(6)} %select_n.50), kind=kLoop, calls=%fused_computation.106 | loop fusion | flops 491456 | bytes 1179912 | tf_op jit(solution)/shard_map/reduce_sum | solution.py:27
  46.5 0.2 multiply_reduce_fusion
  46.7 0.1 bitcast_dynamic-update-slice_fusion.2
  46.9 1.6 %collective-permute-start.5 = (bf16[2,32,1536]{2,1,0:T(8,128)(2,1)S(1)}, bf16[2,32,1536]{2,1,0:T(8,128)(2,1)S(1)}, u32[]{:S(2)}, u32[]{:S(2)}) collective-permute-start(bf16[2,32,1536]{2,1,0:T(8,128)(2,1)S(1)} %get-tuple-element.6), channel_id=1, source_target_pairs={{0,2},{1,3},{2,0},{3,1},{4,6},{5,7},{6,4},{7,5},{8,10},{9,11},{10,... | collective-permute-start | bytes 589832 | tf_op jit(solution)/shard_map/ppermute | solution.py:71
  48.4 0.1 broadcast_compare_fusion.1
  48.5 4.6 %collective-permute-done.5 = bf16[2,32,1536]{2,1,0:T(8,128)(2,1)S(1)} collective-permute-done((bf16[2,32,1536]{2,1,0:T(8,128)(2,1)S(1)}, bf16[2,32,1536]{2,1,0:T(8,128)(2,1)S(1)}, u32[]{:S(2)}, u32[]{:S(2)}) %collective-permute-start.5) | collective-permute-done | bytes 196640 | tf_op jit(solution)/shard_map/ppermute | solution.py:71
  53.1 0.1 collective-permute-start.6
  53.3 1.6 %collective-permute-done.6 = bf16[2,2,32,1536]{3,2,1,0:T(8,128)(2,1)S(1)} collective-permute-done((bf16[2,2,32,1536]{3,2,1,0:T(8,128)(2,1)S(1)}, bf16[2,2,32,1536]{3,2,1,0:T(8,128)(2,1)S(1)}, u32[]{:S(2)}, u32[]{:S(2)}) %collective-permute-start.6) | collective-permute-done | bytes 393248 | tf_op jit(solution)/shard_map/ppermute | solution.py:71
  54.9 0.8 %fusion.12 = f32[2,2,128,384]{3,2,0,1:T(8,128)S(1)} fusion(bf16[2,128,1536,1]{2,1,3,0:T(8,128)(2,1)S(1)} %bitcast.125, bf16[2,1536,384]{2,1,0:T(8,128)(2,1)S(1)} %copy-done.6), kind=kOutput, calls=%fused_computation.18 | convolution fusion | flops 603979776 | bytes 3932160 | tf_op jit(solution)/shard_map/std,gdc->gstc/dot_general | solution.py:34
  55.7 0.1 bitcast_select_fusion
  55.9 1.6 %collective-permute-start.7 = (bf16[2,15,384]{2,1,0:T(8,128)(2,1)S(1)}, bf16[2,15,384]{2,1,0:T(8,128)(2,1)S(1)}, u32[]{:S(2)}, u32[]{:S(2)}) collective-permute-start(bf16[2,15,384]{2,1,0:T(8,128)(2,1)S(1)} %get-tuple-element.17), channel_id=1, source_target_pairs={{0,4},{4,8},{8,12},{1,5},{5,9},{9,13},{2,6},{6,10},{10,14},{3,7},{... | collective-permute-start | bytes 69128 | tf_op jit(solution)/shard_map/ppermute | solution.py:20
  57.5 1.3 %collective-permute-start.8 = (bf16[2,15,384]{2,1,0:T(8,128)(2,1)S(1)}, bf16[2,15,384]{2,1,0:T(8,128)(2,1)S(1)}, u32[]{:S(2)}, u32[]{:S(2)}) collective-permute-start(bf16[2,15,384]{2,1,0:T(8,128)(2,1)S(1)} %get-tuple-element.18), channel_id=1, source_target_pairs={{4,0},{8,4},{12,8},{5,1},{9,5},{13,9},{6,2},{10,6},{14,10},{7,3},{... | collective-permute-start | bytes 69128 | tf_op jit(solution)/shard_map/ppermute | solution.py:21
  58.8 0.2 collective-permute-done.7
  59.0 4.2 %collective-permute-done.8 = bf16[2,15,384]{2,1,0:T(8,128)(2,1)S(1)} collective-permute-done((bf16[2,15,384]{2,1,0:T(8,128)(2,1)S(1)}, bf16[2,15,384]{2,1,0:T(8,128)(2,1)S(1)}, u32[]{:S(2)}, u32[]{:S(2)}) %collective-permute-start.8) | collective-permute-done | bytes 23072 | tf_op jit(solution)/shard_map/ppermute | solution.py:21
  63.3 1.1 %fusion.52 = f32[2,128,384]{2,0,1:T(2,128)S(1)} fusion(bf16[2,158,384]{2,1,0:T(8,128)(2,1)S(1)} %pad_maximum_fusion.1, f32[31,1,384]{2,0,1:T(8,128)S(1)} %bitcast.133), kind=kOutput, calls=%fused_computation.70 | convolution fusion | flops 36569088 | bytes 683520 | tf_op jit(solution)/shard_map/conv_general_dilated | solution.py:192
  64.4 0.2 copy-done.7
  64.6 0.6 convolution_convert_fusion.1
  65.3 0.1 collective-permute-start.9
  65.4 1.8 %collective-permute-done.9 = bf16[2,2,32,1536]{3,2,0,1:T(8,128)(2,1)} collective-permute-done((bf16[2,2,32,1536]{3,2,0,1:T(8,128)(2,1)S(1)}, bf16[2,2,32,1536]{3,2,0,1:T(8,128)(2,1)}, u32[]{:S(2)}, u32[]{:S(2)}) %collective-permute-start.9) | collective-permute-done | bytes 393248 | tf_op jit(solution)/shard_map/ppermute | solution.py:59
  67.2 1.1 %convert_add_fusion = f32[2,2,32,1536]{3,2,0,1:T(8,128)S(1)} fusion(bf16[2,2,32,1536]{3,2,0,1:T(8,128)(2,1)} %collective-permute-done.9, bf16[2,2,1,32,1536]{4,3,2,1,0:T(8,128)(2,1)S(1)} %get-tuple-element.11), kind=kLoop, calls=%fused_computation.31 | loop fusion | flops 589824 | bytes 1572864 | tf_op jit(solution)/shard_map/add | solution.py:60
  68.4 1.6 %collective-permute-start.10 = (bf16[2,32,1536]{2,1,0:T(8,128)(2,1)S(1)}, bf16[2,32,1536]{2,1,0:T(8,128)(2,1)S(1)}, u32[]{:S(2)}, u32[]{:S(2)}) collective-permute-start(bf16[2,32,1536]{2,1,0:T(8,128)(2,1)S(1)} %fusion.55), channel_id=1, source_target_pairs={{0,2},{1,3},{2,0},{3,1},{4,6},{5,7},{6,4},{7,5},{8,10},{9,11},{10,... | collective-permute-start | bytes 589832 | tf_op jit(solution)/shard_map/ppermute | solution.py:59
  69.9 0.1 broadcast_compare_fusion.2
  70.0 5.4 %collective-permute-done.10 = bf16[2,32,1536]{2,1,0:T(8,128)(2,1)S(1)} collective-permute-done((bf16[2,32,1536]{2,1,0:T(8,128)(2,1)S(1)}, bf16[2,32,1536]{2,1,0:T(8,128)(2,1)S(1)}, u32[]{:S(2)}, u32[]{:S(2)}) %collective-permute-start.10) | collective-permute-done | bytes 196640 | tf_op jit(solution)/shard_map/ppermute | solution.py:59
  75.4 0.8 %fusion.48 = bf16[2,32,1536]{2,1,0:T(8,128)(2,1)} fusion(f32[2,32,1536]{2,1,0:T(8,128)S(1)} %get-tuple-element.8, bf16[2,32,1536]{2,1,0:T(8,128)(2,1)S(1)} %collective-permute-done.10, f32[2,2,32,1536]{3,2,0,1:T(8,128)S(1)} %convert_add_fusion, s32[]{:T(128)S(6)} %select_n.55, bf16[1536]{0:T(1024)(128)(2,1)S(1)} %get-tuple-element.20, ...), kind=kLoop, calls=%fused_computation.56 | loop fusion | flops 884736 | bytes 1185860 | tf_op jit(solution)/shard_map/convert_element_type | solution.py:209
  (45 shorter events, 0.7 us)
Async XLA Ops:
  0.0 3.0 %copy-start = (bf16[3,1536,256]{2,1,0:T(8,128)(2,1)S(1)}, bf16[3,1536,256]{2,1,0:T(8,128)(2,1)}, u32[]{:S(2)}) copy-start(bf16[3,1536,256]{2,1,0:T(8,128)(2,1)} %param.15) | copy-start | bytes 7077892
  3.0 14.7 %copy-start.5 = (s32[2]{0:T(128)S(1)}, s32[2]{0:T(128)}, u32[]{:S(2)}) copy-start(s32[2]{0:T(128)} %param.13) | copy-start | bytes 28
  5.0 12.4 %collective-permute-start.1 = (bf16[2,2,128,256]{3,2,0,1:T(8,128)(2,1)S(1)}, bf16[2,2,128,256]{3,2,0,1:T(8,128)(2,1)}, u32[]{:S(2)}, u32[]{:S(2)}) collective-permute-start(bf16[2,2,128,256]{3,2,0,1:T(8,128)(2,1)S(1)} %get-tuple-element.16), channel_id=1, source_target_pairs={{0,4},{4,8},{8,12},{12,0},{1,5},{5,9},{9,13},{13,1},{2,6},{6,10},{... | collective-permute-start | bytes 786440 | tf_op jit(solution)/shard_map/ppermute | solution.py:87
  8.1 13.7 %collective-permute-start = (bf16[2,2,128,256]{3,2,0,1:T(8,128)(2,1)S(1)}, bf16[2,2,128,256]{3,2,0,1:T(8,128)(2,1)}, u32[]{:S(2)}, u32[]{:S(2)}) collective-permute-start(bf16[2,2,128,256]{3,2,0,1:T(8,128)(2,1)S(1)} %get-tuple-element.16), channel_id=1, source_target_pairs={{0,12},{4,0},{8,4},{12,8},{1,13},{5,1},{9,5},{13,9},{2,14},{6,2},{... | collective-permute-start | bytes 786440 | tf_op jit(solution)/shard_map/ppermute | solution.py:90
  17.4 10.4 %collective-permute-start.2 = (bf16[2,2,128,256]{3,2,0,1:T(8,128)(2,1)}, bf16[2,2,128,256]{3,2,0,1:T(8,128)(2,1)}, u32[]{:S(2)}, u32[]{:S(2)}) collective-permute-start(bf16[2,2,128,256]{3,2,0,1:T(8,128)(2,1)} %collective-permute-done.1), channel_id=1, source_target_pairs={{0,4},{4,8},{8,12},{12,0},{1,5},{5,9},{9,13},{13,1},{2,6},{6,10},{... | collective-permute-start | bytes 786440 | tf_op jit(solution)/shard_map/ppermute | solution.py:87
  32.3 1.2 %copy-start.2 = (bf16[4,1,2,128,256]{3,4,2,0,1:T(8,128)(2,1)S(1)}, bf16[4,1,2,128,256]{3,4,2,0,1:T(8,128)(2,1)}, u32[]{:S(2)}) copy-start(bf16[4,1,2,128,256]{3,4,2,0,1:T(8,128)(2,1)} %copy.43) | copy-start | bytes 1572868
  33.5 1.1 %copy-start.1 = (bf16[256,1536]{1,0:T(8,128)(2,1)S(1)}, bf16[256,1536]{1,0:T(8,128)(2,1)}, u32[]{:S(2)}) copy-start(bf16[256,1536]{1,0:T(8,128)(2,1)} %param.16) | copy-start | bytes 2359300
  35.1 11.6 %copy-start.3 = (f32[1536]{0:T(1024)S(1)}, f32[1536]{0:T(1024)}, u32[]{:S(2)}) copy-start(f32[1536]{0:T(1024)} %param.17) | copy-start | bytes 18436
  35.1 1.9 %collective-permute-start.3 = (bf16[2,2,32,1536]{3,2,0,1:T(8,128)(2,1)S(1)}, bf16[2,2,32,1536]{3,2,0,1:T(8,128)(2,1)}, u32[]{:S(2)}, u32[]{:S(2)}) collective-permute-start(bf16[2,2,32,1536]{3,2,0,1:T(8,128)(2,1)S(1)} %bitcast.129), channel_id=1, source_target_pairs={{0,1},{1,0},{2,3},{3,2},{4,5},{5,4},{6,7},{7,6},{8,9},{9,8},{10,11... | collective-permute-start | bytes 1179656 | tf_op jit(solution)/shard_map/ppermute | solution.py:59
  38.2 7.1 %collective-permute-start.4 = (bf16[2,32,1536]{2,1,0:T(8,128)(2,1)S(1)}, bf16[2,32,1536]{2,1,0:T(8,128)(2,1)}, u32[]{:S(2)}, u32[]{:S(2)}) collective-permute-start(bf16[2,32,1536]{2,1,0:T(8,128)(2,1)S(1)} %fusion.54), channel_id=1, source_target_pairs={{0,2},{1,3},{2,0},{3,1},{4,6},{5,7},{6,4},{7,5},{8,10},{9,11},{10,... | collective-permute-start | bytes 589832 | tf_op jit(solution)/shard_map/ppermute | solution.py:59
  46.5 8.4 %copy-start.6 = (bf16[2,1536,384]{2,1,0:T(8,128)(2,1)S(1)}, bf16[2,1536,384]{2,1,0:T(8,128)(2,1)}, u32[]{:S(2)}) copy-start(bf16[2,1536,384]{2,1,0:T(8,128)(2,1)} %param.18) | copy-start | bytes 7077892
  46.9 6.2 %collective-permute-start.5 = (bf16[2,32,1536]{2,1,0:T(8,128)(2,1)S(1)}, bf16[2,32,1536]{2,1,0:T(8,128)(2,1)S(1)}, u32[]{:S(2)}, u32[]{:S(2)}) collective-permute-start(bf16[2,32,1536]{2,1,0:T(8,128)(2,1)S(1)} %get-tuple-element.6), channel_id=1, source_target_pairs={{0,2},{1,3},{2,0},{3,1},{4,6},{5,7},{6,4},{7,5},{8,10},{9,11},{10,... | collective-permute-start | bytes 589832 | tf_op jit(solution)/shard_map/ppermute | solution.py:71
  53.1 1.8 %collective-permute-start.6 = (bf16[2,2,32,1536]{3,2,1,0:T(8,128)(2,1)S(1)}, bf16[2,2,32,1536]{3,2,1,0:T(8,128)(2,1)S(1)}, u32[]{:S(2)}, u32[]{:S(2)}) collective-permute-start(bf16[2,2,32,1536]{3,2,1,0:T(8,128)(2,1)S(1)} %bitcast_dynamic-update-slice_fusion.3), channel_id=1, source_target_pairs={{0,1},{1,0},{2,3},{3,2},{4,5},{5,4},{6,7},{7,6},{8,9},{9,8},{10,11... | collective-permute-start | bytes 1179656 | tf_op jit(solution)/shard_map/ppermute | solution.py:71
  54.9 8.4 %copy-start.8 = (f32[31,384]{1,0:T(8,128)S(1)}, f32[31,384]{1,0:T(8,128)}, u32[]{:S(2)}) copy-start(f32[31,384]{1,0:T(8,128)} %param.19) | copy-start | bytes 142852
  55.9 3.1 %collective-permute-start.7 = (bf16[2,15,384]{2,1,0:T(8,128)(2,1)S(1)}, bf16[2,15,384]{2,1,0:T(8,128)(2,1)S(1)}, u32[]{:S(2)}, u32[]{:S(2)}) collective-permute-start(bf16[2,15,384]{2,1,0:T(8,128)(2,1)S(1)} %get-tuple-element.17), channel_id=1, source_target_pairs={{0,4},{4,8},{8,12},{1,5},{5,9},{9,13},{2,6},{6,10},{10,14},{3,7},{... | collective-permute-start | bytes 69128 | tf_op jit(solution)/shard_map/ppermute | solution.py:20
  57.5 5.7 %collective-permute-start.8 = (bf16[2,15,384]{2,1,0:T(8,128)(2,1)S(1)}, bf16[2,15,384]{2,1,0:T(8,128)(2,1)S(1)}, u32[]{:S(2)}, u32[]{:S(2)}) collective-permute-start(bf16[2,15,384]{2,1,0:T(8,128)(2,1)S(1)} %get-tuple-element.18), channel_id=1, source_target_pairs={{4,0},{8,4},{12,8},{5,1},{9,5},{13,9},{6,2},{10,6},{14,10},{7,3},{... | collective-permute-start | bytes 69128 | tf_op jit(solution)/shard_map/ppermute | solution.py:21
  63.3 1.3 %copy-start.7 = (bf16[384,1536]{1,0:T(8,128)(2,1)S(1)}, bf16[384,1536]{1,0:T(8,128)(2,1)}, u32[]{:S(2)}) copy-start(bf16[384,1536]{1,0:T(8,128)(2,1)} %param.22) | copy-start | bytes 3538948
  63.3 1.3 %copy-start.9 = (f32[384]{0:T(512)S(1)}, f32[384]{0:T(512)}, u32[]{:S(2)}) copy-start(f32[384]{0:T(512)} %param.21) | copy-start | bytes 4612
  63.3 1.3 %copy-start.10 = (f32[384]{0:T(512)S(1)}, f32[384]{0:T(512)}, u32[]{:S(2)}) copy-start(f32[384]{0:T(512)} %param.20) | copy-start | bytes 4612
  64.6 0.8 %copy-start.4 = (s32[1536]{0:T(1024)S(1)}, s32[1536]{0:T(1024)}, u32[]{:S(2)}) copy-start(s32[1536]{0:T(1024)} %param.23) | copy-start | bytes 18436
  65.3 1.9 %collective-permute-start.9 = (bf16[2,2,32,1536]{3,2,0,1:T(8,128)(2,1)S(1)}, bf16[2,2,32,1536]{3,2,0,1:T(8,128)(2,1)}, u32[]{:S(2)}, u32[]{:S(2)}) collective-permute-start(bf16[2,2,32,1536]{3,2,0,1:T(8,128)(2,1)S(1)} %bitcast.130), channel_id=1, source_target_pairs={{0,1},{1,0},{2,3},{3,2},{4,5},{5,4},{6,7},{7,6},{8,9},{9,8},{10,11... | collective-permute-start | bytes 1179656 | tf_op jit(solution)/shard_map/ppermute | solution.py:59
  68.4 7.0 %collective-permute-start.10 = (bf16[2,32,1536]{2,1,0:T(8,128)(2,1)S(1)}, bf16[2,32,1536]{2,1,0:T(8,128)(2,1)S(1)}, u32[]{:S(2)}, u32[]{:S(2)}) collective-permute-start(bf16[2,32,1536]{2,1,0:T(8,128)(2,1)S(1)} %fusion.55), channel_id=1, source_target_pairs={{0,2},{1,3},{2,0},{3,1},{4,6},{5,7},{6,4},{7,5},{8,10},{9,11},{10,... | collective-permute-start | bytes 589832 | tf_op jit(solution)/shard_map/ppermute | solution.py:59

commit v17 on v9

--- a/solution.py
+++ b/solution.py
@@ -188,16 +188,26 @@
     frame_live = frame_ids[None, :] < frame_counts[:, None]
     gated_rows = jnp.where(frame_live[..., None], gated_rows, jnp.zeros((), jnp.bfloat16))
     rim_width = kernel.shape[0] // 2
-    padded = with_halo(gated_rows, (("ctx", 1),), rim_width)
-    depthwise = lax.conv_general_dilated(
-        padded.astype(jnp.float32),
-        kernel[:, None, :],
-        window_strides=(1,),
-        padding="VALID",
-        dimension_numbers=("NWC", "WIO", "NWC"),
-        feature_group_count=kernel.shape[1],
-        precision=lax.Precision.HIGHEST,
-    )
+    ctx_up = [(i, i + 1) for i in range(ctx_count - 1)]
+    ctx_down = [(j, i) for i, j in ctx_up]
+    before = lax.ppermute(gated_rows[:, frames_here - rim_width :], "ctx", ctx_up)
+    after = lax.ppermute(gated_rows[:, :rim_width], "ctx", ctx_down)
+
+    def depthwise_of(rows):
+        return lax.conv_general_dilated(
+            rows.astype(jnp.float32),
+            kernel[:, None, :],
+            window_strides=(1,),
+            padding="VALID",
+            dimension_numbers=("NWC", "WIO", "NWC"),
+            feature_group_count=kernel.shape[1],
+            precision=lax.Precision.HIGHEST,
+        )
+
+    middle = depthwise_of(gated_rows)
+    low = depthwise_of(jnp.concatenate([before, gated_rows[:, : 2 * rim_width]], axis=1))
+    high = depthwise_of(jnp.concatenate([gated_rows[:, frames_here - 2 * rim_width :], after], axis=1))
+    depthwise = jnp.concatenate([low, middle, high], axis=1)
     activated = jax.nn.silu(depthwise * bn_scale + bn_shift).astype(jnp.bfloat16)
     conv_part = jnp.einsum("stc,cd->std", activated, w_pw, preferred_element_type=jnp.float32)
     conv_rows = reduce_scatter_rows(conv_part.astype(jnp.bfloat16), "mp", 1)

time: 71.6 us -> 71.7 us (level)
  transfers between devices with their start and end apart: 14 -> 14, of which waited for: 13 -> 12; matrix products, arithmetic and copies ran while one was open for 1% -> 2% of each run, Pallas kernels for 0% -> 0%
where the time goes in v17:
time: 71.7 us; the launch traced here: 71.4 us
  waiting for transfers between devices  34.9 us (49%)
  starting transfers between devices  18.9 us (26%)
  other arithmetic  8.39 us (12%)
  matrix products  6.43 us (9%)
  local copies, waits for them, and re-layouts  2.16 us (3%)
    ppermute x4, waiting for transfers between devices, reduce_scatter_rows(): lax.ppermute(send.astype(jnp.bfloat16), axis, xor_pairs(count, 1 << b))  14 us
    ppermute x3, starting transfers between devices, attend_by_heads(): pieces.append(lax.ppermute(send, axis, pairs))  7.01 us
    ppermute x2, waiting for transfers between devices, all_gather_rows(): got = lax.ppermute(acc, axis, xor_pairs(count, 1 << b))  6.15 us
    ppermute x3, waiting for transfers between devices, attend_by_heads(): back.append(lax.ppermute(rows, axis, pairs))  5.44 us
    ppermute x3, waiting for transfers between devices, attend_by_heads(): pieces.append(lax.ppermute(send, axis, pairs))  5.16 us
    ppermute x3, starting transfers between devices, attend_by_heads(): back.append(lax.ppermute(rows, axis, pairs))  4.3 us
    ppermute x1, waiting for transfers between devices, shards(): after = lax.ppermute(gated_rows[:, :rim_width], 'ctx', ctx_down)  4.19 us
    ppermute x4, starting transfers between devices, reduce_scatter_rows(): lax.ppermute(send.astype(jnp.bfloat16), axis, xor_pairs(count, 1 << b))  3.26 us
  transfers between devices with their start and end apart: 14, of which 12 were waited for; matrix products, arithmetic and copies ran while one was open for 2% of the time, Pallas kernels for 0%

profile of v17, /device:TPU:0, one launch (start us, length us, event | category | flops | bytes accessed | tf_op | source)
XLA Modules:
  0.0 71.4 jit_solution(12759560749292139758)
XLA Ops:
  0.0 1.5 %convert_reduce_fusion = f32[2,128]{1,0:T(2,128)S(1)} fusion(bf16[2,128,1536]{2,1,0:T(8,128)(2,1)} %param.12), kind=kLoop, calls=%fused_computation.9 | loop fusion | flops 786176 | bytes 787456 | tf_op jit(solution)/shard_map/reduce_sum | solution.py:27
  1.5 1.5 %fusion.9 = f32[2,128]{1,0:T(2,128)S(1)} fusion(bf16[2,128,1536]{2,1,0:T(8,128)(2,1)} %param.12, f32[2,128]{1,0:T(2,128)S(1)} %broadcast_multiply_fusion.1), kind=kLoop, calls=%fused_computation.15 | loop fusion | flops 1572608 | bytes 788480 | tf_op jit(solution)/shard_map/reduce_sum | solution.py:29
  3.0 2.0 %fusion.18 = bf16[3,2,128,256]{3,2,0,1:T(8,128)(2,1)S(1)} fusion(bf16[3,1536,256]{2,1,0:T(8,128)(2,1)S(1)} %copy-done, bf16[2,128,1536]{2,1,0:T(8,128)(2,1)} %param.12, f32[1536]{0:T(1024)} %param.14, f32[2,128]{1,0:T(2,128)S(1)} %add_rsqrt_fusion.1, f32[2,128]{1,0:T(2,128)S(1)} %broadcast_multiply_fusion.1), kind=kOutput, calls=%fused_computation.20 | convolution fusion | flops 606142464 | bytes 3547136 | tf_op jit(solution)/shard_map/std,idc->istc/dot_general | solution.py:160
  5.0 0.2 copy.47
  5.3 3.1 %collective-permute-start = (bf16[3,2,128,1,64]{2,4,1,3,0:T(8,128)(2,1)S(1)}, bf16[3,2,128,1,64]{2,4,1,3,0:T(8,128)(2,1)S(1)}, u32[]{:S(2)}, u32[]{:S(2)}) collective-permute-start(bf16[3,2,128,1,64]{2,4,1,3,0:T(8,128)(2,1)S(1)} %get-tuple-element.16), channel_id=1, source_target_pairs={{0,4},{4,8},{8,12},{12,0},{1,5},{5,9},{9,13},{13,1},{2,6},{6,10},{... | collective-permute-start | bytes 294920 | tf_op jit(solution)/shard_map/ppermute | solution.py:124
  8.4 2.6 %collective-permute-start.1 = (bf16[3,2,128,1,64]{2,4,1,3,0:T(8,128)(2,1)S(1)}, bf16[3,2,128,1,64]{2,4,1,3,0:T(8,128)(2,1)S(1)}, u32[]{:S(2)}, u32[]{:S(2)}) collective-permute-start(bf16[3,2,128,1,64]{2,4,1,3,0:T(8,128)(2,1)S(1)} %get-tuple-element.15), channel_id=1, source_target_pairs={{0,8},{4,12},{8,0},{12,4},{1,9},{5,13},{9,1},{13,5},{2,10},{6,14},... | collective-permute-start | bytes 294920 | tf_op jit(solution)/shard_map/ppermute | solution.py:124
  10.9 1.3 %collective-permute-start.2 = (bf16[3,2,128,1,64]{2,4,1,3,0:T(8,128)(2,1)S(1)}, bf16[3,2,128,1,64]{2,4,1,3,0:T(8,128)(2,1)S(1)}, u32[]{:S(2)}, u32[]{:S(2)}) collective-permute-start(bf16[3,2,128,1,64]{2,4,1,3,0:T(8,128)(2,1)S(1)} %get-tuple-element.14), channel_id=1, source_target_pairs={{0,12},{4,0},{8,4},{12,8},{1,13},{5,1},{9,5},{13,9},{2,14},{6,2},{... | collective-permute-start | bytes 294920 | tf_op jit(solution)/shard_map/ppermute | solution.py:124
  12.3 0.1 broadcast_compare_fusion
  12.4 1.6 %collective-permute-done = bf16[3,2,128,1,64]{2,4,1,3,0:T(8,128)(2,1)S(1)} collective-permute-done((bf16[3,2,128,1,64]{2,4,1,3,0:T(8,128)(2,1)S(1)}, bf16[3,2,128,1,64]{2,4,1,3,0:T(8,128)(2,1)S(1)}, u32[]{:S(2)}, u32[]{:S(2)}) %collective-permute-start) | collective-permute-done | bytes 98336 | tf_op jit(solution)/shard_map/ppermute | solution.py:124
  14.0 3.5 %collective-permute-done.1 = bf16[3,2,128,1,64]{2,4,1,3,0:T(8,128)(2,1)S(1)} collective-permute-done((bf16[3,2,128,1,64]{2,4,1,3,0:T(8,128)(2,1)S(1)}, bf16[3,2,128,1,64]{2,4,1,3,0:T(8,128)(2,1)S(1)}, u32[]{:S(2)}, u32[]{:S(2)}) %collective-permute-start.1) | collective-permute-done | bytes 98336 | tf_op jit(solution)/shard_map/ppermute | solution.py:124
  17.6 0.8 %fusion.6 = (f32[2,512]{1,0:T(2,128)S(1)}, f32[2,512,512]{1,2,0:T(8,128)S(1)}) fusion(pred[2,512]{1,0:T(4,128)(4,1)S(1)} %broadcast_compare_fusion, bf16[3,2,512,1,64]{2,4,1,3,0:T(8,128)(2,1)S(1)} %pad_maximum_fusion), kind=kOutput, calls=%fused_computation.12 | convolution fusion | flops 68680704 | bytes 2365440 | tf_op jit(solution)/shard_map/sqhe,skhe->shqk/dot_general | solution.py:96
  18.4 0.5 fusion.7
  18.9 0.6 fusion.23
  19.6 3.6 %collective-permute-start.3 = (bf16[2,1,128,64]{2,3,0,1:T(8,128)(2,1)S(1)}, bf16[2,1,128,64]{2,3,0,1:T(8,128)(2,1)S(1)}, u32[]{:S(2)}, u32[]{:S(2)}) collective-permute-start(bf16[2,1,128,64]{2,3,0,1:T(8,128)(2,1)S(1)} %get-tuple-element.23), channel_id=1, source_target_pairs={{0,12},{4,0},{8,4},{12,8},{1,13},{5,1},{9,5},{13,9},{2,14},{6,2},{... | collective-permute-start | bytes 98312 | tf_op jit(solution)/shard_map/ppermute | solution.py:134
  23.3 0.4 collective-permute-start.4
  23.7 0.2 collective-permute-start.5
  23.9 0.9 %collective-permute-done.3 = bf16[2,1,128,64]{2,3,0,1:T(8,128)(2,1)S(1)} collective-permute-done((bf16[2,1,128,64]{2,3,0,1:T(8,128)(2,1)S(1)}, bf16[2,1,128,64]{2,3,0,1:T(8,128)(2,1)S(1)}, u32[]{:S(2)}, u32[]{:S(2)}) %collective-permute-start.3) | collective-permute-done | bytes 32800 | tf_op jit(solution)/shard_map/ppermute | solution.py:134
  24.9 3.4 %collective-permute-done.4 = bf16[2,1,128,64]{2,3,0,1:T(8,128)(2,1)S(1)} collective-permute-done((bf16[2,1,128,64]{2,3,0,1:T(8,128)(2,1)S(1)}, bf16[2,1,128,64]{2,3,0,1:T(8,128)(2,1)S(1)}, u32[]{:S(2)}, u32[]{:S(2)}) %collective-permute-start.4) | collective-permute-done | bytes 32800 | tf_op jit(solution)/shard_map/ppermute | solution.py:134
  28.2 1.2 %collective-permute-done.5 = bf16[2,1,128,64]{2,3,0,1:T(8,128)(2,1)S(1)} collective-permute-done((bf16[2,1,128,64]{2,3,0,1:T(8,128)(2,1)S(1)}, bf16[2,1,128,64]{2,3,0,1:T(8,128)(2,1)S(1)}, u32[]{:S(2)}, u32[]{:S(2)}) %collective-permute-start.5) | collective-permute-done | bytes 32800 | tf_op jit(solution)/shard_map/ppermute | solution.py:134
  29.5 0.4 convolution_convert_fusion
  30.1 1.7 %collective-permute-done.6 = bf16[2,2,32,1536]{3,2,0,1:T(8,128)(2,1)S(1)} collective-permute-done((bf16[2,2,32,1536]{3,2,0,1:T(8,128)(2,1)S(1)}, bf16[2,2,32,1536]{3,2,0,1:T(8,128)(2,1)S(1)}, u32[]{:S(2)}, u32[]{:S(2)}) %collective-permute-start.6) | collective-permute-done | bytes 393248 | tf_op jit(solution)/shard_map/ppermute | solution.py:59
  31.8 0.8 %copy-done.2 = bf16[2,2,32,1536]{3,2,0,1:T(8,128)(2,1)} copy-done((bf16[2,2,32,1536]{3,2,0,1:T(8,128)(2,1)}, bf16[2,2,32,1536]{3,2,0,1:T(8,128)(2,1)S(1)}, u32[]{:S(2)}) %copy-start.2) | copy-done | bytes 393240
  32.6 1.1 %convert_add_fusion.1 = f32[2,2,32,1536]{3,2,0,1:T(8,128)S(1)} fusion(bf16[2,2,32,1536]{3,2,0,1:T(8,128)(2,1)} %copy-done.2, bf16[2,2,1,32,1536]{4,3,2,1,0:T(8,128)(2,1)S(1)} %get-tuple-element.11), kind=kLoop, calls=%fused_computation.30 | loop fusion | flops 589824 | bytes 1572864 | tf_op jit(solution)/shard_map/add | solution.py:60
  33.7 1.6 %collective-permute-start.7 = (bf16[2,32,1536]{2,1,0:T(8,128)(2,1)S(1)}, bf16[2,32,1536]{2,1,0:T(8,128)(2,1)}, u32[]{:S(2)}, u32[]{:S(2)}) collective-permute-start(bf16[2,32,1536]{2,1,0:T(8,128)(2,1)S(1)} %fusion.46), channel_id=1, source_target_pairs={{0,2},{1,3},{2,0},{3,1},{4,6},{5,7},{6,4},{7,5},{8,10},{9,11},{10,... | collective-permute-start | bytes 589832 | tf_op jit(solution)/shard_map/ppermute | solution.py:59
  35.2 5.6 %collective-permute-done.7 = bf16[2,32,1536]{2,1,0:T(8,128)(2,1)} collective-permute-done((bf16[2,32,1536]{2,1,0:T(8,128)(2,1)S(1)}, bf16[2,32,1536]{2,1,0:T(8,128)(2,1)}, u32[]{:S(2)}, u32[]{:S(2)}) %collective-permute-start.7) | collective-permute-done | bytes 196640 | tf_op jit(solution)/shard_map/ppermute | solution.py:59
  40.8 1.2 %fusion.68 = (f32[2,32]{1,0:T(2,128)S(1)}, f32[2,32,1536]{2,1,0:T(8,128)S(1)}) fusion(bf16[2,32,1536]{2,1,0:T(8,128)(2,1)} %collective-permute-done.7, f32[2,2,32,1536]{3,2,0,1:T(8,128)S(1)} %convert_add_fusion.1, s32[]{:T(128)S(6)} %select_n.108, bf16[2,128,1536]{2,1,0:T(8,128)(2,1)} %param.12, s32[]{:T(128)S(6)} %select_n.92), kind=kLoop, calls=%fused_computation.123 | loop fusion | flops 491456 | bytes 1179912 | tf_op jit(solution)/shard_map/reduce_sum | solution.py:27
  42.0 0.2 multiply_reduce_fusion
  42.2 0.1 bitcast_dynamic-update-slice_fusion.2
  42.4 1.6 %collective-permute-start.8 = (bf16[2,32,1536]{2,1,0:T(8,128)(2,1)S(1)}, bf16[2,32,1536]{2,1,0:T(8,128)(2,1)S(1)}, u32[]{:S(2)}, u32[]{:S(2)}) collective-permute-start(bf16[2,32,1536]{2,1,0:T(8,128)(2,1)S(1)} %get-tuple-element.6), channel_id=1, source_target_pairs={{0,2},{1,3},{2,0},{3,1},{4,6},{5,7},{6,4},{7,5},{8,10},{9,11},{10,... | collective-permute-start | bytes 589832 | tf_op jit(solution)/shard_map/ppermute | solution.py:71
  43.9 0.1 broadcast_compare_fusion.1
  44.0 4.6 %collective-permute-done.8 = bf16[2,32,1536]{2,1,0:T(8,128)(2,1)S(1)} collective-permute-done((bf16[2,32,1536]{2,1,0:T(8,128)(2,1)S(1)}, bf16[2,32,1536]{2,1,0:T(8,128)(2,1)S(1)}, u32[]{:S(2)}, u32[]{:S(2)}) %collective-permute-start.8) | collective-permute-done | bytes 196640 | tf_op jit(solution)/shard_map/ppermute | solution.py:71
  48.8 1.6 %collective-permute-done.9 = bf16[2,2,32,1536]{3,2,1,0:T(8,128)(2,1)S(1)} collective-permute-done((bf16[2,2,32,1536]{3,2,1,0:T(8,128)(2,1)S(1)}, bf16[2,2,32,1536]{3,2,1,0:T(8,128)(2,1)S(1)}, u32[]{:S(2)}, u32[]{:S(2)}) %collective-permute-start.9) | collective-permute-done | bytes 393248 | tf_op jit(solution)/shard_map/ppermute | solution.py:71
  50.4 0.8 %fusion.12 = f32[2,2,128,384]{3,2,0,1:T(8,128)S(1)} fusion(bf16[2,128,1536,1]{2,1,3,0:T(8,128)(2,1)S(1)} %bitcast.134, bf16[2,1536,384]{2,1,0:T(8,128)(2,1)S(1)} %copy-done.6), kind=kOutput, calls=%fused_computation.18 | convolution fusion | flops 603979776 | bytes 3932160 | tf_op jit(solution)/shard_map/std,gdc->gstc/dot_general | solution.py:34
  51.2 0.1 bitcast_select_fusion
  51.4 1.3 %collective-permute-start.10 = (bf16[2,15,384]{2,1,0:T(8,128)(2,1)S(1)}, bf16[2,15,384]{2,1,0:T(8,128)(2,1)S(1)}, u32[]{:S(2)}, u32[]{:S(2)}) collective-permute-start(bf16[2,15,384]{2,1,0:T(8,128)(2,1)S(1)} %get-tuple-element.17), channel_id=1, source_target_pairs={{0,4},{4,8},{8,12},{1,5},{5,9},{9,13},{2,6},{6,10},{10,14},{3,7},{... | collective-permute-start | bytes 69128 | tf_op jit(solution)/shard_map/ppermute | solution.py:193
  52.7 0.9 %fusion.48 = f32[2,98,384]{2,0,1:T(2,128)S(1)} fusion(bf16[2,128,384]{2,1,0:T(8,128)(2,1)S(1)} %bitcast_select_fusion, f32[31,1,384]{2,0,1:T(8,128)S(1)} %bitcast.139), kind=kOutput, calls=%fused_computation.68 | convolution fusion | flops 27998208 | bytes 545280 | tf_op jit(solution)/shard_map/conv_general_dilated | solution.py:197
  53.7 1.4 %collective-permute-start.11 = (bf16[2,15,384]{2,1,0:T(8,128)(2,1)S(1)}, bf16[2,15,384]{2,1,0:T(8,128)(2,1)S(1)}, u32[]{:S(2)}, u32[]{:S(2)}) collective-permute-start(bf16[2,15,384]{2,1,0:T(8,128)(2,1)S(1)} %get-tuple-element.18), channel_id=1, source_target_pairs={{4,0},{8,4},{12,8},{5,1},{9,5},{13,9},{6,2},{10,6},{14,10},{7,3},{... | collective-permute-start | bytes 69128 | tf_op jit(solution)/shard_map/ppermute | solution.py:194
  55.2 0.2 fusion.56
  55.4 4.2 %collective-permute-done.11 = bf16[2,15,384]{2,1,0:T(8,128)(2,1)S(1)} collective-permute-done((bf16[2,15,384]{2,1,0:T(8,128)(2,1)S(1)}, bf16[2,15,384]{2,1,0:T(8,128)(2,1)S(1)}, u32[]{:S(2)}, u32[]{:S(2)}) %collective-permute-start.11) | collective-permute-done | bytes 23072 | tf_op jit(solution)/shard_map/ppermute | solution.py:194
  59.6 0.2 fusion.54
  59.8 0.6 convolution_convert_fusion.1
  60.6 0.5 copy-done.4
  61.1 1.3 %collective-permute-done.12 = bf16[2,2,32,1536]{3,2,0,1:T(8,128)(2,1)} collective-permute-done((bf16[2,2,32,1536]{3,2,0,1:T(8,128)(2,1)S(1)}, bf16[2,2,32,1536]{3,2,0,1:T(8,128)(2,1)}, u32[]{:S(2)}, u32[]{:S(2)}) %collective-permute-start.12) | collective-permute-done | bytes 393248 | tf_op jit(solution)/shard_map/ppermute | solution.py:59
  62.4 1.1 %convert_add_fusion = f32[2,2,32,1536]{3,2,0,1:T(8,128)S(1)} fusion(bf16[2,2,32,1536]{3,2,0,1:T(8,128)(2,1)} %collective-permute-done.12, bf16[2,2,1,32,1536]{4,3,2,1,0:T(8,128)(2,1)S(1)} %get-tuple-element.9), kind=kLoop, calls=%fused_computation.29 | loop fusion | flops 589824 | bytes 1572864 | tf_op jit(solution)/shard_map/add | solution.py:60
  63.6 1.6 %collective-permute-start.13 = (bf16[2,32,1536]{2,1,0:T(8,128)(2,1)S(1)}, bf16[2,32,1536]{2,1,0:T(8,128)(2,1)S(1)}, u32[]{:S(2)}, u32[]{:S(2)}) collective-permute-start(bf16[2,32,1536]{2,1,0:T(8,128)(2,1)S(1)} %fusion.47), channel_id=1, source_target_pairs={{0,2},{1,3},{2,0},{3,1},{4,6},{5,7},{6,4},{7,5},{8,10},{9,11},{10,... | collective-permute-start | bytes 589832 | tf_op jit(solution)/shard_map/ppermute | solution.py:59
  65.1 0.1 broadcast_compare_fusion.2
  65.2 5.4 %collective-permute-done.13 = bf16[2,32,1536]{2,1,0:T(8,128)(2,1)S(1)} collective-permute-done((bf16[2,32,1536]{2,1,0:T(8,128)(2,1)S(1)}, bf16[2,32,1536]{2,1,0:T(8,128)(2,1)S(1)}, u32[]{:S(2)}, u32[]{:S(2)}) %collective-permute-start.13) | collective-permute-done | bytes 196640 | tf_op jit(solution)/shard_map/ppermute | solution.py:59
  70.6 0.8 %fusion.43 = bf16[2,32,1536]{2,1,0:T(8,128)(2,1)} fusion(f32[2,32,1536]{2,1,0:T(8,128)S(1)} %get-tuple-element.8, bf16[2,32,1536]{2,1,0:T(8,128)(2,1)S(1)} %collective-permute-done.13, f32[2,2,32,1536]{3,2,0,1:T(8,128)S(1)} %convert_add_fusion, s32[]{:T(128)S(6)} %select_n.108, bf16[1536]{0:T(1024)(128)(2,1)S(1)} %get-tuple-element.25, ...), kind=kLoop, calls=%fused_computation.52 | loop fusion | flops 884736 | bytes 1185860 | tf_op jit(solution)/shard_map/convert_element_type | solution.py:219
  (66 shorter events, 1.1 us)
Async XLA Ops:
  0.0 3.0 %copy-start = (bf16[3,1536,256]{2,1,0:T(8,128)(2,1)S(1)}, bf16[3,1536,256]{2,1,0:T(8,128)(2,1)}, u32[]{:S(2)}) copy-start(bf16[3,1536,256]{2,1,0:T(8,128)(2,1)} %param.15) | copy-start | bytes 7077892
  3.0 9.3 %copy-start.5 = (s32[2]{0:T(128)S(1)}, s32[2]{0:T(128)}, u32[]{:S(2)}) copy-start(s32[2]{0:T(128)} %param.13) | copy-start | bytes 28
  5.3 8.8 %collective-permute-start = (bf16[3,2,128,1,64]{2,4,1,3,0:T(8,128)(2,1)S(1)}, bf16[3,2,128,1,64]{2,4,1,3,0:T(8,128)(2,1)S(1)}, u32[]{:S(2)}, u32[]{:S(2)}) collective-permute-start(bf16[3,2,128,1,64]{2,4,1,3,0:T(8,128)(2,1)S(1)} %get-tuple-element.16), channel_id=1, source_target_pairs={{0,4},{4,8},{8,12},{12,0},{1,5},{5,9},{9,13},{13,1},{2,6},{6,10},{... | collective-permute-start | bytes 294920 | tf_op jit(solution)/shard_map/ppermute | solution.py:124
  8.4 9.2 %collective-permute-start.1 = (bf16[3,2,128,1,64]{2,4,1,3,0:T(8,128)(2,1)S(1)}, bf16[3,2,128,1,64]{2,4,1,3,0:T(8,128)(2,1)S(1)}, u32[]{:S(2)}, u32[]{:S(2)}) collective-permute-start(bf16[3,2,128,1,64]{2,4,1,3,0:T(8,128)(2,1)S(1)} %get-tuple-element.15), channel_id=1, source_target_pairs={{0,8},{4,12},{8,0},{12,4},{1,9},{5,13},{9,1},{13,5},{2,10},{6,14},... | collective-permute-start | bytes 294920 | tf_op jit(solution)/shard_map/ppermute | solution.py:124
  10.9 6.6 %collective-permute-start.2 = (bf16[3,2,128,1,64]{2,4,1,3,0:T(8,128)(2,1)S(1)}, bf16[3,2,128,1,64]{2,4,1,3,0:T(8,128)(2,1)S(1)}, u32[]{:S(2)}, u32[]{:S(2)}) collective-permute-start(bf16[3,2,128,1,64]{2,4,1,3,0:T(8,128)(2,1)S(1)} %get-tuple-element.14), channel_id=1, source_target_pairs={{0,12},{4,0},{8,4},{12,8},{1,13},{5,1},{9,5},{13,9},{2,14},{6,2},{... | collective-permute-start | bytes 294920 | tf_op jit(solution)/shard_map/ppermute | solution.py:124
  18.9 10.6 %copy-start.1 = (bf16[256,1536]{1,0:T(8,128)(2,1)S(1)}, bf16[256,1536]{1,0:T(8,128)(2,1)}, u32[]{:S(2)}) copy-start(bf16[256,1536]{1,0:T(8,128)(2,1)} %param.16) | copy-start | bytes 2359300
  19.6 5.2 %collective-permute-start.3 = (bf16[2,1,128,64]{2,3,0,1:T(8,128)(2,1)S(1)}, bf16[2,1,128,64]{2,3,0,1:T(8,128)(2,1)S(1)}, u32[]{:S(2)}, u32[]{:S(2)}) collective-permute-start(bf16[2,1,128,64]{2,3,0,1:T(8,128)(2,1)S(1)} %get-tuple-element.23), channel_id=1, source_target_pairs={{0,12},{4,0},{8,4},{12,8},{1,13},{5,1},{9,5},{13,9},{2,14},{6,2},{... | collective-permute-start | bytes 98312 | tf_op jit(solution)/shard_map/ppermute | solution.py:134
  23.3 5.0 %collective-permute-start.4 = (bf16[2,1,128,64]{2,3,0,1:T(8,128)(2,1)S(1)}, bf16[2,1,128,64]{2,3,0,1:T(8,128)(2,1)S(1)}, u32[]{:S(2)}, u32[]{:S(2)}) collective-permute-start(bf16[2,1,128,64]{2,3,0,1:T(8,128)(2,1)S(1)} %get-tuple-element.22), channel_id=1, source_target_pairs={{0,8},{4,12},{8,0},{12,4},{1,9},{5,13},{9,1},{13,5},{2,10},{6,14},... | collective-permute-start | bytes 98312 | tf_op jit(solution)/shard_map/ppermute | solution.py:134
  23.7 5.7 %collective-permute-start.5 = (bf16[2,1,128,64]{2,3,0,1:T(8,128)(2,1)S(1)}, bf16[2,1,128,64]{2,3,0,1:T(8,128)(2,1)S(1)}, u32[]{:S(2)}, u32[]{:S(2)}) collective-permute-start(bf16[2,1,128,64]{2,3,0,1:T(8,128)(2,1)S(1)} %get-tuple-element.21), channel_id=1, source_target_pairs={{0,4},{4,8},{8,12},{12,0},{1,5},{5,9},{9,13},{13,1},{2,6},{6,10},{... | collective-permute-start | bytes 98312 | tf_op jit(solution)/shard_map/ppermute | solution.py:134
  30.0 12.2 %copy-start.3 = (f32[1536]{0:T(1024)S(1)}, f32[1536]{0:T(1024)}, u32[]{:S(2)}) copy-start(f32[1536]{0:T(1024)} %param.17) | copy-start | bytes 18436
  30.0 1.8 %collective-permute-start.6 = (bf16[2,2,32,1536]{3,2,0,1:T(8,128)(2,1)S(1)}, bf16[2,2,32,1536]{3,2,0,1:T(8,128)(2,1)S(1)}, u32[]{:S(2)}, u32[]{:S(2)}) collective-permute-start(bf16[2,2,32,1536]{3,2,0,1:T(8,128)(2,1)S(1)} %bitcast.137), channel_id=1, source_target_pairs={{0,1},{1,0},{2,3},{3,2},{4,5},{5,4},{6,7},{7,6},{8,9},{9,8},{10,11... | collective-permute-start | bytes 1179656 | tf_op jit(solution)/shard_map/ppermute | solution.py:59
  31.8 0.8 %copy-start.2 = (bf16[2,2,32,1536]{3,2,0,1:T(8,128)(2,1)}, bf16[2,2,32,1536]{3,2,0,1:T(8,128)(2,1)S(1)}, u32[]{:S(2)}) copy-start(bf16[2,2,32,1536]{3,2,0,1:T(8,128)(2,1)S(1)} %collective-permute-done.6) | copy-start | bytes 1179652
  33.7 7.1 %collective-permute-start.7 = (bf16[2,32,1536]{2,1,0:T(8,128)(2,1)S(1)}, bf16[2,32,1536]{2,1,0:T(8,128)(2,1)}, u32[]{:S(2)}, u32[]{:S(2)}) collective-permute-start(bf16[2,32,1536]{2,1,0:T(8,128)(2,1)S(1)} %fusion.46), channel_id=1, source_target_pairs={{0,2},{1,3},{2,0},{3,1},{4,6},{5,7},{6,4},{7,5},{8,10},{9,11},{10,... | collective-permute-start | bytes 589832 | tf_op jit(solution)/shard_map/ppermute | solution.py:59
  42.0 8.4 %copy-start.6 = (bf16[2,1536,384]{2,1,0:T(8,128)(2,1)S(1)}, bf16[2,1536,384]{2,1,0:T(8,128)(2,1)}, u32[]{:S(2)}) copy-start(bf16[2,1536,384]{2,1,0:T(8,128)(2,1)} %param.18) | copy-start | bytes 7077892
  42.4 6.2 %collective-permute-start.8 = (bf16[2,32,1536]{2,1,0:T(8,128)(2,1)S(1)}, bf16[2,32,1536]{2,1,0:T(8,128)(2,1)S(1)}, u32[]{:S(2)}, u32[]{:S(2)}) collective-permute-start(bf16[2,32,1536]{2,1,0:T(8,128)(2,1)S(1)} %get-tuple-element.6), channel_id=1, source_target_pairs={{0,2},{1,3},{2,0},{3,1},{4,6},{5,7},{6,4},{7,5},{8,10},{9,11},{10,... | collective-permute-start | bytes 589832 | tf_op jit(solution)/shard_map/ppermute | solution.py:71
  48.6 1.8 %collective-permute-start.9 = (bf16[2,2,32,1536]{3,2,1,0:T(8,128)(2,1)S(1)}, bf16[2,2,32,1536]{3,2,1,0:T(8,128)(2,1)S(1)}, u32[]{:S(2)}, u32[]{:S(2)}) collective-permute-start(bf16[2,2,32,1536]{3,2,1,0:T(8,128)(2,1)S(1)} %bitcast_dynamic-update-slice_fusion.3), channel_id=1, source_target_pairs={{0,1},{1,0},{2,3},{3,2},{4,5},{5,4},{6,7},{7,6},{8,9},{9,8},{10,11... | collective-permute-start | bytes 1179656 | tf_op jit(solution)/shard_map/ppermute | solution.py:71
  50.4 2.3 %copy-start.8 = (f32[31,384]{1,0:T(8,128)S(1)}, f32[31,384]{1,0:T(8,128)}, u32[]{:S(2)}) copy-start(f32[31,384]{1,0:T(8,128)} %param.19) | copy-start | bytes 142852
  51.4 3.7 %collective-permute-start.10 = (bf16[2,15,384]{2,1,0:T(8,128)(2,1)S(1)}, bf16[2,15,384]{2,1,0:T(8,128)(2,1)S(1)}, u32[]{:S(2)}, u32[]{:S(2)}) collective-permute-start(bf16[2,15,384]{2,1,0:T(8,128)(2,1)S(1)} %get-tuple-element.17), channel_id=1, source_target_pairs={{0,4},{4,8},{8,12},{1,5},{5,9},{9,13},{2,6},{6,10},{10,14},{3,7},{... | collective-permute-start | bytes 69128 | tf_op jit(solution)/shard_map/ppermute | solution.py:193
  53.6 6.2 %copy-start.7 = (bf16[384,1536]{1,0:T(8,128)(2,1)S(1)}, bf16[384,1536]{1,0:T(8,128)(2,1)}, u32[]{:S(2)}) copy-start(bf16[384,1536]{1,0:T(8,128)(2,1)} %param.22) | copy-start | bytes 3538948
  53.6 6.2 %copy-start.9 = (f32[384]{0:T(512)S(1)}, f32[384]{0:T(512)}, u32[]{:S(2)}) copy-start(f32[384]{0:T(512)} %param.21) | copy-start | bytes 4612
  53.6 6.2 %copy-start.10 = (f32[384]{0:T(512)S(1)}, f32[384]{0:T(512)}, u32[]{:S(2)}) copy-start(f32[384]{0:T(512)} %param.20) | copy-start | bytes 4612
  53.7 5.9 %collective-permute-start.11 = (bf16[2,15,384]{2,1,0:T(8,128)(2,1)S(1)}, bf16[2,15,384]{2,1,0:T(8,128)(2,1)S(1)}, u32[]{:S(2)}, u32[]{:S(2)}) collective-permute-start(bf16[2,15,384]{2,1,0:T(8,128)(2,1)S(1)} %get-tuple-element.18), channel_id=1, source_target_pairs={{4,0},{8,4},{12,8},{5,1},{9,5},{13,9},{6,2},{10,6},{14,10},{7,3},{... | collective-permute-start | bytes 69128 | tf_op jit(solution)/shard_map/ppermute | solution.py:194
  60.4 0.7 copy-start.4
  60.5 1.9 %collective-permute-start.12 = (bf16[2,2,32,1536]{3,2,0,1:T(8,128)(2,1)S(1)}, bf16[2,2,32,1536]{3,2,0,1:T(8,128)(2,1)}, u32[]{:S(2)}, u32[]{:S(2)}) collective-permute-start(bf16[2,2,32,1536]{3,2,0,1:T(8,128)(2,1)S(1)} %bitcast.138), channel_id=1, source_target_pairs={{0,1},{1,0},{2,3},{3,2},{4,5},{5,4},{6,7},{7,6},{8,9},{9,8},{10,11... | collective-permute-start | bytes 1179656 | tf_op jit(solution)/shard_map/ppermute | solution.py:59
  63.6 7.0 %collective-permute-start.13 = (bf16[2,32,1536]{2,1,0:T(8,128)(2,1)S(1)}, bf16[2,32,1536]{2,1,0:T(8,128)(2,1)S(1)}, u32[]{:S(2)}, u32[]{:S(2)}) collective-permute-start(bf16[2,32,1536]{2,1,0:T(8,128)(2,1)S(1)} %fusion.47), channel_id=1, source_target_pairs={{0,2},{1,3},{2,0},{3,1},{4,6},{5,7},{6,4},{7,5},{8,10},{9,11},{10,... | collective-permute-start | bytes 589832 | tf_op jit(solution)/shard_map/ppermute | solution.py:59

commit v18 on v9

--- a/solution.py
+++ b/solution.py
@@ -61,18 +61,18 @@
     return acc
 
 
-def all_gather_rows(x, axis, dim):
+def all_gather_rows(x, axis, dim, last_bit=0):
     count, rank = lax.axis_size(axis), lax.axis_index(axis)
     bits = bit_count(count)
     shape = x.shape
     acc = x
-    for k, b in enumerate(reversed(range(bits))):
+    for k, b in enumerate(reversed(range(last_bit, bits))):
         mine = (rank >> b) & 1
         got = lax.ppermute(acc, axis, xor_pairs(count, 1 << b))
         both = jnp.zeros(acc.shape[: dim + k] + (2,) + acc.shape[dim + k :], acc.dtype)
         both = lax.dynamic_update_index_in_dim(both, acc, mine, dim + k)
         acc = lax.dynamic_update_index_in_dim(both, got, 1 - mine, dim + k)
-    return acc.reshape(shape[:dim] + (shape[dim] * count,) + shape[dim + 1 :])
+    return acc.reshape(shape[:dim] + (shape[dim] * (count >> last_bit),) + shape[dim + 1 :])
 
 
 def ring_gather(x, axis):
@@ -156,6 +156,7 @@
     ctx_count = lax.axis_size("ctx")
     score_scale = HEAD_DIM ** (-0.5)
     first_frame = ctx_rank * frames_here
+    w_glu_pair = lax.ppermute(w_glu, "mp", xor_pairs(lax.axis_size("mp"), 1))
     normed = layer_norm(features.astype(jnp.float32), attn_gain).astype(jnp.bfloat16)
     projected = jnp.einsum(
         "std,idc->istc", normed, w_qkv, preferred_element_type=jnp.float32
@@ -182,8 +183,16 @@
     features_mine = lax.dynamic_slice_in_dim(features, row_start, rows_mine, 1)
     residual_mine = features_mine.astype(jnp.float32) + attn_mine
     normed_mine = layer_norm(residual_mine, conv_gain).astype(jnp.bfloat16)
-    normed_conv = all_gather_rows(normed_mine, "mp", 1)
-    gated_rows = gated_units(normed_conv, w_glu)
+    pair = xor_pairs(mp_count, 1)
+    held_rows = all_gather_rows(normed_mine, "mp", 1, last_bit=1)
+    gated_mine = gated_units(held_rows, w_glu)
+    gated_lent = lax.ppermute(gated_units(held_rows, w_glu_pair), "mp", pair)
+    bit0 = mp_rank & 1
+    split_rows = (records, mp_count // 2, rows_mine, gated_mine.shape[-1])
+    gated_rows = jnp.zeros((records, mp_count // 2, 2, rows_mine, gated_mine.shape[-1]), jnp.bfloat16)
+    gated_rows = lax.dynamic_update_index_in_dim(gated_rows, gated_mine.reshape(split_rows), bit0, 2)
+    gated_rows = lax.dynamic_update_index_in_dim(gated_rows, gated_lent.reshape(split_rows), 1 - bit0, 2)
+    gated_rows = gated_rows.reshape(records, frames_here, gated_mine.shape[-1])
     frame_ids = first_frame + jnp.arange(frames_here, dtype=jnp.int32)
     frame_live = frame_ids[None, :] < frame_counts[:, None]
     gated_rows = jnp.where(frame_live[..., None], gated_rows, jnp.zeros((), jnp.bfloat16))

time: 71.6 us -> 73.4 us (1.025)
  matrix products: 6.24 us -> 8.15 us
    dot_general x1 -> x2, matrix products: 0.8 us -> 2.62 us  [gated_units(): jnp.einsum('std,gdc->gstc', normed, w_glu, preferred_element_type=jnp.flo...]
    ppermute x2 -> x1, waiting for transfers between devices: 6.15 us -> 4.5 us  [all_gather_rows(): got = lax.ppermute(acc, axis, xor_pairs(count, 1 << b))]
    ppermute x0 -> x2, waiting for transfers between devices: none -> 1.04 us  [the longest x1 1.04 us: shards(): gated_lent = lax.ppermute(gated_units(held_rows, w_glu_pair), 'mp', pair)]
    ppermute x2 -> x1, starting transfers between devices: 1.63 us -> 1.55 us  [all_gather_rows(): got = lax.ppermute(acc, axis, xor_pairs(count, 1 << b))]
  transfers between devices with their start and end apart: 14 -> 15, of which waited for: 13 -> 13; matrix products, arithmetic and copies ran while one was open for 1% -> 4% of each run, Pallas kernels for 0% -> 0%
where the time goes in v18:
time: 73.4 us; the launch traced here: 73.1 us
  waiting for transfers between devices  35 us (48%)
  starting transfers between devices  18.8 us (26%)
  other arithmetic  8.67 us (12%)
  matrix products  8.15 us (11%)
  local copies, waits for them, and re-layouts  2 us (3%)
    ppermute x4, waiting for transfers between devices, reduce_scatter_rows(): lax.ppermute(send.astype(jnp.bfloat16), axis, xor_pairs(count, 1 << b))  14.4 us
    ppermute x3, starting transfers between devices, attend_by_heads(): pieces.append(lax.ppermute(send, axis, pairs))  7.01 us
    ppermute x3, waiting for transfers between devices, attend_by_heads(): back.append(lax.ppermute(rows, axis, pairs))  5.45 us
    ppermute x3, waiting for transfers between devices, attend_by_heads(): pieces.append(lax.ppermute(send, axis, pairs))  5.16 us
    ppermute x1, waiting for transfers between devices, all_gather_rows(): got = lax.ppermute(acc, axis, xor_pairs(count, 1 << b))  4.5 us
    ppermute x3, starting transfers between devices, attend_by_heads(): back.append(lax.ppermute(rows, axis, pairs))  4.3 us
    ppermute x1, waiting for transfers between devices, with_halo(): after = lax.ppermute(initial, axis, down)  4.22 us
    ppermute x4, starting transfers between devices, reduce_scatter_rows(): lax.ppermute(send.astype(jnp.bfloat16), axis, xor_pairs(count, 1 << b))  3.26 us
  transfers between devices with their start and end apart: 15, of which 13 were waited for; matrix products, arithmetic and copies ran while one was open for 4% of the time, Pallas kernels for 0%

profile of v18, /device:TPU:0, one launch (start us, length us, event | category | flops | bytes accessed | tf_op | source)
XLA Modules:
  0.0 73.1 jit_solution(7873024071117726994)
XLA Ops:
  0.0 1.5 %convert_reduce_fusion = f32[2,128]{1,0:T(2,128)S(1)} fusion(bf16[2,128,1536]{2,1,0:T(8,128)(2,1)} %param.12), kind=kLoop, calls=%fused_computation.11 | loop fusion | flops 786176 | bytes 787456 | tf_op jit(solution)/shard_map/reduce_sum | solution.py:27
  1.5 1.5 %fusion.11 = f32[2,128]{1,0:T(2,128)S(1)} fusion(bf16[2,128,1536]{2,1,0:T(8,128)(2,1)} %param.12, f32[2,128]{1,0:T(2,128)S(1)} %broadcast_multiply_fusion.1), kind=kLoop, calls=%fused_computation.17 | loop fusion | flops 1572608 | bytes 788480 | tf_op jit(solution)/shard_map/reduce_sum | solution.py:29
  3.0 2.0 %fusion.23 = bf16[3,2,128,256]{3,2,0,1:T(8,128)(2,1)S(1)} fusion(bf16[3,1536,256]{2,1,0:T(8,128)(2,1)S(1)} %copy-done, bf16[2,128,1536]{2,1,0:T(8,128)(2,1)} %param.12, f32[1536]{0:T(1024)} %param.14, f32[2,128]{1,0:T(2,128)S(1)} %add_rsqrt_fusion.1, f32[2,128]{1,0:T(2,128)S(1)} %broadcast_multiply_fusion.1), kind=kOutput, calls=%fused_computation.23 | convolution fusion | flops 606142464 | bytes 3547136 | tf_op jit(solution)/shard_map/std,idc->istc/dot_general | solution.py:161
  5.0 0.2 copy.42
  5.3 3.1 %collective-permute-start = (bf16[3,2,128,1,64]{2,4,1,3,0:T(8,128)(2,1)S(1)}, bf16[3,2,128,1,64]{2,4,1,3,0:T(8,128)(2,1)S(1)}, u32[]{:S(2)}, u32[]{:S(2)}) collective-permute-start(bf16[3,2,128,1,64]{2,4,1,3,0:T(8,128)(2,1)S(1)} %get-tuple-element.16), channel_id=1, source_target_pairs={{0,4},{4,8},{8,12},{12,0},{1,5},{5,9},{9,13},{13,1},{2,6},{6,10},{... | collective-permute-start | bytes 294920 | tf_op jit(solution)/shard_map/ppermute | solution.py:124
  8.4 2.6 %collective-permute-start.1 = (bf16[3,2,128,1,64]{2,4,1,3,0:T(8,128)(2,1)S(1)}, bf16[3,2,128,1,64]{2,4,1,3,0:T(8,128)(2,1)S(1)}, u32[]{:S(2)}, u32[]{:S(2)}) collective-permute-start(bf16[3,2,128,1,64]{2,4,1,3,0:T(8,128)(2,1)S(1)} %get-tuple-element.15), channel_id=1, source_target_pairs={{0,8},{4,12},{8,0},{12,4},{1,9},{5,13},{9,1},{13,5},{2,10},{6,14},... | collective-permute-start | bytes 294920 | tf_op jit(solution)/shard_map/ppermute | solution.py:124
  10.9 1.3 %collective-permute-start.2 = (bf16[3,2,128,1,64]{2,4,1,3,0:T(8,128)(2,1)S(1)}, bf16[3,2,128,1,64]{2,4,1,3,0:T(8,128)(2,1)S(1)}, u32[]{:S(2)}, u32[]{:S(2)}) collective-permute-start(bf16[3,2,128,1,64]{2,4,1,3,0:T(8,128)(2,1)S(1)} %get-tuple-element.14), channel_id=1, source_target_pairs={{0,12},{4,0},{8,4},{12,8},{1,13},{5,1},{9,5},{13,9},{2,14},{6,2},{... | collective-permute-start | bytes 294920 | tf_op jit(solution)/shard_map/ppermute | solution.py:124
  12.4 1.6 %collective-permute-done = bf16[3,2,128,1,64]{2,4,1,3,0:T(8,128)(2,1)S(1)} collective-permute-done((bf16[3,2,128,1,64]{2,4,1,3,0:T(8,128)(2,1)S(1)}, bf16[3,2,128,1,64]{2,4,1,3,0:T(8,128)(2,1)S(1)}, u32[]{:S(2)}, u32[]{:S(2)}) %collective-permute-start) | collective-permute-done | bytes 98336 | tf_op jit(solution)/shard_map/ppermute | solution.py:124
  14.0 3.5 %collective-permute-done.1 = bf16[3,2,128,1,64]{2,4,1,3,0:T(8,128)(2,1)S(1)} collective-permute-done((bf16[3,2,128,1,64]{2,4,1,3,0:T(8,128)(2,1)S(1)}, bf16[3,2,128,1,64]{2,4,1,3,0:T(8,128)(2,1)S(1)}, u32[]{:S(2)}, u32[]{:S(2)}) %collective-permute-start.1) | collective-permute-done | bytes 98336 | tf_op jit(solution)/shard_map/ppermute | solution.py:124
  17.6 0.8 %fusion.8 = (f32[2,512]{1,0:T(2,128)S(1)}, f32[2,512,512]{1,2,0:T(8,128)S(1)}) fusion(pred[2,512]{1,0:T(4,128)(4,1)S(1)} %broadcast_compare_fusion.1, bf16[3,2,512,1,64]{2,4,1,3,0:T(8,128)(2,1)S(1)} %pad_maximum_fusion), kind=kOutput, calls=%fused_computation.14 | convolution fusion | flops 68680704 | bytes 2365440 | tf_op jit(solution)/shard_map/sqhe,skhe->shqk/dot_general | solution.py:96
  18.4 0.5 fusion.9
  18.9 0.6 fusion.28
  19.6 3.6 %collective-permute-start.3 = (bf16[2,1,128,64]{2,3,0,1:T(8,128)(2,1)S(1)}, bf16[2,1,128,64]{2,3,0,1:T(8,128)(2,1)S(1)}, u32[]{:S(2)}, u32[]{:S(2)}) collective-permute-start(bf16[2,1,128,64]{2,3,0,1:T(8,128)(2,1)S(1)} %get-tuple-element.21), channel_id=1, source_target_pairs={{0,12},{4,0},{8,4},{12,8},{1,13},{5,1},{9,5},{13,9},{2,14},{6,2},{... | collective-permute-start | bytes 98312 | tf_op jit(solution)/shard_map/ppermute | solution.py:134
  23.3 0.4 collective-permute-start.4
  23.7 0.2 collective-permute-start.5
  23.9 0.9 %collective-permute-done.3 = bf16[2,1,128,64]{2,3,0,1:T(8,128)(2,1)S(1)} collective-permute-done((bf16[2,1,128,64]{2,3,0,1:T(8,128)(2,1)S(1)}, bf16[2,1,128,64]{2,3,0,1:T(8,128)(2,1)S(1)}, u32[]{:S(2)}, u32[]{:S(2)}) %collective-permute-start.3) | collective-permute-done | bytes 32800 | tf_op jit(solution)/shard_map/ppermute | solution.py:134
  24.9 3.4 %collective-permute-done.4 = bf16[2,1,128,64]{2,3,0,1:T(8,128)(2,1)S(1)} collective-permute-done((bf16[2,1,128,64]{2,3,0,1:T(8,128)(2,1)S(1)}, bf16[2,1,128,64]{2,3,0,1:T(8,128)(2,1)S(1)}, u32[]{:S(2)}, u32[]{:S(2)}) %collective-permute-start.4) | collective-permute-done | bytes 32800 | tf_op jit(solution)/shard_map/ppermute | solution.py:134
  28.2 1.2 %collective-permute-done.5 = bf16[2,1,128,64]{2,3,0,1:T(8,128)(2,1)S(1)} collective-permute-done((bf16[2,1,128,64]{2,3,0,1:T(8,128)(2,1)S(1)}, bf16[2,1,128,64]{2,3,0,1:T(8,128)(2,1)S(1)}, u32[]{:S(2)}, u32[]{:S(2)}) %collective-permute-start.5) | collective-permute-done | bytes 32800 | tf_op jit(solution)/shard_map/ppermute | solution.py:134
  29.5 0.4 convolution_convert_fusion
  30.1 1.7 %collective-permute-done.6 = bf16[2,2,32,1536]{3,2,0,1:T(8,128)(2,1)S(1)} collective-permute-done((bf16[2,2,32,1536]{3,2,0,1:T(8,128)(2,1)S(1)}, bf16[2,2,32,1536]{3,2,0,1:T(8,128)(2,1)S(1)}, u32[]{:S(2)}, u32[]{:S(2)}) %collective-permute-start.6) | collective-permute-done | bytes 393248 | tf_op jit(solution)/shard_map/ppermute | solution.py:59
  31.8 0.8 %copy-done.3 = bf16[2,2,32,1536]{3,2,0,1:T(8,128)(2,1)} copy-done((bf16[2,2,32,1536]{3,2,0,1:T(8,128)(2,1)}, bf16[2,2,32,1536]{3,2,0,1:T(8,128)(2,1)S(1)}, u32[]{:S(2)}) %copy-start.3) | copy-done | bytes 393240
  32.6 1.1 %convert_add_fusion.1 = f32[2,2,32,1536]{3,2,0,1:T(8,128)S(1)} fusion(bf16[2,2,32,1536]{3,2,0,1:T(8,128)(2,1)} %copy-done.3, bf16[2,2,1,32,1536]{4,3,2,1,0:T(8,128)(2,1)S(1)} %get-tuple-element.11), kind=kLoop, calls=%fused_computation.33 | loop fusion | flops 589824 | bytes 1572864 | tf_op jit(solution)/shard_map/add | solution.py:60
  33.7 1.6 %collective-permute-start.7 = (bf16[2,32,1536]{2,1,0:T(8,128)(2,1)S(1)}, bf16[2,32,1536]{2,1,0:T(8,128)(2,1)}, u32[]{:S(2)}, u32[]{:S(2)}) collective-permute-start(bf16[2,32,1536]{2,1,0:T(8,128)(2,1)S(1)} %fusion.52), channel_id=1, source_target_pairs={{0,2},{1,3},{2,0},{3,1},{4,6},{5,7},{6,4},{7,5},{8,10},{9,11},{10,... | collective-permute-start | bytes 589832 | tf_op jit(solution)/shard_map/ppermute | solution.py:59
  35.2 5.6 %collective-permute-done.7 = bf16[2,32,1536]{2,1,0:T(8,128)(2,1)} collective-permute-done((bf16[2,32,1536]{2,1,0:T(8,128)(2,1)S(1)}, bf16[2,32,1536]{2,1,0:T(8,128)(2,1)}, u32[]{:S(2)}, u32[]{:S(2)}) %collective-permute-start.7) | collective-permute-done | bytes 196640 | tf_op jit(solution)/shard_map/ppermute | solution.py:59
  40.8 1.2 %fusion.77 = (f32[2,32]{1,0:T(2,128)S(1)}, f32[2,32,1536]{2,1,0:T(8,128)S(1)}) fusion(bf16[2,32,1536]{2,1,0:T(8,128)(2,1)} %collective-permute-done.7, f32[2,2,32,1536]{3,2,0,1:T(8,128)S(1)} %convert_add_fusion.1, s32[]{:T(128)S(6)} %select_n.112, bf16[2,128,1536]{2,1,0:T(8,128)(2,1)} %param.12, s32[]{:T(128)S(6)} %select_n.96), kind=kLoop, calls=%fused_computation.129 | loop fusion | flops 491456 | bytes 1179912 | tf_op jit(solution)/shard_map/reduce_sum | solution.py:27
  42.0 0.2 multiply_reduce_fusion
  42.2 0.1 bitcast_dynamic-update-slice_fusion.1
  42.4 1.6 %collective-permute-start.8 = (bf16[2,32,1536]{2,1,0:T(8,128)(2,1)S(1)}, bf16[2,32,1536]{2,1,0:T(8,128)(2,1)S(1)}, u32[]{:S(2)}, u32[]{:S(2)}) collective-permute-start(bf16[2,32,1536]{2,1,0:T(8,128)(2,1)S(1)} %get-tuple-element.6), channel_id=1, source_target_pairs={{0,2},{1,3},{2,0},{3,1},{4,6},{5,7},{6,4},{7,5},{8,10},{9,11},{10,... | collective-permute-start | bytes 589832 | tf_op jit(solution)/shard_map/ppermute | solution.py:71
  44.1 4.5 %collective-permute-done.8 = bf16[2,32,1536]{2,1,0:T(8,128)(2,1)S(1)} collective-permute-done((bf16[2,32,1536]{2,1,0:T(8,128)(2,1)S(1)}, bf16[2,32,1536]{2,1,0:T(8,128)(2,1)S(1)}, u32[]{:S(2)}, u32[]{:S(2)}) %collective-permute-start.8) | collective-permute-done | bytes 196640 | tf_op jit(solution)/shard_map/ppermute | solution.py:71
  48.6 0.5 fusion.17
  49.2 2.1 %fusion.20 = f32[2,2,64,384]{3,2,0,1:T(8,128)S(1)} fusion(bf16[2,64,1536,1]{2,1,3,0:T(8,128)(2,1)S(1)} %bitcast.137, bf16[2,1536,384]{2,1,0:T(8,128)(2,1)} %collective-permute-done.9), kind=kOutput, calls=%fused_computation.22 | convolution fusion | flops 301989888 | bytes 3145728 | tf_op jit(solution)/shard_map/std,gdc->gstc/dot_general | solution.py:34
  51.5 0.1 broadcast_in_dim.84
  51.6 0.1 copy_dynamic-update-slice_fusion.1
  51.7 1.0 %collective-permute-done.10 = bf16[2,64,384]{2,1,0:T(8,128)(2,1)S(1)} collective-permute-done((bf16[2,64,384]{2,1,0:T(8,128)(2,1)S(1)}, bf16[2,64,384]{2,1,0:T(8,128)(2,1)S(1)}, u32[]{:S(2)}, u32[]{:S(2)}) %collective-permute-start.10) | collective-permute-done | bytes 98336 | tf_op jit(solution)/shard_map/ppermute | solution.py:189
  52.7 0.1 copy_dynamic-update-slice_fusion
  52.9 0.3 broadcast_select_fusion
  53.2 1.3 %collective-permute-start.11 = (bf16[2,15,384]{2,0,1:T(2,128)(2,1)S(1)}, bf16[2,15,384]{2,0,1:T(2,128)(2,1)S(1)}, u32[]{:S(2)}, u32[]{:S(2)}) collective-permute-start(bf16[2,15,384]{2,0,1:T(2,128)(2,1)S(1)} %get-tuple-element.17), channel_id=1, source_target_pairs={{0,4},{4,8},{8,12},{1,5},{5,9},{9,13},{2,6},{6,10},{10,14},{3,7},{... | collective-permute-start | bytes 69128 | tf_op jit(solution)/shard_map/ppermute | solution.py:20
  54.5 1.3 %collective-permute-start.12 = (bf16[2,15,384]{2,0,1:T(2,128)(2,1)S(1)}, bf16[2,15,384]{2,0,1:T(2,128)(2,1)S(1)}, u32[]{:S(2)}, u32[]{:S(2)}) collective-permute-start(bf16[2,15,384]{2,0,1:T(2,128)(2,1)S(1)} %get-tuple-element.18), channel_id=1, source_target_pairs={{4,0},{8,4},{12,8},{5,1},{9,5},{13,9},{6,2},{10,6},{14,10},{7,3},{... | collective-permute-start | bytes 69128 | tf_op jit(solution)/shard_map/ppermute | solution.py:21
  55.8 0.2 collective-permute-done.11
  56.0 4.2 %collective-permute-done.12 = bf16[2,15,384]{2,0,1:T(2,128)(2,1)S(1)} collective-permute-done((bf16[2,15,384]{2,0,1:T(2,128)(2,1)S(1)}, bf16[2,15,384]{2,0,1:T(2,128)(2,1)S(1)}, u32[]{:S(2)}, u32[]{:S(2)}) %collective-permute-start.12) | collective-permute-done | bytes 23072 | tf_op jit(solution)/shard_map/ppermute | solution.py:21
  60.2 1.2 %fusion.46 = f32[2,128,384]{2,0,1:T(2,128)S(1)} fusion(bf16[2,15,384]{2,0,1:T(2,128)(2,1)S(1)} %collective-permute-done.12, bf16[2,128,384]{2,0,1:T(2,128)(2,1)S(1)} %broadcast_select_fusion, bf16[2,15,384]{2,0,1:T(2,128)(2,1)S(1)} %collective-permute-done.11, f32[31,1,384]{2,0,1:T(8,128)S(1)} %bitcast.146), kind=kOutput, calls=%fused_computation.59 | convolution fusion | flops 37297152 | bytes 683520 | tf_op jit(solution)/shard_map/conv_general_dilated | solution.py:201
  61.4 0.1 copy-done.7
  61.5 0.6 convolution_convert_fusion.1
  62.3 1.8 %collective-permute-done.13 = bf16[2,2,32,1536]{3,2,0,1:T(8,128)(2,1)} collective-permute-done((bf16[2,2,32,1536]{3,2,0,1:T(8,128)(2,1)S(1)}, bf16[2,2,32,1536]{3,2,0,1:T(8,128)(2,1)}, u32[]{:S(2)}, u32[]{:S(2)}) %collective-permute-start.13) | collective-permute-done | bytes 393248 | tf_op jit(solution)/shard_map/ppermute | solution.py:59
  64.1 1.1 %convert_add_fusion = f32[2,2,32,1536]{3,2,0,1:T(8,128)S(1)} fusion(bf16[2,2,32,1536]{3,2,0,1:T(8,128)(2,1)} %collective-permute-done.13, bf16[2,2,1,32,1536]{4,3,2,1,0:T(8,128)(2,1)S(1)} %get-tuple-element.9), kind=kLoop, calls=%fused_computation.32 | loop fusion | flops 589824 | bytes 1572864 | tf_op jit(solution)/shard_map/add | solution.py:60
  65.3 1.6 %collective-permute-start.14 = (bf16[2,32,1536]{2,1,0:T(8,128)(2,1)S(1)}, bf16[2,32,1536]{2,1,0:T(8,128)(2,1)S(1)}, u32[]{:S(2)}, u32[]{:S(2)}) collective-permute-start(bf16[2,32,1536]{2,1,0:T(8,128)(2,1)S(1)} %fusion.53), channel_id=1, source_target_pairs={{0,2},{1,3},{2,0},{3,1},{4,6},{5,7},{6,4},{7,5},{8,10},{9,11},{10,... | collective-permute-start | bytes 589832 | tf_op jit(solution)/shard_map/ppermute | solution.py:59
  66.9 5.4 %collective-permute-done.14 = bf16[2,32,1536]{2,1,0:T(8,128)(2,1)S(1)} collective-permute-done((bf16[2,32,1536]{2,1,0:T(8,128)(2,1)S(1)}, bf16[2,32,1536]{2,1,0:T(8,128)(2,1)S(1)}, u32[]{:S(2)}, u32[]{:S(2)}) %collective-permute-start.14) | collective-permute-done | bytes 196640 | tf_op jit(solution)/shard_map/ppermute | solution.py:59
  72.3 0.8 %fusion.43 = bf16[2,32,1536]{2,1,0:T(8,128)(2,1)} fusion(f32[2,32,1536]{2,1,0:T(8,128)S(1)} %get-tuple-element.8, bf16[2,32,1536]{2,1,0:T(8,128)(2,1)S(1)} %collective-permute-done.14, f32[2,2,32,1536]{3,2,0,1:T(8,128)S(1)} %convert_add_fusion, s32[]{:T(128)S(6)} %select_n.112, bf16[1536]{0:T(1024)(128)(2,1)S(1)} %get-tuple-element.23, ...), kind=kLoop, calls=%fused_computation.46 | loop fusion | flops 884736 | bytes 1185860 | tf_op jit(solution)/shard_map/convert_element_type | solution.py:218
  (64 shorter events, 1.3 us)
Async XLA Ops:
  0.0 3.0 %copy-start = (bf16[3,1536,256]{2,1,0:T(8,128)(2,1)S(1)}, bf16[3,1536,256]{2,1,0:T(8,128)(2,1)}, u32[]{:S(2)}) copy-start(bf16[3,1536,256]{2,1,0:T(8,128)(2,1)} %param.15) | copy-start | bytes 7077892
  3.0 9.3 %copy-start.6 = (s32[2]{0:T(128)S(1)}, s32[2]{0:T(128)}, u32[]{:S(2)}) copy-start(s32[2]{0:T(128)} %param.13) | copy-start | bytes 28
  5.3 8.8 %collective-permute-start = (bf16[3,2,128,1,64]{2,4,1,3,0:T(8,128)(2,1)S(1)}, bf16[3,2,128,1,64]{2,4,1,3,0:T(8,128)(2,1)S(1)}, u32[]{:S(2)}, u32[]{:S(2)}) collective-permute-start(bf16[3,2,128,1,64]{2,4,1,3,0:T(8,128)(2,1)S(1)} %get-tuple-element.16), channel_id=1, source_target_pairs={{0,4},{4,8},{8,12},{12,0},{1,5},{5,9},{9,13},{13,1},{2,6},{6,10},{... | collective-permute-start | bytes 294920 | tf_op jit(solution)/shard_map/ppermute | solution.py:124
  8.4 9.2 %collective-permute-start.1 = (bf16[3,2,128,1,64]{2,4,1,3,0:T(8,128)(2,1)S(1)}, bf16[3,2,128,1,64]{2,4,1,3,0:T(8,128)(2,1)S(1)}, u32[]{:S(2)}, u32[]{:S(2)}) collective-permute-start(bf16[3,2,128,1,64]{2,4,1,3,0:T(8,128)(2,1)S(1)} %get-tuple-element.15), channel_id=1, source_target_pairs={{0,8},{4,12},{8,0},{12,4},{1,9},{5,13},{9,1},{13,5},{2,10},{6,14},... | collective-permute-start | bytes 294920 | tf_op jit(solution)/shard_map/ppermute | solution.py:124
  10.9 6.6 %collective-permute-start.2 = (bf16[3,2,128,1,64]{2,4,1,3,0:T(8,128)(2,1)S(1)}, bf16[3,2,128,1,64]{2,4,1,3,0:T(8,128)(2,1)S(1)}, u32[]{:S(2)}, u32[]{:S(2)}) collective-permute-start(bf16[3,2,128,1,64]{2,4,1,3,0:T(8,128)(2,1)S(1)} %get-tuple-element.14), channel_id=1, source_target_pairs={{0,12},{4,0},{8,4},{12,8},{1,13},{5,1},{9,5},{13,9},{2,14},{6,2},{... | collective-permute-start | bytes 294920 | tf_op jit(solution)/shard_map/ppermute | solution.py:124
  18.9 10.6 %copy-start.2 = (bf16[256,1536]{1,0:T(8,128)(2,1)S(1)}, bf16[256,1536]{1,0:T(8,128)(2,1)}, u32[]{:S(2)}) copy-start(bf16[256,1536]{1,0:T(8,128)(2,1)} %param.16) | copy-start | bytes 2359300
  19.6 5.2 %collective-permute-start.3 = (bf16[2,1,128,64]{2,3,0,1:T(8,128)(2,1)S(1)}, bf16[2,1,128,64]{2,3,0,1:T(8,128)(2,1)S(1)}, u32[]{:S(2)}, u32[]{:S(2)}) collective-permute-start(bf16[2,1,128,64]{2,3,0,1:T(8,128)(2,1)S(1)} %get-tuple-element.21), channel_id=1, source_target_pairs={{0,12},{4,0},{8,4},{12,8},{1,13},{5,1},{9,5},{13,9},{2,14},{6,2},{... | collective-permute-start | bytes 98312 | tf_op jit(solution)/shard_map/ppermute | solution.py:134
  23.3 5.0 %collective-permute-start.4 = (bf16[2,1,128,64]{2,3,0,1:T(8,128)(2,1)S(1)}, bf16[2,1,128,64]{2,3,0,1:T(8,128)(2,1)S(1)}, u32[]{:S(2)}, u32[]{:S(2)}) collective-permute-start(bf16[2,1,128,64]{2,3,0,1:T(8,128)(2,1)S(1)} %get-tuple-element.20), channel_id=1, source_target_pairs={{0,8},{4,12},{8,0},{12,4},{1,9},{5,13},{9,1},{13,5},{2,10},{6,14},... | collective-permute-start | bytes 98312 | tf_op jit(solution)/shard_map/ppermute | solution.py:134
  23.7 5.7 %collective-permute-start.5 = (bf16[2,1,128,64]{2,3,0,1:T(8,128)(2,1)S(1)}, bf16[2,1,128,64]{2,3,0,1:T(8,128)(2,1)S(1)}, u32[]{:S(2)}, u32[]{:S(2)}) collective-permute-start(bf16[2,1,128,64]{2,3,0,1:T(8,128)(2,1)S(1)} %get-tuple-element.19), channel_id=1, source_target_pairs={{0,4},{4,8},{8,12},{12,0},{1,5},{5,9},{9,13},{13,1},{2,6},{6,10},{... | collective-permute-start | bytes 98312 | tf_op jit(solution)/shard_map/ppermute | solution.py:134
  30.0 12.2 %copy-start.4 = (f32[1536]{0:T(1024)S(1)}, f32[1536]{0:T(1024)}, u32[]{:S(2)}) copy-start(f32[1536]{0:T(1024)} %param.17) | copy-start | bytes 18436
  30.0 1.8 %collective-permute-start.6 = (bf16[2,2,32,1536]{3,2,0,1:T(8,128)(2,1)S(1)}, bf16[2,2,32,1536]{3,2,0,1:T(8,128)(2,1)S(1)}, u32[]{:S(2)}, u32[]{:S(2)}) collective-permute-start(bf16[2,2,32,1536]{3,2,0,1:T(8,128)(2,1)S(1)} %bitcast.142), channel_id=1, source_target_pairs={{0,1},{1,0},{2,3},{3,2},{4,5},{5,4},{6,7},{7,6},{8,9},{9,8},{10,11... | collective-permute-start | bytes 1179656 | tf_op jit(solution)/shard_map/ppermute | solution.py:59
  31.8 0.8 %copy-start.3 = (bf16[2,2,32,1536]{3,2,0,1:T(8,128)(2,1)}, bf16[2,2,32,1536]{3,2,0,1:T(8,128)(2,1)S(1)}, u32[]{:S(2)}) copy-start(bf16[2,2,32,1536]{3,2,0,1:T(8,128)(2,1)S(1)} %collective-permute-done.6) | copy-start | bytes 1179652
  33.7 7.1 %collective-permute-start.7 = (bf16[2,32,1536]{2,1,0:T(8,128)(2,1)S(1)}, bf16[2,32,1536]{2,1,0:T(8,128)(2,1)}, u32[]{:S(2)}, u32[]{:S(2)}) collective-permute-start(bf16[2,32,1536]{2,1,0:T(8,128)(2,1)S(1)} %fusion.52), channel_id=1, source_target_pairs={{0,2},{1,3},{2,0},{3,1},{4,6},{5,7},{6,4},{7,5},{8,10},{9,11},{10,... | collective-permute-start | bytes 589832 | tf_op jit(solution)/shard_map/ppermute | solution.py:59
  35.2 13.9 %collective-permute-start.9 = (bf16[2,1536,384]{2,1,0:T(8,128)(2,1)}, bf16[2,1536,384]{2,1,0:T(8,128)(2,1)}, u32[]{:S(2)}, u32[]{:S(2)}) collective-permute-start(bf16[2,1536,384]{2,1,0:T(8,128)(2,1)} %param.18), channel_id=1, source_target_pairs={{0,1},{1,0},{2,3},{3,2},{4,5},{5,4},{6,7},{7,6},{8,9},{9,8},{10,11... | collective-permute-start | bytes 7077896 | tf_op jit(solution)/shard_map/ppermute | solution.py:159
  35.2 13.3 %copy-start.1 = (bf16[2,1536,384]{2,1,0:T(8,128)(2,1)S(1)}, bf16[2,1536,384]{2,1,0:T(8,128)(2,1)}, u32[]{:S(2)}) copy-start(bf16[2,1536,384]{2,1,0:T(8,128)(2,1)} %param.18) | copy-start | bytes 7077892
  42.4 6.2 %collective-permute-start.8 = (bf16[2,32,1536]{2,1,0:T(8,128)(2,1)S(1)}, bf16[2,32,1536]{2,1,0:T(8,128)(2,1)S(1)}, u32[]{:S(2)}, u32[]{:S(2)}) collective-permute-start(bf16[2,32,1536]{2,1,0:T(8,128)(2,1)S(1)} %get-tuple-element.6), channel_id=1, source_target_pairs={{0,2},{1,3},{2,0},{3,1},{4,6},{5,7},{6,4},{7,5},{8,10},{9,11},{10,... | collective-permute-start | bytes 589832 | tf_op jit(solution)/shard_map/ppermute | solution.py:71
  49.1 11.1 %copy-start.8 = (f32[31,384]{1,0:T(8,128)S(1)}, f32[31,384]{1,0:T(8,128)}, u32[]{:S(2)}) copy-start(f32[31,384]{1,0:T(8,128)} %param.19) | copy-start | bytes 142852
  51.4 1.4 %collective-permute-start.10 = (bf16[2,64,384]{2,1,0:T(8,128)(2,1)S(1)}, bf16[2,64,384]{2,1,0:T(8,128)(2,1)S(1)}, u32[]{:S(2)}, u32[]{:S(2)}) collective-permute-start(bf16[2,64,384]{2,1,0:T(8,128)(2,1)S(1)} %fusion.68), channel_id=1, source_target_pairs={{0,1},{1,0},{2,3},{3,2},{4,5},{5,4},{6,7},{7,6},{8,9},{9,8},{10,11... | collective-permute-start | bytes 294920 | tf_op jit(solution)/shard_map/ppermute | solution.py:189
  53.2 2.8 %collective-permute-start.11 = (bf16[2,15,384]{2,0,1:T(2,128)(2,1)S(1)}, bf16[2,15,384]{2,0,1:T(2,128)(2,1)S(1)}, u32[]{:S(2)}, u32[]{:S(2)}) collective-permute-start(bf16[2,15,384]{2,0,1:T(2,128)(2,1)S(1)} %get-tuple-element.17), channel_id=1, source_target_pairs={{0,4},{4,8},{8,12},{1,5},{5,9},{9,13},{2,6},{6,10},{10,14},{3,7},{... | collective-permute-start | bytes 69128 | tf_op jit(solution)/shard_map/ppermute | solution.py:20
  54.5 5.7 %collective-permute-start.12 = (bf16[2,15,384]{2,0,1:T(2,128)(2,1)S(1)}, bf16[2,15,384]{2,0,1:T(2,128)(2,1)S(1)}, u32[]{:S(2)}, u32[]{:S(2)}) collective-permute-start(bf16[2,15,384]{2,0,1:T(2,128)(2,1)S(1)} %get-tuple-element.18), channel_id=1, source_target_pairs={{4,0},{8,4},{12,8},{5,1},{9,5},{13,9},{6,2},{10,6},{14,10},{7,3},{... | collective-permute-start | bytes 69128 | tf_op jit(solution)/shard_map/ppermute | solution.py:21
  60.2 1.3 %copy-start.7 = (bf16[384,1536]{1,0:T(8,128)(2,1)S(1)}, bf16[384,1536]{1,0:T(8,128)(2,1)}, u32[]{:S(2)}) copy-start(bf16[384,1536]{1,0:T(8,128)(2,1)} %param.22) | copy-start | bytes 3538948
  60.2 1.3 %copy-start.9 = (f32[384]{0:T(512)S(1)}, f32[384]{0:T(512)}, u32[]{:S(2)}) copy-start(f32[384]{0:T(512)} %param.21) | copy-start | bytes 4612
  60.2 1.3 %copy-start.10 = (f32[384]{0:T(512)S(1)}, f32[384]{0:T(512)}, u32[]{:S(2)}) copy-start(f32[384]{0:T(512)} %param.20) | copy-start | bytes 4612
  61.5 0.8 %copy-start.5 = (s32[1536]{0:T(1024)S(1)}, s32[1536]{0:T(1024)}, u32[]{:S(2)}) copy-start(s32[1536]{0:T(1024)} %param.23) | copy-start | bytes 18436
  62.2 1.9 %collective-permute-start.13 = (bf16[2,2,32,1536]{3,2,0,1:T(8,128)(2,1)S(1)}, bf16[2,2,32,1536]{3,2,0,1:T(8,128)(2,1)}, u32[]{:S(2)}, u32[]{:S(2)}) collective-permute-start(bf16[2,2,32,1536]{3,2,0,1:T(8,128)(2,1)S(1)} %bitcast.143), channel_id=1, source_target_pairs={{0,1},{1,0},{2,3},{3,2},{4,5},{5,4},{6,7},{7,6},{8,9},{9,8},{10,11... | collective-permute-start | bytes 1179656 | tf_op jit(solution)/shard_map/ppermute | solution.py:59
  65.3 7.0 %collective-permute-start.14 = (bf16[2,32,1536]{2,1,0:T(8,128)(2,1)S(1)}, bf16[2,32,1536]{2,1,0:T(8,128)(2,1)S(1)}, u32[]{:S(2)}, u32[]{:S(2)}) collective-permute-start(bf16[2,32,1536]{2,1,0:T(8,128)(2,1)S(1)} %fusion.53), channel_id=1, source_target_pairs={{0,2},{1,3},{2,0},{3,1},{4,6},{5,7},{6,4},{7,5},{8,10},{9,11},{10,... | collective-permute-start | bytes 589832 | tf_op jit(solution)/shard_map/ppermute | solution.py:59

commit v19 on v9

--- a/solution.py
+++ b/solution.py
@@ -51,7 +51,27 @@
     shape = x.shape
     block = shape[dim] // count
     acc = x.reshape(shape[:dim] + (2,) * bits + (block,) + shape[dim + 1 :])
-    for b in range(bits):
+    first = 0
+    if bits >= 2:
+        mine, onward = rank & 1, (rank >> 1) & 1
+        keep = lax.dynamic_index_in_dim(acc, mine, dim + bits - 1, keepdims=False)
+        send = lax.dynamic_index_in_dim(acc, 1 - mine, dim + bits - 1, keepdims=False)
+        got_far = lax.ppermute(
+            lax.dynamic_index_in_dim(send, 1 - onward, dim + bits - 2, keepdims=False),
+            axis, xor_pairs(count, 1),
+        )
+        got_near = lax.ppermute(
+            lax.dynamic_index_in_dim(send, onward, dim + bits - 2, keepdims=False),
+            axis, xor_pairs(count, 1),
+        )
+        far = lax.dynamic_index_in_dim(keep, 1 - onward, dim + bits - 2, keepdims=False)
+        far = far.astype(jnp.float32) + got_far.astype(jnp.float32)
+        near = lax.dynamic_index_in_dim(keep, onward, dim + bits - 2, keepdims=False)
+        near = near.astype(jnp.float32) + got_near.astype(jnp.float32)
+        got = lax.ppermute(far.astype(jnp.bfloat16), axis, xor_pairs(count, 2))
+        acc = near + got.astype(jnp.float32)
+        first = 2
+    for b in range(first, bits):
         bit_axis = dim + bits - 1 - b
         mine = (rank >> b) & 1
         keep = lax.dynamic_index_in_dim(acc, mine, bit_axis, keepdims=False)

time: 71.6 us -> 69.1 us (0.965)
  waiting for transfers between devices: 35.6 us -> 34.1 us
  other arithmetic: 8.42 us -> 7.44 us
  local copies, waits for them, and re-layouts: 1.79 us -> 0.86 us
  starting transfers between devices: 18.8 us -> 19.7 us
    add x2 -> x0, other arithmetic: 2.18 us -> none  [reduce_scatter_rows(): acc = keep.astype(jnp.float32) + got.astype(jnp.float32)]
    ppermute x4 -> x6, waiting for transfers between devices: 14.4 us -> 12.9 us  [the longest x2 10.9 us: reduce_scatter_rows(): got = lax.ppermute(far.astype(jnp.bfloat16), axis, xor_pairs(count, 2))]
    convert_element_type x0 -> x2, other arithmetic: none -> 1.03 us  [reduce_scatter_rows(): got = lax.ppermute(far.astype(jnp.bfloat16), axis, xor_pairs(count, 2))]
    ppermute x4 -> x6, starting transfers between devices: 3.25 us -> 4.22 us  [the longest x2 3.11 us: reduce_scatter_rows(): got = lax.ppermute(far.astype(jnp.bfloat16), axis, xor_pairs(count, 2))]
    unnamed x29 -> x27, local copies, waits for them, and re-layouts: 1.04 us -> 0.28 us
  transfers between devices with their start and end apart: 14 -> 16, of which waited for: 13 -> 13; matrix products, arithmetic and copies ran while one was open for 1% -> 2% of each run, Pallas kernels for 0% -> 0%
where the time goes in v19:
time: 69.1 us; the launch traced here: 68.8 us
  waiting for transfers between devices  34.1 us (49%)
  starting transfers between devices  19.7 us (29%)
  other arithmetic  7.44 us (11%)
  matrix products  6.25 us (9%)
  local copies, waits for them, and re-layouts  0.86 us (1%)
    ppermute x2, waiting for transfers between devices, reduce_scatter_rows(): got = lax.ppermute(far.astype(jnp.bfloat16), axis, xor_pairs(count, 2))  10.9 us
    ppermute x3, starting transfers between devices, attend_by_heads(): pieces.append(lax.ppermute(send, axis, pairs))  7.01 us
    ppermute x2, waiting for transfers between devices, all_gather_rows(): got = lax.ppermute(acc, axis, xor_pairs(count, 1 << b))  6.15 us
    ppermute x3, waiting for transfers between devices, attend_by_heads(): back.append(lax.ppermute(rows, axis, pairs))  5.45 us
    ppermute x3, waiting for transfers between devices, attend_by_heads(): pieces.append(lax.ppermute(send, axis, pairs))  5.16 us
    ppermute x3, starting transfers between devices, attend_by_heads(): back.append(lax.ppermute(rows, axis, pairs))  4.3 us
    ppermute x1, waiting for transfers between devices, with_halo(): after = lax.ppermute(initial, axis, down)  4.22 us
    ppermute x2, starting transfers between devices, reduce_scatter_rows(): got = lax.ppermute(far.astype(jnp.bfloat16), axis, xor_pairs(count, 2))  3.11 us
  transfers between devices with their start and end apart: 16, of which 13 were waited for; matrix products, arithmetic and copies ran while one was open for 2% of the time, Pallas kernels for 0%

profile of v19, /device:TPU:0, one launch (start us, length us, event | category | flops | bytes accessed | tf_op | source)
XLA Modules:
  0.0 68.8 jit_solution(14792137635395198132)
XLA Ops:
  0.0 1.5 %convert_reduce_fusion = f32[2,128]{1,0:T(2,128)S(1)} fusion(bf16[2,128,1536]{2,1,0:T(8,128)(2,1)} %param.12), kind=kLoop, calls=%fused_computation.9 | loop fusion | flops 786176 | bytes 787456 | tf_op jit(solution)/shard_map/reduce_sum | solution.py:27
  1.5 1.5 %fusion.9 = f32[2,128]{1,0:T(2,128)S(1)} fusion(bf16[2,128,1536]{2,1,0:T(8,128)(2,1)} %param.12, f32[2,128]{1,0:T(2,128)S(1)} %broadcast_multiply_fusion.1), kind=kLoop, calls=%fused_computation.15 | loop fusion | flops 1572608 | bytes 788480 | tf_op jit(solution)/shard_map/reduce_sum | solution.py:29
  3.0 2.0 %fusion.18 = bf16[3,2,128,256]{3,2,0,1:T(8,128)(2,1)S(1)} fusion(bf16[3,1536,256]{2,1,0:T(8,128)(2,1)S(1)} %copy-done, bf16[2,128,1536]{2,1,0:T(8,128)(2,1)} %param.12, f32[1536]{0:T(1024)} %param.14, f32[2,128]{1,0:T(2,128)S(1)} %add_rsqrt_fusion.1, f32[2,128]{1,0:T(2,128)S(1)} %broadcast_multiply_fusion.1), kind=kOutput, calls=%fused_computation.20 | convolution fusion | flops 606142464 | bytes 3547136 | tf_op jit(solution)/shard_map/std,idc->istc/dot_general | solution.py:180
  5.0 0.2 copy.39
  5.3 3.1 %collective-permute-start = (bf16[3,2,128,1,64]{2,4,1,3,0:T(8,128)(2,1)S(1)}, bf16[3,2,128,1,64]{2,4,1,3,0:T(8,128)(2,1)S(1)}, u32[]{:S(2)}, u32[]{:S(2)}) collective-permute-start(bf16[3,2,128,1,64]{2,4,1,3,0:T(8,128)(2,1)S(1)} %get-tuple-element.16), channel_id=1, source_target_pairs={{0,4},{4,8},{8,12},{12,0},{1,5},{5,9},{9,13},{13,1},{2,6},{6,10},{... | collective-permute-start | bytes 294920 | tf_op jit(solution)/shard_map/ppermute | solution.py:144
  8.4 2.6 %collective-permute-start.1 = (bf16[3,2,128,1,64]{2,4,1,3,0:T(8,128)(2,1)S(1)}, bf16[3,2,128,1,64]{2,4,1,3,0:T(8,128)(2,1)S(1)}, u32[]{:S(2)}, u32[]{:S(2)}) collective-permute-start(bf16[3,2,128,1,64]{2,4,1,3,0:T(8,128)(2,1)S(1)} %get-tuple-element.15), channel_id=1, source_target_pairs={{0,8},{4,12},{8,0},{12,4},{1,9},{5,13},{9,1},{13,5},{2,10},{6,14},... | collective-permute-start | bytes 294920 | tf_op jit(solution)/shard_map/ppermute | solution.py:144
  10.9 1.3 %collective-permute-start.2 = (bf16[3,2,128,1,64]{2,4,1,3,0:T(8,128)(2,1)S(1)}, bf16[3,2,128,1,64]{2,4,1,3,0:T(8,128)(2,1)S(1)}, u32[]{:S(2)}, u32[]{:S(2)}) collective-permute-start(bf16[3,2,128,1,64]{2,4,1,3,0:T(8,128)(2,1)S(1)} %get-tuple-element.14), channel_id=1, source_target_pairs={{0,12},{4,0},{8,4},{12,8},{1,13},{5,1},{9,5},{13,9},{2,14},{6,2},{... | collective-permute-start | bytes 294920 | tf_op jit(solution)/shard_map/ppermute | solution.py:144
  12.3 0.1 broadcast_compare_fusion
  12.4 1.6 %collective-permute-done = bf16[3,2,128,1,64]{2,4,1,3,0:T(8,128)(2,1)S(1)} collective-permute-done((bf16[3,2,128,1,64]{2,4,1,3,0:T(8,128)(2,1)S(1)}, bf16[3,2,128,1,64]{2,4,1,3,0:T(8,128)(2,1)S(1)}, u32[]{:S(2)}, u32[]{:S(2)}) %collective-permute-start) | collective-permute-done | bytes 98336 | tf_op jit(solution)/shard_map/ppermute | solution.py:144
  14.0 3.5 %collective-permute-done.1 = bf16[3,2,128,1,64]{2,4,1,3,0:T(8,128)(2,1)S(1)} collective-permute-done((bf16[3,2,128,1,64]{2,4,1,3,0:T(8,128)(2,1)S(1)}, bf16[3,2,128,1,64]{2,4,1,3,0:T(8,128)(2,1)S(1)}, u32[]{:S(2)}, u32[]{:S(2)}) %collective-permute-start.1) | collective-permute-done | bytes 98336 | tf_op jit(solution)/shard_map/ppermute | solution.py:144
  17.6 0.8 %fusion.6 = (f32[2,512]{1,0:T(2,128)S(1)}, f32[2,512,512]{1,2,0:T(8,128)S(1)}) fusion(pred[2,512]{1,0:T(4,128)(4,1)S(1)} %broadcast_compare_fusion, bf16[3,2,512,1,64]{2,4,1,3,0:T(8,128)(2,1)S(1)} %pad_maximum_fusion), kind=kOutput, calls=%fused_computation.12 | convolution fusion | flops 68680704 | bytes 2365440 | tf_op jit(solution)/shard_map/sqhe,skhe->shqk/dot_general | solution.py:116
  18.4 0.5 fusion.7
  18.9 0.6 fusion.23
  19.6 3.6 %collective-permute-start.3 = (bf16[2,1,128,64]{2,3,0,1:T(8,128)(2,1)S(1)}, bf16[2,1,128,64]{2,3,0,1:T(8,128)(2,1)S(1)}, u32[]{:S(2)}, u32[]{:S(2)}) collective-permute-start(bf16[2,1,128,64]{2,3,0,1:T(8,128)(2,1)S(1)} %get-tuple-element.21), channel_id=1, source_target_pairs={{0,12},{4,0},{8,4},{12,8},{1,13},{5,1},{9,5},{13,9},{2,14},{6,2},{... | collective-permute-start | bytes 98312 | tf_op jit(solution)/shard_map/ppermute | solution.py:154
  23.3 0.4 collective-permute-start.4
  23.7 0.2 collective-permute-start.5
  23.9 0.9 %collective-permute-done.3 = bf16[2,1,128,64]{2,3,0,1:T(8,128)(2,1)S(1)} collective-permute-done((bf16[2,1,128,64]{2,3,0,1:T(8,128)(2,1)S(1)}, bf16[2,1,128,64]{2,3,0,1:T(8,128)(2,1)S(1)}, u32[]{:S(2)}, u32[]{:S(2)}) %collective-permute-start.3) | collective-permute-done | bytes 32800 | tf_op jit(solution)/shard_map/ppermute | solution.py:154
  24.9 3.4 %collective-permute-done.4 = bf16[2,1,128,64]{2,3,0,1:T(8,128)(2,1)S(1)} collective-permute-done((bf16[2,1,128,64]{2,3,0,1:T(8,128)(2,1)S(1)}, bf16[2,1,128,64]{2,3,0,1:T(8,128)(2,1)S(1)}, u32[]{:S(2)}, u32[]{:S(2)}) %collective-permute-start.4) | collective-permute-done | bytes 32800 | tf_op jit(solution)/shard_map/ppermute | solution.py:154
  28.2 1.2 %collective-permute-done.5 = bf16[2,1,128,64]{2,3,0,1:T(8,128)(2,1)S(1)} collective-permute-done((bf16[2,1,128,64]{2,3,0,1:T(8,128)(2,1)S(1)}, bf16[2,1,128,64]{2,3,0,1:T(8,128)(2,1)S(1)}, u32[]{:S(2)}, u32[]{:S(2)}) %collective-permute-start.5) | collective-permute-done | bytes 32800 | tf_op jit(solution)/shard_map/ppermute | solution.py:154
  29.5 0.4 convolution_convert_fusion
  30.0 0.1 collective-permute-start.7
  30.0 0.5 collective-permute-start.6
  30.5 1.1 %collective-permute-done.7 = bf16[2,32,1536]{2,1,0:T(8,128)(2,1)} collective-permute-done((bf16[2,32,1536]{2,1,0:T(8,128)(2,1)S(1)}, bf16[2,32,1536]{2,1,0:T(8,128)(2,1)}, u32[]{:S(2)}, u32[]{:S(2)}) %collective-permute-start.7) | collective-permute-done | bytes 196640 | tf_op jit(solution)/shard_map/ppermute | solution.py:59
  31.6 1.0 %fusion.45 = bf16[2,32,1536]{2,1,0:T(8,128)(2,1)S(1)} fusion(bf16[2,32,1536]{2,1,0:T(8,128)(2,1)} %collective-permute-done.7, bf16[2,2,2,32,1536]{4,3,2,1,0:T(8,128)(2,1)S(1)} %bitcast.125, s32[]{:T(128)S(6)} %select_n.129, s32[]{:T(128)S(6)} %select_n.125), kind=kLoop, calls=%fused_computation.51 | loop fusion | flops 393216 | bytes 589832 | tf_op jit(solution)/shard_map/convert_element_type | solution.py:71
  32.6 1.6 %collective-permute-start.8 = (bf16[2,32,1536]{2,1,0:T(8,128)(2,1)S(1)}, bf16[2,32,1536]{2,1,0:T(8,128)(2,1)}, u32[]{:S(2)}, u32[]{:S(2)}) collective-permute-start(bf16[2,32,1536]{2,1,0:T(8,128)(2,1)S(1)} %fusion.45), channel_id=1, source_target_pairs={{0,2},{1,3},{2,0},{3,1},{4,6},{5,7},{6,4},{7,5},{8,10},{9,11},{10,... | collective-permute-start | bytes 589832 | tf_op jit(solution)/shard_map/ppermute | solution.py:71
  34.1 5.6 %collective-permute-done.8 = bf16[2,32,1536]{2,1,0:T(8,128)(2,1)} collective-permute-done((bf16[2,32,1536]{2,1,0:T(8,128)(2,1)S(1)}, bf16[2,32,1536]{2,1,0:T(8,128)(2,1)}, u32[]{:S(2)}, u32[]{:S(2)}) %collective-permute-start.8) | collective-permute-done | bytes 196640 | tf_op jit(solution)/shard_map/ppermute | solution.py:71
  39.7 1.3 %fusion.63 = (f32[2,32]{1,0:T(2,128)S(1)}, f32[2,32,1536]{2,1,0:T(8,128)S(1)}) fusion(bf16[2,32,1536]{2,1,0:T(8,128)(2,1)} %collective-permute-done.8, bf16[2,32,1536]{2,1,0:T(8,128)(2,1)} %collective-permute-done.6, bf16[2,2,2,32,1536]{4,3,2,1,0:T(8,128)(2,1)S(1)} %bitcast.126, s32[]{:T(128)S(6)} %select_n.123, s32[]{:T(128)S(6)} %select_n.125, ...), kind=kLoop, calls=%fused_computation.111 | loop fusion | flops 786368 | bytes 1179916 | tf_op jit(solution)/shard_map/reduce_sum | solution.py:27
  41.0 0.2 multiply_reduce_fusion
  41.3 0.1 bitcast_dynamic-update-slice_fusion.2
  41.4 1.6 %collective-permute-start.9 = (bf16[2,32,1536]{2,1,0:T(8,128)(2,1)S(1)}, bf16[2,32,1536]{2,1,0:T(8,128)(2,1)S(1)}, u32[]{:S(2)}, u32[]{:S(2)}) collective-permute-start(bf16[2,32,1536]{2,1,0:T(8,128)(2,1)S(1)} %get-tuple-element.6), channel_id=1, source_target_pairs={{0,2},{1,3},{2,0},{3,1},{4,6},{5,7},{6,4},{7,5},{8,10},{9,11},{10,... | collective-permute-start | bytes 589832 | tf_op jit(solution)/shard_map/ppermute | solution.py:91
  42.9 0.1 broadcast_compare_fusion.1
  43.0 4.6 %collective-permute-done.9 = bf16[2,32,1536]{2,1,0:T(8,128)(2,1)S(1)} collective-permute-done((bf16[2,32,1536]{2,1,0:T(8,128)(2,1)S(1)}, bf16[2,32,1536]{2,1,0:T(8,128)(2,1)S(1)}, u32[]{:S(2)}, u32[]{:S(2)}) %collective-permute-start.9) | collective-permute-done | bytes 196640 | tf_op jit(solution)/shard_map/ppermute | solution.py:91
  47.8 1.6 %collective-permute-done.10 = bf16[2,2,32,1536]{3,2,1,0:T(8,128)(2,1)S(1)} collective-permute-done((bf16[2,2,32,1536]{3,2,1,0:T(8,128)(2,1)S(1)}, bf16[2,2,32,1536]{3,2,1,0:T(8,128)(2,1)S(1)}, u32[]{:S(2)}, u32[]{:S(2)}) %collective-permute-start.10) | collective-permute-done | bytes 393248 | tf_op jit(solution)/shard_map/ppermute | solution.py:91
  49.4 0.8 %fusion.12 = f32[2,2,128,384]{3,2,0,1:T(8,128)S(1)} fusion(bf16[2,128,1536,1]{2,1,3,0:T(8,128)(2,1)S(1)} %bitcast.131, bf16[2,1536,384]{2,1,0:T(8,128)(2,1)S(1)} %copy-done.5), kind=kOutput, calls=%fused_computation.18 | convolution fusion | flops 603979776 | bytes 3932160 | tf_op jit(solution)/shard_map/std,gdc->gstc/dot_general | solution.py:34
  50.2 0.1 bitcast_select_fusion
  50.4 1.3 %collective-permute-start.11 = (bf16[2,15,384]{2,1,0:T(8,128)(2,1)S(1)}, bf16[2,15,384]{2,1,0:T(8,128)(2,1)S(1)}, u32[]{:S(2)}, u32[]{:S(2)}) collective-permute-start(bf16[2,15,384]{2,1,0:T(8,128)(2,1)S(1)} %get-tuple-element.17), channel_id=1, source_target_pairs={{0,4},{4,8},{8,12},{1,5},{5,9},{9,13},{2,6},{6,10},{10,14},{3,7},{... | collective-permute-start | bytes 69128 | tf_op jit(solution)/shard_map/ppermute | solution.py:20
  51.7 1.3 %collective-permute-start.12 = (bf16[2,15,384]{2,1,0:T(8,128)(2,1)S(1)}, bf16[2,15,384]{2,1,0:T(8,128)(2,1)S(1)}, u32[]{:S(2)}, u32[]{:S(2)}) collective-permute-start(bf16[2,15,384]{2,1,0:T(8,128)(2,1)S(1)} %get-tuple-element.18), channel_id=1, source_target_pairs={{4,0},{8,4},{12,8},{5,1},{9,5},{13,9},{6,2},{10,6},{14,10},{7,3},{... | collective-permute-start | bytes 69128 | tf_op jit(solution)/shard_map/ppermute | solution.py:21
  53.0 0.2 collective-permute-done.11
  53.2 4.2 %collective-permute-done.12 = bf16[2,15,384]{2,1,0:T(8,128)(2,1)S(1)} collective-permute-done((bf16[2,15,384]{2,1,0:T(8,128)(2,1)S(1)}, bf16[2,15,384]{2,1,0:T(8,128)(2,1)S(1)}, u32[]{:S(2)}, u32[]{:S(2)}) %collective-permute-start.12) | collective-permute-done | bytes 23072 | tf_op jit(solution)/shard_map/ppermute | solution.py:21
  57.5 1.1 %fusion.50 = f32[2,128,384]{2,0,1:T(2,128)S(1)} fusion(bf16[2,158,384]{2,1,0:T(8,128)(2,1)S(1)} %pad_maximum_fusion.1, f32[31,1,384]{2,0,1:T(8,128)S(1)} %bitcast.133), kind=kOutput, calls=%fused_computation.62 | convolution fusion | flops 36569088 | bytes 683520 | tf_op jit(solution)/shard_map/conv_general_dilated | solution.py:212
  58.6 0.2 copy-done.6
  58.8 0.6 convolution_convert_fusion.1
  59.5 0.5 collective-permute-start.13
  60.0 0.9 %collective-permute-done.14 = bf16[2,32,1536]{2,1,0:T(8,128)(2,1)S(1)} collective-permute-done((bf16[2,32,1536]{2,1,0:T(8,128)(2,1)S(1)}, bf16[2,32,1536]{2,1,0:T(8,128)(2,1)S(1)}, u32[]{:S(2)}, u32[]{:S(2)}) %collective-permute-start.14) | collective-permute-done | bytes 196640 | tf_op jit(solution)/shard_map/ppermute | solution.py:59
  61.0 1.6 %collective-permute-start.15 = (bf16[2,32,1536]{2,1,0:T(8,128)(2,1)S(1)}, bf16[2,32,1536]{2,1,0:T(8,128)(2,1)S(1)}, u32[]{:S(2)}, u32[]{:S(2)}) collective-permute-start(bf16[2,32,1536]{2,1,0:T(8,128)(2,1)S(1)} %fusion.38), channel_id=1, source_target_pairs={{0,2},{1,3},{2,0},{3,1},{4,6},{5,7},{6,4},{7,5},{8,10},{9,11},{10,... | collective-permute-start | bytes 589832 | tf_op jit(solution)/shard_map/ppermute | solution.py:71
  62.5 0.1 broadcast_compare_fusion.2
  62.6 5.4 %collective-permute-done.15 = bf16[2,32,1536]{2,1,0:T(8,128)(2,1)S(1)} collective-permute-done((bf16[2,32,1536]{2,1,0:T(8,128)(2,1)S(1)}, bf16[2,32,1536]{2,1,0:T(8,128)(2,1)S(1)}, u32[]{:S(2)}, u32[]{:S(2)}) %collective-permute-start.15) | collective-permute-done | bytes 196640 | tf_op jit(solution)/shard_map/ppermute | solution.py:71
  68.0 0.8 %fusion.44 = bf16[2,32,1536]{2,1,0:T(8,128)(2,1)} fusion(f32[2,32,1536]{2,1,0:T(8,128)S(1)} %get-tuple-element.8, bf16[2,32,1536]{2,1,0:T(8,128)(2,1)S(1)} %collective-permute-done.15, bf16[2,32,1536]{2,1,0:T(8,128)(2,1)S(1)} %collective-permute-done.13, bf16[2,2,2,32,1536]{4,3,2,1,0:T(8,128)(2,1)S(1)} %bitcast.130, s32[]{:T(128)S(6)} %select_n.123, ...), kind=kLoop, calls=%fused_computation.47 | loop fusion | flops 1179648 | bytes 1185864 | tf_op jit(solution)/shard_map/convert_element_type | solution.py:229
  (57 shorter events, 0.9 us)
Async XLA Ops:
  0.0 3.0 %copy-start = (bf16[3,1536,256]{2,1,0:T(8,128)(2,1)S(1)}, bf16[3,1536,256]{2,1,0:T(8,128)(2,1)}, u32[]{:S(2)}) copy-start(bf16[3,1536,256]{2,1,0:T(8,128)(2,1)} %param.15) | copy-start | bytes 7077892
  3.0 9.3 %copy-start.4 = (s32[2]{0:T(128)S(1)}, s32[2]{0:T(128)}, u32[]{:S(2)}) copy-start(s32[2]{0:T(128)} %param.13) | copy-start | bytes 28
  5.3 8.8 %collective-permute-start = (bf16[3,2,128,1,64]{2,4,1,3,0:T(8,128)(2,1)S(1)}, bf16[3,2,128,1,64]{2,4,1,3,0:T(8,128)(2,1)S(1)}, u32[]{:S(2)}, u32[]{:S(2)}) collective-permute-start(bf16[3,2,128,1,64]{2,4,1,3,0:T(8,128)(2,1)S(1)} %get-tuple-element.16), channel_id=1, source_target_pairs={{0,4},{4,8},{8,12},{12,0},{1,5},{5,9},{9,13},{13,1},{2,6},{6,10},{... | collective-permute-start | bytes 294920 | tf_op jit(solution)/shard_map/ppermute | solution.py:144
  8.4 9.2 %collective-permute-start.1 = (bf16[3,2,128,1,64]{2,4,1,3,0:T(8,128)(2,1)S(1)}, bf16[3,2,128,1,64]{2,4,1,3,0:T(8,128)(2,1)S(1)}, u32[]{:S(2)}, u32[]{:S(2)}) collective-permute-start(bf16[3,2,128,1,64]{2,4,1,3,0:T(8,128)(2,1)S(1)} %get-tuple-element.15), channel_id=1, source_target_pairs={{0,8},{4,12},{8,0},{12,4},{1,9},{5,13},{9,1},{13,5},{2,10},{6,14},... | collective-permute-start | bytes 294920 | tf_op jit(solution)/shard_map/ppermute | solution.py:144
  10.9 6.6 %collective-permute-start.2 = (bf16[3,2,128,1,64]{2,4,1,3,0:T(8,128)(2,1)S(1)}, bf16[3,2,128,1,64]{2,4,1,3,0:T(8,128)(2,1)S(1)}, u32[]{:S(2)}, u32[]{:S(2)}) collective-permute-start(bf16[3,2,128,1,64]{2,4,1,3,0:T(8,128)(2,1)S(1)} %get-tuple-element.14), channel_id=1, source_target_pairs={{0,12},{4,0},{8,4},{12,8},{1,13},{5,1},{9,5},{13,9},{2,14},{6,2},{... | collective-permute-start | bytes 294920 | tf_op jit(solution)/shard_map/ppermute | solution.py:144
  18.9 10.6 %copy-start.1 = (bf16[256,1536]{1,0:T(8,128)(2,1)S(1)}, bf16[256,1536]{1,0:T(8,128)(2,1)}, u32[]{:S(2)}) copy-start(bf16[256,1536]{1,0:T(8,128)(2,1)} %param.16) | copy-start | bytes 2359300
  19.6 5.2 %collective-permute-start.3 = (bf16[2,1,128,64]{2,3,0,1:T(8,128)(2,1)S(1)}, bf16[2,1,128,64]{2,3,0,1:T(8,128)(2,1)S(1)}, u32[]{:S(2)}, u32[]{:S(2)}) collective-permute-start(bf16[2,1,128,64]{2,3,0,1:T(8,128)(2,1)S(1)} %get-tuple-element.21), channel_id=1, source_target_pairs={{0,12},{4,0},{8,4},{12,8},{1,13},{5,1},{9,5},{13,9},{2,14},{6,2},{... | collective-permute-start | bytes 98312 | tf_op jit(solution)/shard_map/ppermute | solution.py:154
  23.3 5.0 %collective-permute-start.4 = (bf16[2,1,128,64]{2,3,0,1:T(8,128)(2,1)S(1)}, bf16[2,1,128,64]{2,3,0,1:T(8,128)(2,1)S(1)}, u32[]{:S(2)}, u32[]{:S(2)}) collective-permute-start(bf16[2,1,128,64]{2,3,0,1:T(8,128)(2,1)S(1)} %get-tuple-element.20), channel_id=1, source_target_pairs={{0,8},{4,12},{8,0},{12,4},{1,9},{5,13},{9,1},{13,5},{2,10},{6,14},... | collective-permute-start | bytes 98312 | tf_op jit(solution)/shard_map/ppermute | solution.py:154
  23.7 5.7 %collective-permute-start.5 = (bf16[2,1,128,64]{2,3,0,1:T(8,128)(2,1)S(1)}, bf16[2,1,128,64]{2,3,0,1:T(8,128)(2,1)S(1)}, u32[]{:S(2)}, u32[]{:S(2)}) collective-permute-start(bf16[2,1,128,64]{2,3,0,1:T(8,128)(2,1)S(1)} %get-tuple-element.19), channel_id=1, source_target_pairs={{0,4},{4,8},{8,12},{12,0},{1,5},{5,9},{9,13},{13,1},{2,6},{6,10},{... | collective-permute-start | bytes 98312 | tf_op jit(solution)/shard_map/ppermute | solution.py:154
  29.9 11.3 %copy-start.2 = (f32[1536]{0:T(1024)S(1)}, f32[1536]{0:T(1024)}, u32[]{:S(2)}) copy-start(f32[1536]{0:T(1024)} %param.17) | copy-start | bytes 18436
  30.0 1.6 %collective-permute-start.7 = (bf16[2,32,1536]{2,1,0:T(8,128)(2,1)S(1)}, bf16[2,32,1536]{2,1,0:T(8,128)(2,1)}, u32[]{:S(2)}, u32[]{:S(2)}) collective-permute-start(bf16[2,32,1536]{2,1,0:T(8,128)(2,1)S(1)} %get-tuple-element.12), channel_id=1, source_target_pairs={{0,1},{1,0},{2,3},{3,2},{4,5},{5,4},{6,7},{7,6},{8,9},{9,8},{10,11... | collective-permute-start | bytes 589832 | tf_op jit(solution)/shard_map/ppermute | solution.py:59
  30.0 4.1 %collective-permute-start.6 = (bf16[2,32,1536]{2,1,0:T(8,128)(2,1)S(1)}, bf16[2,32,1536]{2,1,0:T(8,128)(2,1)}, u32[]{:S(2)}, u32[]{:S(2)}) collective-permute-start(bf16[2,32,1536]{2,1,0:T(8,128)(2,1)S(1)} %get-tuple-element.11), channel_id=1, source_target_pairs={{0,1},{1,0},{2,3},{3,2},{4,5},{5,4},{6,7},{7,6},{8,9},{9,8},{10,11... | collective-permute-start | bytes 589832 | tf_op jit(solution)/shard_map/ppermute | solution.py:63
  32.6 7.1 %collective-permute-start.8 = (bf16[2,32,1536]{2,1,0:T(8,128)(2,1)S(1)}, bf16[2,32,1536]{2,1,0:T(8,128)(2,1)}, u32[]{:S(2)}, u32[]{:S(2)}) collective-permute-start(bf16[2,32,1536]{2,1,0:T(8,128)(2,1)S(1)} %fusion.45), channel_id=1, source_target_pairs={{0,2},{1,3},{2,0},{3,1},{4,6},{5,7},{6,4},{7,5},{8,10},{9,11},{10,... | collective-permute-start | bytes 589832 | tf_op jit(solution)/shard_map/ppermute | solution.py:71
  41.0 8.4 %copy-start.5 = (bf16[2,1536,384]{2,1,0:T(8,128)(2,1)S(1)}, bf16[2,1536,384]{2,1,0:T(8,128)(2,1)}, u32[]{:S(2)}) copy-start(bf16[2,1536,384]{2,1,0:T(8,128)(2,1)} %param.18) | copy-start | bytes 7077892
  41.4 6.2 %collective-permute-start.9 = (bf16[2,32,1536]{2,1,0:T(8,128)(2,1)S(1)}, bf16[2,32,1536]{2,1,0:T(8,128)(2,1)S(1)}, u32[]{:S(2)}, u32[]{:S(2)}) collective-permute-start(bf16[2,32,1536]{2,1,0:T(8,128)(2,1)S(1)} %get-tuple-element.6), channel_id=1, source_target_pairs={{0,2},{1,3},{2,0},{3,1},{4,6},{5,7},{6,4},{7,5},{8,10},{9,11},{10,... | collective-permute-start | bytes 589832 | tf_op jit(solution)/shard_map/ppermute | solution.py:91
  47.6 1.8 %collective-permute-start.10 = (bf16[2,2,32,1536]{3,2,1,0:T(8,128)(2,1)S(1)}, bf16[2,2,32,1536]{3,2,1,0:T(8,128)(2,1)S(1)}, u32[]{:S(2)}, u32[]{:S(2)}) collective-permute-start(bf16[2,2,32,1536]{3,2,1,0:T(8,128)(2,1)S(1)} %bitcast_dynamic-update-slice_fusion.3), channel_id=1, source_target_pairs={{0,1},{1,0},{2,3},{3,2},{4,5},{5,4},{6,7},{7,6},{8,9},{9,8},{10,11... | collective-permute-start | bytes 1179656 | tf_op jit(solution)/shard_map/ppermute | solution.py:91
  49.4 8.1 %copy-start.7 = (f32[31,384]{1,0:T(8,128)S(1)}, f32[31,384]{1,0:T(8,128)}, u32[]{:S(2)}) copy-start(f32[31,384]{1,0:T(8,128)} %param.19) | copy-start | bytes 142852
  50.4 2.8 %collective-permute-start.11 = (bf16[2,15,384]{2,1,0:T(8,128)(2,1)S(1)}, bf16[2,15,384]{2,1,0:T(8,128)(2,1)S(1)}, u32[]{:S(2)}, u32[]{:S(2)}) collective-permute-start(bf16[2,15,384]{2,1,0:T(8,128)(2,1)S(1)} %get-tuple-element.17), channel_id=1, source_target_pairs={{0,4},{4,8},{8,12},{1,5},{5,9},{9,13},{2,6},{6,10},{10,14},{3,7},{... | collective-permute-start | bytes 69128 | tf_op jit(solution)/shard_map/ppermute | solution.py:20
  51.7 5.7 %collective-permute-start.12 = (bf16[2,15,384]{2,1,0:T(8,128)(2,1)S(1)}, bf16[2,15,384]{2,1,0:T(8,128)(2,1)S(1)}, u32[]{:S(2)}, u32[]{:S(2)}) collective-permute-start(bf16[2,15,384]{2,1,0:T(8,128)(2,1)S(1)} %get-tuple-element.18), channel_id=1, source_target_pairs={{4,0},{8,4},{12,8},{5,1},{9,5},{13,9},{6,2},{10,6},{14,10},{7,3},{... | collective-permute-start | bytes 69128 | tf_op jit(solution)/shard_map/ppermute | solution.py:21
  57.5 1.3 %copy-start.6 = (bf16[384,1536]{1,0:T(8,128)(2,1)S(1)}, bf16[384,1536]{1,0:T(8,128)(2,1)}, u32[]{:S(2)}) copy-start(bf16[384,1536]{1,0:T(8,128)(2,1)} %param.22) | copy-start | bytes 3538948
  57.5 1.3 %copy-start.8 = (f32[384]{0:T(512)S(1)}, f32[384]{0:T(512)}, u32[]{:S(2)}) copy-start(f32[384]{0:T(512)} %param.21) | copy-start | bytes 4612
  57.5 1.3 %copy-start.9 = (f32[384]{0:T(512)S(1)}, f32[384]{0:T(512)}, u32[]{:S(2)}) copy-start(f32[384]{0:T(512)} %param.20) | copy-start | bytes 4612
  58.8 0.7 %copy-start.3 = (s32[1536]{0:T(1024)S(1)}, s32[1536]{0:T(1024)}, u32[]{:S(2)}) copy-start(s32[1536]{0:T(1024)} %param.23) | copy-start | bytes 18436
  59.4 1.5 %collective-permute-start.14 = (bf16[2,32,1536]{2,1,0:T(8,128)(2,1)S(1)}, bf16[2,32,1536]{2,1,0:T(8,128)(2,1)S(1)}, u32[]{:S(2)}, u32[]{:S(2)}) collective-permute-start(bf16[2,32,1536]{2,1,0:T(8,128)(2,1)S(1)} %get-tuple-element.10), channel_id=1, source_target_pairs={{0,1},{1,0},{2,3},{3,2},{4,5},{5,4},{6,7},{7,6},{8,9},{9,8},{10,11... | collective-permute-start | bytes 589832 | tf_op jit(solution)/shard_map/ppermute | solution.py:59
  59.5 3.1 %collective-permute-start.13 = (bf16[2,32,1536]{2,1,0:T(8,128)(2,1)S(1)}, bf16[2,32,1536]{2,1,0:T(8,128)(2,1)S(1)}, u32[]{:S(2)}, u32[]{:S(2)}) collective-permute-start(bf16[2,32,1536]{2,1,0:T(8,128)(2,1)S(1)} %get-tuple-element.9), channel_id=1, source_target_pairs={{0,1},{1,0},{2,3},{3,2},{4,5},{5,4},{6,7},{7,6},{8,9},{9,8},{10,11... | collective-permute-start | bytes 589832 | tf_op jit(solution)/shard_map/ppermute | solution.py:63
  61.0 7.0 %collective-permute-start.15 = (bf16[2,32,1536]{2,1,0:T(8,128)(2,1)S(1)}, bf16[2,32,1536]{2,1,0:T(8,128)(2,1)S(1)}, u32[]{:S(2)}, u32[]{:S(2)}) collective-permute-start(bf16[2,32,1536]{2,1,0:T(8,128)(2,1)S(1)} %fusion.38), channel_id=1, source_target_pairs={{0,2},{1,3},{2,0},{3,1},{4,6},{5,7},{6,4},{7,5},{8,10},{9,11},{10,... | collective-permute-start | bytes 589832 | tf_op jit(solution)/shard_map/ppermute | solution.py:71

commit v20 on v19

--- a/solution.py
+++ b/solution.py
@@ -81,17 +81,25 @@
     return acc
 
 
+def place_pair(mine, other, bit, axis):
+    both = jnp.zeros(mine.shape[:axis] + (2,) + mine.shape[axis:], mine.dtype)
+    both = lax.dynamic_update_index_in_dim(both, mine, bit, axis)
+    return lax.dynamic_update_index_in_dim(both, other, 1 - bit, axis)
+
+
 def all_gather_rows(x, axis, dim):
     count, rank = lax.axis_size(axis), lax.axis_index(axis)
     bits = bit_count(count)
     shape = x.shape
-    acc = x
-    for k, b in enumerate(reversed(range(bits))):
-        mine = (rank >> b) & 1
-        got = lax.ppermute(acc, axis, xor_pairs(count, 1 << b))
-        both = jnp.zeros(acc.shape[: dim + k] + (2,) + acc.shape[dim + k :], acc.dtype)
-        both = lax.dynamic_update_index_in_dim(both, acc, mine, dim + k)
-        acc = lax.dynamic_update_index_in_dim(both, got, 1 - mine, dim + k)
+    mine_acc = x
+    their_acc = lax.ppermute(x, axis, xor_pairs(count, 1))
+    for k, b in enumerate(reversed(range(1, bits))):
+        bit = (rank >> b) & 1
+        got = lax.ppermute(mine_acc, axis, xor_pairs(count, 1 << b))
+        forwarded = lax.ppermute(got, axis, xor_pairs(count, 1))
+        mine_acc = place_pair(mine_acc, got, bit, dim + k)
+        their_acc = place_pair(their_acc, forwarded, bit, dim + k)
+    acc = place_pair(mine_acc, their_acc, rank & 1, dim + bits - 1)
     return acc.reshape(shape[:dim] + (shape[dim] * count,) + shape[dim + 1 :])
 
 

time: 69.1 us -> 68.8 us (level)
    ppermute x2 -> x3, waiting for transfers between devices: 6.15 us -> 5.78 us  [the longest x1 4.55 us: all_gather_rows(): got = lax.ppermute(mine_acc, axis, xor_pairs(count, 1 << b))]
    ppermute x2 -> x3, starting transfers between devices: 1.63 us -> 1.56 us  [the longest x1 1.56 us: all_gather_rows(): got = lax.ppermute(mine_acc, axis, xor_pairs(count, 1 << b))]
  transfers between devices with their start and end apart: 16 -> 17, of which waited for: 13 -> 13; matrix products, arithmetic and copies ran while one was open for 2% -> 2% of each run, Pallas kernels for 0% -> 0%
where the time goes in v20:
time: 68.8 us; the launch traced here: 68.5 us
  waiting for transfers between devices  33.7 us (49%)
  starting transfers between devices  19.7 us (29%)
  other arithmetic  7.44 us (11%)
  matrix products  6.24 us (9%)
  local copies, waits for them, and re-layouts  0.94 us (1%)
    ppermute x2, waiting for transfers between devices, reduce_scatter_rows(): got = lax.ppermute(far.astype(jnp.bfloat16), axis, xor_pairs(count, 2))  10.9 us
    ppermute x3, starting transfers between devices, attend_by_heads(): pieces.append(lax.ppermute(send, axis, pairs))  7.01 us
    ppermute x3, waiting for transfers between devices, attend_by_heads(): back.append(lax.ppermute(rows, axis, pairs))  5.45 us
    ppermute x3, waiting for transfers between devices, attend_by_heads(): pieces.append(lax.ppermute(send, axis, pairs))  5.16 us
    ppermute x1, waiting for transfers between devices, all_gather_rows(): got = lax.ppermute(mine_acc, axis, xor_pairs(count, 1 << b))  4.55 us
    ppermute x3, starting transfers between devices, attend_by_heads(): back.append(lax.ppermute(rows, axis, pairs))  4.3 us
    ppermute x1, waiting for transfers between devices, with_halo(): after = lax.ppermute(initial, axis, down)  4.22 us
    ppermute x2, starting transfers between devices, reduce_scatter_rows(): got = lax.ppermute(far.astype(jnp.bfloat16), axis, xor_pairs(count, 2))  3.12 us
  transfers between devices with their start and end apart: 17, of which 13 were waited for; matrix products, arithmetic and copies ran while one was open for 2% of the time, Pallas kernels for 0%

profile of v20, /device:TPU:0, one launch (start us, length us, event | category | flops | bytes accessed | tf_op | source)
XLA Modules:
  0.0 68.5 jit_solution(15681626876675080301)
XLA Ops:
  0.0 1.5 %convert_reduce_fusion = f32[2,128]{1,0:T(2,128)S(1)} fusion(bf16[2,128,1536]{2,1,0:T(8,128)(2,1)} %param.12), kind=kLoop, calls=%fused_computation.9 | loop fusion | flops 786176 | bytes 787456 | tf_op jit(solution)/shard_map/reduce_sum | solution.py:27
  1.5 1.5 %fusion.9 = f32[2,128]{1,0:T(2,128)S(1)} fusion(bf16[2,128,1536]{2,1,0:T(8,128)(2,1)} %param.12, f32[2,128]{1,0:T(2,128)S(1)} %broadcast_multiply_fusion.1), kind=kLoop, calls=%fused_computation.15 | loop fusion | flops 1572608 | bytes 788480 | tf_op jit(solution)/shard_map/reduce_sum | solution.py:29
  3.0 2.0 %fusion.18 = bf16[3,2,128,256]{3,2,0,1:T(8,128)(2,1)S(1)} fusion(bf16[3,1536,256]{2,1,0:T(8,128)(2,1)S(1)} %copy-done, bf16[2,128,1536]{2,1,0:T(8,128)(2,1)} %param.12, f32[1536]{0:T(1024)} %param.14, f32[2,128]{1,0:T(2,128)S(1)} %add_rsqrt_fusion.1, f32[2,128]{1,0:T(2,128)S(1)} %broadcast_multiply_fusion.1), kind=kOutput, calls=%fused_computation.20 | convolution fusion | flops 606142464 | bytes 3547136 | tf_op jit(solution)/shard_map/std,idc->istc/dot_general | solution.py:188
  5.0 0.2 copy.44
  5.3 3.1 %collective-permute-start = (bf16[3,2,128,1,64]{2,4,1,3,0:T(8,128)(2,1)S(1)}, bf16[3,2,128,1,64]{2,4,1,3,0:T(8,128)(2,1)S(1)}, u32[]{:S(2)}, u32[]{:S(2)}) collective-permute-start(bf16[3,2,128,1,64]{2,4,1,3,0:T(8,128)(2,1)S(1)} %get-tuple-element.16), channel_id=1, source_target_pairs={{0,4},{4,8},{8,12},{12,0},{1,5},{5,9},{9,13},{13,1},{2,6},{6,10},{... | collective-permute-start | bytes 294920 | tf_op jit(solution)/shard_map/ppermute | solution.py:152
  8.4 2.6 %collective-permute-start.1 = (bf16[3,2,128,1,64]{2,4,1,3,0:T(8,128)(2,1)S(1)}, bf16[3,2,128,1,64]{2,4,1,3,0:T(8,128)(2,1)S(1)}, u32[]{:S(2)}, u32[]{:S(2)}) collective-permute-start(bf16[3,2,128,1,64]{2,4,1,3,0:T(8,128)(2,1)S(1)} %get-tuple-element.15), channel_id=1, source_target_pairs={{0,8},{4,12},{8,0},{12,4},{1,9},{5,13},{9,1},{13,5},{2,10},{6,14},... | collective-permute-start | bytes 294920 | tf_op jit(solution)/shard_map/ppermute | solution.py:152
  10.9 1.3 %collective-permute-start.2 = (bf16[3,2,128,1,64]{2,4,1,3,0:T(8,128)(2,1)S(1)}, bf16[3,2,128,1,64]{2,4,1,3,0:T(8,128)(2,1)S(1)}, u32[]{:S(2)}, u32[]{:S(2)}) collective-permute-start(bf16[3,2,128,1,64]{2,4,1,3,0:T(8,128)(2,1)S(1)} %get-tuple-element.14), channel_id=1, source_target_pairs={{0,12},{4,0},{8,4},{12,8},{1,13},{5,1},{9,5},{13,9},{2,14},{6,2},{... | collective-permute-start | bytes 294920 | tf_op jit(solution)/shard_map/ppermute | solution.py:152
  12.3 0.1 broadcast_compare_fusion
  12.4 1.6 %collective-permute-done = bf16[3,2,128,1,64]{2,4,1,3,0:T(8,128)(2,1)S(1)} collective-permute-done((bf16[3,2,128,1,64]{2,4,1,3,0:T(8,128)(2,1)S(1)}, bf16[3,2,128,1,64]{2,4,1,3,0:T(8,128)(2,1)S(1)}, u32[]{:S(2)}, u32[]{:S(2)}) %collective-permute-start) | collective-permute-done | bytes 98336 | tf_op jit(solution)/shard_map/ppermute | solution.py:152
  14.0 3.5 %collective-permute-done.1 = bf16[3,2,128,1,64]{2,4,1,3,0:T(8,128)(2,1)S(1)} collective-permute-done((bf16[3,2,128,1,64]{2,4,1,3,0:T(8,128)(2,1)S(1)}, bf16[3,2,128,1,64]{2,4,1,3,0:T(8,128)(2,1)S(1)}, u32[]{:S(2)}, u32[]{:S(2)}) %collective-permute-start.1) | collective-permute-done | bytes 98336 | tf_op jit(solution)/shard_map/ppermute | solution.py:152
  17.6 0.8 %fusion.6 = (f32[2,512]{1,0:T(2,128)S(1)}, f32[2,512,512]{1,2,0:T(8,128)S(1)}) fusion(pred[2,512]{1,0:T(4,128)(4,1)S(1)} %broadcast_compare_fusion, bf16[3,2,512,1,64]{2,4,1,3,0:T(8,128)(2,1)S(1)} %pad_maximum_fusion), kind=kOutput, calls=%fused_computation.12 | convolution fusion | flops 68680704 | bytes 2365440 | tf_op jit(solution)/shard_map/sqhe,skhe->shqk/dot_general | solution.py:124
  18.4 0.5 fusion.7
  18.9 0.6 fusion.23
  19.6 3.6 %collective-permute-start.3 = (bf16[2,1,128,64]{2,3,0,1:T(8,128)(2,1)S(1)}, bf16[2,1,128,64]{2,3,0,1:T(8,128)(2,1)S(1)}, u32[]{:S(2)}, u32[]{:S(2)}) collective-permute-start(bf16[2,1,128,64]{2,3,0,1:T(8,128)(2,1)S(1)} %get-tuple-element.21), channel_id=1, source_target_pairs={{0,12},{4,0},{8,4},{12,8},{1,13},{5,1},{9,5},{13,9},{2,14},{6,2},{... | collective-permute-start | bytes 98312 | tf_op jit(solution)/shard_map/ppermute | solution.py:162
  23.3 0.4 collective-permute-start.4
  23.7 0.2 collective-permute-start.5
  23.9 0.9 %collective-permute-done.3 = bf16[2,1,128,64]{2,3,0,1:T(8,128)(2,1)S(1)} collective-permute-done((bf16[2,1,128,64]{2,3,0,1:T(8,128)(2,1)S(1)}, bf16[2,1,128,64]{2,3,0,1:T(8,128)(2,1)S(1)}, u32[]{:S(2)}, u32[]{:S(2)}) %collective-permute-start.3) | collective-permute-done | bytes 32800 | tf_op jit(solution)/shard_map/ppermute | solution.py:162
  24.9 3.4 %collective-permute-done.4 = bf16[2,1,128,64]{2,3,0,1:T(8,128)(2,1)S(1)} collective-permute-done((bf16[2,1,128,64]{2,3,0,1:T(8,128)(2,1)S(1)}, bf16[2,1,128,64]{2,3,0,1:T(8,128)(2,1)S(1)}, u32[]{:S(2)}, u32[]{:S(2)}) %collective-permute-start.4) | collective-permute-done | bytes 32800 | tf_op jit(solution)/shard_map/ppermute | solution.py:162
  28.2 1.2 %collective-permute-done.5 = bf16[2,1,128,64]{2,3,0,1:T(8,128)(2,1)S(1)} collective-permute-done((bf16[2,1,128,64]{2,3,0,1:T(8,128)(2,1)S(1)}, bf16[2,1,128,64]{2,3,0,1:T(8,128)(2,1)S(1)}, u32[]{:S(2)}, u32[]{:S(2)}) %collective-permute-start.5) | collective-permute-done | bytes 32800 | tf_op jit(solution)/shard_map/ppermute | solution.py:162
  29.5 0.4 convolution_convert_fusion
  30.0 0.1 collective-permute-start.7
  30.0 0.5 collective-permute-start.6
  30.5 1.1 %collective-permute-done.7 = bf16[2,32,1536]{2,1,0:T(8,128)(2,1)} collective-permute-done((bf16[2,32,1536]{2,1,0:T(8,128)(2,1)S(1)}, bf16[2,32,1536]{2,1,0:T(8,128)(2,1)}, u32[]{:S(2)}, u32[]{:S(2)}) %collective-permute-start.7) | collective-permute-done | bytes 196640 | tf_op jit(solution)/shard_map/ppermute | solution.py:59
  31.6 1.0 %fusion.45 = bf16[2,32,1536]{2,1,0:T(8,128)(2,1)S(1)} fusion(bf16[2,32,1536]{2,1,0:T(8,128)(2,1)} %collective-permute-done.7, bf16[2,2,2,32,1536]{4,3,2,1,0:T(8,128)(2,1)S(1)} %bitcast.127, s32[]{:T(128)S(6)} %select_n.127, s32[]{:T(128)S(6)} %select_n.123), kind=kLoop, calls=%fused_computation.49 | loop fusion | flops 393216 | bytes 589832 | tf_op jit(solution)/shard_map/convert_element_type | solution.py:71
  32.6 1.6 %collective-permute-start.8 = (bf16[2,32,1536]{2,1,0:T(8,128)(2,1)S(1)}, bf16[2,32,1536]{2,1,0:T(8,128)(2,1)}, u32[]{:S(2)}, u32[]{:S(2)}) collective-permute-start(bf16[2,32,1536]{2,1,0:T(8,128)(2,1)S(1)} %fusion.45), channel_id=1, source_target_pairs={{0,2},{1,3},{2,0},{3,1},{4,6},{5,7},{6,4},{7,5},{8,10},{9,11},{10,... | collective-permute-start | bytes 589832 | tf_op jit(solution)/shard_map/ppermute | solution.py:71
  34.1 5.6 %collective-permute-done.8 = bf16[2,32,1536]{2,1,0:T(8,128)(2,1)} collective-permute-done((bf16[2,32,1536]{2,1,0:T(8,128)(2,1)S(1)}, bf16[2,32,1536]{2,1,0:T(8,128)(2,1)}, u32[]{:S(2)}, u32[]{:S(2)}) %collective-permute-start.8) | collective-permute-done | bytes 196640 | tf_op jit(solution)/shard_map/ppermute | solution.py:71
  39.7 1.3 %fusion.63 = (f32[2,32]{1,0:T(2,128)S(1)}, f32[2,32,1536]{2,1,0:T(8,128)S(1)}) fusion(bf16[2,32,1536]{2,1,0:T(8,128)(2,1)} %collective-permute-done.8, bf16[2,32,1536]{2,1,0:T(8,128)(2,1)} %collective-permute-done.6, bf16[2,2,2,32,1536]{4,3,2,1,0:T(8,128)(2,1)S(1)} %bitcast.128, s32[]{:T(128)S(6)} %select_n.121, s32[]{:T(128)S(6)} %select_n.123, ...), kind=kLoop, calls=%fused_computation.113 | loop fusion | flops 786368 | bytes 1179916 | tf_op jit(solution)/shard_map/reduce_sum | solution.py:27
  41.0 0.2 multiply_reduce_fusion
  41.3 0.1 bitcast_dynamic-update-slice_fusion.3
  41.4 1.6 %collective-permute-start.9 = (bf16[2,32,1536]{2,1,0:T(8,128)(2,1)S(1)}, bf16[2,32,1536]{2,1,0:T(8,128)(2,1)S(1)}, u32[]{:S(2)}, u32[]{:S(2)}) collective-permute-start(bf16[2,32,1536]{2,1,0:T(8,128)(2,1)S(1)} %get-tuple-element.6), channel_id=1, source_target_pairs={{0,2},{1,3},{2,0},{3,1},{4,6},{5,7},{6,4},{7,5},{8,10},{9,11},{10,... | collective-permute-start | bytes 589832 | tf_op jit(solution)/shard_map/ppermute | solution.py:98
  43.0 0.1 broadcast_compare_fusion.1
  43.0 4.5 %collective-permute-done.9 = bf16[2,32,1536]{2,1,0:T(8,128)(2,1)S(1)} collective-permute-done((bf16[2,32,1536]{2,1,0:T(8,128)(2,1)S(1)}, bf16[2,32,1536]{2,1,0:T(8,128)(2,1)S(1)}, u32[]{:S(2)}, u32[]{:S(2)}) %collective-permute-start.9) | collective-permute-done | bytes 196640 | tf_op jit(solution)/shard_map/ppermute | solution.py:98
  47.8 1.2 %collective-permute-done.11 = bf16[2,32,1536]{2,1,0:T(8,128)(2,1)S(1)} collective-permute-done((bf16[2,32,1536]{2,1,0:T(8,128)(2,1)S(1)}, bf16[2,32,1536]{2,1,0:T(8,128)(2,1)S(1)}, u32[]{:S(2)}, u32[]{:S(2)}) %collective-permute-start.11) | collective-permute-done | bytes 196640 | tf_op jit(solution)/shard_map/ppermute | solution.py:99
  49.1 0.8 %fusion.12 = f32[2,2,128,384]{3,2,0,1:T(8,128)S(1)} fusion(bf16[2,128,1536,1]{2,1,3,0:T(8,128)(2,1)S(1)} %bitcast.133, bf16[2,1536,384]{2,1,0:T(8,128)(2,1)S(1)} %copy-done.5), kind=kOutput, calls=%fused_computation.18 | convolution fusion | flops 603979776 | bytes 3932160 | tf_op jit(solution)/shard_map/std,gdc->gstc/dot_general | solution.py:34
  49.9 0.1 bitcast_select_fusion
  50.1 1.3 %collective-permute-start.12 = (bf16[2,15,384]{2,1,0:T(8,128)(2,1)S(1)}, bf16[2,15,384]{2,1,0:T(8,128)(2,1)S(1)}, u32[]{:S(2)}, u32[]{:S(2)}) collective-permute-start(bf16[2,15,384]{2,1,0:T(8,128)(2,1)S(1)} %get-tuple-element.17), channel_id=1, source_target_pairs={{0,4},{4,8},{8,12},{1,5},{5,9},{9,13},{2,6},{6,10},{10,14},{3,7},{... | collective-permute-start | bytes 69128 | tf_op jit(solution)/shard_map/ppermute | solution.py:20
  51.4 1.3 %collective-permute-start.13 = (bf16[2,15,384]{2,1,0:T(8,128)(2,1)S(1)}, bf16[2,15,384]{2,1,0:T(8,128)(2,1)S(1)}, u32[]{:S(2)}, u32[]{:S(2)}) collective-permute-start(bf16[2,15,384]{2,1,0:T(8,128)(2,1)S(1)} %get-tuple-element.18), channel_id=1, source_target_pairs={{4,0},{8,4},{12,8},{5,1},{9,5},{13,9},{6,2},{10,6},{14,10},{7,3},{... | collective-permute-start | bytes 69128 | tf_op jit(solution)/shard_map/ppermute | solution.py:21
  52.7 0.2 collective-permute-done.12
  52.9 4.2 %collective-permute-done.13 = bf16[2,15,384]{2,1,0:T(8,128)(2,1)S(1)} collective-permute-done((bf16[2,15,384]{2,1,0:T(8,128)(2,1)S(1)}, bf16[2,15,384]{2,1,0:T(8,128)(2,1)S(1)}, u32[]{:S(2)}, u32[]{:S(2)}) %collective-permute-start.13) | collective-permute-done | bytes 23072 | tf_op jit(solution)/shard_map/ppermute | solution.py:21
  57.2 1.1 %fusion.50 = f32[2,128,384]{2,0,1:T(2,128)S(1)} fusion(bf16[2,158,384]{2,1,0:T(8,128)(2,1)S(1)} %pad_maximum_fusion.1, f32[31,1,384]{2,0,1:T(8,128)S(1)} %bitcast.135), kind=kOutput, calls=%fused_computation.60 | convolution fusion | flops 36569088 | bytes 683520 | tf_op jit(solution)/shard_map/conv_general_dilated | solution.py:220
  58.3 0.2 copy-done.6
  58.4 0.6 convolution_convert_fusion.1
  59.2 0.5 collective-permute-start.14
  59.7 0.9 %collective-permute-done.15 = bf16[2,32,1536]{2,1,0:T(8,128)(2,1)S(1)} collective-permute-done((bf16[2,32,1536]{2,1,0:T(8,128)(2,1)S(1)}, bf16[2,32,1536]{2,1,0:T(8,128)(2,1)S(1)}, u32[]{:S(2)}, u32[]{:S(2)}) %collective-permute-start.15) | collective-permute-done | bytes 196640 | tf_op jit(solution)/shard_map/ppermute | solution.py:59
  60.7 1.6 %collective-permute-start.16 = (bf16[2,32,1536]{2,1,0:T(8,128)(2,1)S(1)}, bf16[2,32,1536]{2,1,0:T(8,128)(2,1)S(1)}, u32[]{:S(2)}, u32[]{:S(2)}) collective-permute-start(bf16[2,32,1536]{2,1,0:T(8,128)(2,1)S(1)} %fusion.38), channel_id=1, source_target_pairs={{0,2},{1,3},{2,0},{3,1},{4,6},{5,7},{6,4},{7,5},{8,10},{9,11},{10,... | collective-permute-start | bytes 589832 | tf_op jit(solution)/shard_map/ppermute | solution.py:71
  62.2 0.1 broadcast_compare_fusion.2
  62.3 5.4 %collective-permute-done.16 = bf16[2,32,1536]{2,1,0:T(8,128)(2,1)S(1)} collective-permute-done((bf16[2,32,1536]{2,1,0:T(8,128)(2,1)S(1)}, bf16[2,32,1536]{2,1,0:T(8,128)(2,1)S(1)}, u32[]{:S(2)}, u32[]{:S(2)}) %collective-permute-start.16) | collective-permute-done | bytes 196640 | tf_op jit(solution)/shard_map/ppermute | solution.py:71
  67.7 0.8 %fusion.44 = bf16[2,32,1536]{2,1,0:T(8,128)(2,1)} fusion(f32[2,32,1536]{2,1,0:T(8,128)S(1)} %get-tuple-element.8, bf16[2,32,1536]{2,1,0:T(8,128)(2,1)S(1)} %collective-permute-done.16, bf16[2,32,1536]{2,1,0:T(8,128)(2,1)S(1)} %collective-permute-done.14, bf16[2,2,2,32,1536]{4,3,2,1,0:T(8,128)(2,1)S(1)} %bitcast.132, s32[]{:T(128)S(6)} %select_n.121, ...), kind=kLoop, calls=%fused_computation.47 | loop fusion | flops 1179648 | bytes 1185864 | tf_op jit(solution)/shard_map/convert_element_type | solution.py:237
  (62 shorter events, 0.9 us)
Async XLA Ops:
  0.0 3.0 %copy-start = (bf16[3,1536,256]{2,1,0:T(8,128)(2,1)S(1)}, bf16[3,1536,256]{2,1,0:T(8,128)(2,1)}, u32[]{:S(2)}) copy-start(bf16[3,1536,256]{2,1,0:T(8,128)(2,1)} %param.15) | copy-start | bytes 7077892
  3.0 9.3 %copy-start.4 = (s32[2]{0:T(128)S(1)}, s32[2]{0:T(128)}, u32[]{:S(2)}) copy-start(s32[2]{0:T(128)} %param.13) | copy-start | bytes 28
  5.3 8.8 %collective-permute-start = (bf16[3,2,128,1,64]{2,4,1,3,0:T(8,128)(2,1)S(1)}, bf16[3,2,128,1,64]{2,4,1,3,0:T(8,128)(2,1)S(1)}, u32[]{:S(2)}, u32[]{:S(2)}) collective-permute-start(bf16[3,2,128,1,64]{2,4,1,3,0:T(8,128)(2,1)S(1)} %get-tuple-element.16), channel_id=1, source_target_pairs={{0,4},{4,8},{8,12},{12,0},{1,5},{5,9},{9,13},{13,1},{2,6},{6,10},{... | collective-permute-start | bytes 294920 | tf_op jit(solution)/shard_map/ppermute | solution.py:152
  8.4 9.2 %collective-permute-start.1 = (bf16[3,2,128,1,64]{2,4,1,3,0:T(8,128)(2,1)S(1)}, bf16[3,2,128,1,64]{2,4,1,3,0:T(8,128)(2,1)S(1)}, u32[]{:S(2)}, u32[]{:S(2)}) collective-permute-start(bf16[3,2,128,1,64]{2,4,1,3,0:T(8,128)(2,1)S(1)} %get-tuple-element.15), channel_id=1, source_target_pairs={{0,8},{4,12},{8,0},{12,4},{1,9},{5,13},{9,1},{13,5},{2,10},{6,14},... | collective-permute-start | bytes 294920 | tf_op jit(solution)/shard_map/ppermute | solution.py:152
  10.9 6.6 %collective-permute-start.2 = (bf16[3,2,128,1,64]{2,4,1,3,0:T(8,128)(2,1)S(1)}, bf16[3,2,128,1,64]{2,4,1,3,0:T(8,128)(2,1)S(1)}, u32[]{:S(2)}, u32[]{:S(2)}) collective-permute-start(bf16[3,2,128,1,64]{2,4,1,3,0:T(8,128)(2,1)S(1)} %get-tuple-element.14), channel_id=1, source_target_pairs={{0,12},{4,0},{8,4},{12,8},{1,13},{5,1},{9,5},{13,9},{2,14},{6,2},{... | collective-permute-start | bytes 294920 | tf_op jit(solution)/shard_map/ppermute | solution.py:152
  18.9 10.6 %copy-start.1 = (bf16[256,1536]{1,0:T(8,128)(2,1)S(1)}, bf16[256,1536]{1,0:T(8,128)(2,1)}, u32[]{:S(2)}) copy-start(bf16[256,1536]{1,0:T(8,128)(2,1)} %param.16) | copy-start | bytes 2359300
  19.6 5.2 %collective-permute-start.3 = (bf16[2,1,128,64]{2,3,0,1:T(8,128)(2,1)S(1)}, bf16[2,1,128,64]{2,3,0,1:T(8,128)(2,1)S(1)}, u32[]{:S(2)}, u32[]{:S(2)}) collective-permute-start(bf16[2,1,128,64]{2,3,0,1:T(8,128)(2,1)S(1)} %get-tuple-element.21), channel_id=1, source_target_pairs={{0,12},{4,0},{8,4},{12,8},{1,13},{5,1},{9,5},{13,9},{2,14},{6,2},{... | collective-permute-start | bytes 98312 | tf_op jit(solution)/shard_map/ppermute | solution.py:162
  23.3 5.0 %collective-permute-start.4 = (bf16[2,1,128,64]{2,3,0,1:T(8,128)(2,1)S(1)}, bf16[2,1,128,64]{2,3,0,1:T(8,128)(2,1)S(1)}, u32[]{:S(2)}, u32[]{:S(2)}) collective-permute-start(bf16[2,1,128,64]{2,3,0,1:T(8,128)(2,1)S(1)} %get-tuple-element.20), channel_id=1, source_target_pairs={{0,8},{4,12},{8,0},{12,4},{1,9},{5,13},{9,1},{13,5},{2,10},{6,14},... | collective-permute-start | bytes 98312 | tf_op jit(solution)/shard_map/ppermute | solution.py:162
  23.7 5.7 %collective-permute-start.5 = (bf16[2,1,128,64]{2,3,0,1:T(8,128)(2,1)S(1)}, bf16[2,1,128,64]{2,3,0,1:T(8,128)(2,1)S(1)}, u32[]{:S(2)}, u32[]{:S(2)}) collective-permute-start(bf16[2,1,128,64]{2,3,0,1:T(8,128)(2,1)S(1)} %get-tuple-element.19), channel_id=1, source_target_pairs={{0,4},{4,8},{8,12},{12,0},{1,5},{5,9},{9,13},{13,1},{2,6},{6,10},{... | collective-permute-start | bytes 98312 | tf_op jit(solution)/shard_map/ppermute | solution.py:162
  29.9 11.3 %copy-start.2 = (f32[1536]{0:T(1024)S(1)}, f32[1536]{0:T(1024)}, u32[]{:S(2)}) copy-start(f32[1536]{0:T(1024)} %param.17) | copy-start | bytes 18436
  30.0 1.6 %collective-permute-start.7 = (bf16[2,32,1536]{2,1,0:T(8,128)(2,1)S(1)}, bf16[2,32,1536]{2,1,0:T(8,128)(2,1)}, u32[]{:S(2)}, u32[]{:S(2)}) collective-permute-start(bf16[2,32,1536]{2,1,0:T(8,128)(2,1)S(1)} %get-tuple-element.12), channel_id=1, source_target_pairs={{0,1},{1,0},{2,3},{3,2},{4,5},{5,4},{6,7},{7,6},{8,9},{9,8},{10,11... | collective-permute-start | bytes 589832 | tf_op jit(solution)/shard_map/ppermute | solution.py:59
  30.0 4.1 %collective-permute-start.6 = (bf16[2,32,1536]{2,1,0:T(8,128)(2,1)S(1)}, bf16[2,32,1536]{2,1,0:T(8,128)(2,1)}, u32[]{:S(2)}, u32[]{:S(2)}) collective-permute-start(bf16[2,32,1536]{2,1,0:T(8,128)(2,1)S(1)} %get-tuple-element.11), channel_id=1, source_target_pairs={{0,1},{1,0},{2,3},{3,2},{4,5},{5,4},{6,7},{7,6},{8,9},{9,8},{10,11... | collective-permute-start | bytes 589832 | tf_op jit(solution)/shard_map/ppermute | solution.py:63
  32.6 7.1 %collective-permute-start.8 = (bf16[2,32,1536]{2,1,0:T(8,128)(2,1)S(1)}, bf16[2,32,1536]{2,1,0:T(8,128)(2,1)}, u32[]{:S(2)}, u32[]{:S(2)}) collective-permute-start(bf16[2,32,1536]{2,1,0:T(8,128)(2,1)S(1)} %fusion.45), channel_id=1, source_target_pairs={{0,2},{1,3},{2,0},{3,1},{4,6},{5,7},{6,4},{7,5},{8,10},{9,11},{10,... | collective-permute-start | bytes 589832 | tf_op jit(solution)/shard_map/ppermute | solution.py:71
  41.4 7.7 %copy-start.5 = (bf16[2,1536,384]{2,1,0:T(8,128)(2,1)S(1)}, bf16[2,1536,384]{2,1,0:T(8,128)(2,1)}, u32[]{:S(2)}) copy-start(bf16[2,1536,384]{2,1,0:T(8,128)(2,1)} %param.18) | copy-start | bytes 7077892
  41.4 6.2 %collective-permute-start.9 = (bf16[2,32,1536]{2,1,0:T(8,128)(2,1)S(1)}, bf16[2,32,1536]{2,1,0:T(8,128)(2,1)S(1)}, u32[]{:S(2)}, u32[]{:S(2)}) collective-permute-start(bf16[2,32,1536]{2,1,0:T(8,128)(2,1)S(1)} %get-tuple-element.6), channel_id=1, source_target_pairs={{0,2},{1,3},{2,0},{3,1},{4,6},{5,7},{6,4},{7,5},{8,10},{9,11},{10,... | collective-permute-start | bytes 589832 | tf_op jit(solution)/shard_map/ppermute | solution.py:98
  43.0 4.6 %collective-permute-start.10 = (bf16[2,32,1536]{2,1,0:T(8,128)(2,1)S(1)}, bf16[2,32,1536]{2,1,0:T(8,128)(2,1)S(1)}, u32[]{:S(2)}, u32[]{:S(2)}) collective-permute-start(bf16[2,32,1536]{2,1,0:T(8,128)(2,1)S(1)} %get-tuple-element.6), channel_id=1, source_target_pairs={{0,1},{1,0},{2,3},{3,2},{4,5},{5,4},{6,7},{7,6},{8,9},{9,8},{10,11... | collective-permute-start | bytes 589832 | tf_op jit(solution)/shard_map/ppermute | solution.py:95
  47.6 1.4 %collective-permute-start.11 = (bf16[2,32,1536]{2,1,0:T(8,128)(2,1)S(1)}, bf16[2,32,1536]{2,1,0:T(8,128)(2,1)S(1)}, u32[]{:S(2)}, u32[]{:S(2)}) collective-permute-start(bf16[2,32,1536]{2,1,0:T(8,128)(2,1)S(1)} %collective-permute-done.9), channel_id=1, source_target_pairs={{0,1},{1,0},{2,3},{3,2},{4,5},{5,4},{6,7},{7,6},{8,9},{9,8},{10,11... | collective-permute-start | bytes 589832 | tf_op jit(solution)/shard_map/ppermute | solution.py:99
  49.1 8.1 %copy-start.7 = (f32[31,384]{1,0:T(8,128)S(1)}, f32[31,384]{1,0:T(8,128)}, u32[]{:S(2)}) copy-start(f32[31,384]{1,0:T(8,128)} %param.19) | copy-start | bytes 142852
  50.1 2.8 %collective-permute-start.12 = (bf16[2,15,384]{2,1,0:T(8,128)(2,1)S(1)}, bf16[2,15,384]{2,1,0:T(8,128)(2,1)S(1)}, u32[]{:S(2)}, u32[]{:S(2)}) collective-permute-start(bf16[2,15,384]{2,1,0:T(8,128)(2,1)S(1)} %get-tuple-element.17), channel_id=1, source_target_pairs={{0,4},{4,8},{8,12},{1,5},{5,9},{9,13},{2,6},{6,10},{10,14},{3,7},{... | collective-permute-start | bytes 69128 | tf_op jit(solution)/shard_map/ppermute | solution.py:20
  51.4 5.7 %collective-permute-start.13 = (bf16[2,15,384]{2,1,0:T(8,128)(2,1)S(1)}, bf16[2,15,384]{2,1,0:T(8,128)(2,1)S(1)}, u32[]{:S(2)}, u32[]{:S(2)}) collective-permute-start(bf16[2,15,384]{2,1,0:T(8,128)(2,1)S(1)} %get-tuple-element.18), channel_id=1, source_target_pairs={{4,0},{8,4},{12,8},{5,1},{9,5},{13,9},{6,2},{10,6},{14,10},{7,3},{... | collective-permute-start | bytes 69128 | tf_op jit(solution)/shard_map/ppermute | solution.py:21
  57.2 1.3 %copy-start.6 = (bf16[384,1536]{1,0:T(8,128)(2,1)S(1)}, bf16[384,1536]{1,0:T(8,128)(2,1)}, u32[]{:S(2)}) copy-start(bf16[384,1536]{1,0:T(8,128)(2,1)} %param.22) | copy-start | bytes 3538948
  57.2 1.3 %copy-start.8 = (f32[384]{0:T(512)S(1)}, f32[384]{0:T(512)}, u32[]{:S(2)}) copy-start(f32[384]{0:T(512)} %param.21) | copy-start | bytes 4612
  57.2 1.3 %copy-start.9 = (f32[384]{0:T(512)S(1)}, f32[384]{0:T(512)}, u32[]{:S(2)}) copy-start(f32[384]{0:T(512)} %param.20) | copy-start | bytes 4612
  58.4 0.7 %copy-start.3 = (s32[1536]{0:T(1024)S(1)}, s32[1536]{0:T(1024)}, u32[]{:S(2)}) copy-start(s32[1536]{0:T(1024)} %param.23) | copy-start | bytes 18436
  59.1 1.5 %collective-permute-start.15 = (bf16[2,32,1536]{2,1,0:T(8,128)(2,1)S(1)}, bf16[2,32,1536]{2,1,0:T(8,128)(2,1)S(1)}, u32[]{:S(2)}, u32[]{:S(2)}) collective-permute-start(bf16[2,32,1536]{2,1,0:T(8,128)(2,1)S(1)} %get-tuple-element.10), channel_id=1, source_target_pairs={{0,1},{1,0},{2,3},{3,2},{4,5},{5,4},{6,7},{7,6},{8,9},{9,8},{10,11... | collective-permute-start | bytes 589832 | tf_op jit(solution)/shard_map/ppermute | solution.py:59
  59.2 3.1 %collective-permute-start.14 = (bf16[2,32,1536]{2,1,0:T(8,128)(2,1)S(1)}, bf16[2,32,1536]{2,1,0:T(8,128)(2,1)S(1)}, u32[]{:S(2)}, u32[]{:S(2)}) collective-permute-start(bf16[2,32,1536]{2,1,0:T(8,128)(2,1)S(1)} %get-tuple-element.9), channel_id=1, source_target_pairs={{0,1},{1,0},{2,3},{3,2},{4,5},{5,4},{6,7},{7,6},{8,9},{9,8},{10,11... | collective-permute-start | bytes 589832 | tf_op jit(solution)/shard_map/ppermute | solution.py:63
  60.7 7.0 %collective-permute-start.16 = (bf16[2,32,1536]{2,1,0:T(8,128)(2,1)S(1)}, bf16[2,32,1536]{2,1,0:T(8,128)(2,1)S(1)}, u32[]{:S(2)}, u32[]{:S(2)}) collective-permute-start(bf16[2,32,1536]{2,1,0:T(8,128)(2,1)S(1)} %fusion.38), channel_id=1, source_target_pairs={{0,2},{1,3},{2,0},{3,1},{4,6},{5,7},{6,4},{7,5},{8,10},{9,11},{10,... | collective-permute-start | bytes 589832 | tf_op jit(solution)/shard_map/ppermute | solution.py:71

commit v21 on v20

--- a/solution.py
+++ b/solution.py
@@ -87,7 +87,7 @@
     return lax.dynamic_update_index_in_dim(both, other, 1 - bit, axis)
 
 
-def all_gather_rows(x, axis, dim):
+def all_gather_rows(x, axis, dim, apply=None):
     count, rank = lax.axis_size(axis), lax.axis_index(axis)
     bits = bit_count(count)
     shape = x.shape
@@ -99,8 +99,10 @@
         forwarded = lax.ppermute(got, axis, xor_pairs(count, 1))
         mine_acc = place_pair(mine_acc, got, bit, dim + k)
         their_acc = place_pair(their_acc, forwarded, bit, dim + k)
+    if apply is not None:
+        mine_acc, their_acc = apply(mine_acc), apply(their_acc)
     acc = place_pair(mine_acc, their_acc, rank & 1, dim + bits - 1)
-    return acc.reshape(shape[:dim] + (shape[dim] * count,) + shape[dim + 1 :])
+    return acc.reshape(acc.shape[:dim] + (shape[dim] * count,) + acc.shape[dim + bits + 1 :])
 
 
 def ring_gather(x, axis):
@@ -210,8 +212,12 @@
     features_mine = lax.dynamic_slice_in_dim(features, row_start, rows_mine, 1)
     residual_mine = features_mine.astype(jnp.float32) + attn_mine
     normed_mine = layer_norm(residual_mine, conv_gain).astype(jnp.bfloat16)
-    normed_conv = all_gather_rows(normed_mine, "mp", 1)
-    gated_rows = gated_units(normed_conv, w_glu)
+    def glu_blocks(rows):
+        flat = rows.reshape(records, -1, model_width)
+        gated = gated_units(flat, w_glu)
+        return gated.reshape(rows.shape[:-1] + gated.shape[-1:])
+
+    gated_rows = all_gather_rows(normed_mine, "mp", 1, apply=glu_blocks)
     frame_ids = first_frame + jnp.arange(frames_here, dtype=jnp.int32)
     frame_live = frame_ids[None, :] < frame_counts[:, None]
     gated_rows = jnp.where(frame_live[..., None], gated_rows, jnp.zeros((), jnp.bfloat16))

time: 68.8 us -> 69.2 us (level)
  transfers between devices with their start and end apart: 17 -> 17, of which waited for: 13 -> 13; matrix products, arithmetic and copies ran while one was open for 2% -> 3% of each run, Pallas kernels for 0% -> 0%
where the time goes in v21:
time: 69.2 us; the launch traced here: 69 us
  waiting for transfers between devices  33.4 us (48%)
  starting transfers between devices  19.8 us (29%)
  other arithmetic  7.68 us (11%)
  matrix products  6.49 us (9%)
  local copies, waits for them, and re-layouts  1.11 us (2%)
    ppermute x2, waiting for transfers between devices, reduce_scatter_rows(): got = lax.ppermute(far.astype(jnp.bfloat16), axis, xor_pairs(count, 2))  10.9 us
    ppermute x3, starting transfers between devices, attend_by_heads(): pieces.append(lax.ppermute(send, axis, pairs))  7.01 us
    ppermute x3, waiting for transfers between devices, attend_by_heads(): back.append(lax.ppermute(rows, axis, pairs))  5.45 us
    ppermute x3, waiting for transfers between devices, attend_by_heads(): pieces.append(lax.ppermute(send, axis, pairs))  5.16 us
    ppermute x1, waiting for transfers between devices, all_gather_rows(): got = lax.ppermute(mine_acc, axis, xor_pairs(count, 1 << b))  4.46 us
    ppermute x3, starting transfers between devices, attend_by_heads(): back.append(lax.ppermute(rows, axis, pairs))  4.3 us
    ppermute x1, waiting for transfers between devices, with_halo(): after = lax.ppermute(initial, axis, down)  4.22 us
    ppermute x2, starting transfers between devices, reduce_scatter_rows(): got = lax.ppermute(far.astype(jnp.bfloat16), axis, xor_pairs(count, 2))  3.11 us
  transfers between devices with their start and end apart: 17, of which 13 were waited for; matrix products, arithmetic and copies ran while one was open for 3% of the time, Pallas kernels for 0%

profile of v21, /device:TPU:0, one launch (start us, length us, event | category | flops | bytes accessed | tf_op | source)
XLA Modules:
  0.0 69.0 jit_solution(17408203010561931872)
XLA Ops:
  0.0 1.5 %convert_reduce_fusion = f32[2,128]{1,0:T(2,128)S(1)} fusion(bf16[2,128,1536]{2,1,0:T(8,128)(2,1)} %param.12), kind=kLoop, calls=%fused_computation.11 | loop fusion | flops 786176 | bytes 787456 | tf_op jit(solution)/shard_map/reduce_sum | solution.py:27
  1.5 1.5 %fusion.11 = f32[2,128]{1,0:T(2,128)S(1)} fusion(bf16[2,128,1536]{2,1,0:T(8,128)(2,1)} %param.12, f32[2,128]{1,0:T(2,128)S(1)} %broadcast_multiply_fusion.1), kind=kLoop, calls=%fused_computation.17 | loop fusion | flops 1572608 | bytes 788480 | tf_op jit(solution)/shard_map/reduce_sum | solution.py:29
  3.0 2.0 %fusion.23 = bf16[3,2,128,256]{3,2,0,1:T(8,128)(2,1)S(1)} fusion(bf16[3,1536,256]{2,1,0:T(8,128)(2,1)S(1)} %copy-done, bf16[2,128,1536]{2,1,0:T(8,128)(2,1)} %param.12, f32[1536]{0:T(1024)} %param.14, f32[2,128]{1,0:T(2,128)S(1)} %add_rsqrt_fusion.1, f32[2,128]{1,0:T(2,128)S(1)} %broadcast_multiply_fusion.1), kind=kOutput, calls=%fused_computation.23 | convolution fusion | flops 606142464 | bytes 3547136 | tf_op jit(solution)/shard_map/std,idc->istc/dot_general | solution.py:190
  5.0 0.2 copy.46
  5.3 3.1 %collective-permute-start = (bf16[3,2,128,1,64]{2,4,1,3,0:T(8,128)(2,1)S(1)}, bf16[3,2,128,1,64]{2,4,1,3,0:T(8,128)(2,1)S(1)}, u32[]{:S(2)}, u32[]{:S(2)}) collective-permute-start(bf16[3,2,128,1,64]{2,4,1,3,0:T(8,128)(2,1)S(1)} %get-tuple-element.16), channel_id=1, source_target_pairs={{0,4},{4,8},{8,12},{12,0},{1,5},{5,9},{9,13},{13,1},{2,6},{6,10},{... | collective-permute-start | bytes 294920 | tf_op jit(solution)/shard_map/ppermute | solution.py:154
  8.4 2.6 %collective-permute-start.1 = (bf16[3,2,128,1,64]{2,4,1,3,0:T(8,128)(2,1)S(1)}, bf16[3,2,128,1,64]{2,4,1,3,0:T(8,128)(2,1)S(1)}, u32[]{:S(2)}, u32[]{:S(2)}) collective-permute-start(bf16[3,2,128,1,64]{2,4,1,3,0:T(8,128)(2,1)S(1)} %get-tuple-element.15), channel_id=1, source_target_pairs={{0,8},{4,12},{8,0},{12,4},{1,9},{5,13},{9,1},{13,5},{2,10},{6,14},... | collective-permute-start | bytes 294920 | tf_op jit(solution)/shard_map/ppermute | solution.py:154
  10.9 1.3 %collective-permute-start.2 = (bf16[3,2,128,1,64]{2,4,1,3,0:T(8,128)(2,1)S(1)}, bf16[3,2,128,1,64]{2,4,1,3,0:T(8,128)(2,1)S(1)}, u32[]{:S(2)}, u32[]{:S(2)}) collective-permute-start(bf16[3,2,128,1,64]{2,4,1,3,0:T(8,128)(2,1)S(1)} %get-tuple-element.14), channel_id=1, source_target_pairs={{0,12},{4,0},{8,4},{12,8},{1,13},{5,1},{9,5},{13,9},{2,14},{6,2},{... | collective-permute-start | bytes 294920 | tf_op jit(solution)/shard_map/ppermute | solution.py:154
  12.4 1.6 %collective-permute-done = bf16[3,2,128,1,64]{2,4,1,3,0:T(8,128)(2,1)S(1)} collective-permute-done((bf16[3,2,128,1,64]{2,4,1,3,0:T(8,128)(2,1)S(1)}, bf16[3,2,128,1,64]{2,4,1,3,0:T(8,128)(2,1)S(1)}, u32[]{:S(2)}, u32[]{:S(2)}) %collective-permute-start) | collective-permute-done | bytes 98336 | tf_op jit(solution)/shard_map/ppermute | solution.py:154
  14.0 3.5 %collective-permute-done.1 = bf16[3,2,128,1,64]{2,4,1,3,0:T(8,128)(2,1)S(1)} collective-permute-done((bf16[3,2,128,1,64]{2,4,1,3,0:T(8,128)(2,1)S(1)}, bf16[3,2,128,1,64]{2,4,1,3,0:T(8,128)(2,1)S(1)}, u32[]{:S(2)}, u32[]{:S(2)}) %collective-permute-start.1) | collective-permute-done | bytes 98336 | tf_op jit(solution)/shard_map/ppermute | solution.py:154
  17.6 0.8 %fusion.8 = (f32[2,512]{1,0:T(2,128)S(1)}, f32[2,512,512]{1,2,0:T(8,128)S(1)}) fusion(pred[2,512]{1,0:T(4,128)(4,1)S(1)} %broadcast_compare_fusion.1, bf16[3,2,512,1,64]{2,4,1,3,0:T(8,128)(2,1)S(1)} %pad_maximum_fusion), kind=kOutput, calls=%fused_computation.14 | convolution fusion | flops 68680704 | bytes 2365440 | tf_op jit(solution)/shard_map/sqhe,skhe->shqk/dot_general | solution.py:126
  18.4 0.5 fusion.9
  18.9 0.6 fusion.28
  19.6 3.6 %collective-permute-start.3 = (bf16[2,1,128,64]{2,3,0,1:T(8,128)(2,1)S(1)}, bf16[2,1,128,64]{2,3,0,1:T(8,128)(2,1)S(1)}, u32[]{:S(2)}, u32[]{:S(2)}) collective-permute-start(bf16[2,1,128,64]{2,3,0,1:T(8,128)(2,1)S(1)} %get-tuple-element.21), channel_id=1, source_target_pairs={{0,12},{4,0},{8,4},{12,8},{1,13},{5,1},{9,5},{13,9},{2,14},{6,2},{... | collective-permute-start | bytes 98312 | tf_op jit(solution)/shard_map/ppermute | solution.py:164
  23.3 0.4 collective-permute-start.4
  23.7 0.2 collective-permute-start.5
  23.9 0.9 %collective-permute-done.3 = bf16[2,1,128,64]{2,3,0,1:T(8,128)(2,1)S(1)} collective-permute-done((bf16[2,1,128,64]{2,3,0,1:T(8,128)(2,1)S(1)}, bf16[2,1,128,64]{2,3,0,1:T(8,128)(2,1)S(1)}, u32[]{:S(2)}, u32[]{:S(2)}) %collective-permute-start.3) | collective-permute-done | bytes 32800 | tf_op jit(solution)/shard_map/ppermute | solution.py:164
  24.9 3.4 %collective-permute-done.4 = bf16[2,1,128,64]{2,3,0,1:T(8,128)(2,1)S(1)} collective-permute-done((bf16[2,1,128,64]{2,3,0,1:T(8,128)(2,1)S(1)}, bf16[2,1,128,64]{2,3,0,1:T(8,128)(2,1)S(1)}, u32[]{:S(2)}, u32[]{:S(2)}) %collective-permute-start.4) | collective-permute-done | bytes 32800 | tf_op jit(solution)/shard_map/ppermute | solution.py:164
  28.2 1.2 %collective-permute-done.5 = bf16[2,1,128,64]{2,3,0,1:T(8,128)(2,1)S(1)} collective-permute-done((bf16[2,1,128,64]{2,3,0,1:T(8,128)(2,1)S(1)}, bf16[2,1,128,64]{2,3,0,1:T(8,128)(2,1)S(1)}, u32[]{:S(2)}, u32[]{:S(2)}) %collective-permute-start.5) | collective-permute-done | bytes 32800 | tf_op jit(solution)/shard_map/ppermute | solution.py:164
  29.5 0.4 convolution_convert_fusion
  30.0 0.5 collective-permute-start.6
  30.5 1.1 %collective-permute-done.7 = bf16[2,32,1536]{2,1,0:T(8,128)(2,1)} collective-permute-done((bf16[2,32,1536]{2,1,0:T(8,128)(2,1)S(1)}, bf16[2,32,1536]{2,1,0:T(8,128)(2,1)}, u32[]{:S(2)}, u32[]{:S(2)}) %collective-permute-start.7) | collective-permute-done | bytes 196640 | tf_op jit(solution)/shard_map/ppermute | solution.py:59
  31.6 1.0 %fusion.46 = bf16[2,32,1536]{2,1,0:T(8,128)(2,1)S(1)} fusion(bf16[2,32,1536]{2,1,0:T(8,128)(2,1)} %collective-permute-done.7, bf16[2,2,2,32,1536]{4,3,2,1,0:T(8,128)(2,1)S(1)} %bitcast.141, s32[]{:T(128)S(6)} %select_n.127, s32[]{:T(128)S(6)} %select_n.123), kind=kLoop, calls=%fused_computation.47 | loop fusion | flops 393216 | bytes 589832 | tf_op jit(solution)/shard_map/convert_element_type | solution.py:71
  32.6 1.6 %collective-permute-start.8 = (bf16[2,32,1536]{2,1,0:T(8,128)(2,1)S(1)}, bf16[2,32,1536]{2,1,0:T(8,128)(2,1)}, u32[]{:S(2)}, u32[]{:S(2)}) collective-permute-start(bf16[2,32,1536]{2,1,0:T(8,128)(2,1)S(1)} %fusion.46), channel_id=1, source_target_pairs={{0,2},{1,3},{2,0},{3,1},{4,6},{5,7},{6,4},{7,5},{8,10},{9,11},{10,... | collective-permute-start | bytes 589832 | tf_op jit(solution)/shard_map/ppermute | solution.py:71
  34.1 5.6 %collective-permute-done.8 = bf16[2,32,1536]{2,1,0:T(8,128)(2,1)} collective-permute-done((bf16[2,32,1536]{2,1,0:T(8,128)(2,1)S(1)}, bf16[2,32,1536]{2,1,0:T(8,128)(2,1)}, u32[]{:S(2)}, u32[]{:S(2)}) %collective-permute-start.8) | collective-permute-done | bytes 196640 | tf_op jit(solution)/shard_map/ppermute | solution.py:71
  39.7 1.3 %fusion.78 = (f32[2,32]{1,0:T(2,128)S(1)}, f32[2,32,1536]{2,1,0:T(8,128)S(1)}) fusion(bf16[2,32,1536]{2,1,0:T(8,128)(2,1)} %collective-permute-done.8, bf16[2,32,1536]{2,1,0:T(8,128)(2,1)} %collective-permute-done.6, bf16[2,2,2,32,1536]{4,3,2,1,0:T(8,128)(2,1)S(1)} %bitcast.142, s32[]{:T(128)S(6)} %select_n.121, s32[]{:T(128)S(6)} %select_n.123, ...), kind=kLoop, calls=%fused_computation.126 | loop fusion | flops 786368 | bytes 1179916 | tf_op jit(solution)/shard_map/reduce_sum | solution.py:27
  41.0 0.2 multiply_reduce_fusion
  41.3 0.1 bitcast_dynamic-update-slice_fusion.3
  41.4 1.6 %collective-permute-start.9 = (bf16[2,32,1536]{2,1,0:T(8,128)(2,1)S(1)}, bf16[2,32,1536]{2,1,0:T(8,128)(2,1)S(1)}, u32[]{:S(2)}, u32[]{:S(2)}) collective-permute-start(bf16[2,32,1536]{2,1,0:T(8,128)(2,1)S(1)} %get-tuple-element.6), channel_id=1, source_target_pairs={{0,2},{1,3},{2,0},{3,1},{4,6},{5,7},{6,4},{7,5},{8,10},{9,11},{10,... | collective-permute-start | bytes 589832 | tf_op jit(solution)/shard_map/ppermute | solution.py:98
  43.1 4.5 %collective-permute-done.9 = bf16[2,32,1536]{2,1,0:T(8,128)(2,1)S(1)} collective-permute-done((bf16[2,32,1536]{2,1,0:T(8,128)(2,1)S(1)}, bf16[2,32,1536]{2,1,0:T(8,128)(2,1)S(1)}, u32[]{:S(2)}, u32[]{:S(2)}) %collective-permute-start.9) | collective-permute-done | bytes 196640 | tf_op jit(solution)/shard_map/ppermute | solution.py:98
  47.6 0.5 fusion.17
  48.3 0.1 broadcast_in_dim.85
  48.4 0.1 copy_dynamic-update-slice_fusion.1
  48.6 1.0 %collective-permute-done.11 = bf16[2,32,1536]{2,1,0:T(8,128)(2,1)S(1)} collective-permute-done((bf16[2,32,1536]{2,1,0:T(8,128)(2,1)S(1)}, bf16[2,32,1536]{2,1,0:T(8,128)(2,1)S(1)}, u32[]{:S(2)}, u32[]{:S(2)}) %collective-permute-start.11) | collective-permute-done | bytes 196640 | tf_op jit(solution)/shard_map/ppermute | solution.py:99
  49.6 0.5 fusion.20
  50.2 0.1 copy_dynamic-update-slice_fusion
  50.3 0.3 broadcast_select_fusion
  50.7 1.3 %collective-permute-start.12 = (bf16[2,15,384]{2,0,1:T(2,128)(2,1)S(1)}, bf16[2,15,384]{2,0,1:T(2,128)(2,1)S(1)}, u32[]{:S(2)}, u32[]{:S(2)}) collective-permute-start(bf16[2,15,384]{2,0,1:T(2,128)(2,1)S(1)} %get-tuple-element.17), channel_id=1, source_target_pairs={{0,4},{4,8},{8,12},{1,5},{5,9},{9,13},{2,6},{6,10},{10,14},{3,7},{... | collective-permute-start | bytes 69128 | tf_op jit(solution)/shard_map/ppermute | solution.py:20
  52.0 1.3 %collective-permute-start.13 = (bf16[2,15,384]{2,0,1:T(2,128)(2,1)S(1)}, bf16[2,15,384]{2,0,1:T(2,128)(2,1)S(1)}, u32[]{:S(2)}, u32[]{:S(2)}) collective-permute-start(bf16[2,15,384]{2,0,1:T(2,128)(2,1)S(1)} %get-tuple-element.18), channel_id=1, source_target_pairs={{4,0},{8,4},{12,8},{5,1},{9,5},{13,9},{6,2},{10,6},{14,10},{7,3},{... | collective-permute-start | bytes 69128 | tf_op jit(solution)/shard_map/ppermute | solution.py:21
  53.3 0.2 collective-permute-done.12
  53.5 4.2 %collective-permute-done.13 = bf16[2,15,384]{2,0,1:T(2,128)(2,1)S(1)} collective-permute-done((bf16[2,15,384]{2,0,1:T(2,128)(2,1)S(1)}, bf16[2,15,384]{2,0,1:T(2,128)(2,1)S(1)}, u32[]{:S(2)}, u32[]{:S(2)}) %collective-permute-start.13) | collective-permute-done | bytes 23072 | tf_op jit(solution)/shard_map/ppermute | solution.py:21
  57.7 1.2 %fusion.50 = f32[2,128,384]{2,0,1:T(2,128)S(1)} fusion(bf16[2,15,384]{2,0,1:T(2,128)(2,1)S(1)} %collective-permute-done.13, bf16[2,128,384]{2,0,1:T(2,128)(2,1)S(1)} %broadcast_select_fusion, bf16[2,15,384]{2,0,1:T(2,128)(2,1)S(1)} %collective-permute-done.12, f32[31,1,384]{2,0,1:T(8,128)S(1)} %bitcast.152), kind=kOutput, calls=%fused_computation.57 | convolution fusion | flops 37297152 | bytes 683520 | tf_op jit(solution)/shard_map/conv_general_dilated | solution.py:226
  58.8 0.1 copy-done.6
  59.0 0.6 convolution_convert_fusion.1
  59.7 0.5 collective-permute-start.14
  60.2 0.9 %collective-permute-done.15 = bf16[2,32,1536]{2,1,0:T(8,128)(2,1)S(1)} collective-permute-done((bf16[2,32,1536]{2,1,0:T(8,128)(2,1)S(1)}, bf16[2,32,1536]{2,1,0:T(8,128)(2,1)S(1)}, u32[]{:S(2)}, u32[]{:S(2)}) %collective-permute-start.15) | collective-permute-done | bytes 196640 | tf_op jit(solution)/shard_map/ppermute | solution.py:59
  61.2 1.6 %collective-permute-start.16 = (bf16[2,32,1536]{2,1,0:T(8,128)(2,1)S(1)}, bf16[2,32,1536]{2,1,0:T(8,128)(2,1)S(1)}, u32[]{:S(2)}, u32[]{:S(2)}) collective-permute-start(bf16[2,32,1536]{2,1,0:T(8,128)(2,1)S(1)} %fusion.39), channel_id=1, source_target_pairs={{0,2},{1,3},{2,0},{3,1},{4,6},{5,7},{6,4},{7,5},{8,10},{9,11},{10,... | collective-permute-start | bytes 589832 | tf_op jit(solution)/shard_map/ppermute | solution.py:71
  62.8 5.4 %collective-permute-done.16 = bf16[2,32,1536]{2,1,0:T(8,128)(2,1)S(1)} collective-permute-done((bf16[2,32,1536]{2,1,0:T(8,128)(2,1)S(1)}, bf16[2,32,1536]{2,1,0:T(8,128)(2,1)S(1)}, u32[]{:S(2)}, u32[]{:S(2)}) %collective-permute-start.16) | collective-permute-done | bytes 196640 | tf_op jit(solution)/shard_map/ppermute | solution.py:71
  68.2 0.8 %fusion.45 = bf16[2,32,1536]{2,1,0:T(8,128)(2,1)} fusion(f32[2,32,1536]{2,1,0:T(8,128)S(1)} %get-tuple-element.8, bf16[2,32,1536]{2,1,0:T(8,128)(2,1)S(1)} %collective-permute-done.16, bf16[2,32,1536]{2,1,0:T(8,128)(2,1)S(1)} %collective-permute-done.14, bf16[2,2,2,32,1536]{4,3,2,1,0:T(8,128)(2,1)S(1)} %bitcast.148, s32[]{:T(128)S(6)} %select_n.121, ...), kind=kLoop, calls=%fused_computation.45 | loop fusion | flops 1179648 | bytes 1185864 | tf_op jit(solution)/shard_map/convert_element_type | solution.py:243
  (64 shorter events, 1.3 us)
Async XLA Ops:
  0.0 3.0 %copy-start = (bf16[3,1536,256]{2,1,0:T(8,128)(2,1)S(1)}, bf16[3,1536,256]{2,1,0:T(8,128)(2,1)}, u32[]{:S(2)}) copy-start(bf16[3,1536,256]{2,1,0:T(8,128)(2,1)} %param.15) | copy-start | bytes 7077892
  3.0 9.3 %copy-start.5 = (s32[2]{0:T(128)S(1)}, s32[2]{0:T(128)}, u32[]{:S(2)}) copy-start(s32[2]{0:T(128)} %param.13) | copy-start | bytes 28
  5.3 8.8 %collective-permute-start = (bf16[3,2,128,1,64]{2,4,1,3,0:T(8,128)(2,1)S(1)}, bf16[3,2,128,1,64]{2,4,1,3,0:T(8,128)(2,1)S(1)}, u32[]{:S(2)}, u32[]{:S(2)}) collective-permute-start(bf16[3,2,128,1,64]{2,4,1,3,0:T(8,128)(2,1)S(1)} %get-tuple-element.16), channel_id=1, source_target_pairs={{0,4},{4,8},{8,12},{12,0},{1,5},{5,9},{9,13},{13,1},{2,6},{6,10},{... | collective-permute-start | bytes 294920 | tf_op jit(solution)/shard_map/ppermute | solution.py:154
  8.4 9.2 %collective-permute-start.1 = (bf16[3,2,128,1,64]{2,4,1,3,0:T(8,128)(2,1)S(1)}, bf16[3,2,128,1,64]{2,4,1,3,0:T(8,128)(2,1)S(1)}, u32[]{:S(2)}, u32[]{:S(2)}) collective-permute-start(bf16[3,2,128,1,64]{2,4,1,3,0:T(8,128)(2,1)S(1)} %get-tuple-element.15), channel_id=1, source_target_pairs={{0,8},{4,12},{8,0},{12,4},{1,9},{5,13},{9,1},{13,5},{2,10},{6,14},... | collective-permute-start | bytes 294920 | tf_op jit(solution)/shard_map/ppermute | solution.py:154
  10.9 6.6 %collective-permute-start.2 = (bf16[3,2,128,1,64]{2,4,1,3,0:T(8,128)(2,1)S(1)}, bf16[3,2,128,1,64]{2,4,1,3,0:T(8,128)(2,1)S(1)}, u32[]{:S(2)}, u32[]{:S(2)}) collective-permute-start(bf16[3,2,128,1,64]{2,4,1,3,0:T(8,128)(2,1)S(1)} %get-tuple-element.14), channel_id=1, source_target_pairs={{0,12},{4,0},{8,4},{12,8},{1,13},{5,1},{9,5},{13,9},{2,14},{6,2},{... | collective-permute-start | bytes 294920 | tf_op jit(solution)/shard_map/ppermute | solution.py:154
  18.9 10.6 %copy-start.2 = (bf16[256,1536]{1,0:T(8,128)(2,1)S(1)}, bf16[256,1536]{1,0:T(8,128)(2,1)}, u32[]{:S(2)}) copy-start(bf16[256,1536]{1,0:T(8,128)(2,1)} %param.16) | copy-start | bytes 2359300
  19.6 5.2 %collective-permute-start.3 = (bf16[2,1,128,64]{2,3,0,1:T(8,128)(2,1)S(1)}, bf16[2,1,128,64]{2,3,0,1:T(8,128)(2,1)S(1)}, u32[]{:S(2)}, u32[]{:S(2)}) collective-permute-start(bf16[2,1,128,64]{2,3,0,1:T(8,128)(2,1)S(1)} %get-tuple-element.21), channel_id=1, source_target_pairs={{0,12},{4,0},{8,4},{12,8},{1,13},{5,1},{9,5},{13,9},{2,14},{6,2},{... | collective-permute-start | bytes 98312 | tf_op jit(solution)/shard_map/ppermute | solution.py:164
  23.3 5.0 %collective-permute-start.4 = (bf16[2,1,128,64]{2,3,0,1:T(8,128)(2,1)S(1)}, bf16[2,1,128,64]{2,3,0,1:T(8,128)(2,1)S(1)}, u32[]{:S(2)}, u32[]{:S(2)}) collective-permute-start(bf16[2,1,128,64]{2,3,0,1:T(8,128)(2,1)S(1)} %get-tuple-element.20), channel_id=1, source_target_pairs={{0,8},{4,12},{8,0},{12,4},{1,9},{5,13},{9,1},{13,5},{2,10},{6,14},... | collective-permute-start | bytes 98312 | tf_op jit(solution)/shard_map/ppermute | solution.py:164
  23.7 5.7 %collective-permute-start.5 = (bf16[2,1,128,64]{2,3,0,1:T(8,128)(2,1)S(1)}, bf16[2,1,128,64]{2,3,0,1:T(8,128)(2,1)S(1)}, u32[]{:S(2)}, u32[]{:S(2)}) collective-permute-start(bf16[2,1,128,64]{2,3,0,1:T(8,128)(2,1)S(1)} %get-tuple-element.19), channel_id=1, source_target_pairs={{0,4},{4,8},{8,12},{12,0},{1,5},{5,9},{9,13},{13,1},{2,6},{6,10},{... | collective-permute-start | bytes 98312 | tf_op jit(solution)/shard_map/ppermute | solution.py:164
  29.9 11.3 %copy-start.3 = (f32[1536]{0:T(1024)S(1)}, f32[1536]{0:T(1024)}, u32[]{:S(2)}) copy-start(f32[1536]{0:T(1024)} %param.17) | copy-start | bytes 18436
  30.0 1.6 %collective-permute-start.7 = (bf16[2,32,1536]{2,1,0:T(8,128)(2,1)S(1)}, bf16[2,32,1536]{2,1,0:T(8,128)(2,1)}, u32[]{:S(2)}, u32[]{:S(2)}) collective-permute-start(bf16[2,32,1536]{2,1,0:T(8,128)(2,1)S(1)} %get-tuple-element.12), channel_id=1, source_target_pairs={{0,1},{1,0},{2,3},{3,2},{4,5},{5,4},{6,7},{7,6},{8,9},{9,8},{10,11... | collective-permute-start | bytes 589832 | tf_op jit(solution)/shard_map/ppermute | solution.py:59
  30.0 4.1 %collective-permute-start.6 = (bf16[2,32,1536]{2,1,0:T(8,128)(2,1)S(1)}, bf16[2,32,1536]{2,1,0:T(8,128)(2,1)}, u32[]{:S(2)}, u32[]{:S(2)}) collective-permute-start(bf16[2,32,1536]{2,1,0:T(8,128)(2,1)S(1)} %get-tuple-element.11), channel_id=1, source_target_pairs={{0,1},{1,0},{2,3},{3,2},{4,5},{5,4},{6,7},{7,6},{8,9},{9,8},{10,11... | collective-permute-start | bytes 589832 | tf_op jit(solution)/shard_map/ppermute | solution.py:63
  32.6 7.1 %collective-permute-start.8 = (bf16[2,32,1536]{2,1,0:T(8,128)(2,1)S(1)}, bf16[2,32,1536]{2,1,0:T(8,128)(2,1)}, u32[]{:S(2)}, u32[]{:S(2)}) collective-permute-start(bf16[2,32,1536]{2,1,0:T(8,128)(2,1)S(1)} %fusion.46), channel_id=1, source_target_pairs={{0,2},{1,3},{2,0},{3,1},{4,6},{5,7},{6,4},{7,5},{8,10},{9,11},{10,... | collective-permute-start | bytes 589832 | tf_op jit(solution)/shard_map/ppermute | solution.py:71
  34.1 13.5 %copy-start.1 = (bf16[2,1536,384]{2,1,0:T(8,128)(2,1)S(1)}, bf16[2,1536,384]{2,1,0:T(8,128)(2,1)}, u32[]{:S(2)}) copy-start(bf16[2,1536,384]{2,1,0:T(8,128)(2,1)} %param.18) | copy-start | bytes 7077892
  41.4 6.2 %collective-permute-start.9 = (bf16[2,32,1536]{2,1,0:T(8,128)(2,1)S(1)}, bf16[2,32,1536]{2,1,0:T(8,128)(2,1)S(1)}, u32[]{:S(2)}, u32[]{:S(2)}) collective-permute-start(bf16[2,32,1536]{2,1,0:T(8,128)(2,1)S(1)} %get-tuple-element.6), channel_id=1, source_target_pairs={{0,2},{1,3},{2,0},{3,1},{4,6},{5,7},{6,4},{7,5},{8,10},{9,11},{10,... | collective-permute-start | bytes 589832 | tf_op jit(solution)/shard_map/ppermute | solution.py:98
  43.0 5.2 %collective-permute-start.10 = (bf16[2,32,1536]{2,1,0:T(8,128)(2,1)S(1)}, bf16[2,32,1536]{2,1,0:T(8,128)(2,1)S(1)}, u32[]{:S(2)}, u32[]{:S(2)}) collective-permute-start(bf16[2,32,1536]{2,1,0:T(8,128)(2,1)S(1)} %get-tuple-element.6), channel_id=1, source_target_pairs={{0,1},{1,0},{2,3},{3,2},{4,5},{5,4},{6,7},{7,6},{8,9},{9,8},{10,11... | collective-permute-start | bytes 589832 | tf_op jit(solution)/shard_map/ppermute | solution.py:95
  48.1 1.5 %collective-permute-start.11 = (bf16[2,32,1536]{2,1,0:T(8,128)(2,1)S(1)}, bf16[2,32,1536]{2,1,0:T(8,128)(2,1)S(1)}, u32[]{:S(2)}, u32[]{:S(2)}) collective-permute-start(bf16[2,32,1536]{2,1,0:T(8,128)(2,1)S(1)} %collective-permute-done.9), channel_id=1, source_target_pairs={{0,1},{1,0},{2,3},{3,2},{4,5},{5,4},{6,7},{7,6},{8,9},{9,8},{10,11... | collective-permute-start | bytes 589832 | tf_op jit(solution)/shard_map/ppermute | solution.py:99
  49.6 8.1 %copy-start.7 = (f32[31,384]{1,0:T(8,128)S(1)}, f32[31,384]{1,0:T(8,128)}, u32[]{:S(2)}) copy-start(f32[31,384]{1,0:T(8,128)} %param.19) | copy-start | bytes 142852
  50.7 2.8 %collective-permute-start.12 = (bf16[2,15,384]{2,0,1:T(2,128)(2,1)S(1)}, bf16[2,15,384]{2,0,1:T(2,128)(2,1)S(1)}, u32[]{:S(2)}, u32[]{:S(2)}) collective-permute-start(bf16[2,15,384]{2,0,1:T(2,128)(2,1)S(1)} %get-tuple-element.17), channel_id=1, source_target_pairs={{0,4},{4,8},{8,12},{1,5},{5,9},{9,13},{2,6},{6,10},{10,14},{3,7},{... | collective-permute-start | bytes 69128 | tf_op jit(solution)/shard_map/ppermute | solution.py:20
  52.0 5.7 %collective-permute-start.13 = (bf16[2,15,384]{2,0,1:T(2,128)(2,1)S(1)}, bf16[2,15,384]{2,0,1:T(2,128)(2,1)S(1)}, u32[]{:S(2)}, u32[]{:S(2)}) collective-permute-start(bf16[2,15,384]{2,0,1:T(2,128)(2,1)S(1)} %get-tuple-element.18), channel_id=1, source_target_pairs={{4,0},{8,4},{12,8},{5,1},{9,5},{13,9},{6,2},{10,6},{14,10},{7,3},{... | collective-permute-start | bytes 69128 | tf_op jit(solution)/shard_map/ppermute | solution.py:21
  57.7 1.3 %copy-start.6 = (bf16[384,1536]{1,0:T(8,128)(2,1)S(1)}, bf16[384,1536]{1,0:T(8,128)(2,1)}, u32[]{:S(2)}) copy-start(bf16[384,1536]{1,0:T(8,128)(2,1)} %param.22) | copy-start | bytes 3538948
  57.7 1.3 %copy-start.8 = (f32[384]{0:T(512)S(1)}, f32[384]{0:T(512)}, u32[]{:S(2)}) copy-start(f32[384]{0:T(512)} %param.21) | copy-start | bytes 4612
  57.7 1.3 %copy-start.9 = (f32[384]{0:T(512)S(1)}, f32[384]{0:T(512)}, u32[]{:S(2)}) copy-start(f32[384]{0:T(512)} %param.20) | copy-start | bytes 4612
  58.9 0.7 %copy-start.4 = (s32[1536]{0:T(1024)S(1)}, s32[1536]{0:T(1024)}, u32[]{:S(2)}) copy-start(s32[1536]{0:T(1024)} %param.23) | copy-start | bytes 18436
  59.6 1.5 %collective-permute-start.15 = (bf16[2,32,1536]{2,1,0:T(8,128)(2,1)S(1)}, bf16[2,32,1536]{2,1,0:T(8,128)(2,1)S(1)}, u32[]{:S(2)}, u32[]{:S(2)}) collective-permute-start(bf16[2,32,1536]{2,1,0:T(8,128)(2,1)S(1)} %get-tuple-element.10), channel_id=1, source_target_pairs={{0,1},{1,0},{2,3},{3,2},{4,5},{5,4},{6,7},{7,6},{8,9},{9,8},{10,11... | collective-permute-start | bytes 589832 | tf_op jit(solution)/shard_map/ppermute | solution.py:59
  59.7 3.1 %collective-permute-start.14 = (bf16[2,32,1536]{2,1,0:T(8,128)(2,1)S(1)}, bf16[2,32,1536]{2,1,0:T(8,128)(2,1)S(1)}, u32[]{:S(2)}, u32[]{:S(2)}) collective-permute-start(bf16[2,32,1536]{2,1,0:T(8,128)(2,1)S(1)} %get-tuple-element.9), channel_id=1, source_target_pairs={{0,1},{1,0},{2,3},{3,2},{4,5},{5,4},{6,7},{7,6},{8,9},{9,8},{10,11... | collective-permute-start | bytes 589832 | tf_op jit(solution)/shard_map/ppermute | solution.py:63
  61.2 7.0 %collective-permute-start.16 = (bf16[2,32,1536]{2,1,0:T(8,128)(2,1)S(1)}, bf16[2,32,1536]{2,1,0:T(8,128)(2,1)S(1)}, u32[]{:S(2)}, u32[]{:S(2)}) collective-permute-start(bf16[2,32,1536]{2,1,0:T(8,128)(2,1)S(1)} %fusion.39), channel_id=1, source_target_pairs={{0,2},{1,3},{2,0},{3,1},{4,6},{5,7},{6,4},{7,5},{8,10},{9,11},{10,... | collective-permute-start | bytes 589832 | tf_op jit(solution)/shard_map/ppermute | solution.py:71

commit v22 on v20

--- a/solution.py
+++ b/solution.py
@@ -56,19 +56,28 @@
         mine, onward = rank & 1, (rank >> 1) & 1
         keep = lax.dynamic_index_in_dim(acc, mine, dim + bits - 1, keepdims=False)
         send = lax.dynamic_index_in_dim(acc, 1 - mine, dim + bits - 1, keepdims=False)
-        got_far = lax.ppermute(
-            lax.dynamic_index_in_dim(send, 1 - onward, dim + bits - 2, keepdims=False),
-            axis, xor_pairs(count, 1),
-        )
+        send_far = lax.dynamic_index_in_dim(send, 1 - onward, dim + bits - 2, keepdims=False)
+        cut = send_far.shape[0] // 2 if send_far.shape[0] > 1 else send_far.shape[0]
+        got_far = [
+            lax.ppermute(piece, axis, xor_pairs(count, 1))
+            for piece in (send_far[:cut], send_far[cut:])
+            if piece.shape[0] > 0
+        ]
         got_near = lax.ppermute(
             lax.dynamic_index_in_dim(send, onward, dim + bits - 2, keepdims=False),
             axis, xor_pairs(count, 1),
         )
         far = lax.dynamic_index_in_dim(keep, 1 - onward, dim + bits - 2, keepdims=False)
-        far = far.astype(jnp.float32) + got_far.astype(jnp.float32)
+        far = jnp.concatenate(
+            [
+                (piece_keep.astype(jnp.float32) + piece_got.astype(jnp.float32)).astype(jnp.bfloat16)
+                for piece_keep, piece_got in zip((far[:cut], far[cut:]), got_far)
+            ],
+            axis=0,
+        )
         near = lax.dynamic_index_in_dim(keep, onward, dim + bits - 2, keepdims=False)
         near = near.astype(jnp.float32) + got_near.astype(jnp.float32)
-        got = lax.ppermute(far.astype(jnp.bfloat16), axis, xor_pairs(count, 2))
+        got = lax.ppermute(far, axis, xor_pairs(count, 2))
         acc = near + got.astype(jnp.float32)
         first = 2
     for b in range(first, bits):

time: 68.8 us -> 68.1 us (0.990)
  other arithmetic: 7.44 us -> 6.39 us
    ppermute x4 -> x6, starting transfers between devices: 3.26 us -> 4.27 us  [the longest x2 3.14 us: reduce_scatter_rows(): got = lax.ppermute(far, axis, xor_pairs(count, 2))]
    convert_element_type x2, other arithmetic: 1.03 us -> 0.11 us  [reduce_scatter_rows(): (piece_keep.astype(jnp.float32) + piece_got.astype(jnp.float32)).astype(j...]
    ppermute x4 -> x6, waiting for transfers between devices: 12.9 us -> 12.8 us  [the longest x2 11.2 us: reduce_scatter_rows(): got = lax.ppermute(far, axis, xor_pairs(count, 2))]
  transfers between devices with their start and end apart: 17 -> 19, of which waited for: 13 -> 15; matrix products, arithmetic and copies ran while one was open for 2% -> 1% of each run, Pallas kernels for 0% -> 0%
where the time goes in v22:
time: 68.1 us; the launch traced here: 67.9 us
  waiting for transfers between devices  33.8 us (50%)
  starting transfers between devices  20 us (29%)
  other arithmetic  6.39 us (9%)
  matrix products  6.25 us (9%)
  local copies, waits for them, and re-layouts  0.94 us (1%)
    ppermute x2, waiting for transfers between devices, reduce_scatter_rows(): got = lax.ppermute(far, axis, xor_pairs(count, 2))  11.2 us
    ppermute x3, starting transfers between devices, attend_by_heads(): pieces.append(lax.ppermute(send, axis, pairs))  7.01 us
    ppermute x3, waiting for transfers between devices, attend_by_heads(): back.append(lax.ppermute(rows, axis, pairs))  5.45 us
    ppermute x3, waiting for transfers between devices, attend_by_heads(): pieces.append(lax.ppermute(send, axis, pairs))  5.16 us
    ppermute x1, waiting for transfers between devices, all_gather_rows(): got = lax.ppermute(mine_acc, axis, xor_pairs(count, 1 << b))  4.78 us
    ppermute x3, starting transfers between devices, attend_by_heads(): back.append(lax.ppermute(rows, axis, pairs))  4.3 us
    ppermute x1, waiting for transfers between devices, with_halo(): after = lax.ppermute(initial, axis, down)  4.22 us
    ppermute x2, starting transfers between devices, reduce_scatter_rows(): got = lax.ppermute(far, axis, xor_pairs(count, 2))  3.14 us
  transfers between devices with their start and end apart: 19, of which 15 were waited for; matrix products, arithmetic and copies ran while one was open for 1% of the time, Pallas kernels for 0%

profile of v22, /device:TPU:0, one launch (start us, length us, event | category | flops | bytes accessed | tf_op | source)
XLA Modules:
  0.0 67.9 jit_solution(9788753699015335790)
XLA Ops:
  0.0 1.5 %convert_reduce_fusion = f32[2,128]{1,0:T(2,128)S(1)} fusion(bf16[2,128,1536]{2,1,0:T(8,128)(2,1)} %param.12), kind=kLoop, calls=%fused_computation.9 | loop fusion | flops 786176 | bytes 787456 | tf_op jit(solution)/shard_map/reduce_sum | solution.py:27
  1.5 1.5 %fusion.9 = f32[2,128]{1,0:T(2,128)S(1)} fusion(bf16[2,128,1536]{2,1,0:T(8,128)(2,1)} %param.12, f32[2,128]{1,0:T(2,128)S(1)} %broadcast_multiply_fusion.1), kind=kLoop, calls=%fused_computation.15 | loop fusion | flops 1572608 | bytes 788480 | tf_op jit(solution)/shard_map/reduce_sum | solution.py:29
  3.0 2.0 %fusion.18 = bf16[3,2,128,256]{3,2,0,1:T(8,128)(2,1)S(1)} fusion(bf16[3,1536,256]{2,1,0:T(8,128)(2,1)S(1)} %copy-done, bf16[2,128,1536]{2,1,0:T(8,128)(2,1)} %param.12, f32[1536]{0:T(1024)} %param.14, f32[2,128]{1,0:T(2,128)S(1)} %add_rsqrt_fusion.1, f32[2,128]{1,0:T(2,128)S(1)} %broadcast_multiply_fusion.1), kind=kOutput, calls=%fused_computation.20 | convolution fusion | flops 606142464 | bytes 3547136 | tf_op jit(solution)/shard_map/std,idc->istc/dot_general | solution.py:197
  5.0 0.2 copy.36
  5.3 3.1 %collective-permute-start = (bf16[3,2,128,1,64]{2,4,1,3,0:T(8,128)(2,1)S(1)}, bf16[3,2,128,1,64]{2,4,1,3,0:T(8,128)(2,1)S(1)}, u32[]{:S(2)}, u32[]{:S(2)}) collective-permute-start(bf16[3,2,128,1,64]{2,4,1,3,0:T(8,128)(2,1)S(1)} %get-tuple-element.20), channel_id=1, source_target_pairs={{0,4},{4,8},{8,12},{12,0},{1,5},{5,9},{9,13},{13,1},{2,6},{6,10},{... | collective-permute-start | bytes 294920 | tf_op jit(solution)/shard_map/ppermute | solution.py:161
  8.4 2.6 %collective-permute-start.1 = (bf16[3,2,128,1,64]{2,4,1,3,0:T(8,128)(2,1)S(1)}, bf16[3,2,128,1,64]{2,4,1,3,0:T(8,128)(2,1)S(1)}, u32[]{:S(2)}, u32[]{:S(2)}) collective-permute-start(bf16[3,2,128,1,64]{2,4,1,3,0:T(8,128)(2,1)S(1)} %get-tuple-element.19), channel_id=1, source_target_pairs={{0,8},{4,12},{8,0},{12,4},{1,9},{5,13},{9,1},{13,5},{2,10},{6,14},... | collective-permute-start | bytes 294920 | tf_op jit(solution)/shard_map/ppermute | solution.py:161
  10.9 1.3 %collective-permute-start.2 = (bf16[3,2,128,1,64]{2,4,1,3,0:T(8,128)(2,1)S(1)}, bf16[3,2,128,1,64]{2,4,1,3,0:T(8,128)(2,1)S(1)}, u32[]{:S(2)}, u32[]{:S(2)}) collective-permute-start(bf16[3,2,128,1,64]{2,4,1,3,0:T(8,128)(2,1)S(1)} %get-tuple-element.18), channel_id=1, source_target_pairs={{0,12},{4,0},{8,4},{12,8},{1,13},{5,1},{9,5},{13,9},{2,14},{6,2},{... | collective-permute-start | bytes 294920 | tf_op jit(solution)/shard_map/ppermute | solution.py:161
  12.3 0.1 broadcast_compare_fusion
  12.4 1.6 %collective-permute-done = bf16[3,2,128,1,64]{2,4,1,3,0:T(8,128)(2,1)S(1)} collective-permute-done((bf16[3,2,128,1,64]{2,4,1,3,0:T(8,128)(2,1)S(1)}, bf16[3,2,128,1,64]{2,4,1,3,0:T(8,128)(2,1)S(1)}, u32[]{:S(2)}, u32[]{:S(2)}) %collective-permute-start) | collective-permute-done | bytes 98336 | tf_op jit(solution)/shard_map/ppermute | solution.py:161
  14.0 3.5 %collective-permute-done.1 = bf16[3,2,128,1,64]{2,4,1,3,0:T(8,128)(2,1)S(1)} collective-permute-done((bf16[3,2,128,1,64]{2,4,1,3,0:T(8,128)(2,1)S(1)}, bf16[3,2,128,1,64]{2,4,1,3,0:T(8,128)(2,1)S(1)}, u32[]{:S(2)}, u32[]{:S(2)}) %collective-permute-start.1) | collective-permute-done | bytes 98336 | tf_op jit(solution)/shard_map/ppermute | solution.py:161
  17.6 0.8 %fusion.6 = (f32[2,512]{1,0:T(2,128)S(1)}, f32[2,512,512]{1,2,0:T(8,128)S(1)}) fusion(pred[2,512]{1,0:T(4,128)(4,1)S(1)} %broadcast_compare_fusion, bf16[3,2,512,1,64]{2,4,1,3,0:T(8,128)(2,1)S(1)} %pad_maximum_fusion), kind=kOutput, calls=%fused_computation.12 | convolution fusion | flops 68680704 | bytes 2365440 | tf_op jit(solution)/shard_map/sqhe,skhe->shqk/dot_general | solution.py:133
  18.4 0.5 fusion.7
  18.9 0.6 fusion.23
  19.6 3.6 %collective-permute-start.3 = (bf16[2,1,128,64]{2,3,0,1:T(8,128)(2,1)S(1)}, bf16[2,1,128,64]{2,3,0,1:T(8,128)(2,1)S(1)}, u32[]{:S(2)}, u32[]{:S(2)}) collective-permute-start(bf16[2,1,128,64]{2,3,0,1:T(8,128)(2,1)S(1)} %get-tuple-element.25), channel_id=1, source_target_pairs={{0,12},{4,0},{8,4},{12,8},{1,13},{5,1},{9,5},{13,9},{2,14},{6,2},{... | collective-permute-start | bytes 98312 | tf_op jit(solution)/shard_map/ppermute | solution.py:171
  23.3 0.4 collective-permute-start.4
  23.7 0.2 collective-permute-start.5
  23.9 0.9 %collective-permute-done.3 = bf16[2,1,128,64]{2,3,0,1:T(8,128)(2,1)S(1)} collective-permute-done((bf16[2,1,128,64]{2,3,0,1:T(8,128)(2,1)S(1)}, bf16[2,1,128,64]{2,3,0,1:T(8,128)(2,1)S(1)}, u32[]{:S(2)}, u32[]{:S(2)}) %collective-permute-start.3) | collective-permute-done | bytes 32800 | tf_op jit(solution)/shard_map/ppermute | solution.py:171
  24.9 3.4 %collective-permute-done.4 = bf16[2,1,128,64]{2,3,0,1:T(8,128)(2,1)S(1)} collective-permute-done((bf16[2,1,128,64]{2,3,0,1:T(8,128)(2,1)S(1)}, bf16[2,1,128,64]{2,3,0,1:T(8,128)(2,1)S(1)}, u32[]{:S(2)}, u32[]{:S(2)}) %collective-permute-start.4) | collective-permute-done | bytes 32800 | tf_op jit(solution)/shard_map/ppermute | solution.py:171
  28.2 1.2 %collective-permute-done.5 = bf16[2,1,128,64]{2,3,0,1:T(8,128)(2,1)S(1)} collective-permute-done((bf16[2,1,128,64]{2,3,0,1:T(8,128)(2,1)S(1)}, bf16[2,1,128,64]{2,3,0,1:T(8,128)(2,1)S(1)}, u32[]{:S(2)}, u32[]{:S(2)}) %collective-permute-start.5) | collective-permute-done | bytes 32800 | tf_op jit(solution)/shard_map/ppermute | solution.py:171
  29.5 0.4 convolution_convert_fusion
  30.0 0.5 collective-permute-start.8
  30.5 0.1 collective-permute-start.6
  30.7 0.6 collective-permute-done.7
  31.3 0.2 collective-permute-done.8
  31.6 1.6 %collective-permute-start.9 = (bf16[2,32,1536]{2,1,0:T(8,128)(2,1)S(1)}, bf16[2,32,1536]{2,1,0:T(8,128)(2,1)S(1)}, u32[]{:S(2)}, u32[]{:S(2)}) collective-permute-start(bf16[2,32,1536]{2,1,0:T(8,128)(2,1)S(1)} %pad_maximum_fusion.2), channel_id=1, source_target_pairs={{0,2},{1,3},{2,0},{3,1},{4,6},{5,7},{6,4},{7,5},{8,10},{9,11},{10,... | collective-permute-start | bytes 589832 | tf_op jit(solution)/shard_map/ppermute | solution.py:80
  33.1 5.6 %collective-permute-done.9 = bf16[2,32,1536]{2,1,0:T(8,128)(2,1)S(1)} collective-permute-done((bf16[2,32,1536]{2,1,0:T(8,128)(2,1)S(1)}, bf16[2,32,1536]{2,1,0:T(8,128)(2,1)S(1)}, u32[]{:S(2)}, u32[]{:S(2)}) %collective-permute-start.9) | collective-permute-done | bytes 196640 | tf_op jit(solution)/shard_map/ppermute | solution.py:80
  38.8 1.1 %fusion.65 = (f32[2,32]{1,0:T(2,128)S(1)}, f32[2,32,1536]{2,1,0:T(8,128)S(1)}) fusion(bf16[2,32,1536]{2,1,0:T(8,128)(2,1)S(1)} %collective-permute-done.9, bf16[2,32,1536]{2,1,0:T(8,128)(2,1)S(1)} %collective-permute-done.6, bf16[2,2,2,32,1536]{4,3,2,1,0:T(8,128)(2,1)S(1)} %bitcast.139, s32[]{:T(128)S(6)} %select_n.121, s32[]{:T(128)S(6)} %select_n.123, ...), kind=kLoop, calls=%fused_computation.125 | loop fusion | flops 786368 | bytes 1179916 | tf_op jit(solution)/shard_map/reduce_sum | solution.py:27
  39.9 0.2 multiply_reduce_fusion
  40.2 0.1 bitcast_dynamic-update-slice_fusion.3
  40.3 1.6 %collective-permute-start.10 = (bf16[2,32,1536]{2,1,0:T(8,128)(2,1)S(1)}, bf16[2,32,1536]{2,1,0:T(8,128)(2,1)S(1)}, u32[]{:S(2)}, u32[]{:S(2)}) collective-permute-start(bf16[2,32,1536]{2,1,0:T(8,128)(2,1)S(1)} %get-tuple-element.6), channel_id=1, source_target_pairs={{0,2},{1,3},{2,0},{3,1},{4,6},{5,7},{6,4},{7,5},{8,10},{9,11},{10,... | collective-permute-start | bytes 589832 | tf_op jit(solution)/shard_map/ppermute | solution.py:107
  42.0 4.8 %collective-permute-done.10 = bf16[2,32,1536]{2,1,0:T(8,128)(2,1)S(1)} collective-permute-done((bf16[2,32,1536]{2,1,0:T(8,128)(2,1)S(1)}, bf16[2,32,1536]{2,1,0:T(8,128)(2,1)S(1)}, u32[]{:S(2)}, u32[]{:S(2)}) %collective-permute-start.10) | collective-permute-done | bytes 196640 | tf_op jit(solution)/shard_map/ppermute | solution.py:107
  47.0 1.2 %collective-permute-done.12 = bf16[2,32,1536]{2,1,0:T(8,128)(2,1)S(1)} collective-permute-done((bf16[2,32,1536]{2,1,0:T(8,128)(2,1)S(1)}, bf16[2,32,1536]{2,1,0:T(8,128)(2,1)S(1)}, u32[]{:S(2)}, u32[]{:S(2)}) %collective-permute-start.12) | collective-permute-done | bytes 196640 | tf_op jit(solution)/shard_map/ppermute | solution.py:108
  48.3 0.8 %fusion.12 = f32[2,2,128,384]{3,2,0,1:T(8,128)S(1)} fusion(bf16[2,128,1536,1]{2,1,3,0:T(8,128)(2,1)S(1)} %bitcast.145, bf16[2,1536,384]{2,1,0:T(8,128)(2,1)S(1)} %copy-done.5), kind=kOutput, calls=%fused_computation.18 | convolution fusion | flops 603979776 | bytes 3932160 | tf_op jit(solution)/shard_map/std,gdc->gstc/dot_general | solution.py:34
  49.1 0.1 bitcast_select_fusion
  49.2 1.3 %collective-permute-start.13 = (bf16[2,15,384]{2,1,0:T(8,128)(2,1)S(1)}, bf16[2,15,384]{2,1,0:T(8,128)(2,1)S(1)}, u32[]{:S(2)}, u32[]{:S(2)}) collective-permute-start(bf16[2,15,384]{2,1,0:T(8,128)(2,1)S(1)} %get-tuple-element.21), channel_id=1, source_target_pairs={{0,4},{4,8},{8,12},{1,5},{5,9},{9,13},{2,6},{6,10},{10,14},{3,7},{... | collective-permute-start | bytes 69128 | tf_op jit(solution)/shard_map/ppermute | solution.py:20
  50.5 1.3 %collective-permute-start.14 = (bf16[2,15,384]{2,1,0:T(8,128)(2,1)S(1)}, bf16[2,15,384]{2,1,0:T(8,128)(2,1)S(1)}, u32[]{:S(2)}, u32[]{:S(2)}) collective-permute-start(bf16[2,15,384]{2,1,0:T(8,128)(2,1)S(1)} %get-tuple-element.22), channel_id=1, source_target_pairs={{4,0},{8,4},{12,8},{5,1},{9,5},{13,9},{6,2},{10,6},{14,10},{7,3},{... | collective-permute-start | bytes 69128 | tf_op jit(solution)/shard_map/ppermute | solution.py:21
  51.8 0.2 collective-permute-done.13
  52.0 4.2 %collective-permute-done.14 = bf16[2,15,384]{2,1,0:T(8,128)(2,1)S(1)} collective-permute-done((bf16[2,15,384]{2,1,0:T(8,128)(2,1)S(1)}, bf16[2,15,384]{2,1,0:T(8,128)(2,1)S(1)}, u32[]{:S(2)}, u32[]{:S(2)}) %collective-permute-start.14) | collective-permute-done | bytes 23072 | tf_op jit(solution)/shard_map/ppermute | solution.py:21
  56.4 1.1 %fusion.48 = f32[2,128,384]{2,0,1:T(2,128)S(1)} fusion(bf16[2,158,384]{2,1,0:T(8,128)(2,1)S(1)} %pad_maximum_fusion.1, f32[31,1,384]{2,0,1:T(8,128)S(1)} %bitcast.147), kind=kOutput, calls=%fused_computation.56 | convolution fusion | flops 36569088 | bytes 683520 | tf_op jit(solution)/shard_map/conv_general_dilated | solution.py:229
  57.4 0.2 copy-done.6
  57.6 0.6 convolution_convert_fusion.1
  58.3 0.5 collective-permute-start.17
  58.8 0.1 collective-permute-start.15
  59.0 0.6 collective-permute-done.16
  59.6 0.2 collective-permute-done.17
  59.9 1.6 %collective-permute-start.18 = (bf16[2,32,1536]{2,1,0:T(8,128)(2,1)S(1)}, bf16[2,32,1536]{2,1,0:T(8,128)(2,1)S(1)}, u32[]{:S(2)}, u32[]{:S(2)}) collective-permute-start(bf16[2,32,1536]{2,1,0:T(8,128)(2,1)S(1)} %pad_maximum_fusion.3), channel_id=1, source_target_pairs={{0,2},{1,3},{2,0},{3,1},{4,6},{5,7},{6,4},{7,5},{8,10},{9,11},{10,... | collective-permute-start | bytes 589832 | tf_op jit(solution)/shard_map/ppermute | solution.py:80
  61.5 5.6 %collective-permute-done.18 = bf16[2,32,1536]{2,1,0:T(8,128)(2,1)S(1)} collective-permute-done((bf16[2,32,1536]{2,1,0:T(8,128)(2,1)S(1)}, bf16[2,32,1536]{2,1,0:T(8,128)(2,1)S(1)}, u32[]{:S(2)}, u32[]{:S(2)}) %collective-permute-start.18) | collective-permute-done | bytes 196640 | tf_op jit(solution)/shard_map/ppermute | solution.py:80
  67.1 0.8 %fusion.43 = bf16[2,32,1536]{2,1,0:T(8,128)(2,1)} fusion(f32[2,32,1536]{2,1,0:T(8,128)S(1)} %get-tuple-element.8, bf16[2,32,1536]{2,1,0:T(8,128)(2,1)S(1)} %collective-permute-done.18, bf16[2,32,1536]{2,1,0:T(8,128)(2,1)S(1)} %collective-permute-done.15, bf16[2,2,2,32,1536]{4,3,2,1,0:T(8,128)(2,1)S(1)} %bitcast.144, s32[]{:T(128)S(6)} %select_n.121, ...), kind=kLoop, calls=%fused_computation.45 | loop fusion | flops 1179648 | bytes 1185864 | tf_op jit(solution)/shard_map/convert_element_type | solution.py:246
  (70 shorter events, 1.2 us)
Async XLA Ops:
  0.0 3.0 %copy-start = (bf16[3,1536,256]{2,1,0:T(8,128)(2,1)S(1)}, bf16[3,1536,256]{2,1,0:T(8,128)(2,1)}, u32[]{:S(2)}) copy-start(bf16[3,1536,256]{2,1,0:T(8,128)(2,1)} %param.15) | copy-start | bytes 7077892
  3.0 9.3 %copy-start.4 = (s32[2]{0:T(128)S(1)}, s32[2]{0:T(128)}, u32[]{:S(2)}) copy-start(s32[2]{0:T(128)} %param.13) | copy-start | bytes 28
  5.3 8.8 %collective-permute-start = (bf16[3,2,128,1,64]{2,4,1,3,0:T(8,128)(2,1)S(1)}, bf16[3,2,128,1,64]{2,4,1,3,0:T(8,128)(2,1)S(1)}, u32[]{:S(2)}, u32[]{:S(2)}) collective-permute-start(bf16[3,2,128,1,64]{2,4,1,3,0:T(8,128)(2,1)S(1)} %get-tuple-element.20), channel_id=1, source_target_pairs={{0,4},{4,8},{8,12},{12,0},{1,5},{5,9},{9,13},{13,1},{2,6},{6,10},{... | collective-permute-start | bytes 294920 | tf_op jit(solution)/shard_map/ppermute | solution.py:161
  8.4 9.2 %collective-permute-start.1 = (bf16[3,2,128,1,64]{2,4,1,3,0:T(8,128)(2,1)S(1)}, bf16[3,2,128,1,64]{2,4,1,3,0:T(8,128)(2,1)S(1)}, u32[]{:S(2)}, u32[]{:S(2)}) collective-permute-start(bf16[3,2,128,1,64]{2,4,1,3,0:T(8,128)(2,1)S(1)} %get-tuple-element.19), channel_id=1, source_target_pairs={{0,8},{4,12},{8,0},{12,4},{1,9},{5,13},{9,1},{13,5},{2,10},{6,14},... | collective-permute-start | bytes 294920 | tf_op jit(solution)/shard_map/ppermute | solution.py:161
  10.9 6.6 %collective-permute-start.2 = (bf16[3,2,128,1,64]{2,4,1,3,0:T(8,128)(2,1)S(1)}, bf16[3,2,128,1,64]{2,4,1,3,0:T(8,128)(2,1)S(1)}, u32[]{:S(2)}, u32[]{:S(2)}) collective-permute-start(bf16[3,2,128,1,64]{2,4,1,3,0:T(8,128)(2,1)S(1)} %get-tuple-element.18), channel_id=1, source_target_pairs={{0,12},{4,0},{8,4},{12,8},{1,13},{5,1},{9,5},{13,9},{2,14},{6,2},{... | collective-permute-start | bytes 294920 | tf_op jit(solution)/shard_map/ppermute | solution.py:161
  18.9 10.6 %copy-start.1 = (bf16[256,1536]{1,0:T(8,128)(2,1)S(1)}, bf16[256,1536]{1,0:T(8,128)(2,1)}, u32[]{:S(2)}) copy-start(bf16[256,1536]{1,0:T(8,128)(2,1)} %param.16) | copy-start | bytes 2359300
  19.6 5.2 %collective-permute-start.3 = (bf16[2,1,128,64]{2,3,0,1:T(8,128)(2,1)S(1)}, bf16[2,1,128,64]{2,3,0,1:T(8,128)(2,1)S(1)}, u32[]{:S(2)}, u32[]{:S(2)}) collective-permute-start(bf16[2,1,128,64]{2,3,0,1:T(8,128)(2,1)S(1)} %get-tuple-element.25), channel_id=1, source_target_pairs={{0,12},{4,0},{8,4},{12,8},{1,13},{5,1},{9,5},{13,9},{2,14},{6,2},{... | collective-permute-start | bytes 98312 | tf_op jit(solution)/shard_map/ppermute | solution.py:171
  23.3 5.0 %collective-permute-start.4 = (bf16[2,1,128,64]{2,3,0,1:T(8,128)(2,1)S(1)}, bf16[2,1,128,64]{2,3,0,1:T(8,128)(2,1)S(1)}, u32[]{:S(2)}, u32[]{:S(2)}) collective-permute-start(bf16[2,1,128,64]{2,3,0,1:T(8,128)(2,1)S(1)} %get-tuple-element.24), channel_id=1, source_target_pairs={{0,8},{4,12},{8,0},{12,4},{1,9},{5,13},{9,1},{13,5},{2,10},{6,14},... | collective-permute-start | bytes 98312 | tf_op jit(solution)/shard_map/ppermute | solution.py:171
  23.7 5.7 %collective-permute-start.5 = (bf16[2,1,128,64]{2,3,0,1:T(8,128)(2,1)S(1)}, bf16[2,1,128,64]{2,3,0,1:T(8,128)(2,1)S(1)}, u32[]{:S(2)}, u32[]{:S(2)}) collective-permute-start(bf16[2,1,128,64]{2,3,0,1:T(8,128)(2,1)S(1)} %get-tuple-element.23), channel_id=1, source_target_pairs={{0,4},{4,8},{8,12},{12,0},{1,5},{5,9},{9,13},{13,1},{2,6},{6,10},{... | collective-permute-start | bytes 98312 | tf_op jit(solution)/shard_map/ppermute | solution.py:171
  29.4 3.7 %copy-start.3 = (s32[1536]{0:T(1024)S(1)}, s32[1536]{0:T(1024)}, u32[]{:S(2)}) copy-start(s32[1536]{0:T(1024)} %param.23) | copy-start | bytes 18436
  29.9 10.3 %copy-start.2 = (f32[1536]{0:T(1024)S(1)}, f32[1536]{0:T(1024)}, u32[]{:S(2)}) copy-start(f32[1536]{0:T(1024)} %param.17) | copy-start | bytes 18436
  30.0 1.4 %collective-permute-start.7 = (bf16[1,32,1536]{2,1,0:T(8,128)(2,1)S(1)}, bf16[1,32,1536]{2,1,0:T(8,128)(2,1)S(1)}, u32[]{:S(2)}, u32[]{:S(2)}) collective-permute-start(bf16[1,32,1536]{2,1,0:T(8,128)(2,1)S(1)} %get-tuple-element.15), channel_id=1, source_target_pairs={{0,1},{1,0},{2,3},{3,2},{4,5},{5,4},{6,7},{7,6},{8,9},{9,8},{10,11... | collective-permute-start | bytes 294920 | tf_op jit(solution)/shard_map/ppermute | solution.py:62
  30.0 1.4 %collective-permute-start.8 = (bf16[1,32,1536]{2,1,0:T(8,128)(2,1)S(1)}, bf16[1,32,1536]{2,1,0:T(8,128)(2,1)S(1)}, u32[]{:S(2)}, u32[]{:S(2)}) collective-permute-start(bf16[1,32,1536]{2,1,0:T(8,128)(2,1)S(1)} %get-tuple-element.16), channel_id=1, source_target_pairs={{0,1},{1,0},{2,3},{3,2},{4,5},{5,4},{6,7},{7,6},{8,9},{9,8},{10,11... | collective-permute-start | bytes 294920 | tf_op jit(solution)/shard_map/ppermute | solution.py:62
  30.5 2.6 %collective-permute-start.6 = (bf16[2,32,1536]{2,1,0:T(8,128)(2,1)S(1)}, bf16[2,32,1536]{2,1,0:T(8,128)(2,1)S(1)}, u32[]{:S(2)}, u32[]{:S(2)}) collective-permute-start(bf16[2,32,1536]{2,1,0:T(8,128)(2,1)S(1)} %dynamic-slice_bitcast_fusion.1), channel_id=1, source_target_pairs={{0,1},{1,0},{2,3},{3,2},{4,5},{5,4},{6,7},{7,6},{8,9},{9,8},{10,11... | collective-permute-start | bytes 589832 | tf_op jit(solution)/shard_map/ppermute | solution.py:66
  31.6 7.2 %collective-permute-start.9 = (bf16[2,32,1536]{2,1,0:T(8,128)(2,1)S(1)}, bf16[2,32,1536]{2,1,0:T(8,128)(2,1)S(1)}, u32[]{:S(2)}, u32[]{:S(2)}) collective-permute-start(bf16[2,32,1536]{2,1,0:T(8,128)(2,1)S(1)} %pad_maximum_fusion.2), channel_id=1, source_target_pairs={{0,2},{1,3},{2,0},{3,1},{4,6},{5,7},{6,4},{7,5},{8,10},{9,11},{10,... | collective-permute-start | bytes 589832 | tf_op jit(solution)/shard_map/ppermute | solution.py:80
  40.3 7.9 %copy-start.5 = (bf16[2,1536,384]{2,1,0:T(8,128)(2,1)S(1)}, bf16[2,1536,384]{2,1,0:T(8,128)(2,1)}, u32[]{:S(2)}) copy-start(bf16[2,1536,384]{2,1,0:T(8,128)(2,1)} %param.18) | copy-start | bytes 7077892
  40.3 6.4 %collective-permute-start.10 = (bf16[2,32,1536]{2,1,0:T(8,128)(2,1)S(1)}, bf16[2,32,1536]{2,1,0:T(8,128)(2,1)S(1)}, u32[]{:S(2)}, u32[]{:S(2)}) collective-permute-start(bf16[2,32,1536]{2,1,0:T(8,128)(2,1)S(1)} %get-tuple-element.6), channel_id=1, source_target_pairs={{0,2},{1,3},{2,0},{3,1},{4,6},{5,7},{6,4},{7,5},{8,10},{9,11},{10,... | collective-permute-start | bytes 589832 | tf_op jit(solution)/shard_map/ppermute | solution.py:107
  42.0 4.8 %collective-permute-start.11 = (bf16[2,32,1536]{2,1,0:T(8,128)(2,1)S(1)}, bf16[2,32,1536]{2,1,0:T(8,128)(2,1)S(1)}, u32[]{:S(2)}, u32[]{:S(2)}) collective-permute-start(bf16[2,32,1536]{2,1,0:T(8,128)(2,1)S(1)} %get-tuple-element.6), channel_id=1, source_target_pairs={{0,1},{1,0},{2,3},{3,2},{4,5},{5,4},{6,7},{7,6},{8,9},{9,8},{10,11... | collective-permute-start | bytes 589832 | tf_op jit(solution)/shard_map/ppermute | solution.py:104
  46.7 1.4 %collective-permute-start.12 = (bf16[2,32,1536]{2,1,0:T(8,128)(2,1)S(1)}, bf16[2,32,1536]{2,1,0:T(8,128)(2,1)S(1)}, u32[]{:S(2)}, u32[]{:S(2)}) collective-permute-start(bf16[2,32,1536]{2,1,0:T(8,128)(2,1)S(1)} %collective-permute-done.10), channel_id=1, source_target_pairs={{0,1},{1,0},{2,3},{3,2},{4,5},{5,4},{6,7},{7,6},{8,9},{9,8},{10,11... | collective-permute-start | bytes 589832 | tf_op jit(solution)/shard_map/ppermute | solution.py:108
  48.3 8.1 %copy-start.7 = (f32[31,384]{1,0:T(8,128)S(1)}, f32[31,384]{1,0:T(8,128)}, u32[]{:S(2)}) copy-start(f32[31,384]{1,0:T(8,128)} %param.19) | copy-start | bytes 142852
  49.2 2.8 %collective-permute-start.13 = (bf16[2,15,384]{2,1,0:T(8,128)(2,1)S(1)}, bf16[2,15,384]{2,1,0:T(8,128)(2,1)S(1)}, u32[]{:S(2)}, u32[]{:S(2)}) collective-permute-start(bf16[2,15,384]{2,1,0:T(8,128)(2,1)S(1)} %get-tuple-element.21), channel_id=1, source_target_pairs={{0,4},{4,8},{8,12},{1,5},{5,9},{9,13},{2,6},{6,10},{10,14},{3,7},{... | collective-permute-start | bytes 69128 | tf_op jit(solution)/shard_map/ppermute | solution.py:20
  50.5 5.7 %collective-permute-start.14 = (bf16[2,15,384]{2,1,0:T(8,128)(2,1)S(1)}, bf16[2,15,384]{2,1,0:T(8,128)(2,1)S(1)}, u32[]{:S(2)}, u32[]{:S(2)}) collective-permute-start(bf16[2,15,384]{2,1,0:T(8,128)(2,1)S(1)} %get-tuple-element.22), channel_id=1, source_target_pairs={{4,0},{8,4},{12,8},{5,1},{9,5},{13,9},{6,2},{10,6},{14,10},{7,3},{... | collective-permute-start | bytes 69128 | tf_op jit(solution)/shard_map/ppermute | solution.py:21
  56.3 1.3 %copy-start.6 = (bf16[384,1536]{1,0:T(8,128)(2,1)S(1)}, bf16[384,1536]{1,0:T(8,128)(2,1)}, u32[]{:S(2)}) copy-start(bf16[384,1536]{1,0:T(8,128)(2,1)} %param.22) | copy-start | bytes 3538948
  56.3 1.3 %copy-start.8 = (f32[384]{0:T(512)S(1)}, f32[384]{0:T(512)}, u32[]{:S(2)}) copy-start(f32[384]{0:T(512)} %param.21) | copy-start | bytes 4612
  56.4 1.3 %copy-start.9 = (f32[384]{0:T(512)S(1)}, f32[384]{0:T(512)}, u32[]{:S(2)}) copy-start(f32[384]{0:T(512)} %param.20) | copy-start | bytes 4612
  58.2 1.4 %collective-permute-start.16 = (bf16[1,32,1536]{2,1,0:T(8,128)(2,1)S(1)}, bf16[1,32,1536]{2,1,0:T(8,128)(2,1)S(1)}, u32[]{:S(2)}, u32[]{:S(2)}) collective-permute-start(bf16[1,32,1536]{2,1,0:T(8,128)(2,1)S(1)} %get-tuple-element.11), channel_id=1, source_target_pairs={{0,1},{1,0},{2,3},{3,2},{4,5},{5,4},{6,7},{7,6},{8,9},{9,8},{10,11... | collective-permute-start | bytes 294920 | tf_op jit(solution)/shard_map/ppermute | solution.py:62
  58.3 1.4 %collective-permute-start.17 = (bf16[1,32,1536]{2,1,0:T(8,128)(2,1)S(1)}, bf16[1,32,1536]{2,1,0:T(8,128)(2,1)S(1)}, u32[]{:S(2)}, u32[]{:S(2)}) collective-permute-start(bf16[1,32,1536]{2,1,0:T(8,128)(2,1)S(1)} %get-tuple-element.12), channel_id=1, source_target_pairs={{0,1},{1,0},{2,3},{3,2},{4,5},{5,4},{6,7},{7,6},{8,9},{9,8},{10,11... | collective-permute-start | bytes 294920 | tf_op jit(solution)/shard_map/ppermute | solution.py:62
  58.8 2.7 %collective-permute-start.15 = (bf16[2,32,1536]{2,1,0:T(8,128)(2,1)S(1)}, bf16[2,32,1536]{2,1,0:T(8,128)(2,1)S(1)}, u32[]{:S(2)}, u32[]{:S(2)}) collective-permute-start(bf16[2,32,1536]{2,1,0:T(8,128)(2,1)S(1)} %dynamic-slice_bitcast_fusion), channel_id=1, source_target_pairs={{0,1},{1,0},{2,3},{3,2},{4,5},{5,4},{6,7},{7,6},{8,9},{9,8},{10,11... | collective-permute-start | bytes 589832 | tf_op jit(solution)/shard_map/ppermute | solution.py:66
  59.9 7.2 %collective-permute-start.18 = (bf16[2,32,1536]{2,1,0:T(8,128)(2,1)S(1)}, bf16[2,32,1536]{2,1,0:T(8,128)(2,1)S(1)}, u32[]{:S(2)}, u32[]{:S(2)}) collective-permute-start(bf16[2,32,1536]{2,1,0:T(8,128)(2,1)S(1)} %pad_maximum_fusion.3), channel_id=1, source_target_pairs={{0,2},{1,3},{2,0},{3,1},{4,6},{5,7},{6,4},{7,5},{8,10},{9,11},{10,... | collective-permute-start | bytes 589832 | tf_op jit(solution)/shard_map/ppermute | solution.py:80

commit v23 on v20

--- a/solution.py
+++ b/solution.py
@@ -56,19 +56,33 @@
         mine, onward = rank & 1, (rank >> 1) & 1
         keep = lax.dynamic_index_in_dim(acc, mine, dim + bits - 1, keepdims=False)
         send = lax.dynamic_index_in_dim(acc, 1 - mine, dim + bits - 1, keepdims=False)
-        got_far = lax.ppermute(
-            lax.dynamic_index_in_dim(send, 1 - onward, dim + bits - 2, keepdims=False),
-            axis, xor_pairs(count, 1),
-        )
+        send_far = lax.dynamic_index_in_dim(send, 1 - onward, dim + bits - 2, keepdims=False)
+        rows = send_far.shape[dim]
+        spans = [
+            (r, r + 1, h, h + rows // 2)
+            for r in range(send_far.shape[0])
+            for h in (0, rows // 2)
+        ] if rows % 2 == 0 and send_far.shape[0] <= 2 else [(0, send_far.shape[0], 0, rows)]
+        got_far = [
+            lax.ppermute(send_far[a:b, c:d], axis, xor_pairs(count, 1)) for a, b, c, d in spans
+        ]
+        far = lax.dynamic_index_in_dim(keep, 1 - onward, dim + bits - 2, keepdims=False)
+        summed = [
+            (far[a:b, c:d].astype(jnp.float32) + piece.astype(jnp.float32)).astype(jnp.bfloat16)
+            for (a, b, c, d), piece in zip(spans, got_far)
+        ]
+        if len(spans) > 1:
+            halves = [jnp.concatenate(summed[i : i + 2], axis=dim) for i in range(0, len(summed), 2)]
+            far = jnp.concatenate(halves, axis=0)
+        else:
+            far = summed[0]
         got_near = lax.ppermute(
             lax.dynamic_index_in_dim(send, onward, dim + bits - 2, keepdims=False),
             axis, xor_pairs(count, 1),
         )
-        far = lax.dynamic_index_in_dim(keep, 1 - onward, dim + bits - 2, keepdims=False)
-        far = far.astype(jnp.float32) + got_far.astype(jnp.float32)
         near = lax.dynamic_index_in_dim(keep, onward, dim + bits - 2, keepdims=False)
         near = near.astype(jnp.float32) + got_near.astype(jnp.float32)
-        got = lax.ppermute(far.astype(jnp.bfloat16), axis, xor_pairs(count, 2))
+        got = lax.ppermute(far, axis, xor_pairs(count, 2))
         acc = near + got.astype(jnp.float32)
         first = 2
     for b in range(first, bits):

time: 68.8 us -> 70 us (1.017)
  starting transfers between devices: 19.7 us -> 20.9 us
  other arithmetic: 7.44 us -> 6.54 us
  local copies, waits for them, and re-layouts: 0.94 us -> 1.68 us
    ppermute x4 -> x10, starting transfers between devices: 3.26 us -> 5.27 us  [the longest x2 3.12 us: reduce_scatter_rows(): got = lax.ppermute(far, axis, xor_pairs(count, 2))]
    convert_element_type x2, other arithmetic: 1.03 us -> 0.1 us  [reduce_scatter_rows(): (far[a:b, c:d].astype(jnp.float32) + piece.astype(jnp.float32)).astype(jn...]
    ppermute x2, starting transfers between devices: 0.97 us -> 0.16 us  [reduce_scatter_rows(): lax.ppermute(lax.dynamic_index_in_dim(send, onward, dim + bits - 2, keepd...]
    squeeze x2, local copies, waits for them, and re-layouts: 0.08 us -> 0.79 us  [reduce_scatter_rows(): lax.dynamic_index_in_dim(send, onward, dim + bits - 2, keepdims=False)]
    ppermute x4 -> x10, waiting for transfers between devices: 12.9 us -> 12.9 us  [the longest x2 11.4 us: reduce_scatter_rows(): got = lax.ppermute(far, axis, xor_pairs(count, 2))]
  transfers between devices with their start and end apart: 17 -> 23, of which waited for: 13 -> 19; matrix products, arithmetic and copies ran while one was open for 2% -> 1% of each run, Pallas kernels for 0% -> 0%
where the time goes in v23:
time: 70 us; the launch traced here: 69.8 us
  waiting for transfers between devices  34 us (49%)
  starting transfers between devices  20.9 us (30%)
  other arithmetic  6.54 us (9%)
  matrix products  6.24 us (9%)
  local copies, waits for them, and re-layouts  1.68 us (2%)
    ppermute x2, waiting for transfers between devices, reduce_scatter_rows(): got = lax.ppermute(far, axis, xor_pairs(count, 2))  11.4 us
    ppermute x3, starting transfers between devices, attend_by_heads(): pieces.append(lax.ppermute(send, axis, pairs))  7.01 us
    ppermute x3, waiting for transfers between devices, attend_by_heads(): back.append(lax.ppermute(rows, axis, pairs))  5.45 us
    ppermute x3, waiting for transfers between devices, attend_by_heads(): pieces.append(lax.ppermute(send, axis, pairs))  5.16 us
    ppermute x1, waiting for transfers between devices, all_gather_rows(): got = lax.ppermute(mine_acc, axis, xor_pairs(count, 1 << b))  4.78 us
    ppermute x3, starting transfers between devices, attend_by_heads(): back.append(lax.ppermute(rows, axis, pairs))  4.3 us
    ppermute x1, waiting for transfers between devices, with_halo(): after = lax.ppermute(initial, axis, down)  4.22 us
    ppermute x2, starting transfers between devices, reduce_scatter_rows(): got = lax.ppermute(far, axis, xor_pairs(count, 2))  3.12 us
  transfers between devices with their start and end apart: 23, of which 19 were waited for; matrix products, arithmetic and copies ran while one was open for 1% of the time, Pallas kernels for 0%

profile of v23, /device:TPU:0, one launch (start us, length us, event | category | flops | bytes accessed | tf_op | source)
XLA Modules:
  0.0 69.8 jit_solution(13667338425548521153)
XLA Ops:
  0.0 1.5 %convert_reduce_fusion = f32[2,128]{1,0:T(2,128)S(1)} fusion(bf16[2,128,1536]{2,1,0:T(8,128)(2,1)} %param.12), kind=kLoop, calls=%fused_computation.9 | loop fusion | flops 786176 | bytes 787456 | tf_op jit(solution)/shard_map/reduce_sum | solution.py:27
  1.5 1.5 %fusion.9 = f32[2,128]{1,0:T(2,128)S(1)} fusion(bf16[2,128,1536]{2,1,0:T(8,128)(2,1)} %param.12, f32[2,128]{1,0:T(2,128)S(1)} %broadcast_multiply_fusion.1), kind=kLoop, calls=%fused_computation.15 | loop fusion | flops 1572608 | bytes 788480 | tf_op jit(solution)/shard_map/reduce_sum | solution.py:29
  3.0 2.0 %fusion.18 = bf16[3,2,128,256]{3,2,0,1:T(8,128)(2,1)S(1)} fusion(bf16[3,1536,256]{2,1,0:T(8,128)(2,1)S(1)} %copy-done, bf16[2,128,1536]{2,1,0:T(8,128)(2,1)} %param.12, f32[1536]{0:T(1024)} %param.14, f32[2,128]{1,0:T(2,128)S(1)} %add_rsqrt_fusion.1, f32[2,128]{1,0:T(2,128)S(1)} %broadcast_multiply_fusion.1), kind=kOutput, calls=%fused_computation.20 | convolution fusion | flops 606142464 | bytes 3547136 | tf_op jit(solution)/shard_map/std,idc->istc/dot_general | solution.py:202
  5.0 0.2 copy.40
  5.3 3.1 %collective-permute-start = (bf16[3,2,128,1,64]{2,4,1,3,0:T(8,128)(2,1)S(1)}, bf16[3,2,128,1,64]{2,4,1,3,0:T(8,128)(2,1)S(1)}, u32[]{:S(2)}, u32[]{:S(2)}) collective-permute-start(bf16[3,2,128,1,64]{2,4,1,3,0:T(8,128)(2,1)S(1)} %get-tuple-element.18), channel_id=1, source_target_pairs={{0,4},{4,8},{8,12},{12,0},{1,5},{5,9},{9,13},{13,1},{2,6},{6,10},{... | collective-permute-start | bytes 294920 | tf_op jit(solution)/shard_map/ppermute | solution.py:166
  8.4 2.6 %collective-permute-start.1 = (bf16[3,2,128,1,64]{2,4,1,3,0:T(8,128)(2,1)S(1)}, bf16[3,2,128,1,64]{2,4,1,3,0:T(8,128)(2,1)S(1)}, u32[]{:S(2)}, u32[]{:S(2)}) collective-permute-start(bf16[3,2,128,1,64]{2,4,1,3,0:T(8,128)(2,1)S(1)} %get-tuple-element.17), channel_id=1, source_target_pairs={{0,8},{4,12},{8,0},{12,4},{1,9},{5,13},{9,1},{13,5},{2,10},{6,14},... | collective-permute-start | bytes 294920 | tf_op jit(solution)/shard_map/ppermute | solution.py:166
  10.9 1.3 %collective-permute-start.2 = (bf16[3,2,128,1,64]{2,4,1,3,0:T(8,128)(2,1)S(1)}, bf16[3,2,128,1,64]{2,4,1,3,0:T(8,128)(2,1)S(1)}, u32[]{:S(2)}, u32[]{:S(2)}) collective-permute-start(bf16[3,2,128,1,64]{2,4,1,3,0:T(8,128)(2,1)S(1)} %get-tuple-element.16), channel_id=1, source_target_pairs={{0,12},{4,0},{8,4},{12,8},{1,13},{5,1},{9,5},{13,9},{2,14},{6,2},{... | collective-permute-start | bytes 294920 | tf_op jit(solution)/shard_map/ppermute | solution.py:166
  12.4 1.6 %collective-permute-done = bf16[3,2,128,1,64]{2,4,1,3,0:T(8,128)(2,1)S(1)} collective-permute-done((bf16[3,2,128,1,64]{2,4,1,3,0:T(8,128)(2,1)S(1)}, bf16[3,2,128,1,64]{2,4,1,3,0:T(8,128)(2,1)S(1)}, u32[]{:S(2)}, u32[]{:S(2)}) %collective-permute-start) | collective-permute-done | bytes 98336 | tf_op jit(solution)/shard_map/ppermute | solution.py:166
  14.0 3.5 %collective-permute-done.1 = bf16[3,2,128,1,64]{2,4,1,3,0:T(8,128)(2,1)S(1)} collective-permute-done((bf16[3,2,128,1,64]{2,4,1,3,0:T(8,128)(2,1)S(1)}, bf16[3,2,128,1,64]{2,4,1,3,0:T(8,128)(2,1)S(1)}, u32[]{:S(2)}, u32[]{:S(2)}) %collective-permute-start.1) | collective-permute-done | bytes 98336 | tf_op jit(solution)/shard_map/ppermute | solution.py:166
  17.6 0.8 %fusion.6 = (f32[2,512]{1,0:T(2,128)S(1)}, f32[2,512,512]{1,2,0:T(8,128)S(1)}) fusion(pred[2,512]{1,0:T(4,128)(4,1)S(1)} %broadcast_compare_fusion, bf16[3,2,512,1,64]{2,4,1,3,0:T(8,128)(2,1)S(1)} %pad_maximum_fusion), kind=kOutput, calls=%fused_computation.12 | convolution fusion | flops 68680704 | bytes 2365440 | tf_op jit(solution)/shard_map/sqhe,skhe->shqk/dot_general | solution.py:138
  18.4 0.5 fusion.7
  18.9 0.6 fusion.23
  19.6 3.6 %collective-permute-start.3 = (bf16[2,1,128,64]{2,3,0,1:T(8,128)(2,1)S(1)}, bf16[2,1,128,64]{2,3,0,1:T(8,128)(2,1)S(1)}, u32[]{:S(2)}, u32[]{:S(2)}) collective-permute-start(bf16[2,1,128,64]{2,3,0,1:T(8,128)(2,1)S(1)} %get-tuple-element.39), channel_id=1, source_target_pairs={{0,12},{4,0},{8,4},{12,8},{1,13},{5,1},{9,5},{13,9},{2,14},{6,2},{... | collective-permute-start | bytes 98312 | tf_op jit(solution)/shard_map/ppermute | solution.py:176
  23.3 0.4 collective-permute-start.4
  23.7 0.2 collective-permute-start.5
  23.9 0.9 %collective-permute-done.3 = bf16[2,1,128,64]{2,3,0,1:T(8,128)(2,1)S(1)} collective-permute-done((bf16[2,1,128,64]{2,3,0,1:T(8,128)(2,1)S(1)}, bf16[2,1,128,64]{2,3,0,1:T(8,128)(2,1)S(1)}, u32[]{:S(2)}, u32[]{:S(2)}) %collective-permute-start.3) | collective-permute-done | bytes 32800 | tf_op jit(solution)/shard_map/ppermute | solution.py:176
  24.9 3.4 %collective-permute-done.4 = bf16[2,1,128,64]{2,3,0,1:T(8,128)(2,1)S(1)} collective-permute-done((bf16[2,1,128,64]{2,3,0,1:T(8,128)(2,1)S(1)}, bf16[2,1,128,64]{2,3,0,1:T(8,128)(2,1)S(1)}, u32[]{:S(2)}, u32[]{:S(2)}) %collective-permute-start.4) | collective-permute-done | bytes 32800 | tf_op jit(solution)/shard_map/ppermute | solution.py:176
  28.2 1.2 %collective-permute-done.5 = bf16[2,1,128,64]{2,3,0,1:T(8,128)(2,1)S(1)} collective-permute-done((bf16[2,1,128,64]{2,3,0,1:T(8,128)(2,1)S(1)}, bf16[2,1,128,64]{2,3,0,1:T(8,128)(2,1)S(1)}, u32[]{:S(2)}, u32[]{:S(2)}) %collective-permute-start.5) | collective-permute-done | bytes 32800 | tf_op jit(solution)/shard_map/ppermute | solution.py:176
  29.5 0.4 convolution_convert_fusion
  29.9 0.7 %dynamic-slice_bitcast_fusion.5 = (bf16[2,32,1536]{2,1,0:T(8,128)(2,1)}, bf16[2,32,1536]{2,1,0:T(8,128)(2,1)S(1)}, bf16[2,32,1536]{2,1,0:T(8,128)(2,1)S(1)}) fusion(bf16[2,2,2,32,1536]{4,3,2,1,0:T(8,128)(2,1)S(1)} %bitcast.120, s32[]{:T(128)S(6)} %select_n.121, s32[]{:T(128)S(6)} %select_n.125, s32[]{:T(128)S(6)} %select_n.127, s32[]{:T(128)S(6)} %select_n.123), kind=kLoop, calls=%fused_computation.73 | loop fusion | bytes 1179664 | tf_op jit(solution)/shard_map/jit(dynamic_index_in_dim)/squeeze | solution.py:80
  30.7 0.5 collective-permute-start.7
  31.3 0.4 collective-permute-start.9
  32.0 0.2 collective-permute-done.7
  32.1 0.3 collective-permute-done.8
  32.5 0.2 collective-permute-done.9
  32.7 1.6 %collective-permute-start.11 = (bf16[2,32,1536]{2,1,0:T(8,128)(2,1)S(1)}, bf16[2,32,1536]{2,1,0:T(8,128)(2,1)}, u32[]{:S(2)}, u32[]{:S(2)}) collective-permute-start(bf16[2,32,1536]{2,1,0:T(8,128)(2,1)S(1)} %maximum_maximum_fusion), channel_id=1, source_target_pairs={{0,2},{1,3},{2,0},{3,1},{4,6},{5,7},{6,4},{7,5},{8,10},{9,11},{10,... | collective-permute-start | bytes 589832 | tf_op jit(solution)/shard_map/ppermute | solution.py:85
  34.3 5.8 %collective-permute-done.11 = bf16[2,32,1536]{2,1,0:T(8,128)(2,1)} collective-permute-done((bf16[2,32,1536]{2,1,0:T(8,128)(2,1)S(1)}, bf16[2,32,1536]{2,1,0:T(8,128)(2,1)}, u32[]{:S(2)}, u32[]{:S(2)}) %collective-permute-start.11) | collective-permute-done | bytes 196640 | tf_op jit(solution)/shard_map/ppermute | solution.py:85
  40.0 1.3 %fusion.61 = (f32[2,32]{1,0:T(2,128)S(1)}, f32[2,32,1536]{2,1,0:T(8,128)S(1)}) fusion(bf16[2,32,1536]{2,1,0:T(8,128)(2,1)} %collective-permute-done.11, bf16[2,32,1536]{2,1,0:T(8,128)(2,1)} %collective-permute-done.6, bf16[2,2,2,32,1536]{4,3,2,1,0:T(8,128)(2,1)S(1)} %bitcast.121, s32[]{:T(128)S(6)} %select_n.121, s32[]{:T(128)S(6)} %select_n.123, ...), kind=kLoop, calls=%fused_computation.121 | loop fusion | flops 786368 | bytes 1179916 | tf_op jit(solution)/shard_map/reduce_sum | solution.py:27
  41.3 0.2 multiply_reduce_fusion
  41.7 1.6 %collective-permute-start.12 = (bf16[2,32,1536]{2,1,0:T(8,128)(2,1)S(1)}, bf16[2,32,1536]{2,1,0:T(8,128)(2,1)S(1)}, u32[]{:S(2)}, u32[]{:S(2)}) collective-permute-start(bf16[2,32,1536]{2,1,0:T(8,128)(2,1)S(1)} %get-tuple-element.6), channel_id=1, source_target_pairs={{0,2},{1,3},{2,0},{3,1},{4,6},{5,7},{6,4},{7,5},{8,10},{9,11},{10,... | collective-permute-start | bytes 589832 | tf_op jit(solution)/shard_map/ppermute | solution.py:112
  43.4 4.8 %collective-permute-done.12 = bf16[2,32,1536]{2,1,0:T(8,128)(2,1)S(1)} collective-permute-done((bf16[2,32,1536]{2,1,0:T(8,128)(2,1)S(1)}, bf16[2,32,1536]{2,1,0:T(8,128)(2,1)S(1)}, u32[]{:S(2)}, u32[]{:S(2)}) %collective-permute-start.12) | collective-permute-done | bytes 196640 | tf_op jit(solution)/shard_map/ppermute | solution.py:112
  48.4 1.2 %collective-permute-done.14 = bf16[2,32,1536]{2,1,0:T(8,128)(2,1)S(1)} collective-permute-done((bf16[2,32,1536]{2,1,0:T(8,128)(2,1)S(1)}, bf16[2,32,1536]{2,1,0:T(8,128)(2,1)S(1)}, u32[]{:S(2)}, u32[]{:S(2)}) %collective-permute-start.14) | collective-permute-done | bytes 196640 | tf_op jit(solution)/shard_map/ppermute | solution.py:113
  49.7 0.8 %fusion.12 = f32[2,2,128,384]{3,2,0,1:T(8,128)S(1)} fusion(bf16[2,128,1536,1]{2,1,3,0:T(8,128)(2,1)S(1)} %bitcast.125, bf16[2,1536,384]{2,1,0:T(8,128)(2,1)S(1)} %copy-done.5), kind=kOutput, calls=%fused_computation.18 | convolution fusion | flops 603979776 | bytes 3932160 | tf_op jit(solution)/shard_map/std,gdc->gstc/dot_general | solution.py:34
  50.7 1.3 %collective-permute-start.15 = (bf16[2,15,384]{2,1,0:T(8,128)(2,1)S(1)}, bf16[2,15,384]{2,1,0:T(8,128)(2,1)S(1)}, u32[]{:S(2)}, u32[]{:S(2)}) collective-permute-start(bf16[2,15,384]{2,1,0:T(8,128)(2,1)S(1)} %get-tuple-element.27), channel_id=1, source_target_pairs={{0,4},{4,8},{8,12},{1,5},{5,9},{9,13},{2,6},{6,10},{10,14},{3,7},{... | collective-permute-start | bytes 69128 | tf_op jit(solution)/shard_map/ppermute | solution.py:20
  52.0 1.3 %collective-permute-start.16 = (bf16[2,15,384]{2,1,0:T(8,128)(2,1)S(1)}, bf16[2,15,384]{2,1,0:T(8,128)(2,1)S(1)}, u32[]{:S(2)}, u32[]{:S(2)}) collective-permute-start(bf16[2,15,384]{2,1,0:T(8,128)(2,1)S(1)} %get-tuple-element.28), channel_id=1, source_target_pairs={{4,0},{8,4},{12,8},{5,1},{9,5},{13,9},{6,2},{10,6},{14,10},{7,3},{... | collective-permute-start | bytes 69128 | tf_op jit(solution)/shard_map/ppermute | solution.py:21
  53.3 0.2 collective-permute-done.15
  53.5 4.2 %collective-permute-done.16 = bf16[2,15,384]{2,1,0:T(8,128)(2,1)S(1)} collective-permute-done((bf16[2,15,384]{2,1,0:T(8,128)(2,1)S(1)}, bf16[2,15,384]{2,1,0:T(8,128)(2,1)S(1)}, u32[]{:S(2)}, u32[]{:S(2)}) %collective-permute-start.16) | collective-permute-done | bytes 23072 | tf_op jit(solution)/shard_map/ppermute | solution.py:21
  57.8 1.1 %fusion.48 = f32[2,128,384]{2,0,1:T(2,128)S(1)} fusion(bf16[2,158,384]{2,1,0:T(8,128)(2,1)S(1)} %pad_maximum_fusion.1, f32[31,1,384]{2,0,1:T(8,128)S(1)} %bitcast.127), kind=kOutput, calls=%fused_computation.56 | convolution fusion | flops 36569088 | bytes 683520 | tf_op jit(solution)/shard_map/conv_general_dilated | solution.py:234
  58.9 0.2 copy-done.6
  59.0 0.6 convolution_convert_fusion.1
  59.8 0.5 collective-permute-start.19
  60.4 0.4 collective-permute-start.21
  61.0 0.2 collective-permute-done.19
  61.2 0.3 collective-permute-done.20
  61.5 0.2 collective-permute-done.21
  61.8 1.6 %collective-permute-start.22 = (bf16[2,32,1536]{2,1,0:T(8,128)(2,1)S(1)}, bf16[2,32,1536]{2,1,0:T(8,128)(2,1)S(1)}, u32[]{:S(2)}, u32[]{:S(2)}) collective-permute-start(bf16[2,32,1536]{2,1,0:T(8,128)(2,1)S(1)} %maximum_maximum_fusion.1), channel_id=1, source_target_pairs={{0,2},{1,3},{2,0},{3,1},{4,6},{5,7},{6,4},{7,5},{8,10},{9,11},{10,... | collective-permute-start | bytes 589832 | tf_op jit(solution)/shard_map/ppermute | solution.py:85
  63.4 5.6 %collective-permute-done.22 = bf16[2,32,1536]{2,1,0:T(8,128)(2,1)S(1)} collective-permute-done((bf16[2,32,1536]{2,1,0:T(8,128)(2,1)S(1)}, bf16[2,32,1536]{2,1,0:T(8,128)(2,1)S(1)}, u32[]{:S(2)}, u32[]{:S(2)}) %collective-permute-start.22) | collective-permute-done | bytes 196640 | tf_op jit(solution)/shard_map/ppermute | solution.py:85
  69.0 0.8 %fusion.43 = bf16[2,32,1536]{2,1,0:T(8,128)(2,1)} fusion(f32[2,32,1536]{2,1,0:T(8,128)S(1)} %get-tuple-element.8, bf16[2,32,1536]{2,1,0:T(8,128)(2,1)S(1)} %collective-permute-done.22, bf16[2,32,1536]{2,1,0:T(8,128)(2,1)S(1)} %collective-permute-done.17, bf16[2,2,2,32,1536]{4,3,2,1,0:T(8,128)(2,1)S(1)} %bitcast.124, s32[]{:T(128)S(6)} %select_n.121, ...), kind=kLoop, calls=%fused_computation.45 | loop fusion | flops 1179648 | bytes 1185864 | tf_op jit(solution)/shard_map/convert_element_type | solution.py:251
  (78 shorter events, 2.1 us)
Async XLA Ops:
  0.0 3.0 %copy-start = (bf16[3,1536,256]{2,1,0:T(8,128)(2,1)S(1)}, bf16[3,1536,256]{2,1,0:T(8,128)(2,1)}, u32[]{:S(2)}) copy-start(bf16[3,1536,256]{2,1,0:T(8,128)(2,1)} %param.15) | copy-start | bytes 7077892
  3.0 9.3 %copy-start.4 = (s32[2]{0:T(128)S(1)}, s32[2]{0:T(128)}, u32[]{:S(2)}) copy-start(s32[2]{0:T(128)} %param.13) | copy-start | bytes 28
  5.3 8.8 %collective-permute-start = (bf16[3,2,128,1,64]{2,4,1,3,0:T(8,128)(2,1)S(1)}, bf16[3,2,128,1,64]{2,4,1,3,0:T(8,128)(2,1)S(1)}, u32[]{:S(2)}, u32[]{:S(2)}) collective-permute-start(bf16[3,2,128,1,64]{2,4,1,3,0:T(8,128)(2,1)S(1)} %get-tuple-element.18), channel_id=1, source_target_pairs={{0,4},{4,8},{8,12},{12,0},{1,5},{5,9},{9,13},{13,1},{2,6},{6,10},{... | collective-permute-start | bytes 294920 | tf_op jit(solution)/shard_map/ppermute | solution.py:166
  8.4 9.2 %collective-permute-start.1 = (bf16[3,2,128,1,64]{2,4,1,3,0:T(8,128)(2,1)S(1)}, bf16[3,2,128,1,64]{2,4,1,3,0:T(8,128)(2,1)S(1)}, u32[]{:S(2)}, u32[]{:S(2)}) collective-permute-start(bf16[3,2,128,1,64]{2,4,1,3,0:T(8,128)(2,1)S(1)} %get-tuple-element.17), channel_id=1, source_target_pairs={{0,8},{4,12},{8,0},{12,4},{1,9},{5,13},{9,1},{13,5},{2,10},{6,14},... | collective-permute-start | bytes 294920 | tf_op jit(solution)/shard_map/ppermute | solution.py:166
  10.9 6.6 %collective-permute-start.2 = (bf16[3,2,128,1,64]{2,4,1,3,0:T(8,128)(2,1)S(1)}, bf16[3,2,128,1,64]{2,4,1,3,0:T(8,128)(2,1)S(1)}, u32[]{:S(2)}, u32[]{:S(2)}) collective-permute-start(bf16[3,2,128,1,64]{2,4,1,3,0:T(8,128)(2,1)S(1)} %get-tuple-element.16), channel_id=1, source_target_pairs={{0,12},{4,0},{8,4},{12,8},{1,13},{5,1},{9,5},{13,9},{2,14},{6,2},{... | collective-permute-start | bytes 294920 | tf_op jit(solution)/shard_map/ppermute | solution.py:166
  18.9 10.6 %copy-start.1 = (bf16[256,1536]{1,0:T(8,128)(2,1)S(1)}, bf16[256,1536]{1,0:T(8,128)(2,1)}, u32[]{:S(2)}) copy-start(bf16[256,1536]{1,0:T(8,128)(2,1)} %param.16) | copy-start | bytes 2359300
  19.6 5.2 %collective-permute-start.3 = (bf16[2,1,128,64]{2,3,0,1:T(8,128)(2,1)S(1)}, bf16[2,1,128,64]{2,3,0,1:T(8,128)(2,1)S(1)}, u32[]{:S(2)}, u32[]{:S(2)}) collective-permute-start(bf16[2,1,128,64]{2,3,0,1:T(8,128)(2,1)S(1)} %get-tuple-element.39), channel_id=1, source_target_pairs={{0,12},{4,0},{8,4},{12,8},{1,13},{5,1},{9,5},{13,9},{2,14},{6,2},{... | collective-permute-start | bytes 98312 | tf_op jit(solution)/shard_map/ppermute | solution.py:176
  23.3 5.0 %collective-permute-start.4 = (bf16[2,1,128,64]{2,3,0,1:T(8,128)(2,1)S(1)}, bf16[2,1,128,64]{2,3,0,1:T(8,128)(2,1)S(1)}, u32[]{:S(2)}, u32[]{:S(2)}) collective-permute-start(bf16[2,1,128,64]{2,3,0,1:T(8,128)(2,1)S(1)} %get-tuple-element.38), channel_id=1, source_target_pairs={{0,8},{4,12},{8,0},{12,4},{1,9},{5,13},{9,1},{13,5},{2,10},{6,14},... | collective-permute-start | bytes 98312 | tf_op jit(solution)/shard_map/ppermute | solution.py:176
  23.7 5.7 %collective-permute-start.5 = (bf16[2,1,128,64]{2,3,0,1:T(8,128)(2,1)S(1)}, bf16[2,1,128,64]{2,3,0,1:T(8,128)(2,1)S(1)}, u32[]{:S(2)}, u32[]{:S(2)}) collective-permute-start(bf16[2,1,128,64]{2,3,0,1:T(8,128)(2,1)S(1)} %get-tuple-element.37), channel_id=1, source_target_pairs={{0,4},{4,8},{8,12},{12,0},{1,5},{5,9},{9,13},{13,1},{2,6},{6,10},{... | collective-permute-start | bytes 98312 | tf_op jit(solution)/shard_map/ppermute | solution.py:176
  29.9 11.7 %copy-start.2 = (f32[1536]{0:T(1024)S(1)}, f32[1536]{0:T(1024)}, u32[]{:S(2)}) copy-start(f32[1536]{0:T(1024)} %param.17) | copy-start | bytes 18436
  30.7 1.3 %collective-permute-start.10 = (bf16[1,16,1536]{2,1,0:T(8,128)(2,1)S(1)}, bf16[1,16,1536]{2,1,0:T(8,128)(2,1)S(1)}, u32[]{:S(2)}, u32[]{:S(2)}) collective-permute-start(bf16[1,16,1536]{2,1,0:T(8,128)(2,1)S(1)} %get-tuple-element.34), channel_id=1, source_target_pairs={{0,1},{1,0},{2,3},{3,2},{4,5},{5,4},{6,7},{7,6},{8,9},{9,8},{10,11... | collective-permute-start | bytes 147464 | tf_op jit(solution)/shard_map/ppermute | solution.py:67
  30.7 1.4 %collective-permute-start.7 = (bf16[1,16,1536]{2,1,0:T(8,128)(2,1)S(1)}, bf16[1,16,1536]{2,1,0:T(8,128)(2,1)S(1)}, u32[]{:S(2)}, u32[]{:S(2)}) collective-permute-start(bf16[1,16,1536]{2,1,0:T(8,128)(2,1)S(1)} %get-tuple-element.33), channel_id=1, source_target_pairs={{0,1},{1,0},{2,3},{3,2},{4,5},{5,4},{6,7},{7,6},{8,9},{9,8},{10,11... | collective-permute-start | bytes 147464 | tf_op jit(solution)/shard_map/ppermute | solution.py:67
  31.2 1.2 %collective-permute-start.8 = (bf16[1,16,1536]{2,1,0:T(8,128)(2,1)S(1)}, bf16[1,16,1536]{2,1,0:T(8,128)(2,1)S(1)}, u32[]{:S(2)}, u32[]{:S(2)}) collective-permute-start(bf16[1,16,1536]{2,1,0:T(8,128)(2,1)S(1)} %get-tuple-element.36), channel_id=1, source_target_pairs={{0,1},{1,0},{2,3},{3,2},{4,5},{5,4},{6,7},{7,6},{8,9},{9,8},{10,11... | collective-permute-start | bytes 147464 | tf_op jit(solution)/shard_map/ppermute | solution.py:67
  31.3 1.3 %collective-permute-start.9 = (bf16[1,16,1536]{2,1,0:T(8,128)(2,1)S(1)}, bf16[1,16,1536]{2,1,0:T(8,128)(2,1)S(1)}, u32[]{:S(2)}, u32[]{:S(2)}) collective-permute-start(bf16[1,16,1536]{2,1,0:T(8,128)(2,1)S(1)} %get-tuple-element.35), channel_id=1, source_target_pairs={{0,1},{1,0},{2,3},{3,2},{4,5},{5,4},{6,7},{7,6},{8,9},{9,8},{10,11... | collective-permute-start | bytes 147464 | tf_op jit(solution)/shard_map/ppermute | solution.py:67
  31.7 2.5 %collective-permute-start.6 = (bf16[2,32,1536]{2,1,0:T(8,128)(2,1)}, bf16[2,32,1536]{2,1,0:T(8,128)(2,1)}, u32[]{:S(2)}, u32[]{:S(2)}) collective-permute-start(bf16[2,32,1536]{2,1,0:T(8,128)(2,1)} %get-tuple-element.12), channel_id=1, source_target_pairs={{0,1},{1,0},{2,3},{3,2},{4,5},{5,4},{6,7},{7,6},{8,9},{9,8},{10,11... | collective-permute-start | bytes 589832 | tf_op jit(solution)/shard_map/ppermute | solution.py:79
  32.7 7.3 %collective-permute-start.11 = (bf16[2,32,1536]{2,1,0:T(8,128)(2,1)S(1)}, bf16[2,32,1536]{2,1,0:T(8,128)(2,1)}, u32[]{:S(2)}, u32[]{:S(2)}) collective-permute-start(bf16[2,32,1536]{2,1,0:T(8,128)(2,1)S(1)} %maximum_maximum_fusion), channel_id=1, source_target_pairs={{0,2},{1,3},{2,0},{3,1},{4,6},{5,7},{6,4},{7,5},{8,10},{9,11},{10,... | collective-permute-start | bytes 589832 | tf_op jit(solution)/shard_map/ppermute | solution.py:85
  41.7 7.9 %copy-start.5 = (bf16[2,1536,384]{2,1,0:T(8,128)(2,1)S(1)}, bf16[2,1536,384]{2,1,0:T(8,128)(2,1)}, u32[]{:S(2)}) copy-start(bf16[2,1536,384]{2,1,0:T(8,128)(2,1)} %param.18) | copy-start | bytes 7077892
  41.7 6.4 %collective-permute-start.12 = (bf16[2,32,1536]{2,1,0:T(8,128)(2,1)S(1)}, bf16[2,32,1536]{2,1,0:T(8,128)(2,1)S(1)}, u32[]{:S(2)}, u32[]{:S(2)}) collective-permute-start(bf16[2,32,1536]{2,1,0:T(8,128)(2,1)S(1)} %get-tuple-element.6), channel_id=1, source_target_pairs={{0,2},{1,3},{2,0},{3,1},{4,6},{5,7},{6,4},{7,5},{8,10},{9,11},{10,... | collective-permute-start | bytes 589832 | tf_op jit(solution)/shard_map/ppermute | solution.py:112
  43.4 4.8 %collective-permute-start.13 = (bf16[2,32,1536]{2,1,0:T(8,128)(2,1)S(1)}, bf16[2,32,1536]{2,1,0:T(8,128)(2,1)S(1)}, u32[]{:S(2)}, u32[]{:S(2)}) collective-permute-start(bf16[2,32,1536]{2,1,0:T(8,128)(2,1)S(1)} %get-tuple-element.6), channel_id=1, source_target_pairs={{0,1},{1,0},{2,3},{3,2},{4,5},{5,4},{6,7},{7,6},{8,9},{9,8},{10,11... | collective-permute-start | bytes 589832 | tf_op jit(solution)/shard_map/ppermute | solution.py:109
  48.2 1.4 %collective-permute-start.14 = (bf16[2,32,1536]{2,1,0:T(8,128)(2,1)S(1)}, bf16[2,32,1536]{2,1,0:T(8,128)(2,1)S(1)}, u32[]{:S(2)}, u32[]{:S(2)}) collective-permute-start(bf16[2,32,1536]{2,1,0:T(8,128)(2,1)S(1)} %collective-permute-done.12), channel_id=1, source_target_pairs={{0,1},{1,0},{2,3},{3,2},{4,5},{5,4},{6,7},{7,6},{8,9},{9,8},{10,11... | collective-permute-start | bytes 589832 | tf_op jit(solution)/shard_map/ppermute | solution.py:113
  49.7 3.6 %copy-start.3 = (s32[1536]{0:T(1024)S(1)}, s32[1536]{0:T(1024)}, u32[]{:S(2)}) copy-start(s32[1536]{0:T(1024)} %param.23) | copy-start | bytes 18436
  49.7 8.1 %copy-start.7 = (f32[31,384]{1,0:T(8,128)S(1)}, f32[31,384]{1,0:T(8,128)}, u32[]{:S(2)}) copy-start(f32[31,384]{1,0:T(8,128)} %param.19) | copy-start | bytes 142852
  50.7 2.8 %collective-permute-start.15 = (bf16[2,15,384]{2,1,0:T(8,128)(2,1)S(1)}, bf16[2,15,384]{2,1,0:T(8,128)(2,1)S(1)}, u32[]{:S(2)}, u32[]{:S(2)}) collective-permute-start(bf16[2,15,384]{2,1,0:T(8,128)(2,1)S(1)} %get-tuple-element.27), channel_id=1, source_target_pairs={{0,4},{4,8},{8,12},{1,5},{5,9},{9,13},{2,6},{6,10},{10,14},{3,7},{... | collective-permute-start | bytes 69128 | tf_op jit(solution)/shard_map/ppermute | solution.py:20
  52.0 5.7 %collective-permute-start.16 = (bf16[2,15,384]{2,1,0:T(8,128)(2,1)S(1)}, bf16[2,15,384]{2,1,0:T(8,128)(2,1)S(1)}, u32[]{:S(2)}, u32[]{:S(2)}) collective-permute-start(bf16[2,15,384]{2,1,0:T(8,128)(2,1)S(1)} %get-tuple-element.28), channel_id=1, source_target_pairs={{4,0},{8,4},{12,8},{5,1},{9,5},{13,9},{6,2},{10,6},{14,10},{7,3},{... | collective-permute-start | bytes 69128 | tf_op jit(solution)/shard_map/ppermute | solution.py:21
  57.8 1.3 %copy-start.6 = (bf16[384,1536]{1,0:T(8,128)(2,1)S(1)}, bf16[384,1536]{1,0:T(8,128)(2,1)}, u32[]{:S(2)}) copy-start(bf16[384,1536]{1,0:T(8,128)(2,1)} %param.22) | copy-start | bytes 3538948
  57.8 1.3 %copy-start.8 = (f32[384]{0:T(512)S(1)}, f32[384]{0:T(512)}, u32[]{:S(2)}) copy-start(f32[384]{0:T(512)} %param.21) | copy-start | bytes 4612
  57.8 1.3 %copy-start.9 = (f32[384]{0:T(512)S(1)}, f32[384]{0:T(512)}, u32[]{:S(2)}) copy-start(f32[384]{0:T(512)} %param.20) | copy-start | bytes 4612
  59.7 1.3 %collective-permute-start.18 = (bf16[1,16,1536]{2,1,0:T(8,128)(2,1)S(1)}, bf16[1,16,1536]{2,1,0:T(8,128)(2,1)S(1)}, u32[]{:S(2)}, u32[]{:S(2)}) collective-permute-start(bf16[1,16,1536]{2,1,0:T(8,128)(2,1)S(1)} %get-tuple-element.23), channel_id=1, source_target_pairs={{0,1},{1,0},{2,3},{3,2},{4,5},{5,4},{6,7},{7,6},{8,9},{9,8},{10,11... | collective-permute-start | bytes 147464 | tf_op jit(solution)/shard_map/ppermute | solution.py:67
  59.8 1.4 %collective-permute-start.19 = (bf16[1,16,1536]{2,1,0:T(8,128)(2,1)S(1)}, bf16[1,16,1536]{2,1,0:T(8,128)(2,1)S(1)}, u32[]{:S(2)}, u32[]{:S(2)}) collective-permute-start(bf16[1,16,1536]{2,1,0:T(8,128)(2,1)S(1)} %get-tuple-element.26), channel_id=1, source_target_pairs={{0,1},{1,0},{2,3},{3,2},{4,5},{5,4},{6,7},{7,6},{8,9},{9,8},{10,11... | collective-permute-start | bytes 147464 | tf_op jit(solution)/shard_map/ppermute | solution.py:67
  60.3 1.2 %collective-permute-start.20 = (bf16[1,16,1536]{2,1,0:T(8,128)(2,1)S(1)}, bf16[1,16,1536]{2,1,0:T(8,128)(2,1)S(1)}, u32[]{:S(2)}, u32[]{:S(2)}) collective-permute-start(bf16[1,16,1536]{2,1,0:T(8,128)(2,1)S(1)} %get-tuple-element.25), channel_id=1, source_target_pairs={{0,1},{1,0},{2,3},{3,2},{4,5},{5,4},{6,7},{7,6},{8,9},{9,8},{10,11... | collective-permute-start | bytes 147464 | tf_op jit(solution)/shard_map/ppermute | solution.py:67
  60.4 1.3 %collective-permute-start.21 = (bf16[1,16,1536]{2,1,0:T(8,128)(2,1)S(1)}, bf16[1,16,1536]{2,1,0:T(8,128)(2,1)S(1)}, u32[]{:S(2)}, u32[]{:S(2)}) collective-permute-start(bf16[1,16,1536]{2,1,0:T(8,128)(2,1)S(1)} %get-tuple-element.24), channel_id=1, source_target_pairs={{0,1},{1,0},{2,3},{3,2},{4,5},{5,4},{6,7},{7,6},{8,9},{9,8},{10,11... | collective-permute-start | bytes 147464 | tf_op jit(solution)/shard_map/ppermute | solution.py:67
  60.8 2.6 %collective-permute-start.17 = (bf16[2,32,1536]{2,1,0:T(8,128)(2,1)S(1)}, bf16[2,32,1536]{2,1,0:T(8,128)(2,1)S(1)}, u32[]{:S(2)}, u32[]{:S(2)}) collective-permute-start(bf16[2,32,1536]{2,1,0:T(8,128)(2,1)S(1)} %get-tuple-element.9), channel_id=1, source_target_pairs={{0,1},{1,0},{2,3},{3,2},{4,5},{5,4},{6,7},{7,6},{8,9},{9,8},{10,11... | collective-permute-start | bytes 589832 | tf_op jit(solution)/shard_map/ppermute | solution.py:79
  61.8 7.2 %collective-permute-start.22 = (bf16[2,32,1536]{2,1,0:T(8,128)(2,1)S(1)}, bf16[2,32,1536]{2,1,0:T(8,128)(2,1)S(1)}, u32[]{:S(2)}, u32[]{:S(2)}) collective-permute-start(bf16[2,32,1536]{2,1,0:T(8,128)(2,1)S(1)} %maximum_maximum_fusion.1), channel_id=1, source_target_pairs={{0,2},{1,3},{2,0},{3,1},{4,6},{5,7},{6,4},{7,5},{8,10},{9,11},{10,... | collective-permute-start | bytes 589832 | tf_op jit(solution)/shard_map/ppermute | solution.py:85

commit v24 on v22

--- a/solution.py
+++ b/solution.py
@@ -210,7 +210,13 @@
         value_heads = value_heads.transpose(1, 0, 2, 3, 4).reshape(records, -1, head_count, HEAD_DIM)
         attended = attend(query_heads, key_heads, value_heads, positions.reshape(-1), frame_counts)
         attended = attended.transpose(0, 2, 1, 3).reshape(records, frames_here, head_count * HEAD_DIM)
-    attn_part = jnp.einsum("stc,cd->std", attended, w_out, preferred_element_type=jnp.float32)
+    attn_part = jnp.concatenate(
+        [
+            jnp.einsum("stc,cd->std", attended[r : r + 1], w_out, preferred_element_type=jnp.float32)
+            for r in range(attended.shape[0])
+        ],
+        axis=0,
+    )
     mp_count = lax.axis_size("mp")
     mp_rank = lax.axis_index("mp")
     rows_mine = frames_here // mp_count
@@ -236,7 +242,13 @@
         precision=lax.Precision.HIGHEST,
     )
     activated = jax.nn.silu(depthwise * bn_scale + bn_shift).astype(jnp.bfloat16)
-    conv_part = jnp.einsum("stc,cd->std", activated, w_pw, preferred_element_type=jnp.float32)
+    conv_part = jnp.concatenate(
+        [
+            jnp.einsum("stc,cd->std", activated[r : r + 1], w_pw, preferred_element_type=jnp.float32)
+            for r in range(activated.shape[0])
+        ],
+        axis=0,
+    )
     conv_rows = reduce_scatter_rows(conv_part.astype(jnp.bfloat16), "mp", 1)
     combined = residual_mine + conv_rows
     clip_bound = clip_level.astype(jnp.float32) / 16.0

time: 68.1 us -> 72.4 us (1.063)
  matrix products: 6.25 us -> 8.81 us
  other arithmetic: 6.39 us -> 7.48 us
  local copies, waits for them, and re-layouts: 0.94 us -> 2.01 us
    dot_general x2 -> x4, matrix products: 0.99 us -> 3.54 us  [the longest x2 2.8 us: shards(): jnp.einsum('stc,cd->std', attended[r:r + 1], w_out, preferred_element_typ...]
    squeeze x0 -> x2, other arithmetic: none -> 0.81 us  [reduce_scatter_rows(): lax.dynamic_index_in_dim(send, onward, dim + bits - 2, keepdims=False)]
where the time goes in v24:
time: 72.4 us; the launch traced here: 72.1 us
  waiting for transfers between devices  33.4 us (46%)
  starting transfers between devices  19.9 us (27%)
  matrix products  8.81 us (12%)
  other arithmetic  7.48 us (10%)
  local copies, waits for them, and re-layouts  2.01 us (3%)
    ppermute x2, waiting for transfers between devices, reduce_scatter_rows(): got = lax.ppermute(far, axis, xor_pairs(count, 2))  10.7 us
    ppermute x3, starting transfers between devices, attend_by_heads(): pieces.append(lax.ppermute(send, axis, pairs))  7.01 us
    ppermute x3, waiting for transfers between devices, attend_by_heads(): back.append(lax.ppermute(rows, axis, pairs))  5.45 us
    ppermute x3, waiting for transfers between devices, attend_by_heads(): pieces.append(lax.ppermute(send, axis, pairs))  5.16 us
    ppermute x1, waiting for transfers between devices, all_gather_rows(): got = lax.ppermute(mine_acc, axis, xor_pairs(count, 1 << b))  4.78 us
    ppermute x3, starting transfers between devices, attend_by_heads(): back.append(lax.ppermute(rows, axis, pairs))  4.3 us
    ppermute x1, waiting for transfers between devices, with_halo(): after = lax.ppermute(initial, axis, down)  4.22 us
    ppermute x2, starting transfers between devices, reduce_scatter_rows(): got = lax.ppermute(far, axis, xor_pairs(count, 2))  3.13 us
  transfers between devices with their start and end apart: 19, of which 15 were waited for; matrix products, arithmetic and copies ran while one was open for 1% of the time, Pallas kernels for 0%

profile of v24, /device:TPU:0, one launch (start us, length us, event | category | flops | bytes accessed | tf_op | source)
XLA Modules:
  0.0 72.1 jit_solution(7987660989077570377)
XLA Ops:
  0.0 1.5 %convert_reduce_fusion = f32[2,128]{1,0:T(2,128)S(1)} fusion(bf16[2,128,1536]{2,1,0:T(8,128)(2,1)} %param.12), kind=kLoop, calls=%fused_computation.15 | loop fusion | flops 786176 | bytes 787456 | tf_op jit(solution)/shard_map/reduce_sum | solution.py:27
  1.5 1.5 %fusion.13 = f32[2,128]{1,0:T(2,128)S(1)} fusion(bf16[2,128,1536]{2,1,0:T(8,128)(2,1)} %param.12, f32[2,128]{1,0:T(2,128)S(1)} %broadcast_multiply_fusion.1), kind=kLoop, calls=%fused_computation.21 | loop fusion | flops 1572608 | bytes 788480 | tf_op jit(solution)/shard_map/reduce_sum | solution.py:29
  3.0 2.0 %fusion.22 = bf16[3,2,128,256]{3,2,0,1:T(8,128)(2,1)S(1)} fusion(bf16[3,1536,256]{2,1,0:T(8,128)(2,1)S(1)} %copy-done, bf16[2,128,1536]{2,1,0:T(8,128)(2,1)} %param.12, f32[1536]{0:T(1024)} %param.14, f32[2,128]{1,0:T(2,128)S(1)} %add_rsqrt_fusion.1, f32[2,128]{1,0:T(2,128)S(1)} %broadcast_multiply_fusion.1), kind=kOutput, calls=%fused_computation.26 | convolution fusion | flops 606142464 | bytes 3547136 | tf_op jit(solution)/shard_map/std,idc->istc/dot_general | solution.py:197
  5.0 0.2 copy.38
  5.3 3.1 %collective-permute-start = (bf16[3,2,128,1,64]{2,4,1,3,0:T(8,128)(2,1)S(1)}, bf16[3,2,128,1,64]{2,4,1,3,0:T(8,128)(2,1)S(1)}, u32[]{:S(2)}, u32[]{:S(2)}) collective-permute-start(bf16[3,2,128,1,64]{2,4,1,3,0:T(8,128)(2,1)S(1)} %get-tuple-element.18), channel_id=1, source_target_pairs={{0,4},{4,8},{8,12},{12,0},{1,5},{5,9},{9,13},{13,1},{2,6},{6,10},{... | collective-permute-start | bytes 294920 | tf_op jit(solution)/shard_map/ppermute | solution.py:161
  8.4 2.6 %collective-permute-start.1 = (bf16[3,2,128,1,64]{2,4,1,3,0:T(8,128)(2,1)S(1)}, bf16[3,2,128,1,64]{2,4,1,3,0:T(8,128)(2,1)S(1)}, u32[]{:S(2)}, u32[]{:S(2)}) collective-permute-start(bf16[3,2,128,1,64]{2,4,1,3,0:T(8,128)(2,1)S(1)} %get-tuple-element.17), channel_id=1, source_target_pairs={{0,8},{4,12},{8,0},{12,4},{1,9},{5,13},{9,1},{13,5},{2,10},{6,14},... | collective-permute-start | bytes 294920 | tf_op jit(solution)/shard_map/ppermute | solution.py:161
  10.9 1.3 %collective-permute-start.2 = (bf16[3,2,128,1,64]{2,4,1,3,0:T(8,128)(2,1)S(1)}, bf16[3,2,128,1,64]{2,4,1,3,0:T(8,128)(2,1)S(1)}, u32[]{:S(2)}, u32[]{:S(2)}) collective-permute-start(bf16[3,2,128,1,64]{2,4,1,3,0:T(8,128)(2,1)S(1)} %get-tuple-element.16), channel_id=1, source_target_pairs={{0,12},{4,0},{8,4},{12,8},{1,13},{5,1},{9,5},{13,9},{2,14},{6,2},{... | collective-permute-start | bytes 294920 | tf_op jit(solution)/shard_map/ppermute | solution.py:161
  12.4 1.6 %collective-permute-done = bf16[3,2,128,1,64]{2,4,1,3,0:T(8,128)(2,1)S(1)} collective-permute-done((bf16[3,2,128,1,64]{2,4,1,3,0:T(8,128)(2,1)S(1)}, bf16[3,2,128,1,64]{2,4,1,3,0:T(8,128)(2,1)S(1)}, u32[]{:S(2)}, u32[]{:S(2)}) %collective-permute-start) | collective-permute-done | bytes 98336 | tf_op jit(solution)/shard_map/ppermute | solution.py:161
  14.0 3.5 %collective-permute-done.1 = bf16[3,2,128,1,64]{2,4,1,3,0:T(8,128)(2,1)S(1)} collective-permute-done((bf16[3,2,128,1,64]{2,4,1,3,0:T(8,128)(2,1)S(1)}, bf16[3,2,128,1,64]{2,4,1,3,0:T(8,128)(2,1)S(1)}, u32[]{:S(2)}, u32[]{:S(2)}) %collective-permute-start.1) | collective-permute-done | bytes 98336 | tf_op jit(solution)/shard_map/ppermute | solution.py:161
  17.6 0.8 %fusion.10 = (f32[2,512]{1,0:T(2,128)S(1)}, f32[2,512,512]{1,2,0:T(8,128)S(1)}) fusion(pred[2,512]{1,0:T(4,128)(4,1)S(1)} %broadcast_compare_fusion, bf16[3,2,512,1,64]{2,4,1,3,0:T(8,128)(2,1)S(1)} %pad_maximum_fusion), kind=kOutput, calls=%fused_computation.18 | convolution fusion | flops 68680704 | bytes 2365440 | tf_op jit(solution)/shard_map/sqhe,skhe->shqk/dot_general | solution.py:133
  18.4 0.5 fusion.11
  18.9 0.6 fusion.28
  19.6 3.6 %collective-permute-start.3 = (bf16[2,1,128,64]{2,3,0,1:T(8,128)(2,1)S(1)}, bf16[2,1,128,64]{2,3,0,1:T(8,128)(2,1)S(1)}, u32[]{:S(2)}, u32[]{:S(2)}) collective-permute-start(bf16[2,1,128,64]{2,3,0,1:T(8,128)(2,1)S(1)} %get-tuple-element.35), channel_id=1, source_target_pairs={{0,12},{4,0},{8,4},{12,8},{1,13},{5,1},{9,5},{13,9},{2,14},{6,2},{... | collective-permute-start | bytes 98312 | tf_op jit(solution)/shard_map/ppermute | solution.py:171
  23.2 0.4 collective-permute-start.4
  23.6 0.2 collective-permute-start.5
  23.9 0.9 %collective-permute-done.3 = bf16[2,1,128,64]{2,3,0,1:T(8,128)(2,1)S(1)} collective-permute-done((bf16[2,1,128,64]{2,3,0,1:T(8,128)(2,1)S(1)}, bf16[2,1,128,64]{2,3,0,1:T(8,128)(2,1)S(1)}, u32[]{:S(2)}, u32[]{:S(2)}) %collective-permute-start.3) | collective-permute-done | bytes 32800 | tf_op jit(solution)/shard_map/ppermute | solution.py:171
  24.8 3.4 %collective-permute-done.4 = bf16[2,1,128,64]{2,3,0,1:T(8,128)(2,1)S(1)} collective-permute-done((bf16[2,1,128,64]{2,3,0,1:T(8,128)(2,1)S(1)}, bf16[2,1,128,64]{2,3,0,1:T(8,128)(2,1)S(1)}, u32[]{:S(2)}, u32[]{:S(2)}) %collective-permute-start.4) | collective-permute-done | bytes 32800 | tf_op jit(solution)/shard_map/ppermute | solution.py:171
  28.2 1.2 %collective-permute-done.5 = bf16[2,1,128,64]{2,3,0,1:T(8,128)(2,1)S(1)} collective-permute-done((bf16[2,1,128,64]{2,3,0,1:T(8,128)(2,1)S(1)}, bf16[2,1,128,64]{2,3,0,1:T(8,128)(2,1)S(1)}, u32[]{:S(2)}, u32[]{:S(2)}) %collective-permute-start.5) | collective-permute-done | bytes 32800 | tf_op jit(solution)/shard_map/ppermute | solution.py:171
  29.6 0.1 reshape.315
  29.9 0.1 reshape.316
  30.1 1.4 %fusion.4 = bf16[1,2,2,32,1536]{4,3,2,1,0:T(8,128)(2,1)S(1)} fusion(bf16[2,2,32,256]{3,2,1,0:T(8,128)(2,1)S(1)} %reshape.315, bf16[256,1536]{1,0:T(8,128)(2,1)} %param.16), kind=kOutput, calls=%fused_computation.8 | convolution fusion | flops 100859904 | bytes 1245184 | tf_op jit(solution)/shard_map/stc,cd->std/dot_general | solution.py:215
  31.5 1.4 %fusion.5 = bf16[1,2,2,32,1536]{4,3,2,1,0:T(8,128)(2,1)S(1)} fusion(bf16[2,2,32,256]{3,2,1,0:T(8,128)(2,1)S(1)} %reshape.316, bf16[256,1536]{1,0:T(8,128)(2,1)} %param.16), kind=kOutput, calls=%fused_computation.9 | convolution fusion | flops 100859904 | bytes 1245184 | tf_op jit(solution)/shard_map/stc,cd->std/dot_general | solution.py:215
  32.9 0.7 %fusion.66 = (bf16[2,32,1536]{2,1,0:T(8,128)(2,1)}, bf16[2,1,1,32,1536]{4,3,2,1,0:T(8,128)(2,1)S(1)}, bf16[2,1,1,32,1536]{4,3,2,1,0:T(8,128)(2,1)S(1)}) fusion(s32[]{:T(128)S(6)} %select_n.121, s32[]{:T(128)S(6)} %select_n.125, bf16[1,2,2,32,1536]{4,3,2,1,0:T(8,128)(2,1)S(1)} %fusion.4, bf16[1,2,2,32,1536]{4,3,2,1,0:T(8,128)(2,1)S(1)} %fusion.5, ...), kind=kLoop, calls=%fused_computation.92 | loop fusion | flops 294912 | bytes 1376272 | tf_op jit(solution)/shard_map/jit(dynamic_index_in_dim)/squeeze | solution.py:67
  33.7 0.5 collective-permute-start.8
  34.3 0.7 collective-permute-done.7
  35.0 0.2 collective-permute-done.8
  35.3 1.6 %collective-permute-start.9 = (bf16[2,32,1536]{2,1,0:T(8,128)(2,1)S(1)}, bf16[2,32,1536]{2,1,0:T(8,128)(2,1)}, u32[]{:S(2)}, u32[]{:S(2)}) collective-permute-start(bf16[2,32,1536]{2,1,0:T(8,128)(2,1)S(1)} %pad_maximum_fusion.2), channel_id=1, source_target_pairs={{0,2},{1,3},{2,0},{3,1},{4,6},{5,7},{6,4},{7,5},{8,10},{9,11},{10,... | collective-permute-start | bytes 589832 | tf_op jit(solution)/shard_map/ppermute | solution.py:80
  36.8 0.7 copy-done.2
  37.5 5.1 %collective-permute-done.9 = bf16[2,32,1536]{2,1,0:T(8,128)(2,1)} collective-permute-done((bf16[2,32,1536]{2,1,0:T(8,128)(2,1)S(1)}, bf16[2,32,1536]{2,1,0:T(8,128)(2,1)}, u32[]{:S(2)}, u32[]{:S(2)}) %collective-permute-start.9) | collective-permute-done | bytes 196640 | tf_op jit(solution)/shard_map/ppermute | solution.py:80
  42.6 1.3 %fusion.79 = (f32[2,32]{1,0:T(2,128)S(1)}, f32[2,32,1536]{2,1,0:T(8,128)S(1)}) fusion(bf16[2,32,1536]{2,1,0:T(8,128)(2,1)} %collective-permute-done.9, bf16[2,32,1536]{2,1,0:T(8,128)(2,1)} %copy-done.2, s32[]{:T(128)S(6)} %select_n.121, s32[]{:T(128)S(6)} %select_n.123, bf16[1,2,2,32,1536]{4,3,2,1,0:T(8,128)(2,1)S(1)} %fusion.5, ...), kind=kLoop, calls=%fused_computation.155 | loop fusion | flops 1179584 | bytes 1769740 | tf_op jit(solution)/shard_map/reduce_sum | solution.py:27
  43.9 0.2 multiply_reduce_fusion
  44.3 1.6 %collective-permute-start.10 = (bf16[2,32,1536]{2,1,0:T(8,128)(2,1)S(1)}, bf16[2,32,1536]{2,1,0:T(8,128)(2,1)S(1)}, u32[]{:S(2)}, u32[]{:S(2)}) collective-permute-start(bf16[2,32,1536]{2,1,0:T(8,128)(2,1)S(1)} %get-tuple-element.6), channel_id=1, source_target_pairs={{0,2},{1,3},{2,0},{3,1},{4,6},{5,7},{6,4},{7,5},{8,10},{9,11},{10,... | collective-permute-start | bytes 589832 | tf_op jit(solution)/shard_map/ppermute | solution.py:107
  45.9 4.8 %collective-permute-done.10 = bf16[2,32,1536]{2,1,0:T(8,128)(2,1)S(1)} collective-permute-done((bf16[2,32,1536]{2,1,0:T(8,128)(2,1)S(1)}, bf16[2,32,1536]{2,1,0:T(8,128)(2,1)S(1)}, u32[]{:S(2)}, u32[]{:S(2)}) %collective-permute-start.10) | collective-permute-done | bytes 196640 | tf_op jit(solution)/shard_map/ppermute | solution.py:107
  50.9 1.2 %collective-permute-done.12 = bf16[2,32,1536]{2,1,0:T(8,128)(2,1)S(1)} collective-permute-done((bf16[2,32,1536]{2,1,0:T(8,128)(2,1)S(1)}, bf16[2,32,1536]{2,1,0:T(8,128)(2,1)S(1)}, u32[]{:S(2)}, u32[]{:S(2)}) %collective-permute-start.12) | collective-permute-done | bytes 196640 | tf_op jit(solution)/shard_map/ppermute | solution.py:108
  52.3 0.8 %fusion.16 = f32[2,2,128,384]{3,2,0,1:T(8,128)S(1)} fusion(bf16[2,128,1536,1]{2,1,3,0:T(8,128)(2,1)S(1)} %bitcast.165, bf16[2,1536,384]{2,1,0:T(8,128)(2,1)S(1)} %copy-done.8), kind=kOutput, calls=%fused_computation.24 | convolution fusion | flops 603979776 | bytes 3932160 | tf_op jit(solution)/shard_map/std,gdc->gstc/dot_general | solution.py:34
  53.2 1.3 %collective-permute-start.13 = (bf16[2,15,384]{2,1,0:T(8,128)(2,1)S(1)}, bf16[2,15,384]{2,1,0:T(8,128)(2,1)S(1)}, u32[]{:S(2)}, u32[]{:S(2)}) collective-permute-start(bf16[2,15,384]{2,1,0:T(8,128)(2,1)S(1)} %get-tuple-element.25), channel_id=1, source_target_pairs={{0,4},{4,8},{8,12},{1,5},{5,9},{9,13},{2,6},{6,10},{10,14},{3,7},{... | collective-permute-start | bytes 69128 | tf_op jit(solution)/shard_map/ppermute | solution.py:20
  54.5 1.3 %collective-permute-start.14 = (bf16[2,15,384]{2,1,0:T(8,128)(2,1)S(1)}, bf16[2,15,384]{2,1,0:T(8,128)(2,1)S(1)}, u32[]{:S(2)}, u32[]{:S(2)}) collective-permute-start(bf16[2,15,384]{2,1,0:T(8,128)(2,1)S(1)} %get-tuple-element.26), channel_id=1, source_target_pairs={{4,0},{8,4},{12,8},{5,1},{9,5},{13,9},{6,2},{10,6},{14,10},{7,3},{... | collective-permute-start | bytes 69128 | tf_op jit(solution)/shard_map/ppermute | solution.py:21
  55.8 0.2 collective-permute-done.13
  56.0 4.2 %collective-permute-done.14 = bf16[2,15,384]{2,1,0:T(8,128)(2,1)S(1)} collective-permute-done((bf16[2,15,384]{2,1,0:T(8,128)(2,1)S(1)}, bf16[2,15,384]{2,1,0:T(8,128)(2,1)S(1)}, u32[]{:S(2)}, u32[]{:S(2)}) %collective-permute-start.14) | collective-permute-done | bytes 23072 | tf_op jit(solution)/shard_map/ppermute | solution.py:21
  60.3 1.1 %fusion.54 = f32[2,128,384]{2,0,1:T(2,128)S(1)} fusion(bf16[2,158,384]{2,1,0:T(8,128)(2,1)S(1)} %pad_maximum_fusion.1, f32[31,1,384]{2,0,1:T(8,128)S(1)} %bitcast.168), kind=kOutput, calls=%fused_computation.80 | convolution fusion | flops 36569088 | bytes 683520 | tf_op jit(solution)/shard_map/conv_general_dilated | solution.py:235
  61.6 0.4 fusion.6
  62.0 0.4 fusion.7
  62.5 0.5 collective-permute-start.17
  63.1 0.7 collective-permute-done.16
  63.8 0.2 collective-permute-done.17
  64.1 1.6 %collective-permute-start.18 = (bf16[2,32,1536]{2,1,0:T(8,128)(2,1)S(1)}, bf16[2,32,1536]{2,1,0:T(8,128)(2,1)S(1)}, u32[]{:S(2)}, u32[]{:S(2)}) collective-permute-start(bf16[2,32,1536]{2,1,0:T(8,128)(2,1)S(1)} %pad_maximum_fusion.3), channel_id=1, source_target_pairs={{0,2},{1,3},{2,0},{3,1},{4,6},{5,7},{6,4},{7,5},{8,10},{9,11},{10,... | collective-permute-start | bytes 589832 | tf_op jit(solution)/shard_map/ppermute | solution.py:80
  65.7 5.6 %collective-permute-done.18 = bf16[2,32,1536]{2,1,0:T(8,128)(2,1)S(1)} collective-permute-done((bf16[2,32,1536]{2,1,0:T(8,128)(2,1)S(1)}, bf16[2,32,1536]{2,1,0:T(8,128)(2,1)S(1)}, u32[]{:S(2)}, u32[]{:S(2)}) %collective-permute-start.18) | collective-permute-done | bytes 196640 | tf_op jit(solution)/shard_map/ppermute | solution.py:80
  71.3 0.8 %fusion.49 = bf16[2,32,1536]{2,1,0:T(8,128)(2,1)} fusion(f32[2,32,1536]{2,1,0:T(8,128)S(1)} %get-tuple-element.8, bf16[2,32,1536]{2,1,0:T(8,128)(2,1)S(1)} %collective-permute-done.18, bf16[2,32,1536]{2,1,0:T(8,128)(2,1)S(1)} %collective-permute-done.15, s32[]{:T(128)S(6)} %select_n.121, s32[]{:T(128)S(6)} %select_n.123, ...), kind=kLoop, calls=%fused_computation.69 | loop fusion | flops 1572864 | bytes 1775688 | tf_op jit(solution)/shard_map/convert_element_type | solution.py:258
  (78 shorter events, 2.1 us)
Async XLA Ops:
  0.0 3.0 %copy-start = (bf16[3,1536,256]{2,1,0:T(8,128)(2,1)S(1)}, bf16[3,1536,256]{2,1,0:T(8,128)(2,1)}, u32[]{:S(2)}) copy-start(bf16[3,1536,256]{2,1,0:T(8,128)(2,1)} %param.15) | copy-start | bytes 7077892
  3.0 9.3 %copy-start.7 = (s32[2]{0:T(128)S(1)}, s32[2]{0:T(128)}, u32[]{:S(2)}) copy-start(s32[2]{0:T(128)} %param.13) | copy-start | bytes 28
  5.3 8.8 %collective-permute-start = (bf16[3,2,128,1,64]{2,4,1,3,0:T(8,128)(2,1)S(1)}, bf16[3,2,128,1,64]{2,4,1,3,0:T(8,128)(2,1)S(1)}, u32[]{:S(2)}, u32[]{:S(2)}) collective-permute-start(bf16[3,2,128,1,64]{2,4,1,3,0:T(8,128)(2,1)S(1)} %get-tuple-element.18), channel_id=1, source_target_pairs={{0,4},{4,8},{8,12},{12,0},{1,5},{5,9},{9,13},{13,1},{2,6},{6,10},{... | collective-permute-start | bytes 294920 | tf_op jit(solution)/shard_map/ppermute | solution.py:161
  8.4 9.2 %collective-permute-start.1 = (bf16[3,2,128,1,64]{2,4,1,3,0:T(8,128)(2,1)S(1)}, bf16[3,2,128,1,64]{2,4,1,3,0:T(8,128)(2,1)S(1)}, u32[]{:S(2)}, u32[]{:S(2)}) collective-permute-start(bf16[3,2,128,1,64]{2,4,1,3,0:T(8,128)(2,1)S(1)} %get-tuple-element.17), channel_id=1, source_target_pairs={{0,8},{4,12},{8,0},{12,4},{1,9},{5,13},{9,1},{13,5},{2,10},{6,14},... | collective-permute-start | bytes 294920 | tf_op jit(solution)/shard_map/ppermute | solution.py:161
  10.9 6.6 %collective-permute-start.2 = (bf16[3,2,128,1,64]{2,4,1,3,0:T(8,128)(2,1)S(1)}, bf16[3,2,128,1,64]{2,4,1,3,0:T(8,128)(2,1)S(1)}, u32[]{:S(2)}, u32[]{:S(2)}) collective-permute-start(bf16[3,2,128,1,64]{2,4,1,3,0:T(8,128)(2,1)S(1)} %get-tuple-element.16), channel_id=1, source_target_pairs={{0,12},{4,0},{8,4},{12,8},{1,13},{5,1},{9,5},{13,9},{2,14},{6,2},{... | collective-permute-start | bytes 294920 | tf_op jit(solution)/shard_map/ppermute | solution.py:161
  19.6 5.2 %collective-permute-start.3 = (bf16[2,1,128,64]{2,3,0,1:T(8,128)(2,1)S(1)}, bf16[2,1,128,64]{2,3,0,1:T(8,128)(2,1)S(1)}, u32[]{:S(2)}, u32[]{:S(2)}) collective-permute-start(bf16[2,1,128,64]{2,3,0,1:T(8,128)(2,1)S(1)} %get-tuple-element.35), channel_id=1, source_target_pairs={{0,12},{4,0},{8,4},{12,8},{1,13},{5,1},{9,5},{13,9},{2,14},{6,2},{... | collective-permute-start | bytes 98312 | tf_op jit(solution)/shard_map/ppermute | solution.py:171
  23.2 5.0 %collective-permute-start.4 = (bf16[2,1,128,64]{2,3,0,1:T(8,128)(2,1)S(1)}, bf16[2,1,128,64]{2,3,0,1:T(8,128)(2,1)S(1)}, u32[]{:S(2)}, u32[]{:S(2)}) collective-permute-start(bf16[2,1,128,64]{2,3,0,1:T(8,128)(2,1)S(1)} %get-tuple-element.34), channel_id=1, source_target_pairs={{0,8},{4,12},{8,0},{12,4},{1,9},{5,13},{9,1},{13,5},{2,10},{6,14},... | collective-permute-start | bytes 98312 | tf_op jit(solution)/shard_map/ppermute | solution.py:171
  23.6 5.7 %collective-permute-start.5 = (bf16[2,1,128,64]{2,3,0,1:T(8,128)(2,1)S(1)}, bf16[2,1,128,64]{2,3,0,1:T(8,128)(2,1)S(1)}, u32[]{:S(2)}, u32[]{:S(2)}) collective-permute-start(bf16[2,1,128,64]{2,3,0,1:T(8,128)(2,1)S(1)} %get-tuple-element.33), channel_id=1, source_target_pairs={{0,4},{4,8},{8,12},{12,0},{1,5},{5,9},{9,13},{13,1},{2,6},{6,10},{... | collective-permute-start | bytes 98312 | tf_op jit(solution)/shard_map/ppermute | solution.py:171
  33.6 10.5 %copy-start.3 = (f32[1536]{0:T(1024)S(1)}, f32[1536]{0:T(1024)}, u32[]{:S(2)}) copy-start(f32[1536]{0:T(1024)} %param.17) | copy-start | bytes 18436
  33.7 1.4 %collective-permute-start.7 = (bf16[1,32,1536]{2,1,0:T(8,128)(2,1)S(1)}, bf16[1,32,1536]{2,1,0:T(8,128)(2,1)S(1)}, u32[]{:S(2)}, u32[]{:S(2)}) collective-permute-start(bf16[1,32,1536]{2,1,0:T(8,128)(2,1)S(1)} %get-tuple-element.29), channel_id=1, source_target_pairs={{0,1},{1,0},{2,3},{3,2},{4,5},{5,4},{6,7},{7,6},{8,9},{9,8},{10,11... | collective-permute-start | bytes 294920 | tf_op jit(solution)/shard_map/ppermute | solution.py:62
  33.7 1.4 %collective-permute-start.8 = (bf16[1,32,1536]{2,1,0:T(8,128)(2,1)S(1)}, bf16[1,32,1536]{2,1,0:T(8,128)(2,1)S(1)}, u32[]{:S(2)}, u32[]{:S(2)}) collective-permute-start(bf16[1,32,1536]{2,1,0:T(8,128)(2,1)S(1)} %get-tuple-element.30), channel_id=1, source_target_pairs={{0,1},{1,0},{2,3},{3,2},{4,5},{5,4},{6,7},{7,6},{8,9},{9,8},{10,11... | collective-permute-start | bytes 294920 | tf_op jit(solution)/shard_map/ppermute | solution.py:62
  34.2 2.6 %collective-permute-start.6 = (bf16[2,32,1536]{2,1,0:T(8,128)(2,1)}, bf16[2,32,1536]{2,1,0:T(8,128)(2,1)S(1)}, u32[]{:S(2)}, u32[]{:S(2)}) collective-permute-start(bf16[2,32,1536]{2,1,0:T(8,128)(2,1)} %get-tuple-element.12), channel_id=1, source_target_pairs={{0,1},{1,0},{2,3},{3,2},{4,5},{5,4},{6,7},{7,6},{8,9},{9,8},{10,11... | collective-permute-start | bytes 589832 | tf_op jit(solution)/shard_map/ppermute | solution.py:66
  35.3 7.3 %collective-permute-start.9 = (bf16[2,32,1536]{2,1,0:T(8,128)(2,1)S(1)}, bf16[2,32,1536]{2,1,0:T(8,128)(2,1)}, u32[]{:S(2)}, u32[]{:S(2)}) collective-permute-start(bf16[2,32,1536]{2,1,0:T(8,128)(2,1)S(1)} %pad_maximum_fusion.2), channel_id=1, source_target_pairs={{0,2},{1,3},{2,0},{3,1},{4,6},{5,7},{6,4},{7,5},{8,10},{9,11},{10,... | collective-permute-start | bytes 589832 | tf_op jit(solution)/shard_map/ppermute | solution.py:80
  36.8 0.7 copy-start.2
  44.3 7.9 %copy-start.8 = (bf16[2,1536,384]{2,1,0:T(8,128)(2,1)S(1)}, bf16[2,1536,384]{2,1,0:T(8,128)(2,1)}, u32[]{:S(2)}) copy-start(bf16[2,1536,384]{2,1,0:T(8,128)(2,1)} %param.18) | copy-start | bytes 7077892
  44.3 6.4 %collective-permute-start.10 = (bf16[2,32,1536]{2,1,0:T(8,128)(2,1)S(1)}, bf16[2,32,1536]{2,1,0:T(8,128)(2,1)S(1)}, u32[]{:S(2)}, u32[]{:S(2)}) collective-permute-start(bf16[2,32,1536]{2,1,0:T(8,128)(2,1)S(1)} %get-tuple-element.6), channel_id=1, source_target_pairs={{0,2},{1,3},{2,0},{3,1},{4,6},{5,7},{6,4},{7,5},{8,10},{9,11},{10,... | collective-permute-start | bytes 589832 | tf_op jit(solution)/shard_map/ppermute | solution.py:107
  45.9 4.8 %collective-permute-start.11 = (bf16[2,32,1536]{2,1,0:T(8,128)(2,1)S(1)}, bf16[2,32,1536]{2,1,0:T(8,128)(2,1)S(1)}, u32[]{:S(2)}, u32[]{:S(2)}) collective-permute-start(bf16[2,32,1536]{2,1,0:T(8,128)(2,1)S(1)} %get-tuple-element.6), channel_id=1, source_target_pairs={{0,1},{1,0},{2,3},{3,2},{4,5},{5,4},{6,7},{7,6},{8,9},{9,8},{10,11... | collective-permute-start | bytes 589832 | tf_op jit(solution)/shard_map/ppermute | solution.py:104
  50.7 1.4 %collective-permute-start.12 = (bf16[2,32,1536]{2,1,0:T(8,128)(2,1)S(1)}, bf16[2,32,1536]{2,1,0:T(8,128)(2,1)S(1)}, u32[]{:S(2)}, u32[]{:S(2)}) collective-permute-start(bf16[2,32,1536]{2,1,0:T(8,128)(2,1)S(1)} %collective-permute-done.10), channel_id=1, source_target_pairs={{0,1},{1,0},{2,3},{3,2},{4,5},{5,4},{6,7},{7,6},{8,9},{9,8},{10,11... | collective-permute-start | bytes 589832 | tf_op jit(solution)/shard_map/ppermute | solution.py:108
  52.2 3.6 %copy-start.4 = (s32[1536]{0:T(1024)S(1)}, s32[1536]{0:T(1024)}, u32[]{:S(2)}) copy-start(s32[1536]{0:T(1024)} %param.23) | copy-start | bytes 18436
  52.2 8.1 %copy-start.9 = (f32[31,384]{1,0:T(8,128)S(1)}, f32[31,384]{1,0:T(8,128)}, u32[]{:S(2)}) copy-start(f32[31,384]{1,0:T(8,128)} %param.19) | copy-start | bytes 142852
  53.2 2.8 %collective-permute-start.13 = (bf16[2,15,384]{2,1,0:T(8,128)(2,1)S(1)}, bf16[2,15,384]{2,1,0:T(8,128)(2,1)S(1)}, u32[]{:S(2)}, u32[]{:S(2)}) collective-permute-start(bf16[2,15,384]{2,1,0:T(8,128)(2,1)S(1)} %get-tuple-element.25), channel_id=1, source_target_pairs={{0,4},{4,8},{8,12},{1,5},{5,9},{9,13},{2,6},{6,10},{10,14},{3,7},{... | collective-permute-start | bytes 69128 | tf_op jit(solution)/shard_map/ppermute | solution.py:20
  54.5 5.7 %collective-permute-start.14 = (bf16[2,15,384]{2,1,0:T(8,128)(2,1)S(1)}, bf16[2,15,384]{2,1,0:T(8,128)(2,1)S(1)}, u32[]{:S(2)}, u32[]{:S(2)}) collective-permute-start(bf16[2,15,384]{2,1,0:T(8,128)(2,1)S(1)} %get-tuple-element.26), channel_id=1, source_target_pairs={{4,0},{8,4},{12,8},{5,1},{9,5},{13,9},{6,2},{10,6},{14,10},{7,3},{... | collective-permute-start | bytes 69128 | tf_op jit(solution)/shard_map/ppermute | solution.py:21
  60.3 1.1 %copy-start.5 = (f32[384]{0:T(512)S(1)}, f32[384]{0:T(512)}, u32[]{:S(2)}) copy-start(f32[384]{0:T(512)} %param.21) | copy-start | bytes 4612
  60.3 1.1 %copy-start.6 = (f32[384]{0:T(512)S(1)}, f32[384]{0:T(512)}, u32[]{:S(2)}) copy-start(f32[384]{0:T(512)} %param.20) | copy-start | bytes 4612
  60.3 1.3 %copy-start.1 = (bf16[384,1536]{1,0:T(8,128)(2,1)S(1)}, bf16[384,1536]{1,0:T(8,128)(2,1)}, u32[]{:S(2)}) copy-start(bf16[384,1536]{1,0:T(8,128)(2,1)} %param.22) | copy-start | bytes 3538948
  62.5 1.4 %collective-permute-start.16 = (bf16[1,32,1536]{2,1,0:T(8,128)(2,1)S(1)}, bf16[1,32,1536]{2,1,0:T(8,128)(2,1)S(1)}, u32[]{:S(2)}, u32[]{:S(2)}) collective-permute-start(bf16[1,32,1536]{2,1,0:T(8,128)(2,1)S(1)} %get-tuple-element.21), channel_id=1, source_target_pairs={{0,1},{1,0},{2,3},{3,2},{4,5},{5,4},{6,7},{7,6},{8,9},{9,8},{10,11... | collective-permute-start | bytes 294920 | tf_op jit(solution)/shard_map/ppermute | solution.py:62
  62.5 1.4 %collective-permute-start.17 = (bf16[1,32,1536]{2,1,0:T(8,128)(2,1)S(1)}, bf16[1,32,1536]{2,1,0:T(8,128)(2,1)S(1)}, u32[]{:S(2)}, u32[]{:S(2)}) collective-permute-start(bf16[1,32,1536]{2,1,0:T(8,128)(2,1)S(1)} %get-tuple-element.22), channel_id=1, source_target_pairs={{0,1},{1,0},{2,3},{3,2},{4,5},{5,4},{6,7},{7,6},{8,9},{9,8},{10,11... | collective-permute-start | bytes 294920 | tf_op jit(solution)/shard_map/ppermute | solution.py:62
  63.0 2.7 %collective-permute-start.15 = (bf16[2,32,1536]{2,1,0:T(8,128)(2,1)S(1)}, bf16[2,32,1536]{2,1,0:T(8,128)(2,1)S(1)}, u32[]{:S(2)}, u32[]{:S(2)}) collective-permute-start(bf16[2,32,1536]{2,1,0:T(8,128)(2,1)S(1)} %get-tuple-element.9), channel_id=1, source_target_pairs={{0,1},{1,0},{2,3},{3,2},{4,5},{5,4},{6,7},{7,6},{8,9},{9,8},{10,11... | collective-permute-start | bytes 589832 | tf_op jit(solution)/shard_map/ppermute | solution.py:66
  64.1 7.2 %collective-permute-start.18 = (bf16[2,32,1536]{2,1,0:T(8,128)(2,1)S(1)}, bf16[2,32,1536]{2,1,0:T(8,128)(2,1)S(1)}, u32[]{:S(2)}, u32[]{:S(2)}) collective-permute-start(bf16[2,32,1536]{2,1,0:T(8,128)(2,1)S(1)} %pad_maximum_fusion.3), channel_id=1, source_target_pairs={{0,2},{1,3},{2,0},{3,1},{4,6},{5,7},{6,4},{7,5},{8,10},{9,11},{10,... | collective-permute-start | bytes 589832 | tf_op jit(solution)/shard_map/ppermute | solution.py:80
